TPU v7x, 32 devices: a whole 2x2x4 slice. The times are simulated.
32 devices in a mesh: group: 2 (over x), blk: 16 (over z, y, core).
Axes of the slice: x: 2, y: 2, z: 4, core: 2. Of those that a mesh axis runs over, the one named last changes fastest.
Arguments:
- latents: bfloat16 [32, 32, 8, 512], P(('group', 'blk')), parts along dimension 0, may hold values from -6 to 6
- norm_gain: float32 [512], replicated, may hold values from 0.1 to 1.9
- metric: float32 [16, 9, 32, 8], P('blk'), may hold values from 0.1 to 1
- w_query: bfloat16 [512, 512], replicated, may hold values from -1 to 1
- w_key: bfloat16 [512, 512], replicated, may hold values from -1 to 1
- w_value: bfloat16 [512, 512], replicated, may hold values from -0.25 to 0.25
- w_output: bfloat16 [512, 512], replicated, may hold values from -0.25 to 0.25
- seam_table: int32 [16, 2, 3], P('blk'), may hold values from 0 to 15, as said below
Outputs:
- updated: bfloat16 [32, 32, 8, 512], P(('group', 'blk')), parts along dimension 0
There are 2 independent parts, one for each index of `group`. A program takes and returns all parts, laid end to end along the dimension named above; an argument that names none is the same for every part. Nothing has to cross between parts.
Inputs may be any that keep to these rules, and one draw needn't show every extreme that they name: `seam_table`: entry [d, e] names the source tile, the source edge (0 or 1) and the orientation code (0 to 3) of the rim placed beyond edge e of tile d. The pairs (source tile, source edge) of all entries are distinct.
All inputs are finite; a program needn't handle non-finite values.
Results may differ from a plain program's by a relative error of at most 0.0094.
Values may be sent and summed in bfloat16 or wider, within the bound.
No kernel may reach another device: no remote copies, remote signals or barrier semaphores. Data moves between devices by JAX's collectives and lax.ppermute only.
A program may use at most 192 MiB of HBM per device.

v0:
```python
import jax
import jax.numpy as jnp
from jax import lax
from jax.sharding import PartitionSpec as P

HEADS = 8
RADIUS = 3


def padded_2(array, sides, width):
    for axis, dim in sides:
        count, length = (lax.axis_size(axis), array.shape[dim])
        up = [(i, (i + 1) % count) for i in range(count)]
        down = [(j, i) for i, j in up]
        last = lax.slice_in_dim(array, length - width, length, axis=dim)
        first = lax.slice_in_dim(array, 0, width, axis=dim)
        before = lax.ppermute(last, axis, up)
        after = lax.ppermute(first, axis, down)
        array = jnp.concatenate([before, array, after], axis=dim)
    return array


def normalize(latents, norm_gain):
    values = latents.astype(jnp.float32)
    factor = lax.rsqrt(jnp.mean(values * values, axis=-1, keepdims=True) + 1e-05)
    return (values * factor * norm_gain).astype(jnp.bfloat16)


def pick_rims(seam_rows, piece):
    number = piece.shape[0]
    tile_ids = jnp.arange(number, dtype=jnp.int32)
    tile_hit = tile_ids[None, :] == seam_rows[:, 0:1]
    edge_hit = jnp.arange(2, dtype=jnp.int32)[None, :] == seam_rows[:, 1:2]
    chosen = (tile_hit[:, :, None] & edge_hit[:, None, :]).astype(piece.dtype)
    return jnp.einsum("enf,nfrwc->erwc", chosen, piece, preferred_element_type=jnp.float32)


def edge_rows(widened, margin):
    return jnp.stack([widened[:, :margin], widened[:, -margin:]], axis=1)


def orient_rims(received, seam_pair):
    arrived = received.astype(jnp.bfloat16)
    orient = seam_pair[:, 2]
    flip_along = (orient % 2 == 1)[:, None, None, None]
    arrived = jnp.where(flip_along, arrived[:, :, ::-1], arrived)
    flip_across = (orient // 2 == 1)[:, None, None, None]
    return jnp.where(flip_across, arrived[:, ::-1], arrived)


def place_rims(widened, received, seam_pair):
    arrived = orient_rims(received, seam_pair)
    return jnp.concatenate([arrived[0], widened, arrived[1]], axis=0)


def smooth(padded, metric):
    rows, cols = (metric.shape[-2], metric.shape[-1])
    total = jnp.zeros((rows, cols, padded.shape[-1]), jnp.float32)
    for stencil in range(9):
        row_off = stencil // 3
        col_off = stencil % 3
        total = (
            total
            + metric[stencil, :, :, None]
            * padded[row_off : row_off + rows, col_off : col_off + cols, :]
        )
    return total.astype(jnp.bfloat16)


def project(values, weight):
    shape = values.shape
    flat = values.reshape(-1, shape[-1])
    return (
        jnp.dot(flat, weight, preferred_element_type=jnp.float32)
        .astype(jnp.bfloat16)
        .reshape(shape[:-1] + (weight.shape[1],))
    )


def window_attention(query, keys, vals):
    rows, cols, channels = query.shape
    head_size = channels // HEADS
    channel_ids = jnp.arange(channels, dtype=jnp.int32) // head_size
    head_map = (channel_ids[:, None] == channel_ids[None, :]).astype(jnp.float32)
    query_wide = query.astype(jnp.float32)
    span = 2 * RADIUS + 1
    scale = head_size ** (-0.5)
    scores = []
    for row_off in range(span):
        for col_off in range(span):
            key_part = keys[row_off : row_off + rows, col_off : col_off + cols]
            products = (query_wide * key_part.astype(jnp.float32)).reshape(rows * cols, channels)
            scores.append(jnp.dot(products, head_map, precision=lax.Precision.HIGHEST) * scale)
    stacked = jnp.stack(scores)
    row_max = jnp.max(stacked, axis=0, keepdims=True)
    exp_scores = jnp.exp(stacked - row_max)
    weights = (exp_scores / jnp.sum(exp_scores, axis=0, keepdims=True)).astype(jnp.bfloat16)
    total = jnp.zeros((rows * cols, channels), jnp.float32)
    for row_off in range(span):
        for col_off in range(span):
            value_part = vals[row_off : row_off + rows, col_off : col_off + cols].reshape(
                rows * cols, channels
            )
            total = total + weights[row_off * span + col_off].astype(
                jnp.float32
            ) * value_part.astype(jnp.float32)
    return total.reshape(rows, cols, channels).astype(jnp.bfloat16)


def local(latents, norm_gain, metric, w_query, w_key, w_value, w_output, seam_table):
    own_tile = latents[0]
    channels = own_tile.shape[-1]
    normed = normalize(own_tile, norm_gain)
    margin = 1
    seam_rows = seam_table[0]
    widened = padded_2(normed[None], (("blk", 2),), margin)
    received = pick_rims(
        seam_rows, lax.all_gather(edge_rows(widened, 1), "blk", axis=0, tiled=True)
    )
    padded = place_rims(widened[0], received, seam_rows)
    smoothed = smooth(padded, metric[0])
    query = project(smoothed, w_query)
    field_wide = padded_2(smoothed[None], (("blk", 2),), RADIUS)
    field_got = pick_rims(
        seam_rows, lax.all_gather(edge_rows(field_wide, RADIUS), "blk", axis=0, tiled=True)
    )
    field_pad = place_rims(field_wide[0], field_got, seam_rows)
    key_pad = project(field_pad, w_key)
    value_pad = project(field_pad, w_value)
    attended = window_attention(query, key_pad, value_pad)
    mixed = jnp.dot(attended.reshape(-1, channels), w_output, preferred_element_type=jnp.float32)
    updated = own_tile.astype(jnp.float32) + mixed.reshape(own_tile.shape)
    return updated.astype(jnp.bfloat16)[None]


def solution(mesh):
    return jax.shard_map(
        local,
        mesh=mesh,
        in_specs=(
            P(("group", "blk"), None, None, None),
            P(),
            P("blk", None, None, None),
            P(),
            P(),
            P(),
            P(),
            P("blk", None, None),
        ),
        out_specs=P(("group", "blk"), None, None, None),
        check_vma=False,
    )
```

profile of v0, /device:TPU:0, one launch (start us, length us, event | category | flops | bytes accessed | tf_op | source)
XLA Modules:
  0.0 234.2 jit_solution(17446876268001313689)
XLA Ops:
  9.4 5.1 %collective-permute-start.1 = (bf16[1,32,1,512]{3,2,1,0:T(2,128)(2,1)S(1)}, bf16[1,32,1,512]{3,2,1,0:T(2,128)(2,1)S(1)}, u32[]{:S(2)}, u32[]{:S(2)}) collective-permute-start(bf16[1,32,1,512]{3,2,1,0:T(2,128)(2,1)S(1)} %get-tuple-element.19), channel_id=1, source_target_pairs={{1,0},{2,1},{3,2},{4,3},{5,4},{6,5},{7,6},{8,7},{9,8},{10,9},{11,1... | collective-permute-start | bytes 98312 | tf_op jit(solution)/shard_map/ppermute | solution.py:18
  18.3 20.3 %all_gather.6 = bf16[16,2,1,10,512]{4,1,3,2,0:T(2,128)(2,1)S(1)} all-gather(bf16[1,2,1,10,512]{4,1,3,2,0:T(2,128)(2,1)S(1)} %copy.96), channel_id=1, replica_groups=mesh['group'=2,'blk'=16] {'blk'}, dimensions={0}, use_global_device_ids=true | all-gather | bytes 348160 | tf_op jit(solution)/shard_map/all_gather | solution.py:118
  40.7 4.1 %collective-permute-start.3 = (bf16[1,32,3,512]{3,2,1,0:T(4,128)(2,1)S(1)}, bf16[1,32,3,512]{3,2,1,0:T(4,128)(2,1)S(1)}, u32[]{:S(2)}, u32[]{:S(2)}) collective-permute-start(bf16[1,32,3,512]{3,2,1,0:T(4,128)(2,1)S(1)} %get-tuple-element.17), channel_id=1, source_target_pairs={{1,0},{2,1},{3,2},{4,3},{5,4},{6,5},{7,6},{8,7},{9,8},{10,9},{11,1... | collective-permute-start | bytes 294920 | tf_op jit(solution)/shard_map/ppermute | solution.py:18
  44.8 2.6 %collective-permute-done.2 = bf16[1,32,3,512]{3,2,1,0:T(4,128)(2,1)S(1)} collective-permute-done((bf16[1,32,3,512]{3,2,1,0:T(4,128)(2,1)S(1)}, bf16[1,32,3,512]{3,2,1,0:T(4,128)(2,1)S(1)}, u32[]{:S(2)}, u32[]{:S(2)}) %collective-permute-start.2) | collective-permute-done | bytes 98336 | tf_op jit(solution)/shard_map/ppermute | solution.py:17
  48.5 2.6 %fusion.249 = bf16[32,8,512]{2,1,0:T(8,128)(2,1)S(1)} fusion(bf16[512,512]{1,0:T(8,128)(2,1)} %param.11, bf16[32,10,512]{2,1,0:T(8,128)(2,1)S(1)} %get-tuple-element.15, bf16[1,10,512]{2,1,0:T(8,128)(2,1)S(1)} %copy.105, bf16[1,10,512]{2,1,0:T(8,128)(2,1)S(1)} %copy.98, f32[32,8]{1,0:T(8,128)S(1)} %copy.107, f32[32,8]{1,0:T(8,128)S(1)} %copy.106, ...), kind=kOutput, calls=%fused_computation.206 | convolution fusion | flops 140247040 | bytes 2277376 | tf_op jit(solution)/shard_map/dot_general | solution.py:74
  51.1 37.6 %all-gather.2.cloned.1.call-done = bf16[16,2,3,14,512]{4,1,3,2,0:T(2,128)(2,1)} async-done(((bf16[1,2,3,14,512]{4,1,3,2,0:T(2,128)(2,1)}), bf16[16,2,3,14,512]{4,1,3,2,0:T(2,128)(2,1)}) %all-gather.2.cloned.1.call-update) | async-done | bytes 1376272 | tf_op jit(solution)/shard_map/all_gather | solution.py:125
  88.8 1.8 fusion.254
  95.1 1.8 bitcast_dynamic-update-slice_fusion.46
  96.9 1.8 bitcast_dynamic-update-slice_fusion.45
  98.7 1.8 bitcast_dynamic-update-slice_fusion.44
  100.5 1.8 bitcast_dynamic-update-slice_fusion.43
  102.3 1.8 bitcast_dynamic-update-slice_fusion.42
  107.2 1.8 bitcast_dynamic-update-slice_fusion.39
  109.0 1.8 bitcast_dynamic-update-slice_fusion.38
  110.8 1.8 bitcast_dynamic-update-slice_fusion.37
  112.6 1.8 bitcast_dynamic-update-slice_fusion.36
  114.4 1.8 bitcast_dynamic-update-slice_fusion.35
  116.2 1.8 bitcast_dynamic-update-slice_fusion.34
  118.0 2.1 bitcast_dynamic-update-slice_fusion.33
  120.0 1.8 bitcast_dynamic-update-slice_fusion.32
  121.8 1.8 bitcast_dynamic-update-slice_fusion.31
  123.6 1.8 bitcast_dynamic-update-slice_fusion.30
  125.4 1.8 bitcast_dynamic-update-slice_fusion.29
  130.7 1.8 bitcast_dynamic-update-slice_fusion.26
  132.5 1.9 bitcast_dynamic-update-slice_fusion.25
  134.4 1.8 bitcast_dynamic-update-slice_fusion.24
  136.2 1.8 bitcast_dynamic-update-slice_fusion.23
  138.0 1.8 bitcast_dynamic-update-slice_fusion.22
  139.8 1.8 bitcast_dynamic-update-slice_fusion.21
  143.3 1.8 bitcast_dynamic-update-slice_fusion.19
  145.1 1.8 bitcast_dynamic-update-slice_fusion.18
  146.9 1.8 bitcast_dynamic-update-slice_fusion.17
  148.7 2.2 bitcast_dynamic-update-slice_fusion.16
  151.0 1.8 bitcast_dynamic-update-slice_fusion.15
  156.3 1.8 bitcast_dynamic-update-slice_fusion.12
  158.0 1.8 bitcast_dynamic-update-slice_fusion.11
  159.8 1.8 bitcast_dynamic-update-slice_fusion.10
  161.6 1.8 bitcast_dynamic-update-slice_fusion.9
  163.4 1.8 bitcast_dynamic-update-slice_fusion.8
  165.2 1.8 bitcast_dynamic-update-slice_fusion.7
  170.5 1.8 bitcast_dynamic-update-slice_fusion.4
  174.1 1.8 bitcast_dynamic-update-slice_fusion.2
  175.9 1.8 bitcast_dynamic-update-slice_fusion.1
  177.7 1.8 bitcast_dynamic-update-slice_fusion
  179.5 11.0 %maximum_maximum_fusion = f32[256,512]{1,0:T(8,128)S(1)} fusion(f32[256,512]{1,0:T(8,128)} %get-tuple-element.132, f32[256,512]{1,0:T(8,128)} %get-tuple-element.130, f32[256,512]{1,0:T(8,128)} %get-tuple-element.128, f32[256,512]{1,0:T(8,128)} %get-tuple-element.126, f32[256,512]{1,0:T(8,128)} %get-tuple-element.124, f32[256,512]{1,0:T(8,128)} %get-tuple-element.122, ...), kind=kLoop, calls=%fused_computation.422 | loop fusion | flops 6291456 | bytes 26214400 | tf_op jit(solution)/shard_map/reduce_max | solution.py:95
  190.6 11.1 %fusion = f32[256,512]{1,0:T(8,128)S(1)} fusion(f32[49,256,512]{2,1,0:T(8,128)} %get-tuple-element.131, f32[256,512]{1,0:T(8,128)S(1)} %maximum_maximum_fusion), kind=kLoop, calls=%fused_computation.2 | loop fusion | flops 12713984 | bytes 26738688 | tf_op jit(solution)/shard_map/reduce_sum | solution.py:97
  201.8 16.4 %divide_convert_fusion = bf16[49,256,512]{2,1,0:T(8,128)(2,1)} fusion(f32[49,256,512]{2,1,0:T(8,128)} %get-tuple-element.131, f32[256,512]{1,0:T(8,128)S(1)} %fusion, f32[256,512]{1,0:T(8,128)S(1)} %maximum_maximum_fusion), kind=kLoop, calls=%fused_computation | loop fusion | flops 19267584 | bytes 39583744 | tf_op jit(solution)/shard_map/convert_element_type | solution.py:97
  218.8 8.3 %fusion.250 = bf16[1,32,8,512]{3,2,1,0:T(8,128)(2,1)} fusion(bf16[1,32,8,512]{3,2,1,0:T(8,128)(2,1)S(1)} %copy-done.2, bf16[512,512]{1,0:T(8,128)(2,1)} %param.14, bf16[38,14,512]{2,1,0:T(8,128)(2,1)S(1)} %reshape.734, bf16[49,256,512]{2,1,0:T(8,128)(2,1)} %divide_convert_fusion), kind=kOutput, calls=%fused_computation.207 | convolution fusion | flops 160301056 | bytes 26738688 | tf_op jit(solution)/shard_map/dot_general | solution.py:131
  (72 shorter events, 32.0 us)
Async XLA Ops:
  6.5 84.8 %copy-start = (bf16[512,512]{1,0:T(8,128)(2,1)S(1)}, bf16[512,512]{1,0:T(8,128)(2,1)}, u32[]{:S(2)}) copy-start(bf16[512,512]{1,0:T(8,128)(2,1)} %param.12) | copy-start | bytes 1572868
  6.5 82.2 %all-gather.2.cloned.1.call-start = ((), (), s32[]{:S(2)}) async-start(), calls=%async_computation | async-start | bytes 1462272 | tf_op jit(solution)/shard_map/all_gather | solution.py:125
  8.9 9.0 %collective-permute-start = (bf16[1,32,1,512]{3,2,1,0:T(2,128)(2,1)S(1)}, bf16[1,32,1,512]{3,2,1,0:T(2,128)(2,1)S(1)}, u32[]{:S(2)}, u32[]{:S(2)}) collective-permute-start(bf16[1,32,1,512]{3,2,1,0:T(2,128)(2,1)S(1)} %get-tuple-element.18), channel_id=1, source_target_pairs={{0,1},{1,2},{2,3},{3,4},{4,5},{5,6},{6,7},{7,8},{8,9},{9,10},{10,1... | collective-permute-start | bytes 98312 | tf_op jit(solution)/shard_map/ppermute | solution.py:17
  9.4 8.5 %collective-permute-start.1 = (bf16[1,32,1,512]{3,2,1,0:T(2,128)(2,1)S(1)}, bf16[1,32,1,512]{3,2,1,0:T(2,128)(2,1)S(1)}, u32[]{:S(2)}, u32[]{:S(2)}) collective-permute-start(bf16[1,32,1,512]{3,2,1,0:T(2,128)(2,1)S(1)} %get-tuple-element.19), channel_id=1, source_target_pairs={{1,0},{2,1},{3,2},{4,3},{5,4},{6,5},{7,6},{8,7},{9,8},{10,9},{11,1... | collective-permute-start | bytes 98312 | tf_op jit(solution)/shard_map/ppermute | solution.py:18
  40.3 7.1 %collective-permute-start.2 = (bf16[1,32,3,512]{3,2,1,0:T(4,128)(2,1)S(1)}, bf16[1,32,3,512]{3,2,1,0:T(4,128)(2,1)S(1)}, u32[]{:S(2)}, u32[]{:S(2)}) collective-permute-start(bf16[1,32,3,512]{3,2,1,0:T(4,128)(2,1)S(1)} %get-tuple-element.16), channel_id=1, source_target_pairs={{0,1},{1,2},{2,3},{3,4},{4,5},{5,6},{6,7},{7,8},{8,9},{9,10},{10,1... | collective-permute-start | bytes 294920 | tf_op jit(solution)/shard_map/ppermute | solution.py:17
  40.7 6.7 %collective-permute-start.3 = (bf16[1,32,3,512]{3,2,1,0:T(4,128)(2,1)S(1)}, bf16[1,32,3,512]{3,2,1,0:T(4,128)(2,1)S(1)}, u32[]{:S(2)}, u32[]{:S(2)}) collective-permute-start(bf16[1,32,3,512]{3,2,1,0:T(4,128)(2,1)S(1)} %get-tuple-element.17), channel_id=1, source_target_pairs={{1,0},{2,1},{3,2},{4,3},{5,4},{6,5},{7,6},{8,7},{9,8},{10,9},{11,1... | collective-permute-start | bytes 294920 | tf_op jit(solution)/shard_map/ppermute | solution.py:18
  201.7 16.4 %copy-start.3 = (bf16[512,512]{1,0:T(8,128)(2,1)S(1)}, bf16[512,512]{1,0:T(8,128)(2,1)}, u32[]{:S(2)}) copy-start(bf16[512,512]{1,0:T(8,128)(2,1)} %param.13) | copy-start | bytes 1572868
  201.7 17.0 %copy-start.2 = (bf16[1,32,8,512]{3,2,1,0:T(8,128)(2,1)S(1)}, bf16[1,32,8,512]{3,2,1,0:T(8,128)(2,1)}, u32[]{:S(2)}) copy-start(bf16[1,32,8,512]{3,2,1,0:T(8,128)(2,1)} %param.8) | copy-start | bytes 786436
  201.8 25.3 %copy-start.1 = (bf16[512,512]{1,0:T(8,128)(2,1)S(1)}, bf16[512,512]{1,0:T(8,128)(2,1)}, u32[]{:S(2)}) copy-start(bf16[512,512]{1,0:T(8,128)(2,1)} %param.12) | copy-start | bytes 1572868
Sparse Core Ops, SparseCore 0:
  48.6 40.0 all-gather.1
where the time goes:
time: 238 us; the launch traced here: 234 us
  matrix products  101 us (42%)
  other arithmetic  43.9 us (18%)
  waiting for transfers between devices  40.3 us (17%)
  blocking collectives  20.3 us (9%)
  between operations  13.9 us (6%)
  starting transfers between devices  10.1 us (4%)
  local copies, waits for them, and re-layouts  4.13 us (2%)
    dot_general x49, matrix products, window_attention(): jnp.dot(products, head_map, precision=lax.Precision.HIGHEST) * scale  87.6 us
    all_gather x1, waiting for transfers between devices, local(): lax.all_gather(edge_rows(field_wide, RADIUS), 'blk', axis=0, tiled=True)  37.6 us
    all_gather x1, blocking collectives, local(): lax.all_gather(edge_rows(widened, 1), 'blk', axis=0, tiled=True)  20.3 us
    convert_element_type x1, other arithmetic, window_attention(): (exp_scores / jnp.sum(exp_scores, axis=0, keepdims=True)).astype(jnp.bflo...  16.4 us
    reduce_sum x1, other arithmetic, window_attention(): jnp.sum(exp_scores, axis=0, keepdims=True)  11.1 us
    reduce_max x1, other arithmetic, window_attention(): row_max = jnp.max(stacked, axis=0, keepdims=True)  11 us
    ppermute x2, starting transfers between devices, padded_2(): after = lax.ppermute(first, axis, down)  9.15 us
    dot_general x1, matrix products, local(): jnp.dot(attended.reshape(-1, channels), w_output, preferred_element_type=...  8.31 us
  transfers between devices with their start and end apart: 5, of which 2 were waited for; matrix products, arithmetic and copies ran while one was open for 3% of the time, Pallas kernels for 0%

commit v1 on v0

--- a/solution.py
+++ b/solution.py
@@ -2,6 +2,8 @@
 import jax.numpy as jnp
 from jax import lax
 from jax.sharding import PartitionSpec as P
+from jax.experimental import pallas as pl
+from jax.experimental.pallas import tpu as pltpu
 
 HEADS = 8
 RADIUS = 3
@@ -77,34 +79,86 @@
     )
 
 
-def window_attention(query, keys, vals):
-    rows, cols, channels = query.shape
+def attention_kernel(q_ref, k_ref, v_ref, lat_ref, wo_ref, out_ref, s_ref):
+    span = 2 * RADIUS + 1
+    cells, channels = q_ref.shape
+    rows = cells // k_ref.shape[2]
     head_size = channels // HEADS
-    channel_ids = jnp.arange(channels, dtype=jnp.int32) // head_size
-    head_map = (channel_ids[:, None] == channel_ids[None, :]).astype(jnp.float32)
-    query_wide = query.astype(jnp.float32)
+    lanes = s_ref.shape[-1]
+    c_ids = lax.broadcasted_iota(jnp.int32, (channels, lanes), 0) // head_size
+    h_ids = lax.broadcasted_iota(jnp.int32, (channels, lanes), 1)
+    head_sum = (c_ids == h_ids).astype(jnp.bfloat16)
+    h_ids2 = lax.broadcasted_iota(jnp.int32, (lanes, channels), 0)
+    c_ids2 = lax.broadcasted_iota(jnp.int32, (lanes, channels), 1) // head_size
+    head_spread = (c_ids2 == h_ids2).astype(jnp.bfloat16)
+    scale = head_size ** (-0.5)
+    q = q_ref[...].astype(jnp.float32)
+
+    def window(ref, o):
+        a = o // span
+        b = o % span
+        return ref[b, pl.ds(a, rows)].reshape(cells, channels)
+
+    def score_step(o, running):
+        prod = q * window(k_ref, o)
+        hi = prod.astype(jnp.bfloat16)
+        lo = (prod - hi.astype(jnp.float32)).astype(jnp.bfloat16)
+        s = (
+            jnp.dot(hi, head_sum, preferred_element_type=jnp.float32)
+            + jnp.dot(lo, head_sum, preferred_element_type=jnp.float32)
+        ) * scale
+        s_ref[o] = s
+        return jnp.maximum(running, s)
+
+    top = lax.fori_loop(
+        0, span * span, score_step, jnp.full((cells, lanes), -jnp.inf, jnp.float32)
+    )
+
+    def exp_step(o, total):
+        e = jnp.exp(s_ref[o] - top)
+        s_ref[o] = e
+        return total + e
+
+    denom = lax.fori_loop(0, span * span, exp_step, jnp.zeros((cells, lanes), jnp.float32))
+
+    def value_step(o, acc):
+        w = (s_ref[o] / denom).astype(jnp.bfloat16)
+        wide = jnp.dot(w, head_spread, preferred_element_type=jnp.float32)
+        return acc + wide * window(v_ref, o)
+
+    acc = lax.fori_loop(
+        0, span * span, value_step, jnp.zeros((cells, channels), jnp.float32)
+    )
+    attended = acc.astype(jnp.bfloat16)
+    mixed = jnp.dot(attended, wo_ref[...], preferred_element_type=jnp.float32)
+    out_ref[...] = (lat_ref[...].astype(jnp.float32) + mixed).astype(out_ref.dtype)
+
+
+def column_shifts(padded, cols):
+    span = padded.shape[1] - cols + 1
+    return jnp.stack([padded[:, b : b + cols] for b in range(span)]).astype(jnp.float32)
+
+
+def attend_and_mix(query, key_pad, value_pad, own_tile, w_output):
+    rows, cols, channels = own_tile.shape
+    cells = rows * cols
     span = 2 * RADIUS + 1
-    scale = head_size ** (-0.5)
-    scores = []
-    for row_off in range(span):
-        for col_off in range(span):
-            key_part = keys[row_off : row_off + rows, col_off : col_off + cols]
-            products = (query_wide * key_part.astype(jnp.float32)).reshape(rows * cols, channels)
-            scores.append(jnp.dot(products, head_map, precision=lax.Precision.HIGHEST) * scale)
-    stacked = jnp.stack(scores)
-    row_max = jnp.max(stacked, axis=0, keepdims=True)
-    exp_scores = jnp.exp(stacked - row_max)
-    weights = (exp_scores / jnp.sum(exp_scores, axis=0, keepdims=True)).astype(jnp.bfloat16)
-    total = jnp.zeros((rows * cols, channels), jnp.float32)
-    for row_off in range(span):
-        for col_off in range(span):
-            value_part = vals[row_off : row_off + rows, col_off : col_off + cols].reshape(
-                rows * cols, channels
-            )
-            total = total + weights[row_off * span + col_off].astype(
-                jnp.float32
-            ) * value_part.astype(jnp.float32)
-    return total.reshape(rows, cols, channels).astype(jnp.bfloat16)
+    vmem = pl.BlockSpec(memory_space=pltpu.VMEM)
+    out = pl.pallas_call(
+        attention_kernel,
+        out_shape=jax.ShapeDtypeStruct((cells, channels), own_tile.dtype),
+        in_specs=[vmem] * 5,
+        out_specs=vmem,
+        scratch_shapes=[pltpu.VMEM((span * span, cells, 128), jnp.float32)],
+        compiler_params=pltpu.CompilerParams(vmem_limit_bytes=60 * 1024 * 1024),
+    )(
+        query.reshape(cells, channels),
+        column_shifts(key_pad, cols),
+        column_shifts(value_pad, cols),
+        own_tile.reshape(cells, channels),
+        w_output,
+    )
+    return out.reshape(rows, cols, channels)
 
 
 def local(latents, norm_gain, metric, w_query, w_key, w_value, w_output, seam_table):
@@ -127,10 +181,7 @@
     field_pad = place_rims(field_wide[0], field_got, seam_rows)
     key_pad = project(field_pad, w_key)
     value_pad = project(field_pad, w_value)
-    attended = window_attention(query, key_pad, value_pad)
-    mixed = jnp.dot(attended.reshape(-1, channels), w_output, preferred_element_type=jnp.float32)
-    updated = own_tile.astype(jnp.float32) + mixed.reshape(own_tile.shape)
-    return updated.astype(jnp.bfloat16)[None]
+    return attend_and_mix(query, key_pad, value_pad, own_tile, w_output)[None]
 
 
 def solution(mesh):

time: 238 us -> 141 us (0.59); the launches traced: 234 us -> 141 us
  matrix products: 101 us -> 5.02 us
  Pallas kernels: 0 us -> 34.6 us
  other arithmetic: 43.9 us -> 10.7 us
    dot_general x50 -> x0, matrix products: 95.9 us -> none  [the longest x49 87.6 us: window_attention(): jnp.dot(products, head_map, precision=lax.Precision.HIGHEST) * scale]
    pallas_call x0 -> x1, Pallas kernels: none -> 34.6 us  [attend_and_mix(): pl.pallas_call(attention_kernel, out_shape=jax.ShapeDtypeStruct((cells, c...]
    reduce_sum x1 -> x0, other arithmetic: 11.1 us -> none  [window_attention(): jnp.sum(exp_scores, axis=0, keepdims=True)]
    convert_element_type x1 -> x2, other arithmetic: 16.4 us -> 5.3 us  [column_shifts(): jnp.stack([padded[:, b:b + cols] for b in range(span)]).astype(jnp.float32)]
    reduce_max x1 -> x0, other arithmetic: 11 us -> none  [window_attention(): row_max = jnp.max(stacked, axis=0, keepdims=True)]
  transfers between devices with their start and end apart: 5 -> 5, of which waited for: 2 -> 2; matrix products, arithmetic and copies ran while one was open for 3% -> 4% of each run, Pallas kernels for 0% -> 0%
where the time goes in v1:
time: 141 us
  waiting for transfers between devices  40.9 us (29%)
  Pallas kernels  34.6 us (25%)
  blocking collectives  20.3 us (14%)
  between operations  13.7 us (10%)
  other arithmetic  10.7 us (8%)
  starting transfers between devices  10.1 us (7%)
  local copies, waits for them, and re-layouts  5.59 us (4%)
  matrix products  5.02 us (4%)
    all_gather x1, waiting for transfers between devices, local(): lax.all_gather(edge_rows(field_wide, RADIUS), 'blk', axis=0, tiled=True)  38.2 us
    pallas_call x1, Pallas kernels, attend_and_mix(): pl.pallas_call(attention_kernel, out_shape=jax.ShapeDtypeStruct((cells, c...  34.6 us
    all_gather x1, blocking collectives, local(): lax.all_gather(edge_rows(widened, 1), 'blk', axis=0, tiled=True)  20.3 us
    ppermute x2, starting transfers between devices, padded_2(): after = lax.ppermute(first, axis, down)  9.15 us
    convert_element_type x2, other arithmetic, column_shifts(): jnp.stack([padded[:, b:b + cols] for b in range(span)]).astype(jnp.float32)  5.3 us
    dot_general x3, matrix products, project(): jnp.dot(flat, weight, preferred_element_type=jnp.float32)  2.93 us
  transfers between devices with their start and end apart: 5, of which 2 were waited for; matrix products, arithmetic and copies ran while one was open for 4% of the time, Pallas kernels for 0%

profile of v1, /device:TPU:0, one launch (start us, length us, event | category | flops | bytes accessed | tf_op | source)
XLA Modules:
  0.0 140.9 jit_solution(6543504255450224890)
XLA Ops:
  6.5 1.1 fusion.9
  7.7 1.1 fusion.11
  8.8 0.1 fusion.43
  8.9 0.5 collective-permute-start
  9.4 5.1 %collective-permute-start.1 = (bf16[1,32,1,512]{3,2,1,0:T(2,128)(2,1)S(1)}, bf16[1,32,1,512]{3,2,1,0:T(2,128)(2,1)S(1)}, u32[]{:S(2)}, u32[]{:S(2)}) collective-permute-start(bf16[1,32,1,512]{3,2,1,0:T(2,128)(2,1)S(1)} %get-tuple-element.19), channel_id=1, source_target_pairs={{1,0},{2,1},{3,2},{4,3},{5,4},{6,5},{7,6},{8,7},{9,8},{10,9},{11,1... | collective-permute-start | bytes 98312 | tf_op jit(solution)/shard_map/ppermute | solution.py:20
  14.4 1.0 slice_reduce_fusion.2
  15.5 0.8 slice_bitcast_fusion.26
  16.4 0.9 compare_reduce_fusion
  17.3 0.1 copy.104
  17.9 0.3 pad_maximum_fusion.1
  18.3 20.3 %all_gather.6 = bf16[16,2,1,10,512]{4,1,3,2,0:T(2,128)(2,1)S(1)} all-gather(bf16[1,2,1,10,512]{4,1,3,2,0:T(2,128)(2,1)S(1)} %copy.96), channel_id=1, replica_groups=mesh['group'=2,'blk'=16] {'blk'}, dimensions={0}, use_global_device_ids=true | all-gather | bytes 348160 | tf_op jit(solution)/shard_map/all_gather | solution.py:172
  38.6 0.3 fusion.8
  38.9 0.1 broadcast_select_fusion.2
  39.1 1.1 fusion.51
  40.2 0.1 fusion.42
  40.3 0.4 collective-permute-start.2
  40.7 4.1 %collective-permute-start.3 = (bf16[1,32,3,512]{3,2,1,0:T(4,128)(2,1)S(1)}, bf16[1,32,3,512]{3,2,1,0:T(4,128)(2,1)S(1)}, u32[]{:S(2)}, u32[]{:S(2)}) collective-permute-start(bf16[1,32,3,512]{3,2,1,0:T(4,128)(2,1)S(1)} %get-tuple-element.17), channel_id=1, source_target_pairs={{1,0},{2,1},{3,2},{4,3},{5,4},{6,5},{7,6},{8,7},{9,8},{10,9},{11,1... | collective-permute-start | bytes 294920 | tf_op jit(solution)/shard_map/ppermute | solution.py:20
  44.8 2.6 %collective-permute-done.2 = bf16[1,32,3,512]{3,2,1,0:T(4,128)(2,1)S(1)} collective-permute-done((bf16[1,32,3,512]{3,2,1,0:T(4,128)(2,1)S(1)}, bf16[1,32,3,512]{3,2,1,0:T(4,128)(2,1)S(1)}, u32[]{:S(2)}, u32[]{:S(2)}) %collective-permute-start.2) | collective-permute-done | bytes 98336 | tf_op jit(solution)/shard_map/ppermute | solution.py:19
  47.4 0.3 fusion.41
  47.8 0.7 copy.108
  48.5 2.0 %convolution_convert_fusion.2.q_ref = bf16[256,512]{1,0:T(8,128)(2,1)} fusion(bf16[512,512]{1,0:T(8,128)(2,1)S(1)} %copy-done.2, bf16[32,10,512]{2,1,0:T(8,128)(2,1)S(1)} %get-tuple-element.15, bf16[1,10,512]{2,1,0:T(8,128)(2,1)S(1)} %copy.105, bf16[1,10,512]{2,1,0:T(8,128)(2,1)S(1)} %copy.98, f32[32,8]{1,0:T(8,128)S(1)} %copy.107, f32[32,8]{1,0:T(8,128)S(1)} %copy.106, ...), kind=kOutput, calls=%fused_computation.4 | convolution fusion | flops 140247040 | bytes 2277376 | tf_op jit(solution)/shard_map/dot_general | solution.py:76
  50.6 38.2 %all-gather.2.cloned.1.call-done = bf16[16,2,3,14,512]{4,1,3,2,0:T(2,128)(2,1)} async-done(((bf16[1,2,3,14,512]{4,1,3,2,0:T(2,128)(2,1)}), bf16[16,2,3,14,512]{4,1,3,2,0:T(2,128)(2,1)}) %all-gather.2.cloned.1.call-update) | async-done | bytes 1376272 | tf_op jit(solution)/shard_map/all_gather | solution.py:179
  88.8 1.8 %fusion.5 = bf16[2,3,14,512]{3,0,2,1:T(2,128)(2,1)S(1)} fusion(bf16[16,2,3,14,512]{4,1,3,2,0:T(2,128)(2,1)} %all-gather.2.cloned.1.call-done, pred[2,2]{0,1:T(4,128)(4,1)S(1)} %iota_compare_fusion, pred[2,16]{1,0:T(4,128)(4,1)S(1)} %iota_compare_fusion.1), kind=kOutput, calls=%fused_computation.6 | convolution fusion | flops 2795584 | bytes 1462308 | tf_op jit(solution)/shard_map/enf,nfrwc->erwc/dot_general | solution.py:37
  90.6 0.2 broadcast_select_fusion
  90.7 0.1 broadcast_select_fusion.1
  90.9 0.1 fusion.44
  91.1 0.1 pad_maximum_fusion
  91.2 0.2 reshape.109
  91.3 0.4 convolution_convert_fusion
  91.8 0.3 copy-done.1
  92.1 0.4 convolution_convert_fusion.1
  92.5 0.2 reshape.110
  92.7 0.2 reshape.111
  92.9 0.1 fusion.19
  93.0 0.1 fusion.18
  93.1 0.1 fusion.17
  93.2 0.1 fusion.16
  93.3 0.1 fusion.15
  93.4 0.1 fusion.14
  93.5 2.7 %convert_element_type.81.v_ref = f32[7,38,8,512]{3,2,1,0:T(8,128)} convert(bf16[7,38,8,512]{3,2,1,0:T(8,128)(2,1)S(1)} %fusion.14) | non-fusion elementwise | flops 1089536 | bytes 6537216 | tf_op jit(solution)/shard_map/convert_element_type | solution.py:139
  96.2 0.1 fusion.26
  96.3 0.1 fusion.25
  96.4 0.1 fusion.24
  96.5 0.1 fusion.23
  96.6 0.1 fusion.22
  96.7 0.1 fusion.21
  96.8 2.6 %convert_element_type.79.k_ref = f32[7,38,8,512]{3,2,1,0:T(8,128)} convert(bf16[7,38,8,512]{3,2,1,0:T(8,128)(2,1)S(1)} %fusion.21) | non-fusion elementwise | flops 1089536 | bytes 6537216 | tf_op jit(solution)/shard_map/convert_element_type | solution.py:139
  99.4 34.6 %shard_map.82 = bf16[256,512]{1,0:T(8,128)(2,1)} custom-call(bf16[256,512]{1,0:T(8,128)(2,1)} %convolution_convert_fusion.2.q_ref, f32[7,38,8,512]{3,2,1,0:T(8,128)} %convert_element_type.79.k_ref, f32[7,38,8,512]{3,2,1,0:T(8,128)} %convert_element_type.81.v_ref, bf16[256,512]{1,0:T(8,128)(2,1)} %bitcast.124, bf16[512,512]{1,0:T(8,128)(2,1)} %wo_ref.1), custom_call_target="tpu_custom_call" | custom-call | tf_op jit(solution)/shard_map/pallas_call | solution.py:147
  (33 shorter events, 0.9 us)
Async XLA Ops:
  6.5 84.8 %copy-start = (bf16[512,512]{1,0:T(8,128)(2,1)S(1)}, bf16[512,512]{1,0:T(8,128)(2,1)}, u32[]{:S(2)}) copy-start(bf16[512,512]{1,0:T(8,128)(2,1)} %param.13) | copy-start | bytes 1572868
  6.5 82.2 %all-gather.2.cloned.1.call-start = ((), (), s32[]{:S(2)}) async-start(), calls=%async_computation | async-start | bytes 1462272 | tf_op jit(solution)/shard_map/all_gather | solution.py:179
  8.9 9.0 %collective-permute-start = (bf16[1,32,1,512]{3,2,1,0:T(2,128)(2,1)S(1)}, bf16[1,32,1,512]{3,2,1,0:T(2,128)(2,1)S(1)}, u32[]{:S(2)}, u32[]{:S(2)}) collective-permute-start(bf16[1,32,1,512]{3,2,1,0:T(2,128)(2,1)S(1)} %get-tuple-element.18), channel_id=1, source_target_pairs={{0,1},{1,2},{2,3},{3,4},{4,5},{5,6},{6,7},{7,8},{8,9},{9,10},{10,1... | collective-permute-start | bytes 98312 | tf_op jit(solution)/shard_map/ppermute | solution.py:19
  9.4 8.5 %collective-permute-start.1 = (bf16[1,32,1,512]{3,2,1,0:T(2,128)(2,1)S(1)}, bf16[1,32,1,512]{3,2,1,0:T(2,128)(2,1)S(1)}, u32[]{:S(2)}, u32[]{:S(2)}) collective-permute-start(bf16[1,32,1,512]{3,2,1,0:T(2,128)(2,1)S(1)} %get-tuple-element.19), channel_id=1, source_target_pairs={{1,0},{2,1},{3,2},{4,3},{5,4},{6,5},{7,6},{8,7},{9,8},{10,9},{11,1... | collective-permute-start | bytes 98312 | tf_op jit(solution)/shard_map/ppermute | solution.py:20
  39.1 9.4 %copy-start.2 = (bf16[512,512]{1,0:T(8,128)(2,1)S(1)}, bf16[512,512]{1,0:T(8,128)(2,1)}, u32[]{:S(2)}) copy-start(bf16[512,512]{1,0:T(8,128)(2,1)} %param.11) | copy-start | bytes 1572868
  40.3 7.1 %collective-permute-start.2 = (bf16[1,32,3,512]{3,2,1,0:T(4,128)(2,1)S(1)}, bf16[1,32,3,512]{3,2,1,0:T(4,128)(2,1)S(1)}, u32[]{:S(2)}, u32[]{:S(2)}) collective-permute-start(bf16[1,32,3,512]{3,2,1,0:T(4,128)(2,1)S(1)} %get-tuple-element.16), channel_id=1, source_target_pairs={{0,1},{1,2},{2,3},{3,4},{4,5},{5,6},{6,7},{7,8},{8,9},{9,10},{10,1... | collective-permute-start | bytes 294920 | tf_op jit(solution)/shard_map/ppermute | solution.py:19
  40.7 6.7 %collective-permute-start.3 = (bf16[1,32,3,512]{3,2,1,0:T(4,128)(2,1)S(1)}, bf16[1,32,3,512]{3,2,1,0:T(4,128)(2,1)S(1)}, u32[]{:S(2)}, u32[]{:S(2)}) collective-permute-start(bf16[1,32,3,512]{3,2,1,0:T(4,128)(2,1)S(1)} %get-tuple-element.17), channel_id=1, source_target_pairs={{1,0},{2,1},{3,2},{4,3},{5,4},{6,5},{7,6},{8,7},{9,8},{10,9},{11,1... | collective-permute-start | bytes 294920 | tf_op jit(solution)/shard_map/ppermute | solution.py:20
  91.0 1.0 copy-start.1
Sparse Core Ops, SparseCore 0:
  48.6 40.0 all-gather.1

commit v2 on v1

--- a/solution.py
+++ b/solution.py
@@ -161,24 +161,91 @@
     return out.reshape(rows, cols, channels)
 
 
+def smooth_batched(padded, metric):
+    rows, cols = (metric.shape[-2], metric.shape[-1])
+    total = jnp.zeros(padded.shape[:-3] + (rows, cols, padded.shape[-1]), jnp.float32)
+    for stencil in range(9):
+        row_off = stencil // 3
+        col_off = stencil % 3
+        total = (
+            total
+            + metric[..., stencil, :, :, None]
+            * padded[..., row_off : row_off + rows, col_off : col_off + cols, :]
+        )
+    return total.astype(jnp.bfloat16)
+
+
+def widen_tiles(field, margin):
+    west = jnp.roll(field, 1, axis=0)[:, :, -margin:]
+    east = jnp.roll(field, -1, axis=0)[:, :, :margin]
+    return jnp.concatenate([west, field, east], axis=2)
+
+
+def pick_all(table, edges):
+    number = edges.shape[0]
+    tile_hit = jnp.arange(number, dtype=jnp.int32) == table[..., 0:1]
+    edge_hit = jnp.arange(2, dtype=jnp.int32) == table[..., 1:2]
+    chosen = (tile_hit[..., :, None] & edge_hit[..., None, :]).astype(edges.dtype)
+    got = jnp.einsum("...nf,nfrwc->...rwc", chosen, edges, preferred_element_type=jnp.float32)
+    return got.astype(edges.dtype)
+
+
 def local(latents, norm_gain, metric, w_query, w_key, w_value, w_output, seam_table):
     own_tile = latents[0]
-    channels = own_tile.shape[-1]
+    rows, cols, channels = own_tile.shape
+    count = lax.axis_size("blk")
+    me = lax.axis_index("blk")
+    up = [(i, (i + 1) % count) for i in range(count)]
+    down = [(j, i) for i, j in up]
+    side = RADIUS + 1
+    band = jnp.concatenate([own_tile[:side], own_tile[rows - side :]], axis=0)
+    bands = lax.all_gather(band[None], "blk", axis=0, tiled=True)
+    metric_all = lax.all_gather(metric, "blk", axis=0, tiled=True)
+    table_all = lax.all_gather(seam_table, "blk", axis=0, tiled=True)
+    west_cols = lax.ppermute(own_tile[:, cols - side :], "blk", up)
+    east_cols = lax.ppermute(own_tile[:, :side], "blk", down)
+
+    normed_bands = widen_tiles(normalize(bands, norm_gain), 1)
+    edges1 = jnp.stack([normed_bands[:, 0], normed_bands[:, -1]], axis=1)[:, :, None]
+    rims1 = pick_all(table_all, edges1)[:, :, 0]
+    flip = (table_all[:, :, 2] % 2 == 1)[:, :, None, None]
+    rims1 = jnp.where(flip, rims1[:, :, ::-1], rims1)
+
+    top = jnp.concatenate([rims1[:, 0:1], normed_bands[:, :side]], axis=1)
+    bottom = jnp.concatenate([normed_bands[:, side:], rims1[:, 1:2]], axis=1)
+    sm_top = smooth_batched(top, metric_all[:, :, :RADIUS])
+    sm_bottom = smooth_batched(bottom, metric_all[:, :, rows - RADIUS :])
+    sm_bands = widen_tiles(jnp.concatenate([sm_top, sm_bottom], axis=1), RADIUS)
+    edges3 = jnp.stack([sm_bands[:, :RADIUS], sm_bands[:, RADIUS:]], axis=1)
+
     normed = normalize(own_tile, norm_gain)
-    margin = 1
+    west = normalize(west_cols, norm_gain)
+    east = normalize(east_cols, norm_gain)
+    prev = (me + count - 1) % count
+    nxt = (me + 1) % count
+    rims_prev = lax.dynamic_index_in_dim(rims1, prev, 0, keepdims=False)
+    rims_me = lax.dynamic_index_in_dim(rims1, me, 0, keepdims=False)
+    rims_next = lax.dynamic_index_in_dim(rims1, nxt, 0, keepdims=False)
+    met_prev = lax.dynamic_index_in_dim(metric_all, prev, 0, keepdims=False)
+    met_next = lax.dynamic_index_in_dim(metric_all, nxt, 0, keepdims=False)
+
+    def pad_rows(body, rims, lo, hi):
+        return jnp.concatenate([rims[0:1, lo:hi], body, rims[1:2, lo:hi]], axis=0)
+
+    wide_me = jnp.concatenate([west[:, -1:], normed, east[:, :1]], axis=1)
+    sm_me = smooth_batched(pad_rows(wide_me, rims_me, 0, cols + 2), metric[0])
+    wide_prev = jnp.concatenate([west, normed[:, :1]], axis=1)
+    sm_prev = smooth_batched(
+        pad_rows(wide_prev, rims_prev, cols - RADIUS, cols + 2), met_prev[:, :, cols - RADIUS :]
+    )
+    wide_next = jnp.concatenate([normed[:, -1:], east], axis=1)
+    sm_next = smooth_batched(pad_rows(wide_next, rims_next, 0, RADIUS + 2), met_next[:, :, :RADIUS])
+    field_wide = jnp.concatenate([sm_prev, sm_me, sm_next], axis=1)
+
     seam_rows = seam_table[0]
-    widened = padded_2(normed[None], (("blk", 2),), margin)
-    received = pick_rims(
-        seam_rows, lax.all_gather(edge_rows(widened, 1), "blk", axis=0, tiled=True)
-    )
-    padded = place_rims(widened[0], received, seam_rows)
-    smoothed = smooth(padded, metric[0])
-    query = project(smoothed, w_query)
-    field_wide = padded_2(smoothed[None], (("blk", 2),), RADIUS)
-    field_got = pick_rims(
-        seam_rows, lax.all_gather(edge_rows(field_wide, RADIUS), "blk", axis=0, tiled=True)
-    )
-    field_pad = place_rims(field_wide[0], field_got, seam_rows)
+    field_got = pick_all(seam_rows, edges3)
+    field_pad = place_rims(field_wide, field_got, seam_rows)
+    query = project(sm_me, w_query)
     key_pad = project(field_pad, w_key)
     value_pad = project(field_pad, w_value)
     return attend_and_mix(query, key_pad, value_pad, own_tile, w_output)[None]

time: 141 us -> 143 us (1.014)
  waiting for transfers between devices: 40.9 us -> 0.04 us
  blocking collectives: 20.3 us -> 40 us
  local copies, waits for them, and re-layouts: 5.59 us -> 22.6 us
  other arithmetic: 10.7 us -> 22.3 us
  starting transfers between devices: 10.1 us -> 5.56 us
  matrix products: 5.02 us -> 2.71 us
    all_gather x1, waiting for transfers between devices: 38.2 us -> 0.02 us  [local(): bands = lax.all_gather(band[None], 'blk', axis=0, tiled=True)]
    all_gather x1 -> x2, blocking collectives: 20.3 us -> 40 us  [the longest x1 22.3 us: local(): metric_all = lax.all_gather(metric, 'blk', axis=0, tiled=True)]
    mul x10 -> x48, local copies, waits for them, and re-layouts: 1.51 us -> 14.4 us  [smooth_batched(): metric[..., stencil, :, :, None]]
    convert_element_type x0 -> x6, other arithmetic: none -> 5.6 us  [the longest x5 4.1 us: smooth_batched(): return total.astype(jnp.bfloat16)]
    ppermute x4 -> x2, starting transfers between devices: 10.1 us -> 5.56 us  [the longest x1 5.06 us: local(): east_cols = lax.ppermute(own_tile[:, :side], 'blk', down)]
    slice x2 -> x20, local copies, waits for them, and re-layouts: 0.18 us -> 3.62 us  [the longest x1 1.14 us: local(): west_cols = lax.ppermute(own_tile[:, cols - side:], 'blk', up)]
    ppermute x4 -> x2, waiting for transfers between devices: 2.65 us -> 0.01 us  [the longest x1 0.01 us: local(): west_cols = lax.ppermute(own_tile[:, cols - side:], 'blk', up)]
    concatenate x1 -> x8, other arithmetic: 0.3 us -> 2.57 us  [the longest x2 0.94 us: pad_rows(): return jnp.concatenate([rims[0:1, lo:hi], body, rims[1:2, lo:hi]], axis=0)]
  transfers between devices with their start and end apart: 5 -> 3, of which waited for: 2 -> 0; matrix products, arithmetic and copies ran while one was open for 4% -> 16% of each run, Pallas kernels for 0% -> 0%
where the time goes in v2:
time: 143 us; the launch traced here: 142 us
  blocking collectives  40 us (28%)
  Pallas kernels  34.6 us (24%)
  local copies, waits for them, and re-layouts  22.6 us (16%)
  other arithmetic  22.3 us (16%)
  between operations  14.2 us (10%)
  starting transfers between devices  5.56 us (4%)
  matrix products  2.71 us (2%)
    pallas_call x1, Pallas kernels, attend_and_mix(): pl.pallas_call(attention_kernel, out_shape=jax.ShapeDtypeStruct((cells, c...  34.6 us
    all_gather x1, blocking collectives, local(): metric_all = lax.all_gather(metric, 'blk', axis=0, tiled=True)  22.3 us
    all_gather x1, blocking collectives, local(): table_all = lax.all_gather(seam_table, 'blk', axis=0, tiled=True)  17.7 us
    mul x48, local copies, waits for them, and re-layouts, smooth_batched(): metric[..., stencil, :, :, None]  14.4 us
    convert_element_type x2, other arithmetic, column_shifts(): jnp.stack([padded[:, b:b + cols] for b in range(span)]).astype(jnp.float32)  5.32 us
    ppermute x1, starting transfers between devices, local(): east_cols = lax.ppermute(own_tile[:, :side], 'blk', down)  5.06 us
    convert_element_type x5, other arithmetic, smooth_batched(): return total.astype(jnp.bfloat16)  4.1 us
    reduce_sum x4, other arithmetic, normalize(): jnp.mean(values * values, axis=-1, keepdims=True) + 1e-05  2.88 us
  transfers between devices with their start and end apart: 3, of which 0 were waited for; matrix products, arithmetic and copies ran while one was open for 16% of the time, Pallas kernels for 0%

profile of v2, /device:TPU:0, one launch (start us, length us, event | category | flops | bytes accessed | tf_op | source)
XLA Modules:
  0.0 142.0 jit_solution(13325973482641902626)
XLA Ops:
  6.5 0.9 slice_bitcast_fusion.35
  7.4 0.6 pad_maximum_fusion.20
  8.1 1.1 fusion.94
  9.2 0.5 collective-permute-start
  9.7 5.1 %collective-permute-start.1 = (bf16[32,4,512]{2,1,0:T(4,128)(2,1)S(1)}, bf16[32,4,512]{2,1,0:T(4,128)(2,1)S(1)}, u32[]{:S(2)}, u32[]{:S(2)}) collective-permute-start(bf16[32,4,512]{2,1,0:T(4,128)(2,1)S(1)} %get-tuple-element.49), channel_id=1, source_target_pairs={{1,0},{2,1},{3,2},{4,3},{5,4},{6,5},{7,6},{8,7},{9,8},{10,9},{11,1... | collective-permute-start | bytes 393224 | tf_op jit(solution)/shard_map/ppermute | solution.py:206
  14.8 1.1 fusion.21
  15.8 0.8 slice_bitcast_fusion.44
  16.7 22.3 %all_gather.11 = f32[16,9,32,8]{2,3,1,0:T(8,128)S(1)} all-gather(f32[1,9,32,8]{2,3,1,0:T(8,128)} %param.10), channel_id=1, replica_groups=mesh['group'=2,'blk'=16] {'blk'}, dimensions={0}, use_global_device_ids=true | all-gather | bytes 156672 | tf_op jit(solution)/shard_map/all_gather | solution.py:203
  38.9 17.7 %all_gather.9 = s32[16,2,3]{2,1,0:T(2,128)S(1)} all-gather(s32[1,2,3]{2,1,0:T(2,128)} %param.15), channel_id=1, replica_groups=mesh['group'=2,'blk'=16] {'blk'}, dimensions={0}, use_global_device_ids=true | all-gather | bytes 408 | tf_op jit(solution)/shard_map/all_gather | solution.py:204
  56.6 1.0 slice_reduce_fusion.2
  57.6 0.6 fusion.87
  58.4 0.5 fusion.85
  59.0 0.6 iota_compare_fusion.3
  59.7 0.7 iota_compare_fusion.2
  60.4 0.6 slice_bitcast_fusion.53
  61.0 0.5 iota_compare_fusion.4
  62.0 0.6 iota_compare_fusion.5
  63.9 0.7 copy.219
  64.6 0.7 copy.218
  65.6 0.8 copy.210
  66.3 1.3 copy.211
  67.6 1.3 copy.212
  69.0 1.4 copy.214
  70.3 1.4 copy.215
  71.7 1.3 copy.205
  76.1 1.5 %multiply_reduce_fusion = f32[16,8,8]{2,1,0:T(8,128)S(1)} fusion(bf16[16,8,8,512]{3,2,1,0:T(8,128)(2,1)} %bitcast.219), kind=kLoop, calls=%fused_computation.3 | loop fusion | flops 1571840 | bytes 1052672 | tf_op jit(solution)/shard_map/reduce_sum | solution.py:27
  77.8 1.5 %bitcast_convert_fusion = f32[16,8,8,512]{3,2,1,0:T(8,128)S(1)} fusion(bf16[128,8,512]{2,1,0:T(8,128)(2,1)} %all-gather.3.cloned.1.call-done), kind=kLoop, calls=%fused_computation.243 | loop fusion | flops 524288 | bytes 3145728 | tf_op jit(solution)/shard_map/convert_element_type | solution.py:26
  79.3 1.2 fusion.1
  80.8 0.5 fusion.91
  81.4 0.6 copy-done.13
  82.0 0.4 fusion.6
  83.4 1.1 add_convert_fusion
  84.5 0.9 add_convert_fusion.1
  85.6 0.5 fusion.2
  86.3 0.5 copy-done.18
  86.8 0.4 fusion.10
  87.8 0.5 maximum_maximum_fusion
  88.3 0.8 add_convert_fusion.2
  89.1 1.0 convolution_convert_fusion.2.q_ref
  90.2 0.4 maximum_maximum_fusion.1
  90.6 0.7 add_convert_fusion.3
  91.4 0.7 add_convert_fusion.4
  92.1 0.3 pad_maximum_fusion.6
  92.6 0.4 convolution_convert_fusion
  93.1 0.4 convolution_convert_fusion.1
  94.5 2.7 %convert_element_type.262.v_ref = f32[7,38,8,512]{3,2,1,0:T(8,128)} convert(bf16[7,38,8,512]{3,2,1,0:T(8,128)(2,1)S(1)} %fusion.53) | non-fusion elementwise | flops 1089536 | bytes 6537216 | tf_op jit(solution)/shard_map/convert_element_type | solution.py:139
  97.9 2.6 %convert_element_type.260.k_ref = f32[7,38,8,512]{3,2,1,0:T(8,128)} convert(bf16[7,38,8,512]{3,2,1,0:T(8,128)(2,1)S(1)} %fusion.60) | non-fusion elementwise | flops 1089536 | bytes 6537216 | tf_op jit(solution)/shard_map/convert_element_type | solution.py:139
  100.5 34.6 %shard_map.82 = bf16[256,512]{1,0:T(8,128)(2,1)} custom-call(bf16[256,512]{1,0:T(8,128)(2,1)} %convolution_convert_fusion.2.q_ref, f32[7,38,8,512]{3,2,1,0:T(8,128)} %convert_element_type.260.k_ref, f32[7,38,8,512]{3,2,1,0:T(8,128)} %convert_element_type.262.v_ref, bf16[256,512]{1,0:T(8,128)(2,1)} %bitcast.218, bf16[512,512]{1,0:T(8,128)(2,1)} %wo_ref.1), custom_call_target="tpu_custom_call" | custom-call | tf_op jit(solution)/shard_map/pallas_call | solution.py:147
  (140 shorter events, 9.5 us)
Async XLA Ops:
  6.5 86.0 %copy-start = (bf16[512,512]{1,0:T(8,128)(2,1)S(1)}, bf16[512,512]{1,0:T(8,128)(2,1)}, u32[]{:S(2)}) copy-start(bf16[512,512]{1,0:T(8,128)(2,1)} %param.13) | copy-start | bytes 1572868
  6.5 55.0 %copy-start.1 = (bf16[1,32,8,512]{3,2,1,0:T(8,128)(2,1)S(1)}, bf16[1,32,8,512]{3,2,1,0:T(8,128)(2,1)}, u32[]{:S(2)}) copy-start(bf16[1,32,8,512]{3,2,1,0:T(8,128)(2,1)} %param.8) | copy-start | bytes 786436
  6.5 55.0 %copy-start.11 = (f32[512]{0:T(512)S(1)}, f32[512]{0:T(512)}, u32[]{:S(2)}) copy-start(f32[512]{0:T(512)} %param.9) | copy-start | bytes 6148
  6.5 69.6 %all-gather.3.cloned.1.call-start = ((), (), s32[]{:S(2)}) async-start(), calls=%async_computation | async-start | bytes 1114112 | tf_op jit(solution)/shard_map/all_gather | solution.py:202
  9.2 66.2 %collective-permute-start = (bf16[32,4,512]{2,1,0:T(4,128)(2,1)S(1)}, bf16[32,4,512]{2,1,0:T(4,128)(2,1)S(1)}, u32[]{:S(2)}, u32[]{:S(2)}) collective-permute-start(bf16[32,4,512]{2,1,0:T(4,128)(2,1)S(1)} %get-tuple-element.48), channel_id=1, source_target_pairs={{0,1},{1,2},{2,3},{3,4},{4,5},{5,6},{6,7},{7,8},{8,9},{9,10},{10,1... | collective-permute-start | bytes 393224 | tf_op jit(solution)/shard_map/ppermute | solution.py:205
  9.7 65.9 %collective-permute-start.1 = (bf16[32,4,512]{2,1,0:T(4,128)(2,1)S(1)}, bf16[32,4,512]{2,1,0:T(4,128)(2,1)S(1)}, u32[]{:S(2)}, u32[]{:S(2)}) collective-permute-start(bf16[32,4,512]{2,1,0:T(4,128)(2,1)S(1)} %get-tuple-element.49), channel_id=1, source_target_pairs={{1,0},{2,1},{3,2},{4,3},{5,4},{6,5},{7,6},{8,7},{9,8},{10,9},{11,1... | collective-permute-start | bytes 393224 | tf_op jit(solution)/shard_map/ppermute | solution.py:206
  62.0 13.8 %copy-start.12 = (f32[512]{0:T(512)S(1)}, f32[512]{0:T(512)}, u32[]{:S(2)}) copy-start(f32[512]{0:T(512)} %param.9) | copy-start | bytes 6148
  81.3 0.7 copy-start.13
  81.3 0.7 copy-start.14
  82.0 0.6 copy-start.17
  86.1 0.6 copy-start.18
  86.1 0.6 copy-start.19
  86.3 0.9 copy-start.16
  86.3 1.1 copy-start.15
  87.7 1.4 copy-start.3
  88.3 2.3 %copy-start.4 = (f32[32,3]{1,0:T(8,128)S(1)}, f32[32,3]{1,0:T(8,128)}, u32[]{:S(2)}) copy-start(f32[32,3]{1,0:T(8,128)} %copy.219) | copy-start | bytes 1156
  88.3 2.3 %copy-start.6 = (f32[32,3]{1,0:T(8,128)S(1)}, f32[32,3]{1,0:T(8,128)}, u32[]{:S(2)}) copy-start(f32[32,3]{1,0:T(8,128)} %copy.218) | copy-start | bytes 1156
  89.1 2.2 %copy-start.5 = (f32[32,3]{1,0:T(8,128)S(1)}, f32[32,3]{1,0:T(8,128)}, u32[]{:S(2)}) copy-start(f32[32,3]{1,0:T(8,128)} %copy.211) | copy-start | bytes 1156
  89.1 2.2 %copy-start.7 = (f32[32,3]{1,0:T(8,128)S(1)}, f32[32,3]{1,0:T(8,128)}, u32[]{:S(2)}) copy-start(f32[32,3]{1,0:T(8,128)} %copy.212) | copy-start | bytes 1156
  89.1 2.2 %copy-start.8 = (f32[32,3]{1,0:T(8,128)S(1)}, f32[32,3]{1,0:T(8,128)}, u32[]{:S(2)}) copy-start(f32[32,3]{1,0:T(8,128)} %copy.214) | copy-start | bytes 1156
  89.1 2.2 %copy-start.9 = (f32[32,3]{1,0:T(8,128)S(1)}, f32[32,3]{1,0:T(8,128)}, u32[]{:S(2)}) copy-start(f32[32,3]{1,0:T(8,128)} %copy.215) | copy-start | bytes 1156
  89.1 2.2 %copy-start.10 = (f32[32,3]{1,0:T(8,128)S(1)}, f32[32,3]{1,0:T(8,128)}, u32[]{:S(2)}) copy-start(f32[32,3]{1,0:T(8,128)} %copy.205) | copy-start | bytes 1156
  92.1 1.0 copy-start.2
Sparse Core Ops, SparseCore 0:
  9.5 41.0 all-gather.2

commit v3 on v2

--- a/solution.py
+++ b/solution.py
@@ -190,6 +190,31 @@
     return got.astype(edges.dtype)
 
 
+def split_exact(values):
+    hi = values.astype(jnp.bfloat16)
+    rest = values - hi.astype(jnp.float32)
+    mid = rest.astype(jnp.bfloat16)
+    lo = (rest - mid.astype(jnp.float32)).astype(jnp.bfloat16)
+    return jnp.stack([hi, mid, lo])
+
+
+def gather_parts(band, metric, table, width):
+    pieces = [band.reshape(-1), split_exact(metric).reshape(-1), table.astype(jnp.bfloat16).reshape(-1)]
+    sizes = [p.size for p in pieces]
+    flat = jnp.concatenate(pieces)
+    total = -(-flat.size // width) * width
+    flat = jnp.pad(flat, (0, total - flat.size)).reshape(1, total // width, width)
+    got = lax.all_gather(flat, "blk", axis=0, tiled=True)
+    count = got.shape[0]
+    got = got.reshape(count, total)
+    bands = got[:, : sizes[0]].reshape((count,) + band.shape)
+    parts = got[:, sizes[0] : sizes[0] + sizes[1]].reshape((count, 3) + metric.shape)
+    parts = parts.astype(jnp.float32)
+    metric_all = parts[:, 0] + (parts[:, 1] + parts[:, 2])
+    table_all = got[:, sizes[0] + sizes[1] : sum(sizes)].reshape((count,) + table.shape)
+    return bands, metric_all, table_all.astype(jnp.int32)
+
+
 def local(latents, norm_gain, metric, w_query, w_key, w_value, w_output, seam_table):
     own_tile = latents[0]
     rows, cols, channels = own_tile.shape
@@ -199,9 +224,7 @@
     down = [(j, i) for i, j in up]
     side = RADIUS + 1
     band = jnp.concatenate([own_tile[:side], own_tile[rows - side :]], axis=0)
-    bands = lax.all_gather(band[None], "blk", axis=0, tiled=True)
-    metric_all = lax.all_gather(metric, "blk", axis=0, tiled=True)
-    table_all = lax.all_gather(seam_table, "blk", axis=0, tiled=True)
+    bands, metric_all, table_all = gather_parts(band, metric[0], seam_table[0], channels)
     west_cols = lax.ppermute(own_tile[:, cols - side :], "blk", up)
     east_cols = lax.ppermute(own_tile[:, :side], "blk", down)
 

time: 143 us -> 177 us (1.24)
  local copies, waits for them, and re-layouts: 22.6 us -> 66.6 us
  blocking collectives: 40 us -> 0 us
  waiting for transfers between devices: 0.04 us -> 25.7 us
  other arithmetic: 22.3 us -> 26 us
    all_gather x2 -> x0, blocking collectives: 40 us -> none  [the longest x1 22.3 us: local(): metric_all = lax.all_gather(metric, 'blk', axis=0, tiled=True)]
    all_gather x1, waiting for transfers between devices: 0.02 us -> 25.7 us  [gather_parts(): got = lax.all_gather(flat, 'blk', axis=0, tiled=True)]
    mul x48 -> x49, local copies, waits for them, and re-layouts: 14.4 us -> 37.6 us  [smooth_batched(): metric[..., stencil, :, :, None]]
    dynamic_slice x0 -> x3, local copies, waits for them, and re-layouts: none -> 5.65 us  [the longest x2 4.55 us: local(): met_prev = lax.dynamic_index_in_dim(metric_all, prev, 0, keepdims=False)]
    unnamed x56 -> x142, local copies, waits for them, and re-layouts: 2.48 us -> 7.3 us
    add x0 -> x2, other arithmetic: none -> 3.54 us  [gather_parts(): metric_all = parts[:, 0] + (parts[:, 1] + parts[:, 2])]
    slice x7, local copies, waits for them, and re-layouts: 0.11 us -> 3.39 us  [pad_rows(): return jnp.concatenate([rims[0:1, lo:hi], body, rims[1:2, lo:hi]], axis=0)]
    convert_element_type x0 -> x3, local copies, waits for them, and re-layouts: none -> 2.46 us  [the longest x1 2.36 us: gather_parts(): parts = parts.astype(jnp.float32)]
  transfers between devices with their start and end apart: 3 -> 3, of which waited for: 0 -> 1; matrix products, arithmetic and copies ran while one was open for 16% -> 6% of each run, Pallas kernels for 0% -> 0%
where the time goes in v3:
time: 177 us; the launch traced here: 176 us
  local copies, waits for them, and re-layouts  66.6 us (38%)
  Pallas kernels  34.6 us (20%)
  other arithmetic  26 us (15%)
  waiting for transfers between devices  25.7 us (15%)
  between operations  14.6 us (8%)
  starting transfers between devices  5.6 us (3%)
  matrix products  2.68 us (2%)
    mul x49, local copies, waits for them, and re-layouts, smooth_batched(): metric[..., stencil, :, :, None]  37.6 us
    pallas_call x1, Pallas kernels, attend_and_mix(): pl.pallas_call(attention_kernel, out_shape=jax.ShapeDtypeStruct((cells, c...  34.6 us
    all_gather x1, waiting for transfers between devices, gather_parts(): got = lax.all_gather(flat, 'blk', axis=0, tiled=True)  25.7 us
    unnamed x142, local copies, waits for them, and re-layouts  7.3 us
    convert_element_type x2, other arithmetic, column_shifts(): jnp.stack([padded[:, b:b + cols] for b in range(span)]).astype(jnp.float32)  5.34 us
    convert_element_type x5, other arithmetic, smooth_batched(): return total.astype(jnp.bfloat16)  5.09 us
    ppermute x1, starting transfers between devices, local(): east_cols = lax.ppermute(own_tile[:, :side], 'blk', down)  5.06 us
    dynamic_slice x2, local copies, waits for them, and re-layouts, local(): met_prev = lax.dynamic_index_in_dim(metric_all, prev, 0, keepdims=False)  4.55 us
  transfers between devices with their start and end apart: 3, of which 1 were waited for; matrix products, arithmetic and copies ran while one was open for 6% of the time, Pallas kernels for 0%

profile of v3, /device:TPU:0, one launch (start us, length us, event | category | flops | bytes accessed | tf_op | source)
XLA Modules:
  0.0 175.8 jit_solution(6086189215385271580)
XLA Ops:
  6.6 0.8 convert_element_type.251
  7.4 0.9 fusion.103
  8.3 0.8 slice_bitcast_fusion.17
  9.6 0.7 reshape.271
  10.9 5.1 %collective-permute-start.1 = (bf16[32,4,512]{2,1,0:T(4,128)(2,1)S(1)}, bf16[32,4,512]{2,1,0:T(4,128)(2,1)S(1)}, u32[]{:S(2)}, u32[]{:S(2)}) collective-permute-start(bf16[32,4,512]{2,1,0:T(4,128)(2,1)S(1)} %get-tuple-element.49), channel_id=1, source_target_pairs={{1,0},{2,1},{3,2},{4,3},{5,4},{6,5},{7,6},{8,7},{9,8},{10,9},{11,1... | collective-permute-start | bytes 393224 | tf_op jit(solution)/shard_map/ppermute | solution.py:229
  17.5 0.7 fusion.100
  19.0 0.7 copy.222
  24.9 0.7 slice.734
  26.3 25.7 %all-gather.2.cloned.1.call-done = bf16[16,78,512]{2,1,0:T(8,128)(2,1)} async-done(((bf16[1,78,512]{2,1,0:T(8,128)(2,1)}), bf16[16,78,512]{2,1,0:T(8,128)(2,1)}) %all-gather.2.cloned.1.call-update) | async-done | bytes 1277968 | tf_op jit(solution)/shard_map/all_gather | solution.py:207
  51.9 2.0 %copy.282 = bf16[2,8,78,512]{3,1,2,0:T(8,128)(2,1)S(1)} copy(bf16[2,8,78,512]{3,2,1,0:T(8,128)(2,1)} %bitcast.234) | data formatting | bytes 2555904
  54.2 1.2 copy.283
  55.4 1.3 copy-done.2
  57.0 2.8 %fusion.1 = bf16[16,8,8,512]{3,0,1,2:T(8,128)(2,1)S(1)} fusion(f32[16,8,8,512]{3,2,1,0:T(8,128)} %bitcast.227, f32[512]{0:T(512)S(1)} %copy-done.55, f32[16,8,8]{0,1,2:T(8,128)S(1)} %copy.214), kind=kLoop, calls=%fused_computation.2 | loop fusion | flops 1572864 | bytes 3151872 | tf_op jit(solution)/shard_map/convert_element_type | solution.py:28
  59.8 0.9 fusion.97
  60.8 1.9 %fusion.98 = (bf16[15,8,8,512]{3,0,1,2:T(8,128)(2,1)}, bf16[15,8,8,512]{3,0,1,2:T(8,128)(2,1)}) fusion(bf16[16,8,8,512]{3,0,1,2:T(8,128)(2,1)S(1)} %fusion.1), kind=kLoop, calls=%fused_computation.259 | loop fusion | bytes 3932160 | tf_op jit(solution)/shard_map/jit(_roll_static)/slice | solution.py:179
  62.7 2.4 %copy.225 = f32[16,6912]{0,1:T(8,128)} copy(f32[16,6912]{1,0:T(8,128)S(1)} %slice_convert_fusion.1) | data formatting | bytes 884736 | tf_op jit(solution)/shard_map/convert_element_type | solution.py:212
  65.0 3.4 %fusion.112 = f32[16,9,32,8]{0,3,2,1:T(8,128)} fusion(f32[16,3,9,32,8]{0,4,3,2,1:T(8,128)} %bitcast.224), kind=kLoop, calls=%fused_computation.268 | loop fusion | flops 73728 | bytes 589824 | tf_op jit(solution)/shard_map/add | solution.py:213
  68.8 1.0 pad_maximum_fusion.19
  70.0 0.8 pad_maximum_fusion.18
  71.5 0.8 fusion.99
  74.9 1.2 fusion.96
  76.1 0.9 slice_bitcast_fusion.26
  87.9 2.1 %constant_dynamic-slice_fusion.4 = (f32[1,1,9,32,8]{0,4,3,2,1:T(8,128)}, f32[1,1,9,32,8]{0,4,3,2,1:T(8,128)}) fusion(f32[16,1,9,32,8]{0,4,3,2,1:T(8,128)S(1)} %fusion.7, s32[]{:T(128)S(6)} %select_n.72, s32[]{:T(128)S(6)} %select_n.74), kind=kLoop, calls=%fused_computation.242 | loop fusion | bytes 36872 | tf_op jit(solution)/shard_map/jit(dynamic_index_in_dim)/dynamic_slice | solution.py:252
  90.0 2.5 %copy.245 = f32[1,1,9,32,8]{3,4,2,1,0:T(8,128)} copy(f32[1,1,9,32,8]{0,4,3,2,1:T(8,128)} %get-tuple-element.12) | data formatting | bytes 18432 | tf_op jit(solution)/shard_map/jit(dynamic_index_in_dim)/dynamic_slice | solution.py:252
  92.4 1.3 slice_bitcast_fusion.62
  93.8 1.3 copy.246
  95.1 1.3 copy.256
  96.5 1.3 copy.255
  97.8 1.3 copy.253
  99.1 1.4 copy.252
  100.5 1.4 copy.251
  101.9 1.4 copy.250
  103.2 1.4 copy.249
  104.6 1.3 copy.248
  105.9 1.1 copy.257
  107.0 0.7 slice_bitcast_fusion.53
  107.8 0.7 copy.258
  109.8 0.7 copy.265
  113.2 0.7 copy.260
  114.0 2.1 %add_convert_fusion = bf16[16,3,8,512]{3,0,1,2:T(8,128)(2,1)S(1)} fusion(bf16[16,4,10,512]{3,0,1,2:T(8,128)(2,1)} %get-tuple-element.10, bf16[16,8,8,512]{3,0,1,2:T(8,128)(2,1)S(1)} %fusion.1, bf16[16,1,10,512]{3,0,1,2:T(8,128)(2,1)} %get-tuple-element.42, bf16[16,8,1,512]{3,0,1,2:T(8,128)(2,1)S(1)} %pad_maximum_fusion.18, ...), kind=kLoop, calls=%fused_computation.50 | loop fusion | flops 6684672 | bytes 3323392 | tf_op jit(solution)/shard_map/convert_element_type | solution.py:175
  116.2 0.9 add_convert_fusion.1
  119.8 1.0 constant_dynamic-slice_fusion
  121.5 0.8 add_convert_fusion.2
  122.4 1.0 convolution_convert_fusion.2.q_ref
  124.1 0.7 add_convert_fusion.4
  128.4 2.7 %convert_element_type.322.v_ref = f32[7,38,8,512]{3,2,1,0:T(8,128)} convert(bf16[7,38,8,512]{3,2,1,0:T(8,128)(2,1)S(1)} %fusion.54) | non-fusion elementwise | flops 1089536 | bytes 6537216 | tf_op jit(solution)/shard_map/convert_element_type | solution.py:139
  131.7 2.7 %convert_element_type.320.k_ref = f32[7,38,8,512]{3,2,1,0:T(8,128)} convert(bf16[7,38,8,512]{3,2,1,0:T(8,128)(2,1)S(1)} %fusion.61) | non-fusion elementwise | flops 1089536 | bytes 6537216 | tf_op jit(solution)/shard_map/convert_element_type | solution.py:139
  134.4 34.6 %shard_map.82 = bf16[256,512]{1,0:T(8,128)(2,1)} custom-call(bf16[256,512]{1,0:T(8,128)(2,1)} %convolution_convert_fusion.2.q_ref, f32[7,38,8,512]{3,2,1,0:T(8,128)} %convert_element_type.320.k_ref, f32[7,38,8,512]{3,2,1,0:T(8,128)} %convert_element_type.322.v_ref, bf16[256,512]{1,0:T(8,128)(2,1)} %bitcast.232, bf16[512,512]{1,0:T(8,128)(2,1)} %wo_ref.1), custom_call_target="tpu_custom_call" | custom-call | tf_op jit(solution)/shard_map/pallas_call | solution.py:147
  (239 shorter events, 36.4 us)
Async XLA Ops:
  6.5 119.6 %copy-start = (bf16[512,512]{1,0:T(8,128)(2,1)S(1)}, bf16[512,512]{1,0:T(8,128)(2,1)}, u32[]{:S(2)}) copy-start(bf16[512,512]{1,0:T(8,128)(2,1)} %param.13) | copy-start | bytes 1572868
  6.5 9.4 %copy-start.56 = (s32[1,2,3]{2,1,0:T(2,128)S(1)}, s32[1,2,3]{2,1,0:T(2,128)}, u32[]{:S(2)}) copy-start(s32[1,2,3]{2,1,0:T(2,128)} %param.15) | copy-start | bytes 76
  6.5 10.8 %copy-start.15 = (f32[1,9,32,8]{2,3,1,0:T(8,128)S(1)}, f32[1,9,32,8]{2,3,1,0:T(8,128)}, u32[]{:S(2)}) copy-start(f32[1,9,32,8]{2,3,1,0:T(8,128)} %param.10) | copy-start | bytes 27652
  6.5 3.7 %copy-start.3 = (bf16[1,32,8,512]{3,2,1,0:T(8,128)(2,1)S(1)}, bf16[1,32,8,512]{3,2,1,0:T(8,128)(2,1)}, u32[]{:S(2)}) copy-start(bf16[1,32,8,512]{3,2,1,0:T(8,128)(2,1)} %param.8) | copy-start | bytes 786436
  6.5 10.8 %copy-start.55 = (f32[512]{0:T(512)S(1)}, f32[512]{0:T(512)}, u32[]{:S(2)}) copy-start(f32[512]{0:T(512)} %param.9) | copy-start | bytes 6148
  6.5 45.4 %all-gather.2.cloned.1.call-start = ((), (), s32[]{:S(2)}) async-start(), calls=%async_computation | async-start | bytes 1392640 | tf_op jit(solution)/shard_map/all_gather | solution.py:207
  10.4 14.0 %collective-permute-start = (bf16[32,4,512]{2,1,0:T(4,128)(2,1)S(1)}, bf16[32,4,512]{2,1,0:T(4,128)(2,1)S(1)}, u32[]{:S(2)}, u32[]{:S(2)}) collective-permute-start(bf16[32,4,512]{2,1,0:T(4,128)(2,1)S(1)} %get-tuple-element.48), channel_id=1, source_target_pairs={{0,1},{1,2},{2,3},{3,4},{4,5},{5,6},{6,7},{7,8},{8,9},{9,10},{10,1... | collective-permute-start | bytes 393224 | tf_op jit(solution)/shard_map/ppermute | solution.py:228
  10.9 13.6 %collective-permute-start.1 = (bf16[32,4,512]{2,1,0:T(4,128)(2,1)S(1)}, bf16[32,4,512]{2,1,0:T(4,128)(2,1)S(1)}, u32[]{:S(2)}, u32[]{:S(2)}) collective-permute-start(bf16[32,4,512]{2,1,0:T(4,128)(2,1)S(1)} %get-tuple-element.49), channel_id=1, source_target_pairs={{1,0},{2,1},{3,2},{4,3},{5,4},{6,5},{7,6},{8,7},{9,8},{10,9},{11,1... | collective-permute-start | bytes 393224 | tf_op jit(solution)/shard_map/ppermute | solution.py:229
  55.4 1.3 copy-start.2
  65.0 3.4 %copy-start.1 = (f32[16,6912]{0,1:T(8,128)S(1)}, f32[16,6912]{0,1:T(8,128)}, u32[]{:S(2)}) copy-start(f32[16,6912]{0,1:T(8,128)} %copy.225) | copy-start | bytes 1327108
  90.0 15.9 %copy-start.4 = (f32[1,1,9,32,8]{0,4,3,2,1:T(8,128)S(1)}, f32[1,1,9,32,8]{0,4,3,2,1:T(8,128)}, u32[]{:S(2)}) copy-start(f32[1,1,9,32,8]{0,4,3,2,1:T(8,128)} %get-tuple-element.13) | copy-start | bytes 27652
  113.9 2.2 %copy-start.6 = (bf16[16,4,10,512]{3,0,1,2:T(8,128)(2,1)S(1)}, bf16[16,4,10,512]{3,0,1,2:T(8,128)(2,1)}, u32[]{:S(2)}) copy-start(bf16[16,4,10,512]{3,0,1,2:T(8,128)(2,1)} %get-tuple-element.11) | copy-start | bytes 1966084
  113.9 2.2 %copy-start.8 = (bf16[16,1,10,512]{3,0,1,2:T(8,128)(2,1)S(1)}, bf16[16,1,10,512]{3,0,1,2:T(8,128)(2,1)}, u32[]{:S(2)}) copy-start(bf16[16,1,10,512]{3,0,1,2:T(8,128)(2,1)} %get-tuple-element.43) | copy-start | bytes 491524
  113.9 2.2 %copy-start.24 = (f32[16,3,8]{0,1,2:T(4,128)S(1)}, f32[16,3,8]{0,1,2:T(4,128)}, u32[]{:S(2)}) copy-start(f32[16,3,8]{0,1,2:T(4,128)} %copy.234) | copy-start | bytes 4612
  113.9 2.2 %copy-start.25 = (f32[16,3,8]{0,1,2:T(4,128)S(1)}, f32[16,3,8]{0,1,2:T(4,128)}, u32[]{:S(2)}) copy-start(f32[16,3,8]{0,1,2:T(4,128)} %copy.233) | copy-start | bytes 4612
  113.9 2.2 %copy-start.26 = (f32[16,3,8]{0,1,2:T(4,128)S(1)}, f32[16,3,8]{0,1,2:T(4,128)}, u32[]{:S(2)}) copy-start(f32[16,3,8]{0,1,2:T(4,128)} %copy.232) | copy-start | bytes 4612
  113.9 2.2 %copy-start.27 = (f32[16,3,8]{0,1,2:T(4,128)S(1)}, f32[16,3,8]{0,1,2:T(4,128)}, u32[]{:S(2)}) copy-start(f32[16,3,8]{0,1,2:T(4,128)} %copy.231) | copy-start | bytes 4612
  114.0 2.2 %copy-start.28 = (f32[16,3,8]{0,1,2:T(4,128)S(1)}, f32[16,3,8]{0,1,2:T(4,128)}, u32[]{:S(2)}) copy-start(f32[16,3,8]{0,1,2:T(4,128)} %copy.230) | copy-start | bytes 4612
  114.0 2.2 %copy-start.29 = (f32[16,3,8]{0,1,2:T(4,128)S(1)}, f32[16,3,8]{0,1,2:T(4,128)}, u32[]{:S(2)}) copy-start(f32[16,3,8]{0,1,2:T(4,128)} %copy.229) | copy-start | bytes 4612
  114.0 2.2 %copy-start.30 = (f32[16,3,8]{0,1,2:T(4,128)S(1)}, f32[16,3,8]{0,1,2:T(4,128)}, u32[]{:S(2)}) copy-start(f32[16,3,8]{0,1,2:T(4,128)} %copy.228) | copy-start | bytes 4612
  114.0 2.2 %copy-start.31 = (f32[16,3,8]{0,1,2:T(4,128)S(1)}, f32[16,3,8]{0,1,2:T(4,128)}, u32[]{:S(2)}) copy-start(f32[16,3,8]{0,1,2:T(4,128)} %copy.227) | copy-start | bytes 4612
  114.0 2.2 %copy-start.32 = (f32[16,3,8]{0,1,2:T(4,128)S(1)}, f32[16,3,8]{0,1,2:T(4,128)}, u32[]{:S(2)}) copy-start(f32[16,3,8]{0,1,2:T(4,128)} %copy.226) | copy-start | bytes 4612
  118.7 2.1 %copy-start.9 = (bf16[32,1,512]{2,1,0:T(2,128)(2,1)S(1)}, bf16[32,1,512]{2,1,0:T(2,128)(2,1)}, u32[]{:S(2)}) copy-start(bf16[32,1,512]{2,1,0:T(2,128)(2,1)} %slice.734) | copy-start | bytes 98308
  118.7 2.1 %copy-start.10 = (bf16[32,1,512]{2,1,0:T(2,128)(2,1)S(1)}, bf16[32,1,512]{2,1,0:T(2,128)(2,1)}, u32[]{:S(2)}) copy-start(bf16[32,1,512]{2,1,0:T(2,128)(2,1)} %slice.736) | copy-start | bytes 98308
  119.1 2.2 %copy-start.16 = (f32[32,8]{1,0:T(8,128)S(1)}, f32[32,8]{1,0:T(8,128)}, u32[]{:S(2)}) copy-start(f32[32,8]{1,0:T(8,128)} %copy.222) | copy-start | bytes 3076
  119.2 2.2 %copy-start.17 = (f32[32,8]{1,0:T(8,128)S(1)}, f32[32,8]{1,0:T(8,128)}, u32[]{:S(2)}) copy-start(f32[32,8]{1,0:T(8,128)} %copy.221) | copy-start | bytes 3076
  119.2 2.2 %copy-start.18 = (f32[32,8]{1,0:T(8,128)S(1)}, f32[32,8]{1,0:T(8,128)}, u32[]{:S(2)}) copy-start(f32[32,8]{1,0:T(8,128)} %copy.220) | copy-start | bytes 3076
  119.2 2.2 %copy-start.19 = (f32[32,8]{1,0:T(8,128)S(1)}, f32[32,8]{1,0:T(8,128)}, u32[]{:S(2)}) copy-start(f32[32,8]{1,0:T(8,128)} %copy.219) | copy-start | bytes 3076
  119.2 2.2 %copy-start.20 = (f32[32,8]{1,0:T(8,128)S(1)}, f32[32,8]{1,0:T(8,128)}, u32[]{:S(2)}) copy-start(f32[32,8]{1,0:T(8,128)} %copy.218) | copy-start | bytes 3076
  119.2 2.2 %copy-start.21 = (f32[32,8]{1,0:T(8,128)S(1)}, f32[32,8]{1,0:T(8,128)}, u32[]{:S(2)}) copy-start(f32[32,8]{1,0:T(8,128)} %copy.217) | copy-start | bytes 3076
  119.2 2.2 %copy-start.22 = (f32[32,8]{1,0:T(8,128)S(1)}, f32[32,8]{1,0:T(8,128)}, u32[]{:S(2)}) copy-start(f32[32,8]{1,0:T(8,128)} %copy.224) | copy-start | bytes 3076
  119.2 2.2 %copy-start.23 = (f32[32,8]{1,0:T(8,128)S(1)}, f32[32,8]{1,0:T(8,128)}, u32[]{:S(2)}) copy-start(f32[32,8]{1,0:T(8,128)} %copy.223) | copy-start | bytes 3076
  121.4 2.0 %copy-start.11 = (bf16[32,1,512]{2,1,0:T(2,128)(2,1)S(1)}, bf16[32,1,512]{2,1,0:T(2,128)(2,1)}, u32[]{:S(2)}) copy-start(bf16[32,1,512]{2,1,0:T(2,128)(2,1)} %get-tuple-element.47) | copy-start | bytes 98308
  121.4 2.0 %copy-start.12 = (bf16[32,1,512]{2,1,0:T(2,128)(2,1)S(1)}, bf16[32,1,512]{2,1,0:T(2,128)(2,1)}, u32[]{:S(2)}) copy-start(bf16[32,1,512]{2,1,0:T(2,128)(2,1)} %get-tuple-element.46) | copy-start | bytes 98308
  121.4 2.0 %copy-start.51 = (bf16[1,5,512]{2,1,0:T(8,128)(2,1)S(1)}, bf16[1,5,512]{2,1,0:T(8,128)(2,1)}, u32[]{:S(2)}) copy-start(bf16[1,5,512]{2,1,0:T(8,128)(2,1)} %copy.247) | copy-start | bytes 15364
  121.4 2.0 %copy-start.52 = (bf16[1,5,512]{2,1,0:T(8,128)(2,1)S(1)}, bf16[1,5,512]{2,1,0:T(8,128)(2,1)}, u32[]{:S(2)}) copy-start(bf16[1,5,512]{2,1,0:T(8,128)(2,1)} %copy.254) | copy-start | bytes 15364
  121.4 2.0 %copy-start.53 = (bf16[1,5,512]{2,1,0:T(8,128)(2,1)S(1)}, bf16[1,5,512]{2,1,0:T(8,128)(2,1)}, u32[]{:S(2)}) copy-start(bf16[1,5,512]{2,1,0:T(8,128)(2,1)} %copy.259) | copy-start | bytes 15364
  121.5 2.0 %copy-start.54 = (bf16[1,5,512]{2,1,0:T(8,128)(2,1)S(1)}, bf16[1,5,512]{2,1,0:T(8,128)(2,1)}, u32[]{:S(2)}) copy-start(bf16[1,5,512]{2,1,0:T(8,128)(2,1)} %copy.266) | copy-start | bytes 15364
  122.4 1.7 copy-start.33
  122.4 1.7 copy-start.34
  122.4 1.7 copy-start.35
  122.4 1.7 copy-start.36
  122.4 1.7 copy-start.37
  122.4 1.7 copy-start.38
  122.4 1.7 copy-start.39
  122.4 1.7 copy-start.40
  122.4 1.7 copy-start.41
  123.5 1.3 copy-start.42
  (16 other events, 17.4 us)
Sparse Core Ops, SparseCore 0:
  10.4 41.5 all-gather.1

commit v4 on v0

--- a/solution.py
+++ b/solution.py
@@ -2,6 +2,8 @@
 import jax.numpy as jnp
 from jax import lax
 from jax.sharding import PartitionSpec as P
+from jax.experimental import pallas as pl
+from jax.experimental.pallas import tpu as pltpu
 
 HEADS = 8
 RADIUS = 3
@@ -77,34 +79,62 @@
     )
 
 
-def window_attention(query, keys, vals):
-    rows, cols, channels = query.shape
+def attention_kernel(q_ref, k_ref, v_ref, lat_ref, wo_ref, out_ref, att_ref):
+    cells, channels = q_ref.shape
+    positions = k_ref.shape[0]
+    rows, cols = lat_ref.shape[0], lat_ref.shape[1]
+    wide = cols + 2 * RADIUS
+    span = 2 * RADIUS + 1
     head_size = channels // HEADS
-    channel_ids = jnp.arange(channels, dtype=jnp.int32) // head_size
-    head_map = (channel_ids[:, None] == channel_ids[None, :]).astype(jnp.float32)
-    query_wide = query.astype(jnp.float32)
-    span = 2 * RADIUS + 1
+    group = 128
     scale = head_size ** (-0.5)
-    scores = []
-    for row_off in range(span):
-        for col_off in range(span):
-            key_part = keys[row_off : row_off + rows, col_off : col_off + cols]
-            products = (query_wide * key_part.astype(jnp.float32)).reshape(rows * cols, channels)
-            scores.append(jnp.dot(products, head_map, precision=lax.Precision.HIGHEST) * scale)
-    stacked = jnp.stack(scores)
-    row_max = jnp.max(stacked, axis=0, keepdims=True)
-    exp_scores = jnp.exp(stacked - row_max)
-    weights = (exp_scores / jnp.sum(exp_scores, axis=0, keepdims=True)).astype(jnp.bfloat16)
-    total = jnp.zeros((rows * cols, channels), jnp.float32)
-    for row_off in range(span):
-        for col_off in range(span):
-            value_part = vals[row_off : row_off + rows, col_off : col_off + cols].reshape(
-                rows * cols, channels
+    cell = lax.broadcasted_iota(jnp.int32, (cells, positions), 0)
+    place = lax.broadcasted_iota(jnp.int32, (cells, positions), 1)
+    row_gap = place // wide - cell // cols
+    col_gap = place % wide - cell % cols
+    valid = (row_gap >= 0) & (row_gap < span) & (col_gap >= 0) & (col_gap < span)
+    lane = lax.broadcasted_iota(jnp.int32, (cells, group), 1) // head_size
+    for g in range(channels // group):
+        lanes = slice(g * group, (g + 1) * group)
+        q_g = q_ref[:, lanes]
+        k_g = k_ref[:, lanes]
+        v_g = v_ref[:, lanes]
+        acc = jnp.zeros((cells, group), jnp.float32)
+        for part in range(group // head_size):
+            q_h = jnp.where(lane == part, q_g, jnp.zeros_like(q_g))
+            s = lax.dot_general(
+                q_h, k_g, (((1,), (1,)), ((), ())), preferred_element_type=jnp.float32
             )
-            total = total + weights[row_off * span + col_off].astype(
-                jnp.float32
-            ) * value_part.astype(jnp.float32)
-    return total.reshape(rows, cols, channels).astype(jnp.bfloat16)
+            s = jnp.where(valid, s * scale, -jnp.inf)
+            top = jnp.max(s, axis=1, keepdims=True)
+            e = jnp.exp(s - top)
+            total = jnp.sum(e, axis=1, keepdims=True)
+            w = (e / total).astype(jnp.bfloat16)
+            o = jnp.dot(w, v_g, preferred_element_type=jnp.float32)
+            acc = jnp.where(lane == part, o, acc)
+        att_ref[:, lanes] = acc.astype(jnp.bfloat16)
+    mixed = jnp.dot(att_ref[...], wo_ref[...], preferred_element_type=jnp.float32)
+    lat = lat_ref[...].reshape(cells, channels)
+    out_ref[...] = (lat.astype(jnp.float32) + mixed).astype(out_ref.dtype)
+
+
+def attend_and_mix(query, field_pad, w_key, w_value, own_tile, w_output):
+    rows, cols, channels = own_tile.shape
+    cells = rows * cols
+    flat = field_pad.reshape(-1, channels)
+    positions = -(-flat.shape[0] // 128) * 128
+    flat = jnp.pad(flat, ((0, positions - flat.shape[0]), (0, 0)))
+    key_flat = project(flat, w_key)
+    value_flat = project(flat, w_value)
+    vmem = pl.BlockSpec(memory_space=pltpu.VMEM)
+    out = pl.pallas_call(
+        attention_kernel,
+        out_shape=jax.ShapeDtypeStruct((cells, channels), own_tile.dtype),
+        in_specs=[vmem] * 5,
+        out_specs=vmem,
+        scratch_shapes=[pltpu.VMEM((cells, channels), jnp.bfloat16)],
+    )(query.reshape(cells, channels), key_flat, value_flat, own_tile, w_output)
+    return out.reshape(rows, cols, channels)
 
 
 def local(latents, norm_gain, metric, w_query, w_key, w_value, w_output, seam_table):
@@ -125,12 +155,7 @@
         seam_rows, lax.all_gather(edge_rows(field_wide, RADIUS), "blk", axis=0, tiled=True)
     )
     field_pad = place_rims(field_wide[0], field_got, seam_rows)
-    key_pad = project(field_pad, w_key)
-    value_pad = project(field_pad, w_value)
-    attended = window_attention(query, key_pad, value_pad)
-    mixed = jnp.dot(attended.reshape(-1, channels), w_output, preferred_element_type=jnp.float32)
-    updated = own_tile.astype(jnp.float32) + mixed.reshape(own_tile.shape)
-    return updated.astype(jnp.bfloat16)[None]
+    return attend_and_mix(query, field_pad, w_key, w_value, own_tile, w_output)[None]
 
 
 def solution(mesh):

time: 238 us -> 107 us (0.45); the launches traced: 234 us -> 107 us
  matrix products: 101 us -> 6.82 us
  other arithmetic: 43.9 us -> 5.39 us
  Pallas kernels: 0 us -> 7 us
  waiting for transfers between devices: 40.3 us -> 44.5 us
  starting transfers between devices: 10.1 us -> 7.35 us
    dot_general x50 -> x0, matrix products: 95.9 us -> none  [the longest x49 87.6 us: window_attention(): jnp.dot(products, head_map, precision=lax.Precision.HIGHEST) * scale]
    convert_element_type x1 -> x0, other arithmetic: 16.4 us -> none  [window_attention(): (exp_scores / jnp.sum(exp_scores, axis=0, keepdims=True)).astype(jnp.bflo...]
    reduce_sum x1 -> x0, other arithmetic: 11.1 us -> none  [window_attention(): jnp.sum(exp_scores, axis=0, keepdims=True)]
    reduce_max x1 -> x0, other arithmetic: 11 us -> none  [window_attention(): row_max = jnp.max(stacked, axis=0, keepdims=True)]
    pallas_call x0 -> x1, Pallas kernels: none -> 7 us  [attend_and_mix(): pl.pallas_call(attention_kernel, out_shape=jax.ShapeDtypeStruct((cells, c...]
    ppermute x2, waiting for transfers between devices: 2.65 us -> 7.54 us  [padded_2(): before = lax.ppermute(last, axis, up)]
    all_gather x1, waiting for transfers between devices: 37.6 us -> 34.4 us  [local(): lax.all_gather(edge_rows(field_wide, RADIUS), 'blk', axis=0, tiled=True)]
    ppermute x2, waiting for transfers between devices: 0.01 us -> 2.52 us  [padded_2(): after = lax.ppermute(first, axis, down)]
  transfers between devices with their start and end apart: 5 -> 5, of which waited for: 2 -> 4; matrix products, arithmetic and copies ran while one was open for 3% -> 5% of each run, Pallas kernels for 0% -> 0%
where the time goes in v4:
time: 107 us
  waiting for transfers between devices  44.5 us (42%)
  blocking collectives  18.2 us (17%)
  between operations  13.6 us (13%)
  starting transfers between devices  7.35 us (7%)
  Pallas kernels  7 us (7%)
  matrix products  6.82 us (6%)
  other arithmetic  5.39 us (5%)
  local copies, waits for them, and re-layouts  3.81 us (4%)
    all_gather x1, waiting for transfers between devices, local(): lax.all_gather(edge_rows(field_wide, RADIUS), 'blk', axis=0, tiled=True)  34.4 us
    all_gather x1, blocking collectives, local(): lax.all_gather(edge_rows(widened, 1), 'blk', axis=0, tiled=True)  18.2 us
    ppermute x2, waiting for transfers between devices, padded_2(): before = lax.ppermute(last, axis, up)  7.54 us
    ppermute x2, starting transfers between devices, padded_2(): after = lax.ppermute(first, axis, down)  7.35 us
    pallas_call x1, Pallas kernels, attend_and_mix(): pl.pallas_call(attention_kernel, out_shape=jax.ShapeDtypeStruct((cells, c...  7 us
    dot_general x3, matrix products, project(): jnp.dot(flat, weight, preferred_element_type=jnp.float32)  4.73 us
    ppermute x2, waiting for transfers between devices, padded_2(): after = lax.ppermute(first, axis, down)  2.52 us
  transfers between devices with their start and end apart: 5, of which 4 were waited for; matrix products, arithmetic and copies ran while one was open for 5% of the time, Pallas kernels for 0%

profile of v4, /device:TPU:0, one launch (start us, length us, event | category | flops | bytes accessed | tf_op | source)
XLA Modules:
  0.0 106.7 jit_solution(10756566923163944971)
XLA Ops:
  6.5 0.0 copy-start
  6.5 1.1 %multiply_reduce_fusion = f32[32,8]{1,0:T(8,128)S(1)} fusion(bf16[1,32,8,512]{3,2,1,0:T(8,128)(2,1)} %param.8), kind=kLoop, calls=%fused_computation.20 | loop fusion | flops 392960 | bytes 263168 | tf_op jit(solution)/shard_map/reduce_sum | solution.py:27
  7.7 1.1 %multiply_convert_fusion = bf16[1,32,8,512]{3,2,1,0:T(8,128)(2,1)S(1)} fusion(bf16[1,32,8,512]{3,2,1,0:T(8,128)(2,1)} %param.8, f32[512]{0:T(512)} %param.9, f32[32,8]{1,0:T(8,128)S(1)} %add_rsqrt_fusion), kind=kLoop, calls=%fused_computation.19 | loop fusion | flops 524288 | bytes 527360 | tf_op jit(solution)/shard_map/convert_element_type | solution.py:28
  8.8 0.1 fusion.30
  8.9 5.5 %collective-permute-start.1 = (bf16[1,32,1,512]{3,2,1,0:T(2,128)(2,1)S(1)}, bf16[1,32,1,512]{3,2,1,0:T(2,128)(2,1)S(1)}, u32[]{:S(2)}, u32[]{:S(2)}) collective-permute-start(bf16[1,32,1,512]{3,2,1,0:T(2,128)(2,1)S(1)} %get-tuple-element.19), channel_id=1, source_target_pairs={{1,0},{2,1},{3,2},{4,3},{5,4},{6,5},{7,6},{8,7},{9,8},{10,9},{11,1... | collective-permute-start | bytes 98312 | tf_op jit(solution)/shard_map/ppermute | solution.py:20
  14.4 0.0 collective-permute-start
  14.4 1.0 slice_reduce_fusion.2
  15.4 0.1 iota_compare_fusion.1
  15.5 0.8 slice_bitcast_fusion.12
  16.3 0.9 compare_reduce_fusion
  17.2 0.1 copy.107
  17.2 0.1 copy.106
  17.3 0.1 copy.104
  17.4 0.1 copy.103
  17.5 0.1 copy.102
  17.5 0.1 copy.101
  17.6 0.1 copy.100
  17.7 0.1 copy.99
  17.8 0.1 copy.95
  17.8 0.0 collective-permute-done.1
  17.9 3.0 %collective-permute-done = bf16[1,32,1,512]{3,2,1,0:T(2,128)(2,1)S(1)} collective-permute-done((bf16[1,32,1,512]{3,2,1,0:T(2,128)(2,1)S(1)}, bf16[1,32,1,512]{3,2,1,0:T(2,128)(2,1)S(1)}, u32[]{:S(2)}, u32[]{:S(2)}) %collective-permute-start) | collective-permute-done | bytes 32800 | tf_op jit(solution)/shard_map/ppermute | solution.py:19
  20.8 0.3 pad_maximum_fusion.1
  21.2 18.2 %all_gather.6 = bf16[16,2,1,10,512]{4,1,3,2,0:T(2,128)(2,1)S(1)} all-gather(bf16[1,2,1,10,512]{4,1,3,2,0:T(2,128)(2,1)S(1)} %copy.96), channel_id=1, replica_groups=mesh['group'=2,'blk'=16] {'blk'}, dimensions={0}, use_global_device_ids=true | all-gather | bytes 348160 | tf_op jit(solution)/shard_map/all_gather | solution.py:148
  39.4 0.3 fusion.8
  39.7 0.1 broadcast_select_fusion.2
  39.9 1.1 fusion.36
  41.0 0.0 copy-start.1
  41.0 0.1 fusion.29
  41.1 1.9 %collective-permute-start.3 = (bf16[1,32,3,512]{3,2,1,0:T(4,128)(2,1)S(1)}, bf16[1,32,3,512]{3,2,1,0:T(4,128)(2,1)S(1)}, u32[]{:S(2)}, u32[]{:S(2)}) collective-permute-start(bf16[1,32,3,512]{3,2,1,0:T(4,128)(2,1)S(1)} %get-tuple-element.17), channel_id=1, source_target_pairs={{1,0},{2,1},{3,2},{4,3},{5,4},{6,5},{7,6},{8,7},{9,8},{10,9},{11,1... | collective-permute-start | bytes 294920 | tf_op jit(solution)/shard_map/ppermute | solution.py:20
  42.9 0.0 collective-permute-start.2
  42.9 2.5 %collective-permute-done.3 = bf16[1,32,3,512]{3,2,1,0:T(4,128)(2,1)S(1)} collective-permute-done((bf16[1,32,3,512]{3,2,1,0:T(4,128)(2,1)S(1)}, bf16[1,32,3,512]{3,2,1,0:T(4,128)(2,1)S(1)}, u32[]{:S(2)}, u32[]{:S(2)}) %collective-permute-start.3) | collective-permute-done | bytes 98336 | tf_op jit(solution)/shard_map/ppermute | solution.py:20
  45.4 4.6 %collective-permute-done.2 = bf16[1,32,3,512]{3,2,1,0:T(4,128)(2,1)S(1)} collective-permute-done((bf16[1,32,3,512]{3,2,1,0:T(4,128)(2,1)S(1)}, bf16[1,32,3,512]{3,2,1,0:T(4,128)(2,1)S(1)}, u32[]{:S(2)}, u32[]{:S(2)}) %collective-permute-start.2) | collective-permute-done | bytes 98336 | tf_op jit(solution)/shard_map/ppermute | solution.py:19
  50.0 0.3 fusion.28
  50.4 0.7 copy.108
  51.1 0.0 all-gather.2.cloned.1.call-update
  51.1 2.0 %convolution_convert_fusion.2.q_ref = bf16[256,512]{1,0:T(8,128)(2,1)} fusion(bf16[512,512]{1,0:T(8,128)(2,1)S(1)} %copy-done.1, bf16[32,10,512]{2,1,0:T(8,128)(2,1)S(1)} %get-tuple-element.15, bf16[1,10,512]{2,1,0:T(8,128)(2,1)S(1)} %copy.105, bf16[1,10,512]{2,1,0:T(8,128)(2,1)S(1)} %copy.98, f32[32,8]{1,0:T(8,128)S(1)} %copy.107, f32[32,8]{1,0:T(8,128)S(1)} %copy.106, ...), kind=kOutput, calls=%fused_computation.4 | convolution fusion | flops 140247040 | bytes 2277376 | tf_op jit(solution)/shard_map/dot_general | solution.py:76
  53.2 34.4 %all-gather.2.cloned.1.call-done = bf16[16,2,3,14,512]{4,1,3,2,0:T(2,128)(2,1)} async-done(((bf16[1,2,3,14,512]{4,1,3,2,0:T(2,128)(2,1)}), bf16[16,2,3,14,512]{4,1,3,2,0:T(2,128)(2,1)}) %all-gather.2.cloned.1.call-update) | async-done | bytes 1376272 | tf_op jit(solution)/shard_map/all_gather | solution.py:155
  87.6 1.8 %fusion.5 = bf16[2,3,14,512]{3,0,2,1:T(2,128)(2,1)S(1)} fusion(bf16[16,2,3,14,512]{4,1,3,2,0:T(2,128)(2,1)} %all-gather.2.cloned.1.call-done, pred[2,2]{0,1:T(4,128)(4,1)S(1)} %iota_compare_fusion, pred[2,16]{1,0:T(4,128)(4,1)S(1)} %iota_compare_fusion.1), kind=kOutput, calls=%fused_computation.6 | convolution fusion | flops 2795584 | bytes 1462308 | tf_op jit(solution)/shard_map/enf,nfrwc->erwc/dot_general | solution.py:37
  89.4 0.2 broadcast_select_fusion
  89.5 0.1 broadcast_select_fusion.1
  89.7 0.1 fusion.31
  89.9 0.1 pad_maximum_fusion
  90.0 0.0 copy-start.2
  90.0 0.2 reshape.100
  90.1 1.3 %convolution_convert_fusion.1.k_ref = bf16[640,512]{1,0:T(8,128)(2,1)} fusion(bf16[512,512]{1,0:T(8,128)(2,1)S(1)} %copy-done, bf16[532,512]{1,0:T(8,128)(2,1)S(1)} %reshape.100), kind=kOutput, calls=%fused_computation.3 | convolution fusion | flops 335872000 | bytes 1724416 | tf_op jit(solution)/shard_map/dot_general | solution.py:76
  91.5 0.0 copy-done.2
  91.5 1.3 %convolution_convert_fusion.v_ref = bf16[640,512]{1,0:T(8,128)(2,1)} fusion(bf16[512,512]{1,0:T(8,128)(2,1)S(1)} %copy-done.2, bf16[532,512]{1,0:T(8,128)(2,1)S(1)} %reshape.100), kind=kOutput, calls=%fused_computation.2 | convolution fusion | flops 335872000 | bytes 1724416 | tf_op jit(solution)/shard_map/dot_general | solution.py:76
  92.8 7.0 %shard_map.82 = bf16[256,512]{1,0:T(8,128)(2,1)} custom-call(bf16[256,512]{1,0:T(8,128)(2,1)} %convolution_convert_fusion.2.q_ref, bf16[640,512]{1,0:T(8,128)(2,1)} %convolution_convert_fusion.1.k_ref, bf16[640,512]{1,0:T(8,128)(2,1)} %convolution_convert_fusion.v_ref, bf16[32,8,512]{2,1,0:T(8,128)(2,1)} %bitcast.67, bf16[512,512]{1,0:T(8,128)(2,1)} %wo_ref.1), custom_call_target="tpu_custom_call" | custom-call | tf_op jit(solution)/shard_map/pallas_call | solution.py:130
  (15 shorter events, 0.2 us)
Async XLA Ops:
  6.5 83.6 %copy-start = (bf16[512,512]{1,0:T(8,128)(2,1)S(1)}, bf16[512,512]{1,0:T(8,128)(2,1)}, u32[]{:S(2)}) copy-start(bf16[512,512]{1,0:T(8,128)(2,1)} %param.12) | copy-start | bytes 1572868
  6.5 81.0 %all-gather.2.cloned.1.call-start = ((), (), s32[]{:S(2)}) async-start(), calls=%async_computation | async-start | bytes 1462272 | tf_op jit(solution)/shard_map/all_gather | solution.py:155
  8.9 9.0 %collective-permute-start.1 = (bf16[1,32,1,512]{3,2,1,0:T(2,128)(2,1)S(1)}, bf16[1,32,1,512]{3,2,1,0:T(2,128)(2,1)S(1)}, u32[]{:S(2)}, u32[]{:S(2)}) collective-permute-start(bf16[1,32,1,512]{3,2,1,0:T(2,128)(2,1)S(1)} %get-tuple-element.19), channel_id=1, source_target_pairs={{1,0},{2,1},{3,2},{4,3},{5,4},{6,5},{7,6},{8,7},{9,8},{10,9},{11,1... | collective-permute-start | bytes 98312 | tf_op jit(solution)/shard_map/ppermute | solution.py:20
  14.4 6.4 %collective-permute-start = (bf16[1,32,1,512]{3,2,1,0:T(2,128)(2,1)S(1)}, bf16[1,32,1,512]{3,2,1,0:T(2,128)(2,1)S(1)}, u32[]{:S(2)}, u32[]{:S(2)}) collective-permute-start(bf16[1,32,1,512]{3,2,1,0:T(2,128)(2,1)S(1)} %get-tuple-element.18), channel_id=1, source_target_pairs={{0,1},{1,2},{2,3},{3,4},{4,5},{5,6},{6,7},{7,8},{8,9},{9,10},{10,1... | collective-permute-start | bytes 98312 | tf_op jit(solution)/shard_map/ppermute | solution.py:19
  41.0 10.2 %copy-start.1 = (bf16[512,512]{1,0:T(8,128)(2,1)S(1)}, bf16[512,512]{1,0:T(8,128)(2,1)}, u32[]{:S(2)}) copy-start(bf16[512,512]{1,0:T(8,128)(2,1)} %param.11) | copy-start | bytes 1572868
  41.1 4.4 %collective-permute-start.3 = (bf16[1,32,3,512]{3,2,1,0:T(4,128)(2,1)S(1)}, bf16[1,32,3,512]{3,2,1,0:T(4,128)(2,1)S(1)}, u32[]{:S(2)}, u32[]{:S(2)}) collective-permute-start(bf16[1,32,3,512]{3,2,1,0:T(4,128)(2,1)S(1)} %get-tuple-element.17), channel_id=1, source_target_pairs={{1,0},{2,1},{3,2},{4,3},{5,4},{6,5},{7,6},{8,7},{9,8},{10,9},{11,1... | collective-permute-start | bytes 294920 | tf_op jit(solution)/shard_map/ppermute | solution.py:20
  42.9 7.1 %collective-permute-start.2 = (bf16[1,32,3,512]{3,2,1,0:T(4,128)(2,1)S(1)}, bf16[1,32,3,512]{3,2,1,0:T(4,128)(2,1)S(1)}, u32[]{:S(2)}, u32[]{:S(2)}) collective-permute-start(bf16[1,32,3,512]{3,2,1,0:T(4,128)(2,1)S(1)} %get-tuple-element.16), channel_id=1, source_target_pairs={{0,1},{1,2},{2,3},{3,4},{4,5},{5,6},{6,7},{7,8},{8,9},{9,10},{10,1... | collective-permute-start | bytes 294920 | tf_op jit(solution)/shard_map/ppermute | solution.py:19
  90.0 1.5 %copy-start.2 = (bf16[512,512]{1,0:T(8,128)(2,1)S(1)}, bf16[512,512]{1,0:T(8,128)(2,1)}, u32[]{:S(2)}) copy-start(bf16[512,512]{1,0:T(8,128)(2,1)} %param.13) | copy-start | bytes 1572868
Sparse Core Ops, SparseCore 0:
  51.2 36.2 all-gather.1

commit v5 on v4

--- a/solution.py
+++ b/solution.py
@@ -137,6 +137,21 @@
     return out.reshape(rows, cols, channels)
 
 
+def widen_tiles(field, margin):
+    west = jnp.roll(field, 1, axis=0)[:, :, -margin:]
+    east = jnp.roll(field, -1, axis=0)[:, :, :margin]
+    return jnp.concatenate([west, field, east], axis=2)
+
+
+def pick_all(table, edges):
+    number = edges.shape[0]
+    tile_hit = jnp.arange(number, dtype=jnp.int32) == table[..., 0:1]
+    edge_hit = jnp.arange(2, dtype=jnp.int32) == table[..., 1:2]
+    chosen = (tile_hit[..., :, None] & edge_hit[..., None, :]).astype(edges.dtype)
+    got = jnp.einsum("...nf,nfrwc->...rwc", chosen, edges, preferred_element_type=jnp.float32)
+    return got.astype(edges.dtype)
+
+
 def local(latents, norm_gain, metric, w_query, w_key, w_value, w_output, seam_table):
     own_tile = latents[0]
     channels = own_tile.shape[-1]
@@ -144,16 +159,17 @@
     margin = 1
     seam_rows = seam_table[0]
     widened = padded_2(normed[None], (("blk", 2),), margin)
-    received = pick_rims(
-        seam_rows, lax.all_gather(edge_rows(widened, 1), "blk", axis=0, tiled=True)
-    )
+    rows1 = jnp.stack([normed[0], normed[-1]])
+    got1 = widen_tiles(lax.all_gather(rows1[None], "blk", axis=0, tiled=True), 1)
+    received = pick_all(seam_rows, got1[:, :, None])
     padded = place_rims(widened[0], received, seam_rows)
     smoothed = smooth(padded, metric[0])
     query = project(smoothed, w_query)
     field_wide = padded_2(smoothed[None], (("blk", 2),), RADIUS)
-    field_got = pick_rims(
-        seam_rows, lax.all_gather(edge_rows(field_wide, RADIUS), "blk", axis=0, tiled=True)
-    )
+    rows3 = jnp.concatenate([smoothed[:RADIUS], smoothed[-RADIUS:]], axis=0)
+    got3 = widen_tiles(lax.all_gather(rows3[None], "blk", axis=0, tiled=True), RADIUS)
+    edges3 = jnp.stack([got3[:, :RADIUS], got3[:, RADIUS:]], axis=1)
+    field_got = pick_all(seam_rows, edges3)
     field_pad = place_rims(field_wide[0], field_got, seam_rows)
     return attend_and_mix(query, field_pad, w_key, w_value, own_tile, w_output)[None]
 

time: 107 us -> 72.7 us (0.68)
  waiting for transfers between devices: 44.5 us -> 0.01 us
  blocking collectives: 18.2 us -> 39.6 us
  between operations: 13.6 us -> 0.39 us
  starting transfers between devices: 7.35 us -> 10.1 us
  matrix products: 6.82 us -> 4.43 us
  other arithmetic: 5.39 us -> 7.1 us
    all_gather x1 -> x0, waiting for transfers between devices: 34.4 us -> none  [local(): lax.all_gather(edge_rows(field_wide, RADIUS), 'blk', axis=0, tiled=True)]
    all_gather x1 -> x2, blocking collectives: 18.2 us -> 39.6 us  [the longest x1 20 us: local(): lax.all_gather(rows1[None], 'blk', axis=0, tiled=True)]
    ppermute x2, waiting for transfers between devices: 7.54 us -> 0.01 us  [padded_2(): before = lax.ppermute(last, axis, up)]
    ppermute x2, waiting for transfers between devices: 2.52 us -> 0.01 us  [padded_2(): after = lax.ppermute(first, axis, down)]
    ppermute x2, starting transfers between devices: 7.35 us -> 9.15 us  [padded_2(): after = lax.ppermute(first, axis, down)]
    slice x0 -> x14, local copies, waits for them, and re-layouts: none -> 1.49 us  [the longest x8 0.82 us: widen_tiles(): west = jnp.roll(field, 1, axis=0)[:, :, -margin:]]
    dot_general x2, matrix products: 2.09 us -> 0.74 us  [pick_all(): jnp.einsum('...nf,nfrwc->...rwc', chosen, edges, preferred_element_type=j...]
    convert_element_type x1 -> x2, other arithmetic: 1.08 us -> 2.17 us  [normalize(): return (values * factor * norm_gain).astype(jnp.bfloat16)]
  transfers between devices with their start and end apart: 5 -> 4, of which waited for: 4 -> 0; matrix products, arithmetic and copies ran while one was open for 5% -> 10% of each run, Pallas kernels for 0% -> 0%
where the time goes in v5:
time: 72.7 us; the launch traced here: 72.5 us
  blocking collectives  39.6 us (54%)
  starting transfers between devices  10.1 us (14%)
  other arithmetic  7.1 us (10%)
  Pallas kernels  7 us (10%)
  matrix products  4.43 us (6%)
  local copies, waits for them, and re-layouts  3.82 us (5%)
    all_gather x1, blocking collectives, local(): lax.all_gather(rows1[None], 'blk', axis=0, tiled=True)  20 us
    all_gather x1, blocking collectives, local(): lax.all_gather(rows3[None], 'blk', axis=0, tiled=True)  19.6 us
    ppermute x2, starting transfers between devices, padded_2(): after = lax.ppermute(first, axis, down)  9.15 us
    pallas_call x1, Pallas kernels, attend_and_mix(): pl.pallas_call(attention_kernel, out_shape=jax.ShapeDtypeStruct((cells, c...  7 us
    dot_general x3, matrix products, project(): jnp.dot(flat, weight, preferred_element_type=jnp.float32)  3.69 us
    convert_element_type x2, other arithmetic, normalize(): return (values * factor * norm_gain).astype(jnp.bfloat16)  2.17 us
  transfers between devices with their start and end apart: 4, of which 0 were waited for; matrix products, arithmetic and copies ran while one was open for 10% of the time, Pallas kernels for 0%

profile of v5, /device:TPU:0, one launch (start us, length us, event | category | flops | bytes accessed | tf_op | source)
XLA Modules:
  0.0 72.5 jit_solution(10345603669423486612)
XLA Ops:
  0.0 1.1 %fusion.15 = f32[32,8]{1,0:T(8,128)S(1)} fusion(bf16[1,32,8,512]{3,2,1,0:T(8,128)(2,1)} %param.8), kind=kLoop, calls=%fused_computation.26 | loop fusion | flops 392960 | bytes 263168 | tf_op jit(solution)/shard_map/reduce_sum | solution.py:27
  1.2 1.1 %multiply_convert_fusion = bf16[1,32,8,512]{3,2,1,0:T(8,128)(2,1)S(1)} fusion(bf16[1,32,8,512]{3,2,1,0:T(8,128)(2,1)} %param.8, f32[512]{0:T(512)} %param.9, f32[32,8]{1,0:T(8,128)S(1)} %add_rsqrt_fusion), kind=kLoop, calls=%fused_computation.32 | loop fusion | flops 524288 | bytes 527360 | tf_op jit(solution)/shard_map/convert_element_type | solution.py:28
  2.3 0.1 fusion.46
  2.4 0.5 collective-permute-start
  2.9 5.1 %collective-permute-start.1 = (bf16[1,32,1,512]{3,2,1,0:T(2,128)(2,1)S(1)}, bf16[1,32,1,512]{3,2,1,0:T(2,128)(2,1)S(1)}, u32[]{:S(2)}, u32[]{:S(2)}) collective-permute-start(bf16[1,32,1,512]{3,2,1,0:T(2,128)(2,1)S(1)} %get-tuple-element.25), channel_id=1, source_target_pairs={{1,0},{2,1},{3,2},{4,3},{5,4},{6,5},{7,6},{8,7},{9,8},{10,9},{11,1... | collective-permute-start | bytes 98312 | tf_op jit(solution)/shard_map/ppermute | solution.py:20
  7.9 1.1 %fusion.17 = bf16[32,8,512]{2,1,0:T(8,128)(2,1)S(1)} fusion(f32[512]{0:T(512)} %param.9, f32[32,8]{1,0:T(8,128)S(1)} %add_rsqrt_fusion, bf16[1,32,8,512]{3,2,1,0:T(8,128)(2,1)} %param.8), kind=kLoop, calls=%fused_computation.28 | loop fusion | flops 524288 | bytes 527360 | tf_op jit(solution)/shard_map/convert_element_type | solution.py:28
  9.0 20.0 %all-gather = bf16[32,8,512]{2,1,0:T(8,128)(2,1)S(1)} all-gather(bf16[2,8,512]{2,1,0:T(8,128)(2,1)S(1)} %pad_maximum_fusion.8), channel_id=2, replica_groups=mesh['group'=2,'blk'=16] {'blk'}, dimensions={0}, use_global_device_ids=true | all-gather | bytes 278528 | tf_op jit(solution)/shard_map/all_gather | solution.py:163
  29.1 0.2 slice_reduce_fusion.2
  29.4 0.2 compare_reduce_fusion
  29.6 0.1 copy.115
  29.7 0.1 copy.116
  29.9 0.2 copy.118
  30.2 0.3 fusion.12
  30.5 0.1 broadcast_select_fusion.2
  30.7 0.1 copy.113
  30.8 0.1 copy.120
  30.8 0.1 copy.121
  30.9 0.1 copy.122
  31.0 0.1 copy.123
  31.1 0.1 copy.124
  31.1 0.1 copy.125
  31.4 0.3 maximum_bitcast_fusion
  31.7 1.1 %fusion.52 = bf16[1,32,8,512]{3,2,1,0:T(8,128)(2,1)S(1)} fusion(bf16[1,10,512]{2,1,0:T(8,128)(2,1)S(1)} %copy.126, bf16[32,10,512]{2,1,0:T(8,128)(2,1)S(1)} %maximum_bitcast_fusion, f32[32,8]{1,0:T(8,128)S(1)} %copy.128, f32[32,8]{1,0:T(8,128)S(1)} %copy.127, f32[32,8]{1,0:T(8,128)S(1)} %copy.125, f32[32,8]{1,0:T(8,128)S(1)} %copy.124, ...), kind=kLoop, calls=%fused_computation.107 | loop fusion | flops 5898240 | bytes 1753088 | tf_op jit(solution)/shard_map/broadcast_in_dim | solution.py:168
  32.7 1.1 %add_convert_fusion = bf16[32,8,512]{2,1,0:T(8,128)(2,1)S(1)} fusion(bf16[32,10,512]{2,1,0:T(8,128)(2,1)S(1)} %maximum_bitcast_fusion, bf16[1,10,512]{2,1,0:T(8,128)(2,1)S(1)} %copy.126, bf16[1,10,512]{2,1,0:T(8,128)(2,1)S(1)} %copy.119, f32[32,8]{1,0:T(8,128)S(1)} %copy.128, f32[32,8]{1,0:T(8,128)S(1)} %copy.127, f32[32,8]{1,0:T(8,128)S(1)} %copy.125, ...), kind=kLoop, calls=%fused_computation.31 | loop fusion | flops 5898240 | bytes 1753088 | tf_op jit(solution)/shard_map/convert_element_type | solution.py:69
  33.8 19.6 %all-gather.1 = bf16[96,8,512]{2,1,0:T(8,128)(2,1)S(1)} all-gather(bf16[6,8,512]{2,1,0:T(8,128)(2,1)S(1)} %pad_maximum_fusion.7), channel_id=3, replica_groups=mesh['group'=2,'blk'=16] {'blk'}, dimensions={0}, use_global_device_ids=true | all-gather | bytes 835584 | tf_op jit(solution)/shard_map/all_gather | solution.py:170
  53.4 0.1 fusion.41
  53.6 0.1 fusion.42
  53.7 0.4 collective-permute-start.2
  54.1 4.1 %collective-permute-start.3 = (bf16[1,32,3,512]{3,2,1,0:T(4,128)(2,1)S(1)}, bf16[1,32,3,512]{3,2,1,0:T(4,128)(2,1)S(1)}, u32[]{:S(2)}, u32[]{:S(2)}) collective-permute-start(bf16[1,32,3,512]{3,2,1,0:T(4,128)(2,1)S(1)} %get-tuple-element.15), channel_id=1, source_target_pairs={{1,0},{2,1},{3,2},{4,3},{5,4},{6,5},{7,6},{8,7},{9,8},{10,9},{11,1... | collective-permute-start | bytes 294920 | tf_op jit(solution)/shard_map/ppermute | solution.py:20
  58.2 0.4 copy.130
  58.6 0.4 copy.131
  59.0 0.4 copy.133
  59.4 0.1 copy.129
  59.5 0.1 copy.132
  59.6 0.3 fusion
  59.9 0.2 slice_bitcast_fusion.1
  60.1 0.4 fusion.9
  60.5 0.2 broadcast_select_fusion
  60.7 0.1 broadcast_select_fusion.1
  60.9 0.1 fusion.47
  61.0 0.1 copy-done.1
  61.1 1.0 %convolution_convert_fusion.2.q_ref = bf16[256,512]{1,0:T(8,128)(2,1)} fusion(bf16[512,512]{1,0:T(8,128)(2,1)S(1)} %copy-done.1, bf16[32,8,512]{2,1,0:T(8,128)(2,1)S(1)} %add_convert_fusion), kind=kOutput, calls=%fused_computation.10 | convolution fusion | flops 134348800 | bytes 1048576 | tf_op jit(solution)/shard_map/dot_general | solution.py:76
  62.2 0.3 maximum_bitcast_fusion.1
  62.5 0.1 pad_maximum_fusion.2
  62.6 0.2 reshape.98
  62.8 1.4 %convolution_convert_fusion.v_ref = bf16[640,512]{1,0:T(8,128)(2,1)} fusion(bf16[512,512]{1,0:T(8,128)(2,1)S(1)} %copy-done, bf16[532,512]{1,0:T(8,128)(2,1)S(1)} %reshape.98), kind=kOutput, calls=%fused_computation.8 | convolution fusion | flops 335872000 | bytes 1724416 | tf_op jit(solution)/shard_map/dot_general | solution.py:76
  64.1 1.3 %convolution_convert_fusion.1.k_ref = bf16[640,512]{1,0:T(8,128)(2,1)} fusion(bf16[512,512]{1,0:T(8,128)(2,1)S(1)} %copy-done.4, bf16[532,512]{1,0:T(8,128)(2,1)S(1)} %reshape.98), kind=kOutput, calls=%fused_computation.9 | convolution fusion | flops 335872000 | bytes 1724416 | tf_op jit(solution)/shard_map/dot_general | solution.py:76
  65.5 7.0 %shard_map.82 = bf16[256,512]{1,0:T(8,128)(2,1)} custom-call(bf16[256,512]{1,0:T(8,128)(2,1)} %convolution_convert_fusion.2.q_ref, bf16[640,512]{1,0:T(8,128)(2,1)} %convolution_convert_fusion.1.k_ref, bf16[640,512]{1,0:T(8,128)(2,1)} %convolution_convert_fusion.v_ref, bf16[32,8,512]{2,1,0:T(8,128)(2,1)} %bitcast.78, bf16[512,512]{1,0:T(8,128)(2,1)} %wo_ref.1), custom_call_target="tpu_custom_call" | custom-call | tf_op jit(solution)/shard_map/pallas_call | solution.py:130
  (33 shorter events, 0.5 us)
Async XLA Ops:
  0.0 62.7 %copy-start = (bf16[512,512]{1,0:T(8,128)(2,1)S(1)}, bf16[512,512]{1,0:T(8,128)(2,1)}, u32[]{:S(2)}) copy-start(bf16[512,512]{1,0:T(8,128)(2,1)} %param.13) | copy-start | bytes 1572868
  1.2 28.0 %copy-start.3 = (s32[1,2,3]{2,1,0:T(2,128)S(1)}, s32[1,2,3]{2,1,0:T(2,128)}, u32[]{:S(2)}) copy-start(s32[1,2,3]{2,1,0:T(2,128)} %param.15) | copy-start | bytes 76
  2.4 29.0 %collective-permute-start = (bf16[1,32,1,512]{3,2,1,0:T(2,128)(2,1)S(1)}, bf16[1,32,1,512]{3,2,1,0:T(2,128)(2,1)S(1)}, u32[]{:S(2)}, u32[]{:S(2)}) collective-permute-start(bf16[1,32,1,512]{3,2,1,0:T(2,128)(2,1)S(1)} %get-tuple-element.24), channel_id=1, source_target_pairs={{0,1},{1,2},{2,3},{3,4},{4,5},{5,6},{6,7},{7,8},{8,9},{9,10},{10,1... | collective-permute-start | bytes 98312 | tf_op jit(solution)/shard_map/ppermute | solution.py:19
  2.9 28.5 %collective-permute-start.1 = (bf16[1,32,1,512]{3,2,1,0:T(2,128)(2,1)S(1)}, bf16[1,32,1,512]{3,2,1,0:T(2,128)(2,1)S(1)}, u32[]{:S(2)}, u32[]{:S(2)}) collective-permute-start(bf16[1,32,1,512]{3,2,1,0:T(2,128)(2,1)S(1)} %get-tuple-element.25), channel_id=1, source_target_pairs={{1,0},{2,1},{3,2},{4,3},{5,4},{6,5},{7,6},{8,7},{9,8},{10,9},{11,1... | collective-permute-start | bytes 98312 | tf_op jit(solution)/shard_map/ppermute | solution.py:20
  29.7 0.9 %copy-start.2 = (f32[1,9,32,8]{2,3,1,0:T(8,128)S(1)}, f32[1,9,32,8]{2,3,1,0:T(8,128)}, u32[]{:S(2)}) copy-start(f32[1,9,32,8]{2,3,1,0:T(8,128)} %param.10) | copy-start | bytes 27652
  53.7 8.5 %collective-permute-start.2 = (bf16[1,32,3,512]{3,2,1,0:T(4,128)(2,1)S(1)}, bf16[1,32,3,512]{3,2,1,0:T(4,128)(2,1)S(1)}, u32[]{:S(2)}, u32[]{:S(2)}) collective-permute-start(bf16[1,32,3,512]{3,2,1,0:T(4,128)(2,1)S(1)} %get-tuple-element.14), channel_id=1, source_target_pairs={{0,1},{1,2},{2,3},{3,4},{4,5},{5,6},{6,7},{7,8},{8,9},{9,10},{10,1... | collective-permute-start | bytes 294920 | tf_op jit(solution)/shard_map/ppermute | solution.py:19
  54.1 8.1 %collective-permute-start.3 = (bf16[1,32,3,512]{3,2,1,0:T(4,128)(2,1)S(1)}, bf16[1,32,3,512]{3,2,1,0:T(4,128)(2,1)S(1)}, u32[]{:S(2)}, u32[]{:S(2)}) collective-permute-start(bf16[1,32,3,512]{3,2,1,0:T(4,128)(2,1)S(1)} %get-tuple-element.15), channel_id=1, source_target_pairs={{1,0},{2,1},{3,2},{4,3},{5,4},{6,5},{7,6},{8,7},{9,8},{10,9},{11,1... | collective-permute-start | bytes 294920 | tf_op jit(solution)/shard_map/ppermute | solution.py:20
  60.1 1.0 %copy-start.1 = (bf16[512,512]{1,0:T(8,128)(2,1)S(1)}, bf16[512,512]{1,0:T(8,128)(2,1)}, u32[]{:S(2)}) copy-start(bf16[512,512]{1,0:T(8,128)(2,1)} %param.11) | copy-start | bytes 1572868
  62.6 1.5 %copy-start.4 = (bf16[512,512]{1,0:T(8,128)(2,1)S(1)}, bf16[512,512]{1,0:T(8,128)(2,1)}, u32[]{:S(2)}) copy-start(bf16[512,512]{1,0:T(8,128)(2,1)} %param.12) | copy-start | bytes 1572868

commit v6 on v5

--- a/solution.py
+++ b/solution.py
@@ -152,25 +152,97 @@
     return got.astype(edges.dtype)
 
 
+def smooth_total(padded, metric):
+    rows, cols = (metric.shape[-2], metric.shape[-1])
+    total = jnp.zeros((rows, cols, padded.shape[-1]), jnp.float32)
+    for stencil in range(9):
+        row_off = stencil // 3
+        col_off = stencil % 3
+        total = (
+            total
+            + metric[stencil, :, :, None]
+            * padded[row_off : row_off + rows, col_off : col_off + cols, :]
+        )
+    return total
+
+
+def to_bf16_exact(values):
+    return lax.reduce_precision(values, exponent_bits=8, mantissa_bits=7)
+
+
+def split_parts(values, count):
+    parts = []
+    rest = values
+    for _ in range(count - 1):
+        head = to_bf16_exact(rest)
+        parts.append(head.astype(jnp.bfloat16))
+        rest = rest - head
+    parts.append(rest.astype(jnp.bfloat16))
+    return parts
+
+
 def local(latents, norm_gain, metric, w_query, w_key, w_value, w_output, seam_table):
     own_tile = latents[0]
-    channels = own_tile.shape[-1]
+    rows, cols, channels = own_tile.shape
+    count = lax.axis_size("blk")
+    me = lax.axis_index("blk")
+    seam_rows = seam_table[0]
     normed = normalize(own_tile, norm_gain)
-    margin = 1
-    seam_rows = seam_table[0]
-    widened = padded_2(normed[None], (("blk", 2),), margin)
-    rows1 = jnp.stack([normed[0], normed[-1]])
-    got1 = widen_tiles(lax.all_gather(rows1[None], "blk", axis=0, tiled=True), 1)
-    received = pick_all(seam_rows, got1[:, :, None])
-    padded = place_rims(widened[0], received, seam_rows)
-    smoothed = smooth(padded, metric[0])
-    query = project(smoothed, w_query)
-    field_wide = padded_2(smoothed[None], (("blk", 2),), RADIUS)
-    rows3 = jnp.concatenate([smoothed[:RADIUS], smoothed[-RADIUS:]], axis=0)
-    got3 = widen_tiles(lax.all_gather(rows3[None], "blk", axis=0, tiled=True), RADIUS)
-    edges3 = jnp.stack([got3[:, :RADIUS], got3[:, RADIUS:]], axis=1)
+    widened = padded_2(normed[None], (("blk", 2),), 1)[0]
+    blank = jnp.zeros((1,) + widened.shape[1:], widened.dtype)
+    partial = smooth_total(jnp.concatenate([blank, widened, blank], axis=0), metric[0])
+    smoothed_p = partial.astype(jnp.bfloat16)
+    field_wide = padded_2(smoothed_p[None], (("blk", 2),), RADIUS)[0]
+
+    edge_partial = jnp.stack([partial[0], partial[-1]])
+    taps = jnp.stack([metric[0, 0:3, 0], metric[0, 6:9, rows - 1]])
+    pieces = [
+        jnp.stack([normed[0], normed[-1]]).reshape(-1),
+        *[p.reshape(-1) for p in split_parts(edge_partial, 2)],
+        jnp.stack([smoothed_p[1], smoothed_p[2], smoothed_p[-3], smoothed_p[-2]]).reshape(-1),
+        *[p.reshape(-1) for p in split_parts(taps, 3)],
+        seam_rows.astype(jnp.bfloat16).reshape(-1),
+    ]
+    sizes = [p.size for p in pieces]
+    flat = jnp.concatenate(pieces)
+    total = -(-flat.size // channels) * channels
+    flat = jnp.pad(flat, (0, total - flat.size)).reshape(1, total // channels, channels)
+    got = lax.all_gather(flat, "blk", axis=0, tiled=True).reshape(count, total)
+    offsets = [sum(sizes[:k]) for k in range(len(sizes) + 1)]
+
+    def piece(k, shape):
+        return got[:, offsets[k] : offsets[k + 1]].reshape((count,) + shape)
+
+    edge_rows = piece(0, (2, cols, channels))
+    part_all = piece(1, (2, cols, channels)).astype(jnp.float32) + piece(2, (2, cols, channels)).astype(jnp.float32)
+    inner = piece(3, (4, cols, channels))
+    tap_parts = [piece(4 + k, (2, 3, cols)).astype(jnp.float32) for k in range(3)]
+    taps_all = tap_parts[0] + (tap_parts[1] + tap_parts[2])
+    table_all = piece(7, (2, 3)).astype(jnp.int32)
+
+    edges1 = widen_tiles(edge_rows, 1)
+    rims1 = pick_all(table_all, edges1[:, :, None])[:, :, 0]
+    flip = (table_all[:, :, 2] % 2 == 1)[:, :, None, None]
+    rims1 = jnp.where(flip, rims1[:, :, ::-1], rims1)
+
+    out_col = lax.broadcasted_iota(jnp.int32, (cols, cols + 2), 0)
+    in_col = lax.broadcasted_iota(jnp.int32, (cols, cols + 2), 1)
+    band = jnp.zeros((count, 2, cols, cols + 2), jnp.float32)
+    for b in range(3):
+        band = band + jnp.where(in_col == out_col + b, taps_all[:, :, b, :, None], 0.0)
+    contrib = jnp.einsum(
+        "uejp,uepc->uejc", band, rims1.astype(jnp.float32), precision=lax.Precision.HIGHEST
+    )
+    done = (part_all + contrib).astype(jnp.bfloat16)
+    band6 = jnp.concatenate([done[:, 0:1], inner, done[:, 1:2]], axis=1)
+    wide3 = widen_tiles(band6, RADIUS)
+    mine = lax.dynamic_index_in_dim(wide3, me, 0, keepdims=False)
+    field_wide = jnp.concatenate([mine[0:1], field_wide[1:-1], mine[-1:]], axis=0)
+
+    edges3 = jnp.stack([wide3[:, :RADIUS], wide3[:, RADIUS:]], axis=1)
     field_got = pick_all(seam_rows, edges3)
-    field_pad = place_rims(field_wide[0], field_got, seam_rows)
+    field_pad = place_rims(field_wide, field_got, seam_rows)
+    query = project(field_wide[:, RADIUS : RADIUS + cols], w_query)
     return attend_and_mix(query, field_pad, w_key, w_value, own_tile, w_output)[None]
 
 

time: 72.7 us -> 89.3 us (1.23)
  blocking collectives: 39.6 us -> 0 us
  waiting for transfers between devices: 0.01 us -> 32.6 us
  between operations: 0.39 us -> 14 us
  local copies, waits for them, and re-layouts: 3.82 us -> 10 us
  other arithmetic: 7.1 us -> 9.66 us
  matrix products: 4.43 us -> 5.78 us
    all_gather x2 -> x0, blocking collectives: 39.6 us -> none  [the longest x1 20 us: local(): lax.all_gather(rows1[None], 'blk', axis=0, tiled=True)]
    all_gather x0 -> x1, waiting for transfers between devices: none -> 32.5 us  [local(): got = lax.all_gather(flat, 'blk', axis=0, tiled=True).reshape(count, total)]
    unnamed x11 -> x39, local copies, waits for them, and re-layouts: 0.18 us -> 3.54 us
    eq x1 -> x3, other arithmetic: 0.19 us -> 1.77 us  [the longest x2 1.24 us: local(): in_col == out_col + b]
    eq x1 -> x2, other arithmetic: 0.01 us -> 1.13 us  [pick_all(): edge_hit = jnp.arange(2, dtype=jnp.int32) == table[..., 1:2]]
    broadcast_in_dim x1 -> x0, other arithmetic: 1.05 us -> none  [local(): field_wide = padded_2(smoothed[None], (('blk', 2),), RADIUS)]
  transfers between devices with their start and end apart: 4 -> 5, of which waited for: 0 -> 1; matrix products, arithmetic and copies ran while one was open for 10% -> 19% of each run, Pallas kernels for 0% -> 0%
where the time goes in v6:
time: 89.3 us; the launch traced here: 89 us
  waiting for transfers between devices  32.6 us (37%)
  between operations  14 us (16%)
  local copies, waits for them, and re-layouts  10 us (11%)
  starting transfers between devices  10 us (11%)
  other arithmetic  9.66 us (11%)
  Pallas kernels  7 us (8%)
  matrix products  5.78 us (6%)
    all_gather x1, waiting for transfers between devices, local(): got = lax.all_gather(flat, 'blk', axis=0, tiled=True).reshape(count, total)  32.5 us
    ppermute x2, starting transfers between devices, padded_2(): after = lax.ppermute(first, axis, down)  9.5 us
    pallas_call x1, Pallas kernels, attend_and_mix(): pl.pallas_call(attention_kernel, out_shape=jax.ShapeDtypeStruct((cells, c...  7 us
    dot_general x3, matrix products, project(): jnp.dot(flat, weight, preferred_element_type=jnp.float32)  3.75 us
    unnamed x39, local copies, waits for them, and re-layouts  3.54 us
    convert_element_type x2, other arithmetic, normalize(): return (values * factor * norm_gain).astype(jnp.bfloat16)  2.17 us
  transfers between devices with their start and end apart: 5, of which 1 were waited for; matrix products, arithmetic and copies ran while one was open for 19% of the time, Pallas kernels for 0%

profile of v6, /device:TPU:0, one launch (start us, length us, event | category | flops | bytes accessed | tf_op | source)
XLA Modules:
  0.0 89.0 jit_solution(4383722733935152920)
XLA Ops:
  6.5 1.1 %fusion.16 = f32[32,8]{1,0:T(8,128)S(1)} fusion(bf16[1,32,8,512]{3,2,1,0:T(8,128)(2,1)} %param.8), kind=kLoop, calls=%fused_computation.23 | loop fusion | flops 392960 | bytes 263168 | tf_op jit(solution)/shard_map/reduce_sum | solution.py:27
  7.7 1.1 %multiply_convert_fusion = bf16[1,32,8,512]{3,2,1,0:T(8,128)(2,1)S(1)} fusion(bf16[1,32,8,512]{3,2,1,0:T(8,128)(2,1)} %param.8, f32[512]{0:T(512)} %param.9, f32[32,8]{1,0:T(8,128)S(1)} %add_rsqrt_fusion), kind=kLoop, calls=%fused_computation.31 | loop fusion | flops 524288 | bytes 527360 | tf_op jit(solution)/shard_map/convert_element_type | solution.py:28
  8.9 0.5 collective-permute-start
  9.4 5.1 %collective-permute-start.1 = (bf16[1,32,1,512]{3,2,1,0:T(2,128)(2,1)S(1)}, bf16[1,32,1,512]{3,2,1,0:T(2,128)(2,1)S(1)}, u32[]{:S(2)}, u32[]{:S(2)}) collective-permute-start(bf16[1,32,1,512]{3,2,1,0:T(2,128)(2,1)S(1)} %get-tuple-element.39), channel_id=1, source_target_pairs={{1,0},{2,1},{3,2},{4,3},{5,4},{6,5},{7,6},{8,7},{9,8},{10,9},{11,1... | collective-permute-start | bytes 98312 | tf_op jit(solution)/shard_map/ppermute | solution.py:20
  14.4 1.1 %fusion.18 = bf16[32,8,512]{2,1,0:T(8,128)(2,1)S(1)} fusion(f32[512]{0:T(512)} %param.9, f32[32,8]{1,0:T(8,128)S(1)} %add_rsqrt_fusion, bf16[1,32,8,512]{3,2,1,0:T(8,128)(2,1)} %param.8), kind=kLoop, calls=%fused_computation.25 | loop fusion | flops 524288 | bytes 527360 | tf_op jit(solution)/shard_map/convert_element_type | solution.py:28
  15.6 0.1 slice_reduce_fusion.3
  16.7 0.3 maximum_bitcast_fusion
  17.0 0.6 fusion.65
  17.7 0.1 concatenate.55
  17.8 0.7 reshape.226
  18.5 0.6 iota_compare_fusion.3
  19.1 0.2 slice_reduce_fusion.6
  19.3 0.5 iota_compare_fusion.5
  19.9 0.6 iota_compare_fusion.6
  20.5 0.6 fusion.57
  21.1 0.7 iota_compare_fusion.1
  21.8 0.7 fusion.70
  22.5 4.4 %collective-permute-start.3 = (bf16[1,32,3,512]{3,2,1,0:T(4,128)(2,1)S(1)}, bf16[1,32,3,512]{3,2,1,0:T(4,128)(2,1)S(1)}, u32[]{:S(2)}, u32[]{:S(2)}) collective-permute-start(bf16[1,32,3,512]{3,2,1,0:T(4,128)(2,1)S(1)} %get-tuple-element.33), channel_id=1, source_target_pairs={{1,0},{2,1},{3,2},{4,3},{5,4},{6,5},{7,6},{8,7},{9,8},{10,9},{11,1... | collective-permute-start | bytes 294920 | tf_op jit(solution)/shard_map/ppermute | solution.py:20
  27.0 32.5 %all-gather.2.cloned.1.call-done = bf16[16,81,512]{2,1,0:T(8,128)(2,1)} async-done(((bf16[1,81,512]{2,1,0:T(8,128)(2,1)}), bf16[16,81,512]{2,1,0:T(8,128)(2,1)}) %all-gather.2.cloned.1.call-update) | async-done | bytes 1327120 | tf_op jit(solution)/shard_map/all_gather | solution.py:210
  59.5 1.8 %copy.135 = bf16[2,8,81,512]{3,1,2,0:T(8,128)(2,1)S(1)} copy(bf16[2,8,81,512]{3,2,1,0:T(8,128)(2,1)} %bitcast.129) | data formatting | bytes 2654208
  61.4 0.2 slice_reduce_fusion.1
  61.9 0.1 copy.114
  62.2 0.1 copy.115
  62.4 0.2 copy.117
  62.6 0.6 copy.113
  63.2 0.6 copy.116
  64.1 0.6 iota_compare_fusion.4
  64.7 0.5 fusion.54
  65.2 0.3 copy.136
  65.9 1.1 %fusion.6 = bf16[16,2,10,512]{3,0,2,1:T(8,128)(2,1)S(1)} fusion(bf16[1,2,8,512]{3,0,1,2:T(2,128)(2,1)} %copy.116, bf16[15,2,8,512]{3,0,1,2:T(8,128)(2,1)S(1)} %copy.115, bf16[15,2,8,512]{3,0,1,2:T(8,128)(2,1)S(1)} %copy.114, bf16[1,2,8,512]{3,0,1,2:T(2,128)(2,1)} %copy.113, bf16[16,2,8,512]{3,0,1,2:T(8,128)(2,1)S(1)} %copy.117, ...), kind=kOutput, calls=%fused_computation.12 | convolution fusion | flops 12289024 | bytes 1114688 | tf_op jit(solution)/shard_map/...nf,nfrwc->...rwc/dot_general | solution.py:151
  66.9 0.2 reverse_select_fusion
  67.2 0.5 fusion.7
  67.8 0.2 copy.140
  68.0 0.3 copy_dynamic-update-slice_fusion
  68.3 0.4 fusion.68
  68.7 0.2 fusion.67
  68.9 0.3 fusion
  69.3 0.5 copy-done.10
  69.9 0.4 fusion.11
  70.3 0.2 broadcast_select_fusion
  70.5 0.1 broadcast_select_fusion.1
  70.6 0.1 fusion.75
  70.9 0.3 constant_dynamic-update-slice_fusion.1
  71.2 0.2 reshape.231
  71.4 1.4 %convolution_convert_fusion.v_ref = bf16[640,512]{1,0:T(8,128)(2,1)} fusion(bf16[512,512]{1,0:T(8,128)(2,1)S(1)} %copy-done, bf16[532,512]{1,0:T(8,128)(2,1)S(1)} %reshape.231), kind=kOutput, calls=%fused_computation.8 | convolution fusion | flops 335872000 | bytes 1724416 | tf_op jit(solution)/shard_map/dot_general | solution.py:76
  72.8 1.4 %convolution_convert_fusion.1.k_ref = bf16[640,512]{1,0:T(8,128)(2,1)} fusion(bf16[512,512]{1,0:T(8,128)(2,1)S(1)} %copy-done.7, bf16[532,512]{1,0:T(8,128)(2,1)S(1)} %reshape.231), kind=kOutput, calls=%fused_computation.9 | convolution fusion | flops 335872000 | bytes 1724416 | tf_op jit(solution)/shard_map/dot_general | solution.py:76
  74.1 1.0 %convolution_convert_fusion.2.q_ref = bf16[256,512]{1,0:T(8,128)(2,1)} fusion(bf16[512,512]{1,0:T(8,128)(2,1)S(1)} %copy-done.8, bf16[1,14,512]{2,1,0:T(8,128)(2,1)S(1)} %get-tuple-element.13, bf16[30,14,512]{2,1,0:T(8,128)(2,1)S(1)} %get-tuple-element.15, bf16[1,14,512]{2,1,0:T(8,128)(2,1)S(1)} %get-tuple-element.17), kind=kOutput, calls=%fused_computation.14 | convolution fusion | flops 135135232 | bytes 1245184 | tf_op jit(solution)/shard_map/dot_general | solution.py:76
  75.2 7.0 %shard_map.82 = bf16[256,512]{1,0:T(8,128)(2,1)} custom-call(bf16[256,512]{1,0:T(8,128)(2,1)} %convolution_convert_fusion.2.q_ref, bf16[640,512]{1,0:T(8,128)(2,1)} %convolution_convert_fusion.1.k_ref, bf16[640,512]{1,0:T(8,128)(2,1)} %convolution_convert_fusion.v_ref, bf16[32,8,512]{2,1,0:T(8,128)(2,1)} %bitcast.123, bf16[512,512]{1,0:T(8,128)(2,1)} %wo_ref.1), custom_call_target="tpu_custom_call" | custom-call | tf_op jit(solution)/shard_map/pallas_call | solution.py:130
  (95 shorter events, 2.7 us)
Async XLA Ops:
  6.5 64.9 %copy-start = (bf16[512,512]{1,0:T(8,128)(2,1)S(1)}, bf16[512,512]{1,0:T(8,128)(2,1)}, u32[]{:S(2)}) copy-start(bf16[512,512]{1,0:T(8,128)(2,1)} %param.13) | copy-start | bytes 1572868
  6.5 9.0 %copy-start.1 = (f32[1,9,32,8]{2,3,1,0:T(8,128)S(1)}, f32[1,9,32,8]{2,3,1,0:T(8,128)}, u32[]{:S(2)}) copy-start(f32[1,9,32,8]{2,3,1,0:T(8,128)} %param.10) | copy-start | bytes 27652
  6.5 10.0 %copy-start.2 = (s32[1,2,3]{2,1,0:T(2,128)S(1)}, s32[1,2,3]{2,1,0:T(2,128)}, u32[]{:S(2)}) copy-start(s32[1,2,3]{2,1,0:T(2,128)} %param.15) | copy-start | bytes 76
  6.5 52.9 %all-gather.2.cloned.1.call-start = ((), (), s32[]{:S(2)}) async-start(), calls=%async_computation | async-start | bytes 1531904 | tf_op jit(solution)/shard_map/all_gather | solution.py:210
  8.9 7.8 %collective-permute-start = (bf16[1,32,1,512]{3,2,1,0:T(2,128)(2,1)S(1)}, bf16[1,32,1,512]{3,2,1,0:T(2,128)(2,1)S(1)}, u32[]{:S(2)}, u32[]{:S(2)}) collective-permute-start(bf16[1,32,1,512]{3,2,1,0:T(2,128)(2,1)S(1)} %get-tuple-element.38), channel_id=1, source_target_pairs={{0,1},{1,2},{2,3},{3,4},{4,5},{5,6},{6,7},{7,8},{8,9},{9,10},{10,1... | collective-permute-start | bytes 98312 | tf_op jit(solution)/shard_map/ppermute | solution.py:19
  9.4 7.3 %collective-permute-start.1 = (bf16[1,32,1,512]{3,2,1,0:T(2,128)(2,1)S(1)}, bf16[1,32,1,512]{3,2,1,0:T(2,128)(2,1)S(1)}, u32[]{:S(2)}, u32[]{:S(2)}) collective-permute-start(bf16[1,32,1,512]{3,2,1,0:T(2,128)(2,1)S(1)} %get-tuple-element.39), channel_id=1, source_target_pairs={{1,0},{2,1},{3,2},{4,3},{5,4},{6,5},{7,6},{8,7},{9,8},{10,9},{11,1... | collective-permute-start | bytes 98312 | tf_op jit(solution)/shard_map/ppermute | solution.py:20
  22.5 48.4 %collective-permute-start.2 = (bf16[1,32,3,512]{3,2,1,0:T(4,128)(2,1)}, bf16[1,32,3,512]{3,2,1,0:T(4,128)(2,1)S(1)}, u32[]{:S(2)}, u32[]{:S(2)}) collective-permute-start(bf16[1,32,3,512]{3,2,1,0:T(4,128)(2,1)} %get-tuple-element.32), channel_id=1, source_target_pairs={{0,1},{1,2},{2,3},{3,4},{4,5},{5,6},{6,7},{7,8},{8,9},{9,10},{10,1... | collective-permute-start | bytes 294920 | tf_op jit(solution)/shard_map/ppermute | solution.py:19
  22.5 48.4 %collective-permute-start.3 = (bf16[1,32,3,512]{3,2,1,0:T(4,128)(2,1)S(1)}, bf16[1,32,3,512]{3,2,1,0:T(4,128)(2,1)S(1)}, u32[]{:S(2)}, u32[]{:S(2)}) collective-permute-start(bf16[1,32,3,512]{3,2,1,0:T(4,128)(2,1)S(1)} %get-tuple-element.33), channel_id=1, source_target_pairs={{1,0},{2,1},{3,2},{4,3},{5,4},{6,5},{7,6},{8,7},{9,8},{10,9},{11,1... | collective-permute-start | bytes 294920 | tf_op jit(solution)/shard_map/ppermute | solution.py:20
  65.5 1.4 %copy-start.6 = (pred[16,2]{0,1:T(4,128)(4,1)S(1)}, pred[16,2]{0,1:T(4,128)(4,1)}, u32[]{:S(2)}) copy-start(pred[16,2]{0,1:T(4,128)(4,1)} %fusion.54) | copy-start | bytes 100
  65.5 1.6 %copy-start.3 = (pred[8,10]{1,0:T(8,128)(4,1)S(1)}, pred[8,10]{1,0:T(8,128)(4,1)}, u32[]{:S(2)}) copy-start(pred[8,10]{1,0:T(8,128)(4,1)} %get-tuple-element.67) | copy-start | bytes 244
  65.5 1.6 %copy-start.9 = (pred[8,10]{1,0:T(8,128)(4,1)S(1)}, pred[8,10]{1,0:T(8,128)(4,1)}, u32[]{:S(2)}) copy-start(pred[8,10]{1,0:T(8,128)(4,1)} %iota_compare_fusion.3) | copy-start | bytes 244
  69.2 0.6 copy-start.10
  69.2 0.7 copy-start.11
  69.3 1.0 %copy-start.5 = (pred[2]{0:T(512)(128)(4,1)S(1)}, pred[2]{0:T(512)(128)(4,1)}, u32[]{:S(2)}) copy-start(pred[2]{0:T(512)(128)(4,1)} %get-tuple-element.62) | copy-start | bytes 10
  69.3 1.2 %copy-start.4 = (pred[2]{0:T(512)(128)(4,1)S(1)}, pred[2]{0:T(512)(128)(4,1)}, u32[]{:S(2)}) copy-start(pred[2]{0:T(512)(128)(4,1)} %get-tuple-element.61) | copy-start | bytes 10
  71.2 1.5 %copy-start.7 = (bf16[512,512]{1,0:T(8,128)(2,1)S(1)}, bf16[512,512]{1,0:T(8,128)(2,1)}, u32[]{:S(2)}) copy-start(bf16[512,512]{1,0:T(8,128)(2,1)} %param.12) | copy-start | bytes 1572868
  72.8 1.4 %copy-start.8 = (bf16[512,512]{1,0:T(8,128)(2,1)S(1)}, bf16[512,512]{1,0:T(8,128)(2,1)}, u32[]{:S(2)}) copy-start(bf16[512,512]{1,0:T(8,128)(2,1)} %param.11) | copy-start | bytes 1572868
Sparse Core Ops, SparseCore 0:
  18.6 40.8 all-gather.1

commit v7 on v5

--- a/solution.py
+++ b/solution.py
@@ -79,7 +79,12 @@
     )
 
 
-def attention_kernel(q_ref, k_ref, v_ref, lat_ref, wo_ref, out_ref, att_ref):
+def attention_kernel(
+    sm_ref, field_ref, wq_ref, wk_ref, wv_ref, lat_ref, wo_ref, out_ref, att_ref, q_ref, k_ref, v_ref
+):
+    q_ref[...] = jnp.dot(sm_ref[...], wq_ref[...], preferred_element_type=jnp.float32).astype(q_ref.dtype)
+    k_ref[...] = jnp.dot(field_ref[...], wk_ref[...], preferred_element_type=jnp.float32).astype(k_ref.dtype)
+    v_ref[...] = jnp.dot(field_ref[...], wv_ref[...], preferred_element_type=jnp.float32).astype(v_ref.dtype)
     cells, channels = q_ref.shape
     positions = k_ref.shape[0]
     rows, cols = lat_ref.shape[0], lat_ref.shape[1]
@@ -118,22 +123,25 @@
     out_ref[...] = (lat.astype(jnp.float32) + mixed).astype(out_ref.dtype)
 
 
-def attend_and_mix(query, field_pad, w_key, w_value, own_tile, w_output):
+def attend_and_mix(smoothed, field_pad, w_query, w_key, w_value, own_tile, w_output):
     rows, cols, channels = own_tile.shape
     cells = rows * cols
     flat = field_pad.reshape(-1, channels)
     positions = -(-flat.shape[0] // 128) * 128
     flat = jnp.pad(flat, ((0, positions - flat.shape[0]), (0, 0)))
-    key_flat = project(flat, w_key)
-    value_flat = project(flat, w_value)
     vmem = pl.BlockSpec(memory_space=pltpu.VMEM)
     out = pl.pallas_call(
         attention_kernel,
         out_shape=jax.ShapeDtypeStruct((cells, channels), own_tile.dtype),
-        in_specs=[vmem] * 5,
+        in_specs=[vmem] * 7,
         out_specs=vmem,
-        scratch_shapes=[pltpu.VMEM((cells, channels), jnp.bfloat16)],
-    )(query.reshape(cells, channels), key_flat, value_flat, own_tile, w_output)
+        scratch_shapes=[
+            pltpu.VMEM((cells, channels), jnp.bfloat16),
+            pltpu.VMEM((cells, channels), jnp.bfloat16),
+            pltpu.VMEM((positions, channels), jnp.bfloat16),
+            pltpu.VMEM((positions, channels), jnp.bfloat16),
+        ],
+    )(smoothed.reshape(cells, channels), flat, w_query, w_key, w_value, own_tile, w_output)
     return out.reshape(rows, cols, channels)
 
 
@@ -164,14 +172,13 @@
     received = pick_all(seam_rows, got1[:, :, None])
     padded = place_rims(widened[0], received, seam_rows)
     smoothed = smooth(padded, metric[0])
-    query = project(smoothed, w_query)
     field_wide = padded_2(smoothed[None], (("blk", 2),), RADIUS)
     rows3 = jnp.concatenate([smoothed[:RADIUS], smoothed[-RADIUS:]], axis=0)
     got3 = widen_tiles(lax.all_gather(rows3[None], "blk", axis=0, tiled=True), RADIUS)
     edges3 = jnp.stack([got3[:, :RADIUS], got3[:, RADIUS:]], axis=1)
     field_got = pick_all(seam_rows, edges3)
     field_pad = place_rims(field_wide[0], field_got, seam_rows)
-    return attend_and_mix(query, field_pad, w_key, w_value, own_tile, w_output)[None]
+    return attend_and_mix(smoothed, field_pad, w_query, w_key, w_value, own_tile, w_output)[None]
 
 
 def solution(mesh):

time: 72.7 us -> 73.9 us (1.017)
  matrix products: 4.43 us -> 0.74 us
  other arithmetic: 7.1 us -> 9.42 us
  local copies, waits for them, and re-layouts: 3.82 us -> 5.33 us
  Pallas kernels: 7 us -> 8.15 us
    dot_general x3 -> x0, matrix products: 3.69 us -> none  [project(): jnp.dot(flat, weight, preferred_element_type=jnp.float32)]
    reshape x0 -> x1, other arithmetic: none -> 1.71 us  [attend_and_mix(): smoothed.reshape(cells, channels)]
    pallas_call x1, Pallas kernels: 7 us -> 8.15 us  [attend_and_mix(): pl.pallas_call(attention_kernel, out_shape=jax.ShapeDtypeStruct((cells, c...]
    pad x0 -> x1, local copies, waits for them, and re-layouts: none -> 0.89 us  [attend_and_mix(): flat = jnp.pad(flat, ((0, positions - flat.shape[0]), (0, 0)))]
    slice x1, local copies, waits for them, and re-layouts: 0.21 us -> 1 us  [orient_rims(): orient = seam_pair[:, 2]]
where the time goes in v7:
time: 73.9 us; the launch traced here: 73.7 us
  blocking collectives  39.6 us (54%)
  starting transfers between devices  10.1 us (14%)
  other arithmetic  9.42 us (13%)
  Pallas kernels  8.15 us (11%)
  local copies, waits for them, and re-layouts  5.33 us (7%)
  matrix products  0.74 us (1%)
    all_gather x1, blocking collectives, local(): lax.all_gather(rows1[None], 'blk', axis=0, tiled=True)  20 us
    all_gather x1, blocking collectives, local(): lax.all_gather(rows3[None], 'blk', axis=0, tiled=True)  19.6 us
    ppermute x2, starting transfers between devices, padded_2(): after = lax.ppermute(first, axis, down)  9.15 us
    pallas_call x1, Pallas kernels, attend_and_mix(): pl.pallas_call(attention_kernel, out_shape=jax.ShapeDtypeStruct((cells, c...  8.15 us
    convert_element_type x2, other arithmetic, normalize(): return (values * factor * norm_gain).astype(jnp.bfloat16)  2.19 us
    reshape x1, other arithmetic, attend_and_mix(): smoothed.reshape(cells, channels)  1.71 us
  transfers between devices with their start and end apart: 4, of which 0 were waited for; matrix products, arithmetic and copies ran while one was open for 10% of the time, Pallas kernels for 0%

profile of v7, /device:TPU:0, one launch (start us, length us, event | category | flops | bytes accessed | tf_op | source)
XLA Modules:
  0.0 73.7 jit_solution(16079311175873226317)
XLA Ops:
  0.0 1.1 %fusion.13 = f32[32,8]{1,0:T(8,128)S(1)} fusion(bf16[1,32,8,512]{3,2,1,0:T(8,128)(2,1)} %param.8), kind=kLoop, calls=%fused_computation.21 | loop fusion | flops 392960 | bytes 263168 | tf_op jit(solution)/shard_map/reduce_sum | solution.py:27
  1.1 1.1 %multiply_convert_fusion = bf16[1,32,8,512]{3,2,1,0:T(8,128)(2,1)S(1)} fusion(bf16[1,32,8,512]{3,2,1,0:T(8,128)(2,1)} %param.8, f32[512]{0:T(512)} %param.9, f32[32,8]{1,0:T(8,128)S(1)} %add_rsqrt_fusion), kind=kLoop, calls=%fused_computation.27 | loop fusion | flops 524288 | bytes 527360 | tf_op jit(solution)/shard_map/convert_element_type | solution.py:28
  2.2 0.1 fusion.41
  2.3 0.5 collective-permute-start
  2.8 5.1 %collective-permute-start.1 = (bf16[1,32,1,512]{3,2,1,0:T(2,128)(2,1)S(1)}, bf16[1,32,1,512]{3,2,1,0:T(2,128)(2,1)S(1)}, u32[]{:S(2)}, u32[]{:S(2)}) collective-permute-start(bf16[1,32,1,512]{3,2,1,0:T(2,128)(2,1)S(1)} %get-tuple-element.25), channel_id=1, source_target_pairs={{1,0},{2,1},{3,2},{4,3},{5,4},{6,5},{7,6},{8,7},{9,8},{10,9},{11,1... | collective-permute-start | bytes 98312 | tf_op jit(solution)/shard_map/ppermute | solution.py:20
  7.9 0.9 %compare_reduce_fusion = pred[2]{0:T(512)(128)(4,1)S(1)} fusion(s32[2,3]{1,0:T(2,128)} %bitcast.80), kind=kLoop, calls=%fused_computation.76 | loop fusion | flops 24 | bytes 10 | tf_op jit(solution)/shard_map/eq | solution.py:47
  8.7 1.0 %slice_reduce_fusion.2 = (s32[2]{0:T(128)S(1)}, s32[2]{0:T(128)S(1)}, s32[2]{0:T(128)S(1)}) fusion(s32[2,3]{1,0:T(2,128)} %bitcast.81), kind=kLoop, calls=%fused_computation.86 | loop fusion | bytes 48 | tf_op jit(solution)/shard_map/slice | solution.py:46
  9.7 1.1 %fusion.15 = bf16[32,8,512]{2,1,0:T(8,128)(2,1)S(1)} fusion(f32[512]{0:T(512)} %param.9, f32[32,8]{1,0:T(8,128)S(1)} %add_rsqrt_fusion, bf16[1,32,8,512]{3,2,1,0:T(8,128)(2,1)} %param.8), kind=kLoop, calls=%fused_computation.23 | loop fusion | flops 524288 | bytes 527360 | tf_op jit(solution)/shard_map/convert_element_type | solution.py:28
  10.9 20.0 %all-gather = bf16[32,8,512]{2,1,0:T(8,128)(2,1)S(1)} all-gather(bf16[2,8,512]{2,1,0:T(8,128)(2,1)S(1)} %pad_maximum_fusion.8), channel_id=2, replica_groups=mesh['group'=2,'blk'=16] {'blk'}, dimensions={0}, use_global_device_ids=true | all-gather | bytes 278528 | tf_op jit(solution)/shard_map/all_gather | solution.py:171
  31.1 0.2 copy.118
  31.3 0.1 copy.116
  31.4 0.1 copy.115
  31.6 0.3 fusion.12
  31.9 0.1 broadcast_select_fusion.2
  32.0 0.1 copy.113
  32.1 0.1 copy.125
  32.2 0.1 copy.124
  32.3 0.1 copy.123
  32.3 0.1 copy.122
  32.4 0.1 copy.121
  32.5 0.1 copy.120
  32.6 0.1 copy.128
  32.6 0.1 copy.127
  32.8 0.3 maximum_bitcast_fusion
  33.1 1.1 %fusion.44 = bf16[1,32,8,512]{3,2,1,0:T(8,128)(2,1)S(1)} fusion(bf16[1,10,512]{2,1,0:T(8,128)(2,1)S(1)} %copy.126, bf16[32,10,512]{2,1,0:T(8,128)(2,1)S(1)} %maximum_bitcast_fusion, f32[32,8]{1,0:T(8,128)S(1)} %copy.128, f32[32,8]{1,0:T(8,128)S(1)} %copy.127, f32[32,8]{1,0:T(8,128)S(1)} %copy.125, f32[32,8]{1,0:T(8,128)S(1)} %copy.124, ...), kind=kLoop, calls=%fused_computation.99 | loop fusion | flops 5898240 | bytes 1753088 | tf_op jit(solution)/shard_map/broadcast_in_dim | solution.py:175
  34.1 1.7 %fusion.45.sm_ref = bf16[256,512]{1,0:T(8,128)(2,1)} fusion(bf16[1,10,512]{2,1,0:T(8,128)(2,1)S(1)} %copy.126, bf16[32,10,512]{2,1,0:T(8,128)(2,1)S(1)} %maximum_bitcast_fusion, f32[32,8]{1,0:T(8,128)S(1)} %copy.128, f32[32,8]{1,0:T(8,128)S(1)} %copy.127, f32[32,8]{1,0:T(8,128)S(1)} %copy.125, f32[32,8]{1,0:T(8,128)S(1)} %copy.124, f32[32,8]{1,0:T(8,128)S(1)} %copy.123, ...), kind=kLoop, calls=%fused_computation.100 | loop fusion | flops 5898240 | bytes 1753088 | tf_op jit(solution)/shard_map/reshape | solution.py:144
  35.8 1.0 %add_convert_fusion = bf16[32,8,512]{2,1,0:T(8,128)(2,1)S(1)} fusion(bf16[32,10,512]{2,1,0:T(8,128)(2,1)S(1)} %maximum_bitcast_fusion, bf16[1,10,512]{2,1,0:T(8,128)(2,1)S(1)} %copy.126, bf16[1,10,512]{2,1,0:T(8,128)(2,1)S(1)} %copy.119, f32[32,8]{1,0:T(8,128)S(1)} %copy.128, f32[32,8]{1,0:T(8,128)S(1)} %copy.127, f32[32,8]{1,0:T(8,128)S(1)} %copy.125, ...), kind=kLoop, calls=%fused_computation.26 | loop fusion | flops 5898240 | bytes 1753088 | tf_op jit(solution)/shard_map/convert_element_type | solution.py:69
  36.9 19.6 %all-gather.1 = bf16[96,8,512]{2,1,0:T(8,128)(2,1)S(1)} all-gather(bf16[6,8,512]{2,1,0:T(8,128)(2,1)S(1)} %pad_maximum_fusion.7), channel_id=3, replica_groups=mesh['group'=2,'blk'=16] {'blk'}, dimensions={0}, use_global_device_ids=true | all-gather | bytes 835584 | tf_op jit(solution)/shard_map/all_gather | solution.py:177
  56.5 0.1 fusion.36
  56.6 0.1 fusion.37
  56.7 0.4 collective-permute-start.2
  57.1 4.1 %collective-permute-start.3 = (bf16[1,32,3,512]{3,2,1,0:T(4,128)(2,1)S(1)}, bf16[1,32,3,512]{3,2,1,0:T(4,128)(2,1)S(1)}, u32[]{:S(2)}, u32[]{:S(2)}) collective-permute-start(bf16[1,32,3,512]{3,2,1,0:T(4,128)(2,1)S(1)} %get-tuple-element.15), channel_id=1, source_target_pairs={{1,0},{2,1},{3,2},{4,3},{5,4},{6,5},{7,6},{8,7},{9,8},{10,9},{11,1... | collective-permute-start | bytes 294920 | tf_op jit(solution)/shard_map/ppermute | solution.py:20
  61.2 0.1 copy.129
  61.3 0.1 copy.132
  61.4 0.4 copy.133
  61.8 0.4 copy.131
  62.2 0.4 copy.130
  62.7 0.3 fusion
  63.0 0.2 slice_bitcast_fusion.1
  63.1 0.4 fusion.9
  63.6 0.2 broadcast_select_fusion
  63.7 0.1 broadcast_select_fusion.1
  63.9 0.1 fusion.42
  64.1 0.3 maximum_bitcast_fusion.1
  64.4 0.1 pad_maximum_fusion.2
  64.5 0.2 reshape.98
  64.6 0.9 %pad.4.field_ref = bf16[640,512]{1,0:T(8,128)(2,1)} pad(bf16[532,512]{1,0:T(8,128)(2,1)S(1)} %reshape.98, bf16[]{:T(256)} %constant.43.clone.1), padding=0_108x0_0 | pad | bytes 1200130 | tf_op jit(solution)/shard_map/jit(_pad)/pad | solution.py:131
  65.5 8.2 %shard_map.82 = bf16[256,512]{1,0:T(8,128)(2,1)} custom-call(bf16[256,512]{1,0:T(8,128)(2,1)} %fusion.45.sm_ref, bf16[640,512]{1,0:T(8,128)(2,1)} %pad.4.field_ref, bf16[512,512]{1,0:T(8,128)(2,1)} %wq_ref.1, bf16[512,512]{1,0:T(8,128)(2,1)} %wk_ref.1, bf16[512,512]{1,0:T(8,128)(2,1)} %wv_ref.1, bf16[32,8,512]{2,1,0:T(8,128)(2,1)} %bitcast.74, ...), custom_call_target="tpu_custom_call" | custom-call | tf_op jit(solution)/shard_map/pallas_call | solution.py:133
  (24 shorter events, 0.3 us)
Async XLA Ops:
  1.1 29.9 %copy-start = (f32[1,9,32,8]{2,3,1,0:T(8,128)S(1)}, f32[1,9,32,8]{2,3,1,0:T(8,128)}, u32[]{:S(2)}) copy-start(f32[1,9,32,8]{2,3,1,0:T(8,128)} %param.10) | copy-start | bytes 27652
  2.3 30.4 %collective-permute-start = (bf16[1,32,1,512]{3,2,1,0:T(2,128)(2,1)S(1)}, bf16[1,32,1,512]{3,2,1,0:T(2,128)(2,1)S(1)}, u32[]{:S(2)}, u32[]{:S(2)}) collective-permute-start(bf16[1,32,1,512]{3,2,1,0:T(2,128)(2,1)S(1)} %get-tuple-element.24), channel_id=1, source_target_pairs={{0,1},{1,2},{2,3},{3,4},{4,5},{5,6},{6,7},{7,8},{8,9},{9,10},{10,1... | collective-permute-start | bytes 98312 | tf_op jit(solution)/shard_map/ppermute | solution.py:19
  2.8 30.0 %collective-permute-start.1 = (bf16[1,32,1,512]{3,2,1,0:T(2,128)(2,1)S(1)}, bf16[1,32,1,512]{3,2,1,0:T(2,128)(2,1)S(1)}, u32[]{:S(2)}, u32[]{:S(2)}) collective-permute-start(bf16[1,32,1,512]{3,2,1,0:T(2,128)(2,1)S(1)} %get-tuple-element.25), channel_id=1, source_target_pairs={{1,0},{2,1},{3,2},{4,3},{5,4},{6,5},{7,6},{8,7},{9,8},{10,9},{11,1... | collective-permute-start | bytes 98312 | tf_op jit(solution)/shard_map/ppermute | solution.py:20
  56.7 7.3 %collective-permute-start.2 = (bf16[1,32,3,512]{3,2,1,0:T(4,128)(2,1)S(1)}, bf16[1,32,3,512]{3,2,1,0:T(4,128)(2,1)S(1)}, u32[]{:S(2)}, u32[]{:S(2)}) collective-permute-start(bf16[1,32,3,512]{3,2,1,0:T(4,128)(2,1)S(1)} %get-tuple-element.14), channel_id=1, source_target_pairs={{0,1},{1,2},{2,3},{3,4},{4,5},{5,6},{6,7},{7,8},{8,9},{9,10},{10,1... | collective-permute-start | bytes 294920 | tf_op jit(solution)/shard_map/ppermute | solution.py:19
  57.1 6.9 %collective-permute-start.3 = (bf16[1,32,3,512]{3,2,1,0:T(4,128)(2,1)S(1)}, bf16[1,32,3,512]{3,2,1,0:T(4,128)(2,1)S(1)}, u32[]{:S(2)}, u32[]{:S(2)}) collective-permute-start(bf16[1,32,3,512]{3,2,1,0:T(4,128)(2,1)S(1)} %get-tuple-element.15), channel_id=1, source_target_pairs={{1,0},{2,1},{3,2},{4,3},{5,4},{6,5},{7,6},{8,7},{9,8},{10,9},{11,1... | collective-permute-start | bytes 294920 | tf_op jit(solution)/shard_map/ppermute | solution.py:20

commit v8 on v5

--- a/solution.py
+++ b/solution.py
@@ -152,6 +152,23 @@
     return got.astype(edges.dtype)
 
 
+def doubling_gather(block, axis):
+    count = lax.axis_size(axis)
+    if count & (count - 1):
+        return lax.all_gather(block, axis, axis=0, tiled=True)
+    me = lax.axis_index(axis)
+    held = block
+    step = 1
+    while step < count:
+        other = lax.ppermute(held, axis, [(i, i ^ step) for i in range(count)])
+        low = (me & step) == 0
+        held = jnp.where(
+            low, jnp.concatenate([held, other], axis=0), jnp.concatenate([other, held], axis=0)
+        )
+        step *= 2
+    return held
+
+
 def local(latents, norm_gain, metric, w_query, w_key, w_value, w_output, seam_table):
     own_tile = latents[0]
     channels = own_tile.shape[-1]
@@ -160,14 +177,14 @@
     seam_rows = seam_table[0]
     widened = padded_2(normed[None], (("blk", 2),), margin)
     rows1 = jnp.stack([normed[0], normed[-1]])
-    got1 = widen_tiles(lax.all_gather(rows1[None], "blk", axis=0, tiled=True), 1)
+    got1 = widen_tiles(doubling_gather(rows1[None], "blk"), 1)
     received = pick_all(seam_rows, got1[:, :, None])
     padded = place_rims(widened[0], received, seam_rows)
     smoothed = smooth(padded, metric[0])
     query = project(smoothed, w_query)
     field_wide = padded_2(smoothed[None], (("blk", 2),), RADIUS)
     rows3 = jnp.concatenate([smoothed[:RADIUS], smoothed[-RADIUS:]], axis=0)
-    got3 = widen_tiles(lax.all_gather(rows3[None], "blk", axis=0, tiled=True), RADIUS)
+    got3 = widen_tiles(doubling_gather(rows3[None], "blk"), RADIUS)
     edges3 = jnp.stack([got3[:, :RADIUS], got3[:, RADIUS:]], axis=1)
     field_got = pick_all(seam_rows, edges3)
     field_pad = place_rims(field_wide[0], field_got, seam_rows)

time: 72.7 us -> 72.3 us (level)
  blocking collectives: 39.6 us -> 0 us
  waiting for transfers between devices: 0.01 us -> 35.3 us
  starting transfers between devices: 10.1 us -> 13.7 us
  other arithmetic: 7.1 us -> 8.95 us
  local copies, waits for them, and re-layouts: 3.82 us -> 2.31 us
    all_gather x2 -> x0, blocking collectives: 39.6 us -> none  [the longest x1 20 us: local(): lax.all_gather(rows1[None], 'blk', axis=0, tiled=True)]
    ppermute x0 -> x8, waiting for transfers between devices: none -> 30.5 us  [doubling_gather(): other = lax.ppermute(held, axis, [(i, i ^ step) for i in range(count)])]
    ppermute x2, waiting for transfers between devices: 0.01 us -> 4.72 us  [padded_2(): before = lax.ppermute(last, axis, up)]
    ppermute x0 -> x8, starting transfers between devices: none -> 3.39 us  [doubling_gather(): other = lax.ppermute(held, axis, [(i, i ^ step) for i in range(count)])]
    select_n x0 -> x8, other arithmetic: none -> 1.53 us  [doubling_gather(): jnp.where(low, jnp.concatenate([held, other], axis=0), jnp.concatenate([o...]
    ppermute x2, starting transfers between devices: 9.15 us -> 10.1 us  [padded_2(): after = lax.ppermute(first, axis, down)]
    ppermute x2, starting transfers between devices: 0.91 us -> 0.16 us  [padded_2(): before = lax.ppermute(last, axis, up)]
  transfers between devices with their start and end apart: 4 -> 12, of which waited for: 0 -> 8; matrix products, arithmetic and copies ran while one was open for 10% -> 7% of each run, Pallas kernels for 0% -> 0%
where the time goes in v8:
time: 72.3 us; the launch traced here: 72.1 us
  waiting for transfers between devices  35.3 us (49%)
  starting transfers between devices  13.7 us (19%)
  other arithmetic  8.95 us (12%)
  Pallas kernels  7 us (10%)
  matrix products  4.51 us (6%)
  local copies, waits for them, and re-layouts  2.31 us (3%)
    ppermute x8, waiting for transfers between devices, doubling_gather(): other = lax.ppermute(held, axis, [(i, i ^ step) for i in range(count)])  30.5 us
    ppermute x2, starting transfers between devices, padded_2(): after = lax.ppermute(first, axis, down)  10.1 us
    pallas_call x1, Pallas kernels, attend_and_mix(): pl.pallas_call(attention_kernel, out_shape=jax.ShapeDtypeStruct((cells, c...  7 us
    ppermute x2, waiting for transfers between devices, padded_2(): before = lax.ppermute(last, axis, up)  4.72 us
    dot_general x3, matrix products, project(): jnp.dot(flat, weight, preferred_element_type=jnp.float32)  3.71 us
    ppermute x8, starting transfers between devices, doubling_gather(): other = lax.ppermute(held, axis, [(i, i ^ step) for i in range(count)])  3.39 us
    convert_element_type x2, other arithmetic, normalize(): return (values * factor * norm_gain).astype(jnp.bfloat16)  2.17 us
    select_n x8, other arithmetic, doubling_gather(): jnp.where(low, jnp.concatenate([held, other], axis=0), jnp.concatenate([o...  1.53 us
  transfers between devices with their start and end apart: 12, of which 8 were waited for; matrix products, arithmetic and copies ran while one was open for 7% of the time, Pallas kernels for 0%

profile of v8, /device:TPU:0, one launch (start us, length us, event | category | flops | bytes accessed | tf_op | source)
XLA Modules:
  0.0 72.1 jit_solution(6835977611104861682)
XLA Ops:
  0.0 1.1 %fusion.15 = f32[32,8]{1,0:T(8,128)S(1)} fusion(bf16[1,32,8,512]{3,2,1,0:T(8,128)(2,1)} %param.8), kind=kLoop, calls=%fused_computation.27 | loop fusion | flops 392960 | bytes 263168 | tf_op jit(solution)/shard_map/reduce_sum | solution.py:27
  1.2 1.1 %fusion.17 = bf16[32,8,512]{2,1,0:T(8,128)(2,1)S(1)} fusion(f32[512]{0:T(512)} %param.9, f32[32,8]{1,0:T(8,128)S(1)} %add_rsqrt_fusion, bf16[1,32,8,512]{3,2,1,0:T(8,128)(2,1)} %param.8), kind=kLoop, calls=%fused_computation.29 | loop fusion | flops 524288 | bytes 527360 | tf_op jit(solution)/shard_map/convert_element_type | solution.py:28
  2.3 0.5 collective-permute-start
  2.8 1.1 %multiply_convert_fusion = bf16[1,32,8,512]{3,2,1,0:T(8,128)(2,1)S(1)} fusion(bf16[1,32,8,512]{3,2,1,0:T(8,128)(2,1)} %param.8, f32[512]{0:T(512)} %param.9, f32[32,8]{1,0:T(8,128)S(1)} %add_rsqrt_fusion), kind=kLoop, calls=%fused_computation.37 | loop fusion | flops 524288 | bytes 527360 | tf_op jit(solution)/shard_map/convert_element_type | solution.py:28
  3.9 0.1 fusion.43
  4.0 0.1 collective-permute-start.4
  4.1 5.7 %collective-permute-start.5 = (bf16[1,32,1,512]{3,2,1,0:T(2,128)(2,1)S(1)}, bf16[1,32,1,512]{3,2,1,0:T(2,128)(2,1)S(1)}, u32[]{:S(2)}, u32[]{:S(2)}) collective-permute-start(bf16[1,32,1,512]{3,2,1,0:T(2,128)(2,1)S(1)} %get-tuple-element.25), channel_id=1, source_target_pairs={{1,0},{2,1},{3,2},{4,3},{5,4},{6,5},{7,6},{8,7},{9,8},{10,9},{11,1... | collective-permute-start | bytes 98312 | tf_op jit(solution)/shard_map/ppermute | solution.py:20
  9.8 0.2 slice_reduce_fusion.2
  10.1 3.9 %collective-permute-done.1 = bf16[2,2,8,512]{3,2,1,0:T(8,128)(2,1)S(1)} collective-permute-done((bf16[2,2,8,512]{3,2,1,0:T(8,128)(2,1)S(1)}, bf16[2,2,8,512]{3,2,1,0:T(8,128)(2,1)S(1)}, u32[]{:S(2)}, u32[]{:S(2)}) %collective-permute-start.1) | collective-permute-done | bytes 32800 | tf_op jit(solution)/shard_map/ppermute | solution.py:163
  14.2 4.6 %collective-permute-done.2 = bf16[4,2,8,512]{3,2,1,0:T(8,128)(2,1)S(1)} collective-permute-done((bf16[4,2,8,512]{3,2,1,0:T(8,128)(2,1)S(1)}, bf16[4,2,8,512]{3,2,1,0:T(8,128)(2,1)S(1)}, u32[]{:S(2)}, u32[]{:S(2)}) %collective-permute-start.2) | collective-permute-done | bytes 65568 | tf_op jit(solution)/shard_map/ppermute | solution.py:163
  18.8 0.7 %collective-permute-start.3 = (bf16[8,2,8,512]{3,2,1,0:T(8,128)(2,1)S(1)}, bf16[8,2,8,512]{3,2,1,0:T(8,128)(2,1)S(1)}, u32[]{:S(2)}, u32[]{:S(2)}) collective-permute-start(bf16[8,2,8,512]{3,2,1,0:T(8,128)(2,1)S(1)} %maximum_select_fusion.4), channel_id=1, source_target_pairs={{0,8},{1,9},{2,10},{3,11},{4,12},{5,13},{6,14},{7,15},{8,0},{9,1},... | collective-permute-start | bytes 393224 | tf_op jit(solution)/shard_map/ppermute | solution.py:163
  19.5 0.2 compare_reduce_fusion
  20.4 0.3 maximum_bitcast_fusion
  20.7 4.4 %collective-permute-done.3 = bf16[8,2,8,512]{3,2,1,0:T(8,128)(2,1)S(1)} collective-permute-done((bf16[8,2,8,512]{3,2,1,0:T(8,128)(2,1)S(1)}, bf16[8,2,8,512]{3,2,1,0:T(8,128)(2,1)S(1)}, u32[]{:S(2)}, u32[]{:S(2)}) %collective-permute-start.3) | collective-permute-done | bytes 131104 | tf_op jit(solution)/shard_map/ppermute | solution.py:163
  25.3 0.3 fusion.18
  25.6 0.4 fusion.12
  25.9 0.1 broadcast_select_fusion.3
  26.1 1.1 %add_convert_fusion = bf16[32,8,512]{2,1,0:T(8,128)(2,1)S(1)} fusion(bf16[32,10,512]{2,1,0:T(8,128)(2,1)S(1)} %maximum_bitcast_fusion, bf16[1,10,512]{2,1,0:T(8,128)(2,1)S(1)} %copy.48, bf16[1,10,512]{2,1,0:T(8,128)(2,1)S(1)} %copy.41, f32[32,8]{1,0:T(8,128)S(1)} %copy.50, f32[32,8]{1,0:T(8,128)S(1)} %copy.49, f32[32,8]{1,0:T(8,128)S(1)} %copy.47, ...), kind=kLoop, calls=%fused_computation.36 | loop fusion | flops 5898240 | bytes 1753088 | tf_op jit(solution)/shard_map/convert_element_type | solution.py:69
  27.2 0.1 copy.52
  27.4 1.3 %collective-permute-done.6 = bf16[1,6,8,512]{3,0,2,1:T(2,128)(2,1)S(1)} collective-permute-done((bf16[1,6,8,512]{3,0,2,1:T(2,128)(2,1)S(1)}, bf16[1,6,8,512]{3,0,2,1:T(2,128)(2,1)S(1)}, u32[]{:S(2)}, u32[]{:S(2)}) %collective-permute-start.6) | collective-permute-done | bytes 49184 | tf_op jit(solution)/shard_map/ppermute | solution.py:163
  28.7 0.4 broadcast_select_fusion
  29.1 0.9 %collective-permute-start.7 = (bf16[2,6,8,512]{3,0,2,1:T(2,128)(2,1)S(1)}, bf16[2,6,8,512]{3,0,2,1:T(2,128)(2,1)S(1)}, u32[]{:S(2)}, u32[]{:S(2)}) collective-permute-start(bf16[2,6,8,512]{3,0,2,1:T(2,128)(2,1)S(1)} %broadcast_select_fusion), channel_id=1, source_target_pairs={{0,2},{1,3},{2,0},{3,1},{4,6},{5,7},{6,4},{7,5},{8,10},{9,11},{10,... | collective-permute-start | bytes 294920 | tf_op jit(solution)/shard_map/ppermute | solution.py:163
  30.0 4.0 %collective-permute-done.7 = bf16[2,6,8,512]{3,0,2,1:T(2,128)(2,1)S(1)} collective-permute-done((bf16[2,6,8,512]{3,0,2,1:T(2,128)(2,1)S(1)}, bf16[2,6,8,512]{3,0,2,1:T(2,128)(2,1)S(1)}, u32[]{:S(2)}, u32[]{:S(2)}) %collective-permute-start.7) | collective-permute-done | bytes 98336 | tf_op jit(solution)/shard_map/ppermute | solution.py:163
  34.0 0.4 maximum_select_fusion.3
  34.5 1.1 %fusion.49 = bf16[1,32,8,512]{3,2,1,0:T(8,128)(2,1)S(1)} fusion(bf16[1,10,512]{2,1,0:T(8,128)(2,1)S(1)} %copy.48, bf16[32,10,512]{2,1,0:T(8,128)(2,1)S(1)} %maximum_bitcast_fusion, f32[32,8]{1,0:T(8,128)S(1)} %copy.50, f32[32,8]{1,0:T(8,128)S(1)} %copy.49, f32[32,8]{1,0:T(8,128)S(1)} %copy.47, f32[32,8]{1,0:T(8,128)S(1)} %copy.46, f32[32,8]{1,0:T(8,128)S(1)} %copy.45, ...), kind=kLoop, calls=%fused_computation.110 | loop fusion | flops 5898240 | bytes 1753088 | tf_op jit(solution)/shard_map/broadcast_in_dim | solution.py:185
  35.5 5.1 %collective-permute-done.8 = bf16[4,6,8,512]{3,0,2,1:T(4,128)(2,1)S(1)} collective-permute-done((bf16[4,6,8,512]{3,0,2,1:T(4,128)(2,1)S(1)}, bf16[4,6,8,512]{3,0,2,1:T(4,128)(2,1)S(1)}, u32[]{:S(2)}, u32[]{:S(2)}) %collective-permute-start.8) | collective-permute-done | bytes 196640 | tf_op jit(solution)/shard_map/ppermute | solution.py:163
  40.6 0.3 maximum_select_fusion.1
  40.9 1.0 %collective-permute-start.9 = (bf16[8,6,8,512]{3,0,2,1:T(8,128)(2,1)S(1)}, bf16[8,6,8,512]{3,0,2,1:T(8,128)(2,1)S(1)}, u32[]{:S(2)}, u32[]{:S(2)}) collective-permute-start(bf16[8,6,8,512]{3,0,2,1:T(8,128)(2,1)S(1)} %maximum_select_fusion.1), channel_id=1, source_target_pairs={{0,8},{1,9},{2,10},{3,11},{4,12},{5,13},{6,14},{7,15},{8,0},{9,1},... | collective-permute-start | bytes 1179656 | tf_op jit(solution)/shard_map/ppermute | solution.py:163
  41.9 0.1 fusion.38
  42.1 4.4 %collective-permute-start.11 = (bf16[1,32,3,512]{3,2,1,0:T(4,128)(2,1)S(1)}, bf16[1,32,3,512]{3,2,1,0:T(4,128)(2,1)S(1)}, u32[]{:S(2)}, u32[]{:S(2)}) collective-permute-start(bf16[1,32,3,512]{3,2,1,0:T(4,128)(2,1)S(1)} %get-tuple-element.15), channel_id=1, source_target_pairs={{1,0},{2,1},{3,2},{4,3},{5,4},{6,5},{7,6},{8,7},{9,8},{10,9},{11,1... | collective-permute-start | bytes 294920 | tf_op jit(solution)/shard_map/ppermute | solution.py:20
  46.5 1.0 %convolution_convert_fusion.2.q_ref = bf16[256,512]{1,0:T(8,128)(2,1)} fusion(bf16[512,512]{1,0:T(8,128)(2,1)S(1)} %copy-done.1, bf16[32,8,512]{2,1,0:T(8,128)(2,1)S(1)} %add_convert_fusion), kind=kOutput, calls=%fused_computation.10 | convolution fusion | flops 134348800 | bytes 1048576 | tf_op jit(solution)/shard_map/dot_general | solution.py:76
  47.5 4.7 %collective-permute-done.10 = bf16[1,32,3,512]{3,2,1,0:T(4,128)(2,1)S(1)} collective-permute-done((bf16[1,32,3,512]{3,2,1,0:T(4,128)(2,1)S(1)}, bf16[1,32,3,512]{3,2,1,0:T(4,128)(2,1)S(1)}, u32[]{:S(2)}, u32[]{:S(2)}) %collective-permute-start.10) | collective-permute-done | bytes 98336 | tf_op jit(solution)/shard_map/ppermute | solution.py:19
  52.2 0.3 maximum_bitcast_fusion.1
  52.5 7.2 %collective-permute-done.9 = bf16[8,6,8,512]{3,0,2,1:T(8,128)(2,1)S(1)} collective-permute-done((bf16[8,6,8,512]{3,0,2,1:T(8,128)(2,1)S(1)}, bf16[8,6,8,512]{3,0,2,1:T(8,128)(2,1)S(1)}, u32[]{:S(2)}, u32[]{:S(2)}) %collective-permute-start.9) | collective-permute-done | bytes 393248 | tf_op jit(solution)/shard_map/ppermute | solution.py:163
  59.8 0.3 maximum_select_fusion
  60.1 0.4 fusion.37
  60.5 0.2 fusion.36
  60.7 0.3 fusion
  61.0 0.2 slice_bitcast_fusion.1
  61.1 0.4 fusion.9
  61.6 0.2 broadcast_select_fusion.1
  61.7 0.1 broadcast_select_fusion.2
  61.9 0.1 fusion.44
  62.1 0.1 pad_maximum_fusion.2
  62.2 0.2 reshape.98
  62.3 1.4 %convolution_convert_fusion.v_ref = bf16[640,512]{1,0:T(8,128)(2,1)} fusion(bf16[512,512]{1,0:T(8,128)(2,1)S(1)} %copy-done, bf16[532,512]{1,0:T(8,128)(2,1)S(1)} %reshape.98), kind=kOutput, calls=%fused_computation.8 | convolution fusion | flops 335872000 | bytes 1724416 | tf_op jit(solution)/shard_map/dot_general | solution.py:76
  63.7 1.3 %convolution_convert_fusion.1.k_ref = bf16[640,512]{1,0:T(8,128)(2,1)} fusion(bf16[512,512]{1,0:T(8,128)(2,1)S(1)} %copy-done.4, bf16[532,512]{1,0:T(8,128)(2,1)S(1)} %reshape.98), kind=kOutput, calls=%fused_computation.9 | convolution fusion | flops 335872000 | bytes 1724416 | tf_op jit(solution)/shard_map/dot_general | solution.py:76
  65.1 7.0 %shard_map.82 = bf16[256,512]{1,0:T(8,128)(2,1)} custom-call(bf16[256,512]{1,0:T(8,128)(2,1)} %convolution_convert_fusion.2.q_ref, bf16[640,512]{1,0:T(8,128)(2,1)} %convolution_convert_fusion.1.k_ref, bf16[640,512]{1,0:T(8,128)(2,1)} %convolution_convert_fusion.v_ref, bf16[32,8,512]{2,1,0:T(8,128)(2,1)} %bitcast.67, bf16[512,512]{1,0:T(8,128)(2,1)} %wo_ref.1), custom_call_target="tpu_custom_call" | custom-call | tf_op jit(solution)/shard_map/pallas_call | solution.py:130
  (47 shorter events, 1.4 us)
Async XLA Ops:
  0.0 62.3 %copy-start = (bf16[512,512]{1,0:T(8,128)(2,1)S(1)}, bf16[512,512]{1,0:T(8,128)(2,1)}, u32[]{:S(2)}) copy-start(bf16[512,512]{1,0:T(8,128)(2,1)} %param.13) | copy-start | bytes 1572868
  0.0 9.8 %copy-start.2 = (f32[1,9,32,8]{2,3,1,0:T(8,128)S(1)}, f32[1,9,32,8]{2,3,1,0:T(8,128)}, u32[]{:S(2)}) copy-start(f32[1,9,32,8]{2,3,1,0:T(8,128)} %param.10) | copy-start | bytes 27652
  0.0 9.8 %copy-start.3 = (s32[1,2,3]{2,1,0:T(2,128)S(1)}, s32[1,2,3]{2,1,0:T(2,128)}, u32[]{:S(2)}) copy-start(s32[1,2,3]{2,1,0:T(2,128)} %param.15) | copy-start | bytes 76
  2.3 7.7 %collective-permute-start = (bf16[1,2,8,512]{3,2,1,0:T(8,128)(2,1)S(1)}, bf16[1,2,8,512]{3,2,1,0:T(8,128)(2,1)S(1)}, u32[]{:S(2)}, u32[]{:S(2)}) collective-permute-start(bf16[1,2,8,512]{3,2,1,0:T(8,128)(2,1)S(1)} %maximum_bitcast_fusion.3), channel_id=1, source_target_pairs={{0,1},{1,0},{2,3},{3,2},{4,5},{5,4},{6,7},{7,6},{8,9},{9,8},{10,11... | collective-permute-start | bytes 49160 | tf_op jit(solution)/shard_map/ppermute | solution.py:163
  4.0 16.4 %collective-permute-start.4 = (bf16[1,32,1,512]{3,2,1,0:T(2,128)(2,1)S(1)}, bf16[1,32,1,512]{3,2,1,0:T(2,128)(2,1)S(1)}, u32[]{:S(2)}, u32[]{:S(2)}) collective-permute-start(bf16[1,32,1,512]{3,2,1,0:T(2,128)(2,1)S(1)} %get-tuple-element.24), channel_id=1, source_target_pairs={{0,1},{1,2},{2,3},{3,4},{4,5},{5,6},{6,7},{7,8},{8,9},{9,10},{10,1... | collective-permute-start | bytes 98312 | tf_op jit(solution)/shard_map/ppermute | solution.py:19
  4.1 16.3 %collective-permute-start.5 = (bf16[1,32,1,512]{3,2,1,0:T(2,128)(2,1)S(1)}, bf16[1,32,1,512]{3,2,1,0:T(2,128)(2,1)S(1)}, u32[]{:S(2)}, u32[]{:S(2)}) collective-permute-start(bf16[1,32,1,512]{3,2,1,0:T(2,128)(2,1)S(1)} %get-tuple-element.25), channel_id=1, source_target_pairs={{1,0},{2,1},{3,2},{4,3},{5,4},{6,5},{7,6},{8,7},{9,8},{10,9},{11,1... | collective-permute-start | bytes 98312 | tf_op jit(solution)/shard_map/ppermute | solution.py:20
  10.0 4.0 %collective-permute-start.1 = (bf16[2,2,8,512]{3,2,1,0:T(8,128)(2,1)S(1)}, bf16[2,2,8,512]{3,2,1,0:T(8,128)(2,1)S(1)}, u32[]{:S(2)}, u32[]{:S(2)}) collective-permute-start(bf16[2,2,8,512]{3,2,1,0:T(8,128)(2,1)S(1)} %maximum_select_fusion.6), channel_id=1, source_target_pairs={{0,2},{1,3},{2,0},{3,1},{4,6},{5,7},{6,4},{7,5},{8,10},{9,11},{10,... | collective-permute-start | bytes 98312 | tf_op jit(solution)/shard_map/ppermute | solution.py:163
  14.0 4.8 %collective-permute-start.2 = (bf16[4,2,8,512]{3,2,1,0:T(8,128)(2,1)S(1)}, bf16[4,2,8,512]{3,2,1,0:T(8,128)(2,1)S(1)}, u32[]{:S(2)}, u32[]{:S(2)}) collective-permute-start(bf16[4,2,8,512]{3,2,1,0:T(8,128)(2,1)S(1)} %maximum_select_fusion.5), channel_id=1, source_target_pairs={{0,4},{1,5},{2,6},{3,7},{4,0},{5,1},{6,2},{7,3},{8,12},{9,13},{10,... | collective-permute-start | bytes 196616 | tf_op jit(solution)/shard_map/ppermute | solution.py:163
  18.8 6.4 %collective-permute-start.3 = (bf16[8,2,8,512]{3,2,1,0:T(8,128)(2,1)S(1)}, bf16[8,2,8,512]{3,2,1,0:T(8,128)(2,1)S(1)}, u32[]{:S(2)}, u32[]{:S(2)}) collective-permute-start(bf16[8,2,8,512]{3,2,1,0:T(8,128)(2,1)S(1)} %maximum_select_fusion.4), channel_id=1, source_target_pairs={{0,8},{1,9},{2,10},{3,11},{4,12},{5,13},{6,14},{7,15},{8,0},{9,1},... | collective-permute-start | bytes 393224 | tf_op jit(solution)/shard_map/ppermute | solution.py:163
  27.3 1.4 %collective-permute-start.6 = (bf16[1,6,8,512]{3,0,2,1:T(2,128)(2,1)S(1)}, bf16[1,6,8,512]{3,0,2,1:T(2,128)(2,1)S(1)}, u32[]{:S(2)}, u32[]{:S(2)}) collective-permute-start(bf16[1,6,8,512]{3,0,2,1:T(2,128)(2,1)S(1)} %copy.52), channel_id=1, source_target_pairs={{0,1},{1,0},{2,3},{3,2},{4,5},{5,4},{6,7},{7,6},{8,9},{9,8},{10,11... | collective-permute-start | bytes 147464 | tf_op jit(solution)/shard_map/ppermute | solution.py:163
  29.1 4.9 %collective-permute-start.7 = (bf16[2,6,8,512]{3,0,2,1:T(2,128)(2,1)S(1)}, bf16[2,6,8,512]{3,0,2,1:T(2,128)(2,1)S(1)}, u32[]{:S(2)}, u32[]{:S(2)}) collective-permute-start(bf16[2,6,8,512]{3,0,2,1:T(2,128)(2,1)S(1)} %broadcast_select_fusion), channel_id=1, source_target_pairs={{0,2},{1,3},{2,0},{3,1},{4,6},{5,7},{6,4},{7,5},{8,10},{9,11},{10,... | collective-permute-start | bytes 294920 | tf_op jit(solution)/shard_map/ppermute | solution.py:163
  34.4 12.1 %copy-start.1 = (bf16[512,512]{1,0:T(8,128)(2,1)S(1)}, bf16[512,512]{1,0:T(8,128)(2,1)}, u32[]{:S(2)}) copy-start(bf16[512,512]{1,0:T(8,128)(2,1)} %param.11) | copy-start | bytes 1572868
  34.4 6.2 %collective-permute-start.8 = (bf16[4,6,8,512]{3,0,2,1:T(4,128)(2,1)S(1)}, bf16[4,6,8,512]{3,0,2,1:T(4,128)(2,1)S(1)}, u32[]{:S(2)}, u32[]{:S(2)}) collective-permute-start(bf16[4,6,8,512]{3,0,2,1:T(4,128)(2,1)S(1)} %maximum_select_fusion.3), channel_id=1, source_target_pairs={{0,4},{1,5},{2,6},{3,7},{4,0},{5,1},{6,2},{7,3},{8,12},{9,13},{10,... | collective-permute-start | bytes 589832 | tf_op jit(solution)/shard_map/ppermute | solution.py:163
  40.9 18.8 %collective-permute-start.9 = (bf16[8,6,8,512]{3,0,2,1:T(8,128)(2,1)S(1)}, bf16[8,6,8,512]{3,0,2,1:T(8,128)(2,1)S(1)}, u32[]{:S(2)}, u32[]{:S(2)}) collective-permute-start(bf16[8,6,8,512]{3,0,2,1:T(8,128)(2,1)S(1)} %maximum_select_fusion.1), channel_id=1, source_target_pairs={{0,8},{1,9},{2,10},{3,11},{4,12},{5,13},{6,14},{7,15},{8,0},{9,1},... | collective-permute-start | bytes 1179656 | tf_op jit(solution)/shard_map/ppermute | solution.py:163
  42.0 10.2 %collective-permute-start.10 = (bf16[1,32,3,512]{3,2,1,0:T(4,128)(2,1)S(1)}, bf16[1,32,3,512]{3,2,1,0:T(4,128)(2,1)S(1)}, u32[]{:S(2)}, u32[]{:S(2)}) collective-permute-start(bf16[1,32,3,512]{3,2,1,0:T(4,128)(2,1)S(1)} %get-tuple-element.14), channel_id=1, source_target_pairs={{0,1},{1,2},{2,3},{3,4},{4,5},{5,6},{6,7},{7,8},{8,9},{9,10},{10,1... | collective-permute-start | bytes 294920 | tf_op jit(solution)/shard_map/ppermute | solution.py:19
  42.1 10.2 %collective-permute-start.11 = (bf16[1,32,3,512]{3,2,1,0:T(4,128)(2,1)S(1)}, bf16[1,32,3,512]{3,2,1,0:T(4,128)(2,1)S(1)}, u32[]{:S(2)}, u32[]{:S(2)}) collective-permute-start(bf16[1,32,3,512]{3,2,1,0:T(4,128)(2,1)S(1)} %get-tuple-element.15), channel_id=1, source_target_pairs={{1,0},{2,1},{3,2},{4,3},{5,4},{6,5},{7,6},{8,7},{9,8},{10,9},{11,1... | collective-permute-start | bytes 294920 | tf_op jit(solution)/shard_map/ppermute | solution.py:20
  62.2 1.6 %copy-start.4 = (bf16[512,512]{1,0:T(8,128)(2,1)S(1)}, bf16[512,512]{1,0:T(8,128)(2,1)}, u32[]{:S(2)}) copy-start(bf16[512,512]{1,0:T(8,128)(2,1)} %param.12) | copy-start | bytes 1572868

commit v9 on v5

--- a/solution.py
+++ b/solution.py
@@ -152,6 +152,26 @@
     return got.astype(edges.dtype)
 
 
+def radix_gather(block, axis, radix=16):
+    count = lax.axis_size(axis)
+    if count & (count - 1):
+        return lax.all_gather(block, axis, axis=0, tiled=True)
+    me = lax.axis_index(axis)
+    held = block
+    stride = 1
+    while stride < count:
+        r = min(radix, count // stride)
+        got = [held]
+        for d in range(1, r):
+            got.append(lax.ppermute(held, axis, [(i, i ^ (d * stride)) for i in range(count)]))
+        digit = (me // stride) % r
+        order = digit ^ jnp.arange(r, dtype=jnp.int32)
+        held = jnp.take(jnp.stack(got), order, axis=0)
+        held = held.reshape((r * held.shape[1],) + held.shape[2:])
+        stride *= r
+    return held
+
+
 def local(latents, norm_gain, metric, w_query, w_key, w_value, w_output, seam_table):
     own_tile = latents[0]
     channels = own_tile.shape[-1]
@@ -160,14 +180,14 @@
     seam_rows = seam_table[0]
     widened = padded_2(normed[None], (("blk", 2),), margin)
     rows1 = jnp.stack([normed[0], normed[-1]])
-    got1 = widen_tiles(lax.all_gather(rows1[None], "blk", axis=0, tiled=True), 1)
+    got1 = widen_tiles(radix_gather(rows1[None], "blk"), 1)
     received = pick_all(seam_rows, got1[:, :, None])
     padded = place_rims(widened[0], received, seam_rows)
     smoothed = smooth(padded, metric[0])
     query = project(smoothed, w_query)
     field_wide = padded_2(smoothed[None], (("blk", 2),), RADIUS)
     rows3 = jnp.concatenate([smoothed[:RADIUS], smoothed[-RADIUS:]], axis=0)
-    got3 = widen_tiles(lax.all_gather(rows3[None], "blk", axis=0, tiled=True), RADIUS)
+    got3 = widen_tiles(radix_gather(rows3[None], "blk"), RADIUS)
     edges3 = jnp.stack([got3[:, :RADIUS], got3[:, RADIUS:]], axis=1)
     field_got = pick_all(seam_rows, edges3)
     field_pad = place_rims(field_wide[0], field_got, seam_rows)

time: 72.7 us -> 80.9 us (1.11)
  starting transfers between devices: 10.1 us -> 52.6 us
  blocking collectives: 39.6 us -> 0 us
  waiting for transfers between devices: 0.01 us -> 2.4 us
  other arithmetic: 7.1 us -> 9.3 us
    ppermute x0 -> x30, starting transfers between devices: none -> 43.4 us  [radix_gather(): lax.ppermute(held, axis, [(i, i ^ d * stride) for i in range(count)])]
    all_gather x2 -> x0, blocking collectives: 39.6 us -> none  [the longest x1 20 us: local(): lax.all_gather(rows1[None], 'blk', axis=0, tiled=True)]
    ppermute x0 -> x30, waiting for transfers between devices: none -> 2.39 us  [radix_gather(): lax.ppermute(held, axis, [(i, i ^ d * stride) for i in range(count)])]
    ppermute x2, starting transfers between devices: 9.15 us -> 7.58 us  [padded_2(): after = lax.ppermute(first, axis, down)]
    gather x0 -> x2, local copies, waits for them, and re-layouts: none -> 1.16 us  [radix_gather(): held = jnp.take(jnp.stack(got), order, axis=0)]
    select_n x0 -> x5, other arithmetic: none -> 1.16 us  [radix_gather(): held = jnp.take(jnp.stack(got), order, axis=0)]
  transfers between devices with their start and end apart: 4 -> 34, of which waited for: 0 -> 2; matrix products, arithmetic and copies ran while one was open for 10% -> 13% of each run, Pallas kernels for 0% -> 0%
where the time goes in v9:
time: 80.9 us; the launch traced here: 80.5 us
  starting transfers between devices  52.6 us (65%)
  other arithmetic  9.3 us (11%)
  Pallas kernels  7 us (9%)
  matrix products  4.54 us (6%)
  local copies, waits for them, and re-layouts  4.21 us (5%)
  waiting for transfers between devices  2.4 us (3%)
    ppermute x30, starting transfers between devices, radix_gather(): lax.ppermute(held, axis, [(i, i ^ d * stride) for i in range(count)])  43.4 us
    ppermute x2, starting transfers between devices, padded_2(): after = lax.ppermute(first, axis, down)  7.58 us
    pallas_call x1, Pallas kernels, attend_and_mix(): pl.pallas_call(attention_kernel, out_shape=jax.ShapeDtypeStruct((cells, c...  7 us
    dot_general x3, matrix products, project(): jnp.dot(flat, weight, preferred_element_type=jnp.float32)  3.73 us
    ppermute x30, waiting for transfers between devices, radix_gather(): lax.ppermute(held, axis, [(i, i ^ d * stride) for i in range(count)])  2.39 us
    convert_element_type x2, other arithmetic, normalize(): return (values * factor * norm_gain).astype(jnp.bfloat16)  2.17 us
  transfers between devices with their start and end apart: 34, of which 2 were waited for; matrix products, arithmetic and copies ran while one was open for 13% of the time, Pallas kernels for 0%

profile of v9, /device:TPU:0, one launch (start us, length us, event | category | flops | bytes accessed | tf_op | source)
XLA Modules:
  0.0 80.5 jit_solution(14978268121986727911)
XLA Ops:
  0.0 1.1 %fusion.15 = f32[32,8]{1,0:T(8,128)S(1)} fusion(bf16[1,32,8,512]{3,2,1,0:T(8,128)(2,1)} %param.8), kind=kLoop, calls=%fused_computation.32 | loop fusion | flops 392960 | bytes 263168 | tf_op jit(solution)/shard_map/reduce_sum | solution.py:27
  1.2 1.1 %fusion.17 = bf16[32,8,512]{2,1,0:T(8,128)(2,1)S(1)} fusion(f32[512]{0:T(512)} %param.9, f32[32,8]{1,0:T(8,128)S(1)} %add_rsqrt_fusion, bf16[1,32,8,512]{3,2,1,0:T(8,128)(2,1)} %param.8), kind=kLoop, calls=%fused_computation.34 | loop fusion | flops 524288 | bytes 527360 | tf_op jit(solution)/shard_map/convert_element_type | solution.py:28
  2.3 0.5 collective-permute-start
  2.8 2.6 %collective-permute-start.1 = (bf16[1,2,8,512]{3,2,1,0:T(8,128)(2,1)S(1)}, bf16[1,2,8,512]{3,2,1,0:T(8,128)(2,1)S(1)}, u32[]{:S(2)}, u32[]{:S(2)}) collective-permute-start(bf16[1,2,8,512]{3,2,1,0:T(8,128)(2,1)S(1)} %fusion.27), channel_id=1, source_target_pairs={{0,2},{1,3},{2,0},{3,1},{4,6},{5,7},{6,4},{7,5},{8,10},{9,11},{10,... | collective-permute-start | bytes 49160 | tf_op jit(solution)/shard_map/ppermute | solution.py:166
  5.5 1.8 %collective-permute-start.3 = (bf16[1,2,8,512]{3,2,1,0:T(8,128)(2,1)S(1)}, bf16[1,2,8,512]{3,2,1,0:T(8,128)(2,1)S(1)}, u32[]{:S(2)}, u32[]{:S(2)}) collective-permute-start(bf16[1,2,8,512]{3,2,1,0:T(8,128)(2,1)S(1)} %fusion.27), channel_id=1, source_target_pairs={{0,4},{1,5},{2,6},{3,7},{4,0},{5,1},{6,2},{7,3},{8,12},{9,13},{10,... | collective-permute-start | bytes 49160 | tf_op jit(solution)/shard_map/ppermute | solution.py:166
  7.3 1.0 %slice_reduce_fusion.2 = (s32[2]{0:T(128)S(1)}, s32[2]{0:T(128)S(1)}, s32[2]{0:T(128)S(1)}) fusion(s32[2,3]{1,0:T(2,128)} %bitcast.188), kind=kLoop, calls=%fused_computation.138 | loop fusion | bytes 48 | tf_op jit(solution)/shard_map/slice | solution.py:46
  8.3 0.9 %compare_reduce_fusion = pred[2]{0:T(512)(128)(4,1)S(1)} fusion(s32[2,3]{1,0:T(2,128)} %bitcast.189), kind=kLoop, calls=%fused_computation.128 | loop fusion | flops 24 | bytes 10 | tf_op jit(solution)/shard_map/eq | solution.py:47
  9.2 1.1 %multiply_convert_fusion = bf16[1,32,8,512]{3,2,1,0:T(8,128)(2,1)S(1)} fusion(bf16[1,32,8,512]{3,2,1,0:T(8,128)(2,1)} %param.8, f32[512]{0:T(512)} %param.9, f32[32,8]{1,0:T(8,128)S(1)} %add_rsqrt_fusion), kind=kLoop, calls=%fused_computation.42 | loop fusion | flops 524288 | bytes 527360 | tf_op jit(solution)/shard_map/convert_element_type | solution.py:28
  11.2 2.6 %collective-permute-start.5 = (bf16[1,2,8,512]{3,2,1,0:T(8,128)(2,1)S(1)}, bf16[1,2,8,512]{3,2,1,0:T(8,128)(2,1)S(1)}, u32[]{:S(2)}, u32[]{:S(2)}) collective-permute-start(bf16[1,2,8,512]{3,2,1,0:T(8,128)(2,1)S(1)} %fusion.27), channel_id=1, source_target_pairs={{0,6},{1,7},{2,4},{3,5},{4,2},{5,3},{6,0},{7,1},{8,14},{9,15},{10,... | collective-permute-start | bytes 49160 | tf_op jit(solution)/shard_map/ppermute | solution.py:166
  14.0 2.6 %collective-permute-start.7 = (bf16[1,2,8,512]{3,2,1,0:T(8,128)(2,1)S(1)}, bf16[1,2,8,512]{3,2,1,0:T(8,128)(2,1)S(1)}, u32[]{:S(2)}, u32[]{:S(2)}) collective-permute-start(bf16[1,2,8,512]{3,2,1,0:T(8,128)(2,1)S(1)} %fusion.27), channel_id=1, source_target_pairs={{0,8},{1,9},{2,10},{3,11},{4,12},{5,13},{6,14},{7,15},{8,0},{9,1},... | collective-permute-start | bytes 49160 | tf_op jit(solution)/shard_map/ppermute | solution.py:166
  16.7 3.5 %collective-permute-start.9 = (bf16[1,2,8,512]{3,2,1,0:T(8,128)(2,1)S(1)}, bf16[1,2,8,512]{3,2,1,0:T(8,128)(2,1)S(1)}, u32[]{:S(2)}, u32[]{:S(2)}) collective-permute-start(bf16[1,2,8,512]{3,2,1,0:T(8,128)(2,1)S(1)} %fusion.27), channel_id=1, source_target_pairs={{0,10},{1,11},{2,8},{3,9},{4,14},{5,15},{6,12},{7,13},{8,2},{9,3},... | collective-permute-start | bytes 49160 | tf_op jit(solution)/shard_map/ppermute | solution.py:166
  20.3 3.5 %collective-permute-start.11 = (bf16[1,2,8,512]{3,2,1,0:T(8,128)(2,1)S(1)}, bf16[1,2,8,512]{3,2,1,0:T(8,128)(2,1)S(1)}, u32[]{:S(2)}, u32[]{:S(2)}) collective-permute-start(bf16[1,2,8,512]{3,2,1,0:T(8,128)(2,1)S(1)} %fusion.27), channel_id=1, source_target_pairs={{0,12},{1,13},{2,14},{3,15},{4,8},{5,9},{6,10},{7,11},{8,4},{9,5},... | collective-permute-start | bytes 49160 | tf_op jit(solution)/shard_map/ppermute | solution.py:166
  23.9 4.4 %collective-permute-start.13 = (bf16[1,2,8,512]{3,2,1,0:T(8,128)(2,1)S(1)}, bf16[1,2,8,512]{3,2,1,0:T(8,128)(2,1)S(1)}, u32[]{:S(2)}, u32[]{:S(2)}) collective-permute-start(bf16[1,2,8,512]{3,2,1,0:T(8,128)(2,1)S(1)} %fusion.27), channel_id=1, source_target_pairs={{0,14},{1,15},{2,12},{3,13},{4,10},{5,11},{6,8},{7,9},{8,6},{9,7},... | collective-permute-start | bytes 49160 | tf_op jit(solution)/shard_map/ppermute | solution.py:166
  28.5 0.3 collective-permute-start.15
  28.8 4.1 %collective-permute-start.16 = (bf16[1,32,1,512]{3,2,1,0:T(2,128)(2,1)S(1)}, bf16[1,32,1,512]{3,2,1,0:T(2,128)(2,1)S(1)}, u32[]{:S(2)}, u32[]{:S(2)}) collective-permute-start(bf16[1,32,1,512]{3,2,1,0:T(2,128)(2,1)S(1)} %get-tuple-element.25), channel_id=1, source_target_pairs={{1,0},{2,1},{3,2},{4,3},{5,4},{6,5},{7,6},{8,7},{9,8},{10,9},{11,1... | collective-permute-start | bytes 98312 | tf_op jit(solution)/shard_map/ppermute | solution.py:20
  32.9 1.2 %collective-permute-done.14 = bf16[1,2,8,512]{3,2,1,0:T(8,128)(2,1)S(1)} collective-permute-done((bf16[1,2,8,512]{3,2,1,0:T(8,128)(2,1)S(1)}, bf16[1,2,8,512]{3,2,1,0:T(8,128)(2,1)S(1)}, u32[]{:S(2)}, u32[]{:S(2)}) %collective-permute-start.14) | collective-permute-done | bytes 16416 | tf_op jit(solution)/shard_map/ppermute | solution.py:166
  34.2 0.6 gather_fusion
  35.0 0.3 fusion.18
  35.3 0.4 fusion.12
  35.9 0.3 maximum_bitcast_fusion
  36.2 1.1 %fusion.48 = bf16[1,32,8,512]{3,2,1,0:T(8,128)(2,1)S(1)} fusion(bf16[1,10,512]{2,1,0:T(8,128)(2,1)S(1)} %copy.49, bf16[32,10,512]{2,1,0:T(8,128)(2,1)S(1)} %maximum_bitcast_fusion, f32[32,8]{1,0:T(8,128)S(1)} %copy.51, f32[32,8]{1,0:T(8,128)S(1)} %copy.50, f32[32,8]{1,0:T(8,128)S(1)} %copy.48, f32[32,8]{1,0:T(8,128)S(1)} %copy.47, f32[32,8]{1,0:T(8,128)S(1)} %copy.46, ...), kind=kLoop, calls=%fused_computation.151 | loop fusion | flops 5898240 | bytes 1753088 | tf_op jit(solution)/shard_map/broadcast_in_dim | solution.py:188
  37.3 1.1 %add_convert_fusion = bf16[32,8,512]{2,1,0:T(8,128)(2,1)S(1)} fusion(bf16[32,10,512]{2,1,0:T(8,128)(2,1)S(1)} %maximum_bitcast_fusion, bf16[1,10,512]{2,1,0:T(8,128)(2,1)S(1)} %copy.49, bf16[1,10,512]{2,1,0:T(8,128)(2,1)S(1)} %copy.42, f32[32,8]{1,0:T(8,128)S(1)} %copy.51, f32[32,8]{1,0:T(8,128)S(1)} %copy.50, f32[32,8]{1,0:T(8,128)S(1)} %copy.48, ...), kind=kLoop, calls=%fused_computation.41 | loop fusion | flops 5898240 | bytes 1753088 | tf_op jit(solution)/shard_map/convert_element_type | solution.py:69
  38.4 0.7 collective-permute-start.17
  39.1 1.4 %collective-permute-start.19 = (bf16[1,6,8,512]{3,2,1,0:T(8,128)(2,1)S(1)}, bf16[1,6,8,512]{3,2,1,0:T(8,128)(2,1)S(1)}, u32[]{:S(2)}, u32[]{:S(2)}) collective-permute-start(bf16[1,6,8,512]{3,2,1,0:T(8,128)(2,1)S(1)} %fusion.26), channel_id=1, source_target_pairs={{0,3},{1,2},{2,1},{3,0},{4,7},{5,6},{6,5},{7,4},{8,11},{9,10},{10,... | collective-permute-start | bytes 147464 | tf_op jit(solution)/shard_map/ppermute | solution.py:166
  40.5 2.1 %collective-permute-start.21 = (bf16[1,6,8,512]{3,2,1,0:T(8,128)(2,1)S(1)}, bf16[1,6,8,512]{3,2,1,0:T(8,128)(2,1)S(1)}, u32[]{:S(2)}, u32[]{:S(2)}) collective-permute-start(bf16[1,6,8,512]{3,2,1,0:T(8,128)(2,1)S(1)} %fusion.26), channel_id=1, source_target_pairs={{0,5},{1,4},{2,7},{3,6},{4,1},{5,0},{6,3},{7,2},{8,13},{9,12},{10,... | collective-permute-start | bytes 147464 | tf_op jit(solution)/shard_map/ppermute | solution.py:166
  42.7 1.0 %convolution_convert_fusion.2.q_ref = bf16[256,512]{1,0:T(8,128)(2,1)} fusion(bf16[512,512]{1,0:T(8,128)(2,1)S(1)} %copy-done.1, bf16[32,8,512]{2,1,0:T(8,128)(2,1)S(1)} %add_convert_fusion), kind=kOutput, calls=%fused_computation.12 | convolution fusion | flops 134348800 | bytes 1048576 | tf_op jit(solution)/shard_map/dot_general | solution.py:76
  43.8 2.3 %collective-permute-start.23 = (bf16[1,6,8,512]{3,2,1,0:T(8,128)(2,1)S(1)}, bf16[1,6,8,512]{3,2,1,0:T(8,128)(2,1)S(1)}, u32[]{:S(2)}, u32[]{:S(2)}) collective-permute-start(bf16[1,6,8,512]{3,2,1,0:T(8,128)(2,1)S(1)} %fusion.26), channel_id=1, source_target_pairs={{0,7},{1,6},{2,5},{3,4},{4,3},{5,2},{6,1},{7,0},{8,15},{9,14},{10,... | collective-permute-start | bytes 147464 | tf_op jit(solution)/shard_map/ppermute | solution.py:166
  46.1 1.5 %collective-permute-start.24 = (bf16[1,6,8,512]{3,2,1,0:T(8,128)(2,1)S(1)}, bf16[1,6,8,512]{3,2,1,0:T(8,128)(2,1)S(1)}, u32[]{:S(2)}, u32[]{:S(2)}) collective-permute-start(bf16[1,6,8,512]{3,2,1,0:T(8,128)(2,1)S(1)} %fusion.26), channel_id=1, source_target_pairs={{0,8},{1,9},{2,10},{3,11},{4,12},{5,13},{6,14},{7,15},{8,0},{9,1},... | collective-permute-start | bytes 147464 | tf_op jit(solution)/shard_map/ppermute | solution.py:166
  47.6 1.6 %collective-permute-start.25 = (bf16[1,6,8,512]{3,2,1,0:T(8,128)(2,1)S(1)}, bf16[1,6,8,512]{3,2,1,0:T(8,128)(2,1)S(1)}, u32[]{:S(2)}, u32[]{:S(2)}) collective-permute-start(bf16[1,6,8,512]{3,2,1,0:T(8,128)(2,1)S(1)} %fusion.26), channel_id=1, source_target_pairs={{0,9},{1,8},{2,11},{3,10},{4,13},{5,12},{6,15},{7,14},{8,1},{9,0},... | collective-permute-start | bytes 147464 | tf_op jit(solution)/shard_map/ppermute | solution.py:166
  49.2 2.1 %collective-permute-start.26 = (bf16[1,6,8,512]{3,2,1,0:T(8,128)(2,1)S(1)}, bf16[1,6,8,512]{3,2,1,0:T(8,128)(2,1)S(1)}, u32[]{:S(2)}, u32[]{:S(2)}) collective-permute-start(bf16[1,6,8,512]{3,2,1,0:T(8,128)(2,1)S(1)} %fusion.26), channel_id=1, source_target_pairs={{0,10},{1,11},{2,8},{3,9},{4,14},{5,15},{6,12},{7,13},{8,2},{9,3},... | collective-permute-start | bytes 147464 | tf_op jit(solution)/shard_map/ppermute | solution.py:166
  51.3 1.3 %collective-permute-start.27 = (bf16[1,6,8,512]{3,2,1,0:T(8,128)(2,1)S(1)}, bf16[1,6,8,512]{3,2,1,0:T(8,128)(2,1)S(1)}, u32[]{:S(2)}, u32[]{:S(2)}) collective-permute-start(bf16[1,6,8,512]{3,2,1,0:T(8,128)(2,1)S(1)} %fusion.26), channel_id=1, source_target_pairs={{0,11},{1,10},{2,9},{3,8},{4,15},{5,14},{6,13},{7,12},{8,3},{9,2},... | collective-permute-start | bytes 147464 | tf_op jit(solution)/shard_map/ppermute | solution.py:166
  52.6 2.4 %collective-permute-start.28 = (bf16[1,6,8,512]{3,2,1,0:T(8,128)(2,1)S(1)}, bf16[1,6,8,512]{3,2,1,0:T(8,128)(2,1)S(1)}, u32[]{:S(2)}, u32[]{:S(2)}) collective-permute-start(bf16[1,6,8,512]{3,2,1,0:T(8,128)(2,1)S(1)} %fusion.26), channel_id=1, source_target_pairs={{0,12},{1,13},{2,14},{3,15},{4,8},{5,9},{6,10},{7,11},{8,4},{9,5},... | collective-permute-start | bytes 147464 | tf_op jit(solution)/shard_map/ppermute | solution.py:166
  55.0 1.6 %collective-permute-start.29 = (bf16[1,6,8,512]{3,2,1,0:T(8,128)(2,1)S(1)}, bf16[1,6,8,512]{3,2,1,0:T(8,128)(2,1)S(1)}, u32[]{:S(2)}, u32[]{:S(2)}) collective-permute-start(bf16[1,6,8,512]{3,2,1,0:T(8,128)(2,1)S(1)} %fusion.26), channel_id=1, source_target_pairs={{0,13},{1,12},{2,15},{3,14},{4,9},{5,8},{6,11},{7,10},{8,5},{9,4},... | collective-permute-start | bytes 147464 | tf_op jit(solution)/shard_map/ppermute | solution.py:166
  56.6 3.2 %collective-permute-start.30 = (bf16[1,6,8,512]{3,2,1,0:T(8,128)(2,1)S(1)}, bf16[1,6,8,512]{3,2,1,0:T(8,128)(2,1)S(1)}, u32[]{:S(2)}, u32[]{:S(2)}) collective-permute-start(bf16[1,6,8,512]{3,2,1,0:T(8,128)(2,1)S(1)} %fusion.26), channel_id=1, source_target_pairs={{0,14},{1,15},{2,12},{3,13},{4,10},{5,11},{6,8},{7,9},{8,6},{9,7},... | collective-permute-start | bytes 147464 | tf_op jit(solution)/shard_map/ppermute | solution.py:166
  59.8 1.0 %collective-permute-start.31 = (bf16[1,6,8,512]{3,2,1,0:T(8,128)(2,1)S(1)}, bf16[1,6,8,512]{3,2,1,0:T(8,128)(2,1)S(1)}, u32[]{:S(2)}, u32[]{:S(2)}) collective-permute-start(bf16[1,6,8,512]{3,2,1,0:T(8,128)(2,1)S(1)} %fusion.26), channel_id=1, source_target_pairs={{0,15},{1,14},{2,13},{3,12},{4,11},{5,10},{6,9},{7,8},{8,7},{9,6},... | collective-permute-start | bytes 147464 | tf_op jit(solution)/shard_map/ppermute | solution.py:166
  60.9 1.2 %collective-permute-start.32 = (bf16[1,32,3,512]{3,2,1,0:T(4,128)(2,1)S(1)}, bf16[1,32,3,512]{3,2,1,0:T(4,128)(2,1)S(1)}, u32[]{:S(2)}, u32[]{:S(2)}) collective-permute-start(bf16[1,32,3,512]{3,2,1,0:T(4,128)(2,1)S(1)} %get-tuple-element.14), channel_id=1, source_target_pairs={{0,1},{1,2},{2,3},{3,4},{4,5},{5,6},{6,7},{7,8},{8,9},{9,10},{10,1... | collective-permute-start | bytes 294920 | tf_op jit(solution)/shard_map/ppermute | solution.py:19
  62.1 3.5 %collective-permute-start.33 = (bf16[1,32,3,512]{3,2,1,0:T(4,128)(2,1)S(1)}, bf16[1,32,3,512]{3,2,1,0:T(4,128)(2,1)S(1)}, u32[]{:S(2)}, u32[]{:S(2)}) collective-permute-start(bf16[1,32,3,512]{3,2,1,0:T(4,128)(2,1)S(1)} %get-tuple-element.15), channel_id=1, source_target_pairs={{1,0},{2,1},{3,2},{4,3},{5,4},{6,5},{7,6},{8,7},{9,8},{10,9},{11,1... | collective-permute-start | bytes 294920 | tf_op jit(solution)/shard_map/ppermute | solution.py:20
  65.6 1.1 %collective-permute-done.31 = bf16[1,6,8,512]{3,2,1,0:T(8,128)(2,1)S(1)} collective-permute-done((bf16[1,6,8,512]{3,2,1,0:T(8,128)(2,1)S(1)}, bf16[1,6,8,512]{3,2,1,0:T(8,128)(2,1)S(1)}, u32[]{:S(2)}, u32[]{:S(2)}) %collective-permute-start.31) | collective-permute-done | bytes 49184 | tf_op jit(solution)/shard_map/ppermute | solution.py:166
  66.7 0.6 gather_fusion.1
  67.3 0.5 bitcast_select_fusion
  67.8 0.4 slice_bitcast_fusion.1
  68.4 0.5 broadcast_select_fusion
  68.9 0.3 fusion
  69.3 0.4 fusion.9
  70.2 0.3 maximum_bitcast_fusion.1
  70.8 1.4 %convolution_convert_fusion.v_ref = bf16[640,512]{1,0:T(8,128)(2,1)} fusion(bf16[512,512]{1,0:T(8,128)(2,1)S(1)} %copy-done, bf16[532,512]{1,0:T(8,128)(2,1)S(1)} %reshape.147), kind=kOutput, calls=%fused_computation.10 | convolution fusion | flops 335872000 | bytes 1724416 | tf_op jit(solution)/shard_map/dot_general | solution.py:76
  72.2 1.4 %convolution_convert_fusion.1.k_ref = bf16[640,512]{1,0:T(8,128)(2,1)} fusion(bf16[512,512]{1,0:T(8,128)(2,1)S(1)} %copy-done.3, bf16[532,512]{1,0:T(8,128)(2,1)S(1)} %reshape.147), kind=kOutput, calls=%fused_computation.11 | convolution fusion | flops 335872000 | bytes 1724416 | tf_op jit(solution)/shard_map/dot_general | solution.py:76
  73.5 7.0 %shard_map.82 = bf16[256,512]{1,0:T(8,128)(2,1)} custom-call(bf16[256,512]{1,0:T(8,128)(2,1)} %convolution_convert_fusion.2.q_ref, bf16[640,512]{1,0:T(8,128)(2,1)} %convolution_convert_fusion.1.k_ref, bf16[640,512]{1,0:T(8,128)(2,1)} %convolution_convert_fusion.v_ref, bf16[32,8,512]{2,1,0:T(8,128)(2,1)} %bitcast.185, bf16[512,512]{1,0:T(8,128)(2,1)} %wo_ref.1), custom_call_target="tpu_custom_call" | custom-call | tf_op jit(solution)/shard_map/pallas_call | solution.py:130
  (121 shorter events, 3.3 us)
Async XLA Ops:
  0.0 70.8 %copy-start = (bf16[512,512]{1,0:T(8,128)(2,1)S(1)}, bf16[512,512]{1,0:T(8,128)(2,1)}, u32[]{:S(2)}) copy-start(bf16[512,512]{1,0:T(8,128)(2,1)} %param.13) | copy-start | bytes 1572868
  0.0 10.5 %copy-start.2 = (f32[1,9,32,8]{2,3,1,0:T(8,128)S(1)}, f32[1,9,32,8]{2,3,1,0:T(8,128)}, u32[]{:S(2)}) copy-start(f32[1,9,32,8]{2,3,1,0:T(8,128)} %param.10) | copy-start | bytes 27652
  2.3 8.9 %collective-permute-start = (bf16[1,2,8,512]{3,2,1,0:T(8,128)(2,1)S(1)}, bf16[1,2,8,512]{3,2,1,0:T(8,128)(2,1)S(1)}, u32[]{:S(2)}, u32[]{:S(2)}) collective-permute-start(bf16[1,2,8,512]{3,2,1,0:T(8,128)(2,1)S(1)} %fusion.27), channel_id=1, source_target_pairs={{0,1},{1,0},{2,3},{3,2},{4,5},{5,4},{6,7},{7,6},{8,9},{9,8},{10,11... | collective-permute-start | bytes 49160 | tf_op jit(solution)/shard_map/ppermute | solution.py:166
  2.8 11.0 %collective-permute-start.1 = (bf16[1,2,8,512]{3,2,1,0:T(8,128)(2,1)S(1)}, bf16[1,2,8,512]{3,2,1,0:T(8,128)(2,1)S(1)}, u32[]{:S(2)}, u32[]{:S(2)}) collective-permute-start(bf16[1,2,8,512]{3,2,1,0:T(8,128)(2,1)S(1)} %fusion.27), channel_id=1, source_target_pairs={{0,2},{1,3},{2,0},{3,1},{4,6},{5,7},{6,4},{7,5},{8,10},{9,11},{10,... | collective-permute-start | bytes 49160 | tf_op jit(solution)/shard_map/ppermute | solution.py:166
  5.4 8.6 %collective-permute-start.2 = (bf16[1,2,8,512]{3,2,1,0:T(8,128)(2,1)S(1)}, bf16[1,2,8,512]{3,2,1,0:T(8,128)(2,1)S(1)}, u32[]{:S(2)}, u32[]{:S(2)}) collective-permute-start(bf16[1,2,8,512]{3,2,1,0:T(8,128)(2,1)S(1)} %fusion.27), channel_id=1, source_target_pairs={{0,3},{1,2},{2,1},{3,0},{4,7},{5,6},{6,5},{7,4},{8,11},{9,10},{10,... | collective-permute-start | bytes 49160 | tf_op jit(solution)/shard_map/ppermute | solution.py:166
  5.5 11.1 %collective-permute-start.3 = (bf16[1,2,8,512]{3,2,1,0:T(8,128)(2,1)S(1)}, bf16[1,2,8,512]{3,2,1,0:T(8,128)(2,1)S(1)}, u32[]{:S(2)}, u32[]{:S(2)}) collective-permute-start(bf16[1,2,8,512]{3,2,1,0:T(8,128)(2,1)S(1)} %fusion.27), channel_id=1, source_target_pairs={{0,4},{1,5},{2,6},{3,7},{4,0},{5,1},{6,2},{7,3},{8,12},{9,13},{10,... | collective-permute-start | bytes 49160 | tf_op jit(solution)/shard_map/ppermute | solution.py:166
  7.3 9.4 %collective-permute-start.4 = (bf16[1,2,8,512]{3,2,1,0:T(8,128)(2,1)S(1)}, bf16[1,2,8,512]{3,2,1,0:T(8,128)(2,1)S(1)}, u32[]{:S(2)}, u32[]{:S(2)}) collective-permute-start(bf16[1,2,8,512]{3,2,1,0:T(8,128)(2,1)S(1)} %fusion.27), channel_id=1, source_target_pairs={{0,5},{1,4},{2,7},{3,6},{4,1},{5,0},{6,3},{7,2},{8,13},{9,12},{10,... | collective-permute-start | bytes 49160 | tf_op jit(solution)/shard_map/ppermute | solution.py:166
  11.2 9.0 %collective-permute-start.5 = (bf16[1,2,8,512]{3,2,1,0:T(8,128)(2,1)S(1)}, bf16[1,2,8,512]{3,2,1,0:T(8,128)(2,1)S(1)}, u32[]{:S(2)}, u32[]{:S(2)}) collective-permute-start(bf16[1,2,8,512]{3,2,1,0:T(8,128)(2,1)S(1)} %fusion.27), channel_id=1, source_target_pairs={{0,6},{1,7},{2,4},{3,5},{4,2},{5,3},{6,0},{7,1},{8,14},{9,15},{10,... | collective-permute-start | bytes 49160 | tf_op jit(solution)/shard_map/ppermute | solution.py:166
  13.9 6.5 %collective-permute-start.6 = (bf16[1,2,8,512]{3,2,1,0:T(8,128)(2,1)S(1)}, bf16[1,2,8,512]{3,2,1,0:T(8,128)(2,1)S(1)}, u32[]{:S(2)}, u32[]{:S(2)}) collective-permute-start(bf16[1,2,8,512]{3,2,1,0:T(8,128)(2,1)S(1)} %fusion.27), channel_id=1, source_target_pairs={{0,7},{1,6},{2,5},{3,4},{4,3},{5,2},{6,1},{7,0},{8,15},{9,14},{10,... | collective-permute-start | bytes 49160 | tf_op jit(solution)/shard_map/ppermute | solution.py:166
  14.0 9.8 %collective-permute-start.7 = (bf16[1,2,8,512]{3,2,1,0:T(8,128)(2,1)S(1)}, bf16[1,2,8,512]{3,2,1,0:T(8,128)(2,1)S(1)}, u32[]{:S(2)}, u32[]{:S(2)}) collective-permute-start(bf16[1,2,8,512]{3,2,1,0:T(8,128)(2,1)S(1)} %fusion.27), channel_id=1, source_target_pairs={{0,8},{1,9},{2,10},{3,11},{4,12},{5,13},{6,14},{7,15},{8,0},{9,1},... | collective-permute-start | bytes 49160 | tf_op jit(solution)/shard_map/ppermute | solution.py:166
  16.6 7.3 %collective-permute-start.8 = (bf16[1,2,8,512]{3,2,1,0:T(8,128)(2,1)S(1)}, bf16[1,2,8,512]{3,2,1,0:T(8,128)(2,1)S(1)}, u32[]{:S(2)}, u32[]{:S(2)}) collective-permute-start(bf16[1,2,8,512]{3,2,1,0:T(8,128)(2,1)S(1)} %fusion.27), channel_id=1, source_target_pairs={{0,9},{1,8},{2,11},{3,10},{4,13},{5,12},{6,15},{7,14},{8,1},{9,0},... | collective-permute-start | bytes 49160 | tf_op jit(solution)/shard_map/ppermute | solution.py:166
  16.7 11.6 %collective-permute-start.9 = (bf16[1,2,8,512]{3,2,1,0:T(8,128)(2,1)S(1)}, bf16[1,2,8,512]{3,2,1,0:T(8,128)(2,1)S(1)}, u32[]{:S(2)}, u32[]{:S(2)}) collective-permute-start(bf16[1,2,8,512]{3,2,1,0:T(8,128)(2,1)S(1)} %fusion.27), channel_id=1, source_target_pairs={{0,10},{1,11},{2,8},{3,9},{4,14},{5,15},{6,12},{7,13},{8,2},{9,3},... | collective-permute-start | bytes 49160 | tf_op jit(solution)/shard_map/ppermute | solution.py:166
  20.2 8.3 %collective-permute-start.10 = (bf16[1,2,8,512]{3,2,1,0:T(8,128)(2,1)S(1)}, bf16[1,2,8,512]{3,2,1,0:T(8,128)(2,1)S(1)}, u32[]{:S(2)}, u32[]{:S(2)}) collective-permute-start(bf16[1,2,8,512]{3,2,1,0:T(8,128)(2,1)S(1)} %fusion.27), channel_id=1, source_target_pairs={{0,11},{1,10},{2,9},{3,8},{4,15},{5,14},{6,13},{7,12},{8,3},{9,2},... | collective-permute-start | bytes 49160 | tf_op jit(solution)/shard_map/ppermute | solution.py:166
  20.3 8.5 %collective-permute-start.11 = (bf16[1,2,8,512]{3,2,1,0:T(8,128)(2,1)S(1)}, bf16[1,2,8,512]{3,2,1,0:T(8,128)(2,1)S(1)}, u32[]{:S(2)}, u32[]{:S(2)}) collective-permute-start(bf16[1,2,8,512]{3,2,1,0:T(8,128)(2,1)S(1)} %fusion.27), channel_id=1, source_target_pairs={{0,12},{1,13},{2,14},{3,15},{4,8},{5,9},{6,10},{7,11},{8,4},{9,5},... | collective-permute-start | bytes 49160 | tf_op jit(solution)/shard_map/ppermute | solution.py:166
  23.8 9.1 %collective-permute-start.12 = (bf16[1,2,8,512]{3,2,1,0:T(8,128)(2,1)S(1)}, bf16[1,2,8,512]{3,2,1,0:T(8,128)(2,1)S(1)}, u32[]{:S(2)}, u32[]{:S(2)}) collective-permute-start(bf16[1,2,8,512]{3,2,1,0:T(8,128)(2,1)S(1)} %fusion.27), channel_id=1, source_target_pairs={{0,13},{1,12},{2,15},{3,14},{4,9},{5,8},{6,11},{7,10},{8,5},{9,4},... | collective-permute-start | bytes 49160 | tf_op jit(solution)/shard_map/ppermute | solution.py:166
  23.9 9.0 %collective-permute-start.13 = (bf16[1,2,8,512]{3,2,1,0:T(8,128)(2,1)S(1)}, bf16[1,2,8,512]{3,2,1,0:T(8,128)(2,1)S(1)}, u32[]{:S(2)}, u32[]{:S(2)}) collective-permute-start(bf16[1,2,8,512]{3,2,1,0:T(8,128)(2,1)S(1)} %fusion.27), channel_id=1, source_target_pairs={{0,14},{1,15},{2,12},{3,13},{4,10},{5,11},{6,8},{7,9},{8,6},{9,7},... | collective-permute-start | bytes 49160 | tf_op jit(solution)/shard_map/ppermute | solution.py:166
  28.3 5.9 %collective-permute-start.14 = (bf16[1,2,8,512]{3,2,1,0:T(8,128)(2,1)S(1)}, bf16[1,2,8,512]{3,2,1,0:T(8,128)(2,1)S(1)}, u32[]{:S(2)}, u32[]{:S(2)}) collective-permute-start(bf16[1,2,8,512]{3,2,1,0:T(8,128)(2,1)S(1)} %fusion.27), channel_id=1, source_target_pairs={{0,15},{1,14},{2,13},{3,12},{4,11},{5,10},{6,9},{7,8},{8,7},{9,6},... | collective-permute-start | bytes 49160 | tf_op jit(solution)/shard_map/ppermute | solution.py:166
  28.5 7.4 %collective-permute-start.15 = (bf16[1,32,1,512]{3,2,1,0:T(2,128)(2,1)S(1)}, bf16[1,32,1,512]{3,2,1,0:T(2,128)(2,1)S(1)}, u32[]{:S(2)}, u32[]{:S(2)}) collective-permute-start(bf16[1,32,1,512]{3,2,1,0:T(2,128)(2,1)S(1)} %get-tuple-element.24), channel_id=1, source_target_pairs={{0,1},{1,2},{2,3},{3,4},{4,5},{5,6},{6,7},{7,8},{8,9},{9,10},{10,1... | collective-permute-start | bytes 98312 | tf_op jit(solution)/shard_map/ppermute | solution.py:19
  28.8 7.1 %collective-permute-start.16 = (bf16[1,32,1,512]{3,2,1,0:T(2,128)(2,1)S(1)}, bf16[1,32,1,512]{3,2,1,0:T(2,128)(2,1)S(1)}, u32[]{:S(2)}, u32[]{:S(2)}) collective-permute-start(bf16[1,32,1,512]{3,2,1,0:T(2,128)(2,1)S(1)} %get-tuple-element.25), channel_id=1, source_target_pairs={{1,0},{2,1},{3,2},{4,3},{5,4},{6,5},{7,6},{8,7},{9,8},{10,9},{11,1... | collective-permute-start | bytes 98312 | tf_op jit(solution)/shard_map/ppermute | solution.py:20
  37.3 5.4 %copy-start.1 = (bf16[512,512]{1,0:T(8,128)(2,1)S(1)}, bf16[512,512]{1,0:T(8,128)(2,1)}, u32[]{:S(2)}) copy-start(bf16[512,512]{1,0:T(8,128)(2,1)} %param.11) | copy-start | bytes 1572868
  38.4 5.3 %collective-permute-start.17 = (bf16[1,6,8,512]{3,2,1,0:T(8,128)(2,1)S(1)}, bf16[1,6,8,512]{3,2,1,0:T(8,128)(2,1)S(1)}, u32[]{:S(2)}, u32[]{:S(2)}) collective-permute-start(bf16[1,6,8,512]{3,2,1,0:T(8,128)(2,1)S(1)} %fusion.26), channel_id=1, source_target_pairs={{0,1},{1,0},{2,3},{3,2},{4,5},{5,4},{6,7},{7,6},{8,9},{9,8},{10,11... | collective-permute-start | bytes 147464 | tf_op jit(solution)/shard_map/ppermute | solution.py:166
  39.0 4.7 %collective-permute-start.18 = (bf16[1,6,8,512]{3,2,1,0:T(8,128)(2,1)S(1)}, bf16[1,6,8,512]{3,2,1,0:T(8,128)(2,1)S(1)}, u32[]{:S(2)}, u32[]{:S(2)}) collective-permute-start(bf16[1,6,8,512]{3,2,1,0:T(8,128)(2,1)S(1)} %fusion.26), channel_id=1, source_target_pairs={{0,2},{1,3},{2,0},{3,1},{4,6},{5,7},{6,4},{7,5},{8,10},{9,11},{10,... | collective-permute-start | bytes 147464 | tf_op jit(solution)/shard_map/ppermute | solution.py:166
  39.1 7.0 %collective-permute-start.19 = (bf16[1,6,8,512]{3,2,1,0:T(8,128)(2,1)S(1)}, bf16[1,6,8,512]{3,2,1,0:T(8,128)(2,1)S(1)}, u32[]{:S(2)}, u32[]{:S(2)}) collective-permute-start(bf16[1,6,8,512]{3,2,1,0:T(8,128)(2,1)S(1)} %fusion.26), channel_id=1, source_target_pairs={{0,3},{1,2},{2,1},{3,0},{4,7},{5,6},{6,5},{7,4},{8,11},{9,10},{10,... | collective-permute-start | bytes 147464 | tf_op jit(solution)/shard_map/ppermute | solution.py:166
  40.5 7.2 %collective-permute-start.20 = (bf16[1,6,8,512]{3,2,1,0:T(8,128)(2,1)S(1)}, bf16[1,6,8,512]{3,2,1,0:T(8,128)(2,1)S(1)}, u32[]{:S(2)}, u32[]{:S(2)}) collective-permute-start(bf16[1,6,8,512]{3,2,1,0:T(8,128)(2,1)S(1)} %fusion.26), channel_id=1, source_target_pairs={{0,4},{1,5},{2,6},{3,7},{4,0},{5,1},{6,2},{7,3},{8,12},{9,13},{10,... | collective-permute-start | bytes 147464 | tf_op jit(solution)/shard_map/ppermute | solution.py:166
  40.5 8.8 %collective-permute-start.21 = (bf16[1,6,8,512]{3,2,1,0:T(8,128)(2,1)S(1)}, bf16[1,6,8,512]{3,2,1,0:T(8,128)(2,1)S(1)}, u32[]{:S(2)}, u32[]{:S(2)}) collective-permute-start(bf16[1,6,8,512]{3,2,1,0:T(8,128)(2,1)S(1)} %fusion.26), channel_id=1, source_target_pairs={{0,5},{1,4},{2,7},{3,6},{4,1},{5,0},{6,3},{7,2},{8,13},{9,12},{10,... | collective-permute-start | bytes 147464 | tf_op jit(solution)/shard_map/ppermute | solution.py:166
  43.7 7.6 %collective-permute-start.22 = (bf16[1,6,8,512]{3,2,1,0:T(8,128)(2,1)S(1)}, bf16[1,6,8,512]{3,2,1,0:T(8,128)(2,1)S(1)}, u32[]{:S(2)}, u32[]{:S(2)}) collective-permute-start(bf16[1,6,8,512]{3,2,1,0:T(8,128)(2,1)S(1)} %fusion.26), channel_id=1, source_target_pairs={{0,6},{1,7},{2,4},{3,5},{4,2},{5,3},{6,0},{7,1},{8,14},{9,15},{10,... | collective-permute-start | bytes 147464 | tf_op jit(solution)/shard_map/ppermute | solution.py:166
  43.8 8.8 %collective-permute-start.23 = (bf16[1,6,8,512]{3,2,1,0:T(8,128)(2,1)S(1)}, bf16[1,6,8,512]{3,2,1,0:T(8,128)(2,1)S(1)}, u32[]{:S(2)}, u32[]{:S(2)}) collective-permute-start(bf16[1,6,8,512]{3,2,1,0:T(8,128)(2,1)S(1)} %fusion.26), channel_id=1, source_target_pairs={{0,7},{1,6},{2,5},{3,4},{4,3},{5,2},{6,1},{7,0},{8,15},{9,14},{10,... | collective-permute-start | bytes 147464 | tf_op jit(solution)/shard_map/ppermute | solution.py:166
  46.1 8.8 %collective-permute-start.24 = (bf16[1,6,8,512]{3,2,1,0:T(8,128)(2,1)S(1)}, bf16[1,6,8,512]{3,2,1,0:T(8,128)(2,1)S(1)}, u32[]{:S(2)}, u32[]{:S(2)}) collective-permute-start(bf16[1,6,8,512]{3,2,1,0:T(8,128)(2,1)S(1)} %fusion.26), channel_id=1, source_target_pairs={{0,8},{1,9},{2,10},{3,11},{4,12},{5,13},{6,14},{7,15},{8,0},{9,1},... | collective-permute-start | bytes 147464 | tf_op jit(solution)/shard_map/ppermute | solution.py:166
  47.6 9.0 %collective-permute-start.25 = (bf16[1,6,8,512]{3,2,1,0:T(8,128)(2,1)S(1)}, bf16[1,6,8,512]{3,2,1,0:T(8,128)(2,1)S(1)}, u32[]{:S(2)}, u32[]{:S(2)}) collective-permute-start(bf16[1,6,8,512]{3,2,1,0:T(8,128)(2,1)S(1)} %fusion.26), channel_id=1, source_target_pairs={{0,9},{1,8},{2,11},{3,10},{4,13},{5,12},{6,15},{7,14},{8,1},{9,0},... | collective-permute-start | bytes 147464 | tf_op jit(solution)/shard_map/ppermute | solution.py:166
  49.2 10.6 %collective-permute-start.26 = (bf16[1,6,8,512]{3,2,1,0:T(8,128)(2,1)S(1)}, bf16[1,6,8,512]{3,2,1,0:T(8,128)(2,1)S(1)}, u32[]{:S(2)}, u32[]{:S(2)}) collective-permute-start(bf16[1,6,8,512]{3,2,1,0:T(8,128)(2,1)S(1)} %fusion.26), channel_id=1, source_target_pairs={{0,10},{1,11},{2,8},{3,9},{4,14},{5,15},{6,12},{7,13},{8,2},{9,3},... | collective-permute-start | bytes 147464 | tf_op jit(solution)/shard_map/ppermute | solution.py:166
  51.3 9.5 %collective-permute-start.27 = (bf16[1,6,8,512]{3,2,1,0:T(8,128)(2,1)S(1)}, bf16[1,6,8,512]{3,2,1,0:T(8,128)(2,1)S(1)}, u32[]{:S(2)}, u32[]{:S(2)}) collective-permute-start(bf16[1,6,8,512]{3,2,1,0:T(8,128)(2,1)S(1)} %fusion.26), channel_id=1, source_target_pairs={{0,11},{1,10},{2,9},{3,8},{4,15},{5,14},{6,13},{7,12},{8,3},{9,2},... | collective-permute-start | bytes 147464 | tf_op jit(solution)/shard_map/ppermute | solution.py:166
  52.6 9.5 %collective-permute-start.28 = (bf16[1,6,8,512]{3,2,1,0:T(8,128)(2,1)S(1)}, bf16[1,6,8,512]{3,2,1,0:T(8,128)(2,1)S(1)}, u32[]{:S(2)}, u32[]{:S(2)}) collective-permute-start(bf16[1,6,8,512]{3,2,1,0:T(8,128)(2,1)S(1)} %fusion.26), channel_id=1, source_target_pairs={{0,12},{1,13},{2,14},{3,15},{4,8},{5,9},{6,10},{7,11},{8,4},{9,5},... | collective-permute-start | bytes 147464 | tf_op jit(solution)/shard_map/ppermute | solution.py:166
  55.0 10.6 %collective-permute-start.29 = (bf16[1,6,8,512]{3,2,1,0:T(8,128)(2,1)S(1)}, bf16[1,6,8,512]{3,2,1,0:T(8,128)(2,1)S(1)}, u32[]{:S(2)}, u32[]{:S(2)}) collective-permute-start(bf16[1,6,8,512]{3,2,1,0:T(8,128)(2,1)S(1)} %fusion.26), channel_id=1, source_target_pairs={{0,13},{1,12},{2,15},{3,14},{4,9},{5,8},{6,11},{7,10},{8,5},{9,4},... | collective-permute-start | bytes 147464 | tf_op jit(solution)/shard_map/ppermute | solution.py:166
  56.6 9.0 %collective-permute-start.30 = (bf16[1,6,8,512]{3,2,1,0:T(8,128)(2,1)S(1)}, bf16[1,6,8,512]{3,2,1,0:T(8,128)(2,1)S(1)}, u32[]{:S(2)}, u32[]{:S(2)}) collective-permute-start(bf16[1,6,8,512]{3,2,1,0:T(8,128)(2,1)S(1)} %fusion.26), channel_id=1, source_target_pairs={{0,14},{1,15},{2,12},{3,13},{4,10},{5,11},{6,8},{7,9},{8,6},{9,7},... | collective-permute-start | bytes 147464 | tf_op jit(solution)/shard_map/ppermute | solution.py:166
  59.8 6.9 %collective-permute-start.31 = (bf16[1,6,8,512]{3,2,1,0:T(8,128)(2,1)S(1)}, bf16[1,6,8,512]{3,2,1,0:T(8,128)(2,1)S(1)}, u32[]{:S(2)}, u32[]{:S(2)}) collective-permute-start(bf16[1,6,8,512]{3,2,1,0:T(8,128)(2,1)S(1)} %fusion.26), channel_id=1, source_target_pairs={{0,15},{1,14},{2,13},{3,12},{4,11},{5,10},{6,9},{7,8},{8,7},{9,6},... | collective-permute-start | bytes 147464 | tf_op jit(solution)/shard_map/ppermute | solution.py:166
  60.9 9.4 %collective-permute-start.32 = (bf16[1,32,3,512]{3,2,1,0:T(4,128)(2,1)S(1)}, bf16[1,32,3,512]{3,2,1,0:T(4,128)(2,1)S(1)}, u32[]{:S(2)}, u32[]{:S(2)}) collective-permute-start(bf16[1,32,3,512]{3,2,1,0:T(4,128)(2,1)S(1)} %get-tuple-element.14), channel_id=1, source_target_pairs={{0,1},{1,2},{2,3},{3,4},{4,5},{5,6},{6,7},{7,8},{8,9},{9,10},{10,1... | collective-permute-start | bytes 294920 | tf_op jit(solution)/shard_map/ppermute | solution.py:19
  62.1 8.1 %collective-permute-start.33 = (bf16[1,32,3,512]{3,2,1,0:T(4,128)(2,1)S(1)}, bf16[1,32,3,512]{3,2,1,0:T(4,128)(2,1)S(1)}, u32[]{:S(2)}, u32[]{:S(2)}) collective-permute-start(bf16[1,32,3,512]{3,2,1,0:T(4,128)(2,1)S(1)} %get-tuple-element.15), channel_id=1, source_target_pairs={{1,0},{2,1},{3,2},{4,3},{5,4},{6,5},{7,6},{8,7},{9,8},{10,9},{11,1... | collective-permute-start | bytes 294920 | tf_op jit(solution)/shard_map/ppermute | solution.py:20
  70.6 1.5 %copy-start.3 = (bf16[512,512]{1,0:T(8,128)(2,1)S(1)}, bf16[512,512]{1,0:T(8,128)(2,1)}, u32[]{:S(2)}) copy-start(bf16[512,512]{1,0:T(8,128)(2,1)} %param.12) | copy-start | bytes 1572868

commit v10 on v8

--- a/solution.py
+++ b/solution.py
@@ -1,3 +1,5 @@
+import functools
+
 import jax
 import jax.numpy as jnp
 from jax import lax
@@ -79,10 +81,9 @@
     )
 
 
-def attention_kernel(q_ref, k_ref, v_ref, lat_ref, wo_ref, out_ref, att_ref):
+def attention_kernel(cols, q_ref, k_ref, v_ref, lat_ref, wo_ref, out_ref, att_ref):
     cells, channels = q_ref.shape
     positions = k_ref.shape[0]
-    rows, cols = lat_ref.shape[0], lat_ref.shape[1]
     wide = cols + 2 * RADIUS
     span = 2 * RADIUS + 1
     head_size = channels // HEADS
@@ -114,27 +115,27 @@
             acc = jnp.where(lane == part, o, acc)
         att_ref[:, lanes] = acc.astype(jnp.bfloat16)
     mixed = jnp.dot(att_ref[...], wo_ref[...], preferred_element_type=jnp.float32)
-    lat = lat_ref[...].reshape(cells, channels)
+    lat = lat_ref[...]
     out_ref[...] = (lat.astype(jnp.float32) + mixed).astype(out_ref.dtype)
 
 
-def attend_and_mix(query, field_pad, w_key, w_value, own_tile, w_output):
-    rows, cols, channels = own_tile.shape
-    cells = rows * cols
-    flat = field_pad.reshape(-1, channels)
+def attend_rows(query, keys_field, w_key, w_value, lat, w_output):
+    q_rows, cols, channels = query.shape
+    cells = q_rows * cols
+    flat = keys_field.reshape(-1, channels)
     positions = -(-flat.shape[0] // 128) * 128
     flat = jnp.pad(flat, ((0, positions - flat.shape[0]), (0, 0)))
     key_flat = project(flat, w_key)
     value_flat = project(flat, w_value)
     vmem = pl.BlockSpec(memory_space=pltpu.VMEM)
     out = pl.pallas_call(
-        attention_kernel,
-        out_shape=jax.ShapeDtypeStruct((cells, channels), own_tile.dtype),
+        functools.partial(attention_kernel, cols),
+        out_shape=jax.ShapeDtypeStruct((cells, channels), lat.dtype),
         in_specs=[vmem] * 5,
         out_specs=vmem,
         scratch_shapes=[pltpu.VMEM((cells, channels), jnp.bfloat16)],
-    )(query.reshape(cells, channels), key_flat, value_flat, own_tile, w_output)
-    return out.reshape(rows, cols, channels)
+    )(query.reshape(cells, channels), key_flat, value_flat, lat.reshape(cells, channels), w_output)
+    return out.reshape(q_rows, cols, channels)
 
 
 def widen_tiles(field, margin):
@@ -183,12 +184,25 @@
     smoothed = smooth(padded, metric[0])
     query = project(smoothed, w_query)
     field_wide = padded_2(smoothed[None], (("blk", 2),), RADIUS)
+    rows = own_tile.shape[0]
+    span = 2 * RADIUS + 1
+    inner = attend_rows(
+        query[RADIUS : rows - RADIUS], field_wide[0], w_key, w_value,
+        own_tile[RADIUS : rows - RADIUS], w_output,
+    )
     rows3 = jnp.concatenate([smoothed[:RADIUS], smoothed[-RADIUS:]], axis=0)
     got3 = widen_tiles(doubling_gather(rows3[None], "blk"), RADIUS)
     edges3 = jnp.stack([got3[:, :RADIUS], got3[:, RADIUS:]], axis=1)
     field_got = pick_all(seam_rows, edges3)
     field_pad = place_rims(field_wide[0], field_got, seam_rows)
-    return attend_and_mix(query, field_pad, w_key, w_value, own_tile, w_output)[None]
+    top = attend_rows(
+        query[:RADIUS], field_pad[: RADIUS + span - 1], w_key, w_value, own_tile[:RADIUS], w_output
+    )
+    bottom = attend_rows(
+        query[rows - RADIUS :], field_pad[rows - RADIUS :], w_key, w_value,
+        own_tile[rows - RADIUS :], w_output,
+    )
+    return jnp.concatenate([top, inner, bottom], axis=0)[None]
 
 
 def solution(mesh):

time: 72.3 us -> 78.2 us (1.082)
  waiting for transfers between devices: 35.3 us -> 25.3 us
  Pallas kernels: 7 us -> 14.9 us
  local copies, waits for them, and re-layouts: 2.31 us -> 5.05 us
  matrix products: 4.51 us -> 7.04 us
  other arithmetic: 8.95 us -> 10.5 us
  starting transfers between devices: 13.7 us -> 14.7 us
    pallas_call x1 -> x3, Pallas kernels: 7 us -> 14.9 us  [attend_rows(): pl.pallas_call(functools.partial(attention_kernel, cols), out_shape=jax.S...]
    ppermute x8, waiting for transfers between devices: 30.5 us -> 23.8 us  [doubling_gather(): other = lax.ppermute(held, axis, [(i, i ^ step) for i in range(count)])]
    ppermute x2, waiting for transfers between devices: 4.72 us -> 1.03 us  [padded_2(): before = lax.ppermute(last, axis, up)]
    dot_general x3 -> x7, matrix products: 3.71 us -> 6.3 us  [project(): jnp.dot(flat, weight, preferred_element_type=jnp.float32)]
    broadcast_in_dim x0 -> x1, other arithmetic: none -> 1.49 us  [local(): return jnp.concatenate([top, inner, bottom], axis=0)[None]]
    slice x0 -> x2, local copies, waits for them, and re-layouts: none -> 1.32 us  [the longest x1 0.7 us: local(): query[RADIUS:rows - RADIUS]]
    ppermute x8, starting transfers between devices: 3.39 us -> 4.66 us  [doubling_gather(): other = lax.ppermute(held, axis, [(i, i ^ step) for i in range(count)])]
    reshape x1 -> x4, local copies, waits for them, and re-layouts: 0.16 us -> 1.4 us  [the longest x2 1.32 us: attend_rows(): lat.reshape(cells, channels)]
  transfers between devices with their start and end apart: 12 -> 12, of which waited for: 8 -> 8; matrix products, arithmetic and copies ran while one was open for 7% -> 12% of each run, Pallas kernels for 0% -> 7%
where the time goes in v10:
time: 78.2 us; the launch traced here: 77.9 us
  waiting for transfers between devices  25.3 us (32%)
  Pallas kernels  14.9 us (19%)
  starting transfers between devices  14.7 us (19%)
  other arithmetic  10.5 us (13%)
  matrix products  7.04 us (9%)
  local copies, waits for them, and re-layouts  5.05 us (6%)
    ppermute x8, waiting for transfers between devices, doubling_gather(): other = lax.ppermute(held, axis, [(i, i ^ step) for i in range(count)])  23.8 us
    pallas_call x3, Pallas kernels, attend_rows(): pl.pallas_call(functools.partial(attention_kernel, cols), out_shape=jax.S...  14.9 us
    ppermute x2, starting transfers between devices, padded_2(): after = lax.ppermute(first, axis, down)  9.49 us
    dot_general x7, matrix products, project(): jnp.dot(flat, weight, preferred_element_type=jnp.float32)  6.3 us
    ppermute x8, starting transfers between devices, doubling_gather(): other = lax.ppermute(held, axis, [(i, i ^ step) for i in range(count)])  4.66 us
    convert_element_type x2, other arithmetic, normalize(): return (values * factor * norm_gain).astype(jnp.bfloat16)  2.16 us
    select_n x8, other arithmetic, doubling_gather(): jnp.where(low, jnp.concatenate([held, other], axis=0), jnp.concatenate([o...  1.92 us
  transfers between devices with their start and end apart: 12, of which 8 were waited for; matrix products, arithmetic and copies ran while one was open for 12% of the time, Pallas kernels for 7%

profile of v10, /device:TPU:0, one launch (start us, length us, event | category | flops | bytes accessed | tf_op | source)
XLA Modules:
  0.0 77.9 jit_solution(7829937539071183788)
XLA Ops:
  0.0 1.2 %fusion.15 = f32[32,8]{1,0:T(8,128)S(1)} fusion(bf16[1,32,8,512]{3,2,1,0:T(8,128)(2,1)} %param.8), kind=kLoop, calls=%fused_computation.30 | loop fusion | flops 392960 | bytes 263168 | tf_op jit(solution)/shard_map/reduce_sum | solution.py:29
  1.2 1.1 %fusion.19 = bf16[1,32,8,512]{3,2,1,0:T(8,128)(2,1)S(1)} fusion(bf16[1,32,8,512]{3,2,1,0:T(8,128)(2,1)} %param.8, f32[512]{0:T(512)} %param.9, f32[32,8]{1,0:T(8,128)S(1)} %add_rsqrt_fusion), kind=kLoop, calls=%fused_computation.34 | loop fusion | flops 524288 | bytes 527360 | tf_op jit(solution)/shard_map/convert_element_type | solution.py:30
  2.4 0.5 collective-permute-start.4
  2.9 5.1 %collective-permute-start.5 = (bf16[1,32,1,512]{3,2,1,0:T(2,128)(2,1)S(1)}, bf16[1,32,1,512]{3,2,1,0:T(2,128)(2,1)S(1)}, u32[]{:S(2)}, u32[]{:S(2)}) collective-permute-start(bf16[1,32,1,512]{3,2,1,0:T(2,128)(2,1)S(1)} %get-tuple-element.33), channel_id=1, source_target_pairs={{1,0},{2,1},{3,2},{4,3},{5,4},{6,5},{7,6},{8,7},{9,8},{10,9},{11,1... | collective-permute-start | bytes 98312 | tf_op jit(solution)/shard_map/ppermute | solution.py:22
  7.9 1.1 %fusion.17 = bf16[32,8,512]{2,1,0:T(8,128)(2,1)S(1)} fusion(bf16[1,32,8,512]{3,2,1,0:T(8,128)(2,1)} %param.8, f32[512]{0:T(512)} %param.9, f32[32,8]{1,0:T(8,128)S(1)} %add_rsqrt_fusion), kind=kLoop, calls=%fused_computation.32 | loop fusion | flops 524288 | bytes 527360 | tf_op jit(solution)/shard_map/convert_element_type | solution.py:30
  9.2 0.6 slice_bitcast_fusion.4
  9.8 0.7 slice_bitcast_fusion.2.lat_ref
  10.5 0.2 slice_reduce_fusion.2
  11.0 3.9 %collective-permute-done.1 = bf16[2,2,8,512]{3,0,1,2:T(2,128)(2,1)S(1)} collective-permute-done((bf16[2,2,8,512]{3,0,1,2:T(2,128)(2,1)S(1)}, bf16[2,2,8,512]{3,0,1,2:T(2,128)(2,1)S(1)}, u32[]{:S(2)}, u32[]{:S(2)}) %collective-permute-start.1) | collective-permute-done | bytes 32800 | tf_op jit(solution)/shard_map/ppermute | solution.py:164
  15.0 0.2 collective-permute-start.2
  15.3 4.0 %collective-permute-done.2 = bf16[4,2,8,512]{3,0,1,2:T(4,128)(2,1)S(1)} collective-permute-done((bf16[4,2,8,512]{3,0,1,2:T(4,128)(2,1)S(1)}, bf16[4,2,8,512]{3,0,1,2:T(4,128)(2,1)S(1)}, u32[]{:S(2)}, u32[]{:S(2)}) %collective-permute-start.2) | collective-permute-done | bytes 65568 | tf_op jit(solution)/shard_map/ppermute | solution.py:164
  19.5 1.2 %collective-permute-start.3 = (bf16[8,2,8,512]{3,0,1,2:T(8,128)(2,1)S(1)}, bf16[8,2,8,512]{3,0,1,2:T(8,128)(2,1)S(1)}, u32[]{:S(2)}, u32[]{:S(2)}) collective-permute-start(bf16[8,2,8,512]{3,0,1,2:T(8,128)(2,1)S(1)} %maximum_select_fusion.4), channel_id=1, source_target_pairs={{0,8},{1,9},{2,10},{3,11},{4,12},{5,13},{6,14},{7,15},{8,0},{9,1},... | collective-permute-start | bytes 393224 | tf_op jit(solution)/shard_map/ppermute | solution.py:164
  20.7 0.2 compare_reduce_fusion
  21.6 0.3 maximum_bitcast_fusion
  21.9 4.7 %collective-permute-done.3 = bf16[8,2,8,512]{3,0,1,2:T(8,128)(2,1)S(1)} collective-permute-done((bf16[8,2,8,512]{3,0,1,2:T(8,128)(2,1)S(1)}, bf16[8,2,8,512]{3,0,1,2:T(8,128)(2,1)S(1)}, u32[]{:S(2)}, u32[]{:S(2)}) %collective-permute-start.3) | collective-permute-done | bytes 131104 | tf_op jit(solution)/shard_map/ppermute | solution.py:164
  26.8 0.3 fusion.12
  27.2 1.1 %fusion.72 = bf16[1,32,8,512]{3,2,1,0:T(8,128)(2,1)S(1)} fusion(bf16[1,10,512]{2,1,0:T(8,128)(2,1)S(1)} %copy.57, bf16[32,10,512]{2,1,0:T(8,128)(2,1)S(1)} %maximum_bitcast_fusion, f32[32,8]{1,0:T(8,128)S(1)} %copy.59, f32[32,8]{1,0:T(8,128)S(1)} %copy.58, f32[32,8]{1,0:T(8,128)S(1)} %copy.56, f32[32,8]{1,0:T(8,128)S(1)} %copy.55, f32[32,8]{1,0:T(8,128)S(1)} %copy.54, ...), kind=kLoop, calls=%fused_computation.135 | loop fusion | flops 5898240 | bytes 1753088 | tf_op jit(solution)/shard_map/broadcast_in_dim | solution.py:186
  28.3 1.1 %add_convert_fusion = bf16[32,8,512]{2,1,0:T(8,128)(2,1)S(1)} fusion(bf16[32,10,512]{2,1,0:T(8,128)(2,1)S(1)} %maximum_bitcast_fusion, bf16[1,10,512]{2,1,0:T(8,128)(2,1)S(1)} %copy.57, bf16[1,10,512]{2,1,0:T(8,128)(2,1)S(1)} %copy.50, f32[32,8]{1,0:T(8,128)S(1)} %copy.59, f32[32,8]{1,0:T(8,128)S(1)} %copy.58, f32[32,8]{1,0:T(8,128)S(1)} %copy.56, ...), kind=kLoop, calls=%fused_computation.37 | loop fusion | flops 5898240 | bytes 1753088 | tf_op jit(solution)/shard_map/convert_element_type | solution.py:71
  29.6 0.3 convolution_convert_fusion.2
  29.9 1.0 %collective-permute-done.6 = bf16[1,6,8,512]{3,0,2,1:T(2,128)(2,1)S(1)} collective-permute-done((bf16[1,6,8,512]{3,0,2,1:T(2,128)(2,1)S(1)}, bf16[1,6,8,512]{3,0,2,1:T(2,128)(2,1)S(1)}, u32[]{:S(2)}, u32[]{:S(2)}) %collective-permute-start.6) | collective-permute-done | bytes 49184 | tf_op jit(solution)/shard_map/ppermute | solution.py:164
  30.9 0.4 broadcast_select_fusion
  31.3 0.8 %collective-permute-start.7 = (bf16[2,6,8,512]{3,0,2,1:T(2,128)(2,1)S(1)}, bf16[2,6,8,512]{3,0,2,1:T(2,128)(2,1)S(1)}, u32[]{:S(2)}, u32[]{:S(2)}) collective-permute-start(bf16[2,6,8,512]{3,0,2,1:T(2,128)(2,1)S(1)} %broadcast_select_fusion), channel_id=1, source_target_pairs={{0,2},{1,3},{2,0},{3,1},{4,6},{5,7},{6,4},{7,5},{8,10},{9,11},{10,... | collective-permute-start | bytes 294920 | tf_op jit(solution)/shard_map/ppermute | solution.py:164
  32.3 4.4 %collective-permute-start.11 = (bf16[1,32,3,512]{3,2,1,0:T(4,128)(2,1)S(1)}, bf16[1,32,3,512]{3,2,1,0:T(4,128)(2,1)S(1)}, u32[]{:S(2)}, u32[]{:S(2)}) collective-permute-start(bf16[1,32,3,512]{3,2,1,0:T(4,128)(2,1)S(1)} %get-tuple-element.23), channel_id=1, source_target_pairs={{1,0},{2,1},{3,2},{4,3},{5,4},{6,5},{7,6},{8,7},{9,8},{10,9},{11,1... | collective-permute-start | bytes 294920 | tf_op jit(solution)/shard_map/ppermute | solution.py:22
  36.7 0.4 maximum_select_fusion.3
  37.1 0.6 fusion.56
  37.8 0.7 slice.292.q_ref
  38.5 1.0 %collective-permute-done.10 = bf16[1,32,3,512]{3,2,1,0:T(4,128)(2,1)S(1)} collective-permute-done((bf16[1,32,3,512]{3,2,1,0:T(4,128)(2,1)S(1)}, bf16[1,32,3,512]{3,2,1,0:T(4,128)(2,1)S(1)}, u32[]{:S(2)}, u32[]{:S(2)}) %collective-permute-start.10) | collective-permute-done | bytes 98336 | tf_op jit(solution)/shard_map/ppermute | solution.py:21
  39.5 0.4 collective-permute-done.11
  39.9 0.3 pad_maximum_fusion.2
  40.3 2.4 %collective-permute-done.8 = bf16[4,6,8,512]{3,0,2,1:T(4,128)(2,1)S(1)} collective-permute-done((bf16[4,6,8,512]{3,0,2,1:T(4,128)(2,1)S(1)}, bf16[4,6,8,512]{3,0,2,1:T(4,128)(2,1)S(1)}, u32[]{:S(2)}, u32[]{:S(2)}) %collective-permute-start.8) | collective-permute-done | bytes 196640 | tf_op jit(solution)/shard_map/ppermute | solution.py:164
  42.8 0.3 maximum_select_fusion.1
  43.1 2.1 %collective-permute-start.9 = (bf16[8,6,8,512]{3,0,2,1:T(8,128)(2,1)S(1)}, bf16[8,6,8,512]{3,0,2,1:T(8,128)(2,1)S(1)}, u32[]{:S(2)}, u32[]{:S(2)}) collective-permute-start(bf16[8,6,8,512]{3,0,2,1:T(8,128)(2,1)S(1)} %maximum_select_fusion.1), channel_id=1, source_target_pairs={{0,8},{1,9},{2,10},{3,11},{4,12},{5,13},{6,14},{7,15},{8,0},{9,1},... | collective-permute-start | bytes 1179656 | tf_op jit(solution)/shard_map/ppermute | solution.py:164
  45.3 1.2 %convolution_convert_fusion.v_ref = bf16[512,512]{1,0:T(8,128)(2,1)} fusion(bf16[512,512]{1,0:T(8,128)(2,1)S(1)} %copy-done, bf16[448,512]{1,0:T(8,128)(2,1)S(1)} %reshape_squeeze.3), kind=kOutput, calls=%fused_computation.8 | convolution fusion | flops 268697600 | bytes 1507328 | tf_op jit(solution)/shard_map/dot_general | solution.py:78
  46.5 1.2 %convolution_convert_fusion.1.k_ref = bf16[512,512]{1,0:T(8,128)(2,1)} fusion(bf16[512,512]{1,0:T(8,128)(2,1)S(1)} %copy-done.1, bf16[448,512]{1,0:T(8,128)(2,1)S(1)} %reshape_squeeze.3), kind=kOutput, calls=%fused_computation.9 | convolution fusion | flops 268697600 | bytes 1507328 | tf_op jit(solution)/shard_map/dot_general | solution.py:78
  47.7 5.7 %shard_map.83 = bf16[208,512]{1,0:T(8,128)(2,1)} custom-call(bf16[208,512]{1,0:T(8,128)(2,1)} %slice.292.q_ref, bf16[512,512]{1,0:T(8,128)(2,1)} %convolution_convert_fusion.1.k_ref, bf16[512,512]{1,0:T(8,128)(2,1)} %convolution_convert_fusion.v_ref, bf16[208,512]{1,0:T(8,128)(2,1)} %slice_bitcast_fusion.2.lat_ref, bf16[512,512]{1,0:T(8,128)(2,1)} %wo_ref.5), custom_call_target="tpu_custom_call" | custom-call | tf_op jit(solution)/shard_map/pallas_call | solution.py:131
  53.5 7.8 %collective-permute-done.9 = bf16[8,6,8,512]{3,0,2,1:T(8,128)(2,1)S(1)} collective-permute-done((bf16[8,6,8,512]{3,0,2,1:T(8,128)(2,1)S(1)}, bf16[8,6,8,512]{3,0,2,1:T(8,128)(2,1)S(1)}, u32[]{:S(2)}, u32[]{:S(2)}) %collective-permute-start.9) | collective-permute-done | bytes 393248 | tf_op jit(solution)/shard_map/ppermute | solution.py:164
  61.3 0.3 maximum_select_fusion
  61.6 0.2 fusion.54
  61.8 0.4 fusion.55
  62.2 0.3 fusion
  62.6 0.4 fusion.9
  63.6 0.9 %convolution_convert_fusion.3.v_ref = bf16[128,512]{1,0:T(8,128)(2,1)} fusion(bf16[512,512]{1,0:T(8,128)(2,1)S(1)} %copy-done, bf16[126,512]{1,0:T(8,128)(2,1)S(1)} %reshape.142), kind=kOutput, calls=%fused_computation.11 | convolution fusion | flops 67174400 | bytes 784384 | tf_op jit(solution)/shard_map/dot_general | solution.py:78
  64.5 0.9 %convolution_convert_fusion.4.k_ref = bf16[128,512]{1,0:T(8,128)(2,1)} fusion(bf16[512,512]{1,0:T(8,128)(2,1)S(1)} %copy-done.1, bf16[126,512]{1,0:T(8,128)(2,1)S(1)} %reshape.142), kind=kOutput, calls=%fused_computation.12 | convolution fusion | flops 67174400 | bytes 784384 | tf_op jit(solution)/shard_map/dot_general | solution.py:78
  65.4 0.9 %convolution_convert_fusion.5.v_ref = bf16[128,512]{1,0:T(8,128)(2,1)} fusion(bf16[512,512]{1,0:T(8,128)(2,1)S(1)} %copy-done, bf16[126,512]{1,0:T(8,128)(2,1)S(1)} %reshape.137), kind=kOutput, calls=%fused_computation.13 | convolution fusion | flops 67174400 | bytes 784384 | tf_op jit(solution)/shard_map/dot_general | solution.py:78
  66.3 0.9 %convolution_convert_fusion.6.k_ref = bf16[128,512]{1,0:T(8,128)(2,1)} fusion(bf16[512,512]{1,0:T(8,128)(2,1)S(1)} %copy-done.1, bf16[126,512]{1,0:T(8,128)(2,1)S(1)} %reshape.137), kind=kOutput, calls=%fused_computation.14 | convolution fusion | flops 67174400 | bytes 784384 | tf_op jit(solution)/shard_map/dot_general | solution.py:78
  67.2 4.6 %shard_map.84 = bf16[24,512]{1,0:T(8,128)(2,1)} custom-call(bf16[24,512]{1,0:T(8,128)(2,1)} %get-tuple-element.21.q_ref, bf16[128,512]{1,0:T(8,128)(2,1)} %convolution_convert_fusion.4.k_ref, bf16[128,512]{1,0:T(8,128)(2,1)} %convolution_convert_fusion.3.v_ref, bf16[24,512]{1,0:T(8,128)(2,1)} %get-tuple-element.19.lat_ref, bf16[512,512]{1,0:T(8,128)(2,1)} %wo_ref.5), custom_call_target="tpu_custom_call" | custom-call | tf_op jit(solution)/shard_map/pallas_call | solution.py:131
  71.8 4.6 %shard_map.82 = bf16[24,512]{1,0:T(8,128)(2,1)} custom-call(bf16[24,512]{1,0:T(8,128)(2,1)} %get-tuple-element.20.q_ref, bf16[128,512]{1,0:T(8,128)(2,1)} %convolution_convert_fusion.6.k_ref, bf16[128,512]{1,0:T(8,128)(2,1)} %convolution_convert_fusion.5.v_ref, bf16[24,512]{1,0:T(8,128)(2,1)} %get-tuple-element.18.lat_ref, bf16[512,512]{1,0:T(8,128)(2,1)} %wo_ref.5), custom_call_target="tpu_custom_call" | custom-call | tf_op jit(solution)/shard_map/pallas_call | solution.py:131
  76.4 1.5 %maximum_bitcast_fusion.1 = bf16[1,32,8,512]{3,2,1,0:T(8,128)(2,1)} fusion(bf16[3,8,512]{2,1,0:T(8,128)(2,1)} %bitcast.91, bf16[26,8,512]{2,1,0:T(8,128)(2,1)S(1)} %bitcast.90, bf16[3,8,512]{2,1,0:T(8,128)(2,1)} %bitcast.92), kind=kLoop, calls=%fused_computation.59 | loop fusion | flops 262144 | bytes 524288 | tf_op jit(solution)/shard_map/broadcast_in_dim | solution.py:205
  (64 shorter events, 3.0 us)
Async XLA Ops:
  0.0 45.3 %copy-start = (bf16[512,512]{1,0:T(8,128)(2,1)S(1)}, bf16[512,512]{1,0:T(8,128)(2,1)}, u32[]{:S(2)}) copy-start(bf16[512,512]{1,0:T(8,128)(2,1)} %param.13) | copy-start | bytes 1572868
  0.0 9.2 %copy-start.2 = (bf16[1,32,8,512]{3,2,1,0:T(8,128)(2,1)S(1)}, bf16[1,32,8,512]{3,2,1,0:T(8,128)(2,1)}, u32[]{:S(2)}) copy-start(bf16[1,32,8,512]{3,2,1,0:T(8,128)(2,1)} %param.8) | copy-start | bytes 786436
  0.0 10.5 %copy-start.6 = (s32[1,2,3]{2,1,0:T(2,128)S(1)}, s32[1,2,3]{2,1,0:T(2,128)}, u32[]{:S(2)}) copy-start(s32[1,2,3]{2,1,0:T(2,128)} %param.15) | copy-start | bytes 76
  0.0 10.7 %copy-start.5 = (f32[1,9,32,8]{2,3,1,0:T(8,128)S(1)}, f32[1,9,32,8]{2,3,1,0:T(8,128)}, u32[]{:S(2)}) copy-start(f32[1,9,32,8]{2,3,1,0:T(8,128)} %param.10) | copy-start | bytes 27652
  2.4 19.2 %collective-permute-start.4 = (bf16[1,32,1,512]{3,2,1,0:T(2,128)(2,1)S(1)}, bf16[1,32,1,512]{3,2,1,0:T(2,128)(2,1)S(1)}, u32[]{:S(2)}, u32[]{:S(2)}) collective-permute-start(bf16[1,32,1,512]{3,2,1,0:T(2,128)(2,1)S(1)} %get-tuple-element.32), channel_id=1, source_target_pairs={{0,1},{1,2},{2,3},{3,4},{4,5},{5,6},{6,7},{7,8},{8,9},{9,10},{10,1... | collective-permute-start | bytes 98312 | tf_op jit(solution)/shard_map/ppermute | solution.py:21
  2.9 18.7 %collective-permute-start.5 = (bf16[1,32,1,512]{3,2,1,0:T(2,128)(2,1)S(1)}, bf16[1,32,1,512]{3,2,1,0:T(2,128)(2,1)S(1)}, u32[]{:S(2)}, u32[]{:S(2)}) collective-permute-start(bf16[1,32,1,512]{3,2,1,0:T(2,128)(2,1)S(1)} %get-tuple-element.33), channel_id=1, source_target_pairs={{1,0},{2,1},{3,2},{4,3},{5,4},{6,5},{7,6},{8,7},{9,8},{10,9},{11,1... | collective-permute-start | bytes 98312 | tf_op jit(solution)/shard_map/ppermute | solution.py:22
  9.1 1.7 %collective-permute-start = (bf16[1,2,8,512]{3,0,1,2:T(2,128)(2,1)S(1)}, bf16[1,2,8,512]{3,0,1,2:T(2,128)(2,1)S(1)}, u32[]{:S(2)}, u32[]{:S(2)}) collective-permute-start(bf16[1,2,8,512]{3,0,1,2:T(2,128)(2,1)S(1)} %copy.48), channel_id=1, source_target_pairs={{0,1},{1,0},{2,3},{3,2},{4,5},{5,4},{6,7},{7,6},{8,9},{9,8},{10,11... | collective-permute-start | bytes 49160 | tf_op jit(solution)/shard_map/ppermute | solution.py:164
  10.9 4.0 %collective-permute-start.1 = (bf16[2,2,8,512]{3,0,1,2:T(2,128)(2,1)S(1)}, bf16[2,2,8,512]{3,0,1,2:T(2,128)(2,1)S(1)}, u32[]{:S(2)}, u32[]{:S(2)}) collective-permute-start(bf16[2,2,8,512]{3,0,1,2:T(2,128)(2,1)S(1)} %broadcast_select_fusion.3), channel_id=1, source_target_pairs={{0,2},{1,3},{2,0},{3,1},{4,6},{5,7},{6,4},{7,5},{8,10},{9,11},{10,... | collective-permute-start | bytes 98312 | tf_op jit(solution)/shard_map/ppermute | solution.py:164
  15.0 4.3 %collective-permute-start.2 = (bf16[4,2,8,512]{3,0,1,2:T(4,128)(2,1)S(1)}, bf16[4,2,8,512]{3,0,1,2:T(4,128)(2,1)S(1)}, u32[]{:S(2)}, u32[]{:S(2)}) collective-permute-start(bf16[4,2,8,512]{3,0,1,2:T(4,128)(2,1)S(1)} %maximum_select_fusion.5), channel_id=1, source_target_pairs={{0,4},{1,5},{2,6},{3,7},{4,0},{5,1},{6,2},{7,3},{8,12},{9,13},{10,... | collective-permute-start | bytes 196616 | tf_op jit(solution)/shard_map/ppermute | solution.py:164
  19.5 7.1 %collective-permute-start.3 = (bf16[8,2,8,512]{3,0,1,2:T(8,128)(2,1)S(1)}, bf16[8,2,8,512]{3,0,1,2:T(8,128)(2,1)S(1)}, u32[]{:S(2)}, u32[]{:S(2)}) collective-permute-start(bf16[8,2,8,512]{3,0,1,2:T(8,128)(2,1)S(1)} %maximum_select_fusion.4), channel_id=1, source_target_pairs={{0,8},{1,9},{2,10},{3,11},{4,12},{5,13},{6,14},{7,15},{8,0},{9,1},... | collective-permute-start | bytes 393224 | tf_op jit(solution)/shard_map/ppermute | solution.py:164
  28.3 1.3 %copy-start.4 = (bf16[512,512]{1,0:T(8,128)(2,1)S(1)}, bf16[512,512]{1,0:T(8,128)(2,1)}, u32[]{:S(2)}) copy-start(bf16[512,512]{1,0:T(8,128)(2,1)} %param.11) | copy-start | bytes 1572868
  29.5 1.4 %collective-permute-start.6 = (bf16[1,6,8,512]{3,0,2,1:T(2,128)(2,1)S(1)}, bf16[1,6,8,512]{3,0,2,1:T(2,128)(2,1)S(1)}, u32[]{:S(2)}, u32[]{:S(2)}) collective-permute-start(bf16[1,6,8,512]{3,0,2,1:T(2,128)(2,1)S(1)} %copy.61), channel_id=1, source_target_pairs={{0,1},{1,0},{2,3},{3,2},{4,5},{5,4},{6,7},{7,6},{8,9},{9,8},{10,11... | collective-permute-start | bytes 147464 | tf_op jit(solution)/shard_map/ppermute | solution.py:164
  31.3 5.4 %collective-permute-start.7 = (bf16[2,6,8,512]{3,0,2,1:T(2,128)(2,1)S(1)}, bf16[2,6,8,512]{3,0,2,1:T(2,128)(2,1)S(1)}, u32[]{:S(2)}, u32[]{:S(2)}) collective-permute-start(bf16[2,6,8,512]{3,0,2,1:T(2,128)(2,1)S(1)} %broadcast_select_fusion), channel_id=1, source_target_pairs={{0,2},{1,3},{2,0},{3,1},{4,6},{5,7},{6,4},{7,5},{8,10},{9,11},{10,... | collective-permute-start | bytes 294920 | tf_op jit(solution)/shard_map/ppermute | solution.py:164
  32.2 7.3 %collective-permute-start.10 = (bf16[1,32,3,512]{3,2,1,0:T(4,128)(2,1)S(1)}, bf16[1,32,3,512]{3,2,1,0:T(4,128)(2,1)S(1)}, u32[]{:S(2)}, u32[]{:S(2)}) collective-permute-start(bf16[1,32,3,512]{3,2,1,0:T(4,128)(2,1)S(1)} %get-tuple-element.22), channel_id=1, source_target_pairs={{0,1},{1,2},{2,3},{3,4},{4,5},{5,6},{6,7},{7,8},{8,9},{9,10},{10,1... | collective-permute-start | bytes 294920 | tf_op jit(solution)/shard_map/ppermute | solution.py:21
  32.3 7.6 %collective-permute-start.11 = (bf16[1,32,3,512]{3,2,1,0:T(4,128)(2,1)S(1)}, bf16[1,32,3,512]{3,2,1,0:T(4,128)(2,1)S(1)}, u32[]{:S(2)}, u32[]{:S(2)}) collective-permute-start(bf16[1,32,3,512]{3,2,1,0:T(4,128)(2,1)S(1)} %get-tuple-element.23), channel_id=1, source_target_pairs={{1,0},{2,1},{3,2},{4,3},{5,4},{6,5},{7,6},{8,7},{9,8},{10,9},{11,1... | collective-permute-start | bytes 294920 | tf_op jit(solution)/shard_map/ppermute | solution.py:22
  37.1 5.7 %collective-permute-start.8 = (bf16[4,6,8,512]{3,0,2,1:T(4,128)(2,1)S(1)}, bf16[4,6,8,512]{3,0,2,1:T(4,128)(2,1)S(1)}, u32[]{:S(2)}, u32[]{:S(2)}) collective-permute-start(bf16[4,6,8,512]{3,0,2,1:T(4,128)(2,1)S(1)} %maximum_select_fusion.3), channel_id=1, source_target_pairs={{0,4},{1,5},{2,6},{3,7},{4,0},{5,1},{6,2},{7,3},{8,12},{9,13},{10,... | collective-permute-start | bytes 589832 | tf_op jit(solution)/shard_map/ppermute | solution.py:164
  40.3 6.2 %copy-start.1 = (bf16[512,512]{1,0:T(8,128)(2,1)S(1)}, bf16[512,512]{1,0:T(8,128)(2,1)}, u32[]{:S(2)}) copy-start(bf16[512,512]{1,0:T(8,128)(2,1)} %param.12) | copy-start | bytes 1572868
  43.1 18.1 %collective-permute-start.9 = (bf16[8,6,8,512]{3,0,2,1:T(8,128)(2,1)S(1)}, bf16[8,6,8,512]{3,0,2,1:T(8,128)(2,1)S(1)}, u32[]{:S(2)}, u32[]{:S(2)}) collective-permute-start(bf16[8,6,8,512]{3,0,2,1:T(8,128)(2,1)S(1)} %maximum_select_fusion.1), channel_id=1, source_target_pairs={{0,8},{1,9},{2,10},{3,11},{4,12},{5,13},{6,14},{7,15},{8,0},{9,1},... | collective-permute-start | bytes 1179656 | tf_op jit(solution)/shard_map/ppermute | solution.py:164
  66.3 10.1 %copy-start.3 = (bf16[208,512]{1,0:T(8,128)(2,1)S(1)}, bf16[208,512]{1,0:T(8,128)(2,1)}, u32[]{:S(2)}) copy-start(bf16[208,512]{1,0:T(8,128)(2,1)} %shard_map.83) | copy-start | bytes 638980

commit v11 on v8

--- a/solution.py
+++ b/solution.py
@@ -157,16 +157,17 @@
     if count & (count - 1):
         return lax.all_gather(block, axis, axis=0, tiled=True)
     me = lax.axis_index(axis)
+    bits = count.bit_length() - 1
     held = block
-    step = 1
-    while step < count:
+    for k in reversed(range(bits)):
+        step = 1 << k
         other = lax.ppermute(held, axis, [(i, i ^ step) for i in range(count)])
         low = (me & step) == 0
         held = jnp.where(
             low, jnp.concatenate([held, other], axis=0), jnp.concatenate([other, held], axis=0)
         )
-        step *= 2
-    return held
+    reverse = [int(format(j, "0%db" % bits)[::-1], 2) for j in range(count)] if bits else [0]
+    return jnp.take(held, jnp.array(reverse, dtype=jnp.int32), axis=0)
 
 
 def local(latents, norm_gain, metric, w_query, w_key, w_value, w_output, seam_table):

time: 72.3 us -> 61.8 us (0.85)
  waiting for transfers between devices: 35.3 us -> 24.6 us
  local copies, waits for them, and re-layouts: 2.31 us -> 3.81 us
  other arithmetic: 8.95 us -> 7.67 us
    ppermute x8, waiting for transfers between devices: 30.5 us -> 22.9 us  [doubling_gather(): other = lax.ppermute(held, axis, [(i, i ^ step) for i in range(count)])]
    ppermute x2, waiting for transfers between devices: 4.72 us -> 1.65 us  [padded_2(): before = lax.ppermute(last, axis, up)]
    ppermute x2, starting transfers between devices: 10.1 us -> 8.38 us  [padded_2(): after = lax.ppermute(first, axis, down)]
    gather x0 -> x3, local copies, waits for them, and re-layouts: none -> 1.6 us  [doubling_gather(): return jnp.take(held, jnp.array(reverse, dtype=jnp.int32), axis=0)]
    select_n x8, other arithmetic: 1.53 us -> 0.25 us  [doubling_gather(): jnp.where(low, jnp.concatenate([held, other], axis=0), jnp.concatenate([o...]
    ppermute x8, starting transfers between devices: 3.39 us -> 4.64 us  [doubling_gather(): other = lax.ppermute(held, axis, [(i, i ^ step) for i in range(count)])]
  transfers between devices with their start and end apart: 12 -> 12, of which waited for: 8 -> 7; matrix products, arithmetic and copies ran while one was open for 7% -> 8% of each run, Pallas kernels for 0% -> 0%
where the time goes in v11:
time: 61.8 us; the launch traced here: 61.6 us
  waiting for transfers between devices  24.6 us (40%)
  starting transfers between devices  13.6 us (22%)
  other arithmetic  7.67 us (12%)
  Pallas kernels  7 us (11%)
  matrix products  4.5 us (7%)
  local copies, waits for them, and re-layouts  3.81 us (6%)
    ppermute x8, waiting for transfers between devices, doubling_gather(): other = lax.ppermute(held, axis, [(i, i ^ step) for i in range(count)])  22.9 us
    ppermute x2, starting transfers between devices, padded_2(): after = lax.ppermute(first, axis, down)  8.38 us
    pallas_call x1, Pallas kernels, attend_and_mix(): pl.pallas_call(attention_kernel, out_shape=jax.ShapeDtypeStruct((cells, c...  7 us
    ppermute x8, starting transfers between devices, doubling_gather(): other = lax.ppermute(held, axis, [(i, i ^ step) for i in range(count)])  4.64 us
    dot_general x3, matrix products, project(): jnp.dot(flat, weight, preferred_element_type=jnp.float32)  3.7 us
    convert_element_type x2, other arithmetic, normalize(): return (values * factor * norm_gain).astype(jnp.bfloat16)  2.17 us
    ppermute x2, waiting for transfers between devices, padded_2(): before = lax.ppermute(last, axis, up)  1.65 us
    gather x3, local copies, waits for them, and re-layouts, doubling_gather(): return jnp.take(held, jnp.array(reverse, dtype=jnp.int32), axis=0)  1.6 us
  transfers between devices with their start and end apart: 12, of which 7 were waited for; matrix products, arithmetic and copies ran while one was open for 8% of the time, Pallas kernels for 0%

profile of v11, /device:TPU:0, one launch (start us, length us, event | category | flops | bytes accessed | tf_op | source)
XLA Modules:
  0.0 61.6 jit_solution(15722342475737979757)
XLA Ops:
  0.0 1.1 %fusion.15 = f32[32,8]{1,0:T(8,128)S(1)} fusion(bf16[1,32,8,512]{3,2,1,0:T(8,128)(2,1)} %param.10), kind=kLoop, calls=%fused_computation.29 | loop fusion | flops 392960 | bytes 263168 | tf_op jit(solution)/shard_map/reduce_sum | solution.py:27
  1.2 1.1 %fusion.17 = bf16[32,8,512]{2,1,0:T(8,128)(2,1)S(1)} fusion(f32[512]{0:T(512)} %param.11, f32[32,8]{1,0:T(8,128)S(1)} %add_rsqrt_fusion, bf16[1,32,8,512]{3,2,1,0:T(8,128)(2,1)} %param.10), kind=kLoop, calls=%fused_computation.31 | loop fusion | flops 524288 | bytes 527360 | tf_op jit(solution)/shard_map/convert_element_type | solution.py:28
  2.3 4.1 %collective-permute-start = (bf16[1,2,8,512]{3,2,1,0:T(8,128)(2,1)S(1)}, bf16[1,2,8,512]{3,2,1,0:T(8,128)(2,1)S(1)}, u32[]{:S(2)}, u32[]{:S(2)}) collective-permute-start(bf16[1,2,8,512]{3,2,1,0:T(8,128)(2,1)S(1)} %maximum_bitcast_fusion.3), channel_id=1, source_target_pairs={{0,8},{1,9},{2,10},{3,11},{4,12},{5,13},{6,14},{7,15},{8,0},{9,1},... | collective-permute-start | bytes 49160 | tf_op jit(solution)/shard_map/ppermute | solution.py:164
  6.4 1.1 %multiply_convert_fusion = bf16[1,32,8,512]{3,2,1,0:T(8,128)(2,1)S(1)} fusion(bf16[1,32,8,512]{3,2,1,0:T(8,128)(2,1)} %param.10, f32[512]{0:T(512)} %param.11, f32[32,8]{1,0:T(8,128)S(1)} %add_rsqrt_fusion), kind=kLoop, calls=%fused_computation.39 | loop fusion | flops 524288 | bytes 527360 | tf_op jit(solution)/shard_map/convert_element_type | solution.py:28
  7.5 0.1 fusion.43
  7.6 4.4 %collective-permute-start.5 = (bf16[1,32,1,512]{3,2,1,0:T(2,128)(2,1)S(1)}, bf16[1,32,1,512]{3,2,1,0:T(2,128)(2,1)S(1)}, u32[]{:S(2)}, u32[]{:S(2)}) collective-permute-start(bf16[1,32,1,512]{3,2,1,0:T(2,128)(2,1)S(1)} %get-tuple-element.25), channel_id=1, source_target_pairs={{1,0},{2,1},{3,2},{4,3},{5,4},{6,5},{7,6},{8,7},{9,8},{10,9},{11,1... | collective-permute-start | bytes 98312 | tf_op jit(solution)/shard_map/ppermute | solution.py:20
  12.1 0.2 slice_reduce_fusion.2
  12.5 3.8 %collective-permute-done.1 = bf16[2,2,8,512]{3,2,1,0:T(8,128)(2,1)S(1)} collective-permute-done((bf16[2,2,8,512]{3,2,1,0:T(8,128)(2,1)S(1)}, bf16[2,2,8,512]{3,2,1,0:T(8,128)(2,1)S(1)}, u32[]{:S(2)}, u32[]{:S(2)}) %collective-permute-start.1) | collective-permute-done | bytes 32800 | tf_op jit(solution)/shard_map/ppermute | solution.py:164
  16.4 0.2 compare_reduce_fusion
  16.6 4.1 %collective-permute-done.2 = bf16[4,2,8,512]{3,2,1,0:T(8,128)(2,1)S(1)} collective-permute-done((bf16[4,2,8,512]{3,2,1,0:T(8,128)(2,1)S(1)}, bf16[4,2,8,512]{3,2,1,0:T(8,128)(2,1)S(1)}, u32[]{:S(2)}, u32[]{:S(2)}) %collective-permute-start.2) | collective-permute-done | bytes 65568 | tf_op jit(solution)/shard_map/ppermute | solution.py:164
  20.8 0.1 copy.24
  20.9 0.1 copy.27
  21.0 0.1 copy.28
  21.0 0.1 copy.29
  21.5 0.3 maximum_bitcast_fusion
  21.8 0.3 collective-permute-done.3
  22.1 0.6 gather_fusion
  22.8 0.3 fusion.18
  23.1 0.4 fusion.12
  23.5 0.1 broadcast_select_fusion.2
  23.6 1.1 %add_convert_fusion = bf16[32,8,512]{2,1,0:T(8,128)(2,1)S(1)} fusion(bf16[32,10,512]{2,1,0:T(8,128)(2,1)S(1)} %maximum_bitcast_fusion, bf16[1,10,512]{2,1,0:T(8,128)(2,1)S(1)} %copy.33, bf16[1,10,512]{2,1,0:T(8,128)(2,1)S(1)} %copy.26, f32[32,8]{1,0:T(8,128)S(1)} %copy.35, f32[32,8]{1,0:T(8,128)S(1)} %copy.34, f32[32,8]{1,0:T(8,128)S(1)} %copy.32, ...), kind=kLoop, calls=%fused_computation.38 | loop fusion | flops 5898240 | bytes 1753088 | tf_op jit(solution)/shard_map/convert_element_type | solution.py:69
  24.8 5.6 %collective-permute-done.6 = bf16[1,6,8,512]{3,2,1,0:T(8,128)(2,1)S(1)} collective-permute-done((bf16[1,6,8,512]{3,2,1,0:T(8,128)(2,1)S(1)}, bf16[1,6,8,512]{3,2,1,0:T(8,128)(2,1)S(1)}, u32[]{:S(2)}, u32[]{:S(2)}) %collective-permute-start.6) | collective-permute-done | bytes 49184 | tf_op jit(solution)/shard_map/ppermute | solution.py:164
  30.5 4.6 %collective-permute-done.7 = bf16[2,6,8,512]{3,2,1,0:T(8,128)(2,1)S(1)} collective-permute-done((bf16[2,6,8,512]{3,2,1,0:T(8,128)(2,1)S(1)}, bf16[2,6,8,512]{3,2,1,0:T(8,128)(2,1)S(1)}, u32[]{:S(2)}, u32[]{:S(2)}) %collective-permute-start.7) | collective-permute-done | bytes 98336 | tf_op jit(solution)/shard_map/ppermute | solution.py:164
  35.1 0.1 collective-permute-start.8
  35.2 1.0 %fusion.49 = bf16[1,32,8,512]{3,2,1,0:T(8,128)(2,1)S(1)} fusion(bf16[1,10,512]{2,1,0:T(8,128)(2,1)S(1)} %copy.33, bf16[32,10,512]{2,1,0:T(8,128)(2,1)S(1)} %maximum_bitcast_fusion, f32[32,8]{1,0:T(8,128)S(1)} %copy.35, f32[32,8]{1,0:T(8,128)S(1)} %copy.34, f32[32,8]{1,0:T(8,128)S(1)} %copy.32, f32[32,8]{1,0:T(8,128)S(1)} %copy.31, f32[32,8]{1,0:T(8,128)S(1)} %copy.30, ...), kind=kLoop, calls=%fused_computation.113 | loop fusion | flops 5898240 | bytes 1753088 | tf_op jit(solution)/shard_map/broadcast_in_dim | solution.py:186
  36.3 4.6 %collective-permute-done.8 = bf16[4,6,8,512]{3,2,1,0:T(8,128)(2,1)S(1)} collective-permute-done((bf16[4,6,8,512]{3,2,1,0:T(8,128)(2,1)S(1)}, bf16[4,6,8,512]{3,2,1,0:T(8,128)(2,1)S(1)}, u32[]{:S(2)}, u32[]{:S(2)}) %collective-permute-start.8) | collective-permute-done | bytes 196640 | tf_op jit(solution)/shard_map/ppermute | solution.py:164
  41.0 0.1 fusion.38
  41.1 0.5 collective-permute-start.10
  41.6 4.0 %collective-permute-start.11 = (bf16[1,32,3,512]{3,2,1,0:T(4,128)(2,1)S(1)}, bf16[1,32,3,512]{3,2,1,0:T(4,128)(2,1)S(1)}, u32[]{:S(2)}, u32[]{:S(2)}) collective-permute-start(bf16[1,32,3,512]{3,2,1,0:T(4,128)(2,1)S(1)} %get-tuple-element.15), channel_id=1, source_target_pairs={{1,0},{2,1},{3,2},{4,3},{5,4},{6,5},{7,6},{8,7},{9,8},{10,9},{11,1... | collective-permute-start | bytes 294920 | tf_op jit(solution)/shard_map/ppermute | solution.py:20
  45.6 1.0 %convolution_convert_fusion.2.q_ref = bf16[256,512]{1,0:T(8,128)(2,1)} fusion(bf16[512,512]{1,0:T(8,128)(2,1)S(1)} %copy-done.1, bf16[32,8,512]{2,1,0:T(8,128)(2,1)S(1)} %add_convert_fusion), kind=kOutput, calls=%fused_computation.12 | convolution fusion | flops 134348800 | bytes 1048576 | tf_op jit(solution)/shard_map/dot_general | solution.py:76
  46.6 1.6 %collective-permute-done.10 = bf16[1,32,3,512]{3,2,1,0:T(4,128)(2,1)S(1)} collective-permute-done((bf16[1,32,3,512]{3,2,1,0:T(4,128)(2,1)S(1)}, bf16[1,32,3,512]{3,2,1,0:T(4,128)(2,1)S(1)}, u32[]{:S(2)}, u32[]{:S(2)}) %collective-permute-start.10) | collective-permute-done | bytes 98336 | tf_op jit(solution)/shard_map/ppermute | solution.py:19
  48.2 0.3 maximum_bitcast_fusion.1
  48.5 0.1 maximum_select_fusion
  48.6 0.6 gather_fusion.1
  49.2 0.4 copy.36
  49.7 0.4 fusion.37
  50.1 0.2 fusion.36
  50.3 0.3 fusion
  50.6 0.1 slice_bitcast_fusion.1
  50.7 0.4 fusion.9
  51.2 0.2 broadcast_select_fusion
  51.3 0.1 broadcast_select_fusion.1
  51.5 0.1 fusion.44
  51.6 0.1 pad_maximum_fusion.2
  51.8 0.2 reshape.108
  51.9 1.4 %convolution_convert_fusion.v_ref = bf16[640,512]{1,0:T(8,128)(2,1)} fusion(bf16[512,512]{1,0:T(8,128)(2,1)S(1)} %copy-done, bf16[532,512]{1,0:T(8,128)(2,1)S(1)} %reshape.108), kind=kOutput, calls=%fused_computation.10 | convolution fusion | flops 335872000 | bytes 1724416 | tf_op jit(solution)/shard_map/dot_general | solution.py:76
  53.3 1.3 %convolution_convert_fusion.1.k_ref = bf16[640,512]{1,0:T(8,128)(2,1)} fusion(bf16[512,512]{1,0:T(8,128)(2,1)S(1)} %copy-done.5, bf16[532,512]{1,0:T(8,128)(2,1)S(1)} %reshape.108), kind=kOutput, calls=%fused_computation.11 | convolution fusion | flops 335872000 | bytes 1724416 | tf_op jit(solution)/shard_map/dot_general | solution.py:76
  54.6 7.0 %shard_map.100 = bf16[256,512]{1,0:T(8,128)(2,1)} custom-call(bf16[256,512]{1,0:T(8,128)(2,1)} %convolution_convert_fusion.2.q_ref, bf16[640,512]{1,0:T(8,128)(2,1)} %convolution_convert_fusion.1.k_ref, bf16[640,512]{1,0:T(8,128)(2,1)} %convolution_convert_fusion.v_ref, bf16[32,8,512]{2,1,0:T(8,128)(2,1)} %bitcast.67, bf16[512,512]{1,0:T(8,128)(2,1)} %wo_ref.1), custom_call_target="tpu_custom_call" | custom-call | tf_op jit(solution)/shard_map/pallas_call | solution.py:130
  (52 shorter events, 1.3 us)
Async XLA Ops:
  0.0 51.9 %copy-start = (bf16[512,512]{1,0:T(8,128)(2,1)S(1)}, bf16[512,512]{1,0:T(8,128)(2,1)}, u32[]{:S(2)}) copy-start(bf16[512,512]{1,0:T(8,128)(2,1)} %param.15) | copy-start | bytes 1572868
  0.0 20.8 %copy-start.4 = (s32[16]{0:T(128)S(1)}, s32[16]{0:T(128)}, u32[]{:S(2)}) copy-start(s32[16]{0:T(128)} %constant.96) | copy-start | bytes 196
  0.0 12.1 %copy-start.3 = (s32[1,2,3]{2,1,0:T(2,128)S(1)}, s32[1,2,3]{2,1,0:T(2,128)}, u32[]{:S(2)}) copy-start(s32[1,2,3]{2,1,0:T(2,128)} %param.17) | copy-start | bytes 76
  0.0 12.3 %copy-start.2 = (f32[1,9,32,8]{2,3,1,0:T(8,128)S(1)}, f32[1,9,32,8]{2,3,1,0:T(8,128)}, u32[]{:S(2)}) copy-start(f32[1,9,32,8]{2,3,1,0:T(8,128)} %param.12) | copy-start | bytes 27652
  2.3 10.0 %collective-permute-start = (bf16[1,2,8,512]{3,2,1,0:T(8,128)(2,1)S(1)}, bf16[1,2,8,512]{3,2,1,0:T(8,128)(2,1)S(1)}, u32[]{:S(2)}, u32[]{:S(2)}) collective-permute-start(bf16[1,2,8,512]{3,2,1,0:T(8,128)(2,1)S(1)} %maximum_bitcast_fusion.3), channel_id=1, source_target_pairs={{0,8},{1,9},{2,10},{3,11},{4,12},{5,13},{6,14},{7,15},{8,0},{9,1},... | collective-permute-start | bytes 49160 | tf_op jit(solution)/shard_map/ppermute | solution.py:164
  7.6 13.9 %collective-permute-start.4 = (bf16[1,32,1,512]{3,2,1,0:T(2,128)(2,1)S(1)}, bf16[1,32,1,512]{3,2,1,0:T(2,128)(2,1)S(1)}, u32[]{:S(2)}, u32[]{:S(2)}) collective-permute-start(bf16[1,32,1,512]{3,2,1,0:T(2,128)(2,1)S(1)} %get-tuple-element.24), channel_id=1, source_target_pairs={{0,1},{1,2},{2,3},{3,4},{4,5},{5,6},{6,7},{7,8},{8,9},{9,10},{10,1... | collective-permute-start | bytes 98312 | tf_op jit(solution)/shard_map/ppermute | solution.py:19
  7.6 13.9 %collective-permute-start.5 = (bf16[1,32,1,512]{3,2,1,0:T(2,128)(2,1)S(1)}, bf16[1,32,1,512]{3,2,1,0:T(2,128)(2,1)S(1)}, u32[]{:S(2)}, u32[]{:S(2)}) collective-permute-start(bf16[1,32,1,512]{3,2,1,0:T(2,128)(2,1)S(1)} %get-tuple-element.25), channel_id=1, source_target_pairs={{1,0},{2,1},{3,2},{4,3},{5,4},{6,5},{7,6},{8,7},{9,8},{10,9},{11,1... | collective-permute-start | bytes 98312 | tf_op jit(solution)/shard_map/ppermute | solution.py:20
  12.4 4.0 %collective-permute-start.1 = (bf16[2,2,8,512]{3,2,1,0:T(8,128)(2,1)S(1)}, bf16[2,2,8,512]{3,2,1,0:T(8,128)(2,1)S(1)}, u32[]{:S(2)}, u32[]{:S(2)}) collective-permute-start(bf16[2,2,8,512]{3,2,1,0:T(8,128)(2,1)S(1)} %maximum_select_fusion.7), channel_id=1, source_target_pairs={{0,4},{1,5},{2,6},{3,7},{4,0},{5,1},{6,2},{7,3},{8,12},{9,13},{10,... | collective-permute-start | bytes 98312 | tf_op jit(solution)/shard_map/ppermute | solution.py:164
  16.4 4.3 %collective-permute-start.2 = (bf16[4,2,8,512]{3,2,1,0:T(8,128)(2,1)S(1)}, bf16[4,2,8,512]{3,2,1,0:T(8,128)(2,1)S(1)}, u32[]{:S(2)}, u32[]{:S(2)}) collective-permute-start(bf16[4,2,8,512]{3,2,1,0:T(8,128)(2,1)S(1)} %maximum_select_fusion.6), channel_id=1, source_target_pairs={{0,2},{1,3},{2,0},{3,1},{4,6},{5,7},{6,4},{7,5},{8,10},{9,11},{10,... | collective-permute-start | bytes 196616 | tf_op jit(solution)/shard_map/ppermute | solution.py:164
  20.7 1.4 %collective-permute-start.3 = (bf16[8,2,8,512]{3,2,1,0:T(8,128)(2,1)S(1)}, bf16[8,2,8,512]{3,2,1,0:T(8,128)(2,1)S(1)}, u32[]{:S(2)}, u32[]{:S(2)}) collective-permute-start(bf16[8,2,8,512]{3,2,1,0:T(8,128)(2,1)S(1)} %maximum_select_fusion.4), channel_id=1, source_target_pairs={{0,1},{1,0},{2,3},{3,2},{4,5},{5,4},{6,7},{7,6},{8,9},{9,8},{10,11... | collective-permute-start | bytes 393224 | tf_op jit(solution)/shard_map/ppermute | solution.py:164
  24.7 5.6 %collective-permute-start.6 = (bf16[1,6,8,512]{3,2,1,0:T(8,128)(2,1)S(1)}, bf16[1,6,8,512]{3,2,1,0:T(8,128)(2,1)S(1)}, u32[]{:S(2)}, u32[]{:S(2)}) collective-permute-start(bf16[1,6,8,512]{3,2,1,0:T(8,128)(2,1)S(1)} %maximum_bitcast_fusion.2), channel_id=1, source_target_pairs={{0,8},{1,9},{2,10},{3,11},{4,12},{5,13},{6,14},{7,15},{8,0},{9,1},... | collective-permute-start | bytes 147464 | tf_op jit(solution)/shard_map/ppermute | solution.py:164
  30.4 4.7 %collective-permute-start.7 = (bf16[2,6,8,512]{3,2,1,0:T(8,128)(2,1)S(1)}, bf16[2,6,8,512]{3,2,1,0:T(8,128)(2,1)S(1)}, u32[]{:S(2)}, u32[]{:S(2)}) collective-permute-start(bf16[2,6,8,512]{3,2,1,0:T(8,128)(2,1)S(1)} %maximum_select_fusion.5), channel_id=1, source_target_pairs={{0,4},{1,5},{2,6},{3,7},{4,0},{5,1},{6,2},{7,3},{8,12},{9,13},{10,... | collective-permute-start | bytes 294920 | tf_op jit(solution)/shard_map/ppermute | solution.py:164
  35.1 10.5 %copy-start.1 = (bf16[512,512]{1,0:T(8,128)(2,1)S(1)}, bf16[512,512]{1,0:T(8,128)(2,1)}, u32[]{:S(2)}) copy-start(bf16[512,512]{1,0:T(8,128)(2,1)} %param.13) | copy-start | bytes 1572868
  35.1 5.7 %collective-permute-start.8 = (bf16[4,6,8,512]{3,2,1,0:T(8,128)(2,1)S(1)}, bf16[4,6,8,512]{3,2,1,0:T(8,128)(2,1)S(1)}, u32[]{:S(2)}, u32[]{:S(2)}) collective-permute-start(bf16[4,6,8,512]{3,2,1,0:T(8,128)(2,1)S(1)} %maximum_select_fusion.3), channel_id=1, source_target_pairs={{0,2},{1,3},{2,0},{3,1},{4,6},{5,7},{6,4},{7,5},{8,10},{9,11},{10,... | collective-permute-start | bytes 589832 | tf_op jit(solution)/shard_map/ppermute | solution.py:164
  40.9 7.6 %collective-permute-start.9 = (bf16[8,6,8,512]{3,2,1,0:T(8,128)(2,1)S(1)}, bf16[8,6,8,512]{3,2,1,0:T(8,128)(2,1)S(1)}, u32[]{:S(2)}, u32[]{:S(2)}) collective-permute-start(bf16[8,6,8,512]{3,2,1,0:T(8,128)(2,1)S(1)} %maximum_select_fusion.1), channel_id=1, source_target_pairs={{0,1},{1,0},{2,3},{3,2},{4,5},{5,4},{6,7},{7,6},{8,9},{9,8},{10,11... | collective-permute-start | bytes 1179656 | tf_op jit(solution)/shard_map/ppermute | solution.py:164
  41.1 7.1 %collective-permute-start.10 = (bf16[1,32,3,512]{3,2,1,0:T(4,128)(2,1)S(1)}, bf16[1,32,3,512]{3,2,1,0:T(4,128)(2,1)S(1)}, u32[]{:S(2)}, u32[]{:S(2)}) collective-permute-start(bf16[1,32,3,512]{3,2,1,0:T(4,128)(2,1)S(1)} %get-tuple-element.14), channel_id=1, source_target_pairs={{0,1},{1,2},{2,3},{3,4},{4,5},{5,6},{6,7},{7,8},{8,9},{9,10},{10,1... | collective-permute-start | bytes 294920 | tf_op jit(solution)/shard_map/ppermute | solution.py:19
  41.6 6.6 %collective-permute-start.11 = (bf16[1,32,3,512]{3,2,1,0:T(4,128)(2,1)S(1)}, bf16[1,32,3,512]{3,2,1,0:T(4,128)(2,1)S(1)}, u32[]{:S(2)}, u32[]{:S(2)}) collective-permute-start(bf16[1,32,3,512]{3,2,1,0:T(4,128)(2,1)S(1)} %get-tuple-element.15), channel_id=1, source_target_pairs={{1,0},{2,1},{3,2},{4,3},{5,4},{6,5},{7,6},{8,7},{9,8},{10,9},{11,1... | collective-permute-start | bytes 294920 | tf_op jit(solution)/shard_map/ppermute | solution.py:20
  51.8 1.5 %copy-start.5 = (bf16[512,512]{1,0:T(8,128)(2,1)S(1)}, bf16[512,512]{1,0:T(8,128)(2,1)}, u32[]{:S(2)}) copy-start(bf16[512,512]{1,0:T(8,128)(2,1)} %param.14) | copy-start | bytes 1572868

commit v12 on v9

--- a/solution.py
+++ b/solution.py
@@ -152,24 +152,27 @@
     return got.astype(edges.dtype)
 
 
-def radix_gather(block, axis, radix=16):
+def doubling_gather(block, axis, radix=4):
     count = lax.axis_size(axis)
     if count & (count - 1):
         return lax.all_gather(block, axis, axis=0, tiled=True)
     me = lax.axis_index(axis)
-    held = block
+    levels = []
     stride = 1
     while stride < count:
         r = min(radix, count // stride)
+        levels.append((stride, r))
+        stride *= r
+    held = block
+    for stride, r in reversed(levels):
         got = [held]
         for d in range(1, r):
             got.append(lax.ppermute(held, axis, [(i, i ^ (d * stride)) for i in range(count)]))
         digit = (me // stride) % r
-        order = digit ^ jnp.arange(r, dtype=jnp.int32)
-        held = jnp.take(jnp.stack(got), order, axis=0)
-        held = held.reshape((r * held.shape[1],) + held.shape[2:])
-        stride *= r
-    return held
+        held = jnp.take(jnp.stack(got), digit ^ jnp.arange(r, dtype=jnp.int32), axis=0)
+    depth = len(levels)
+    held = jnp.transpose(held, tuple(reversed(range(depth))) + tuple(range(depth, held.ndim)))
+    return held.reshape((count * block.shape[0],) + block.shape[1:])
 
 
 def local(latents, norm_gain, metric, w_query, w_key, w_value, w_output, seam_table):
@@ -180,14 +183,14 @@
     seam_rows = seam_table[0]
     widened = padded_2(normed[None], (("blk", 2),), margin)
     rows1 = jnp.stack([normed[0], normed[-1]])
-    got1 = widen_tiles(radix_gather(rows1[None], "blk"), 1)
+    got1 = widen_tiles(doubling_gather(rows1[None], "blk"), 1)
     received = pick_all(seam_rows, got1[:, :, None])
     padded = place_rims(widened[0], received, seam_rows)
     smoothed = smooth(padded, metric[0])
     query = project(smoothed, w_query)
     field_wide = padded_2(smoothed[None], (("blk", 2),), RADIUS)
     rows3 = jnp.concatenate([smoothed[:RADIUS], smoothed[-RADIUS:]], axis=0)
-    got3 = widen_tiles(radix_gather(rows3[None], "blk"), RADIUS)
+    got3 = widen_tiles(doubling_gather(rows3[None], "blk"), RADIUS)
     edges3 = jnp.stack([got3[:, :RADIUS], got3[:, RADIUS:]], axis=1)
     field_got = pick_all(seam_rows, edges3)
     field_pad = place_rims(field_wide[0], field_got, seam_rows)

time: 80.9 us -> 60.6 us (0.75)
  starting transfers between devices: 52.6 us -> 22.9 us
  waiting for transfers between devices: 2.4 us -> 12.1 us
  other arithmetic: 9.3 us -> 7.88 us
  local copies, waits for them, and re-layouts: 4.21 us -> 5.5 us
    ppermute x30 -> x12, starting transfers between devices: 43.4 us -> 13.9 us  [doubling_gather(): lax.ppermute(held, axis, [(i, i ^ d * stride) for i in range(count)])]
    ppermute x30 -> x12, waiting for transfers between devices: 2.39 us -> 12.1 us  [doubling_gather(): lax.ppermute(held, axis, [(i, i ^ d * stride) for i in range(count)])]
    ppermute x2, starting transfers between devices: 1.59 us -> 0.12 us  [padded_2(): before = lax.ppermute(last, axis, up)]
    ppermute x2, starting transfers between devices: 7.58 us -> 8.86 us  [padded_2(): after = lax.ppermute(first, axis, down)]
    gather x2 -> x4, local copies, waits for them, and re-layouts: 1.16 us -> 2.27 us  [doubling_gather(): jnp.take(jnp.stack(got), digit ^ jnp.arange(r, dtype=jnp.int32), axis=0)]
    select_n x5 -> x6, other arithmetic: 1.16 us -> 0.34 us  [doubling_gather(): jnp.take(jnp.stack(got), digit ^ jnp.arange(r, dtype=jnp.int32), axis=0)]
  transfers between devices with their start and end apart: 34 -> 16, of which waited for: 2 -> 4; matrix products, arithmetic and copies ran while one was open for 13% -> 9% of each run, Pallas kernels for 0% -> 0%
where the time goes in v12:
time: 60.6 us; the launch traced here: 60.4 us
  starting transfers between devices  22.9 us (38%)
  waiting for transfers between devices  12.1 us (20%)
  other arithmetic  7.88 us (13%)
  Pallas kernels  7 us (12%)
  local copies, waits for them, and re-layouts  5.5 us (9%)
  matrix products  4.46 us (7%)
    ppermute x12, starting transfers between devices, doubling_gather(): lax.ppermute(held, axis, [(i, i ^ d * stride) for i in range(count)])  13.9 us
    ppermute x12, waiting for transfers between devices, doubling_gather(): lax.ppermute(held, axis, [(i, i ^ d * stride) for i in range(count)])  12.1 us
    ppermute x2, starting transfers between devices, padded_2(): after = lax.ppermute(first, axis, down)  8.86 us
    pallas_call x1, Pallas kernels, attend_and_mix(): pl.pallas_call(attention_kernel, out_shape=jax.ShapeDtypeStruct((cells, c...  7 us
    dot_general x3, matrix products, project(): jnp.dot(flat, weight, preferred_element_type=jnp.float32)  3.72 us
    gather x4, local copies, waits for them, and re-layouts, doubling_gather(): jnp.take(jnp.stack(got), digit ^ jnp.arange(r, dtype=jnp.int32), axis=0)  2.27 us
    convert_element_type x2, other arithmetic, normalize(): return (values * factor * norm_gain).astype(jnp.bfloat16)  2.17 us
  transfers between devices with their start and end apart: 16, of which 4 were waited for; matrix products, arithmetic and copies ran while one was open for 9% of the time, Pallas kernels for 0%

profile of v12, /device:TPU:0, one launch (start us, length us, event | category | flops | bytes accessed | tf_op | source)
XLA Modules:
  0.0 60.4 jit_solution(5373621634361378591)
XLA Ops:
  0.0 1.1 %fusion.16 = f32[32,8]{1,0:T(8,128)S(1)} fusion(bf16[1,32,8,512]{3,2,1,0:T(8,128)(2,1)} %param.8), kind=kLoop, calls=%fused_computation.33 | loop fusion | flops 392960 | bytes 263168 | tf_op jit(solution)/shard_map/reduce_sum | solution.py:27
  1.2 1.1 %fusion.18 = bf16[32,8,512]{2,1,0:T(8,128)(2,1)S(1)} fusion(f32[512]{0:T(512)} %param.9, f32[32,8]{1,0:T(8,128)S(1)} %add_rsqrt_fusion, bf16[1,32,8,512]{3,2,1,0:T(8,128)(2,1)} %param.8), kind=kLoop, calls=%fused_computation.35 | loop fusion | flops 524288 | bytes 527360 | tf_op jit(solution)/shard_map/convert_element_type | solution.py:28
  2.3 3.1 %collective-permute-start = (bf16[1,2,8,512]{3,2,1,0:T(8,128)(2,1)S(1)}, bf16[1,2,8,512]{3,2,1,0:T(8,128)(2,1)S(1)}, u32[]{:S(2)}, u32[]{:S(2)}) collective-permute-start(bf16[1,2,8,512]{3,2,1,0:T(8,128)(2,1)S(1)} %get-tuple-element.42), channel_id=1, source_target_pairs={{0,4},{1,5},{2,6},{3,7},{4,0},{5,1},{6,2},{7,3},{8,12},{9,13},{10,... | collective-permute-start | bytes 49160 | tf_op jit(solution)/shard_map/ppermute | solution.py:170
  5.4 2.6 %collective-permute-start.1 = (bf16[1,2,8,512]{3,2,1,0:T(8,128)(2,1)S(1)}, bf16[1,2,8,512]{3,2,1,0:T(8,128)(2,1)S(1)}, u32[]{:S(2)}, u32[]{:S(2)}) collective-permute-start(bf16[1,2,8,512]{3,2,1,0:T(8,128)(2,1)S(1)} %get-tuple-element.42), channel_id=1, source_target_pairs={{0,8},{1,9},{2,10},{3,11},{4,12},{5,13},{6,14},{7,15},{8,0},{9,1},... | collective-permute-start | bytes 49160 | tf_op jit(solution)/shard_map/ppermute | solution.py:170
  8.0 1.1 %multiply_convert_fusion = bf16[1,32,8,512]{3,2,1,0:T(8,128)(2,1)S(1)} fusion(bf16[1,32,8,512]{3,2,1,0:T(8,128)(2,1)} %param.8, f32[512]{0:T(512)} %param.9, f32[32,8]{1,0:T(8,128)S(1)} %add_rsqrt_fusion), kind=kLoop, calls=%fused_computation.39 | loop fusion | flops 524288 | bytes 527360 | tf_op jit(solution)/shard_map/convert_element_type | solution.py:28
  9.1 0.1 fusion.56
  9.2 4.4 %collective-permute-start.7 = (bf16[1,32,1,512]{3,2,1,0:T(2,128)(2,1)S(1)}, bf16[1,32,1,512]{3,2,1,0:T(2,128)(2,1)S(1)}, u32[]{:S(2)}, u32[]{:S(2)}) collective-permute-start(bf16[1,32,1,512]{3,2,1,0:T(2,128)(2,1)S(1)} %get-tuple-element.25), channel_id=1, source_target_pairs={{1,0},{2,1},{3,2},{4,3},{5,4},{6,5},{7,6},{8,7},{9,8},{10,9},{11,1... | collective-permute-start | bytes 98312 | tf_op jit(solution)/shard_map/ppermute | solution.py:20
  13.7 0.2 slice_reduce_fusion.2
  13.9 0.2 compare_reduce_fusion
  15.0 0.6 gather_fusion
  15.7 0.1 collective-permute-start.4
  15.8 1.7 %collective-permute-start.5 = (bf16[4,1,2,8,512]{4,3,2,0,1:T(8,128)(2,1)S(1)}, bf16[4,1,2,8,512]{4,3,2,0,1:T(8,128)(2,1)S(1)}, u32[]{:S(2)}, u32[]{:S(2)}) collective-permute-start(bf16[4,1,2,8,512]{4,3,2,0,1:T(8,128)(2,1)S(1)} %bitcast_select_fusion.4), channel_id=1, source_target_pairs={{0,3},{1,2},{2,1},{3,0},{4,7},{5,6},{6,5},{7,4},{8,11},{9,10},{10,... | collective-permute-start | bytes 196616 | tf_op jit(solution)/shard_map/ppermute | solution.py:170
  17.6 0.3 maximum_bitcast_fusion.1
  17.9 2.8 %collective-permute-done.4 = bf16[4,1,2,8,512]{4,3,2,0,1:T(8,128)(2,1)S(1)} collective-permute-done((bf16[4,1,2,8,512]{4,3,2,0,1:T(8,128)(2,1)S(1)}, bf16[4,1,2,8,512]{4,3,2,0,1:T(8,128)(2,1)S(1)}, u32[]{:S(2)}, u32[]{:S(2)}) %collective-permute-start.4) | collective-permute-done | bytes 65568 | tf_op jit(solution)/shard_map/ppermute | solution.py:170
  20.7 0.5 collective-permute-done.5
  21.2 0.6 gather_fusion.1
  21.8 0.1 fusion.31
  21.9 0.2 copy.24
  22.2 0.3 fusion.12
  22.7 1.1 %fusion.62 = bf16[1,32,8,512]{3,2,1,0:T(8,128)(2,1)S(1)} fusion(bf16[1,10,512]{2,1,0:T(8,128)(2,1)S(1)} %copy.36, bf16[32,10,512]{2,1,0:T(8,128)(2,1)S(1)} %maximum_bitcast_fusion.1, f32[32,8]{1,0:T(8,128)S(1)} %copy.38, f32[32,8]{1,0:T(8,128)S(1)} %copy.37, f32[32,8]{1,0:T(8,128)S(1)} %copy.35, f32[32,8]{1,0:T(8,128)S(1)} %copy.34, f32[32,8]{1,0:T(8,128)S(1)} %copy.33, ...), kind=kLoop, calls=%fused_computation.135 | loop fusion | flops 5898240 | bytes 1753088 | tf_op jit(solution)/shard_map/broadcast_in_dim | solution.py:191
  23.8 1.1 %add_convert_fusion = bf16[32,8,512]{2,1,0:T(8,128)(2,1)S(1)} fusion(bf16[32,10,512]{2,1,0:T(8,128)(2,1)S(1)} %maximum_bitcast_fusion.1, bf16[1,10,512]{2,1,0:T(8,128)(2,1)S(1)} %copy.36, bf16[1,10,512]{2,1,0:T(8,128)(2,1)S(1)} %copy.29, f32[32,8]{1,0:T(8,128)S(1)} %copy.38, f32[32,8]{1,0:T(8,128)S(1)} %copy.37, f32[32,8]{1,0:T(8,128)S(1)} %copy.35, ...), kind=kLoop, calls=%fused_computation.38 | loop fusion | flops 5898240 | bytes 1753088 | tf_op jit(solution)/shard_map/convert_element_type | solution.py:69
  24.9 2.6 %collective-permute-start.9 = (bf16[1,6,8,512]{3,2,1,0:T(8,128)(2,1)S(1)}, bf16[1,6,8,512]{3,2,1,0:T(8,128)(2,1)S(1)}, u32[]{:S(2)}, u32[]{:S(2)}) collective-permute-start(bf16[1,6,8,512]{3,2,1,0:T(8,128)(2,1)S(1)} %get-tuple-element.29), channel_id=1, source_target_pairs={{0,8},{1,9},{2,10},{3,11},{4,12},{5,13},{6,14},{7,15},{8,0},{9,1},... | collective-permute-start | bytes 147464 | tf_op jit(solution)/shard_map/ppermute | solution.py:170
  27.5 1.8 %collective-permute-start.10 = (bf16[1,6,8,512]{3,2,1,0:T(8,128)(2,1)S(1)}, bf16[1,6,8,512]{3,2,1,0:T(8,128)(2,1)S(1)}, u32[]{:S(2)}, u32[]{:S(2)}) collective-permute-start(bf16[1,6,8,512]{3,2,1,0:T(8,128)(2,1)S(1)} %get-tuple-element.29), channel_id=1, source_target_pairs={{0,12},{1,13},{2,14},{3,15},{4,8},{5,9},{6,10},{7,11},{8,4},{9,5},... | collective-permute-start | bytes 147464 | tf_op jit(solution)/shard_map/ppermute | solution.py:170
  29.5 4.4 %collective-permute-start.15 = (bf16[1,32,3,512]{3,2,1,0:T(4,128)(2,1)S(1)}, bf16[1,32,3,512]{3,2,1,0:T(4,128)(2,1)S(1)}, u32[]{:S(2)}, u32[]{:S(2)}) collective-permute-start(bf16[1,32,3,512]{3,2,1,0:T(4,128)(2,1)S(1)} %get-tuple-element.15), channel_id=1, source_target_pairs={{1,0},{2,1},{3,2},{4,3},{5,4},{6,5},{7,6},{8,7},{9,8},{10,9},{11,1... | collective-permute-start | bytes 294920 | tf_op jit(solution)/shard_map/ppermute | solution.py:20
  33.9 1.0 %convolution_convert_fusion.2.q_ref = bf16[256,512]{1,0:T(8,128)(2,1)} fusion(bf16[512,512]{1,0:T(8,128)(2,1)S(1)} %copy-done.1, bf16[32,8,512]{2,1,0:T(8,128)(2,1)S(1)} %add_convert_fusion), kind=kOutput, calls=%fused_computation.14 | convolution fusion | flops 134348800 | bytes 1048576 | tf_op jit(solution)/shard_map/dot_general | solution.py:76
  34.9 0.6 gather_fusion.2
  35.7 1.8 %collective-permute-start.13 = (bf16[4,1,6,8,512]{4,3,2,0,1:T(8,128)(2,1)S(1)}, bf16[4,1,6,8,512]{4,3,2,0,1:T(8,128)(2,1)S(1)}, u32[]{:S(2)}, u32[]{:S(2)}) collective-permute-start(bf16[4,1,6,8,512]{4,3,2,0,1:T(8,128)(2,1)S(1)} %bitcast_select_fusion.2), channel_id=1, source_target_pairs={{0,3},{1,2},{2,1},{3,0},{4,7},{5,6},{6,5},{7,4},{8,11},{9,10},{10,... | collective-permute-start | bytes 589832 | tf_op jit(solution)/shard_map/ppermute | solution.py:170
  37.6 0.3 maximum_bitcast_fusion.2
  38.0 5.5 %collective-permute-done.12 = bf16[4,1,6,8,512]{4,3,2,0,1:T(8,128)(2,1)S(1)} collective-permute-done((bf16[4,1,6,8,512]{4,3,2,0,1:T(8,128)(2,1)S(1)}, bf16[4,1,6,8,512]{4,3,2,0,1:T(8,128)(2,1)S(1)}, u32[]{:S(2)}, u32[]{:S(2)}) %collective-permute-start.12) | collective-permute-done | bytes 196640 | tf_op jit(solution)/shard_map/ppermute | solution.py:170
  43.4 3.3 %collective-permute-done.13 = bf16[4,1,6,8,512]{4,3,2,0,1:T(8,128)(2,1)S(1)} collective-permute-done((bf16[4,1,6,8,512]{4,3,2,0,1:T(8,128)(2,1)S(1)}, bf16[4,1,6,8,512]{4,3,2,0,1:T(8,128)(2,1)S(1)}, u32[]{:S(2)}, u32[]{:S(2)}) %collective-permute-start.13) | collective-permute-done | bytes 196640 | tf_op jit(solution)/shard_map/ppermute | solution.py:170
  46.7 0.1 maximum_bitcast_fusion
  46.8 0.6 gather_fusion.3
  47.5 0.1 fusion.13
  47.6 0.6 %copy.39 = bf16[4,4,1,6,8,512]{5,1,0,4,3,2:T(4,128)(2,1)S(1)} copy(bf16[4,4,1,6,8,512]{5,4,3,0,1,2:T(8,128)(2,1)S(1)} %fusion.13) | data formatting | bytes 1572864 | tf_op jit(solution)/shard_map/transpose | solution.py:174
  48.2 0.2 reshape.199
  48.4 0.4 fusion.50
  48.8 0.2 fusion.49
  49.0 0.3 fusion
  49.3 0.1 slice_bitcast_fusion.1
  49.4 0.4 fusion.9
  49.9 0.2 broadcast_select_fusion
  50.0 0.1 broadcast_select_fusion.1
  50.2 0.1 fusion.57
  50.3 0.1 pad_maximum_fusion.2
  50.4 0.2 reshape.200
  50.6 1.4 %convolution_convert_fusion.v_ref = bf16[640,512]{1,0:T(8,128)(2,1)} fusion(bf16[512,512]{1,0:T(8,128)(2,1)S(1)} %copy-done, bf16[532,512]{1,0:T(8,128)(2,1)S(1)} %reshape.200), kind=kOutput, calls=%fused_computation.12 | convolution fusion | flops 335872000 | bytes 1724416 | tf_op jit(solution)/shard_map/dot_general | solution.py:76
  52.0 1.4 %convolution_convert_fusion.1.k_ref = bf16[640,512]{1,0:T(8,128)(2,1)} fusion(bf16[512,512]{1,0:T(8,128)(2,1)S(1)} %copy-done.4, bf16[532,512]{1,0:T(8,128)(2,1)S(1)} %reshape.200), kind=kOutput, calls=%fused_computation.13 | convolution fusion | flops 335872000 | bytes 1724416 | tf_op jit(solution)/shard_map/dot_general | solution.py:76
  53.4 7.0 %shard_map.82 = bf16[256,512]{1,0:T(8,128)(2,1)} custom-call(bf16[256,512]{1,0:T(8,128)(2,1)} %convolution_convert_fusion.2.q_ref, bf16[640,512]{1,0:T(8,128)(2,1)} %convolution_convert_fusion.1.k_ref, bf16[640,512]{1,0:T(8,128)(2,1)} %convolution_convert_fusion.v_ref, bf16[32,8,512]{2,1,0:T(8,128)(2,1)} %bitcast.118, bf16[512,512]{1,0:T(8,128)(2,1)} %wo_ref.1), custom_call_target="tpu_custom_call" | custom-call | tf_op jit(solution)/shard_map/pallas_call | solution.py:130
  (69 shorter events, 2.0 us)
Async XLA Ops:
  0.0 50.6 %copy-start = (bf16[512,512]{1,0:T(8,128)(2,1)S(1)}, bf16[512,512]{1,0:T(8,128)(2,1)}, u32[]{:S(2)}) copy-start(bf16[512,512]{1,0:T(8,128)(2,1)} %param.13) | copy-start | bytes 1572868
  0.0 13.7 %copy-start.3 = (s32[1,2,3]{2,1,0:T(2,128)S(1)}, s32[1,2,3]{2,1,0:T(2,128)}, u32[]{:S(2)}) copy-start(s32[1,2,3]{2,1,0:T(2,128)} %param.15) | copy-start | bytes 76
  0.0 14.2 %copy-start.2 = (f32[1,9,32,8]{2,3,1,0:T(8,128)S(1)}, f32[1,9,32,8]{2,3,1,0:T(8,128)}, u32[]{:S(2)}) copy-start(f32[1,9,32,8]{2,3,1,0:T(8,128)} %param.10) | copy-start | bytes 27652
  2.3 12.7 %collective-permute-start = (bf16[1,2,8,512]{3,2,1,0:T(8,128)(2,1)S(1)}, bf16[1,2,8,512]{3,2,1,0:T(8,128)(2,1)S(1)}, u32[]{:S(2)}, u32[]{:S(2)}) collective-permute-start(bf16[1,2,8,512]{3,2,1,0:T(8,128)(2,1)S(1)} %get-tuple-element.42), channel_id=1, source_target_pairs={{0,4},{1,5},{2,6},{3,7},{4,0},{5,1},{6,2},{7,3},{8,12},{9,13},{10,... | collective-permute-start | bytes 49160 | tf_op jit(solution)/shard_map/ppermute | solution.py:170
  5.4 9.6 %collective-permute-start.1 = (bf16[1,2,8,512]{3,2,1,0:T(8,128)(2,1)S(1)}, bf16[1,2,8,512]{3,2,1,0:T(8,128)(2,1)S(1)}, u32[]{:S(2)}, u32[]{:S(2)}) collective-permute-start(bf16[1,2,8,512]{3,2,1,0:T(8,128)(2,1)S(1)} %get-tuple-element.42), channel_id=1, source_target_pairs={{0,8},{1,9},{2,10},{3,11},{4,12},{5,13},{6,14},{7,15},{8,0},{9,1},... | collective-permute-start | bytes 49160 | tf_op jit(solution)/shard_map/ppermute | solution.py:170
  8.0 7.0 %collective-permute-start.2 = (bf16[1,2,8,512]{3,2,1,0:T(8,128)(2,1)S(1)}, bf16[1,2,8,512]{3,2,1,0:T(8,128)(2,1)S(1)}, u32[]{:S(2)}, u32[]{:S(2)}) collective-permute-start(bf16[1,2,8,512]{3,2,1,0:T(8,128)(2,1)S(1)} %get-tuple-element.42), channel_id=1, source_target_pairs={{0,12},{1,13},{2,14},{3,15},{4,8},{5,9},{6,10},{7,11},{8,4},{9,5},... | collective-permute-start | bytes 49160 | tf_op jit(solution)/shard_map/ppermute | solution.py:170
  9.2 8.4 %collective-permute-start.6 = (bf16[1,32,1,512]{3,2,1,0:T(2,128)(2,1)S(1)}, bf16[1,32,1,512]{3,2,1,0:T(2,128)(2,1)S(1)}, u32[]{:S(2)}, u32[]{:S(2)}) collective-permute-start(bf16[1,32,1,512]{3,2,1,0:T(2,128)(2,1)S(1)} %get-tuple-element.24), channel_id=1, source_target_pairs={{0,1},{1,2},{2,3},{3,4},{4,5},{5,6},{6,7},{7,8},{8,9},{9,10},{10,1... | collective-permute-start | bytes 98312 | tf_op jit(solution)/shard_map/ppermute | solution.py:19
  9.2 8.4 %collective-permute-start.7 = (bf16[1,32,1,512]{3,2,1,0:T(2,128)(2,1)S(1)}, bf16[1,32,1,512]{3,2,1,0:T(2,128)(2,1)S(1)}, u32[]{:S(2)}, u32[]{:S(2)}) collective-permute-start(bf16[1,32,1,512]{3,2,1,0:T(2,128)(2,1)S(1)} %get-tuple-element.25), channel_id=1, source_target_pairs={{1,0},{2,1},{3,2},{4,3},{5,4},{6,5},{7,6},{8,7},{9,8},{10,9},{11,1... | collective-permute-start | bytes 98312 | tf_op jit(solution)/shard_map/ppermute | solution.py:20
  15.7 2.2 %collective-permute-start.3 = (bf16[4,1,2,8,512]{4,3,2,0,1:T(8,128)(2,1)S(1)}, bf16[4,1,2,8,512]{4,3,2,0,1:T(8,128)(2,1)S(1)}, u32[]{:S(2)}, u32[]{:S(2)}) collective-permute-start(bf16[4,1,2,8,512]{4,3,2,0,1:T(8,128)(2,1)S(1)} %bitcast_select_fusion.4), channel_id=1, source_target_pairs={{0,1},{1,0},{2,3},{3,2},{4,5},{5,4},{6,7},{7,6},{8,9},{9,8},{10,11... | collective-permute-start | bytes 196616 | tf_op jit(solution)/shard_map/ppermute | solution.py:170
  15.7 5.0 %collective-permute-start.4 = (bf16[4,1,2,8,512]{4,3,2,0,1:T(8,128)(2,1)S(1)}, bf16[4,1,2,8,512]{4,3,2,0,1:T(8,128)(2,1)S(1)}, u32[]{:S(2)}, u32[]{:S(2)}) collective-permute-start(bf16[4,1,2,8,512]{4,3,2,0,1:T(8,128)(2,1)S(1)} %bitcast_select_fusion.4), channel_id=1, source_target_pairs={{0,2},{1,3},{2,0},{3,1},{4,6},{5,7},{6,4},{7,5},{8,10},{9,11},{10,... | collective-permute-start | bytes 196616 | tf_op jit(solution)/shard_map/ppermute | solution.py:170
  15.8 5.3 %collective-permute-start.5 = (bf16[4,1,2,8,512]{4,3,2,0,1:T(8,128)(2,1)S(1)}, bf16[4,1,2,8,512]{4,3,2,0,1:T(8,128)(2,1)S(1)}, u32[]{:S(2)}, u32[]{:S(2)}) collective-permute-start(bf16[4,1,2,8,512]{4,3,2,0,1:T(8,128)(2,1)S(1)} %bitcast_select_fusion.4), channel_id=1, source_target_pairs={{0,3},{1,2},{2,1},{3,0},{4,7},{5,6},{6,5},{7,4},{8,11},{9,10},{10,... | collective-permute-start | bytes 196616 | tf_op jit(solution)/shard_map/ppermute | solution.py:170
  23.7 10.1 %copy-start.1 = (bf16[512,512]{1,0:T(8,128)(2,1)S(1)}, bf16[512,512]{1,0:T(8,128)(2,1)}, u32[]{:S(2)}) copy-start(bf16[512,512]{1,0:T(8,128)(2,1)} %param.11) | copy-start | bytes 1572868
  24.8 10.0 %collective-permute-start.8 = (bf16[1,6,8,512]{3,2,1,0:T(8,128)(2,1)S(1)}, bf16[1,6,8,512]{3,2,1,0:T(8,128)(2,1)S(1)}, u32[]{:S(2)}, u32[]{:S(2)}) collective-permute-start(bf16[1,6,8,512]{3,2,1,0:T(8,128)(2,1)S(1)} %get-tuple-element.29), channel_id=1, source_target_pairs={{0,4},{1,5},{2,6},{3,7},{4,0},{5,1},{6,2},{7,3},{8,12},{9,13},{10,... | collective-permute-start | bytes 147464 | tf_op jit(solution)/shard_map/ppermute | solution.py:170
  24.9 10.0 %collective-permute-start.9 = (bf16[1,6,8,512]{3,2,1,0:T(8,128)(2,1)S(1)}, bf16[1,6,8,512]{3,2,1,0:T(8,128)(2,1)S(1)}, u32[]{:S(2)}, u32[]{:S(2)}) collective-permute-start(bf16[1,6,8,512]{3,2,1,0:T(8,128)(2,1)S(1)} %get-tuple-element.29), channel_id=1, source_target_pairs={{0,8},{1,9},{2,10},{3,11},{4,12},{5,13},{6,14},{7,15},{8,0},{9,1},... | collective-permute-start | bytes 147464 | tf_op jit(solution)/shard_map/ppermute | solution.py:170
  27.5 7.4 %collective-permute-start.10 = (bf16[1,6,8,512]{3,2,1,0:T(8,128)(2,1)S(1)}, bf16[1,6,8,512]{3,2,1,0:T(8,128)(2,1)S(1)}, u32[]{:S(2)}, u32[]{:S(2)}) collective-permute-start(bf16[1,6,8,512]{3,2,1,0:T(8,128)(2,1)S(1)} %get-tuple-element.29), channel_id=1, source_target_pairs={{0,12},{1,13},{2,14},{3,15},{4,8},{5,9},{6,10},{7,11},{8,4},{9,5},... | collective-permute-start | bytes 147464 | tf_op jit(solution)/shard_map/ppermute | solution.py:170
  29.4 8.2 %collective-permute-start.14 = (bf16[1,32,3,512]{3,2,1,0:T(4,128)(2,1)S(1)}, bf16[1,32,3,512]{3,2,1,0:T(4,128)(2,1)S(1)}, u32[]{:S(2)}, u32[]{:S(2)}) collective-permute-start(bf16[1,32,3,512]{3,2,1,0:T(4,128)(2,1)S(1)} %get-tuple-element.14), channel_id=1, source_target_pairs={{0,1},{1,2},{2,3},{3,4},{4,5},{5,6},{6,7},{7,8},{8,9},{9,10},{10,1... | collective-permute-start | bytes 294920 | tf_op jit(solution)/shard_map/ppermute | solution.py:19
  29.5 8.2 %collective-permute-start.15 = (bf16[1,32,3,512]{3,2,1,0:T(4,128)(2,1)S(1)}, bf16[1,32,3,512]{3,2,1,0:T(4,128)(2,1)S(1)}, u32[]{:S(2)}, u32[]{:S(2)}) collective-permute-start(bf16[1,32,3,512]{3,2,1,0:T(4,128)(2,1)S(1)} %get-tuple-element.15), channel_id=1, source_target_pairs={{1,0},{2,1},{3,2},{4,3},{5,4},{6,5},{7,6},{8,7},{9,8},{10,9},{11,1... | collective-permute-start | bytes 294920 | tf_op jit(solution)/shard_map/ppermute | solution.py:20
  35.6 2.4 %collective-permute-start.11 = (bf16[4,1,6,8,512]{4,3,2,0,1:T(8,128)(2,1)S(1)}, bf16[4,1,6,8,512]{4,3,2,0,1:T(8,128)(2,1)S(1)}, u32[]{:S(2)}, u32[]{:S(2)}) collective-permute-start(bf16[4,1,6,8,512]{4,3,2,0,1:T(8,128)(2,1)S(1)} %bitcast_select_fusion.2), channel_id=1, source_target_pairs={{0,1},{1,0},{2,3},{3,2},{4,5},{5,4},{6,7},{7,6},{8,9},{9,8},{10,11... | collective-permute-start | bytes 589832 | tf_op jit(solution)/shard_map/ppermute | solution.py:170
  35.7 7.8 %collective-permute-start.12 = (bf16[4,1,6,8,512]{4,3,2,0,1:T(8,128)(2,1)S(1)}, bf16[4,1,6,8,512]{4,3,2,0,1:T(8,128)(2,1)S(1)}, u32[]{:S(2)}, u32[]{:S(2)}) collective-permute-start(bf16[4,1,6,8,512]{4,3,2,0,1:T(8,128)(2,1)S(1)} %bitcast_select_fusion.2), channel_id=1, source_target_pairs={{0,2},{1,3},{2,0},{3,1},{4,6},{5,7},{6,4},{7,5},{8,10},{9,11},{10,... | collective-permute-start | bytes 589832 | tf_op jit(solution)/shard_map/ppermute | solution.py:170
  35.7 11.0 %collective-permute-start.13 = (bf16[4,1,6,8,512]{4,3,2,0,1:T(8,128)(2,1)S(1)}, bf16[4,1,6,8,512]{4,3,2,0,1:T(8,128)(2,1)S(1)}, u32[]{:S(2)}, u32[]{:S(2)}) collective-permute-start(bf16[4,1,6,8,512]{4,3,2,0,1:T(8,128)(2,1)S(1)} %bitcast_select_fusion.2), channel_id=1, source_target_pairs={{0,3},{1,2},{2,1},{3,0},{4,7},{5,6},{6,5},{7,4},{8,11},{9,10},{10,... | collective-permute-start | bytes 589832 | tf_op jit(solution)/shard_map/ppermute | solution.py:170
  50.4 1.5 %copy-start.4 = (bf16[512,512]{1,0:T(8,128)(2,1)S(1)}, bf16[512,512]{1,0:T(8,128)(2,1)}, u32[]{:S(2)}) copy-start(bf16[512,512]{1,0:T(8,128)(2,1)} %param.12) | copy-start | bytes 1572868

commit v13 on v12

--- a/solution.py
+++ b/solution.py
@@ -81,38 +81,42 @@
 
 def attention_kernel(q_ref, k_ref, v_ref, lat_ref, wo_ref, out_ref, att_ref):
     cells, channels = q_ref.shape
-    positions = k_ref.shape[0]
     rows, cols = lat_ref.shape[0], lat_ref.shape[1]
     wide = cols + 2 * RADIUS
     span = 2 * RADIUS + 1
     head_size = channels // HEADS
     group = 128
     scale = head_size ** (-0.5)
-    cell = lax.broadcasted_iota(jnp.int32, (cells, positions), 0)
-    place = lax.broadcasted_iota(jnp.int32, (cells, positions), 1)
+    band_rows = 8
+    band_cells = band_rows * cols
+    band_keys = -(-(band_rows + span - 1) * wide // group) * group
+    cell = lax.broadcasted_iota(jnp.int32, (band_cells, band_keys), 0)
+    place = lax.broadcasted_iota(jnp.int32, (band_cells, band_keys), 1)
     row_gap = place // wide - cell // cols
     col_gap = place % wide - cell % cols
     valid = (row_gap >= 0) & (row_gap < span) & (col_gap >= 0) & (col_gap < span)
-    lane = lax.broadcasted_iota(jnp.int32, (cells, group), 1) // head_size
+    lane = lax.broadcasted_iota(jnp.int32, (band_cells, group), 1) // head_size
     for g in range(channels // group):
         lanes = slice(g * group, (g + 1) * group)
-        q_g = q_ref[:, lanes]
-        k_g = k_ref[:, lanes]
-        v_g = v_ref[:, lanes]
-        acc = jnp.zeros((cells, group), jnp.float32)
-        for part in range(group // head_size):
-            q_h = jnp.where(lane == part, q_g, jnp.zeros_like(q_g))
-            s = lax.dot_general(
-                q_h, k_g, (((1,), (1,)), ((), ())), preferred_element_type=jnp.float32
-            )
-            s = jnp.where(valid, s * scale, -jnp.inf)
-            top = jnp.max(s, axis=1, keepdims=True)
-            e = jnp.exp(s - top)
-            total = jnp.sum(e, axis=1, keepdims=True)
-            w = (e / total).astype(jnp.bfloat16)
-            o = jnp.dot(w, v_g, preferred_element_type=jnp.float32)
-            acc = jnp.where(lane == part, o, acc)
-        att_ref[:, lanes] = acc.astype(jnp.bfloat16)
+        for band in range(rows // band_rows):
+            q_g = q_ref[pl.ds(band * band_cells, band_cells), lanes]
+            first = band * band_rows * wide
+            k_g = k_ref[pl.ds(first, band_keys), lanes]
+            v_g = v_ref[pl.ds(first, band_keys), lanes]
+            acc = jnp.zeros((band_cells, group), jnp.float32)
+            for part in range(group // head_size):
+                q_h = jnp.where(lane == part, q_g, jnp.zeros_like(q_g))
+                s = lax.dot_general(
+                    q_h, k_g, (((1,), (1,)), ((), ())), preferred_element_type=jnp.float32
+                )
+                s = jnp.where(valid, s * scale, -jnp.inf)
+                top = jnp.max(s, axis=1, keepdims=True)
+                e = jnp.exp(s - top)
+                total = jnp.sum(e, axis=1, keepdims=True)
+                w = (e / total).astype(jnp.bfloat16)
+                o = jnp.dot(w, v_g, preferred_element_type=jnp.float32)
+                acc = jnp.where(lane == part, o, acc)
+            att_ref[pl.ds(band * band_cells, band_cells), lanes] = acc.astype(jnp.bfloat16)
     mixed = jnp.dot(att_ref[...], wo_ref[...], preferred_element_type=jnp.float32)
     lat = lat_ref[...].reshape(cells, channels)
     out_ref[...] = (lat.astype(jnp.float32) + mixed).astype(out_ref.dtype)
@@ -122,7 +126,9 @@
     rows, cols, channels = own_tile.shape
     cells = rows * cols
     flat = field_pad.reshape(-1, channels)
-    positions = -(-flat.shape[0] // 128) * 128
+    wide = cols + 2 * RADIUS
+    band_keys = -(-(8 + 2 * RADIUS) * wide // 128) * 128
+    positions = max(-(-flat.shape[0] // 128) * 128, (rows - 8) * wide + band_keys)
     flat = jnp.pad(flat, ((0, positions - flat.shape[0]), (0, 0)))
     key_flat = project(flat, w_key)
     value_flat = project(flat, w_value)

time: 60.6 us -> 66.4 us (1.096)
  Pallas kernels: 7 us -> 12.8 us
    pallas_call x1, Pallas kernels: 7 us -> 12.8 us  [attend_and_mix(): pl.pallas_call(attention_kernel, out_shape=jax.ShapeDtypeStruct((cells, c...]
  transfers between devices with their start and end apart: 16 -> 16, of which waited for: 4 -> 4; matrix products, arithmetic and copies ran while one was open for 9% -> 8% of each run, Pallas kernels for 0% -> 0%
where the time goes in v13:
time: 66.4 us; the launch traced here: 66.2 us
  starting transfers between devices  22.9 us (34%)
  Pallas kernels  12.8 us (19%)
  waiting for transfers between devices  12.1 us (18%)
  other arithmetic  7.88 us (12%)
  local copies, waits for them, and re-layouts  5.5 us (8%)
  matrix products  4.46 us (7%)
    ppermute x12, starting transfers between devices, doubling_gather(): lax.ppermute(held, axis, [(i, i ^ d * stride) for i in range(count)])  13.9 us
    pallas_call x1, Pallas kernels, attend_and_mix(): pl.pallas_call(attention_kernel, out_shape=jax.ShapeDtypeStruct((cells, c...  12.8 us
    ppermute x12, waiting for transfers between devices, doubling_gather(): lax.ppermute(held, axis, [(i, i ^ d * stride) for i in range(count)])  12.1 us
    ppermute x2, starting transfers between devices, padded_2(): after = lax.ppermute(first, axis, down)  8.86 us
    dot_general x3, matrix products, project(): jnp.dot(flat, weight, preferred_element_type=jnp.float32)  3.72 us
    gather x4, local copies, waits for them, and re-layouts, doubling_gather(): jnp.take(jnp.stack(got), digit ^ jnp.arange(r, dtype=jnp.int32), axis=0)  2.27 us
    convert_element_type x2, other arithmetic, normalize(): return (values * factor * norm_gain).astype(jnp.bfloat16)  2.17 us
  transfers between devices with their start and end apart: 16, of which 4 were waited for; matrix products, arithmetic and copies ran while one was open for 8% of the time, Pallas kernels for 0%

profile of v13, /device:TPU:0, one launch (start us, length us, event | category | flops | bytes accessed | tf_op | source)
XLA Modules:
  0.0 66.2 jit_solution(7120427524745132896)
XLA Ops:
  0.0 1.1 %fusion.16 = f32[32,8]{1,0:T(8,128)S(1)} fusion(bf16[1,32,8,512]{3,2,1,0:T(8,128)(2,1)} %param.8), kind=kLoop, calls=%fused_computation.33 | loop fusion | flops 392960 | bytes 263168 | tf_op jit(solution)/shard_map/reduce_sum | solution.py:27
  1.2 1.1 %fusion.18 = bf16[32,8,512]{2,1,0:T(8,128)(2,1)S(1)} fusion(f32[512]{0:T(512)} %param.9, f32[32,8]{1,0:T(8,128)S(1)} %add_rsqrt_fusion, bf16[1,32,8,512]{3,2,1,0:T(8,128)(2,1)} %param.8), kind=kLoop, calls=%fused_computation.35 | loop fusion | flops 524288 | bytes 527360 | tf_op jit(solution)/shard_map/convert_element_type | solution.py:28
  2.3 3.1 %collective-permute-start = (bf16[1,2,8,512]{3,2,1,0:T(8,128)(2,1)S(1)}, bf16[1,2,8,512]{3,2,1,0:T(8,128)(2,1)S(1)}, u32[]{:S(2)}, u32[]{:S(2)}) collective-permute-start(bf16[1,2,8,512]{3,2,1,0:T(8,128)(2,1)S(1)} %get-tuple-element.42), channel_id=1, source_target_pairs={{0,4},{1,5},{2,6},{3,7},{4,0},{5,1},{6,2},{7,3},{8,12},{9,13},{10,... | collective-permute-start | bytes 49160 | tf_op jit(solution)/shard_map/ppermute | solution.py:176
  5.4 2.6 %collective-permute-start.1 = (bf16[1,2,8,512]{3,2,1,0:T(8,128)(2,1)S(1)}, bf16[1,2,8,512]{3,2,1,0:T(8,128)(2,1)S(1)}, u32[]{:S(2)}, u32[]{:S(2)}) collective-permute-start(bf16[1,2,8,512]{3,2,1,0:T(8,128)(2,1)S(1)} %get-tuple-element.42), channel_id=1, source_target_pairs={{0,8},{1,9},{2,10},{3,11},{4,12},{5,13},{6,14},{7,15},{8,0},{9,1},... | collective-permute-start | bytes 49160 | tf_op jit(solution)/shard_map/ppermute | solution.py:176
  8.0 1.1 %multiply_convert_fusion = bf16[1,32,8,512]{3,2,1,0:T(8,128)(2,1)S(1)} fusion(bf16[1,32,8,512]{3,2,1,0:T(8,128)(2,1)} %param.8, f32[512]{0:T(512)} %param.9, f32[32,8]{1,0:T(8,128)S(1)} %add_rsqrt_fusion), kind=kLoop, calls=%fused_computation.39 | loop fusion | flops 524288 | bytes 527360 | tf_op jit(solution)/shard_map/convert_element_type | solution.py:28
  9.2 4.4 %collective-permute-start.7 = (bf16[1,32,1,512]{3,2,1,0:T(2,128)(2,1)S(1)}, bf16[1,32,1,512]{3,2,1,0:T(2,128)(2,1)S(1)}, u32[]{:S(2)}, u32[]{:S(2)}) collective-permute-start(bf16[1,32,1,512]{3,2,1,0:T(2,128)(2,1)S(1)} %get-tuple-element.25), channel_id=1, source_target_pairs={{1,0},{2,1},{3,2},{4,3},{5,4},{6,5},{7,6},{8,7},{9,8},{10,9},{11,1... | collective-permute-start | bytes 98312 | tf_op jit(solution)/shard_map/ppermute | solution.py:20
  13.7 0.2 slice_reduce_fusion.2
  13.9 0.2 compare_reduce_fusion
  15.0 0.6 gather_fusion
  15.7 0.1 collective-permute-start.4
  15.8 1.7 %collective-permute-start.5 = (bf16[4,1,2,8,512]{4,3,2,0,1:T(8,128)(2,1)S(1)}, bf16[4,1,2,8,512]{4,3,2,0,1:T(8,128)(2,1)S(1)}, u32[]{:S(2)}, u32[]{:S(2)}) collective-permute-start(bf16[4,1,2,8,512]{4,3,2,0,1:T(8,128)(2,1)S(1)} %bitcast_select_fusion.4), channel_id=1, source_target_pairs={{0,3},{1,2},{2,1},{3,0},{4,7},{5,6},{6,5},{7,4},{8,11},{9,10},{10,... | collective-permute-start | bytes 196616 | tf_op jit(solution)/shard_map/ppermute | solution.py:176
  17.6 0.3 maximum_bitcast_fusion.1
  17.9 2.8 %collective-permute-done.4 = bf16[4,1,2,8,512]{4,3,2,0,1:T(8,128)(2,1)S(1)} collective-permute-done((bf16[4,1,2,8,512]{4,3,2,0,1:T(8,128)(2,1)S(1)}, bf16[4,1,2,8,512]{4,3,2,0,1:T(8,128)(2,1)S(1)}, u32[]{:S(2)}, u32[]{:S(2)}) %collective-permute-start.4) | collective-permute-done | bytes 65568 | tf_op jit(solution)/shard_map/ppermute | solution.py:176
  20.7 0.5 collective-permute-done.5
  21.2 0.6 gather_fusion.1
  21.8 0.1 fusion.31
  21.9 0.2 copy.24
  22.2 0.3 fusion.12
  22.5 0.1 broadcast_select_fusion.2
  22.7 1.1 %fusion.62 = bf16[1,32,8,512]{3,2,1,0:T(8,128)(2,1)S(1)} fusion(bf16[1,10,512]{2,1,0:T(8,128)(2,1)S(1)} %copy.36, bf16[32,10,512]{2,1,0:T(8,128)(2,1)S(1)} %maximum_bitcast_fusion.1, f32[32,8]{1,0:T(8,128)S(1)} %copy.38, f32[32,8]{1,0:T(8,128)S(1)} %copy.37, f32[32,8]{1,0:T(8,128)S(1)} %copy.35, f32[32,8]{1,0:T(8,128)S(1)} %copy.34, f32[32,8]{1,0:T(8,128)S(1)} %copy.33, ...), kind=kLoop, calls=%fused_computation.135 | loop fusion | flops 5898240 | bytes 1753088 | tf_op jit(solution)/shard_map/broadcast_in_dim | solution.py:197
  23.8 1.1 %add_convert_fusion = bf16[32,8,512]{2,1,0:T(8,128)(2,1)S(1)} fusion(bf16[32,10,512]{2,1,0:T(8,128)(2,1)S(1)} %maximum_bitcast_fusion.1, bf16[1,10,512]{2,1,0:T(8,128)(2,1)S(1)} %copy.36, bf16[1,10,512]{2,1,0:T(8,128)(2,1)S(1)} %copy.29, f32[32,8]{1,0:T(8,128)S(1)} %copy.38, f32[32,8]{1,0:T(8,128)S(1)} %copy.37, f32[32,8]{1,0:T(8,128)S(1)} %copy.35, ...), kind=kLoop, calls=%fused_computation.38 | loop fusion | flops 5898240 | bytes 1753088 | tf_op jit(solution)/shard_map/convert_element_type | solution.py:69
  24.9 2.6 %collective-permute-start.9 = (bf16[1,6,8,512]{3,2,1,0:T(8,128)(2,1)S(1)}, bf16[1,6,8,512]{3,2,1,0:T(8,128)(2,1)S(1)}, u32[]{:S(2)}, u32[]{:S(2)}) collective-permute-start(bf16[1,6,8,512]{3,2,1,0:T(8,128)(2,1)S(1)} %get-tuple-element.29), channel_id=1, source_target_pairs={{0,8},{1,9},{2,10},{3,11},{4,12},{5,13},{6,14},{7,15},{8,0},{9,1},... | collective-permute-start | bytes 147464 | tf_op jit(solution)/shard_map/ppermute | solution.py:176
  27.5 1.8 %collective-permute-start.10 = (bf16[1,6,8,512]{3,2,1,0:T(8,128)(2,1)S(1)}, bf16[1,6,8,512]{3,2,1,0:T(8,128)(2,1)S(1)}, u32[]{:S(2)}, u32[]{:S(2)}) collective-permute-start(bf16[1,6,8,512]{3,2,1,0:T(8,128)(2,1)S(1)} %get-tuple-element.29), channel_id=1, source_target_pairs={{0,12},{1,13},{2,14},{3,15},{4,8},{5,9},{6,10},{7,11},{8,4},{9,5},... | collective-permute-start | bytes 147464 | tf_op jit(solution)/shard_map/ppermute | solution.py:176
  29.5 4.4 %collective-permute-start.15 = (bf16[1,32,3,512]{3,2,1,0:T(4,128)(2,1)S(1)}, bf16[1,32,3,512]{3,2,1,0:T(4,128)(2,1)S(1)}, u32[]{:S(2)}, u32[]{:S(2)}) collective-permute-start(bf16[1,32,3,512]{3,2,1,0:T(4,128)(2,1)S(1)} %get-tuple-element.15), channel_id=1, source_target_pairs={{1,0},{2,1},{3,2},{4,3},{5,4},{6,5},{7,6},{8,7},{9,8},{10,9},{11,1... | collective-permute-start | bytes 294920 | tf_op jit(solution)/shard_map/ppermute | solution.py:20
  33.9 1.0 %convolution_convert_fusion.2.q_ref = bf16[256,512]{1,0:T(8,128)(2,1)} fusion(bf16[512,512]{1,0:T(8,128)(2,1)S(1)} %copy-done.1, bf16[32,8,512]{2,1,0:T(8,128)(2,1)S(1)} %add_convert_fusion), kind=kOutput, calls=%fused_computation.14 | convolution fusion | flops 134348800 | bytes 1048576 | tf_op jit(solution)/shard_map/dot_general | solution.py:76
  34.9 0.6 gather_fusion.2
  35.7 1.8 %collective-permute-start.13 = (bf16[4,1,6,8,512]{4,3,2,0,1:T(8,128)(2,1)S(1)}, bf16[4,1,6,8,512]{4,3,2,0,1:T(8,128)(2,1)S(1)}, u32[]{:S(2)}, u32[]{:S(2)}) collective-permute-start(bf16[4,1,6,8,512]{4,3,2,0,1:T(8,128)(2,1)S(1)} %bitcast_select_fusion.2), channel_id=1, source_target_pairs={{0,3},{1,2},{2,1},{3,0},{4,7},{5,6},{6,5},{7,4},{8,11},{9,10},{10,... | collective-permute-start | bytes 589832 | tf_op jit(solution)/shard_map/ppermute | solution.py:176
  37.6 0.3 maximum_bitcast_fusion.2
  37.9 5.5 %collective-permute-done.12 = bf16[4,1,6,8,512]{4,3,2,0,1:T(8,128)(2,1)S(1)} collective-permute-done((bf16[4,1,6,8,512]{4,3,2,0,1:T(8,128)(2,1)S(1)}, bf16[4,1,6,8,512]{4,3,2,0,1:T(8,128)(2,1)S(1)}, u32[]{:S(2)}, u32[]{:S(2)}) %collective-permute-start.12) | collective-permute-done | bytes 196640 | tf_op jit(solution)/shard_map/ppermute | solution.py:176
  43.4 3.3 %collective-permute-done.13 = bf16[4,1,6,8,512]{4,3,2,0,1:T(8,128)(2,1)S(1)} collective-permute-done((bf16[4,1,6,8,512]{4,3,2,0,1:T(8,128)(2,1)S(1)}, bf16[4,1,6,8,512]{4,3,2,0,1:T(8,128)(2,1)S(1)}, u32[]{:S(2)}, u32[]{:S(2)}) %collective-permute-start.13) | collective-permute-done | bytes 196640 | tf_op jit(solution)/shard_map/ppermute | solution.py:176
  46.7 0.1 maximum_bitcast_fusion
  46.8 0.6 gather_fusion.3
  47.5 0.1 fusion.13
  47.6 0.6 copy.39
  48.2 0.2 reshape.199
  48.4 0.4 fusion.50
  48.8 0.2 fusion.49
  49.0 0.3 fusion
  49.3 0.1 slice_bitcast_fusion.1
  49.4 0.4 fusion.9
  49.9 0.2 broadcast_select_fusion
  50.0 0.1 broadcast_select_fusion.1
  50.2 0.1 fusion.57
  50.3 0.1 pad_maximum_fusion.2
  50.4 0.2 reshape.200
  50.6 1.4 %convolution_convert_fusion.v_ref = bf16[640,512]{1,0:T(8,128)(2,1)} fusion(bf16[512,512]{1,0:T(8,128)(2,1)S(1)} %copy-done, bf16[532,512]{1,0:T(8,128)(2,1)S(1)} %reshape.200), kind=kOutput, calls=%fused_computation.12 | convolution fusion | flops 335872000 | bytes 1724416 | tf_op jit(solution)/shard_map/dot_general | solution.py:76
  52.0 1.4 %convolution_convert_fusion.1.k_ref = bf16[640,512]{1,0:T(8,128)(2,1)} fusion(bf16[512,512]{1,0:T(8,128)(2,1)S(1)} %copy-done.4, bf16[532,512]{1,0:T(8,128)(2,1)S(1)} %reshape.200), kind=kOutput, calls=%fused_computation.13 | convolution fusion | flops 335872000 | bytes 1724416 | tf_op jit(solution)/shard_map/dot_general | solution.py:76
  53.4 12.8 %shard_map.82 = bf16[256,512]{1,0:T(8,128)(2,1)} custom-call(bf16[256,512]{1,0:T(8,128)(2,1)} %convolution_convert_fusion.2.q_ref, bf16[640,512]{1,0:T(8,128)(2,1)} %convolution_convert_fusion.1.k_ref, bf16[640,512]{1,0:T(8,128)(2,1)} %convolution_convert_fusion.v_ref, bf16[32,8,512]{2,1,0:T(8,128)(2,1)} %bitcast.118, bf16[512,512]{1,0:T(8,128)(2,1)} %wo_ref.1), custom_call_target="tpu_custom_call" | custom-call | tf_op jit(solution)/shard_map/pallas_call | solution.py:136
  (69 shorter events, 2.0 us)
Async XLA Ops:
  0.0 50.6 %copy-start = (bf16[512,512]{1,0:T(8,128)(2,1)S(1)}, bf16[512,512]{1,0:T(8,128)(2,1)}, u32[]{:S(2)}) copy-start(bf16[512,512]{1,0:T(8,128)(2,1)} %param.13) | copy-start | bytes 1572868
  0.0 13.7 %copy-start.3 = (s32[1,2,3]{2,1,0:T(2,128)S(1)}, s32[1,2,3]{2,1,0:T(2,128)}, u32[]{:S(2)}) copy-start(s32[1,2,3]{2,1,0:T(2,128)} %param.15) | copy-start | bytes 76
  0.0 14.2 %copy-start.2 = (f32[1,9,32,8]{2,3,1,0:T(8,128)S(1)}, f32[1,9,32,8]{2,3,1,0:T(8,128)}, u32[]{:S(2)}) copy-start(f32[1,9,32,8]{2,3,1,0:T(8,128)} %param.10) | copy-start | bytes 27652
  2.3 12.7 %collective-permute-start = (bf16[1,2,8,512]{3,2,1,0:T(8,128)(2,1)S(1)}, bf16[1,2,8,512]{3,2,1,0:T(8,128)(2,1)S(1)}, u32[]{:S(2)}, u32[]{:S(2)}) collective-permute-start(bf16[1,2,8,512]{3,2,1,0:T(8,128)(2,1)S(1)} %get-tuple-element.42), channel_id=1, source_target_pairs={{0,4},{1,5},{2,6},{3,7},{4,0},{5,1},{6,2},{7,3},{8,12},{9,13},{10,... | collective-permute-start | bytes 49160 | tf_op jit(solution)/shard_map/ppermute | solution.py:176
  5.4 9.6 %collective-permute-start.1 = (bf16[1,2,8,512]{3,2,1,0:T(8,128)(2,1)S(1)}, bf16[1,2,8,512]{3,2,1,0:T(8,128)(2,1)S(1)}, u32[]{:S(2)}, u32[]{:S(2)}) collective-permute-start(bf16[1,2,8,512]{3,2,1,0:T(8,128)(2,1)S(1)} %get-tuple-element.42), channel_id=1, source_target_pairs={{0,8},{1,9},{2,10},{3,11},{4,12},{5,13},{6,14},{7,15},{8,0},{9,1},... | collective-permute-start | bytes 49160 | tf_op jit(solution)/shard_map/ppermute | solution.py:176
  8.0 7.0 %collective-permute-start.2 = (bf16[1,2,8,512]{3,2,1,0:T(8,128)(2,1)S(1)}, bf16[1,2,8,512]{3,2,1,0:T(8,128)(2,1)S(1)}, u32[]{:S(2)}, u32[]{:S(2)}) collective-permute-start(bf16[1,2,8,512]{3,2,1,0:T(8,128)(2,1)S(1)} %get-tuple-element.42), channel_id=1, source_target_pairs={{0,12},{1,13},{2,14},{3,15},{4,8},{5,9},{6,10},{7,11},{8,4},{9,5},... | collective-permute-start | bytes 49160 | tf_op jit(solution)/shard_map/ppermute | solution.py:176
  9.2 8.4 %collective-permute-start.6 = (bf16[1,32,1,512]{3,2,1,0:T(2,128)(2,1)S(1)}, bf16[1,32,1,512]{3,2,1,0:T(2,128)(2,1)S(1)}, u32[]{:S(2)}, u32[]{:S(2)}) collective-permute-start(bf16[1,32,1,512]{3,2,1,0:T(2,128)(2,1)S(1)} %get-tuple-element.24), channel_id=1, source_target_pairs={{0,1},{1,2},{2,3},{3,4},{4,5},{5,6},{6,7},{7,8},{8,9},{9,10},{10,1... | collective-permute-start | bytes 98312 | tf_op jit(solution)/shard_map/ppermute | solution.py:19
  9.2 8.4 %collective-permute-start.7 = (bf16[1,32,1,512]{3,2,1,0:T(2,128)(2,1)S(1)}, bf16[1,32,1,512]{3,2,1,0:T(2,128)(2,1)S(1)}, u32[]{:S(2)}, u32[]{:S(2)}) collective-permute-start(bf16[1,32,1,512]{3,2,1,0:T(2,128)(2,1)S(1)} %get-tuple-element.25), channel_id=1, source_target_pairs={{1,0},{2,1},{3,2},{4,3},{5,4},{6,5},{7,6},{8,7},{9,8},{10,9},{11,1... | collective-permute-start | bytes 98312 | tf_op jit(solution)/shard_map/ppermute | solution.py:20
  15.7 2.2 %collective-permute-start.3 = (bf16[4,1,2,8,512]{4,3,2,0,1:T(8,128)(2,1)S(1)}, bf16[4,1,2,8,512]{4,3,2,0,1:T(8,128)(2,1)S(1)}, u32[]{:S(2)}, u32[]{:S(2)}) collective-permute-start(bf16[4,1,2,8,512]{4,3,2,0,1:T(8,128)(2,1)S(1)} %bitcast_select_fusion.4), channel_id=1, source_target_pairs={{0,1},{1,0},{2,3},{3,2},{4,5},{5,4},{6,7},{7,6},{8,9},{9,8},{10,11... | collective-permute-start | bytes 196616 | tf_op jit(solution)/shard_map/ppermute | solution.py:176
  15.7 5.0 %collective-permute-start.4 = (bf16[4,1,2,8,512]{4,3,2,0,1:T(8,128)(2,1)S(1)}, bf16[4,1,2,8,512]{4,3,2,0,1:T(8,128)(2,1)S(1)}, u32[]{:S(2)}, u32[]{:S(2)}) collective-permute-start(bf16[4,1,2,8,512]{4,3,2,0,1:T(8,128)(2,1)S(1)} %bitcast_select_fusion.4), channel_id=1, source_target_pairs={{0,2},{1,3},{2,0},{3,1},{4,6},{5,7},{6,4},{7,5},{8,10},{9,11},{10,... | collective-permute-start | bytes 196616 | tf_op jit(solution)/shard_map/ppermute | solution.py:176
  15.8 5.3 %collective-permute-start.5 = (bf16[4,1,2,8,512]{4,3,2,0,1:T(8,128)(2,1)S(1)}, bf16[4,1,2,8,512]{4,3,2,0,1:T(8,128)(2,1)S(1)}, u32[]{:S(2)}, u32[]{:S(2)}) collective-permute-start(bf16[4,1,2,8,512]{4,3,2,0,1:T(8,128)(2,1)S(1)} %bitcast_select_fusion.4), channel_id=1, source_target_pairs={{0,3},{1,2},{2,1},{3,0},{4,7},{5,6},{6,5},{7,4},{8,11},{9,10},{10,... | collective-permute-start | bytes 196616 | tf_op jit(solution)/shard_map/ppermute | solution.py:176
  23.7 10.1 %copy-start.1 = (bf16[512,512]{1,0:T(8,128)(2,1)S(1)}, bf16[512,512]{1,0:T(8,128)(2,1)}, u32[]{:S(2)}) copy-start(bf16[512,512]{1,0:T(8,128)(2,1)} %param.11) | copy-start | bytes 1572868
  24.8 10.0 %collective-permute-start.8 = (bf16[1,6,8,512]{3,2,1,0:T(8,128)(2,1)S(1)}, bf16[1,6,8,512]{3,2,1,0:T(8,128)(2,1)S(1)}, u32[]{:S(2)}, u32[]{:S(2)}) collective-permute-start(bf16[1,6,8,512]{3,2,1,0:T(8,128)(2,1)S(1)} %get-tuple-element.29), channel_id=1, source_target_pairs={{0,4},{1,5},{2,6},{3,7},{4,0},{5,1},{6,2},{7,3},{8,12},{9,13},{10,... | collective-permute-start | bytes 147464 | tf_op jit(solution)/shard_map/ppermute | solution.py:176
  24.9 10.0 %collective-permute-start.9 = (bf16[1,6,8,512]{3,2,1,0:T(8,128)(2,1)S(1)}, bf16[1,6,8,512]{3,2,1,0:T(8,128)(2,1)S(1)}, u32[]{:S(2)}, u32[]{:S(2)}) collective-permute-start(bf16[1,6,8,512]{3,2,1,0:T(8,128)(2,1)S(1)} %get-tuple-element.29), channel_id=1, source_target_pairs={{0,8},{1,9},{2,10},{3,11},{4,12},{5,13},{6,14},{7,15},{8,0},{9,1},... | collective-permute-start | bytes 147464 | tf_op jit(solution)/shard_map/ppermute | solution.py:176
  27.5 7.4 %collective-permute-start.10 = (bf16[1,6,8,512]{3,2,1,0:T(8,128)(2,1)S(1)}, bf16[1,6,8,512]{3,2,1,0:T(8,128)(2,1)S(1)}, u32[]{:S(2)}, u32[]{:S(2)}) collective-permute-start(bf16[1,6,8,512]{3,2,1,0:T(8,128)(2,1)S(1)} %get-tuple-element.29), channel_id=1, source_target_pairs={{0,12},{1,13},{2,14},{3,15},{4,8},{5,9},{6,10},{7,11},{8,4},{9,5},... | collective-permute-start | bytes 147464 | tf_op jit(solution)/shard_map/ppermute | solution.py:176
  29.4 8.2 %collective-permute-start.14 = (bf16[1,32,3,512]{3,2,1,0:T(4,128)(2,1)S(1)}, bf16[1,32,3,512]{3,2,1,0:T(4,128)(2,1)S(1)}, u32[]{:S(2)}, u32[]{:S(2)}) collective-permute-start(bf16[1,32,3,512]{3,2,1,0:T(4,128)(2,1)S(1)} %get-tuple-element.14), channel_id=1, source_target_pairs={{0,1},{1,2},{2,3},{3,4},{4,5},{5,6},{6,7},{7,8},{8,9},{9,10},{10,1... | collective-permute-start | bytes 294920 | tf_op jit(solution)/shard_map/ppermute | solution.py:19
  29.5 8.2 %collective-permute-start.15 = (bf16[1,32,3,512]{3,2,1,0:T(4,128)(2,1)S(1)}, bf16[1,32,3,512]{3,2,1,0:T(4,128)(2,1)S(1)}, u32[]{:S(2)}, u32[]{:S(2)}) collective-permute-start(bf16[1,32,3,512]{3,2,1,0:T(4,128)(2,1)S(1)} %get-tuple-element.15), channel_id=1, source_target_pairs={{1,0},{2,1},{3,2},{4,3},{5,4},{6,5},{7,6},{8,7},{9,8},{10,9},{11,1... | collective-permute-start | bytes 294920 | tf_op jit(solution)/shard_map/ppermute | solution.py:20
  35.6 2.4 %collective-permute-start.11 = (bf16[4,1,6,8,512]{4,3,2,0,1:T(8,128)(2,1)S(1)}, bf16[4,1,6,8,512]{4,3,2,0,1:T(8,128)(2,1)S(1)}, u32[]{:S(2)}, u32[]{:S(2)}) collective-permute-start(bf16[4,1,6,8,512]{4,3,2,0,1:T(8,128)(2,1)S(1)} %bitcast_select_fusion.2), channel_id=1, source_target_pairs={{0,1},{1,0},{2,3},{3,2},{4,5},{5,4},{6,7},{7,6},{8,9},{9,8},{10,11... | collective-permute-start | bytes 589832 | tf_op jit(solution)/shard_map/ppermute | solution.py:176
  35.7 7.8 %collective-permute-start.12 = (bf16[4,1,6,8,512]{4,3,2,0,1:T(8,128)(2,1)S(1)}, bf16[4,1,6,8,512]{4,3,2,0,1:T(8,128)(2,1)S(1)}, u32[]{:S(2)}, u32[]{:S(2)}) collective-permute-start(bf16[4,1,6,8,512]{4,3,2,0,1:T(8,128)(2,1)S(1)} %bitcast_select_fusion.2), channel_id=1, source_target_pairs={{0,2},{1,3},{2,0},{3,1},{4,6},{5,7},{6,4},{7,5},{8,10},{9,11},{10,... | collective-permute-start | bytes 589832 | tf_op jit(solution)/shard_map/ppermute | solution.py:176
  35.7 11.0 %collective-permute-start.13 = (bf16[4,1,6,8,512]{4,3,2,0,1:T(8,128)(2,1)S(1)}, bf16[4,1,6,8,512]{4,3,2,0,1:T(8,128)(2,1)S(1)}, u32[]{:S(2)}, u32[]{:S(2)}) collective-permute-start(bf16[4,1,6,8,512]{4,3,2,0,1:T(8,128)(2,1)S(1)} %bitcast_select_fusion.2), channel_id=1, source_target_pairs={{0,3},{1,2},{2,1},{3,0},{4,7},{5,6},{6,5},{7,4},{8,11},{9,10},{10,... | collective-permute-start | bytes 589832 | tf_op jit(solution)/shard_map/ppermute | solution.py:176
  50.4 1.5 %copy-start.4 = (bf16[512,512]{1,0:T(8,128)(2,1)S(1)}, bf16[512,512]{1,0:T(8,128)(2,1)}, u32[]{:S(2)}) copy-start(bf16[512,512]{1,0:T(8,128)(2,1)} %param.12) | copy-start | bytes 1572868

commit v14 on v12

--- a/solution.py
+++ b/solution.py
@@ -118,14 +118,22 @@
     out_ref[...] = (lat.astype(jnp.float32) + mixed).astype(out_ref.dtype)
 
 
-def attend_and_mix(query, field_pad, w_key, w_value, own_tile, w_output):
+def attend_and_mix(query, center, rims, w_key, w_value, own_tile, w_output):
     rows, cols, channels = own_tile.shape
     cells = rows * cols
-    flat = field_pad.reshape(-1, channels)
-    positions = -(-flat.shape[0] // 128) * 128
-    flat = jnp.pad(flat, ((0, positions - flat.shape[0]), (0, 0)))
-    key_flat = project(flat, w_key)
-    value_flat = project(flat, w_value)
+    center_flat = center.reshape(-1, channels)
+    rim_flat = rims.reshape(2, -1, channels)
+    count = center_flat.shape[0] + 2 * rim_flat.shape[1]
+    positions = -(-count // 128) * 128
+    tail = jnp.zeros((positions - count, channels), jnp.bfloat16)
+
+    def both(weight):
+        mid = project(center_flat, weight)
+        edge = project(rim_flat.reshape(-1, channels), weight).reshape(rim_flat.shape)
+        return jnp.concatenate([edge[0], mid, edge[1], tail], axis=0)
+
+    key_flat = both(w_key)
+    value_flat = both(w_value)
     vmem = pl.BlockSpec(memory_space=pltpu.VMEM)
     out = pl.pallas_call(
         attention_kernel,
@@ -193,8 +201,8 @@
     got3 = widen_tiles(doubling_gather(rows3[None], "blk"), RADIUS)
     edges3 = jnp.stack([got3[:, :RADIUS], got3[:, RADIUS:]], axis=1)
     field_got = pick_all(seam_rows, edges3)
-    field_pad = place_rims(field_wide[0], field_got, seam_rows)
-    return attend_and_mix(query, field_pad, w_key, w_value, own_tile, w_output)[None]
+    arrived = orient_rims(field_got, seam_rows)
+    return attend_and_mix(query, field_wide[0], arrived, w_key, w_value, own_tile, w_output)[None]
 
 
 def solution(mesh):

time: 60.6 us -> 60 us (0.990)
  other arithmetic: 7.88 us -> 11.6 us
  starting transfers between devices: 22.9 us -> 19.6 us
  matrix products: 4.46 us -> 2.98 us
  local copies, waits for them, and re-layouts: 5.5 us -> 6.44 us
    ppermute x12, waiting for transfers between devices: 12.1 us -> 5.98 us  [doubling_gather(): lax.ppermute(held, axis, [(i, i ^ d * stride) for i in range(count)])]
    ppermute x2, waiting for transfers between devices: 0.01 us -> 5.61 us  [padded_2(): before = lax.ppermute(last, axis, up)]
    ppermute x2, starting transfers between devices: 8.86 us -> 5.38 us  [padded_2(): after = lax.ppermute(first, axis, down)]
    concatenate x1 -> x2, other arithmetic: 0.1 us -> 1.75 us  [the longest x1 1.46 us: both(): return jnp.concatenate([edge[0], mid, edge[1], tail], axis=0)]
    dot_general x3 -> x5, matrix products: 3.72 us -> 2.24 us  [project(): jnp.dot(flat, weight, preferred_element_type=jnp.float32)]
    another operation x6, other arithmetic: 0.19 us -> 1.31 us  [doubling_gather(): jnp.stack(got)]
    unnamed x11 -> x20, local copies, waits for them, and re-layouts: 0.04 us -> 0.97 us
    select_n x6, other arithmetic: 0.34 us -> 1.02 us  [doubling_gather(): jnp.take(jnp.stack(got), digit ^ jnp.arange(r, dtype=jnp.int32), axis=0)]
  transfers between devices with their start and end apart: 16 -> 16, of which waited for: 4 -> 7; matrix products, arithmetic and copies ran while one was open for 9% -> 15% of each run, Pallas kernels for 0% -> 0%
where the time goes in v14:
time: 60 us; the launch traced here: 59.7 us
  starting transfers between devices  19.6 us (33%)
  other arithmetic  11.6 us (19%)
  waiting for transfers between devices  11.6 us (19%)
  Pallas kernels  7 us (12%)
  local copies, waits for them, and re-layouts  6.44 us (11%)
  matrix products  2.98 us (5%)
    ppermute x12, starting transfers between devices, doubling_gather(): lax.ppermute(held, axis, [(i, i ^ d * stride) for i in range(count)])  14.2 us
    pallas_call x1, Pallas kernels, attend_and_mix(): pl.pallas_call(attention_kernel, out_shape=jax.ShapeDtypeStruct((cells, c...  7 us
    ppermute x12, waiting for transfers between devices, doubling_gather(): lax.ppermute(held, axis, [(i, i ^ d * stride) for i in range(count)])  5.98 us
    ppermute x2, waiting for transfers between devices, padded_2(): before = lax.ppermute(last, axis, up)  5.61 us
    ppermute x2, starting transfers between devices, padded_2(): after = lax.ppermute(first, axis, down)  5.38 us
    gather x4, local copies, waits for them, and re-layouts, doubling_gather(): jnp.take(jnp.stack(got), digit ^ jnp.arange(r, dtype=jnp.int32), axis=0)  2.27 us
    dot_general x5, matrix products, project(): jnp.dot(flat, weight, preferred_element_type=jnp.float32)  2.24 us
    convert_element_type x2, other arithmetic, normalize(): return (values * factor * norm_gain).astype(jnp.bfloat16)  2.17 us
  transfers between devices with their start and end apart: 16, of which 7 were waited for; matrix products, arithmetic and copies ran while one was open for 15% of the time, Pallas kernels for 0%

profile of v14, /device:TPU:0, one launch (start us, length us, event | category | flops | bytes accessed | tf_op | source)
XLA Modules:
  0.0 59.7 jit_solution(5761622113833877394)
XLA Ops:
  0.0 1.1 %fusion.14 = f32[32,8]{1,0:T(8,128)S(1)} fusion(bf16[1,32,8,512]{3,2,1,0:T(8,128)(2,1)} %param.8), kind=kLoop, calls=%fused_computation.34 | loop fusion | flops 392960 | bytes 263168 | tf_op jit(solution)/shard_map/reduce_sum | solution.py:27
  1.2 1.1 %fusion.16 = bf16[32,8,512]{2,1,0:T(8,128)(2,1)S(1)} fusion(f32[512]{0:T(512)} %param.9, f32[32,8]{1,0:T(8,128)S(1)} %add_rsqrt_fusion, bf16[1,32,8,512]{3,2,1,0:T(8,128)(2,1)} %param.8), kind=kLoop, calls=%fused_computation.36 | loop fusion | flops 524288 | bytes 527360 | tf_op jit(solution)/shard_map/convert_element_type | solution.py:28
  2.3 5.1 %collective-permute-start.2 = (bf16[1,2,8,512]{3,2,1,0:T(8,128)(2,1)S(1)}, bf16[1,2,8,512]{3,2,1,0:T(8,128)(2,1)S(1)}, u32[]{:S(2)}, u32[]{:S(2)}) collective-permute-start(bf16[1,2,8,512]{3,2,1,0:T(8,128)(2,1)S(1)} %get-tuple-element.44), channel_id=1, source_target_pairs={{0,12},{1,13},{2,14},{3,15},{4,8},{5,9},{6,10},{7,11},{8,4},{9,5},... | collective-permute-start | bytes 49160 | tf_op jit(solution)/shard_map/ppermute | solution.py:178
  7.4 0.6 %collective-permute-start = (bf16[1,2,8,512]{3,2,1,0:T(8,128)(2,1)S(1)}, bf16[1,2,8,512]{3,2,1,0:T(8,128)(2,1)S(1)}, u32[]{:S(2)}, u32[]{:S(2)}) collective-permute-start(bf16[1,2,8,512]{3,2,1,0:T(8,128)(2,1)S(1)} %get-tuple-element.44), channel_id=1, source_target_pairs={{0,4},{1,5},{2,6},{3,7},{4,0},{5,1},{6,2},{7,3},{8,12},{9,13},{10,... | collective-permute-start | bytes 49160 | tf_op jit(solution)/shard_map/ppermute | solution.py:178
  8.0 1.1 %multiply_convert_fusion = bf16[1,32,8,512]{3,2,1,0:T(8,128)(2,1)S(1)} fusion(bf16[1,32,8,512]{3,2,1,0:T(8,128)(2,1)} %param.8, f32[512]{0:T(512)} %param.9, f32[32,8]{1,0:T(8,128)S(1)} %add_rsqrt_fusion), kind=kLoop, calls=%fused_computation.40 | loop fusion | flops 524288 | bytes 527360 | tf_op jit(solution)/shard_map/convert_element_type | solution.py:28
  9.2 3.4 %collective-permute-start.7 = (bf16[1,32,1,512]{3,2,1,0:T(2,128)(2,1)S(1)}, bf16[1,32,1,512]{3,2,1,0:T(2,128)(2,1)S(1)}, u32[]{:S(2)}, u32[]{:S(2)}) collective-permute-start(bf16[1,32,1,512]{3,2,1,0:T(2,128)(2,1)S(1)} %get-tuple-element.25), channel_id=1, source_target_pairs={{1,0},{2,1},{3,2},{4,3},{5,4},{6,5},{7,6},{8,7},{9,8},{10,9},{11,1... | collective-permute-start | bytes 98312 | tf_op jit(solution)/shard_map/ppermute | solution.py:20
  12.6 0.2 slice_reduce_fusion.2
  12.8 0.2 compare_reduce_fusion
  13.2 0.6 fusion.42
  14.6 0.6 gather_fusion
  15.4 1.7 %collective-permute-start.3 = (bf16[4,1,2,8,512]{4,3,2,0,1:T(8,128)(2,1)S(1)}, bf16[4,1,2,8,512]{4,3,2,0,1:T(8,128)(2,1)S(1)}, u32[]{:S(2)}, u32[]{:S(2)}) collective-permute-start(bf16[4,1,2,8,512]{4,3,2,0,1:T(8,128)(2,1)S(1)} %bitcast_select_fusion.4), channel_id=1, source_target_pairs={{0,1},{1,0},{2,3},{3,2},{4,5},{5,4},{6,7},{7,6},{8,9},{9,8},{10,11... | collective-permute-start | bytes 196616 | tf_op jit(solution)/shard_map/ppermute | solution.py:178
  17.2 1.9 %collective-permute-done.6 = bf16[1,32,1,512]{3,2,1,0:T(2,128)(2,1)S(1)} collective-permute-done((bf16[1,32,1,512]{3,2,1,0:T(2,128)(2,1)S(1)}, bf16[1,32,1,512]{3,2,1,0:T(2,128)(2,1)S(1)}, u32[]{:S(2)}, u32[]{:S(2)}) %collective-permute-start.6) | collective-permute-done | bytes 32800 | tf_op jit(solution)/shard_map/ppermute | solution.py:19
  19.1 0.3 maximum_bitcast_fusion.1
  19.4 0.8 %collective-permute-done.5 = bf16[4,1,2,8,512]{4,3,2,0,1:T(8,128)(2,1)S(1)} collective-permute-done((bf16[4,1,2,8,512]{4,3,2,0,1:T(8,128)(2,1)S(1)}, bf16[4,1,2,8,512]{4,3,2,0,1:T(8,128)(2,1)S(1)}, u32[]{:S(2)}, u32[]{:S(2)}) %collective-permute-start.5) | collective-permute-done | bytes 65568 | tf_op jit(solution)/shard_map/ppermute | solution.py:178
  20.2 0.3 collective-permute-done.4
  20.5 0.6 gather_fusion.1
  21.5 0.3 fusion.12
  22.0 1.1 %add_convert_fusion = bf16[32,8,512]{2,1,0:T(8,128)(2,1)S(1)} fusion(bf16[32,10,512]{2,1,0:T(8,128)(2,1)S(1)} %maximum_bitcast_fusion.1, bf16[1,10,512]{2,1,0:T(8,128)(2,1)S(1)} %copy.36, bf16[1,10,512]{2,1,0:T(8,128)(2,1)S(1)} %copy.29, f32[32,8]{1,0:T(8,128)S(1)} %copy.38, f32[32,8]{1,0:T(8,128)S(1)} %copy.37, f32[32,8]{1,0:T(8,128)S(1)} %copy.35, ...), kind=kLoop, calls=%fused_computation.39 | loop fusion | flops 5898240 | bytes 1753088 | tf_op jit(solution)/shard_map/convert_element_type | solution.py:69
  23.1 4.1 %collective-permute-start.10 = (bf16[1,6,8,512]{3,2,1,0:T(8,128)(2,1)S(1)}, bf16[1,6,8,512]{3,2,1,0:T(8,128)(2,1)S(1)}, u32[]{:S(2)}, u32[]{:S(2)}) collective-permute-start(bf16[1,6,8,512]{3,2,1,0:T(8,128)(2,1)S(1)} %get-tuple-element.31), channel_id=1, source_target_pairs={{0,12},{1,13},{2,14},{3,15},{4,8},{5,9},{6,10},{7,11},{8,4},{9,5},... | collective-permute-start | bytes 147464 | tf_op jit(solution)/shard_map/ppermute | solution.py:178
  27.2 0.6 %collective-permute-start.8 = (bf16[1,6,8,512]{3,2,1,0:T(8,128)(2,1)S(1)}, bf16[1,6,8,512]{3,2,1,0:T(8,128)(2,1)S(1)}, u32[]{:S(2)}, u32[]{:S(2)}) collective-permute-start(bf16[1,6,8,512]{3,2,1,0:T(8,128)(2,1)S(1)} %get-tuple-element.31), channel_id=1, source_target_pairs={{0,4},{1,5},{2,6},{3,7},{4,0},{5,1},{6,2},{7,3},{8,12},{9,13},{10,... | collective-permute-start | bytes 147464 | tf_op jit(solution)/shard_map/ppermute | solution.py:178
  27.8 1.0 %fusion.65 = bf16[1,32,8,512]{3,2,1,0:T(8,128)(2,1)S(1)} fusion(bf16[1,10,512]{2,1,0:T(8,128)(2,1)S(1)} %copy.36, bf16[32,10,512]{2,1,0:T(8,128)(2,1)S(1)} %maximum_bitcast_fusion.1, f32[32,8]{1,0:T(8,128)S(1)} %copy.38, f32[32,8]{1,0:T(8,128)S(1)} %copy.37, f32[32,8]{1,0:T(8,128)S(1)} %copy.35, f32[32,8]{1,0:T(8,128)S(1)} %copy.34, f32[32,8]{1,0:T(8,128)S(1)} %copy.33, ...), kind=kLoop, calls=%fused_computation.133 | loop fusion | flops 5898240 | bytes 1753088 | tf_op jit(solution)/shard_map/broadcast_in_dim | solution.py:199
  28.9 1.0 %convolution_convert_fusion.2.q_ref = bf16[256,512]{1,0:T(8,128)(2,1)} fusion(bf16[512,512]{1,0:T(8,128)(2,1)S(1)} %copy-done.2, bf16[32,8,512]{2,1,0:T(8,128)(2,1)S(1)} %add_convert_fusion), kind=kOutput, calls=%fused_computation.14 | convolution fusion | flops 134348800 | bytes 1048576 | tf_op jit(solution)/shard_map/dot_general | solution.py:76
  30.0 2.0 %collective-permute-start.15 = (bf16[1,32,3,512]{3,2,1,0:T(4,128)(2,1)S(1)}, bf16[1,32,3,512]{3,2,1,0:T(4,128)(2,1)S(1)}, u32[]{:S(2)}, u32[]{:S(2)}) collective-permute-start(bf16[1,32,3,512]{3,2,1,0:T(4,128)(2,1)S(1)} %get-tuple-element.15), channel_id=1, source_target_pairs={{1,0},{2,1},{3,2},{4,3},{5,4},{6,5},{7,6},{8,7},{9,8},{10,9},{11,1... | collective-permute-start | bytes 294920 | tf_op jit(solution)/shard_map/ppermute | solution.py:20
  32.2 0.6 gather_fusion.2
  32.8 0.8 %bitcast_select_fusion.2 = bf16[4,1,6,8,512]{4,3,2,0,1:T(8,128)(2,1)} fusion(bf16[4,6,8,512]{3,2,1,0:T(8,128)(2,1)S(1)} %gather_fusion.2, pred[4]{0:T(512)(128)(4,1)S(1)} %compare_and_fusion), kind=kLoop, calls=%fused_computation.63 | loop fusion | flops 98304 | bytes 393220 | tf_op jit(solution)/shard_map/jit(_take)/select_n | solution.py:180
  33.5 0.7 %collective-permute-start.13 = (bf16[4,1,6,8,512]{4,3,2,0,1:T(8,128)(2,1)}, bf16[4,1,6,8,512]{4,3,2,0,1:T(8,128)(2,1)}, u32[]{:S(2)}, u32[]{:S(2)}) collective-permute-start(bf16[4,1,6,8,512]{4,3,2,0,1:T(8,128)(2,1)} %bitcast_select_fusion.2), channel_id=1, source_target_pairs={{0,3},{1,2},{2,1},{3,0},{4,7},{5,6},{6,5},{7,4},{8,11},{9,10},{10,... | collective-permute-start | bytes 589832 | tf_op jit(solution)/shard_map/ppermute | solution.py:178
  34.2 0.3 collective-permute-start.12
  34.5 0.9 %collective-permute-start.11 = (bf16[4,1,6,8,512]{4,3,2,0,1:T(8,128)(2,1)}, bf16[4,1,6,8,512]{4,3,2,0,1:T(8,128)(2,1)}, u32[]{:S(2)}, u32[]{:S(2)}) collective-permute-start(bf16[4,1,6,8,512]{4,3,2,0,1:T(8,128)(2,1)} %bitcast_select_fusion.2), channel_id=1, source_target_pairs={{0,1},{1,0},{2,3},{3,2},{4,5},{5,4},{6,7},{7,6},{8,9},{9,8},{10,11... | collective-permute-start | bytes 589832 | tf_op jit(solution)/shard_map/ppermute | solution.py:178
  35.5 3.7 %collective-permute-done.14 = bf16[1,32,3,512]{3,2,1,0:T(4,128)(2,1)S(1)} collective-permute-done((bf16[1,32,3,512]{3,2,1,0:T(4,128)(2,1)S(1)}, bf16[1,32,3,512]{3,2,1,0:T(4,128)(2,1)S(1)}, u32[]{:S(2)}, u32[]{:S(2)}) %collective-permute-start.14) | collective-permute-done | bytes 98336 | tf_op jit(solution)/shard_map/ppermute | solution.py:19
  39.2 0.3 pad_maximum_fusion.2
  39.7 0.4 convolution_convert_fusion
  40.1 0.5 copy-done.1
  40.6 0.4 convolution_convert_fusion.1
  41.0 1.4 %collective-permute-done.13 = bf16[4,1,6,8,512]{4,3,2,0,1:T(8,128)(2,1)} collective-permute-done((bf16[4,1,6,8,512]{4,3,2,0,1:T(8,128)(2,1)}, bf16[4,1,6,8,512]{4,3,2,0,1:T(8,128)(2,1)}, u32[]{:S(2)}, u32[]{:S(2)}) %collective-permute-start.13) | collective-permute-done | bytes 196640 | tf_op jit(solution)/shard_map/ppermute | solution.py:178
  42.4 3.3 %collective-permute-done.12 = bf16[4,1,6,8,512]{4,3,2,0,1:T(8,128)(2,1)} collective-permute-done((bf16[4,1,6,8,512]{4,3,2,0,1:T(8,128)(2,1)}, bf16[4,1,6,8,512]{4,3,2,0,1:T(8,128)(2,1)}, u32[]{:S(2)}, u32[]{:S(2)}) %collective-permute-start.12) | collective-permute-done | bytes 196640 | tf_op jit(solution)/shard_map/ppermute | solution.py:178
  45.7 1.2 %maximum_bitcast_fusion = bf16[4,4,6,8,512]{4,3,2,1,0:T(8,128)(2,1)S(1)} fusion(bf16[1,4,1,6,8,512]{5,4,3,1,2,0:T(8,128)(2,1)} %bitcast.45, bf16[1,4,1,6,8,512]{5,4,3,1,2,0:T(8,128)(2,1)} %bitcast.44, bf16[1,4,1,6,8,512]{5,4,3,1,2,0:T(8,128)(2,1)} %bitcast.43, bf16[1,4,1,6,8,512]{5,4,3,1,2,0:T(8,128)(2,1)S(1)} %bitcast_select_fusion.3), kind=kLoop, calls=%fused_computation.21 | loop fusion | flops 1179648 | bytes 1572864 | tf_op jit(solution)/shard_map/stack | solution.py:180
  46.9 0.6 %gather_fusion.3 = bf16[4,4,6,8,512]{4,3,2,1,0:T(8,128)(2,1)S(1)} fusion(bf16[4,4,6,8,512]{4,3,2,1,0:T(8,128)(2,1)S(1)} %maximum_bitcast_fusion, s32[1024]{0:T(1024)S(1)} %pad_clamp_fusion), kind=kCustom, calls=%fused_computation.3 | custom fusion | bytes 1572880 | tf_op jit(solution)/shard_map/jit(_take)/gather | solution.py:180
  47.6 0.6 %copy.39 = bf16[4,4,1,6,8,512]{5,1,0,4,3,2:T(4,128)(2,1)S(1)} copy(bf16[4,4,1,6,8,512]{5,4,3,0,1,2:T(8,128)(2,1)S(1)} %fusion.13) | data formatting | bytes 1572864 | tf_op jit(solution)/shard_map/transpose | solution.py:182
  48.3 0.2 reshape.206
  48.4 0.2 fusion.45
  48.6 0.4 fusion.46
  49.0 0.3 fusion
  49.5 0.4 copy-done.7
  49.9 0.4 fusion.9
  50.8 0.2 convolution_convert_fusion.3
  51.0 0.2 convolution_convert_fusion.4
  51.2 1.5 %maximum_maximum_fusion.1 = (bf16[640,512]{1,0:T(8,128)(2,1)}, bf16[640,512]{1,0:T(8,128)(2,1)}) fusion(bf16[42,512]{1,0:T(8,128)(2,1)S(1)} %get-tuple-element.27, bf16[448,512]{1,0:T(8,128)(2,1)S(1)} %convolution_convert_fusion, bf16[42,512]{1,0:T(8,128)(2,1)S(1)} %get-tuple-element.26, bf16[640]{0:T(1024)(128)(2,1)S(1)} %pad.7.clone, ...), kind=kLoop, calls=%fused_computation.33 | loop fusion | flops 4915200 | bytes 2401536 | tf_op jit(solution)/shard_map/concatenate | solution.py:133
  52.7 7.0 %shard_map.82 = bf16[256,512]{1,0:T(8,128)(2,1)} custom-call(bf16[256,512]{1,0:T(8,128)(2,1)} %convolution_convert_fusion.2.q_ref, bf16[640,512]{1,0:T(8,128)(2,1)} %get-tuple-element.46.k_ref, bf16[640,512]{1,0:T(8,128)(2,1)} %get-tuple-element.45.v_ref, bf16[32,8,512]{2,1,0:T(8,128)(2,1)} %bitcast.118, bf16[512,512]{1,0:T(8,128)(2,1)} %wo_ref.1), custom_call_target="tpu_custom_call" | custom-call | tf_op jit(solution)/shard_map/pallas_call | solution.py:138
  (84 shorter events, 3.2 us)
Async XLA Ops:
  0.0 39.7 %copy-start = (bf16[512,512]{1,0:T(8,128)(2,1)S(1)}, bf16[512,512]{1,0:T(8,128)(2,1)}, u32[]{:S(2)}) copy-start(bf16[512,512]{1,0:T(8,128)(2,1)} %param.13) | copy-start | bytes 1572868
  0.0 12.6 %copy-start.4 = (s32[1,2,3]{2,1,0:T(2,128)S(1)}, s32[1,2,3]{2,1,0:T(2,128)}, u32[]{:S(2)}) copy-start(s32[1,2,3]{2,1,0:T(2,128)} %param.15) | copy-start | bytes 76
  0.0 13.2 %copy-start.3 = (f32[1,9,32,8]{2,3,1,0:T(8,128)S(1)}, f32[1,9,32,8]{2,3,1,0:T(8,128)}, u32[]{:S(2)}) copy-start(f32[1,9,32,8]{2,3,1,0:T(8,128)} %param.10) | copy-start | bytes 27652
  2.3 12.3 %collective-permute-start.2 = (bf16[1,2,8,512]{3,2,1,0:T(8,128)(2,1)S(1)}, bf16[1,2,8,512]{3,2,1,0:T(8,128)(2,1)S(1)}, u32[]{:S(2)}, u32[]{:S(2)}) collective-permute-start(bf16[1,2,8,512]{3,2,1,0:T(8,128)(2,1)S(1)} %get-tuple-element.44), channel_id=1, source_target_pairs={{0,12},{1,13},{2,14},{3,15},{4,8},{5,9},{6,10},{7,11},{8,4},{9,5},... | collective-permute-start | bytes 49160 | tf_op jit(solution)/shard_map/ppermute | solution.py:178
  7.4 7.1 %collective-permute-start.1 = (bf16[1,2,8,512]{3,2,1,0:T(8,128)(2,1)S(1)}, bf16[1,2,8,512]{3,2,1,0:T(8,128)(2,1)S(1)}, u32[]{:S(2)}, u32[]{:S(2)}) collective-permute-start(bf16[1,2,8,512]{3,2,1,0:T(8,128)(2,1)S(1)} %get-tuple-element.44), channel_id=1, source_target_pairs={{0,8},{1,9},{2,10},{3,11},{4,12},{5,13},{6,14},{7,15},{8,0},{9,1},... | collective-permute-start | bytes 49160 | tf_op jit(solution)/shard_map/ppermute | solution.py:178
  7.4 7.1 %collective-permute-start = (bf16[1,2,8,512]{3,2,1,0:T(8,128)(2,1)S(1)}, bf16[1,2,8,512]{3,2,1,0:T(8,128)(2,1)S(1)}, u32[]{:S(2)}, u32[]{:S(2)}) collective-permute-start(bf16[1,2,8,512]{3,2,1,0:T(8,128)(2,1)S(1)} %get-tuple-element.44), channel_id=1, source_target_pairs={{0,4},{1,5},{2,6},{3,7},{4,0},{5,1},{6,2},{7,3},{8,12},{9,13},{10,... | collective-permute-start | bytes 49160 | tf_op jit(solution)/shard_map/ppermute | solution.py:178
  9.2 7.9 %collective-permute-start.7 = (bf16[1,32,1,512]{3,2,1,0:T(2,128)(2,1)S(1)}, bf16[1,32,1,512]{3,2,1,0:T(2,128)(2,1)S(1)}, u32[]{:S(2)}, u32[]{:S(2)}) collective-permute-start(bf16[1,32,1,512]{3,2,1,0:T(2,128)(2,1)S(1)} %get-tuple-element.25), channel_id=1, source_target_pairs={{1,0},{2,1},{3,2},{4,3},{5,4},{6,5},{7,6},{8,7},{9,8},{10,9},{11,1... | collective-permute-start | bytes 98312 | tf_op jit(solution)/shard_map/ppermute | solution.py:20
  12.6 6.5 %collective-permute-start.6 = (bf16[1,32,1,512]{3,2,1,0:T(2,128)(2,1)S(1)}, bf16[1,32,1,512]{3,2,1,0:T(2,128)(2,1)S(1)}, u32[]{:S(2)}, u32[]{:S(2)}) collective-permute-start(bf16[1,32,1,512]{3,2,1,0:T(2,128)(2,1)S(1)} %get-tuple-element.24), channel_id=1, source_target_pairs={{0,1},{1,2},{2,3},{3,4},{4,5},{5,6},{6,7},{7,8},{8,9},{9,10},{10,1... | collective-permute-start | bytes 98312 | tf_op jit(solution)/shard_map/ppermute | solution.py:19
  13.1 8.4 %copy-start.6 = (pred[2,2]{0,1:T(4,128)(4,1)}, pred[2,2]{0,1:T(4,128)(4,1)S(1)}, u32[]{:S(2)}) copy-start(pred[2,2]{0,1:T(4,128)(4,1)S(1)} %iota_compare_fusion) | copy-start | bytes 16
  13.2 8.4 %copy-start.8 = (pred[2,16]{1,0:T(4,128)(4,1)}, pred[2,16]{1,0:T(4,128)(4,1)S(1)}, u32[]{:S(2)}) copy-start(pred[2,16]{1,0:T(4,128)(4,1)S(1)} %iota_compare_fusion.1) | copy-start | bytes 100
  15.2 4.9 %collective-permute-start.5 = (bf16[4,1,2,8,512]{4,3,2,0,1:T(8,128)(2,1)S(1)}, bf16[4,1,2,8,512]{4,3,2,0,1:T(8,128)(2,1)S(1)}, u32[]{:S(2)}, u32[]{:S(2)}) collective-permute-start(bf16[4,1,2,8,512]{4,3,2,0,1:T(8,128)(2,1)S(1)} %bitcast_select_fusion.4), channel_id=1, source_target_pairs={{0,3},{1,2},{2,1},{3,0},{4,7},{5,6},{6,5},{7,4},{8,11},{9,10},{10,... | collective-permute-start | bytes 196616 | tf_op jit(solution)/shard_map/ppermute | solution.py:178
  15.2 5.2 %collective-permute-start.4 = (bf16[4,1,2,8,512]{4,3,2,0,1:T(8,128)(2,1)S(1)}, bf16[4,1,2,8,512]{4,3,2,0,1:T(8,128)(2,1)S(1)}, u32[]{:S(2)}, u32[]{:S(2)}) collective-permute-start(bf16[4,1,2,8,512]{4,3,2,0,1:T(8,128)(2,1)S(1)} %bitcast_select_fusion.4), channel_id=1, source_target_pairs={{0,2},{1,3},{2,0},{3,1},{4,6},{5,7},{6,4},{7,5},{8,10},{9,11},{10,... | collective-permute-start | bytes 196616 | tf_op jit(solution)/shard_map/ppermute | solution.py:178
  15.4 5.1 %collective-permute-start.3 = (bf16[4,1,2,8,512]{4,3,2,0,1:T(8,128)(2,1)S(1)}, bf16[4,1,2,8,512]{4,3,2,0,1:T(8,128)(2,1)S(1)}, u32[]{:S(2)}, u32[]{:S(2)}) collective-permute-start(bf16[4,1,2,8,512]{4,3,2,0,1:T(8,128)(2,1)S(1)} %bitcast_select_fusion.4), channel_id=1, source_target_pairs={{0,1},{1,0},{2,3},{3,2},{4,5},{5,4},{6,7},{7,6},{8,9},{9,8},{10,11... | collective-permute-start | bytes 196616 | tf_op jit(solution)/shard_map/ppermute | solution.py:178
  23.1 5.8 %copy-start.2 = (bf16[512,512]{1,0:T(8,128)(2,1)S(1)}, bf16[512,512]{1,0:T(8,128)(2,1)}, u32[]{:S(2)}) copy-start(bf16[512,512]{1,0:T(8,128)(2,1)} %param.11) | copy-start | bytes 1572868
  23.1 8.9 %collective-permute-start.10 = (bf16[1,6,8,512]{3,2,1,0:T(8,128)(2,1)S(1)}, bf16[1,6,8,512]{3,2,1,0:T(8,128)(2,1)S(1)}, u32[]{:S(2)}, u32[]{:S(2)}) collective-permute-start(bf16[1,6,8,512]{3,2,1,0:T(8,128)(2,1)S(1)} %get-tuple-element.31), channel_id=1, source_target_pairs={{0,12},{1,13},{2,14},{3,15},{4,8},{5,9},{6,10},{7,11},{8,4},{9,5},... | collective-permute-start | bytes 147464 | tf_op jit(solution)/shard_map/ppermute | solution.py:178
  27.2 5.0 %collective-permute-start.9 = (bf16[1,6,8,512]{3,2,1,0:T(8,128)(2,1)S(1)}, bf16[1,6,8,512]{3,2,1,0:T(8,128)(2,1)S(1)}, u32[]{:S(2)}, u32[]{:S(2)}) collective-permute-start(bf16[1,6,8,512]{3,2,1,0:T(8,128)(2,1)S(1)} %get-tuple-element.31), channel_id=1, source_target_pairs={{0,8},{1,9},{2,10},{3,11},{4,12},{5,13},{6,14},{7,15},{8,0},{9,1},... | collective-permute-start | bytes 147464 | tf_op jit(solution)/shard_map/ppermute | solution.py:178
  27.2 5.0 %collective-permute-start.8 = (bf16[1,6,8,512]{3,2,1,0:T(8,128)(2,1)S(1)}, bf16[1,6,8,512]{3,2,1,0:T(8,128)(2,1)S(1)}, u32[]{:S(2)}, u32[]{:S(2)}) collective-permute-start(bf16[1,6,8,512]{3,2,1,0:T(8,128)(2,1)S(1)} %get-tuple-element.31), channel_id=1, source_target_pairs={{0,4},{1,5},{2,6},{3,7},{4,0},{5,1},{6,2},{7,3},{8,12},{9,13},{10,... | collective-permute-start | bytes 147464 | tf_op jit(solution)/shard_map/ppermute | solution.py:178
  30.0 5.5 %collective-permute-start.15 = (bf16[1,32,3,512]{3,2,1,0:T(4,128)(2,1)S(1)}, bf16[1,32,3,512]{3,2,1,0:T(4,128)(2,1)S(1)}, u32[]{:S(2)}, u32[]{:S(2)}) collective-permute-start(bf16[1,32,3,512]{3,2,1,0:T(4,128)(2,1)S(1)} %get-tuple-element.15), channel_id=1, source_target_pairs={{1,0},{2,1},{3,2},{4,3},{5,4},{6,5},{7,6},{8,7},{9,8},{10,9},{11,1... | collective-permute-start | bytes 294920 | tf_op jit(solution)/shard_map/ppermute | solution.py:20
  32.0 7.2 %collective-permute-start.14 = (bf16[1,32,3,512]{3,2,1,0:T(4,128)(2,1)S(1)}, bf16[1,32,3,512]{3,2,1,0:T(4,128)(2,1)S(1)}, u32[]{:S(2)}, u32[]{:S(2)}) collective-permute-start(bf16[1,32,3,512]{3,2,1,0:T(4,128)(2,1)S(1)} %get-tuple-element.14), channel_id=1, source_target_pairs={{0,1},{1,2},{2,3},{3,4},{4,5},{5,6},{6,7},{7,8},{8,9},{9,10},{10,1... | collective-permute-start | bytes 294920 | tf_op jit(solution)/shard_map/ppermute | solution.py:19
  33.5 8.9 %collective-permute-start.13 = (bf16[4,1,6,8,512]{4,3,2,0,1:T(8,128)(2,1)}, bf16[4,1,6,8,512]{4,3,2,0,1:T(8,128)(2,1)}, u32[]{:S(2)}, u32[]{:S(2)}) collective-permute-start(bf16[4,1,6,8,512]{4,3,2,0,1:T(8,128)(2,1)} %bitcast_select_fusion.2), channel_id=1, source_target_pairs={{0,3},{1,2},{2,1},{3,0},{4,7},{5,6},{6,5},{7,4},{8,11},{9,10},{10,... | collective-permute-start | bytes 589832 | tf_op jit(solution)/shard_map/ppermute | solution.py:178
  34.2 11.4 %collective-permute-start.12 = (bf16[4,1,6,8,512]{4,3,2,0,1:T(8,128)(2,1)}, bf16[4,1,6,8,512]{4,3,2,0,1:T(8,128)(2,1)}, u32[]{:S(2)}, u32[]{:S(2)}) collective-permute-start(bf16[4,1,6,8,512]{4,3,2,0,1:T(8,128)(2,1)} %bitcast_select_fusion.2), channel_id=1, source_target_pairs={{0,2},{1,3},{2,0},{3,1},{4,6},{5,7},{6,4},{7,5},{8,10},{9,11},{10,... | collective-permute-start | bytes 589832 | tf_op jit(solution)/shard_map/ppermute | solution.py:178
  34.5 11.2 %collective-permute-start.11 = (bf16[4,1,6,8,512]{4,3,2,0,1:T(8,128)(2,1)}, bf16[4,1,6,8,512]{4,3,2,0,1:T(8,128)(2,1)}, u32[]{:S(2)}, u32[]{:S(2)}) collective-permute-start(bf16[4,1,6,8,512]{4,3,2,0,1:T(8,128)(2,1)} %bitcast_select_fusion.2), channel_id=1, source_target_pairs={{0,1},{1,0},{2,3},{3,2},{4,5},{5,4},{6,7},{7,6},{8,9},{9,8},{10,11... | collective-permute-start | bytes 589832 | tf_op jit(solution)/shard_map/ppermute | solution.py:178
  39.5 1.0 %copy-start.1 = (bf16[512,512]{1,0:T(8,128)(2,1)S(1)}, bf16[512,512]{1,0:T(8,128)(2,1)}, u32[]{:S(2)}) copy-start(bf16[512,512]{1,0:T(8,128)(2,1)} %param.12) | copy-start | bytes 1572868
  49.3 0.6 %copy-start.7 = (pred[2,2]{0,1:T(4,128)(4,1)S(1)}, pred[2,2]{0,1:T(4,128)(4,1)}, u32[]{:S(2)}) copy-start(pred[2,2]{0,1:T(4,128)(4,1)} %copy-done.6) | copy-start | bytes 16
  49.3 0.6 %copy-start.9 = (pred[2,16]{1,0:T(4,128)(4,1)S(1)}, pred[2,16]{1,0:T(4,128)(4,1)}, u32[]{:S(2)}) copy-start(pred[2,16]{1,0:T(4,128)(4,1)} %copy-done.8) | copy-start | bytes 100
  49.5 0.9 %copy-start.5 = (pred[2]{0:T(512)(128)(4,1)S(1)}, pred[2]{0:T(512)(128)(4,1)}, u32[]{:S(2)}) copy-start(pred[2]{0:T(512)(128)(4,1)} %get-tuple-element.48) | copy-start | bytes 10

commit v15 on v14

--- a/solution.py
+++ b/solution.py
@@ -160,11 +160,11 @@
     return got.astype(edges.dtype)
 
 
-def doubling_gather(block, axis, radix=4):
+def raw_gather(block, axis, radix=4):
     count = lax.axis_size(axis)
+    me = lax.axis_index(axis)
     if count & (count - 1):
-        return lax.all_gather(block, axis, axis=0, tiled=True)
-    me = lax.axis_index(axis)
+        return lax.all_gather(block[None], axis, axis=0, tiled=True), (lambda j: j)
     levels = []
     stride = 1
     while stride < count:
@@ -176,11 +176,32 @@
         got = [held]
         for d in range(1, r):
             got.append(lax.ppermute(held, axis, [(i, i ^ (d * stride)) for i in range(count)]))
-        digit = (me // stride) % r
-        held = jnp.take(jnp.stack(got), digit ^ jnp.arange(r, dtype=jnp.int32), axis=0)
-    depth = len(levels)
-    held = jnp.transpose(held, tuple(reversed(range(depth))) + tuple(range(depth, held.ndim)))
-    return held.reshape((count * block.shape[0],) + block.shape[1:])
+        held = jnp.stack(got)
+
+    def locate(j):
+        gap = j ^ me
+        flat = 0
+        for stride, r in levels:
+            flat = flat * r + (gap // stride) % r
+        return flat
+
+    return held.reshape((count,) + block.shape), locate
+
+
+def fetch_rim(raw, locate, seam_pair, depth):
+    count = raw.shape[0]
+    src, edge, orient = seam_pair[0], seam_pair[1], seam_pair[2]
+
+    def rows_of(j):
+        tile = lax.dynamic_index_in_dim(raw, locate(j), 0, keepdims=False)
+        return lax.dynamic_slice_in_dim(tile, edge * depth, depth, 0)
+
+    rim = jnp.concatenate(
+        [rows_of((src + count - 1) % count)[:, -depth:], rows_of(src), rows_of((src + 1) % count)[:, :depth]],
+        axis=1,
+    )
+    rim = jnp.where(orient % 2 == 1, rim[:, ::-1], rim)
+    return jnp.where(orient // 2 == 1, rim[::-1], rim)
 
 
 def local(latents, norm_gain, metric, w_query, w_key, w_value, w_output, seam_table):
@@ -191,17 +212,17 @@
     seam_rows = seam_table[0]
     widened = padded_2(normed[None], (("blk", 2),), margin)
     rows1 = jnp.stack([normed[0], normed[-1]])
-    got1 = widen_tiles(doubling_gather(rows1[None], "blk"), 1)
-    received = pick_all(seam_rows, got1[:, :, None])
-    padded = place_rims(widened[0], received, seam_rows)
+    raw1, locate1 = raw_gather(rows1, "blk")
+    padded = jnp.concatenate(
+        [fetch_rim(raw1, locate1, seam_rows[0], 1), widened[0], fetch_rim(raw1, locate1, seam_rows[1], 1)],
+        axis=0,
+    )
     smoothed = smooth(padded, metric[0])
     query = project(smoothed, w_query)
     field_wide = padded_2(smoothed[None], (("blk", 2),), RADIUS)
     rows3 = jnp.concatenate([smoothed[:RADIUS], smoothed[-RADIUS:]], axis=0)
-    got3 = widen_tiles(doubling_gather(rows3[None], "blk"), RADIUS)
-    edges3 = jnp.stack([got3[:, :RADIUS], got3[:, RADIUS:]], axis=1)
-    field_got = pick_all(seam_rows, edges3)
-    arrived = orient_rims(field_got, seam_rows)
+    raw3, locate3 = raw_gather(rows3, "blk")
+    arrived = jnp.stack([fetch_rim(raw3, locate3, seam_rows[e], RADIUS) for e in range(2)])
     return attend_and_mix(query, field_wide[0], arrived, w_key, w_value, own_tile, w_output)[None]
 
 

time: 60 us -> 66.9 us (1.11)
  between operations: 0.52 us -> 15 us
  other arithmetic: 11.6 us -> 6.97 us
  starting transfers between devices: 19.6 us -> 23.5 us
  waiting for transfers between devices: 11.6 us -> 8.11 us
  local copies, waits for them, and re-layouts: 6.44 us -> 3.25 us
  matrix products: 2.98 us -> 2.23 us
    ppermute x2, waiting for transfers between devices: 5.61 us -> 0.49 us  [padded_2(): before = lax.ppermute(last, axis, up)]
    ppermute x2, starting transfers between devices: 5.38 us -> 8.86 us  [padded_2(): after = lax.ppermute(first, axis, down)]
    gather x4 -> x0, local copies, waits for them, and re-layouts: 2.27 us -> none  [doubling_gather(): jnp.take(jnp.stack(got), digit ^ jnp.arange(r, dtype=jnp.int32), axis=0)]
    ppermute x12, waiting for transfers between devices: 5.98 us -> 7.62 us  [raw_gather(): lax.ppermute(held, axis, [(i, i ^ d * stride) for i in range(count)])]
    select_n x9 -> x4, other arithmetic: 1.42 us -> 0.11 us  [fetch_rim(): rim = jnp.where(orient % 2 == 1, rim[:, ::-1], rim)]
    another operation x6 -> x9, other arithmetic: 1.31 us -> 0.24 us  [the longest x6 0.2 us: raw_gather(): held = jnp.stack(got)]
    convert_element_type x2, other arithmetic: 2.17 us -> 1.22 us  [normalize(): return (values * factor * norm_gain).astype(jnp.bfloat16)]
    eq x4 -> x0, other arithmetic: 0.86 us -> none  [the longest x1 0.59 us: orient_rims(): flip_across = (orient // 2 == 1)[:, None, None, None]]
  transfers between devices with their start and end apart: 16 -> 16, of which waited for: 7 -> 4; matrix products, arithmetic and copies ran while one was open for 15% -> 7% of each run, Pallas kernels for 0% -> 0%
where the time goes in v15:
time: 66.9 us; the launch traced here: 66 us
  starting transfers between devices  23.5 us (35%)
  between operations  15 us (22%)
  waiting for transfers between devices  8.11 us (12%)
  Pallas kernels  7 us (10%)
  other arithmetic  6.97 us (10%)
  local copies, waits for them, and re-layouts  3.25 us (5%)
  matrix products  2.23 us (3%)
    ppermute x12, starting transfers between devices, raw_gather(): lax.ppermute(held, axis, [(i, i ^ d * stride) for i in range(count)])  14.5 us
    ppermute x2, starting transfers between devices, padded_2(): after = lax.ppermute(first, axis, down)  8.86 us
    ppermute x12, waiting for transfers between devices, raw_gather(): lax.ppermute(held, axis, [(i, i ^ d * stride) for i in range(count)])  7.62 us
    pallas_call x1, Pallas kernels, attend_and_mix(): pl.pallas_call(attention_kernel, out_shape=jax.ShapeDtypeStruct((cells, c...  7 us
    dot_general x5, matrix products, project(): jnp.dot(flat, weight, preferred_element_type=jnp.float32)  2.23 us
    concatenate x1, other arithmetic, both(): return jnp.concatenate([edge[0], mid, edge[1], tail], axis=0)  1.46 us
  transfers between devices with their start and end apart: 16, of which 4 were waited for; matrix products, arithmetic and copies ran while one was open for 7% of the time, Pallas kernels for 0%

profile of v15, /device:TPU:0, one launch (start us, length us, event | category | flops | bytes accessed | tf_op | source)
XLA Modules:
  0.0 66.0 jit_solution(17006038455618793129)
XLA Ops:
  0.0 1.1 %fusion = f32[32,8]{1,0:T(8,128)S(1)} fusion(bf16[1,32,8,512]{3,2,1,0:T(8,128)(2,1)} %param.8), kind=kLoop, calls=%fused_computation.14 | loop fusion | flops 392960 | bytes 263168 | tf_op jit(solution)/shard_map/reduce_sum | solution.py:27
  1.2 1.1 %fusion.2 = bf16[32,8,512]{2,1,0:T(8,128)(2,1)S(1)} fusion(f32[512]{0:T(512)} %param.9, f32[32,8]{1,0:T(8,128)S(1)} %add_rsqrt_fusion, bf16[1,32,8,512]{3,2,1,0:T(8,128)(2,1)} %param.8), kind=kLoop, calls=%fused_computation.16 | loop fusion | flops 524288 | bytes 527360 | tf_op jit(solution)/shard_map/convert_element_type | solution.py:28
  2.3 4.1 %collective-permute-start.1 = (bf16[2,8,512]{2,1,0:T(8,128)(2,1)S(1)}, bf16[2,8,512]{2,1,0:T(8,128)(2,1)S(1)}, u32[]{:S(2)}, u32[]{:S(2)}) collective-permute-start(bf16[2,8,512]{2,1,0:T(8,128)(2,1)S(1)} %get-tuple-element.45), channel_id=1, source_target_pairs={{0,8},{1,9},{2,10},{3,11},{4,12},{5,13},{6,14},{7,15},{8,0},{9,1},... | collective-permute-start | bytes 49160 | tf_op jit(solution)/shard_map/ppermute | solution.py:178
  6.4 1.6 %collective-permute-start = (bf16[2,8,512]{2,1,0:T(8,128)(2,1)S(1)}, bf16[2,8,512]{2,1,0:T(8,128)(2,1)S(1)}, u32[]{:S(2)}, u32[]{:S(2)}) collective-permute-start(bf16[2,8,512]{2,1,0:T(8,128)(2,1)S(1)} %get-tuple-element.45), channel_id=1, source_target_pairs={{0,4},{1,5},{2,6},{3,7},{4,0},{5,1},{6,2},{7,3},{8,12},{9,13},{10,... | collective-permute-start | bytes 49160 | tf_op jit(solution)/shard_map/ppermute | solution.py:178
  8.0 0.1 multiply_convert_fusion
  8.2 0.1 fusion.17
  8.3 4.4 %collective-permute-start.7 = (bf16[1,32,1,512]{3,2,1,0:T(2,128)(2,1)S(1)}, bf16[1,32,1,512]{3,2,1,0:T(2,128)(2,1)S(1)}, u32[]{:S(2)}, u32[]{:S(2)}) collective-permute-start(bf16[1,32,1,512]{3,2,1,0:T(2,128)(2,1)S(1)} %get-tuple-element.24), channel_id=1, source_target_pairs={{1,0},{2,1},{3,2},{4,3},{5,4},{6,5},{7,6},{8,7},{9,8},{10,9},{11,1... | collective-permute-start | bytes 98312 | tf_op jit(solution)/shard_map/ppermute | solution.py:20
  12.8 0.7 fusion.20
  27.9 0.1 copy.18
  28.0 0.1 copy.24
  28.1 0.1 copy.23
  28.1 0.1 copy.22
  28.2 0.1 copy.21
  28.3 0.1 copy.20
  28.4 0.1 copy.19
  28.4 0.1 copy.26
  28.5 0.1 copy.25
  28.6 0.1 pad.7.clone
  28.7 0.1 collective-permute-start.4
  28.9 2.0 %collective-permute-start.5 = (bf16[4,2,8,512]{3,2,1,0:T(8,128)(2,1)S(1)}, bf16[4,2,8,512]{3,2,1,0:T(8,128)(2,1)S(1)}, u32[]{:S(2)}, u32[]{:S(2)}) collective-permute-start(bf16[4,2,8,512]{3,2,1,0:T(8,128)(2,1)S(1)} %get-tuple-element.32), channel_id=1, source_target_pairs={{0,3},{1,2},{2,1},{3,0},{4,7},{5,6},{6,5},{7,4},{8,11},{9,10},{10,... | collective-permute-start | bytes 196616 | tf_op jit(solution)/shard_map/ppermute | solution.py:178
  30.9 0.3 maximum_bitcast_fusion
  31.2 2.3 %collective-permute-done.4 = bf16[4,2,8,512]{3,2,1,0:T(8,128)(2,1)S(1)} collective-permute-done((bf16[4,2,8,512]{3,2,1,0:T(8,128)(2,1)S(1)}, bf16[4,2,8,512]{3,2,1,0:T(8,128)(2,1)S(1)}, u32[]{:S(2)}, u32[]{:S(2)}) %collective-permute-start.4) | collective-permute-done | bytes 65568 | tf_op jit(solution)/shard_map/ppermute | solution.py:178
  33.7 0.1 rev.18
  33.9 0.1 rev.19
  34.1 1.1 %fusion.30 = bf16[1,32,8,512]{3,2,1,0:T(8,128)(2,1)S(1)} fusion(bf16[1,10,512]{2,1,0:T(8,128)(2,1)S(1)} %broadcast_select_fusion.2, bf16[32,10,512]{2,1,0:T(8,128)(2,1)S(1)} %maximum_bitcast_fusion, f32[32,8]{1,0:T(8,128)S(1)} %copy.26, f32[32,8]{1,0:T(8,128)S(1)} %copy.25, f32[32,8]{1,0:T(8,128)S(1)} %copy.24, f32[32,8]{1,0:T(8,128)S(1)} %copy.23, ...), kind=kLoop, calls=%fused_computation.83 | loop fusion | flops 5898240 | bytes 1753088 | tf_op jit(solution)/shard_map/broadcast_in_dim | solution.py:222
  35.2 1.1 %add_convert_fusion = bf16[32,8,512]{2,1,0:T(8,128)(2,1)S(1)} fusion(bf16[32,10,512]{2,1,0:T(8,128)(2,1)S(1)} %maximum_bitcast_fusion, bf16[1,10,512]{2,1,0:T(8,128)(2,1)S(1)} %broadcast_select_fusion.2, bf16[1,10,512]{2,1,0:T(8,128)(2,1)S(1)} %broadcast_select_fusion.3, f32[32,8]{1,0:T(8,128)S(1)} %copy.26, f32[32,8]{1,0:T(8,128)S(1)} %copy.25, ...), kind=kLoop, calls=%fused_computation.19 | loop fusion | flops 5898240 | bytes 1753088 | tf_op jit(solution)/shard_map/convert_element_type | solution.py:69
  36.3 0.8 %collective-permute-start.9 = (bf16[6,8,512]{2,1,0:T(8,128)(2,1)S(1)}, bf16[6,8,512]{2,1,0:T(8,128)(2,1)S(1)}, u32[]{:S(2)}, u32[]{:S(2)}) collective-permute-start(bf16[6,8,512]{2,1,0:T(8,128)(2,1)S(1)} %get-tuple-element.34), channel_id=1, source_target_pairs={{0,8},{1,9},{2,10},{3,11},{4,12},{5,13},{6,14},{7,15},{8,0},{9,1},... | collective-permute-start | bytes 147464 | tf_op jit(solution)/shard_map/ppermute | solution.py:178
  37.1 2.0 %collective-permute-start.8 = (bf16[6,8,512]{2,1,0:T(8,128)(2,1)S(1)}, bf16[6,8,512]{2,1,0:T(8,128)(2,1)S(1)}, u32[]{:S(2)}, u32[]{:S(2)}) collective-permute-start(bf16[6,8,512]{2,1,0:T(8,128)(2,1)S(1)} %get-tuple-element.34), channel_id=1, source_target_pairs={{0,4},{1,5},{2,6},{3,7},{4,0},{5,1},{6,2},{7,3},{8,12},{9,13},{10,... | collective-permute-start | bytes 147464 | tf_op jit(solution)/shard_map/ppermute | solution.py:178
  39.1 1.6 %collective-permute-start.10 = (bf16[6,8,512]{2,1,0:T(8,128)(2,1)S(1)}, bf16[6,8,512]{2,1,0:T(8,128)(2,1)S(1)}, u32[]{:S(2)}, u32[]{:S(2)}) collective-permute-start(bf16[6,8,512]{2,1,0:T(8,128)(2,1)S(1)} %get-tuple-element.34), channel_id=1, source_target_pairs={{0,12},{1,13},{2,14},{3,15},{4,8},{5,9},{6,10},{7,11},{8,4},{9,5},... | collective-permute-start | bytes 147464 | tf_op jit(solution)/shard_map/ppermute | solution.py:178
  40.7 1.0 %convolution_convert_fusion.2.q_ref = bf16[256,512]{1,0:T(8,128)(2,1)} fusion(bf16[512,512]{1,0:T(8,128)(2,1)S(1)} %copy-done.3, bf16[32,8,512]{2,1,0:T(8,128)(2,1)S(1)} %add_convert_fusion), kind=kOutput, calls=%fused_computation.2 | convolution fusion | flops 134348800 | bytes 1048576 | tf_op jit(solution)/shard_map/dot_general | solution.py:76
  41.7 0.1 fusion.14
  41.9 4.4 %collective-permute-start.15 = (bf16[1,32,3,512]{3,2,1,0:T(4,128)(2,1)S(1)}, bf16[1,32,3,512]{3,2,1,0:T(4,128)(2,1)S(1)}, u32[]{:S(2)}, u32[]{:S(2)}) collective-permute-start(bf16[1,32,3,512]{3,2,1,0:T(4,128)(2,1)S(1)} %get-tuple-element.12), channel_id=1, source_target_pairs={{1,0},{2,1},{3,2},{4,3},{5,4},{6,5},{7,6},{8,7},{9,8},{10,9},{11,1... | collective-permute-start | bytes 294920 | tf_op jit(solution)/shard_map/ppermute | solution.py:20
  46.5 2.0 %collective-permute-start.13 = (bf16[4,6,8,512]{3,2,1,0:T(8,128)(2,1)S(1)}, bf16[4,6,8,512]{3,2,1,0:T(8,128)(2,1)S(1)}, u32[]{:S(2)}, u32[]{:S(2)}) collective-permute-start(bf16[4,6,8,512]{3,2,1,0:T(8,128)(2,1)S(1)} %get-tuple-element.26), channel_id=1, source_target_pairs={{0,3},{1,2},{2,1},{3,0},{4,7},{5,6},{6,5},{7,4},{8,11},{9,10},{10,... | collective-permute-start | bytes 589832 | tf_op jit(solution)/shard_map/ppermute | solution.py:178
  48.6 0.5 collective-permute-done.14
  49.1 0.3 pad_maximum_fusion.1
  49.4 0.1 reshape_squeeze.3
  49.5 0.4 convolution_convert_fusion
  49.9 0.6 copy-done.2
  50.5 0.4 convolution_convert_fusion.1
  51.0 3.3 %collective-permute-done.12 = bf16[4,6,8,512]{3,2,1,0:T(8,128)(2,1)S(1)} collective-permute-done((bf16[4,6,8,512]{3,2,1,0:T(8,128)(2,1)S(1)}, bf16[4,6,8,512]{3,2,1,0:T(8,128)(2,1)S(1)}, u32[]{:S(2)}, u32[]{:S(2)}) %collective-permute-start.12) | collective-permute-done | bytes 196640 | tf_op jit(solution)/shard_map/ppermute | solution.py:178
  54.3 1.9 %collective-permute-done.13 = bf16[4,6,8,512]{3,2,1,0:T(8,128)(2,1)S(1)} collective-permute-done((bf16[4,6,8,512]{3,2,1,0:T(8,128)(2,1)S(1)}, bf16[4,6,8,512]{3,2,1,0:T(8,128)(2,1)S(1)}, u32[]{:S(2)}, u32[]{:S(2)}) %collective-permute-start.13) | collective-permute-done | bytes 196640 | tf_op jit(solution)/shard_map/ppermute | solution.py:178
  56.2 0.1 pad_maximum_fusion
  56.5 0.2 rev.20
  56.7 0.2 rev.22
  57.1 0.2 convolution_convert_fusion.3
  57.3 0.2 convolution_convert_fusion.4
  57.5 1.5 %maximum_maximum_fusion.1 = (bf16[640,512]{1,0:T(8,128)(2,1)}, bf16[640,512]{1,0:T(8,128)(2,1)}) fusion(bf16[42,512]{1,0:T(8,128)(2,1)S(1)} %get-tuple-element.28, bf16[448,512]{1,0:T(8,128)(2,1)S(1)} %convolution_convert_fusion, bf16[42,512]{1,0:T(8,128)(2,1)S(1)} %get-tuple-element.27, bf16[640]{0:T(1024)(128)(2,1)S(1)} %pad.7.clone, ...), kind=kLoop, calls=%fused_computation.13 | loop fusion | flops 4915200 | bytes 2401536 | tf_op jit(solution)/shard_map/concatenate | solution.py:133
  59.0 7.0 %shard_map.82 = bf16[256,512]{1,0:T(8,128)(2,1)} custom-call(bf16[256,512]{1,0:T(8,128)(2,1)} %convolution_convert_fusion.2.q_ref, bf16[640,512]{1,0:T(8,128)(2,1)} %get-tuple-element.47.k_ref, bf16[640,512]{1,0:T(8,128)(2,1)} %get-tuple-element.46.v_ref, bf16[32,8,512]{2,1,0:T(8,128)(2,1)} %bitcast.94, bf16[512,512]{1,0:T(8,128)(2,1)} %wo_ref.1), custom_call_target="tpu_custom_call" | custom-call | tf_op jit(solution)/shard_map/pallas_call | solution.py:138
  (64 shorter events, 0.9 us)
Async XLA Ops:
  0.0 49.5 %copy-start = (bf16[512,512]{1,0:T(8,128)(2,1)S(1)}, bf16[512,512]{1,0:T(8,128)(2,1)}, u32[]{:S(2)}) copy-start(bf16[512,512]{1,0:T(8,128)(2,1)} %param.13) | copy-start | bytes 1572868
  0.0 8.0 %copy-start.1 = (bf16[1,32,8,512]{3,2,1,0:T(8,128)(2,1)S(1)}, bf16[1,32,8,512]{3,2,1,0:T(8,128)(2,1)}, u32[]{:S(2)}) copy-start(bf16[1,32,8,512]{3,2,1,0:T(8,128)(2,1)} %param.8) | copy-start | bytes 786436
  0.0 8.0 %copy-start.6 = (f32[512]{0:T(512)S(1)}, f32[512]{0:T(512)}, u32[]{:S(2)}) copy-start(f32[512]{0:T(512)} %param.9) | copy-start | bytes 6148
  1.2 11.6 %copy-start.5 = (s32[1,2,3]{2,1,0:T(2,128)S(1)}, s32[1,2,3]{2,1,0:T(2,128)}, u32[]{:S(2)}) copy-start(s32[1,2,3]{2,1,0:T(2,128)} %param.15) | copy-start | bytes 76
  1.2 12.9 %copy-start.4 = (f32[1,9,32,8]{2,3,1,0:T(8,128)S(1)}, f32[1,9,32,8]{2,3,1,0:T(8,128)}, u32[]{:S(2)}) copy-start(f32[1,9,32,8]{2,3,1,0:T(8,128)} %param.10) | copy-start | bytes 27652
  2.3 26.4 %collective-permute-start.1 = (bf16[2,8,512]{2,1,0:T(8,128)(2,1)S(1)}, bf16[2,8,512]{2,1,0:T(8,128)(2,1)S(1)}, u32[]{:S(2)}, u32[]{:S(2)}) collective-permute-start(bf16[2,8,512]{2,1,0:T(8,128)(2,1)S(1)} %get-tuple-element.45), channel_id=1, source_target_pairs={{0,8},{1,9},{2,10},{3,11},{4,12},{5,13},{6,14},{7,15},{8,0},{9,1},... | collective-permute-start | bytes 49160 | tf_op jit(solution)/shard_map/ppermute | solution.py:178
  6.4 22.2 %collective-permute-start = (bf16[2,8,512]{2,1,0:T(8,128)(2,1)S(1)}, bf16[2,8,512]{2,1,0:T(8,128)(2,1)S(1)}, u32[]{:S(2)}, u32[]{:S(2)}) collective-permute-start(bf16[2,8,512]{2,1,0:T(8,128)(2,1)S(1)} %get-tuple-element.45), channel_id=1, source_target_pairs={{0,4},{1,5},{2,6},{3,7},{4,0},{5,1},{6,2},{7,3},{8,12},{9,13},{10,... | collective-permute-start | bytes 49160 | tf_op jit(solution)/shard_map/ppermute | solution.py:178
  8.0 20.7 %collective-permute-start.2 = (bf16[2,8,512]{2,1,0:T(8,128)(2,1)S(1)}, bf16[2,8,512]{2,1,0:T(8,128)(2,1)S(1)}, u32[]{:S(2)}, u32[]{:S(2)}) collective-permute-start(bf16[2,8,512]{2,1,0:T(8,128)(2,1)S(1)} %get-tuple-element.45), channel_id=1, source_target_pairs={{0,12},{1,13},{2,14},{3,15},{4,8},{5,9},{6,10},{7,11},{8,4},{9,5},... | collective-permute-start | bytes 49160 | tf_op jit(solution)/shard_map/ppermute | solution.py:178
  8.3 22.7 %collective-permute-start.6 = (bf16[1,32,1,512]{3,2,1,0:T(2,128)(2,1)S(1)}, bf16[1,32,1,512]{3,2,1,0:T(2,128)(2,1)S(1)}, u32[]{:S(2)}, u32[]{:S(2)}) collective-permute-start(bf16[1,32,1,512]{3,2,1,0:T(2,128)(2,1)S(1)} %get-tuple-element.23), channel_id=1, source_target_pairs={{0,1},{1,2},{2,3},{3,4},{4,5},{5,6},{6,7},{7,8},{8,9},{9,10},{10,1... | collective-permute-start | bytes 98312 | tf_op jit(solution)/shard_map/ppermute | solution.py:19
  8.3 22.6 %collective-permute-start.7 = (bf16[1,32,1,512]{3,2,1,0:T(2,128)(2,1)S(1)}, bf16[1,32,1,512]{3,2,1,0:T(2,128)(2,1)S(1)}, u32[]{:S(2)}, u32[]{:S(2)}) collective-permute-start(bf16[1,32,1,512]{3,2,1,0:T(2,128)(2,1)S(1)} %get-tuple-element.24), channel_id=1, source_target_pairs={{1,0},{2,1},{3,2},{4,3},{5,4},{6,5},{7,6},{8,7},{9,8},{10,9},{11,1... | collective-permute-start | bytes 98312 | tf_op jit(solution)/shard_map/ppermute | solution.py:20
  28.7 4.9 %collective-permute-start.4 = (bf16[4,2,8,512]{3,2,1,0:T(8,128)(2,1)S(1)}, bf16[4,2,8,512]{3,2,1,0:T(8,128)(2,1)S(1)}, u32[]{:S(2)}, u32[]{:S(2)}) collective-permute-start(bf16[4,2,8,512]{3,2,1,0:T(8,128)(2,1)S(1)} %get-tuple-element.32), channel_id=1, source_target_pairs={{0,2},{1,3},{2,0},{3,1},{4,6},{5,7},{6,4},{7,5},{8,10},{9,11},{10,... | collective-permute-start | bytes 196616 | tf_op jit(solution)/shard_map/ppermute | solution.py:178
  28.8 4.8 %collective-permute-start.3 = (bf16[4,2,8,512]{3,2,1,0:T(8,128)(2,1)S(1)}, bf16[4,2,8,512]{3,2,1,0:T(8,128)(2,1)S(1)}, u32[]{:S(2)}, u32[]{:S(2)}) collective-permute-start(bf16[4,2,8,512]{3,2,1,0:T(8,128)(2,1)S(1)} %get-tuple-element.32), channel_id=1, source_target_pairs={{0,1},{1,0},{2,3},{3,2},{4,5},{5,4},{6,7},{7,6},{8,9},{9,8},{10,11... | collective-permute-start | bytes 196616 | tf_op jit(solution)/shard_map/ppermute | solution.py:178
  28.9 4.7 %collective-permute-start.5 = (bf16[4,2,8,512]{3,2,1,0:T(8,128)(2,1)S(1)}, bf16[4,2,8,512]{3,2,1,0:T(8,128)(2,1)S(1)}, u32[]{:S(2)}, u32[]{:S(2)}) collective-permute-start(bf16[4,2,8,512]{3,2,1,0:T(8,128)(2,1)S(1)} %get-tuple-element.32), channel_id=1, source_target_pairs={{0,3},{1,2},{2,1},{3,0},{4,7},{5,6},{6,5},{7,4},{8,11},{9,10},{10,... | collective-permute-start | bytes 196616 | tf_op jit(solution)/shard_map/ppermute | solution.py:178
  35.2 5.6 %copy-start.3 = (bf16[512,512]{1,0:T(8,128)(2,1)S(1)}, bf16[512,512]{1,0:T(8,128)(2,1)}, u32[]{:S(2)}) copy-start(bf16[512,512]{1,0:T(8,128)(2,1)} %param.11) | copy-start | bytes 1572868
  36.3 10.1 %collective-permute-start.9 = (bf16[6,8,512]{2,1,0:T(8,128)(2,1)S(1)}, bf16[6,8,512]{2,1,0:T(8,128)(2,1)S(1)}, u32[]{:S(2)}, u32[]{:S(2)}) collective-permute-start(bf16[6,8,512]{2,1,0:T(8,128)(2,1)S(1)} %get-tuple-element.34), channel_id=1, source_target_pairs={{0,8},{1,9},{2,10},{3,11},{4,12},{5,13},{6,14},{7,15},{8,0},{9,1},... | collective-permute-start | bytes 147464 | tf_op jit(solution)/shard_map/ppermute | solution.py:178
  37.1 9.2 %collective-permute-start.8 = (bf16[6,8,512]{2,1,0:T(8,128)(2,1)S(1)}, bf16[6,8,512]{2,1,0:T(8,128)(2,1)S(1)}, u32[]{:S(2)}, u32[]{:S(2)}) collective-permute-start(bf16[6,8,512]{2,1,0:T(8,128)(2,1)S(1)} %get-tuple-element.34), channel_id=1, source_target_pairs={{0,4},{1,5},{2,6},{3,7},{4,0},{5,1},{6,2},{7,3},{8,12},{9,13},{10,... | collective-permute-start | bytes 147464 | tf_op jit(solution)/shard_map/ppermute | solution.py:178
  39.1 7.2 %collective-permute-start.10 = (bf16[6,8,512]{2,1,0:T(8,128)(2,1)S(1)}, bf16[6,8,512]{2,1,0:T(8,128)(2,1)S(1)}, u32[]{:S(2)}, u32[]{:S(2)}) collective-permute-start(bf16[6,8,512]{2,1,0:T(8,128)(2,1)S(1)} %get-tuple-element.34), channel_id=1, source_target_pairs={{0,12},{1,13},{2,14},{3,15},{4,8},{5,9},{6,10},{7,11},{8,4},{9,5},... | collective-permute-start | bytes 147464 | tf_op jit(solution)/shard_map/ppermute | solution.py:178
  41.8 7.2 %collective-permute-start.14 = (bf16[1,32,3,512]{3,2,1,0:T(4,128)(2,1)S(1)}, bf16[1,32,3,512]{3,2,1,0:T(4,128)(2,1)S(1)}, u32[]{:S(2)}, u32[]{:S(2)}) collective-permute-start(bf16[1,32,3,512]{3,2,1,0:T(4,128)(2,1)S(1)} %get-tuple-element.11), channel_id=1, source_target_pairs={{0,1},{1,2},{2,3},{3,4},{4,5},{5,6},{6,7},{7,8},{8,9},{9,10},{10,1... | collective-permute-start | bytes 294920 | tf_op jit(solution)/shard_map/ppermute | solution.py:19
  41.9 7.2 %collective-permute-start.15 = (bf16[1,32,3,512]{3,2,1,0:T(4,128)(2,1)S(1)}, bf16[1,32,3,512]{3,2,1,0:T(4,128)(2,1)S(1)}, u32[]{:S(2)}, u32[]{:S(2)}) collective-permute-start(bf16[1,32,3,512]{3,2,1,0:T(4,128)(2,1)S(1)} %get-tuple-element.12), channel_id=1, source_target_pairs={{1,0},{2,1},{3,2},{4,3},{5,4},{6,5},{7,6},{8,7},{9,8},{10,9},{11,1... | collective-permute-start | bytes 294920 | tf_op jit(solution)/shard_map/ppermute | solution.py:20
  46.4 7.9 %collective-permute-start.12 = (bf16[4,6,8,512]{3,2,1,0:T(8,128)(2,1)S(1)}, bf16[4,6,8,512]{3,2,1,0:T(8,128)(2,1)S(1)}, u32[]{:S(2)}, u32[]{:S(2)}) collective-permute-start(bf16[4,6,8,512]{3,2,1,0:T(8,128)(2,1)S(1)} %get-tuple-element.26), channel_id=1, source_target_pairs={{0,2},{1,3},{2,0},{3,1},{4,6},{5,7},{6,4},{7,5},{8,10},{9,11},{10,... | collective-permute-start | bytes 589832 | tf_op jit(solution)/shard_map/ppermute | solution.py:178
  46.4 7.8 %collective-permute-start.11 = (bf16[4,6,8,512]{3,2,1,0:T(8,128)(2,1)S(1)}, bf16[4,6,8,512]{3,2,1,0:T(8,128)(2,1)S(1)}, u32[]{:S(2)}, u32[]{:S(2)}) collective-permute-start(bf16[4,6,8,512]{3,2,1,0:T(8,128)(2,1)S(1)} %get-tuple-element.26), channel_id=1, source_target_pairs={{0,1},{1,0},{2,3},{3,2},{4,5},{5,4},{6,7},{7,6},{8,9},{9,8},{10,11... | collective-permute-start | bytes 589832 | tf_op jit(solution)/shard_map/ppermute | solution.py:178
  46.5 9.7 %collective-permute-start.13 = (bf16[4,6,8,512]{3,2,1,0:T(8,128)(2,1)S(1)}, bf16[4,6,8,512]{3,2,1,0:T(8,128)(2,1)S(1)}, u32[]{:S(2)}, u32[]{:S(2)}) collective-permute-start(bf16[4,6,8,512]{3,2,1,0:T(8,128)(2,1)S(1)} %get-tuple-element.26), channel_id=1, source_target_pairs={{0,3},{1,2},{2,1},{3,0},{4,7},{5,6},{6,5},{7,4},{8,11},{9,10},{10,... | collective-permute-start | bytes 589832 | tf_op jit(solution)/shard_map/ppermute | solution.py:178
  49.5 1.0 %copy-start.2 = (bf16[512,512]{1,0:T(8,128)(2,1)S(1)}, bf16[512,512]{1,0:T(8,128)(2,1)}, u32[]{:S(2)}) copy-start(bf16[512,512]{1,0:T(8,128)(2,1)} %param.12) | copy-start | bytes 1572868

commit v16 on v15

--- a/solution.py
+++ b/solution.py
@@ -160,6 +160,29 @@
     return got.astype(edges.dtype)
 
 
+def doubling_gather(block, axis, radix=4):
+    count = lax.axis_size(axis)
+    if count & (count - 1):
+        return lax.all_gather(block, axis, axis=0, tiled=True)
+    me = lax.axis_index(axis)
+    levels = []
+    stride = 1
+    while stride < count:
+        r = min(radix, count // stride)
+        levels.append((stride, r))
+        stride *= r
+    held = block
+    for stride, r in reversed(levels):
+        got = [held]
+        for d in range(1, r):
+            got.append(lax.ppermute(held, axis, [(i, i ^ (d * stride)) for i in range(count)]))
+        digit = (me // stride) % r
+        held = jnp.take(jnp.stack(got), digit ^ jnp.arange(r, dtype=jnp.int32), axis=0)
+    depth = len(levels)
+    held = jnp.transpose(held, tuple(reversed(range(depth))) + tuple(range(depth, held.ndim)))
+    return held.reshape((count * block.shape[0],) + block.shape[1:])
+
+
 def raw_gather(block, axis, radix=4):
     count = lax.axis_size(axis)
     me = lax.axis_index(axis)
@@ -212,11 +235,9 @@
     seam_rows = seam_table[0]
     widened = padded_2(normed[None], (("blk", 2),), margin)
     rows1 = jnp.stack([normed[0], normed[-1]])
-    raw1, locate1 = raw_gather(rows1, "blk")
-    padded = jnp.concatenate(
-        [fetch_rim(raw1, locate1, seam_rows[0], 1), widened[0], fetch_rim(raw1, locate1, seam_rows[1], 1)],
-        axis=0,
-    )
+    got1 = widen_tiles(doubling_gather(rows1[None], "blk"), 1)
+    received = pick_all(seam_rows, got1[:, :, None])
+    padded = place_rims(widened[0], received, seam_rows)
     smoothed = smooth(padded, metric[0])
     query = project(smoothed, w_query)
     field_wide = padded_2(smoothed[None], (("blk", 2),), RADIUS)

time: 66.9 us -> 64.4 us (0.963)
  the two profiles are of different devices: /device:TPU:0 before, /device:TPU:1 now
where the time goes in v16:
time: 64.4 us; the launch traced here: 64 us
  starting transfers between devices  22 us (34%)
  between operations  11 us (17%)
  waiting for transfers between devices  9.54 us (15%)
  other arithmetic  7.37 us (11%)
  Pallas kernels  7 us (11%)
  local copies, waits for them, and re-layouts  4.6 us (7%)
  matrix products  2.54 us (4%)
    ppermute x6, starting transfers between devices, doubling_gather(): lax.ppermute(held, axis, [(i, i ^ d * stride) for i in range(count)])  9.11 us
    ppermute x6, starting transfers between devices, raw_gather(): lax.ppermute(held, axis, [(i, i ^ d * stride) for i in range(count)])  9.01 us
    pallas_call x1, Pallas kernels, attend_and_mix(): pl.pallas_call(attention_kernel, out_shape=jax.ShapeDtypeStruct((cells, c...  7 us
    ppermute x6, waiting for transfers between devices, raw_gather(): lax.ppermute(held, axis, [(i, i ^ d * stride) for i in range(count)])  6.1 us
    ppermute x2, starting transfers between devices, padded_2(): before = lax.ppermute(last, axis, up)  3.64 us
    ppermute x6, waiting for transfers between devices, doubling_gather(): lax.ppermute(held, axis, [(i, i ^ d * stride) for i in range(count)])  2.94 us
    dot_general x5, matrix products, project(): jnp.dot(flat, weight, preferred_element_type=jnp.float32)  2.23 us
    concatenate x1, other arithmetic, both(): return jnp.concatenate([edge[0], mid, edge[1], tail], axis=0)  1.46 us
  transfers between devices with their start and end apart: 16, of which 4 were waited for; matrix products, arithmetic and copies ran while one was open for 8% of the time, Pallas kernels for 0%

profile of v16, /device:TPU:1, one launch (start us, length us, event | category | flops | bytes accessed | tf_op | source)
XLA Modules:
  0.0 64.0 jit_solution(9623605269366622237)
XLA Ops:
  0.0 1.2 %fusion.1 = f32[32,8]{1,0:T(8,128)S(1)} fusion(bf16[1,32,8,512]{3,2,1,0:T(8,128)(2,1)} %param.8), kind=kLoop, calls=%fused_computation.18 | loop fusion | flops 392960 | bytes 263168 | tf_op jit(solution)/shard_map/reduce_sum | solution.py:27
  1.2 1.1 %fusion.3 = bf16[32,8,512]{2,1,0:T(8,128)(2,1)S(1)} fusion(f32[512]{0:T(512)} %param.9, f32[32,8]{1,0:T(8,128)S(1)} %add_rsqrt_fusion, bf16[1,32,8,512]{3,2,1,0:T(8,128)(2,1)} %param.8), kind=kLoop, calls=%fused_computation.20 | loop fusion | flops 524288 | bytes 527360 | tf_op jit(solution)/shard_map/convert_element_type | solution.py:28
  2.3 4.2 %collective-permute-start.2 = (bf16[1,2,8,512]{3,2,1,0:T(8,128)(2,1)S(1)}, bf16[1,2,8,512]{3,2,1,0:T(8,128)(2,1)S(1)}, u32[]{:S(2)}, u32[]{:S(2)}) collective-permute-start(bf16[1,2,8,512]{3,2,1,0:T(8,128)(2,1)S(1)} %get-tuple-element.46), channel_id=1, source_target_pairs={{0,12},{1,13},{2,14},{3,15},{4,8},{5,9},{6,10},{7,11},{8,4},{9,5},... | collective-permute-start | bytes 49160 | tf_op jit(solution)/shard_map/ppermute | solution.py:178
  6.6 0.4 collective-permute-start
  6.9 0.1 multiply_convert_fusion
  7.1 0.1 fusion.37
  7.2 2.6 %collective-permute-start.6 = (bf16[1,32,1,512]{3,2,1,0:T(2,128)(2,1)S(1)}, bf16[1,32,1,512]{3,2,1,0:T(2,128)(2,1)S(1)}, u32[]{:S(2)}, u32[]{:S(2)}) collective-permute-start(bf16[1,32,1,512]{3,2,1,0:T(2,128)(2,1)S(1)} %get-tuple-element.24), channel_id=1, source_target_pairs={{0,1},{1,2},{2,3},{3,4},{4,5},{5,6},{6,7},{7,8},{8,9},{9,10},{10,1... | collective-permute-start | bytes 98312 | tf_op jit(solution)/shard_map/ppermute | solution.py:19
  9.7 0.7 %fusion.41 = (s32[1,1,1]{2,1,0:T(1,128)}, s32[1,1,1]{2,1,0:T(1,128)}, s32[1,1,1]{2,1,0:T(1,128)}, s32[1,1,1]{2,1,0:T(1,128)}, s32[1,1,1]{2,1,0:T(1,128)}, /*index=5*/s32[1,1,1]{2,1,0:T(1,128)}) fusion(s32[1,2,3]{2,1,0:T(2,128)S(1)} %copy-done.4), kind=kLoop, calls=%fused_computation.116 | loop fusion | bytes 48 | tf_op jit(solution)/shard_map/slice | solution.py:216
  11.1 0.2 slice_reduce_fusion.2
  21.9 0.1 pad.7.clone
  22.1 0.6 gather_fusion
  22.6 0.1 bitcast_select_fusion.1
  22.7 0.1 bitcast_select_fusion.2
  22.8 1.7 %collective-permute-start.5 = (bf16[4,1,2,8,512]{4,3,2,0,1:T(8,128)(2,1)S(1)}, bf16[4,1,2,8,512]{4,3,2,0,1:T(8,128)(2,1)S(1)}, u32[]{:S(2)}, u32[]{:S(2)}) collective-permute-start(bf16[4,1,2,8,512]{4,3,2,0,1:T(8,128)(2,1)S(1)} %bitcast_select_fusion.1), channel_id=1, source_target_pairs={{0,3},{1,2},{2,1},{3,0},{4,7},{5,6},{6,5},{7,4},{8,11},{9,10},{10,... | collective-permute-start | bytes 196616 | tf_op jit(solution)/shard_map/ppermute | solution.py:178
  24.5 2.8 %collective-permute-start.4 = (bf16[4,1,2,8,512]{4,3,2,0,1:T(8,128)(2,1)S(1)}, bf16[4,1,2,8,512]{4,3,2,0,1:T(8,128)(2,1)S(1)}, u32[]{:S(2)}, u32[]{:S(2)}) collective-permute-start(bf16[4,1,2,8,512]{4,3,2,0,1:T(8,128)(2,1)S(1)} %bitcast_select_fusion.1), channel_id=1, source_target_pairs={{0,2},{1,3},{2,0},{3,1},{4,6},{5,7},{6,4},{7,5},{8,10},{9,11},{10,... | collective-permute-start | bytes 196616 | tf_op jit(solution)/shard_map/ppermute | solution.py:178
  27.3 0.3 maximum_bitcast_fusion
  27.6 2.9 %collective-permute-done.4 = bf16[4,1,2,8,512]{4,3,2,0,1:T(8,128)(2,1)S(1)} collective-permute-done((bf16[4,1,2,8,512]{4,3,2,0,1:T(8,128)(2,1)S(1)}, bf16[4,1,2,8,512]{4,3,2,0,1:T(8,128)(2,1)S(1)}, u32[]{:S(2)}, u32[]{:S(2)}) %collective-permute-start.4) | collective-permute-done | bytes 65568 | tf_op jit(solution)/shard_map/ppermute | solution.py:178
  30.6 0.6 gather_fusion.1
  31.2 0.1 fusion.16
  31.3 0.2 copy.22
  31.6 0.3 fusion
  31.9 0.1 broadcast_select_fusion.2
  32.1 1.1 %fusion.51 = bf16[1,32,8,512]{3,2,1,0:T(8,128)(2,1)S(1)} fusion(bf16[1,10,512]{2,1,0:T(8,128)(2,1)S(1)} %copy.34, bf16[32,10,512]{2,1,0:T(8,128)(2,1)S(1)} %maximum_bitcast_fusion, f32[32,8]{1,0:T(8,128)S(1)} %copy.36, f32[32,8]{1,0:T(8,128)S(1)} %copy.35, f32[32,8]{1,0:T(8,128)S(1)} %copy.33, f32[32,8]{1,0:T(8,128)S(1)} %copy.32, f32[32,8]{1,0:T(8,128)S(1)} %copy.31, ...), kind=kLoop, calls=%fused_computation.117 | loop fusion | flops 5898240 | bytes 1753088 | tf_op jit(solution)/shard_map/broadcast_in_dim | solution.py:243
  33.1 1.1 %add_convert_fusion = bf16[32,8,512]{2,1,0:T(8,128)(2,1)S(1)} fusion(bf16[32,10,512]{2,1,0:T(8,128)(2,1)S(1)} %maximum_bitcast_fusion, bf16[1,10,512]{2,1,0:T(8,128)(2,1)S(1)} %copy.34, bf16[1,10,512]{2,1,0:T(8,128)(2,1)S(1)} %copy.27, f32[32,8]{1,0:T(8,128)S(1)} %copy.36, f32[32,8]{1,0:T(8,128)S(1)} %copy.35, f32[32,8]{1,0:T(8,128)S(1)} %copy.33, ...), kind=kLoop, calls=%fused_computation.23 | loop fusion | flops 5898240 | bytes 1753088 | tf_op jit(solution)/shard_map/convert_element_type | solution.py:69
  34.3 1.9 %collective-permute-start.8 = (bf16[6,8,512]{2,1,0:T(8,128)(2,1)S(1)}, bf16[6,8,512]{2,1,0:T(8,128)(2,1)S(1)}, u32[]{:S(2)}, u32[]{:S(2)}) collective-permute-start(bf16[6,8,512]{2,1,0:T(8,128)(2,1)S(1)} %get-tuple-element.33), channel_id=1, source_target_pairs={{0,4},{1,5},{2,6},{3,7},{4,0},{5,1},{6,2},{7,3},{8,12},{9,13},{10,... | collective-permute-start | bytes 147464 | tf_op jit(solution)/shard_map/ppermute | solution.py:201
  36.2 1.6 %collective-permute-start.10 = (bf16[6,8,512]{2,1,0:T(8,128)(2,1)S(1)}, bf16[6,8,512]{2,1,0:T(8,128)(2,1)S(1)}, u32[]{:S(2)}, u32[]{:S(2)}) collective-permute-start(bf16[6,8,512]{2,1,0:T(8,128)(2,1)S(1)} %get-tuple-element.33), channel_id=1, source_target_pairs={{0,12},{1,13},{2,14},{3,15},{4,8},{5,9},{6,10},{7,11},{8,4},{9,5},... | collective-permute-start | bytes 147464 | tf_op jit(solution)/shard_map/ppermute | solution.py:201
  37.8 1.0 %convolution_convert_fusion.2.q_ref = bf16[256,512]{1,0:T(8,128)(2,1)} fusion(bf16[512,512]{1,0:T(8,128)(2,1)S(1)} %copy-done.3, bf16[32,8,512]{2,1,0:T(8,128)(2,1)S(1)} %add_convert_fusion), kind=kOutput, calls=%fused_computation.4 | convolution fusion | flops 134348800 | bytes 1048576 | tf_op jit(solution)/shard_map/dot_general | solution.py:76
  38.9 0.1 fusion.32
  38.9 1.1 %collective-permute-start.14 = (bf16[1,32,3,512]{3,2,1,0:T(4,128)(2,1)S(1)}, bf16[1,32,3,512]{3,2,1,0:T(4,128)(2,1)S(1)}, u32[]{:S(2)}, u32[]{:S(2)}) collective-permute-start(bf16[1,32,3,512]{3,2,1,0:T(4,128)(2,1)S(1)} %get-tuple-element.14), channel_id=1, source_target_pairs={{0,1},{1,2},{2,3},{3,4},{4,5},{5,6},{6,7},{7,8},{8,9},{9,10},{10,1... | collective-permute-start | bytes 294920 | tf_op jit(solution)/shard_map/ppermute | solution.py:19
  40.0 0.3 collective-permute-start.15
  40.3 0.7 %collective-permute-done.10 = bf16[6,8,512]{2,1,0:T(8,128)(2,1)S(1)} collective-permute-done((bf16[6,8,512]{2,1,0:T(8,128)(2,1)S(1)}, bf16[6,8,512]{2,1,0:T(8,128)(2,1)S(1)}, u32[]{:S(2)}, u32[]{:S(2)}) %collective-permute-start.10) | collective-permute-done | bytes 49184 | tf_op jit(solution)/shard_map/ppermute | solution.py:201
  41.0 1.1 %collective-permute-start.12 = (bf16[4,6,8,512]{3,2,1,0:T(8,128)(2,1)S(1)}, bf16[4,6,8,512]{3,2,1,0:T(8,128)(2,1)S(1)}, u32[]{:S(2)}, u32[]{:S(2)}) collective-permute-start(bf16[4,6,8,512]{3,2,1,0:T(8,128)(2,1)S(1)} %get-tuple-element.27), channel_id=1, source_target_pairs={{0,2},{1,3},{2,0},{3,1},{4,6},{5,7},{6,4},{7,5},{8,10},{9,11},{10,... | collective-permute-start | bytes 589832 | tf_op jit(solution)/shard_map/ppermute | solution.py:201
  42.1 2.7 %collective-permute-start.11 = (bf16[4,6,8,512]{3,2,1,0:T(8,128)(2,1)S(1)}, bf16[4,6,8,512]{3,2,1,0:T(8,128)(2,1)S(1)}, u32[]{:S(2)}, u32[]{:S(2)}) collective-permute-start(bf16[4,6,8,512]{3,2,1,0:T(8,128)(2,1)S(1)} %get-tuple-element.27), channel_id=1, source_target_pairs={{0,1},{1,0},{2,3},{3,2},{4,5},{5,4},{6,7},{7,6},{8,9},{9,8},{10,11... | collective-permute-start | bytes 589832 | tf_op jit(solution)/shard_map/ppermute | solution.py:201
  44.9 1.6 %collective-permute-start.13 = (bf16[4,6,8,512]{3,2,1,0:T(8,128)(2,1)S(1)}, bf16[4,6,8,512]{3,2,1,0:T(8,128)(2,1)S(1)}, u32[]{:S(2)}, u32[]{:S(2)}) collective-permute-start(bf16[4,6,8,512]{3,2,1,0:T(8,128)(2,1)S(1)} %get-tuple-element.27), channel_id=1, source_target_pairs={{0,3},{1,2},{2,1},{3,0},{4,7},{5,6},{6,5},{7,4},{8,11},{9,10},{10,... | collective-permute-start | bytes 589832 | tf_op jit(solution)/shard_map/ppermute | solution.py:201
  46.4 0.5 collective-permute-done.15
  46.9 0.3 pad_maximum_fusion.1
  47.2 0.1 reshape_squeeze.3
  47.4 0.4 convolution_convert_fusion
  47.8 0.6 copy-done.2
  48.4 0.4 convolution_convert_fusion.1
  48.8 5.4 %collective-permute-done.13 = bf16[4,6,8,512]{3,2,1,0:T(8,128)(2,1)S(1)} collective-permute-done((bf16[4,6,8,512]{3,2,1,0:T(8,128)(2,1)S(1)}, bf16[4,6,8,512]{3,2,1,0:T(8,128)(2,1)S(1)}, u32[]{:S(2)}, u32[]{:S(2)}) %collective-permute-start.13) | collective-permute-done | bytes 196640 | tf_op jit(solution)/shard_map/ppermute | solution.py:201
  54.2 0.1 pad_maximum_fusion
  54.5 0.2 rev.13
  54.7 0.2 rev.15
  55.1 0.2 convolution_convert_fusion.3
  55.3 0.2 convolution_convert_fusion.4
  55.6 1.5 %maximum_maximum_fusion.1 = (bf16[640,512]{1,0:T(8,128)(2,1)}, bf16[640,512]{1,0:T(8,128)(2,1)}) fusion(bf16[42,512]{1,0:T(8,128)(2,1)S(1)} %get-tuple-element.29, bf16[448,512]{1,0:T(8,128)(2,1)S(1)} %convolution_convert_fusion, bf16[42,512]{1,0:T(8,128)(2,1)S(1)} %get-tuple-element.28, bf16[640]{0:T(1024)(128)(2,1)S(1)} %pad.7.clone, ...), kind=kLoop, calls=%fused_computation.17 | loop fusion | flops 4915200 | bytes 2401536 | tf_op jit(solution)/shard_map/concatenate | solution.py:133
  57.0 7.0 %shard_map.82 = bf16[256,512]{1,0:T(8,128)(2,1)} custom-call(bf16[256,512]{1,0:T(8,128)(2,1)} %convolution_convert_fusion.2.q_ref, bf16[640,512]{1,0:T(8,128)(2,1)} %get-tuple-element.48.k_ref, bf16[640,512]{1,0:T(8,128)(2,1)} %get-tuple-element.47.v_ref, bf16[32,8,512]{2,1,0:T(8,128)(2,1)} %bitcast.109, bf16[512,512]{1,0:T(8,128)(2,1)} %wo_ref.1), custom_call_target="tpu_custom_call" | custom-call | tf_op jit(solution)/shard_map/pallas_call | solution.py:138
  (77 shorter events, 1.6 us)
Async XLA Ops:
  0.0 47.4 %copy-start = (bf16[512,512]{1,0:T(8,128)(2,1)S(1)}, bf16[512,512]{1,0:T(8,128)(2,1)}, u32[]{:S(2)}) copy-start(bf16[512,512]{1,0:T(8,128)(2,1)} %param.13) | copy-start | bytes 1572868
  0.0 6.9 %copy-start.1 = (bf16[1,32,8,512]{3,2,1,0:T(8,128)(2,1)S(1)}, bf16[1,32,8,512]{3,2,1,0:T(8,128)(2,1)}, u32[]{:S(2)}) copy-start(bf16[1,32,8,512]{3,2,1,0:T(8,128)(2,1)} %param.8) | copy-start | bytes 786436
  0.0 6.9 %copy-start.6 = (f32[512]{0:T(512)S(1)}, f32[512]{0:T(512)}, u32[]{:S(2)}) copy-start(f32[512]{0:T(512)} %param.9) | copy-start | bytes 6148
  1.2 8.6 %copy-start.4 = (s32[1,2,3]{2,1,0:T(2,128)S(1)}, s32[1,2,3]{2,1,0:T(2,128)}, u32[]{:S(2)}) copy-start(s32[1,2,3]{2,1,0:T(2,128)} %param.15) | copy-start | bytes 76
  1.2 10.3 %copy-start.5 = (f32[1,9,32,8]{2,3,1,0:T(8,128)S(1)}, f32[1,9,32,8]{2,3,1,0:T(8,128)}, u32[]{:S(2)}) copy-start(f32[1,9,32,8]{2,3,1,0:T(8,128)} %param.10) | copy-start | bytes 27652
  2.3 19.7 %collective-permute-start.2 = (bf16[1,2,8,512]{3,2,1,0:T(8,128)(2,1)S(1)}, bf16[1,2,8,512]{3,2,1,0:T(8,128)(2,1)S(1)}, u32[]{:S(2)}, u32[]{:S(2)}) collective-permute-start(bf16[1,2,8,512]{3,2,1,0:T(8,128)(2,1)S(1)} %get-tuple-element.46), channel_id=1, source_target_pairs={{0,12},{1,13},{2,14},{3,15},{4,8},{5,9},{6,10},{7,11},{8,4},{9,5},... | collective-permute-start | bytes 49160 | tf_op jit(solution)/shard_map/ppermute | solution.py:178
  6.6 15.5 %collective-permute-start.1 = (bf16[1,2,8,512]{3,2,1,0:T(8,128)(2,1)S(1)}, bf16[1,2,8,512]{3,2,1,0:T(8,128)(2,1)S(1)}, u32[]{:S(2)}, u32[]{:S(2)}) collective-permute-start(bf16[1,2,8,512]{3,2,1,0:T(8,128)(2,1)S(1)} %get-tuple-element.46), channel_id=1, source_target_pairs={{0,8},{1,9},{2,10},{3,11},{4,12},{5,13},{6,14},{7,15},{8,0},{9,1},... | collective-permute-start | bytes 49160 | tf_op jit(solution)/shard_map/ppermute | solution.py:178
  6.6 15.5 %collective-permute-start = (bf16[1,2,8,512]{3,2,1,0:T(8,128)(2,1)S(1)}, bf16[1,2,8,512]{3,2,1,0:T(8,128)(2,1)S(1)}, u32[]{:S(2)}, u32[]{:S(2)}) collective-permute-start(bf16[1,2,8,512]{3,2,1,0:T(8,128)(2,1)S(1)} %get-tuple-element.46), channel_id=1, source_target_pairs={{0,4},{1,5},{2,6},{3,7},{4,0},{5,1},{6,2},{7,3},{8,12},{9,13},{10,... | collective-permute-start | bytes 49160 | tf_op jit(solution)/shard_map/ppermute | solution.py:178
  7.2 20.2 %collective-permute-start.6 = (bf16[1,32,1,512]{3,2,1,0:T(2,128)(2,1)S(1)}, bf16[1,32,1,512]{3,2,1,0:T(2,128)(2,1)S(1)}, u32[]{:S(2)}, u32[]{:S(2)}) collective-permute-start(bf16[1,32,1,512]{3,2,1,0:T(2,128)(2,1)S(1)} %get-tuple-element.24), channel_id=1, source_target_pairs={{0,1},{1,2},{2,3},{3,4},{4,5},{5,6},{6,7},{7,8},{8,9},{9,10},{10,1... | collective-permute-start | bytes 98312 | tf_op jit(solution)/shard_map/ppermute | solution.py:19
  9.7 17.6 %collective-permute-start.7 = (bf16[1,32,1,512]{3,2,1,0:T(2,128)(2,1)S(1)}, bf16[1,32,1,512]{3,2,1,0:T(2,128)(2,1)S(1)}, u32[]{:S(2)}, u32[]{:S(2)}) collective-permute-start(bf16[1,32,1,512]{3,2,1,0:T(2,128)(2,1)S(1)} %get-tuple-element.25), channel_id=1, source_target_pairs={{1,0},{2,1},{3,2},{4,3},{5,4},{6,5},{7,6},{8,7},{9,8},{10,9},{11,1... | collective-permute-start | bytes 98312 | tf_op jit(solution)/shard_map/ppermute | solution.py:20
  22.8 4.8 %collective-permute-start.5 = (bf16[4,1,2,8,512]{4,3,2,0,1:T(8,128)(2,1)S(1)}, bf16[4,1,2,8,512]{4,3,2,0,1:T(8,128)(2,1)S(1)}, u32[]{:S(2)}, u32[]{:S(2)}) collective-permute-start(bf16[4,1,2,8,512]{4,3,2,0,1:T(8,128)(2,1)S(1)} %bitcast_select_fusion.1), channel_id=1, source_target_pairs={{0,3},{1,2},{2,1},{3,0},{4,7},{5,6},{6,5},{7,4},{8,11},{9,10},{10,... | collective-permute-start | bytes 196616 | tf_op jit(solution)/shard_map/ppermute | solution.py:178
  24.5 6.0 %collective-permute-start.4 = (bf16[4,1,2,8,512]{4,3,2,0,1:T(8,128)(2,1)S(1)}, bf16[4,1,2,8,512]{4,3,2,0,1:T(8,128)(2,1)S(1)}, u32[]{:S(2)}, u32[]{:S(2)}) collective-permute-start(bf16[4,1,2,8,512]{4,3,2,0,1:T(8,128)(2,1)S(1)} %bitcast_select_fusion.1), channel_id=1, source_target_pairs={{0,2},{1,3},{2,0},{3,1},{4,6},{5,7},{6,4},{7,5},{8,10},{9,11},{10,... | collective-permute-start | bytes 196616 | tf_op jit(solution)/shard_map/ppermute | solution.py:178
  27.3 3.3 %collective-permute-start.3 = (bf16[4,1,2,8,512]{4,3,2,0,1:T(8,128)(2,1)S(1)}, bf16[4,1,2,8,512]{4,3,2,0,1:T(8,128)(2,1)S(1)}, u32[]{:S(2)}, u32[]{:S(2)}) collective-permute-start(bf16[4,1,2,8,512]{4,3,2,0,1:T(8,128)(2,1)S(1)} %bitcast_select_fusion.1), channel_id=1, source_target_pairs={{0,1},{1,0},{2,3},{3,2},{4,5},{5,4},{6,7},{7,6},{8,9},{9,8},{10,11... | collective-permute-start | bytes 196616 | tf_op jit(solution)/shard_map/ppermute | solution.py:178
  33.1 4.7 %copy-start.3 = (bf16[512,512]{1,0:T(8,128)(2,1)S(1)}, bf16[512,512]{1,0:T(8,128)(2,1)}, u32[]{:S(2)}) copy-start(bf16[512,512]{1,0:T(8,128)(2,1)} %param.11) | copy-start | bytes 1572868
  34.2 6.1 %collective-permute-start.9 = (bf16[6,8,512]{2,1,0:T(8,128)(2,1)S(1)}, bf16[6,8,512]{2,1,0:T(8,128)(2,1)S(1)}, u32[]{:S(2)}, u32[]{:S(2)}) collective-permute-start(bf16[6,8,512]{2,1,0:T(8,128)(2,1)S(1)} %get-tuple-element.33), channel_id=1, source_target_pairs={{0,8},{1,9},{2,10},{3,11},{4,12},{5,13},{6,14},{7,15},{8,0},{9,1},... | collective-permute-start | bytes 147464 | tf_op jit(solution)/shard_map/ppermute | solution.py:201
  34.3 6.0 %collective-permute-start.8 = (bf16[6,8,512]{2,1,0:T(8,128)(2,1)S(1)}, bf16[6,8,512]{2,1,0:T(8,128)(2,1)S(1)}, u32[]{:S(2)}, u32[]{:S(2)}) collective-permute-start(bf16[6,8,512]{2,1,0:T(8,128)(2,1)S(1)} %get-tuple-element.33), channel_id=1, source_target_pairs={{0,4},{1,5},{2,6},{3,7},{4,0},{5,1},{6,2},{7,3},{8,12},{9,13},{10,... | collective-permute-start | bytes 147464 | tf_op jit(solution)/shard_map/ppermute | solution.py:201
  36.2 4.7 %collective-permute-start.10 = (bf16[6,8,512]{2,1,0:T(8,128)(2,1)S(1)}, bf16[6,8,512]{2,1,0:T(8,128)(2,1)S(1)}, u32[]{:S(2)}, u32[]{:S(2)}) collective-permute-start(bf16[6,8,512]{2,1,0:T(8,128)(2,1)S(1)} %get-tuple-element.33), channel_id=1, source_target_pairs={{0,12},{1,13},{2,14},{3,15},{4,8},{5,9},{6,10},{7,11},{8,4},{9,5},... | collective-permute-start | bytes 147464 | tf_op jit(solution)/shard_map/ppermute | solution.py:201
  38.9 7.5 %collective-permute-start.14 = (bf16[1,32,3,512]{3,2,1,0:T(4,128)(2,1)S(1)}, bf16[1,32,3,512]{3,2,1,0:T(4,128)(2,1)S(1)}, u32[]{:S(2)}, u32[]{:S(2)}) collective-permute-start(bf16[1,32,3,512]{3,2,1,0:T(4,128)(2,1)S(1)} %get-tuple-element.14), channel_id=1, source_target_pairs={{0,1},{1,2},{2,3},{3,4},{4,5},{5,6},{6,7},{7,8},{8,9},{9,10},{10,1... | collective-permute-start | bytes 294920 | tf_op jit(solution)/shard_map/ppermute | solution.py:19
  40.0 6.9 %collective-permute-start.15 = (bf16[1,32,3,512]{3,2,1,0:T(4,128)(2,1)S(1)}, bf16[1,32,3,512]{3,2,1,0:T(4,128)(2,1)S(1)}, u32[]{:S(2)}, u32[]{:S(2)}) collective-permute-start(bf16[1,32,3,512]{3,2,1,0:T(4,128)(2,1)S(1)} %get-tuple-element.15), channel_id=1, source_target_pairs={{1,0},{2,1},{3,2},{4,3},{5,4},{6,5},{7,6},{8,7},{9,8},{10,9},{11,1... | collective-permute-start | bytes 294920 | tf_op jit(solution)/shard_map/ppermute | solution.py:20
  41.0 7.8 %collective-permute-start.12 = (bf16[4,6,8,512]{3,2,1,0:T(8,128)(2,1)S(1)}, bf16[4,6,8,512]{3,2,1,0:T(8,128)(2,1)S(1)}, u32[]{:S(2)}, u32[]{:S(2)}) collective-permute-start(bf16[4,6,8,512]{3,2,1,0:T(8,128)(2,1)S(1)} %get-tuple-element.27), channel_id=1, source_target_pairs={{0,2},{1,3},{2,0},{3,1},{4,6},{5,7},{6,4},{7,5},{8,10},{9,11},{10,... | collective-permute-start | bytes 589832 | tf_op jit(solution)/shard_map/ppermute | solution.py:201
  42.1 6.7 %collective-permute-start.11 = (bf16[4,6,8,512]{3,2,1,0:T(8,128)(2,1)S(1)}, bf16[4,6,8,512]{3,2,1,0:T(8,128)(2,1)S(1)}, u32[]{:S(2)}, u32[]{:S(2)}) collective-permute-start(bf16[4,6,8,512]{3,2,1,0:T(8,128)(2,1)S(1)} %get-tuple-element.27), channel_id=1, source_target_pairs={{0,1},{1,0},{2,3},{3,2},{4,5},{5,4},{6,7},{7,6},{8,9},{9,8},{10,11... | collective-permute-start | bytes 589832 | tf_op jit(solution)/shard_map/ppermute | solution.py:201
  44.9 9.4 %collective-permute-start.13 = (bf16[4,6,8,512]{3,2,1,0:T(8,128)(2,1)S(1)}, bf16[4,6,8,512]{3,2,1,0:T(8,128)(2,1)S(1)}, u32[]{:S(2)}, u32[]{:S(2)}) collective-permute-start(bf16[4,6,8,512]{3,2,1,0:T(8,128)(2,1)S(1)} %get-tuple-element.27), channel_id=1, source_target_pairs={{0,3},{1,2},{2,1},{3,0},{4,7},{5,6},{6,5},{7,4},{8,11},{9,10},{10,... | collective-permute-start | bytes 589832 | tf_op jit(solution)/shard_map/ppermute | solution.py:201
  47.4 1.0 %copy-start.2 = (bf16[512,512]{1,0:T(8,128)(2,1)S(1)}, bf16[512,512]{1,0:T(8,128)(2,1)}, u32[]{:S(2)}) copy-start(bf16[512,512]{1,0:T(8,128)(2,1)} %param.12) | copy-start | bytes 1572868

commit v17 on v14

--- a/solution.py
+++ b/solution.py
@@ -79,7 +79,14 @@
     )
 
 
-def attention_kernel(q_ref, k_ref, v_ref, lat_ref, wo_ref, out_ref, att_ref):
+def attention_kernel(
+    q_ref, kc_ref, kr_ref, vc_ref, vr_ref, lat_ref, wo_ref, out_ref, att_ref, k_ref, v_ref
+):
+    middle = kc_ref.shape[0]
+    k_ref[pl.ds(0, middle)] = kc_ref[...]
+    k_ref[pl.ds(middle, kr_ref.shape[0])] = kr_ref[...]
+    v_ref[pl.ds(0, middle)] = vc_ref[...]
+    v_ref[pl.ds(middle, vr_ref.shape[0])] = vr_ref[...]
     cells, channels = q_ref.shape
     positions = k_ref.shape[0]
     rows, cols = lat_ref.shape[0], lat_ref.shape[1]
@@ -90,8 +97,21 @@
     scale = head_size ** (-0.5)
     cell = lax.broadcasted_iota(jnp.int32, (cells, positions), 0)
     place = lax.broadcasted_iota(jnp.int32, (cells, positions), 1)
-    row_gap = place // wide - cell // cols
-    col_gap = place % wide - cell % cols
+    rim_rows = RADIUS * wide
+    rows_total = lat_ref.shape[0] + 2 * RADIUS
+    key_row = jnp.where(
+        place < middle,
+        place // wide + RADIUS,
+        jnp.where(
+            place < middle + rim_rows,
+            (place - middle) // wide,
+            (place - middle - rim_rows) // wide + rows_total - RADIUS,
+        ),
+    )
+    key_row = jnp.where(place < middle + 2 * rim_rows, key_row, rows_total + span)
+    key_col = jnp.where(place < middle, place % wide, (place - middle) % wide)
+    row_gap = key_row - cell // cols
+    col_gap = key_col - cell % cols
     valid = (row_gap >= 0) & (row_gap < span) & (col_gap >= 0) & (col_gap < span)
     lane = lax.broadcasted_iota(jnp.int32, (cells, group), 1) // head_size
     for g in range(channels // group):
@@ -122,26 +142,30 @@
     rows, cols, channels = own_tile.shape
     cells = rows * cols
     center_flat = center.reshape(-1, channels)
-    rim_flat = rims.reshape(2, -1, channels)
-    count = center_flat.shape[0] + 2 * rim_flat.shape[1]
+    rim_flat = rims.reshape(-1, channels)
+    count = center_flat.shape[0] + rim_flat.shape[0]
     positions = -(-count // 128) * 128
-    tail = jnp.zeros((positions - count, channels), jnp.bfloat16)
-
-    def both(weight):
-        mid = project(center_flat, weight)
-        edge = project(rim_flat.reshape(-1, channels), weight).reshape(rim_flat.shape)
-        return jnp.concatenate([edge[0], mid, edge[1], tail], axis=0)
-
-    key_flat = both(w_key)
-    value_flat = both(w_value)
+    rim_flat = jnp.pad(rim_flat, ((0, positions - count), (0, 0)))
     vmem = pl.BlockSpec(memory_space=pltpu.VMEM)
     out = pl.pallas_call(
         attention_kernel,
         out_shape=jax.ShapeDtypeStruct((cells, channels), own_tile.dtype),
-        in_specs=[vmem] * 5,
+        in_specs=[vmem] * 7,
         out_specs=vmem,
-        scratch_shapes=[pltpu.VMEM((cells, channels), jnp.bfloat16)],
-    )(query.reshape(cells, channels), key_flat, value_flat, own_tile, w_output)
+        scratch_shapes=[
+            pltpu.VMEM((cells, channels), jnp.bfloat16),
+            pltpu.VMEM((positions, channels), jnp.bfloat16),
+            pltpu.VMEM((positions, channels), jnp.bfloat16),
+        ],
+    )(
+        query.reshape(cells, channels),
+        project(center_flat, w_key),
+        project(rim_flat, w_key),
+        project(center_flat, w_value),
+        project(rim_flat, w_value),
+        own_tile,
+        w_output,
+    )
     return out.reshape(rows, cols, channels)
 
 

time: 60 us -> 59.5 us (level)
  other arithmetic: 11.6 us -> 7.75 us
  starting transfers between devices: 19.6 us -> 22.9 us
  matrix products: 2.98 us -> 5.99 us
  waiting for transfers between devices: 11.6 us -> 9.7 us
  local copies, waits for them, and re-layouts: 6.44 us -> 5.38 us
    ppermute x2, waiting for transfers between devices: 5.61 us -> 0.01 us  [padded_2(): before = lax.ppermute(last, axis, up)]
    ppermute x12, waiting for transfers between devices: 5.98 us -> 9.69 us  [doubling_gather(): lax.ppermute(held, axis, [(i, i ^ d * stride) for i in range(count)])]
    ppermute x2, starting transfers between devices: 5.38 us -> 8.86 us  [padded_2(): after = lax.ppermute(first, axis, down)]
    dot_general x5, matrix products: 2.24 us -> 5.25 us  [project(): jnp.dot(flat, weight, preferred_element_type=jnp.float32)]
    concatenate x1 -> x0, other arithmetic: 1.46 us -> none  [both(): return jnp.concatenate([edge[0], mid, edge[1], tail], axis=0)]
    another operation x6, other arithmetic: 1.31 us -> 0.19 us  [doubling_gather(): jnp.stack(got)]
    unnamed x20 -> x10, local copies, waits for them, and re-layouts: 0.97 us -> 0.02 us
    select_n x6, other arithmetic: 1.02 us -> 0.34 us  [doubling_gather(): jnp.take(jnp.stack(got), digit ^ jnp.arange(r, dtype=jnp.int32), axis=0)]
  transfers between devices with their start and end apart: 16 -> 16, of which waited for: 7 -> 4; matrix products, arithmetic and copies ran while one was open for 15% -> 15% of each run, Pallas kernels for 0% -> 0%
where the time goes in v17:
time: 59.5 us; the launch traced here: 59.3 us
  starting transfers between devices  22.9 us (38%)
  waiting for transfers between devices  9.7 us (16%)
  other arithmetic  7.75 us (13%)
  Pallas kernels  7.05 us (12%)
  matrix products  5.99 us (10%)
  local copies, waits for them, and re-layouts  5.38 us (9%)
    ppermute x12, starting transfers between devices, doubling_gather(): lax.ppermute(held, axis, [(i, i ^ d * stride) for i in range(count)])  13.9 us
    ppermute x12, waiting for transfers between devices, doubling_gather(): lax.ppermute(held, axis, [(i, i ^ d * stride) for i in range(count)])  9.69 us
    ppermute x2, starting transfers between devices, padded_2(): after = lax.ppermute(first, axis, down)  8.86 us
    pallas_call x1, Pallas kernels, attend_and_mix(): pl.pallas_call(attention_kernel, out_shape=jax.ShapeDtypeStruct((cells, c...  7.05 us
    dot_general x5, matrix products, project(): jnp.dot(flat, weight, preferred_element_type=jnp.float32)  5.25 us
    gather x4, local copies, waits for them, and re-layouts, doubling_gather(): jnp.take(jnp.stack(got), digit ^ jnp.arange(r, dtype=jnp.int32), axis=0)  2.27 us
    convert_element_type x2, other arithmetic, normalize(): return (values * factor * norm_gain).astype(jnp.bfloat16)  2.17 us
  transfers between devices with their start and end apart: 16, of which 4 were waited for; matrix products, arithmetic and copies ran while one was open for 15% of the time, Pallas kernels for 0%

profile of v17, /device:TPU:0, one launch (start us, length us, event | category | flops | bytes accessed | tf_op | source)
XLA Modules:
  0.0 59.3 jit_solution(11798833140480690232)
XLA Ops:
  0.0 1.1 %fusion.14 = f32[32,8]{1,0:T(8,128)S(1)} fusion(bf16[1,32,8,512]{3,2,1,0:T(8,128)(2,1)} %param.8), kind=kLoop, calls=%fused_computation.32 | loop fusion | flops 392960 | bytes 263168 | tf_op jit(solution)/shard_map/reduce_sum | solution.py:27
  1.2 1.1 %fusion.16 = bf16[32,8,512]{2,1,0:T(8,128)(2,1)S(1)} fusion(f32[512]{0:T(512)} %param.9, f32[32,8]{1,0:T(8,128)S(1)} %add_rsqrt_fusion, bf16[1,32,8,512]{3,2,1,0:T(8,128)(2,1)} %param.8), kind=kLoop, calls=%fused_computation.34 | loop fusion | flops 524288 | bytes 527360 | tf_op jit(solution)/shard_map/convert_element_type | solution.py:28
  2.3 3.1 %collective-permute-start = (bf16[1,2,8,512]{3,2,1,0:T(8,128)(2,1)S(1)}, bf16[1,2,8,512]{3,2,1,0:T(8,128)(2,1)S(1)}, u32[]{:S(2)}, u32[]{:S(2)}) collective-permute-start(bf16[1,2,8,512]{3,2,1,0:T(8,128)(2,1)S(1)} %get-tuple-element.40), channel_id=1, source_target_pairs={{0,4},{1,5},{2,6},{3,7},{4,0},{5,1},{6,2},{7,3},{8,12},{9,13},{10,... | collective-permute-start | bytes 49160 | tf_op jit(solution)/shard_map/ppermute | solution.py:202
  5.4 2.6 %collective-permute-start.1 = (bf16[1,2,8,512]{3,2,1,0:T(8,128)(2,1)S(1)}, bf16[1,2,8,512]{3,2,1,0:T(8,128)(2,1)S(1)}, u32[]{:S(2)}, u32[]{:S(2)}) collective-permute-start(bf16[1,2,8,512]{3,2,1,0:T(8,128)(2,1)S(1)} %get-tuple-element.40), channel_id=1, source_target_pairs={{0,8},{1,9},{2,10},{3,11},{4,12},{5,13},{6,14},{7,15},{8,0},{9,1},... | collective-permute-start | bytes 49160 | tf_op jit(solution)/shard_map/ppermute | solution.py:202
  8.0 1.1 %multiply_convert_fusion = bf16[1,32,8,512]{3,2,1,0:T(8,128)(2,1)S(1)} fusion(bf16[1,32,8,512]{3,2,1,0:T(8,128)(2,1)} %param.8, f32[512]{0:T(512)} %param.9, f32[32,8]{1,0:T(8,128)S(1)} %add_rsqrt_fusion), kind=kLoop, calls=%fused_computation.38 | loop fusion | flops 524288 | bytes 527360 | tf_op jit(solution)/shard_map/convert_element_type | solution.py:28
  9.2 4.4 %collective-permute-start.7 = (bf16[1,32,1,512]{3,2,1,0:T(2,128)(2,1)S(1)}, bf16[1,32,1,512]{3,2,1,0:T(2,128)(2,1)S(1)}, u32[]{:S(2)}, u32[]{:S(2)}) collective-permute-start(bf16[1,32,1,512]{3,2,1,0:T(2,128)(2,1)S(1)} %get-tuple-element.25), channel_id=1, source_target_pairs={{1,0},{2,1},{3,2},{4,3},{5,4},{6,5},{7,6},{8,7},{9,8},{10,9},{11,1... | collective-permute-start | bytes 98312 | tf_op jit(solution)/shard_map/ppermute | solution.py:20
  13.7 0.2 slice_reduce_fusion.2
  13.9 0.2 compare_reduce_fusion
  15.0 0.6 gather_fusion
  15.7 0.1 collective-permute-start.4
  15.8 1.7 %collective-permute-start.5 = (bf16[4,1,2,8,512]{4,3,2,0,1:T(8,128)(2,1)S(1)}, bf16[4,1,2,8,512]{4,3,2,0,1:T(8,128)(2,1)S(1)}, u32[]{:S(2)}, u32[]{:S(2)}) collective-permute-start(bf16[4,1,2,8,512]{4,3,2,0,1:T(8,128)(2,1)S(1)} %bitcast_select_fusion.4), channel_id=1, source_target_pairs={{0,3},{1,2},{2,1},{3,0},{4,7},{5,6},{6,5},{7,4},{8,11},{9,10},{10,... | collective-permute-start | bytes 196616 | tf_op jit(solution)/shard_map/ppermute | solution.py:202
  17.6 0.3 maximum_bitcast_fusion.1
  17.9 2.8 %collective-permute-done.4 = bf16[4,1,2,8,512]{4,3,2,0,1:T(8,128)(2,1)S(1)} collective-permute-done((bf16[4,1,2,8,512]{4,3,2,0,1:T(8,128)(2,1)S(1)}, bf16[4,1,2,8,512]{4,3,2,0,1:T(8,128)(2,1)S(1)}, u32[]{:S(2)}, u32[]{:S(2)}) %collective-permute-start.4) | collective-permute-done | bytes 65568 | tf_op jit(solution)/shard_map/ppermute | solution.py:202
  20.7 0.5 collective-permute-done.5
  21.2 0.6 gather_fusion.1
  21.8 0.1 fusion.29
  21.9 0.2 copy.24
  22.2 0.3 fusion.12
  22.7 1.1 %add_convert_fusion = bf16[32,8,512]{2,1,0:T(8,128)(2,1)S(1)} fusion(bf16[32,10,512]{2,1,0:T(8,128)(2,1)S(1)} %maximum_bitcast_fusion.1, bf16[1,10,512]{2,1,0:T(8,128)(2,1)S(1)} %copy.36, bf16[1,10,512]{2,1,0:T(8,128)(2,1)S(1)} %copy.29, f32[32,8]{1,0:T(8,128)S(1)} %copy.38, f32[32,8]{1,0:T(8,128)S(1)} %copy.37, f32[32,8]{1,0:T(8,128)S(1)} %copy.35, ...), kind=kLoop, calls=%fused_computation.37 | loop fusion | flops 5898240 | bytes 1753088 | tf_op jit(solution)/shard_map/convert_element_type | solution.py:69
  23.9 2.6 %collective-permute-start.11 = (bf16[1,6,8,512]{3,2,1,0:T(8,128)(2,1)S(1)}, bf16[1,6,8,512]{3,2,1,0:T(8,128)(2,1)S(1)}, u32[]{:S(2)}, u32[]{:S(2)}) collective-permute-start(bf16[1,6,8,512]{3,2,1,0:T(8,128)(2,1)S(1)} %get-tuple-element.27), channel_id=1, source_target_pairs={{0,8},{1,9},{2,10},{3,11},{4,12},{5,13},{6,14},{7,15},{8,0},{9,1},... | collective-permute-start | bytes 147464 | tf_op jit(solution)/shard_map/ppermute | solution.py:202
  26.4 1.8 %collective-permute-start.12 = (bf16[1,6,8,512]{3,2,1,0:T(8,128)(2,1)S(1)}, bf16[1,6,8,512]{3,2,1,0:T(8,128)(2,1)S(1)}, u32[]{:S(2)}, u32[]{:S(2)}) collective-permute-start(bf16[1,6,8,512]{3,2,1,0:T(8,128)(2,1)S(1)} %get-tuple-element.27), channel_id=1, source_target_pairs={{0,12},{1,13},{2,14},{3,15},{4,8},{5,9},{6,10},{7,11},{8,4},{9,5},... | collective-permute-start | bytes 147464 | tf_op jit(solution)/shard_map/ppermute | solution.py:202
  28.2 1.0 %fusion.65 = bf16[1,32,8,512]{3,2,1,0:T(8,128)(2,1)S(1)} fusion(bf16[1,10,512]{2,1,0:T(8,128)(2,1)S(1)} %copy.36, bf16[32,10,512]{2,1,0:T(8,128)(2,1)S(1)} %maximum_bitcast_fusion.1, f32[32,8]{1,0:T(8,128)S(1)} %copy.38, f32[32,8]{1,0:T(8,128)S(1)} %copy.37, f32[32,8]{1,0:T(8,128)S(1)} %copy.35, f32[32,8]{1,0:T(8,128)S(1)} %copy.34, f32[32,8]{1,0:T(8,128)S(1)} %copy.33, ...), kind=kLoop, calls=%fused_computation.133 | loop fusion | flops 5898240 | bytes 1753088 | tf_op jit(solution)/shard_map/broadcast_in_dim | solution.py:223
  29.3 0.1 fusion.52
  29.4 4.4 %collective-permute-start.9 = (bf16[1,32,3,512]{3,2,1,0:T(4,128)(2,1)S(1)}, bf16[1,32,3,512]{3,2,1,0:T(4,128)(2,1)S(1)}, u32[]{:S(2)}, u32[]{:S(2)}) collective-permute-start(bf16[1,32,3,512]{3,2,1,0:T(4,128)(2,1)S(1)} %get-tuple-element.17), channel_id=1, source_target_pairs={{1,0},{2,1},{3,2},{4,3},{5,4},{6,5},{7,6},{8,7},{9,8},{10,9},{11,1... | collective-permute-start | bytes 294920 | tf_op jit(solution)/shard_map/ppermute | solution.py:20
  33.9 1.0 %convolution_convert_fusion.2.q_ref = bf16[256,512]{1,0:T(8,128)(2,1)} fusion(bf16[512,512]{1,0:T(8,128)(2,1)S(1)} %copy-done.2, bf16[32,8,512]{2,1,0:T(8,128)(2,1)S(1)} %add_convert_fusion), kind=kOutput, calls=%fused_computation.14 | convolution fusion | flops 134348800 | bytes 1048576 | tf_op jit(solution)/shard_map/dot_general | solution.py:76
  34.9 0.6 gather_fusion.2
  35.8 1.8 %collective-permute-start.15 = (bf16[4,1,6,8,512]{4,3,2,0,1:T(8,128)(2,1)S(1)}, bf16[4,1,6,8,512]{4,3,2,0,1:T(8,128)(2,1)S(1)}, u32[]{:S(2)}, u32[]{:S(2)}) collective-permute-start(bf16[4,1,6,8,512]{4,3,2,0,1:T(8,128)(2,1)S(1)} %bitcast_select_fusion.2), channel_id=1, source_target_pairs={{0,3},{1,2},{2,1},{3,0},{4,7},{5,6},{6,5},{7,4},{8,11},{9,10},{10,... | collective-permute-start | bytes 589832 | tf_op jit(solution)/shard_map/ppermute | solution.py:202
  37.6 0.3 pad_maximum_fusion.2
  37.9 0.1 reshape_squeeze.3
  38.1 1.2 %convolution_convert_fusion.vc_ref = bf16[448,512]{1,0:T(8,128)(2,1)} fusion(bf16[448,512]{1,0:T(8,128)(2,1)S(1)} %reshape_squeeze.3, bf16[512,512]{1,0:T(8,128)(2,1)S(1)} %copy-done), kind=kOutput, calls=%fused_computation.12 | convolution fusion | flops 235110400 | bytes 1441792 | tf_op jit(solution)/shard_map/dot_general | solution.py:76
  39.3 1.2 %convolution_convert_fusion.1.kc_ref = bf16[448,512]{1,0:T(8,128)(2,1)} fusion(bf16[448,512]{1,0:T(8,128)(2,1)S(1)} %reshape_squeeze.3, bf16[512,512]{1,0:T(8,128)(2,1)S(1)} %copy-done.1), kind=kOutput, calls=%fused_computation.13 | convolution fusion | flops 235110400 | bytes 1441792 | tf_op jit(solution)/shard_map/dot_general | solution.py:76
  40.5 3.1 %collective-permute-done.14 = bf16[4,1,6,8,512]{4,3,2,0,1:T(8,128)(2,1)S(1)} collective-permute-done((bf16[4,1,6,8,512]{4,3,2,0,1:T(8,128)(2,1)S(1)}, bf16[4,1,6,8,512]{4,3,2,0,1:T(8,128)(2,1)S(1)}, u32[]{:S(2)}, u32[]{:S(2)}) %collective-permute-start.14) | collective-permute-done | bytes 196640 | tf_op jit(solution)/shard_map/ppermute | solution.py:202
  43.5 3.3 %collective-permute-done.15 = bf16[4,1,6,8,512]{4,3,2,0,1:T(8,128)(2,1)S(1)} collective-permute-done((bf16[4,1,6,8,512]{4,3,2,0,1:T(8,128)(2,1)S(1)}, bf16[4,1,6,8,512]{4,3,2,0,1:T(8,128)(2,1)S(1)}, u32[]{:S(2)}, u32[]{:S(2)}) %collective-permute-start.15) | collective-permute-done | bytes 196640 | tf_op jit(solution)/shard_map/ppermute | solution.py:202
  46.8 0.1 maximum_bitcast_fusion
  47.0 0.6 %gather_fusion.3 = bf16[4,4,6,8,512]{4,3,2,1,0:T(8,128)(2,1)S(1)} fusion(bf16[4,4,6,8,512]{4,3,2,1,0:T(8,128)(2,1)S(1)} %maximum_bitcast_fusion, s32[1024]{0:T(1024)S(1)} %pad_clamp_fusion), kind=kCustom, calls=%fused_computation.3 | custom fusion | bytes 1572880 | tf_op jit(solution)/shard_map/jit(_take)/gather | solution.py:204
  47.6 0.1 fusion.13
  47.7 0.6 %copy.39 = bf16[4,4,1,6,8,512]{5,1,0,4,3,2:T(4,128)(2,1)S(1)} copy(bf16[4,4,1,6,8,512]{5,4,3,0,1,2:T(8,128)(2,1)S(1)} %fusion.13) | data formatting | bytes 1572864 | tf_op jit(solution)/shard_map/transpose | solution.py:206
  48.3 0.2 reshape.199
  48.5 0.4 fusion.50
  48.9 0.2 fusion.49
  49.1 0.3 fusion
  49.4 0.1 slice_bitcast_fusion.1
  49.5 0.4 fusion.9
  50.0 0.2 broadcast_select_fusion
  50.1 0.1 broadcast_select_fusion.1
  50.3 0.9 %convolution_convert_fusion.3.vr_ref = bf16[192,512]{1,0:T(8,128)(2,1)} fusion(bf16[512,512]{1,0:T(8,128)(2,1)S(1)} %copy-done, bf16[84,512]{1,0:T(8,128)(2,1)S(1)} %reshape.200), kind=kOutput, calls=%fused_computation.15 | convolution fusion | flops 100761600 | bytes 806912 | tf_op jit(solution)/shard_map/dot_general | solution.py:76
  51.3 0.9 %convolution_convert_fusion.4.kr_ref = bf16[192,512]{1,0:T(8,128)(2,1)} fusion(bf16[512,512]{1,0:T(8,128)(2,1)S(1)} %copy-done.1, bf16[84,512]{1,0:T(8,128)(2,1)S(1)} %reshape.200), kind=kOutput, calls=%fused_computation.16 | convolution fusion | flops 100761600 | bytes 806912 | tf_op jit(solution)/shard_map/dot_general | solution.py:76
  52.2 7.0 %shard_map.82 = bf16[256,512]{1,0:T(8,128)(2,1)} custom-call(bf16[256,512]{1,0:T(8,128)(2,1)} %convolution_convert_fusion.2.q_ref, bf16[448,512]{1,0:T(8,128)(2,1)} %convolution_convert_fusion.1.kc_ref, bf16[192,512]{1,0:T(8,128)(2,1)} %convolution_convert_fusion.4.kr_ref, bf16[448,512]{1,0:T(8,128)(2,1)} %convolution_convert_fusion.vc_ref, ...), custom_call_target="tpu_custom_call" | custom-call | tf_op jit(solution)/shard_map/pallas_call | solution.py:150
  (70 shorter events, 2.1 us)
Async XLA Ops:
  0.0 38.1 %copy-start = (bf16[512,512]{1,0:T(8,128)(2,1)S(1)}, bf16[512,512]{1,0:T(8,128)(2,1)}, u32[]{:S(2)}) copy-start(bf16[512,512]{1,0:T(8,128)(2,1)} %param.13) | copy-start | bytes 1572868
  0.0 13.7 %copy-start.4 = (s32[1,2,3]{2,1,0:T(2,128)S(1)}, s32[1,2,3]{2,1,0:T(2,128)}, u32[]{:S(2)}) copy-start(s32[1,2,3]{2,1,0:T(2,128)} %param.15) | copy-start | bytes 76
  0.0 14.2 %copy-start.3 = (f32[1,9,32,8]{2,3,1,0:T(8,128)S(1)}, f32[1,9,32,8]{2,3,1,0:T(8,128)}, u32[]{:S(2)}) copy-start(f32[1,9,32,8]{2,3,1,0:T(8,128)} %param.10) | copy-start | bytes 27652
  2.3 12.7 %collective-permute-start = (bf16[1,2,8,512]{3,2,1,0:T(8,128)(2,1)S(1)}, bf16[1,2,8,512]{3,2,1,0:T(8,128)(2,1)S(1)}, u32[]{:S(2)}, u32[]{:S(2)}) collective-permute-start(bf16[1,2,8,512]{3,2,1,0:T(8,128)(2,1)S(1)} %get-tuple-element.40), channel_id=1, source_target_pairs={{0,4},{1,5},{2,6},{3,7},{4,0},{5,1},{6,2},{7,3},{8,12},{9,13},{10,... | collective-permute-start | bytes 49160 | tf_op jit(solution)/shard_map/ppermute | solution.py:202
  5.4 9.6 %collective-permute-start.1 = (bf16[1,2,8,512]{3,2,1,0:T(8,128)(2,1)S(1)}, bf16[1,2,8,512]{3,2,1,0:T(8,128)(2,1)S(1)}, u32[]{:S(2)}, u32[]{:S(2)}) collective-permute-start(bf16[1,2,8,512]{3,2,1,0:T(8,128)(2,1)S(1)} %get-tuple-element.40), channel_id=1, source_target_pairs={{0,8},{1,9},{2,10},{3,11},{4,12},{5,13},{6,14},{7,15},{8,0},{9,1},... | collective-permute-start | bytes 49160 | tf_op jit(solution)/shard_map/ppermute | solution.py:202
  8.0 7.0 %collective-permute-start.2 = (bf16[1,2,8,512]{3,2,1,0:T(8,128)(2,1)S(1)}, bf16[1,2,8,512]{3,2,1,0:T(8,128)(2,1)S(1)}, u32[]{:S(2)}, u32[]{:S(2)}) collective-permute-start(bf16[1,2,8,512]{3,2,1,0:T(8,128)(2,1)S(1)} %get-tuple-element.40), channel_id=1, source_target_pairs={{0,12},{1,13},{2,14},{3,15},{4,8},{5,9},{6,10},{7,11},{8,4},{9,5},... | collective-permute-start | bytes 49160 | tf_op jit(solution)/shard_map/ppermute | solution.py:202
  9.2 8.4 %collective-permute-start.6 = (bf16[1,32,1,512]{3,2,1,0:T(2,128)(2,1)S(1)}, bf16[1,32,1,512]{3,2,1,0:T(2,128)(2,1)S(1)}, u32[]{:S(2)}, u32[]{:S(2)}) collective-permute-start(bf16[1,32,1,512]{3,2,1,0:T(2,128)(2,1)S(1)} %get-tuple-element.24), channel_id=1, source_target_pairs={{0,1},{1,2},{2,3},{3,4},{4,5},{5,6},{6,7},{7,8},{8,9},{9,10},{10,1... | collective-permute-start | bytes 98312 | tf_op jit(solution)/shard_map/ppermute | solution.py:19
  9.2 8.4 %collective-permute-start.7 = (bf16[1,32,1,512]{3,2,1,0:T(2,128)(2,1)S(1)}, bf16[1,32,1,512]{3,2,1,0:T(2,128)(2,1)S(1)}, u32[]{:S(2)}, u32[]{:S(2)}) collective-permute-start(bf16[1,32,1,512]{3,2,1,0:T(2,128)(2,1)S(1)} %get-tuple-element.25), channel_id=1, source_target_pairs={{1,0},{2,1},{3,2},{4,3},{5,4},{6,5},{7,6},{8,7},{9,8},{10,9},{11,1... | collective-permute-start | bytes 98312 | tf_op jit(solution)/shard_map/ppermute | solution.py:20
  15.7 2.2 %collective-permute-start.3 = (bf16[4,1,2,8,512]{4,3,2,0,1:T(8,128)(2,1)S(1)}, bf16[4,1,2,8,512]{4,3,2,0,1:T(8,128)(2,1)S(1)}, u32[]{:S(2)}, u32[]{:S(2)}) collective-permute-start(bf16[4,1,2,8,512]{4,3,2,0,1:T(8,128)(2,1)S(1)} %bitcast_select_fusion.4), channel_id=1, source_target_pairs={{0,1},{1,0},{2,3},{3,2},{4,5},{5,4},{6,7},{7,6},{8,9},{9,8},{10,11... | collective-permute-start | bytes 196616 | tf_op jit(solution)/shard_map/ppermute | solution.py:202
  15.7 5.0 %collective-permute-start.4 = (bf16[4,1,2,8,512]{4,3,2,0,1:T(8,128)(2,1)S(1)}, bf16[4,1,2,8,512]{4,3,2,0,1:T(8,128)(2,1)S(1)}, u32[]{:S(2)}, u32[]{:S(2)}) collective-permute-start(bf16[4,1,2,8,512]{4,3,2,0,1:T(8,128)(2,1)S(1)} %bitcast_select_fusion.4), channel_id=1, source_target_pairs={{0,2},{1,3},{2,0},{3,1},{4,6},{5,7},{6,4},{7,5},{8,10},{9,11},{10,... | collective-permute-start | bytes 196616 | tf_op jit(solution)/shard_map/ppermute | solution.py:202
  15.8 5.3 %collective-permute-start.5 = (bf16[4,1,2,8,512]{4,3,2,0,1:T(8,128)(2,1)S(1)}, bf16[4,1,2,8,512]{4,3,2,0,1:T(8,128)(2,1)S(1)}, u32[]{:S(2)}, u32[]{:S(2)}) collective-permute-start(bf16[4,1,2,8,512]{4,3,2,0,1:T(8,128)(2,1)S(1)} %bitcast_select_fusion.4), channel_id=1, source_target_pairs={{0,3},{1,2},{2,1},{3,0},{4,7},{5,6},{6,5},{7,4},{8,11},{9,10},{10,... | collective-permute-start | bytes 196616 | tf_op jit(solution)/shard_map/ppermute | solution.py:202
  23.7 10.1 %copy-start.2 = (bf16[512,512]{1,0:T(8,128)(2,1)S(1)}, bf16[512,512]{1,0:T(8,128)(2,1)}, u32[]{:S(2)}) copy-start(bf16[512,512]{1,0:T(8,128)(2,1)} %param.11) | copy-start | bytes 1572868
  23.8 11.1 %collective-permute-start.10 = (bf16[1,6,8,512]{3,2,1,0:T(8,128)(2,1)S(1)}, bf16[1,6,8,512]{3,2,1,0:T(8,128)(2,1)S(1)}, u32[]{:S(2)}, u32[]{:S(2)}) collective-permute-start(bf16[1,6,8,512]{3,2,1,0:T(8,128)(2,1)S(1)} %get-tuple-element.27), channel_id=1, source_target_pairs={{0,4},{1,5},{2,6},{3,7},{4,0},{5,1},{6,2},{7,3},{8,12},{9,13},{10,... | collective-permute-start | bytes 147464 | tf_op jit(solution)/shard_map/ppermute | solution.py:202
  23.9 11.0 %collective-permute-start.11 = (bf16[1,6,8,512]{3,2,1,0:T(8,128)(2,1)S(1)}, bf16[1,6,8,512]{3,2,1,0:T(8,128)(2,1)S(1)}, u32[]{:S(2)}, u32[]{:S(2)}) collective-permute-start(bf16[1,6,8,512]{3,2,1,0:T(8,128)(2,1)S(1)} %get-tuple-element.27), channel_id=1, source_target_pairs={{0,8},{1,9},{2,10},{3,11},{4,12},{5,13},{6,14},{7,15},{8,0},{9,1},... | collective-permute-start | bytes 147464 | tf_op jit(solution)/shard_map/ppermute | solution.py:202
  26.4 8.5 %collective-permute-start.12 = (bf16[1,6,8,512]{3,2,1,0:T(8,128)(2,1)S(1)}, bf16[1,6,8,512]{3,2,1,0:T(8,128)(2,1)S(1)}, u32[]{:S(2)}, u32[]{:S(2)}) collective-permute-start(bf16[1,6,8,512]{3,2,1,0:T(8,128)(2,1)S(1)} %get-tuple-element.27), channel_id=1, source_target_pairs={{0,12},{1,13},{2,14},{3,15},{4,8},{5,9},{6,10},{7,11},{8,4},{9,5},... | collective-permute-start | bytes 147464 | tf_op jit(solution)/shard_map/ppermute | solution.py:202
  29.4 8.3 %collective-permute-start.8 = (bf16[1,32,3,512]{3,2,1,0:T(4,128)(2,1)S(1)}, bf16[1,32,3,512]{3,2,1,0:T(4,128)(2,1)S(1)}, u32[]{:S(2)}, u32[]{:S(2)}) collective-permute-start(bf16[1,32,3,512]{3,2,1,0:T(4,128)(2,1)S(1)} %get-tuple-element.16), channel_id=1, source_target_pairs={{0,1},{1,2},{2,3},{3,4},{4,5},{5,6},{6,7},{7,8},{8,9},{9,10},{10,1... | collective-permute-start | bytes 294920 | tf_op jit(solution)/shard_map/ppermute | solution.py:19
  29.4 8.2 %collective-permute-start.9 = (bf16[1,32,3,512]{3,2,1,0:T(4,128)(2,1)S(1)}, bf16[1,32,3,512]{3,2,1,0:T(4,128)(2,1)S(1)}, u32[]{:S(2)}, u32[]{:S(2)}) collective-permute-start(bf16[1,32,3,512]{3,2,1,0:T(4,128)(2,1)S(1)} %get-tuple-element.17), channel_id=1, source_target_pairs={{1,0},{2,1},{3,2},{4,3},{5,4},{6,5},{7,6},{8,7},{9,8},{10,9},{11,1... | collective-permute-start | bytes 294920 | tf_op jit(solution)/shard_map/ppermute | solution.py:20
  35.7 4.8 %collective-permute-start.13 = (bf16[4,1,6,8,512]{4,3,2,0,1:T(8,128)(2,1)S(1)}, bf16[4,1,6,8,512]{4,3,2,0,1:T(8,128)(2,1)S(1)}, u32[]{:S(2)}, u32[]{:S(2)}) collective-permute-start(bf16[4,1,6,8,512]{4,3,2,0,1:T(8,128)(2,1)S(1)} %bitcast_select_fusion.2), channel_id=1, source_target_pairs={{0,1},{1,0},{2,3},{3,2},{4,5},{5,4},{6,7},{7,6},{8,9},{9,8},{10,11... | collective-permute-start | bytes 589832 | tf_op jit(solution)/shard_map/ppermute | solution.py:202
  35.8 7.8 %collective-permute-start.14 = (bf16[4,1,6,8,512]{4,3,2,0,1:T(8,128)(2,1)S(1)}, bf16[4,1,6,8,512]{4,3,2,0,1:T(8,128)(2,1)S(1)}, u32[]{:S(2)}, u32[]{:S(2)}) collective-permute-start(bf16[4,1,6,8,512]{4,3,2,0,1:T(8,128)(2,1)S(1)} %bitcast_select_fusion.2), channel_id=1, source_target_pairs={{0,2},{1,3},{2,0},{3,1},{4,6},{5,7},{6,4},{7,5},{8,10},{9,11},{10,... | collective-permute-start | bytes 589832 | tf_op jit(solution)/shard_map/ppermute | solution.py:202
  35.8 11.0 %collective-permute-start.15 = (bf16[4,1,6,8,512]{4,3,2,0,1:T(8,128)(2,1)S(1)}, bf16[4,1,6,8,512]{4,3,2,0,1:T(8,128)(2,1)S(1)}, u32[]{:S(2)}, u32[]{:S(2)}) collective-permute-start(bf16[4,1,6,8,512]{4,3,2,0,1:T(8,128)(2,1)S(1)} %bitcast_select_fusion.2), channel_id=1, source_target_pairs={{0,3},{1,2},{2,1},{3,0},{4,7},{5,6},{6,5},{7,4},{8,11},{9,10},{10,... | collective-permute-start | bytes 589832 | tf_op jit(solution)/shard_map/ppermute | solution.py:202
  37.9 1.3 %copy-start.1 = (bf16[512,512]{1,0:T(8,128)(2,1)S(1)}, bf16[512,512]{1,0:T(8,128)(2,1)}, u32[]{:S(2)}) copy-start(bf16[512,512]{1,0:T(8,128)(2,1)} %param.12) | copy-start | bytes 1572868

commit v18 on v17

--- a/solution.py
+++ b/solution.py
@@ -80,13 +80,19 @@
 
 
 def attention_kernel(
-    q_ref, kc_ref, kr_ref, vc_ref, vr_ref, lat_ref, wo_ref, out_ref, att_ref, k_ref, v_ref
+    q_ref, kc_ref, vc_ref, rim_ref, wk_ref, wv_ref, lat_ref, wo_ref, out_ref, att_ref, k_ref, v_ref
 ):
     middle = kc_ref.shape[0]
+    extra = rim_ref.shape[0]
+    rim = rim_ref[...]
     k_ref[pl.ds(0, middle)] = kc_ref[...]
-    k_ref[pl.ds(middle, kr_ref.shape[0])] = kr_ref[...]
+    k_ref[pl.ds(middle, extra)] = jnp.dot(
+        rim, wk_ref[...], preferred_element_type=jnp.float32
+    ).astype(k_ref.dtype)
     v_ref[pl.ds(0, middle)] = vc_ref[...]
-    v_ref[pl.ds(middle, vr_ref.shape[0])] = vr_ref[...]
+    v_ref[pl.ds(middle, extra)] = jnp.dot(
+        rim, wv_ref[...], preferred_element_type=jnp.float32
+    ).astype(v_ref.dtype)
     cells, channels = q_ref.shape
     positions = k_ref.shape[0]
     rows, cols = lat_ref.shape[0], lat_ref.shape[1]
@@ -150,7 +156,7 @@
     out = pl.pallas_call(
         attention_kernel,
         out_shape=jax.ShapeDtypeStruct((cells, channels), own_tile.dtype),
-        in_specs=[vmem] * 7,
+        in_specs=[vmem] * 8,
         out_specs=vmem,
         scratch_shapes=[
             pltpu.VMEM((cells, channels), jnp.bfloat16),
@@ -160,9 +166,10 @@
     )(
         query.reshape(cells, channels),
         project(center_flat, w_key),
-        project(rim_flat, w_key),
         project(center_flat, w_value),
-        project(rim_flat, w_value),
+        rim_flat,
+        w_key,
+        w_value,
         own_tile,
         w_output,
     )

time: 59.5 us -> 61.2 us (1.029)
  matrix products: 5.99 us -> 4.13 us
  other arithmetic: 7.75 us -> 9.36 us
  local copies, waits for them, and re-layouts: 5.38 us -> 6.6 us
    dot_general x5 -> x3, matrix products: 5.25 us -> 3.39 us  [project(): jnp.dot(flat, weight, preferred_element_type=jnp.float32)]
    another operation x6, other arithmetic: 0.19 us -> 1.12 us  [doubling_gather(): jnp.stack(got)]
    pad x0 -> x1, local copies, waits for them, and re-layouts: none -> 0.69 us  [attend_and_mix(): rim_flat = jnp.pad(rim_flat, ((0, positions - count), (0, 0)))]
    select_n x6, other arithmetic: 0.34 us -> 1.02 us  [doubling_gather(): jnp.take(jnp.stack(got), digit ^ jnp.arange(r, dtype=jnp.int32), axis=0)]
  transfers between devices with their start and end apart: 16 -> 16, of which waited for: 4 -> 4; matrix products, arithmetic and copies ran while one was open for 15% -> 16% of each run, Pallas kernels for 0% -> 0%
where the time goes in v18:
time: 61.2 us; the launch traced here: 61 us
  starting transfers between devices  22.8 us (37%)
  waiting for transfers between devices  10.1 us (17%)
  other arithmetic  9.36 us (15%)
  Pallas kernels  7.53 us (12%)
  local copies, waits for them, and re-layouts  6.6 us (11%)
  matrix products  4.13 us (7%)
    ppermute x12, starting transfers between devices, doubling_gather(): lax.ppermute(held, axis, [(i, i ^ d * stride) for i in range(count)])  13.9 us
    ppermute x12, waiting for transfers between devices, doubling_gather(): lax.ppermute(held, axis, [(i, i ^ d * stride) for i in range(count)])  10 us
    ppermute x2, starting transfers between devices, padded_2(): after = lax.ppermute(first, axis, down)  8.86 us
    pallas_call x1, Pallas kernels, attend_and_mix(): pl.pallas_call(attention_kernel, out_shape=jax.ShapeDtypeStruct((cells, c...  7.53 us
    dot_general x3, matrix products, project(): jnp.dot(flat, weight, preferred_element_type=jnp.float32)  3.39 us
    gather x4, local copies, waits for them, and re-layouts, doubling_gather(): jnp.take(jnp.stack(got), digit ^ jnp.arange(r, dtype=jnp.int32), axis=0)  2.27 us
    convert_element_type x2, other arithmetic, normalize(): return (values * factor * norm_gain).astype(jnp.bfloat16)  2.17 us
  transfers between devices with their start and end apart: 16, of which 4 were waited for; matrix products, arithmetic and copies ran while one was open for 16% of the time, Pallas kernels for 0%

profile of v18, /device:TPU:0, one launch (start us, length us, event | category | flops | bytes accessed | tf_op | source)
XLA Modules:
  0.0 61.0 jit_solution(18409965369381084662)
XLA Ops:
  0.0 1.1 %fusion.14 = f32[32,8]{1,0:T(8,128)S(1)} fusion(bf16[1,32,8,512]{3,2,1,0:T(8,128)(2,1)} %param.8), kind=kLoop, calls=%fused_computation.30 | loop fusion | flops 392960 | bytes 263168 | tf_op jit(solution)/shard_map/reduce_sum | solution.py:27
  1.2 1.1 %fusion.16 = bf16[32,8,512]{2,1,0:T(8,128)(2,1)S(1)} fusion(f32[512]{0:T(512)} %param.9, f32[32,8]{1,0:T(8,128)S(1)} %add_rsqrt_fusion, bf16[1,32,8,512]{3,2,1,0:T(8,128)(2,1)} %param.8), kind=kLoop, calls=%fused_computation.32 | loop fusion | flops 524288 | bytes 527360 | tf_op jit(solution)/shard_map/convert_element_type | solution.py:28
  2.3 3.1 %collective-permute-start = (bf16[1,2,8,512]{3,2,1,0:T(8,128)(2,1)S(1)}, bf16[1,2,8,512]{3,2,1,0:T(8,128)(2,1)S(1)}, u32[]{:S(2)}, u32[]{:S(2)}) collective-permute-start(bf16[1,2,8,512]{3,2,1,0:T(8,128)(2,1)S(1)} %get-tuple-element.40), channel_id=1, source_target_pairs={{0,4},{1,5},{2,6},{3,7},{4,0},{5,1},{6,2},{7,3},{8,12},{9,13},{10,... | collective-permute-start | bytes 49160 | tf_op jit(solution)/shard_map/ppermute | solution.py:209
  5.4 2.6 %collective-permute-start.1 = (bf16[1,2,8,512]{3,2,1,0:T(8,128)(2,1)S(1)}, bf16[1,2,8,512]{3,2,1,0:T(8,128)(2,1)S(1)}, u32[]{:S(2)}, u32[]{:S(2)}) collective-permute-start(bf16[1,2,8,512]{3,2,1,0:T(8,128)(2,1)S(1)} %get-tuple-element.40), channel_id=1, source_target_pairs={{0,8},{1,9},{2,10},{3,11},{4,12},{5,13},{6,14},{7,15},{8,0},{9,1},... | collective-permute-start | bytes 49160 | tf_op jit(solution)/shard_map/ppermute | solution.py:209
  8.0 1.1 %multiply_convert_fusion = bf16[1,32,8,512]{3,2,1,0:T(8,128)(2,1)S(1)} fusion(bf16[1,32,8,512]{3,2,1,0:T(8,128)(2,1)} %param.8, f32[512]{0:T(512)} %param.9, f32[32,8]{1,0:T(8,128)S(1)} %add_rsqrt_fusion), kind=kLoop, calls=%fused_computation.36 | loop fusion | flops 524288 | bytes 527360 | tf_op jit(solution)/shard_map/convert_element_type | solution.py:28
  9.2 4.4 %collective-permute-start.7 = (bf16[1,32,1,512]{3,2,1,0:T(2,128)(2,1)S(1)}, bf16[1,32,1,512]{3,2,1,0:T(2,128)(2,1)S(1)}, u32[]{:S(2)}, u32[]{:S(2)}) collective-permute-start(bf16[1,32,1,512]{3,2,1,0:T(2,128)(2,1)S(1)} %get-tuple-element.25), channel_id=1, source_target_pairs={{1,0},{2,1},{3,2},{4,3},{5,4},{6,5},{7,6},{8,7},{9,8},{10,9},{11,1... | collective-permute-start | bytes 98312 | tf_op jit(solution)/shard_map/ppermute | solution.py:20
  13.7 0.2 slice_reduce_fusion.2
  13.9 0.2 compare_reduce_fusion
  15.0 0.6 gather_fusion
  15.7 0.1 collective-permute-start.4
  15.8 1.8 %collective-permute-start.5 = (bf16[4,1,2,8,512]{4,3,2,0,1:T(8,128)(2,1)S(1)}, bf16[4,1,2,8,512]{4,3,2,0,1:T(8,128)(2,1)S(1)}, u32[]{:S(2)}, u32[]{:S(2)}) collective-permute-start(bf16[4,1,2,8,512]{4,3,2,0,1:T(8,128)(2,1)S(1)} %bitcast_select_fusion.4), channel_id=1, source_target_pairs={{0,3},{1,2},{2,1},{3,0},{4,7},{5,6},{6,5},{7,4},{8,11},{9,10},{10,... | collective-permute-start | bytes 196616 | tf_op jit(solution)/shard_map/ppermute | solution.py:209
  17.6 0.3 maximum_bitcast_fusion.1
  17.9 2.8 %collective-permute-done.4 = bf16[4,1,2,8,512]{4,3,2,0,1:T(8,128)(2,1)S(1)} collective-permute-done((bf16[4,1,2,8,512]{4,3,2,0,1:T(8,128)(2,1)S(1)}, bf16[4,1,2,8,512]{4,3,2,0,1:T(8,128)(2,1)S(1)}, u32[]{:S(2)}, u32[]{:S(2)}) %collective-permute-start.4) | collective-permute-done | bytes 65568 | tf_op jit(solution)/shard_map/ppermute | solution.py:209
  20.7 0.5 collective-permute-done.5
  21.2 0.6 gather_fusion.1
  21.8 0.1 fusion.29
  21.9 0.2 copy.25
  22.2 0.3 fusion.12
  22.7 1.1 %add_convert_fusion = bf16[32,8,512]{2,1,0:T(8,128)(2,1)S(1)} fusion(bf16[32,10,512]{2,1,0:T(8,128)(2,1)S(1)} %maximum_bitcast_fusion.1, bf16[1,10,512]{2,1,0:T(8,128)(2,1)S(1)} %copy.37, bf16[1,10,512]{2,1,0:T(8,128)(2,1)S(1)} %copy.30, f32[32,8]{1,0:T(8,128)S(1)} %copy.39, f32[32,8]{1,0:T(8,128)S(1)} %copy.38, f32[32,8]{1,0:T(8,128)S(1)} %copy.36, ...), kind=kLoop, calls=%fused_computation.35 | loop fusion | flops 5898240 | bytes 1753088 | tf_op jit(solution)/shard_map/convert_element_type | solution.py:69
  23.9 2.6 %collective-permute-start.11 = (bf16[1,6,8,512]{3,2,1,0:T(8,128)(2,1)S(1)}, bf16[1,6,8,512]{3,2,1,0:T(8,128)(2,1)S(1)}, u32[]{:S(2)}, u32[]{:S(2)}) collective-permute-start(bf16[1,6,8,512]{3,2,1,0:T(8,128)(2,1)S(1)} %get-tuple-element.27), channel_id=1, source_target_pairs={{0,8},{1,9},{2,10},{3,11},{4,12},{5,13},{6,14},{7,15},{8,0},{9,1},... | collective-permute-start | bytes 147464 | tf_op jit(solution)/shard_map/ppermute | solution.py:209
  26.5 1.8 %collective-permute-start.12 = (bf16[1,6,8,512]{3,2,1,0:T(8,128)(2,1)S(1)}, bf16[1,6,8,512]{3,2,1,0:T(8,128)(2,1)S(1)}, u32[]{:S(2)}, u32[]{:S(2)}) collective-permute-start(bf16[1,6,8,512]{3,2,1,0:T(8,128)(2,1)S(1)} %get-tuple-element.27), channel_id=1, source_target_pairs={{0,12},{1,13},{2,14},{3,15},{4,8},{5,9},{6,10},{7,11},{8,4},{9,5},... | collective-permute-start | bytes 147464 | tf_op jit(solution)/shard_map/ppermute | solution.py:209
  28.3 1.0 %fusion.59 = bf16[1,32,8,512]{3,2,1,0:T(8,128)(2,1)S(1)} fusion(bf16[1,10,512]{2,1,0:T(8,128)(2,1)S(1)} %copy.37, bf16[32,10,512]{2,1,0:T(8,128)(2,1)S(1)} %maximum_bitcast_fusion.1, f32[32,8]{1,0:T(8,128)S(1)} %copy.39, f32[32,8]{1,0:T(8,128)S(1)} %copy.38, f32[32,8]{1,0:T(8,128)S(1)} %copy.36, f32[32,8]{1,0:T(8,128)S(1)} %copy.35, f32[32,8]{1,0:T(8,128)S(1)} %copy.34, ...), kind=kLoop, calls=%fused_computation.127 | loop fusion | flops 5898240 | bytes 1753088 | tf_op jit(solution)/shard_map/broadcast_in_dim | solution.py:230
  29.5 4.4 %collective-permute-start.9 = (bf16[1,32,3,512]{3,2,1,0:T(4,128)(2,1)S(1)}, bf16[1,32,3,512]{3,2,1,0:T(4,128)(2,1)S(1)}, u32[]{:S(2)}, u32[]{:S(2)}) collective-permute-start(bf16[1,32,3,512]{3,2,1,0:T(4,128)(2,1)S(1)} %get-tuple-element.17), channel_id=1, source_target_pairs={{1,0},{2,1},{3,2},{4,3},{5,4},{6,5},{7,6},{8,7},{9,8},{10,9},{11,1... | collective-permute-start | bytes 294920 | tf_op jit(solution)/shard_map/ppermute | solution.py:20
  33.9 1.0 %convolution_convert_fusion.2.q_ref = bf16[256,512]{1,0:T(8,128)(2,1)} fusion(bf16[512,512]{1,0:T(8,128)(2,1)S(1)} %copy-done, bf16[32,8,512]{2,1,0:T(8,128)(2,1)S(1)} %add_convert_fusion), kind=kOutput, calls=%fused_computation.14 | convolution fusion | flops 134348800 | bytes 1048576 | tf_op jit(solution)/shard_map/dot_general | solution.py:76
  35.0 0.6 gather_fusion.2
  35.6 0.8 %bitcast_select_fusion.2 = bf16[4,1,6,8,512]{4,3,2,0,1:T(8,128)(2,1)} fusion(bf16[4,6,8,512]{3,2,1,0:T(8,128)(2,1)S(1)} %gather_fusion.2, pred[4]{0:T(512)(128)(4,1)S(1)} %compare_and_fusion), kind=kLoop, calls=%fused_computation.59 | loop fusion | flops 98304 | bytes 393220 | tf_op jit(solution)/shard_map/jit(_take)/select_n | solution.py:211
  36.4 1.9 %collective-permute-start.15 = (bf16[4,1,6,8,512]{4,3,2,0,1:T(8,128)(2,1)}, bf16[4,1,6,8,512]{4,3,2,0,1:T(8,128)(2,1)}, u32[]{:S(2)}, u32[]{:S(2)}) collective-permute-start(bf16[4,1,6,8,512]{4,3,2,0,1:T(8,128)(2,1)} %bitcast_select_fusion.2), channel_id=1, source_target_pairs={{0,3},{1,2},{2,1},{3,0},{4,7},{5,6},{6,5},{7,4},{8,11},{9,10},{10,... | collective-permute-start | bytes 589832 | tf_op jit(solution)/shard_map/ppermute | solution.py:209
  38.3 0.3 pad_maximum_fusion.2
  38.6 0.1 reshape_squeeze.3
  38.7 1.2 %convolution_convert_fusion.vc_ref = bf16[448,512]{1,0:T(8,128)(2,1)} fusion(bf16[448,512]{1,0:T(8,128)(2,1)S(1)} %reshape_squeeze.3, bf16[512,512]{1,0:T(8,128)(2,1)S(1)} %copy-done.2), kind=kOutput, calls=%fused_computation.12 | convolution fusion | flops 235110400 | bytes 1441792 | tf_op jit(solution)/shard_map/dot_general | solution.py:76
  39.9 1.2 %convolution_convert_fusion.1.kc_ref = bf16[448,512]{1,0:T(8,128)(2,1)} fusion(bf16[448,512]{1,0:T(8,128)(2,1)S(1)} %reshape_squeeze.3, bf16[512,512]{1,0:T(8,128)(2,1)S(1)} %copy-done.1), kind=kOutput, calls=%fused_computation.13 | convolution fusion | flops 235110400 | bytes 1441792 | tf_op jit(solution)/shard_map/dot_general | solution.py:76
  41.1 3.2 %collective-permute-done.14 = bf16[4,1,6,8,512]{4,3,2,0,1:T(8,128)(2,1)S(1)} collective-permute-done((bf16[4,1,6,8,512]{4,3,2,0,1:T(8,128)(2,1)}, bf16[4,1,6,8,512]{4,3,2,0,1:T(8,128)(2,1)S(1)}, u32[]{:S(2)}, u32[]{:S(2)}) %collective-permute-start.14) | collective-permute-done | bytes 196640 | tf_op jit(solution)/shard_map/ppermute | solution.py:209
  44.3 3.5 %collective-permute-done.15 = bf16[4,1,6,8,512]{4,3,2,0,1:T(8,128)(2,1)} collective-permute-done((bf16[4,1,6,8,512]{4,3,2,0,1:T(8,128)(2,1)}, bf16[4,1,6,8,512]{4,3,2,0,1:T(8,128)(2,1)}, u32[]{:S(2)}, u32[]{:S(2)}) %collective-permute-start.15) | collective-permute-done | bytes 196640 | tf_op jit(solution)/shard_map/ppermute | solution.py:209
  47.9 1.0 %maximum_bitcast_fusion = bf16[4,4,6,8,512]{4,3,2,1,0:T(8,128)(2,1)S(1)} fusion(bf16[1,4,1,6,8,512]{5,4,3,1,2,0:T(8,128)(2,1)} %bitcast.46, bf16[1,4,1,6,8,512]{5,4,3,1,2,0:T(8,128)(2,1)S(1)} %bitcast.117, bf16[1,4,1,6,8,512]{5,4,3,1,2,0:T(8,128)(2,1)S(1)} %bitcast.116, bf16[1,4,1,6,8,512]{5,4,3,1,2,0:T(8,128)(2,1)S(1)} %bitcast_select_fusion.3), kind=kLoop, calls=%fused_computation.19 | loop fusion | flops 1179648 | bytes 1572864 | tf_op jit(solution)/shard_map/stack | solution.py:211
  48.9 0.6 gather_fusion.3
  49.5 0.1 fusion.13
  49.6 0.6 %copy.40 = bf16[4,4,1,6,8,512]{5,1,0,4,3,2:T(4,128)(2,1)S(1)} copy(bf16[4,4,1,6,8,512]{5,4,3,0,1,2:T(8,128)(2,1)S(1)} %fusion.13) | data formatting | bytes 1572864 | tf_op jit(solution)/shard_map/transpose | solution.py:213
  50.3 0.2 reshape.199
  50.4 0.4 fusion.46
  50.8 0.2 fusion.45
  51.0 0.3 fusion
  51.3 0.1 slice_bitcast_fusion.1
  51.4 0.6 copy-done.6
  52.0 0.4 fusion.9
  52.4 0.2 broadcast_select_fusion
  52.6 0.1 broadcast_select_fusion.1
  52.8 0.7 %pad.4.rim_ref = bf16[192,512]{1,0:T(8,128)(2,1)} pad(bf16[84,512]{1,0:T(8,128)(2,1)S(1)} %reshape.200, bf16[]{:T(256)} %constant.139.clone.1), padding=0_108x0_0 | pad | bytes 282626 | tf_op jit(solution)/shard_map/jit(_pad)/pad | solution.py:154
  53.5 7.5 %shard_map.82 = bf16[256,512]{1,0:T(8,128)(2,1)} custom-call(bf16[256,512]{1,0:T(8,128)(2,1)} %convolution_convert_fusion.2.q_ref, bf16[448,512]{1,0:T(8,128)(2,1)} %convolution_convert_fusion.1.kc_ref, bf16[448,512]{1,0:T(8,128)(2,1)} %convolution_convert_fusion.vc_ref, bf16[192,512]{1,0:T(8,128)(2,1)} %pad.4.rim_ref, bf16[512,512]{1,0:T(8,128)(2,1)} %wk_ref.1, ...), custom_call_target="tpu_custom_call" | custom-call | tf_op jit(solution)/shard_map/pallas_call | solution.py:156
  (77 shorter events, 2.0 us)
Async XLA Ops:
  0.0 33.9 %copy-start = (bf16[512,512]{1,0:T(8,128)(2,1)S(1)}, bf16[512,512]{1,0:T(8,128)(2,1)}, u32[]{:S(2)}) copy-start(bf16[512,512]{1,0:T(8,128)(2,1)} %param.11) | copy-start | bytes 1572868
  0.0 13.7 %copy-start.4 = (s32[1,2,3]{2,1,0:T(2,128)S(1)}, s32[1,2,3]{2,1,0:T(2,128)}, u32[]{:S(2)}) copy-start(s32[1,2,3]{2,1,0:T(2,128)} %param.15) | copy-start | bytes 76
  0.0 14.2 %copy-start.3 = (f32[1,9,32,8]{2,3,1,0:T(8,128)S(1)}, f32[1,9,32,8]{2,3,1,0:T(8,128)}, u32[]{:S(2)}) copy-start(f32[1,9,32,8]{2,3,1,0:T(8,128)} %param.10) | copy-start | bytes 27652
  2.3 12.7 %collective-permute-start = (bf16[1,2,8,512]{3,2,1,0:T(8,128)(2,1)S(1)}, bf16[1,2,8,512]{3,2,1,0:T(8,128)(2,1)S(1)}, u32[]{:S(2)}, u32[]{:S(2)}) collective-permute-start(bf16[1,2,8,512]{3,2,1,0:T(8,128)(2,1)S(1)} %get-tuple-element.40), channel_id=1, source_target_pairs={{0,4},{1,5},{2,6},{3,7},{4,0},{5,1},{6,2},{7,3},{8,12},{9,13},{10,... | collective-permute-start | bytes 49160 | tf_op jit(solution)/shard_map/ppermute | solution.py:209
  5.4 9.6 %collective-permute-start.1 = (bf16[1,2,8,512]{3,2,1,0:T(8,128)(2,1)S(1)}, bf16[1,2,8,512]{3,2,1,0:T(8,128)(2,1)S(1)}, u32[]{:S(2)}, u32[]{:S(2)}) collective-permute-start(bf16[1,2,8,512]{3,2,1,0:T(8,128)(2,1)S(1)} %get-tuple-element.40), channel_id=1, source_target_pairs={{0,8},{1,9},{2,10},{3,11},{4,12},{5,13},{6,14},{7,15},{8,0},{9,1},... | collective-permute-start | bytes 49160 | tf_op jit(solution)/shard_map/ppermute | solution.py:209
  8.0 7.0 %collective-permute-start.2 = (bf16[1,2,8,512]{3,2,1,0:T(8,128)(2,1)S(1)}, bf16[1,2,8,512]{3,2,1,0:T(8,128)(2,1)S(1)}, u32[]{:S(2)}, u32[]{:S(2)}) collective-permute-start(bf16[1,2,8,512]{3,2,1,0:T(8,128)(2,1)S(1)} %get-tuple-element.40), channel_id=1, source_target_pairs={{0,12},{1,13},{2,14},{3,15},{4,8},{5,9},{6,10},{7,11},{8,4},{9,5},... | collective-permute-start | bytes 49160 | tf_op jit(solution)/shard_map/ppermute | solution.py:209
  9.2 8.4 %collective-permute-start.6 = (bf16[1,32,1,512]{3,2,1,0:T(2,128)(2,1)S(1)}, bf16[1,32,1,512]{3,2,1,0:T(2,128)(2,1)S(1)}, u32[]{:S(2)}, u32[]{:S(2)}) collective-permute-start(bf16[1,32,1,512]{3,2,1,0:T(2,128)(2,1)S(1)} %get-tuple-element.24), channel_id=1, source_target_pairs={{0,1},{1,2},{2,3},{3,4},{4,5},{5,6},{6,7},{7,8},{8,9},{9,10},{10,1... | collective-permute-start | bytes 98312 | tf_op jit(solution)/shard_map/ppermute | solution.py:19
  9.2 8.4 %collective-permute-start.7 = (bf16[1,32,1,512]{3,2,1,0:T(2,128)(2,1)S(1)}, bf16[1,32,1,512]{3,2,1,0:T(2,128)(2,1)S(1)}, u32[]{:S(2)}, u32[]{:S(2)}) collective-permute-start(bf16[1,32,1,512]{3,2,1,0:T(2,128)(2,1)S(1)} %get-tuple-element.25), channel_id=1, source_target_pairs={{1,0},{2,1},{3,2},{4,3},{5,4},{6,5},{7,6},{8,7},{9,8},{10,9},{11,1... | collective-permute-start | bytes 98312 | tf_op jit(solution)/shard_map/ppermute | solution.py:20
  14.1 8.1 %copy-start.5 = (pred[2,2]{0,1:T(4,128)(4,1)}, pred[2,2]{0,1:T(4,128)(4,1)S(1)}, u32[]{:S(2)}) copy-start(pred[2,2]{0,1:T(4,128)(4,1)S(1)} %iota_compare_fusion) | copy-start | bytes 16
  14.2 8.0 %copy-start.7 = (pred[2,16]{1,0:T(4,128)(4,1)}, pred[2,16]{1,0:T(4,128)(4,1)S(1)}, u32[]{:S(2)}) copy-start(pred[2,16]{1,0:T(4,128)(4,1)S(1)} %iota_compare_fusion.1) | copy-start | bytes 100
  15.7 2.2 %collective-permute-start.3 = (bf16[4,1,2,8,512]{4,3,2,0,1:T(8,128)(2,1)S(1)}, bf16[4,1,2,8,512]{4,3,2,0,1:T(8,128)(2,1)S(1)}, u32[]{:S(2)}, u32[]{:S(2)}) collective-permute-start(bf16[4,1,2,8,512]{4,3,2,0,1:T(8,128)(2,1)S(1)} %bitcast_select_fusion.4), channel_id=1, source_target_pairs={{0,1},{1,0},{2,3},{3,2},{4,5},{5,4},{6,7},{7,6},{8,9},{9,8},{10,11... | collective-permute-start | bytes 196616 | tf_op jit(solution)/shard_map/ppermute | solution.py:209
  15.7 5.0 %collective-permute-start.4 = (bf16[4,1,2,8,512]{4,3,2,0,1:T(8,128)(2,1)S(1)}, bf16[4,1,2,8,512]{4,3,2,0,1:T(8,128)(2,1)S(1)}, u32[]{:S(2)}, u32[]{:S(2)}) collective-permute-start(bf16[4,1,2,8,512]{4,3,2,0,1:T(8,128)(2,1)S(1)} %bitcast_select_fusion.4), channel_id=1, source_target_pairs={{0,2},{1,3},{2,0},{3,1},{4,6},{5,7},{6,4},{7,5},{8,10},{9,11},{10,... | collective-permute-start | bytes 196616 | tf_op jit(solution)/shard_map/ppermute | solution.py:209
  15.8 5.3 %collective-permute-start.5 = (bf16[4,1,2,8,512]{4,3,2,0,1:T(8,128)(2,1)S(1)}, bf16[4,1,2,8,512]{4,3,2,0,1:T(8,128)(2,1)S(1)}, u32[]{:S(2)}, u32[]{:S(2)}) collective-permute-start(bf16[4,1,2,8,512]{4,3,2,0,1:T(8,128)(2,1)S(1)} %bitcast_select_fusion.4), channel_id=1, source_target_pairs={{0,3},{1,2},{2,1},{3,0},{4,7},{5,6},{6,5},{7,4},{8,11},{9,10},{10,... | collective-permute-start | bytes 196616 | tf_op jit(solution)/shard_map/ppermute | solution.py:209
  23.8 11.1 %collective-permute-start.10 = (bf16[1,6,8,512]{3,2,1,0:T(8,128)(2,1)S(1)}, bf16[1,6,8,512]{3,2,1,0:T(8,128)(2,1)S(1)}, u32[]{:S(2)}, u32[]{:S(2)}) collective-permute-start(bf16[1,6,8,512]{3,2,1,0:T(8,128)(2,1)S(1)} %get-tuple-element.27), channel_id=1, source_target_pairs={{0,4},{1,5},{2,6},{3,7},{4,0},{5,1},{6,2},{7,3},{8,12},{9,13},{10,... | collective-permute-start | bytes 147464 | tf_op jit(solution)/shard_map/ppermute | solution.py:209
  23.9 11.0 %collective-permute-start.11 = (bf16[1,6,8,512]{3,2,1,0:T(8,128)(2,1)S(1)}, bf16[1,6,8,512]{3,2,1,0:T(8,128)(2,1)S(1)}, u32[]{:S(2)}, u32[]{:S(2)}) collective-permute-start(bf16[1,6,8,512]{3,2,1,0:T(8,128)(2,1)S(1)} %get-tuple-element.27), channel_id=1, source_target_pairs={{0,8},{1,9},{2,10},{3,11},{4,12},{5,13},{6,14},{7,15},{8,0},{9,1},... | collective-permute-start | bytes 147464 | tf_op jit(solution)/shard_map/ppermute | solution.py:209
  26.5 8.5 %collective-permute-start.12 = (bf16[1,6,8,512]{3,2,1,0:T(8,128)(2,1)S(1)}, bf16[1,6,8,512]{3,2,1,0:T(8,128)(2,1)S(1)}, u32[]{:S(2)}, u32[]{:S(2)}) collective-permute-start(bf16[1,6,8,512]{3,2,1,0:T(8,128)(2,1)S(1)} %get-tuple-element.27), channel_id=1, source_target_pairs={{0,12},{1,13},{2,14},{3,15},{4,8},{5,9},{6,10},{7,11},{8,4},{9,5},... | collective-permute-start | bytes 147464 | tf_op jit(solution)/shard_map/ppermute | solution.py:209
  29.4 8.9 %collective-permute-start.8 = (bf16[1,32,3,512]{3,2,1,0:T(4,128)(2,1)S(1)}, bf16[1,32,3,512]{3,2,1,0:T(4,128)(2,1)S(1)}, u32[]{:S(2)}, u32[]{:S(2)}) collective-permute-start(bf16[1,32,3,512]{3,2,1,0:T(4,128)(2,1)S(1)} %get-tuple-element.16), channel_id=1, source_target_pairs={{0,1},{1,2},{2,3},{3,4},{4,5},{5,6},{6,7},{7,8},{8,9},{9,10},{10,1... | collective-permute-start | bytes 294920 | tf_op jit(solution)/shard_map/ppermute | solution.py:19
  29.5 8.8 %collective-permute-start.9 = (bf16[1,32,3,512]{3,2,1,0:T(4,128)(2,1)S(1)}, bf16[1,32,3,512]{3,2,1,0:T(4,128)(2,1)S(1)}, u32[]{:S(2)}, u32[]{:S(2)}) collective-permute-start(bf16[1,32,3,512]{3,2,1,0:T(4,128)(2,1)S(1)} %get-tuple-element.17), channel_id=1, source_target_pairs={{1,0},{2,1},{3,2},{4,3},{5,4},{6,5},{7,6},{8,7},{9,8},{10,9},{11,1... | collective-permute-start | bytes 294920 | tf_op jit(solution)/shard_map/ppermute | solution.py:20
  35.5 3.2 %copy-start.2 = (bf16[512,512]{1,0:T(8,128)(2,1)S(1)}, bf16[512,512]{1,0:T(8,128)(2,1)}, u32[]{:S(2)}) copy-start(bf16[512,512]{1,0:T(8,128)(2,1)} %wv_ref.1) | copy-start | bytes 1572868
  36.4 4.7 %collective-permute-start.13 = (bf16[4,1,6,8,512]{4,3,2,0,1:T(8,128)(2,1)}, bf16[4,1,6,8,512]{4,3,2,0,1:T(8,128)(2,1)S(1)}, u32[]{:S(2)}, u32[]{:S(2)}) collective-permute-start(bf16[4,1,6,8,512]{4,3,2,0,1:T(8,128)(2,1)} %bitcast_select_fusion.2), channel_id=1, source_target_pairs={{0,1},{1,0},{2,3},{3,2},{4,5},{5,4},{6,7},{7,6},{8,9},{9,8},{10,11... | collective-permute-start | bytes 589832 | tf_op jit(solution)/shard_map/ppermute | solution.py:209
  36.4 7.9 %collective-permute-start.14 = (bf16[4,1,6,8,512]{4,3,2,0,1:T(8,128)(2,1)}, bf16[4,1,6,8,512]{4,3,2,0,1:T(8,128)(2,1)S(1)}, u32[]{:S(2)}, u32[]{:S(2)}) collective-permute-start(bf16[4,1,6,8,512]{4,3,2,0,1:T(8,128)(2,1)} %bitcast_select_fusion.2), channel_id=1, source_target_pairs={{0,2},{1,3},{2,0},{3,1},{4,6},{5,7},{6,4},{7,5},{8,10},{9,11},{10,... | collective-permute-start | bytes 589832 | tf_op jit(solution)/shard_map/ppermute | solution.py:209
  36.4 11.5 %collective-permute-start.15 = (bf16[4,1,6,8,512]{4,3,2,0,1:T(8,128)(2,1)}, bf16[4,1,6,8,512]{4,3,2,0,1:T(8,128)(2,1)}, u32[]{:S(2)}, u32[]{:S(2)}) collective-permute-start(bf16[4,1,6,8,512]{4,3,2,0,1:T(8,128)(2,1)} %bitcast_select_fusion.2), channel_id=1, source_target_pairs={{0,3},{1,2},{2,1},{3,0},{4,7},{5,6},{6,5},{7,4},{8,11},{9,10},{10,... | collective-permute-start | bytes 589832 | tf_op jit(solution)/shard_map/ppermute | solution.py:209
  38.6 1.4 %copy-start.1 = (bf16[512,512]{1,0:T(8,128)(2,1)S(1)}, bf16[512,512]{1,0:T(8,128)(2,1)}, u32[]{:S(2)}) copy-start(bf16[512,512]{1,0:T(8,128)(2,1)} %wk_ref.1) | copy-start | bytes 1572868
  51.3 0.7 %copy-start.6 = (pred[2,2]{0,1:T(4,128)(4,1)S(1)}, pred[2,2]{0,1:T(4,128)(4,1)}, u32[]{:S(2)}) copy-start(pred[2,2]{0,1:T(4,128)(4,1)} %copy-done.5) | copy-start | bytes 16
  51.3 0.7 %copy-start.8 = (pred[2,16]{1,0:T(4,128)(4,1)S(1)}, pred[2,16]{1,0:T(4,128)(4,1)}, u32[]{:S(2)}) copy-start(pred[2,16]{1,0:T(4,128)(4,1)} %copy-done.7) | copy-start | bytes 100

commit v19 on v17

--- a/solution.py
+++ b/solution.py
@@ -210,12 +210,15 @@
 def local(latents, norm_gain, metric, w_query, w_key, w_value, w_output, seam_table):
     own_tile = latents[0]
     channels = own_tile.shape[-1]
+    seam_rows = seam_table[0]
+    edges_raw = jnp.stack([own_tile[0], own_tile[-1]])
+    got1 = normalize(doubling_gather(edges_raw[None], "blk"), norm_gain)
+    sides = padded_2(own_tile[None], (("blk", 2),), 1)[0]
     normed = normalize(own_tile, norm_gain)
-    margin = 1
-    seam_rows = seam_table[0]
-    widened = padded_2(normed[None], (("blk", 2),), margin)
-    rows1 = jnp.stack([normed[0], normed[-1]])
-    got1 = widen_tiles(doubling_gather(rows1[None], "blk"), 1)
+    widened = jnp.concatenate(
+        [normalize(sides[:, :1], norm_gain), normed, normalize(sides[:, -1:], norm_gain)], axis=1
+    )[None]
+    got1 = widen_tiles(got1, 1)
     received = pick_all(seam_rows, got1[:, :, None])
     padded = place_rims(widened[0], received, seam_rows)
     smoothed = smooth(padded, metric[0])

time: 59.5 us -> 62.4 us (1.049)
  local copies, waits for them, and re-layouts: 5.38 us -> 9.11 us
    slice x2, local copies, waits for them, and re-layouts: 0.18 us -> 1.22 us  [padded_2(): last = lax.slice_in_dim(array, length - width, length, axis=dim)]
    broadcast_in_dim x1 -> x0, other arithmetic: 1.03 us -> none  [local(): field_wide = padded_2(smoothed[None], (('blk', 2),), RADIUS)]
    mul x10, local copies, waits for them, and re-layouts: 0.68 us -> 1.51 us  [smooth(): metric[stencil, :, :, None]]
    slice x1, local copies, waits for them, and re-layouts: 0.21 us -> 1 us  [orient_rims(): orient = seam_pair[:, 2]]
    slice x1, local copies, waits for them, and re-layouts: 0.01 us -> 0.79 us  [local(): edges_raw = jnp.stack([own_tile[0], own_tile[-1]])]
    convert_element_type x2 -> x3, other arithmetic: 2.17 us -> 1.42 us  [normalize(): return (values * factor * norm_gain).astype(jnp.bfloat16)]
    eq x1, other arithmetic: 0.19 us -> 0.88 us  [orient_rims(): flip_along = (orient % 2 == 1)[:, None, None, None]]
    reduce_sum x1 -> x3, other arithmetic: 1.13 us -> 1.69 us  [normalize(): jnp.mean(values * values, axis=-1, keepdims=True) + 1e-05]
  transfers between devices with their start and end apart: 16 -> 16, of which waited for: 4 -> 4; matrix products, arithmetic and copies ran while one was open for 15% -> 21% of each run, Pallas kernels for 0% -> 0%
where the time goes in v19:
time: 62.4 us; the launch traced here: 62.1 us
  starting transfers between devices  22.8 us (37%)
  local copies, waits for them, and re-layouts  9.11 us (15%)
  waiting for transfers between devices  9.08 us (15%)
  other arithmetic  7.5 us (12%)
  Pallas kernels  7.05 us (11%)
  matrix products  6.02 us (10%)
    ppermute x12, starting transfers between devices, doubling_gather(): lax.ppermute(held, axis, [(i, i ^ d * stride) for i in range(count)])  13.8 us
    ppermute x12, waiting for transfers between devices, doubling_gather(): lax.ppermute(held, axis, [(i, i ^ d * stride) for i in range(count)])  9.07 us
    ppermute x2, starting transfers between devices, padded_2(): after = lax.ppermute(first, axis, down)  8.86 us
    pallas_call x1, Pallas kernels, attend_and_mix(): pl.pallas_call(attention_kernel, out_shape=jax.ShapeDtypeStruct((cells, c...  7.05 us
    dot_general x5, matrix products, project(): jnp.dot(flat, weight, preferred_element_type=jnp.float32)  5.28 us
    gather x4, local copies, waits for them, and re-layouts, doubling_gather(): jnp.take(jnp.stack(got), digit ^ jnp.arange(r, dtype=jnp.int32), axis=0)  2.27 us
    reduce_sum x3, other arithmetic, normalize(): jnp.mean(values * values, axis=-1, keepdims=True) + 1e-05  1.69 us
    mul x10, local copies, waits for them, and re-layouts, smooth(): metric[stencil, :, :, None]  1.51 us
  transfers between devices with their start and end apart: 16, of which 4 were waited for; matrix products, arithmetic and copies ran while one was open for 21% of the time, Pallas kernels for 0%

profile of v19, /device:TPU:0, one launch (start us, length us, event | category | flops | bytes accessed | tf_op | source)
XLA Modules:
  0.0 62.1 jit_solution(5211921614110407933)
XLA Ops:
  0.0 0.8 %slice_bitcast_fusion.3 = (bf16[1,8,512]{2,1,0:T(8,128)(2,1)S(1)}, bf16[1,8,512]{2,1,0:T(8,128)(2,1)S(1)}) fusion(bf16[1,32,8,512]{3,2,1,0:T(8,128)(2,1)} %param.8), kind=kLoop, calls=%fused_computation.78 | loop fusion | bytes 32768 | tf_op jit(solution)/shard_map/slice | solution.py:214
  0.8 3.0 %collective-permute-start = (bf16[1,2,8,512]{3,2,1,0:T(8,128)(2,1)S(1)}, bf16[1,2,8,512]{3,2,1,0:T(8,128)(2,1)S(1)}, u32[]{:S(2)}, u32[]{:S(2)}) collective-permute-start(bf16[1,2,8,512]{3,2,1,0:T(8,128)(2,1)S(1)} %get-tuple-element.46), channel_id=1, source_target_pairs={{0,4},{1,5},{2,6},{3,7},{4,0},{5,1},{6,2},{7,3},{8,12},{9,13},{10,... | collective-permute-start | bytes 49160 | tf_op jit(solution)/shard_map/ppermute | solution.py:202
  3.8 2.6 %collective-permute-start.1 = (bf16[1,2,8,512]{3,2,1,0:T(8,128)(2,1)S(1)}, bf16[1,2,8,512]{3,2,1,0:T(8,128)(2,1)S(1)}, u32[]{:S(2)}, u32[]{:S(2)}) collective-permute-start(bf16[1,2,8,512]{3,2,1,0:T(8,128)(2,1)S(1)} %get-tuple-element.46), channel_id=1, source_target_pairs={{0,8},{1,9},{2,10},{3,11},{4,12},{5,13},{6,14},{7,15},{8,0},{9,1},... | collective-permute-start | bytes 49160 | tf_op jit(solution)/shard_map/ppermute | solution.py:202
  6.4 1.1 %fusion.48 = (bf16[1,32,1,512]{3,2,1,0:T(2,128)(2,1)S(1)}, bf16[1,32,1,512]{3,2,1,0:T(2,128)(2,1)S(1)}) fusion(bf16[1,32,8,512]{3,2,1,0:T(8,128)(2,1)} %param.8), kind=kLoop, calls=%fused_computation.131 | loop fusion | bytes 131072 | tf_op jit(solution)/shard_map/slice | solution.py:17
  7.6 4.4 %collective-permute-start.7 = (bf16[1,32,1,512]{3,2,1,0:T(2,128)(2,1)S(1)}, bf16[1,32,1,512]{3,2,1,0:T(2,128)(2,1)S(1)}, u32[]{:S(2)}, u32[]{:S(2)}) collective-permute-start(bf16[1,32,1,512]{3,2,1,0:T(2,128)(2,1)S(1)} %get-tuple-element.25), channel_id=1, source_target_pairs={{1,0},{2,1},{3,2},{4,3},{5,4},{6,5},{7,6},{8,7},{9,8},{10,9},{11,1... | collective-permute-start | bytes 98312 | tf_op jit(solution)/shard_map/ppermute | solution.py:20
  12.1 1.0 %slice_reduce_fusion.2 = (s32[2]{0:T(128)S(1)}, s32[2]{0:T(128)S(1)}, s32[2]{0:T(128)S(1)}) fusion(s32[2,3]{1,0:T(2,128)} %bitcast.139), kind=kLoop, calls=%fused_computation.116 | loop fusion | bytes 48 | tf_op jit(solution)/shard_map/slice | solution.py:46
  13.1 0.9 %compare_reduce_fusion = pred[2]{0:T(512)(128)(4,1)S(1)} fusion(s32[2,3]{1,0:T(2,128)} %bitcast.140), kind=kLoop, calls=%fused_computation.106 | loop fusion | flops 24 | bytes 10 | tf_op jit(solution)/shard_map/eq | solution.py:47
  14.0 1.1 %fusion.13 = f32[32,8]{1,0:T(8,128)S(1)} fusion(bf16[1,32,8,512]{3,2,1,0:T(8,128)(2,1)} %param.8), kind=kLoop, calls=%fused_computation.31 | loop fusion | flops 392960 | bytes 263168 | tf_op jit(solution)/shard_map/reduce_sum | solution.py:27
  15.2 0.8 %slice_bitcast_fusion.12 = (f32[32,8]{0,1:T(8,128)S(1)}, f32[32,8]{0,1:T(8,128)S(1)}, f32[32,8]{0,1:T(8,128)S(1)}, f32[32,8]{0,1:T(8,128)S(1)}, f32[32,8]{0,1:T(...) fusion(f32[1,9,32,8]{2,3,1,0:T(8,128)} %param.10), kind=kLoop, calls=%fused_computation.91 | loop fusion | bytes 18432 | tf_op jit(solution)/shard_map/mul | solution.py:66
  16.0 1.1 %fusion.15 = bf16[32,8,512]{2,1,0:T(8,128)(2,1)S(1)} fusion(f32[512]{0:T(512)} %param.9, f32[32,8]{1,0:T(8,128)S(1)} %add_rsqrt_fusion, bf16[1,32,8,512]{3,2,1,0:T(8,128)(2,1)} %param.8), kind=kLoop, calls=%fused_computation.33 | loop fusion | flops 524288 | bytes 527360 | tf_op jit(solution)/shard_map/convert_element_type | solution.py:28
  17.9 0.6 gather_fusion
  18.7 1.8 %collective-permute-start.5 = (bf16[4,1,2,8,512]{4,3,2,0,1:T(8,128)(2,1)S(1)}, bf16[4,1,2,8,512]{4,3,2,0,1:T(8,128)(2,1)S(1)}, u32[]{:S(2)}, u32[]{:S(2)}) collective-permute-start(bf16[4,1,2,8,512]{4,3,2,0,1:T(8,128)(2,1)S(1)} %bitcast_select_fusion.4), channel_id=1, source_target_pairs={{0,3},{1,2},{2,1},{3,0},{4,7},{5,6},{6,5},{7,4},{8,11},{9,10},{10,... | collective-permute-start | bytes 196616 | tf_op jit(solution)/shard_map/ppermute | solution.py:202
  20.5 0.3 maximum_bitcast_fusion.1
  20.8 0.4 multiply_reduce_fusion.1
  21.2 0.2 multiply_convert_fusion.2
  21.4 2.2 %collective-permute-done.4 = bf16[4,1,2,8,512]{4,3,2,0,1:T(8,128)(2,1)S(1)} collective-permute-done((bf16[4,1,2,8,512]{4,3,2,0,1:T(8,128)(2,1)S(1)}, bf16[4,1,2,8,512]{4,3,2,0,1:T(8,128)(2,1)S(1)}, u32[]{:S(2)}, u32[]{:S(2)}) %collective-permute-start.4) | collective-permute-done | bytes 65568 | tf_op jit(solution)/shard_map/ppermute | solution.py:202
  23.6 0.5 collective-permute-done.5
  24.1 0.6 gather_fusion.1
  24.8 0.2 fusion.16
  25.0 0.3 copy.42
  25.4 0.2 reshape.249
  25.9 0.3 convolution_bitcast_fusion
  26.3 0.2 reverse.3
  26.5 0.5 maximum_maximum_fusion
  27.1 0.8 %add_convert_fusion = bf16[32,8,512]{2,1,0:T(8,128)(2,1)S(1)} fusion(bf16[32,8,512]{2,1,0:T(8,128)(2,1)S(1)} %fusion.15, bf16[33,10,512]{2,1,0:T(8,128)(2,1)S(1)} %get-tuple-element.19, bf16[32,1,512]{2,1,0:T(2,128)(2,1)S(1)} %get-tuple-element.17, bf16[32,1,512]{2,1,0:T(2,128)(2,1)S(1)} %get-tuple-element.16, ...), kind=kLoop, calls=%fused_computation.37 | loop fusion | flops 4325376 | bytes 2171904 | tf_op jit(solution)/shard_map/convert_element_type | solution.py:69
  27.9 2.6 %collective-permute-start.11 = (bf16[1,6,8,512]{3,2,1,0:T(8,128)(2,1)S(1)}, bf16[1,6,8,512]{3,2,1,0:T(8,128)(2,1)S(1)}, u32[]{:S(2)}, u32[]{:S(2)}) collective-permute-start(bf16[1,6,8,512]{3,2,1,0:T(8,128)(2,1)S(1)} %get-tuple-element.33), channel_id=1, source_target_pairs={{0,8},{1,9},{2,10},{3,11},{4,12},{5,13},{6,14},{7,15},{8,0},{9,1},... | collective-permute-start | bytes 147464 | tf_op jit(solution)/shard_map/ppermute | solution.py:202
  30.5 1.8 %collective-permute-start.12 = (bf16[1,6,8,512]{3,2,1,0:T(8,128)(2,1)S(1)}, bf16[1,6,8,512]{3,2,1,0:T(8,128)(2,1)S(1)}, u32[]{:S(2)}, u32[]{:S(2)}) collective-permute-start(bf16[1,6,8,512]{3,2,1,0:T(8,128)(2,1)S(1)} %get-tuple-element.33), channel_id=1, source_target_pairs={{0,12},{1,13},{2,14},{3,15},{4,8},{5,9},{6,10},{7,11},{8,4},{9,5},... | collective-permute-start | bytes 147464 | tf_op jit(solution)/shard_map/ppermute | solution.py:202
  32.5 4.4 %collective-permute-start.9 = (bf16[1,32,3,512]{3,2,1,0:T(4,128)(2,1)S(1)}, bf16[1,32,3,512]{3,2,1,0:T(4,128)(2,1)S(1)}, u32[]{:S(2)}, u32[]{:S(2)}) collective-permute-start(bf16[1,32,3,512]{3,2,1,0:T(4,128)(2,1)S(1)} %get-tuple-element.23), channel_id=1, source_target_pairs={{1,0},{2,1},{3,2},{4,3},{5,4},{6,5},{7,6},{8,7},{9,8},{10,9},{11,1... | collective-permute-start | bytes 294920 | tf_op jit(solution)/shard_map/ppermute | solution.py:20
  36.9 1.0 %convolution_convert_fusion.2.q_ref = bf16[256,512]{1,0:T(8,128)(2,1)} fusion(bf16[512,512]{1,0:T(8,128)(2,1)S(1)} %copy-done.3, bf16[32,8,512]{2,1,0:T(8,128)(2,1)S(1)} %add_convert_fusion), kind=kOutput, calls=%fused_computation.14 | convolution fusion | flops 134348800 | bytes 1048576 | tf_op jit(solution)/shard_map/dot_general | solution.py:76
  38.0 0.6 gather_fusion.2
  38.9 1.8 %collective-permute-start.15 = (bf16[4,1,6,8,512]{4,3,2,0,1:T(8,128)(2,1)S(1)}, bf16[4,1,6,8,512]{4,3,2,0,1:T(8,128)(2,1)S(1)}, u32[]{:S(2)}, u32[]{:S(2)}) collective-permute-start(bf16[4,1,6,8,512]{4,3,2,0,1:T(8,128)(2,1)S(1)} %bitcast_select_fusion.2), channel_id=1, source_target_pairs={{0,3},{1,2},{2,1},{3,0},{4,7},{5,6},{6,5},{7,4},{8,11},{9,10},{10,... | collective-permute-start | bytes 589832 | tf_op jit(solution)/shard_map/ppermute | solution.py:202
  40.7 0.3 pad_maximum_fusion.3
  41.1 1.2 %convolution_convert_fusion.vc_ref = bf16[448,512]{1,0:T(8,128)(2,1)} fusion(bf16[448,512]{1,0:T(8,128)(2,1)S(1)} %reshape_squeeze.3, bf16[512,512]{1,0:T(8,128)(2,1)S(1)} %copy-done), kind=kOutput, calls=%fused_computation.12 | convolution fusion | flops 235110400 | bytes 1441792 | tf_op jit(solution)/shard_map/dot_general | solution.py:76
  42.3 1.2 %convolution_convert_fusion.1.kc_ref = bf16[448,512]{1,0:T(8,128)(2,1)} fusion(bf16[448,512]{1,0:T(8,128)(2,1)S(1)} %reshape_squeeze.3, bf16[512,512]{1,0:T(8,128)(2,1)S(1)} %copy-done.2), kind=kOutput, calls=%fused_computation.13 | convolution fusion | flops 235110400 | bytes 1441792 | tf_op jit(solution)/shard_map/dot_general | solution.py:76
  43.5 3.1 %collective-permute-done.14 = bf16[4,1,6,8,512]{4,3,2,0,1:T(8,128)(2,1)S(1)} collective-permute-done((bf16[4,1,6,8,512]{4,3,2,0,1:T(8,128)(2,1)S(1)}, bf16[4,1,6,8,512]{4,3,2,0,1:T(8,128)(2,1)S(1)}, u32[]{:S(2)}, u32[]{:S(2)}) %collective-permute-start.14) | collective-permute-done | bytes 196640 | tf_op jit(solution)/shard_map/ppermute | solution.py:202
  46.6 3.3 %collective-permute-done.15 = bf16[4,1,6,8,512]{4,3,2,0,1:T(8,128)(2,1)S(1)} collective-permute-done((bf16[4,1,6,8,512]{4,3,2,0,1:T(8,128)(2,1)S(1)}, bf16[4,1,6,8,512]{4,3,2,0,1:T(8,128)(2,1)S(1)}, u32[]{:S(2)}, u32[]{:S(2)}) %collective-permute-start.15) | collective-permute-done | bytes 196640 | tf_op jit(solution)/shard_map/ppermute | solution.py:202
  50.0 0.6 gather_fusion.3
  50.8 0.4 copy.55
  51.2 0.4 fusion.45
  51.6 0.2 fusion.44
  51.8 0.3 fusion
  52.1 0.1 slice_bitcast_fusion.1
  52.3 0.4 fusion.9
  52.7 0.2 broadcast_select_fusion
  52.9 0.1 broadcast_select_fusion.1
  53.1 1.0 %convolution_convert_fusion.3.vr_ref = bf16[192,512]{1,0:T(8,128)(2,1)} fusion(bf16[512,512]{1,0:T(8,128)(2,1)S(1)} %copy-done, bf16[84,512]{1,0:T(8,128)(2,1)S(1)} %reshape.248), kind=kOutput, calls=%fused_computation.15 | convolution fusion | flops 100761600 | bytes 806912 | tf_op jit(solution)/shard_map/dot_general | solution.py:76
  54.1 1.0 %convolution_convert_fusion.4.kr_ref = bf16[192,512]{1,0:T(8,128)(2,1)} fusion(bf16[512,512]{1,0:T(8,128)(2,1)S(1)} %copy-done.2, bf16[84,512]{1,0:T(8,128)(2,1)S(1)} %reshape.248), kind=kOutput, calls=%fused_computation.16 | convolution fusion | flops 100761600 | bytes 806912 | tf_op jit(solution)/shard_map/dot_general | solution.py:76
  55.0 7.1 %shard_map.82 = bf16[256,512]{1,0:T(8,128)(2,1)} custom-call(bf16[256,512]{1,0:T(8,128)(2,1)} %convolution_convert_fusion.2.q_ref, bf16[448,512]{1,0:T(8,128)(2,1)} %convolution_convert_fusion.1.kc_ref, bf16[192,512]{1,0:T(8,128)(2,1)} %convolution_convert_fusion.4.kr_ref, bf16[448,512]{1,0:T(8,128)(2,1)} %convolution_convert_fusion.vc_ref, ...), custom_call_target="tpu_custom_call" | custom-call | tf_op jit(solution)/shard_map/pallas_call | solution.py:150
  (77 shorter events, 2.8 us)
Async XLA Ops:
  0.0 41.1 %copy-start = (bf16[512,512]{1,0:T(8,128)(2,1)S(1)}, bf16[512,512]{1,0:T(8,128)(2,1)}, u32[]{:S(2)}) copy-start(bf16[512,512]{1,0:T(8,128)(2,1)} %param.13) | copy-start | bytes 1572868
  0.0 20.5 %copy-start.1 = (bf16[1,32,8,512]{3,2,1,0:T(8,128)(2,1)S(1)}, bf16[1,32,8,512]{3,2,1,0:T(8,128)(2,1)}, u32[]{:S(2)}) copy-start(bf16[1,32,8,512]{3,2,1,0:T(8,128)(2,1)} %param.8) | copy-start | bytes 786436
  0.8 17.0 %collective-permute-start = (bf16[1,2,8,512]{3,2,1,0:T(8,128)(2,1)S(1)}, bf16[1,2,8,512]{3,2,1,0:T(8,128)(2,1)S(1)}, u32[]{:S(2)}, u32[]{:S(2)}) collective-permute-start(bf16[1,2,8,512]{3,2,1,0:T(8,128)(2,1)S(1)} %get-tuple-element.46), channel_id=1, source_target_pairs={{0,4},{1,5},{2,6},{3,7},{4,0},{5,1},{6,2},{7,3},{8,12},{9,13},{10,... | collective-permute-start | bytes 49160 | tf_op jit(solution)/shard_map/ppermute | solution.py:202
  3.8 14.0 %collective-permute-start.1 = (bf16[1,2,8,512]{3,2,1,0:T(8,128)(2,1)S(1)}, bf16[1,2,8,512]{3,2,1,0:T(8,128)(2,1)S(1)}, u32[]{:S(2)}, u32[]{:S(2)}) collective-permute-start(bf16[1,2,8,512]{3,2,1,0:T(8,128)(2,1)S(1)} %get-tuple-element.46), channel_id=1, source_target_pairs={{0,8},{1,9},{2,10},{3,11},{4,12},{5,13},{6,14},{7,15},{8,0},{9,1},... | collective-permute-start | bytes 49160 | tf_op jit(solution)/shard_map/ppermute | solution.py:202
  6.4 11.4 %collective-permute-start.2 = (bf16[1,2,8,512]{3,2,1,0:T(8,128)(2,1)S(1)}, bf16[1,2,8,512]{3,2,1,0:T(8,128)(2,1)S(1)}, u32[]{:S(2)}, u32[]{:S(2)}) collective-permute-start(bf16[1,2,8,512]{3,2,1,0:T(8,128)(2,1)S(1)} %get-tuple-element.46), channel_id=1, source_target_pairs={{0,12},{1,13},{2,14},{3,15},{4,8},{5,9},{6,10},{7,11},{8,4},{9,5},... | collective-permute-start | bytes 49160 | tf_op jit(solution)/shard_map/ppermute | solution.py:202
  7.6 12.9 %collective-permute-start.6 = (bf16[1,32,1,512]{3,2,1,0:T(2,128)(2,1)S(1)}, bf16[1,32,1,512]{3,2,1,0:T(2,128)(2,1)S(1)}, u32[]{:S(2)}, u32[]{:S(2)}) collective-permute-start(bf16[1,32,1,512]{3,2,1,0:T(2,128)(2,1)S(1)} %get-tuple-element.24), channel_id=1, source_target_pairs={{0,1},{1,2},{2,3},{3,4},{4,5},{5,6},{6,7},{7,8},{8,9},{9,10},{10,1... | collective-permute-start | bytes 98312 | tf_op jit(solution)/shard_map/ppermute | solution.py:19
  7.6 12.9 %collective-permute-start.7 = (bf16[1,32,1,512]{3,2,1,0:T(2,128)(2,1)S(1)}, bf16[1,32,1,512]{3,2,1,0:T(2,128)(2,1)S(1)}, u32[]{:S(2)}, u32[]{:S(2)}) collective-permute-start(bf16[1,32,1,512]{3,2,1,0:T(2,128)(2,1)S(1)} %get-tuple-element.25), channel_id=1, source_target_pairs={{1,0},{2,1},{3,2},{4,3},{5,4},{6,5},{7,6},{8,7},{9,8},{10,9},{11,1... | collective-permute-start | bytes 98312 | tf_op jit(solution)/shard_map/ppermute | solution.py:20
  13.1 8.1 %copy-start.4 = (f32[512]{0:T(512)S(1)}, f32[512]{0:T(512)}, u32[]{:S(2)}) copy-start(f32[512]{0:T(512)} %param.9) | copy-start | bytes 6148
  18.6 2.8 %collective-permute-start.3 = (bf16[4,1,2,8,512]{4,3,2,0,1:T(8,128)(2,1)S(1)}, bf16[4,1,2,8,512]{4,3,2,0,1:T(8,128)(2,1)S(1)}, u32[]{:S(2)}, u32[]{:S(2)}) collective-permute-start(bf16[4,1,2,8,512]{4,3,2,0,1:T(8,128)(2,1)S(1)} %bitcast_select_fusion.4), channel_id=1, source_target_pairs={{0,1},{1,0},{2,3},{3,2},{4,5},{5,4},{6,7},{7,6},{8,9},{9,8},{10,11... | collective-permute-start | bytes 196616 | tf_op jit(solution)/shard_map/ppermute | solution.py:202
  18.6 5.0 %collective-permute-start.4 = (bf16[4,1,2,8,512]{4,3,2,0,1:T(8,128)(2,1)S(1)}, bf16[4,1,2,8,512]{4,3,2,0,1:T(8,128)(2,1)S(1)}, u32[]{:S(2)}, u32[]{:S(2)}) collective-permute-start(bf16[4,1,2,8,512]{4,3,2,0,1:T(8,128)(2,1)S(1)} %bitcast_select_fusion.4), channel_id=1, source_target_pairs={{0,2},{1,3},{2,0},{3,1},{4,6},{5,7},{6,4},{7,5},{8,10},{9,11},{10,... | collective-permute-start | bytes 196616 | tf_op jit(solution)/shard_map/ppermute | solution.py:202
  18.7 5.4 %collective-permute-start.5 = (bf16[4,1,2,8,512]{4,3,2,0,1:T(8,128)(2,1)S(1)}, bf16[4,1,2,8,512]{4,3,2,0,1:T(8,128)(2,1)S(1)}, u32[]{:S(2)}, u32[]{:S(2)}) collective-permute-start(bf16[4,1,2,8,512]{4,3,2,0,1:T(8,128)(2,1)S(1)} %bitcast_select_fusion.4), channel_id=1, source_target_pairs={{0,3},{1,2},{2,1},{3,0},{4,7},{5,6},{6,5},{7,4},{8,11},{9,10},{10,... | collective-permute-start | bytes 196616 | tf_op jit(solution)/shard_map/ppermute | solution.py:202
  27.1 9.8 %copy-start.3 = (bf16[512,512]{1,0:T(8,128)(2,1)S(1)}, bf16[512,512]{1,0:T(8,128)(2,1)}, u32[]{:S(2)}) copy-start(bf16[512,512]{1,0:T(8,128)(2,1)} %param.11) | copy-start | bytes 1572868
  27.9 10.1 %collective-permute-start.10 = (bf16[1,6,8,512]{3,2,1,0:T(8,128)(2,1)S(1)}, bf16[1,6,8,512]{3,2,1,0:T(8,128)(2,1)S(1)}, u32[]{:S(2)}, u32[]{:S(2)}) collective-permute-start(bf16[1,6,8,512]{3,2,1,0:T(8,128)(2,1)S(1)} %get-tuple-element.33), channel_id=1, source_target_pairs={{0,4},{1,5},{2,6},{3,7},{4,0},{5,1},{6,2},{7,3},{8,12},{9,13},{10,... | collective-permute-start | bytes 147464 | tf_op jit(solution)/shard_map/ppermute | solution.py:202
  27.9 10.0 %collective-permute-start.11 = (bf16[1,6,8,512]{3,2,1,0:T(8,128)(2,1)S(1)}, bf16[1,6,8,512]{3,2,1,0:T(8,128)(2,1)S(1)}, u32[]{:S(2)}, u32[]{:S(2)}) collective-permute-start(bf16[1,6,8,512]{3,2,1,0:T(8,128)(2,1)S(1)} %get-tuple-element.33), channel_id=1, source_target_pairs={{0,8},{1,9},{2,10},{3,11},{4,12},{5,13},{6,14},{7,15},{8,0},{9,1},... | collective-permute-start | bytes 147464 | tf_op jit(solution)/shard_map/ppermute | solution.py:202
  30.5 7.4 %collective-permute-start.12 = (bf16[1,6,8,512]{3,2,1,0:T(8,128)(2,1)S(1)}, bf16[1,6,8,512]{3,2,1,0:T(8,128)(2,1)S(1)}, u32[]{:S(2)}, u32[]{:S(2)}) collective-permute-start(bf16[1,6,8,512]{3,2,1,0:T(8,128)(2,1)S(1)} %get-tuple-element.33), channel_id=1, source_target_pairs={{0,12},{1,13},{2,14},{3,15},{4,8},{5,9},{6,10},{7,11},{8,4},{9,5},... | collective-permute-start | bytes 147464 | tf_op jit(solution)/shard_map/ppermute | solution.py:202
  32.4 8.3 %collective-permute-start.8 = (bf16[1,32,3,512]{3,2,1,0:T(4,128)(2,1)S(1)}, bf16[1,32,3,512]{3,2,1,0:T(4,128)(2,1)S(1)}, u32[]{:S(2)}, u32[]{:S(2)}) collective-permute-start(bf16[1,32,3,512]{3,2,1,0:T(4,128)(2,1)S(1)} %get-tuple-element.22), channel_id=1, source_target_pairs={{0,1},{1,2},{2,3},{3,4},{4,5},{5,6},{6,7},{7,8},{8,9},{9,10},{10,1... | collective-permute-start | bytes 294920 | tf_op jit(solution)/shard_map/ppermute | solution.py:19
  32.5 8.2 %collective-permute-start.9 = (bf16[1,32,3,512]{3,2,1,0:T(4,128)(2,1)S(1)}, bf16[1,32,3,512]{3,2,1,0:T(4,128)(2,1)S(1)}, u32[]{:S(2)}, u32[]{:S(2)}) collective-permute-start(bf16[1,32,3,512]{3,2,1,0:T(4,128)(2,1)S(1)} %get-tuple-element.23), channel_id=1, source_target_pairs={{1,0},{2,1},{3,2},{4,3},{5,4},{6,5},{7,6},{8,7},{9,8},{10,9},{11,1... | collective-permute-start | bytes 294920 | tf_op jit(solution)/shard_map/ppermute | solution.py:20
  38.7 4.8 %collective-permute-start.13 = (bf16[4,1,6,8,512]{4,3,2,0,1:T(8,128)(2,1)S(1)}, bf16[4,1,6,8,512]{4,3,2,0,1:T(8,128)(2,1)S(1)}, u32[]{:S(2)}, u32[]{:S(2)}) collective-permute-start(bf16[4,1,6,8,512]{4,3,2,0,1:T(8,128)(2,1)S(1)} %bitcast_select_fusion.2), channel_id=1, source_target_pairs={{0,1},{1,0},{2,3},{3,2},{4,5},{5,4},{6,7},{7,6},{8,9},{9,8},{10,11... | collective-permute-start | bytes 589832 | tf_op jit(solution)/shard_map/ppermute | solution.py:202
  38.8 7.8 %collective-permute-start.14 = (bf16[4,1,6,8,512]{4,3,2,0,1:T(8,128)(2,1)S(1)}, bf16[4,1,6,8,512]{4,3,2,0,1:T(8,128)(2,1)S(1)}, u32[]{:S(2)}, u32[]{:S(2)}) collective-permute-start(bf16[4,1,6,8,512]{4,3,2,0,1:T(8,128)(2,1)S(1)} %bitcast_select_fusion.2), channel_id=1, source_target_pairs={{0,2},{1,3},{2,0},{3,1},{4,6},{5,7},{6,4},{7,5},{8,10},{9,11},{10,... | collective-permute-start | bytes 589832 | tf_op jit(solution)/shard_map/ppermute | solution.py:202
  38.9 11.0 %collective-permute-start.15 = (bf16[4,1,6,8,512]{4,3,2,0,1:T(8,128)(2,1)S(1)}, bf16[4,1,6,8,512]{4,3,2,0,1:T(8,128)(2,1)S(1)}, u32[]{:S(2)}, u32[]{:S(2)}) collective-permute-start(bf16[4,1,6,8,512]{4,3,2,0,1:T(8,128)(2,1)S(1)} %bitcast_select_fusion.2), channel_id=1, source_target_pairs={{0,3},{1,2},{2,1},{3,0},{4,7},{5,6},{6,5},{7,4},{8,11},{9,10},{10,... | collective-permute-start | bytes 589832 | tf_op jit(solution)/shard_map/ppermute | solution.py:202
  41.0 1.3 %copy-start.2 = (bf16[512,512]{1,0:T(8,128)(2,1)S(1)}, bf16[512,512]{1,0:T(8,128)(2,1)}, u32[]{:S(2)}) copy-start(bf16[512,512]{1,0:T(8,128)(2,1)} %param.12) | copy-start | bytes 1572868

commit v20 on v17

--- a/solution.py
+++ b/solution.py
@@ -94,7 +94,6 @@
     span = 2 * RADIUS + 1
     head_size = channels // HEADS
     group = 128
-    scale = head_size ** (-0.5)
     cell = lax.broadcasted_iota(jnp.int32, (cells, positions), 0)
     place = lax.broadcasted_iota(jnp.int32, (cells, positions), 1)
     rim_rows = RADIUS * wide
@@ -125,7 +124,7 @@
             s = lax.dot_general(
                 q_h, k_g, (((1,), (1,)), ((), ())), preferred_element_type=jnp.float32
             )
-            s = jnp.where(valid, s * scale, -jnp.inf)
+            s = jnp.where(valid, s, -jnp.inf)
             top = jnp.max(s, axis=1, keepdims=True)
             e = jnp.exp(s - top)
             total = jnp.sum(e, axis=1, keepdims=True)
@@ -158,7 +157,7 @@
             pltpu.VMEM((positions, channels), jnp.bfloat16),
         ],
     )(
-        query.reshape(cells, channels),
+        query.reshape(cells, channels) * jnp.asarray((channels // HEADS) ** (-0.5), query.dtype),
         project(center_flat, w_key),
         project(rim_flat, w_key),
         project(center_flat, w_value),

time: 59.5 us -> 59.5 us (level)
  no operation moved by 1% of the time
where the time goes in v20:
time: 59.5 us; the launch traced here: 59.3 us
  starting transfers between devices  22.9 us (38%)
  waiting for transfers between devices  9.7 us (16%)
  other arithmetic  7.75 us (13%)
  Pallas kernels  7.05 us (12%)
  matrix products  5.99 us (10%)
  local copies, waits for them, and re-layouts  5.38 us (9%)
    ppermute x12, starting transfers between devices, doubling_gather(): lax.ppermute(held, axis, [(i, i ^ d * stride) for i in range(count)])  13.9 us
    ppermute x12, waiting for transfers between devices, doubling_gather(): lax.ppermute(held, axis, [(i, i ^ d * stride) for i in range(count)])  9.69 us
    ppermute x2, starting transfers between devices, padded_2(): after = lax.ppermute(first, axis, down)  8.86 us
    pallas_call x1, Pallas kernels, attend_and_mix(): pl.pallas_call(attention_kernel, out_shape=jax.ShapeDtypeStruct((cells, c...  7.05 us
    dot_general x5, matrix products, project(): jnp.dot(flat, weight, preferred_element_type=jnp.float32)  5.25 us
    gather x4, local copies, waits for them, and re-layouts, doubling_gather(): jnp.take(jnp.stack(got), digit ^ jnp.arange(r, dtype=jnp.int32), axis=0)  2.27 us
    convert_element_type x2, other arithmetic, normalize(): return (values * factor * norm_gain).astype(jnp.bfloat16)  2.17 us
  transfers between devices with their start and end apart: 16, of which 4 were waited for; matrix products, arithmetic and copies ran while one was open for 15% of the time, Pallas kernels for 0%

profile of v20, /device:TPU:0, one launch (start us, length us, event | category | flops | bytes accessed | tf_op | source)
XLA Modules:
  0.0 59.3 jit_solution(14364383202660267298)
XLA Ops:
  0.0 1.1 %fusion.15 = f32[32,8]{1,0:T(8,128)S(1)} fusion(bf16[1,32,8,512]{3,2,1,0:T(8,128)(2,1)} %param.8), kind=kLoop, calls=%fused_computation.33 | loop fusion | flops 392960 | bytes 263168 | tf_op jit(solution)/shard_map/reduce_sum | solution.py:27
  1.2 1.1 %fusion.17 = bf16[32,8,512]{2,1,0:T(8,128)(2,1)S(1)} fusion(f32[512]{0:T(512)} %param.9, f32[32,8]{1,0:T(8,128)S(1)} %add_rsqrt_fusion, bf16[1,32,8,512]{3,2,1,0:T(8,128)(2,1)} %param.8), kind=kLoop, calls=%fused_computation.35 | loop fusion | flops 524288 | bytes 527360 | tf_op jit(solution)/shard_map/convert_element_type | solution.py:28
  2.3 3.1 %collective-permute-start = (bf16[1,2,8,512]{3,2,1,0:T(8,128)(2,1)S(1)}, bf16[1,2,8,512]{3,2,1,0:T(8,128)(2,1)S(1)}, u32[]{:S(2)}, u32[]{:S(2)}) collective-permute-start(bf16[1,2,8,512]{3,2,1,0:T(8,128)(2,1)S(1)} %get-tuple-element.40), channel_id=1, source_target_pairs={{0,4},{1,5},{2,6},{3,7},{4,0},{5,1},{6,2},{7,3},{8,12},{9,13},{10,... | collective-permute-start | bytes 49160 | tf_op jit(solution)/shard_map/ppermute | solution.py:201
  5.4 2.6 %collective-permute-start.1 = (bf16[1,2,8,512]{3,2,1,0:T(8,128)(2,1)S(1)}, bf16[1,2,8,512]{3,2,1,0:T(8,128)(2,1)S(1)}, u32[]{:S(2)}, u32[]{:S(2)}) collective-permute-start(bf16[1,2,8,512]{3,2,1,0:T(8,128)(2,1)S(1)} %get-tuple-element.40), channel_id=1, source_target_pairs={{0,8},{1,9},{2,10},{3,11},{4,12},{5,13},{6,14},{7,15},{8,0},{9,1},... | collective-permute-start | bytes 49160 | tf_op jit(solution)/shard_map/ppermute | solution.py:201
  8.0 1.1 %multiply_convert_fusion = bf16[1,32,8,512]{3,2,1,0:T(8,128)(2,1)S(1)} fusion(bf16[1,32,8,512]{3,2,1,0:T(8,128)(2,1)} %param.8, f32[512]{0:T(512)} %param.9, f32[32,8]{1,0:T(8,128)S(1)} %add_rsqrt_fusion), kind=kLoop, calls=%fused_computation.39 | loop fusion | flops 524288 | bytes 527360 | tf_op jit(solution)/shard_map/convert_element_type | solution.py:28
  9.2 4.4 %collective-permute-start.7 = (bf16[1,32,1,512]{3,2,1,0:T(2,128)(2,1)S(1)}, bf16[1,32,1,512]{3,2,1,0:T(2,128)(2,1)S(1)}, u32[]{:S(2)}, u32[]{:S(2)}) collective-permute-start(bf16[1,32,1,512]{3,2,1,0:T(2,128)(2,1)S(1)} %get-tuple-element.25), channel_id=1, source_target_pairs={{1,0},{2,1},{3,2},{4,3},{5,4},{6,5},{7,6},{8,7},{9,8},{10,9},{11,1... | collective-permute-start | bytes 98312 | tf_op jit(solution)/shard_map/ppermute | solution.py:20
  13.7 0.2 slice_reduce_fusion.2
  13.9 0.2 compare_reduce_fusion
  15.0 0.6 gather_fusion
  15.7 0.1 collective-permute-start.4
  15.8 1.7 %collective-permute-start.5 = (bf16[4,1,2,8,512]{4,3,2,0,1:T(8,128)(2,1)S(1)}, bf16[4,1,2,8,512]{4,3,2,0,1:T(8,128)(2,1)S(1)}, u32[]{:S(2)}, u32[]{:S(2)}) collective-permute-start(bf16[4,1,2,8,512]{4,3,2,0,1:T(8,128)(2,1)S(1)} %bitcast_select_fusion.4), channel_id=1, source_target_pairs={{0,3},{1,2},{2,1},{3,0},{4,7},{5,6},{6,5},{7,4},{8,11},{9,10},{10,... | collective-permute-start | bytes 196616 | tf_op jit(solution)/shard_map/ppermute | solution.py:201
  17.6 0.3 maximum_bitcast_fusion.1
  17.9 2.8 %collective-permute-done.4 = bf16[4,1,2,8,512]{4,3,2,0,1:T(8,128)(2,1)S(1)} collective-permute-done((bf16[4,1,2,8,512]{4,3,2,0,1:T(8,128)(2,1)S(1)}, bf16[4,1,2,8,512]{4,3,2,0,1:T(8,128)(2,1)S(1)}, u32[]{:S(2)}, u32[]{:S(2)}) %collective-permute-start.4) | collective-permute-done | bytes 65568 | tf_op jit(solution)/shard_map/ppermute | solution.py:201
  20.7 0.5 collective-permute-done.5
  21.2 0.6 gather_fusion.1
  21.8 0.1 fusion.30
  21.9 0.2 copy.24
  22.2 0.3 fusion.13
  22.7 1.1 %add_convert_fusion = bf16[32,8,512]{2,1,0:T(8,128)(2,1)S(1)} fusion(bf16[32,10,512]{2,1,0:T(8,128)(2,1)S(1)} %maximum_bitcast_fusion.1, bf16[1,10,512]{2,1,0:T(8,128)(2,1)S(1)} %copy.36, bf16[1,10,512]{2,1,0:T(8,128)(2,1)S(1)} %copy.29, f32[32,8]{1,0:T(8,128)S(1)} %copy.38, f32[32,8]{1,0:T(8,128)S(1)} %copy.37, f32[32,8]{1,0:T(8,128)S(1)} %copy.35, ...), kind=kLoop, calls=%fused_computation.38 | loop fusion | flops 5898240 | bytes 1753088 | tf_op jit(solution)/shard_map/convert_element_type | solution.py:69
  23.9 2.6 %collective-permute-start.11 = (bf16[1,6,8,512]{3,2,1,0:T(8,128)(2,1)S(1)}, bf16[1,6,8,512]{3,2,1,0:T(8,128)(2,1)S(1)}, u32[]{:S(2)}, u32[]{:S(2)}) collective-permute-start(bf16[1,6,8,512]{3,2,1,0:T(8,128)(2,1)S(1)} %get-tuple-element.27), channel_id=1, source_target_pairs={{0,8},{1,9},{2,10},{3,11},{4,12},{5,13},{6,14},{7,15},{8,0},{9,1},... | collective-permute-start | bytes 147464 | tf_op jit(solution)/shard_map/ppermute | solution.py:201
  26.4 1.8 %collective-permute-start.12 = (bf16[1,6,8,512]{3,2,1,0:T(8,128)(2,1)S(1)}, bf16[1,6,8,512]{3,2,1,0:T(8,128)(2,1)S(1)}, u32[]{:S(2)}, u32[]{:S(2)}) collective-permute-start(bf16[1,6,8,512]{3,2,1,0:T(8,128)(2,1)S(1)} %get-tuple-element.27), channel_id=1, source_target_pairs={{0,12},{1,13},{2,14},{3,15},{4,8},{5,9},{6,10},{7,11},{8,4},{9,5},... | collective-permute-start | bytes 147464 | tf_op jit(solution)/shard_map/ppermute | solution.py:201
  28.2 1.0 %fusion.66 = bf16[1,32,8,512]{3,2,1,0:T(8,128)(2,1)S(1)} fusion(bf16[1,10,512]{2,1,0:T(8,128)(2,1)S(1)} %copy.36, bf16[32,10,512]{2,1,0:T(8,128)(2,1)S(1)} %maximum_bitcast_fusion.1, f32[32,8]{1,0:T(8,128)S(1)} %copy.38, f32[32,8]{1,0:T(8,128)S(1)} %copy.37, f32[32,8]{1,0:T(8,128)S(1)} %copy.35, f32[32,8]{1,0:T(8,128)S(1)} %copy.34, f32[32,8]{1,0:T(8,128)S(1)} %copy.33, ...), kind=kLoop, calls=%fused_computation.134 | loop fusion | flops 5898240 | bytes 1753088 | tf_op jit(solution)/shard_map/broadcast_in_dim | solution.py:222
  29.3 0.1 fusion.53
  29.4 4.4 %collective-permute-start.9 = (bf16[1,32,3,512]{3,2,1,0:T(4,128)(2,1)S(1)}, bf16[1,32,3,512]{3,2,1,0:T(4,128)(2,1)S(1)}, u32[]{:S(2)}, u32[]{:S(2)}) collective-permute-start(bf16[1,32,3,512]{3,2,1,0:T(4,128)(2,1)S(1)} %get-tuple-element.17), channel_id=1, source_target_pairs={{1,0},{2,1},{3,2},{4,3},{5,4},{6,5},{7,6},{8,7},{9,8},{10,9},{11,1... | collective-permute-start | bytes 294920 | tf_op jit(solution)/shard_map/ppermute | solution.py:20
  33.9 1.0 %fusion.6.q_ref = bf16[256,512]{1,0:T(8,128)(2,1)} fusion(bf16[512,512]{1,0:T(8,128)(2,1)S(1)} %copy-done.2, bf16[32,8,512]{2,1,0:T(8,128)(2,1)S(1)} %add_convert_fusion), kind=kOutput, calls=%fused_computation.17 | convolution fusion | flops 134479872 | bytes 1048576 | tf_op jit(solution)/shard_map/dot_general | solution.py:76
  34.9 0.6 gather_fusion.2
  35.9 1.8 %collective-permute-start.15 = (bf16[4,1,6,8,512]{4,3,2,0,1:T(8,128)(2,1)S(1)}, bf16[4,1,6,8,512]{4,3,2,0,1:T(8,128)(2,1)S(1)}, u32[]{:S(2)}, u32[]{:S(2)}) collective-permute-start(bf16[4,1,6,8,512]{4,3,2,0,1:T(8,128)(2,1)S(1)} %bitcast_select_fusion.2), channel_id=1, source_target_pairs={{0,3},{1,2},{2,1},{3,0},{4,7},{5,6},{6,5},{7,4},{8,11},{9,10},{10,... | collective-permute-start | bytes 589832 | tf_op jit(solution)/shard_map/ppermute | solution.py:201
  37.6 0.3 pad_maximum_fusion.2
  37.9 0.1 reshape_squeeze.3
  38.1 1.2 %convolution_convert_fusion.vc_ref = bf16[448,512]{1,0:T(8,128)(2,1)} fusion(bf16[448,512]{1,0:T(8,128)(2,1)S(1)} %reshape_squeeze.3, bf16[512,512]{1,0:T(8,128)(2,1)S(1)} %copy-done), kind=kOutput, calls=%fused_computation.12 | convolution fusion | flops 235110400 | bytes 1441792 | tf_op jit(solution)/shard_map/dot_general | solution.py:76
  39.3 1.2 %convolution_convert_fusion.1.kc_ref = bf16[448,512]{1,0:T(8,128)(2,1)} fusion(bf16[448,512]{1,0:T(8,128)(2,1)S(1)} %reshape_squeeze.3, bf16[512,512]{1,0:T(8,128)(2,1)S(1)} %copy-done.1), kind=kOutput, calls=%fused_computation.13 | convolution fusion | flops 235110400 | bytes 1441792 | tf_op jit(solution)/shard_map/dot_general | solution.py:76
  40.5 3.1 %collective-permute-done.14 = bf16[4,1,6,8,512]{4,3,2,0,1:T(8,128)(2,1)S(1)} collective-permute-done((bf16[4,1,6,8,512]{4,3,2,0,1:T(8,128)(2,1)S(1)}, bf16[4,1,6,8,512]{4,3,2,0,1:T(8,128)(2,1)S(1)}, u32[]{:S(2)}, u32[]{:S(2)}) %collective-permute-start.14) | collective-permute-done | bytes 196640 | tf_op jit(solution)/shard_map/ppermute | solution.py:201
  43.5 3.3 %collective-permute-done.15 = bf16[4,1,6,8,512]{4,3,2,0,1:T(8,128)(2,1)S(1)} collective-permute-done((bf16[4,1,6,8,512]{4,3,2,0,1:T(8,128)(2,1)S(1)}, bf16[4,1,6,8,512]{4,3,2,0,1:T(8,128)(2,1)S(1)}, u32[]{:S(2)}, u32[]{:S(2)}) %collective-permute-start.15) | collective-permute-done | bytes 196640 | tf_op jit(solution)/shard_map/ppermute | solution.py:201
  46.8 0.1 maximum_bitcast_fusion
  47.0 0.6 %gather_fusion.3 = bf16[4,4,6,8,512]{4,3,2,1,0:T(8,128)(2,1)S(1)} fusion(bf16[4,4,6,8,512]{4,3,2,1,0:T(8,128)(2,1)S(1)} %maximum_bitcast_fusion, s32[1024]{0:T(1024)S(1)} %pad_clamp_fusion), kind=kCustom, calls=%fused_computation.3 | custom fusion | bytes 1572880 | tf_op jit(solution)/shard_map/jit(_take)/gather | solution.py:203
  47.6 0.1 fusion.14
  47.7 0.6 %copy.39 = bf16[4,4,1,6,8,512]{5,1,0,4,3,2:T(4,128)(2,1)S(1)} copy(bf16[4,4,1,6,8,512]{5,4,3,0,1,2:T(8,128)(2,1)S(1)} %fusion.14) | data formatting | bytes 1572864 | tf_op jit(solution)/shard_map/transpose | solution.py:205
  48.3 0.2 reshape.199
  48.5 0.4 fusion.51
  48.9 0.2 fusion.50
  49.1 0.3 fusion
  49.4 0.1 slice_bitcast_fusion.1
  49.5 0.4 fusion.10
  50.0 0.2 broadcast_select_fusion
  50.1 0.1 broadcast_select_fusion.1
  50.3 0.9 %convolution_convert_fusion.3.vr_ref = bf16[192,512]{1,0:T(8,128)(2,1)} fusion(bf16[512,512]{1,0:T(8,128)(2,1)S(1)} %copy-done, bf16[84,512]{1,0:T(8,128)(2,1)S(1)} %reshape.200), kind=kOutput, calls=%fused_computation.15 | convolution fusion | flops 100761600 | bytes 806912 | tf_op jit(solution)/shard_map/dot_general | solution.py:76
  51.3 0.9 %convolution_convert_fusion.4.kr_ref = bf16[192,512]{1,0:T(8,128)(2,1)} fusion(bf16[512,512]{1,0:T(8,128)(2,1)S(1)} %copy-done.1, bf16[84,512]{1,0:T(8,128)(2,1)S(1)} %reshape.200), kind=kOutput, calls=%fused_computation.16 | convolution fusion | flops 100761600 | bytes 806912 | tf_op jit(solution)/shard_map/dot_general | solution.py:76
  52.2 7.1 %shard_map.82 = bf16[256,512]{1,0:T(8,128)(2,1)} custom-call(bf16[256,512]{1,0:T(8,128)(2,1)} %fusion.6.q_ref, bf16[448,512]{1,0:T(8,128)(2,1)} %convolution_convert_fusion.1.kc_ref, bf16[192,512]{1,0:T(8,128)(2,1)} %convolution_convert_fusion.4.kr_ref, bf16[448,512]{1,0:T(8,128)(2,1)} %convolution_convert_fusion.vc_ref, ...), custom_call_target="tpu_custom_call" | custom-call | tf_op jit(solution)/shard_map/pallas_call | solution.py:149
  (70 shorter events, 2.1 us)
Async XLA Ops:
  0.0 38.1 %copy-start = (bf16[512,512]{1,0:T(8,128)(2,1)S(1)}, bf16[512,512]{1,0:T(8,128)(2,1)}, u32[]{:S(2)}) copy-start(bf16[512,512]{1,0:T(8,128)(2,1)} %param.13) | copy-start | bytes 1572868
  0.0 13.7 %copy-start.4 = (s32[1,2,3]{2,1,0:T(2,128)S(1)}, s32[1,2,3]{2,1,0:T(2,128)}, u32[]{:S(2)}) copy-start(s32[1,2,3]{2,1,0:T(2,128)} %param.15) | copy-start | bytes 76
  0.0 14.2 %copy-start.3 = (f32[1,9,32,8]{2,3,1,0:T(8,128)S(1)}, f32[1,9,32,8]{2,3,1,0:T(8,128)}, u32[]{:S(2)}) copy-start(f32[1,9,32,8]{2,3,1,0:T(8,128)} %param.10) | copy-start | bytes 27652
  2.3 12.7 %collective-permute-start = (bf16[1,2,8,512]{3,2,1,0:T(8,128)(2,1)S(1)}, bf16[1,2,8,512]{3,2,1,0:T(8,128)(2,1)S(1)}, u32[]{:S(2)}, u32[]{:S(2)}) collective-permute-start(bf16[1,2,8,512]{3,2,1,0:T(8,128)(2,1)S(1)} %get-tuple-element.40), channel_id=1, source_target_pairs={{0,4},{1,5},{2,6},{3,7},{4,0},{5,1},{6,2},{7,3},{8,12},{9,13},{10,... | collective-permute-start | bytes 49160 | tf_op jit(solution)/shard_map/ppermute | solution.py:201
  5.4 9.6 %collective-permute-start.1 = (bf16[1,2,8,512]{3,2,1,0:T(8,128)(2,1)S(1)}, bf16[1,2,8,512]{3,2,1,0:T(8,128)(2,1)S(1)}, u32[]{:S(2)}, u32[]{:S(2)}) collective-permute-start(bf16[1,2,8,512]{3,2,1,0:T(8,128)(2,1)S(1)} %get-tuple-element.40), channel_id=1, source_target_pairs={{0,8},{1,9},{2,10},{3,11},{4,12},{5,13},{6,14},{7,15},{8,0},{9,1},... | collective-permute-start | bytes 49160 | tf_op jit(solution)/shard_map/ppermute | solution.py:201
  8.0 7.0 %collective-permute-start.2 = (bf16[1,2,8,512]{3,2,1,0:T(8,128)(2,1)S(1)}, bf16[1,2,8,512]{3,2,1,0:T(8,128)(2,1)S(1)}, u32[]{:S(2)}, u32[]{:S(2)}) collective-permute-start(bf16[1,2,8,512]{3,2,1,0:T(8,128)(2,1)S(1)} %get-tuple-element.40), channel_id=1, source_target_pairs={{0,12},{1,13},{2,14},{3,15},{4,8},{5,9},{6,10},{7,11},{8,4},{9,5},... | collective-permute-start | bytes 49160 | tf_op jit(solution)/shard_map/ppermute | solution.py:201
  9.2 8.4 %collective-permute-start.6 = (bf16[1,32,1,512]{3,2,1,0:T(2,128)(2,1)S(1)}, bf16[1,32,1,512]{3,2,1,0:T(2,128)(2,1)S(1)}, u32[]{:S(2)}, u32[]{:S(2)}) collective-permute-start(bf16[1,32,1,512]{3,2,1,0:T(2,128)(2,1)S(1)} %get-tuple-element.24), channel_id=1, source_target_pairs={{0,1},{1,2},{2,3},{3,4},{4,5},{5,6},{6,7},{7,8},{8,9},{9,10},{10,1... | collective-permute-start | bytes 98312 | tf_op jit(solution)/shard_map/ppermute | solution.py:19
  9.2 8.4 %collective-permute-start.7 = (bf16[1,32,1,512]{3,2,1,0:T(2,128)(2,1)S(1)}, bf16[1,32,1,512]{3,2,1,0:T(2,128)(2,1)S(1)}, u32[]{:S(2)}, u32[]{:S(2)}) collective-permute-start(bf16[1,32,1,512]{3,2,1,0:T(2,128)(2,1)S(1)} %get-tuple-element.25), channel_id=1, source_target_pairs={{1,0},{2,1},{3,2},{4,3},{5,4},{6,5},{7,6},{8,7},{9,8},{10,9},{11,1... | collective-permute-start | bytes 98312 | tf_op jit(solution)/shard_map/ppermute | solution.py:20
  15.7 2.2 %collective-permute-start.3 = (bf16[4,1,2,8,512]{4,3,2,0,1:T(8,128)(2,1)S(1)}, bf16[4,1,2,8,512]{4,3,2,0,1:T(8,128)(2,1)S(1)}, u32[]{:S(2)}, u32[]{:S(2)}) collective-permute-start(bf16[4,1,2,8,512]{4,3,2,0,1:T(8,128)(2,1)S(1)} %bitcast_select_fusion.4), channel_id=1, source_target_pairs={{0,1},{1,0},{2,3},{3,2},{4,5},{5,4},{6,7},{7,6},{8,9},{9,8},{10,11... | collective-permute-start | bytes 196616 | tf_op jit(solution)/shard_map/ppermute | solution.py:201
  15.7 5.0 %collective-permute-start.4 = (bf16[4,1,2,8,512]{4,3,2,0,1:T(8,128)(2,1)S(1)}, bf16[4,1,2,8,512]{4,3,2,0,1:T(8,128)(2,1)S(1)}, u32[]{:S(2)}, u32[]{:S(2)}) collective-permute-start(bf16[4,1,2,8,512]{4,3,2,0,1:T(8,128)(2,1)S(1)} %bitcast_select_fusion.4), channel_id=1, source_target_pairs={{0,2},{1,3},{2,0},{3,1},{4,6},{5,7},{6,4},{7,5},{8,10},{9,11},{10,... | collective-permute-start | bytes 196616 | tf_op jit(solution)/shard_map/ppermute | solution.py:201
  15.8 5.3 %collective-permute-start.5 = (bf16[4,1,2,8,512]{4,3,2,0,1:T(8,128)(2,1)S(1)}, bf16[4,1,2,8,512]{4,3,2,0,1:T(8,128)(2,1)S(1)}, u32[]{:S(2)}, u32[]{:S(2)}) collective-permute-start(bf16[4,1,2,8,512]{4,3,2,0,1:T(8,128)(2,1)S(1)} %bitcast_select_fusion.4), channel_id=1, source_target_pairs={{0,3},{1,2},{2,1},{3,0},{4,7},{5,6},{6,5},{7,4},{8,11},{9,10},{10,... | collective-permute-start | bytes 196616 | tf_op jit(solution)/shard_map/ppermute | solution.py:201
  23.7 10.1 %copy-start.2 = (bf16[512,512]{1,0:T(8,128)(2,1)S(1)}, bf16[512,512]{1,0:T(8,128)(2,1)}, u32[]{:S(2)}) copy-start(bf16[512,512]{1,0:T(8,128)(2,1)} %param.11) | copy-start | bytes 1572868
  23.8 11.1 %collective-permute-start.10 = (bf16[1,6,8,512]{3,2,1,0:T(8,128)(2,1)S(1)}, bf16[1,6,8,512]{3,2,1,0:T(8,128)(2,1)S(1)}, u32[]{:S(2)}, u32[]{:S(2)}) collective-permute-start(bf16[1,6,8,512]{3,2,1,0:T(8,128)(2,1)S(1)} %get-tuple-element.27), channel_id=1, source_target_pairs={{0,4},{1,5},{2,6},{3,7},{4,0},{5,1},{6,2},{7,3},{8,12},{9,13},{10,... | collective-permute-start | bytes 147464 | tf_op jit(solution)/shard_map/ppermute | solution.py:201
  23.9 11.0 %collective-permute-start.11 = (bf16[1,6,8,512]{3,2,1,0:T(8,128)(2,1)S(1)}, bf16[1,6,8,512]{3,2,1,0:T(8,128)(2,1)S(1)}, u32[]{:S(2)}, u32[]{:S(2)}) collective-permute-start(bf16[1,6,8,512]{3,2,1,0:T(8,128)(2,1)S(1)} %get-tuple-element.27), channel_id=1, source_target_pairs={{0,8},{1,9},{2,10},{3,11},{4,12},{5,13},{6,14},{7,15},{8,0},{9,1},... | collective-permute-start | bytes 147464 | tf_op jit(solution)/shard_map/ppermute | solution.py:201
  26.4 8.5 %collective-permute-start.12 = (bf16[1,6,8,512]{3,2,1,0:T(8,128)(2,1)S(1)}, bf16[1,6,8,512]{3,2,1,0:T(8,128)(2,1)S(1)}, u32[]{:S(2)}, u32[]{:S(2)}) collective-permute-start(bf16[1,6,8,512]{3,2,1,0:T(8,128)(2,1)S(1)} %get-tuple-element.27), channel_id=1, source_target_pairs={{0,12},{1,13},{2,14},{3,15},{4,8},{5,9},{6,10},{7,11},{8,4},{9,5},... | collective-permute-start | bytes 147464 | tf_op jit(solution)/shard_map/ppermute | solution.py:201
  29.4 8.3 %collective-permute-start.8 = (bf16[1,32,3,512]{3,2,1,0:T(4,128)(2,1)S(1)}, bf16[1,32,3,512]{3,2,1,0:T(4,128)(2,1)S(1)}, u32[]{:S(2)}, u32[]{:S(2)}) collective-permute-start(bf16[1,32,3,512]{3,2,1,0:T(4,128)(2,1)S(1)} %get-tuple-element.16), channel_id=1, source_target_pairs={{0,1},{1,2},{2,3},{3,4},{4,5},{5,6},{6,7},{7,8},{8,9},{9,10},{10,1... | collective-permute-start | bytes 294920 | tf_op jit(solution)/shard_map/ppermute | solution.py:19
  29.4 8.2 %collective-permute-start.9 = (bf16[1,32,3,512]{3,2,1,0:T(4,128)(2,1)S(1)}, bf16[1,32,3,512]{3,2,1,0:T(4,128)(2,1)S(1)}, u32[]{:S(2)}, u32[]{:S(2)}) collective-permute-start(bf16[1,32,3,512]{3,2,1,0:T(4,128)(2,1)S(1)} %get-tuple-element.17), channel_id=1, source_target_pairs={{1,0},{2,1},{3,2},{4,3},{5,4},{6,5},{7,6},{8,7},{9,8},{10,9},{11,1... | collective-permute-start | bytes 294920 | tf_op jit(solution)/shard_map/ppermute | solution.py:20
  35.7 4.8 %collective-permute-start.13 = (bf16[4,1,6,8,512]{4,3,2,0,1:T(8,128)(2,1)S(1)}, bf16[4,1,6,8,512]{4,3,2,0,1:T(8,128)(2,1)S(1)}, u32[]{:S(2)}, u32[]{:S(2)}) collective-permute-start(bf16[4,1,6,8,512]{4,3,2,0,1:T(8,128)(2,1)S(1)} %bitcast_select_fusion.2), channel_id=1, source_target_pairs={{0,1},{1,0},{2,3},{3,2},{4,5},{5,4},{6,7},{7,6},{8,9},{9,8},{10,11... | collective-permute-start | bytes 589832 | tf_op jit(solution)/shard_map/ppermute | solution.py:201
  35.8 7.8 %collective-permute-start.14 = (bf16[4,1,6,8,512]{4,3,2,0,1:T(8,128)(2,1)S(1)}, bf16[4,1,6,8,512]{4,3,2,0,1:T(8,128)(2,1)S(1)}, u32[]{:S(2)}, u32[]{:S(2)}) collective-permute-start(bf16[4,1,6,8,512]{4,3,2,0,1:T(8,128)(2,1)S(1)} %bitcast_select_fusion.2), channel_id=1, source_target_pairs={{0,2},{1,3},{2,0},{3,1},{4,6},{5,7},{6,4},{7,5},{8,10},{9,11},{10,... | collective-permute-start | bytes 589832 | tf_op jit(solution)/shard_map/ppermute | solution.py:201
  35.9 11.0 %collective-permute-start.15 = (bf16[4,1,6,8,512]{4,3,2,0,1:T(8,128)(2,1)S(1)}, bf16[4,1,6,8,512]{4,3,2,0,1:T(8,128)(2,1)S(1)}, u32[]{:S(2)}, u32[]{:S(2)}) collective-permute-start(bf16[4,1,6,8,512]{4,3,2,0,1:T(8,128)(2,1)S(1)} %bitcast_select_fusion.2), channel_id=1, source_target_pairs={{0,3},{1,2},{2,1},{3,0},{4,7},{5,6},{6,5},{7,4},{8,11},{9,10},{10,... | collective-permute-start | bytes 589832 | tf_op jit(solution)/shard_map/ppermute | solution.py:201
  37.9 1.3 %copy-start.1 = (bf16[512,512]{1,0:T(8,128)(2,1)S(1)}, bf16[512,512]{1,0:T(8,128)(2,1)}, u32[]{:S(2)}) copy-start(bf16[512,512]{1,0:T(8,128)(2,1)} %param.12) | copy-start | bytes 1572868

commit v21 on v20

--- a/solution.py
+++ b/solution.py
@@ -221,9 +221,16 @@
     query = project(smoothed, w_query)
     field_wide = padded_2(smoothed[None], (("blk", 2),), RADIUS)
     rows3 = jnp.concatenate([smoothed[:RADIUS], smoothed[-RADIUS:]], axis=0)
-    got3 = widen_tiles(doubling_gather(rows3[None], "blk"), RADIUS)
-    edges3 = jnp.stack([got3[:, :RADIUS], got3[:, RADIUS:]], axis=1)
-    field_got = pick_all(seam_rows, edges3)
+    got3 = doubling_gather(rows3[None], "blk")
+    count = got3.shape[0]
+    edges3 = got3.reshape((count, 2, RADIUS) + got3.shape[2:])
+    near = jnp.stack(
+        [seam_rows.at[:, 0].set((seam_rows[:, 0] + count + k) % count) for k in (-1, 0, 1)], axis=1
+    )
+    picked = pick_all(near, edges3)
+    field_got = jnp.concatenate(
+        [picked[:, 0, :, -RADIUS:], picked[:, 1], picked[:, 2, :, :RADIUS]], axis=2
+    )
     arrived = orient_rims(field_got, seam_rows)
     return attend_and_mix(query, field_wide[0], arrived, w_key, w_value, own_tile, w_output)[None]
 

time: 59.5 us -> 57.8 us (0.971); the launches traced: 59.3 us -> 56.9 us
  waiting for transfers between devices: 9.7 us -> 7.08 us
  other arithmetic: 7.75 us -> 6.84 us
  local copies, waits for them, and re-layouts: 5.38 us -> 6.24 us
    ppermute x12, waiting for transfers between devices: 9.69 us -> 7.05 us  [doubling_gather(): lax.ppermute(held, axis, [(i, i ^ d * stride) for i in range(count)])]
    convert_element_type x2, other arithmetic: 2.17 us -> 0.25 us  [normalize(): return (values * factor * norm_gain).astype(jnp.bfloat16)]
    unnamed x10 -> x16, local copies, waits for them, and re-layouts: 0.02 us -> 1.44 us
    another operation x0 -> x3, other arithmetic: none -> 1.3 us  [the longest x2 0.66 us: local(): jnp.stack([seam_rows.at[:, 0].set((seam_rows[:, 0] + count + k) % count)...]
  transfers between devices with their start and end apart: 16 -> 16, of which waited for: 4 -> 4; matrix products, arithmetic and copies ran while one was open for 15% -> 16% of each run, Pallas kernels for 0% -> 0%
where the time goes in v21:
time: 57.8 us; the launch traced here: 56.9 us
  starting transfers between devices  22.9 us (40%)
  waiting for transfers between devices  7.08 us (12%)
  Pallas kernels  7.06 us (12%)
  other arithmetic  6.84 us (12%)
  local copies, waits for them, and re-layouts  6.24 us (11%)
  matrix products  6.21 us (11%)
    ppermute x12, starting transfers between devices, doubling_gather(): lax.ppermute(held, axis, [(i, i ^ d * stride) for i in range(count)])  14 us
    ppermute x2, starting transfers between devices, padded_2(): after = lax.ppermute(first, axis, down)  8.86 us
    pallas_call x1, Pallas kernels, attend_and_mix(): pl.pallas_call(attention_kernel, out_shape=jax.ShapeDtypeStruct((cells, c...  7.06 us
    ppermute x12, waiting for transfers between devices, doubling_gather(): lax.ppermute(held, axis, [(i, i ^ d * stride) for i in range(count)])  7.05 us
    dot_general x5, matrix products, project(): jnp.dot(flat, weight, preferred_element_type=jnp.float32)  5.27 us
    gather x4, local copies, waits for them, and re-layouts, doubling_gather(): jnp.take(jnp.stack(got), digit ^ jnp.arange(r, dtype=jnp.int32), axis=0)  2.27 us
    unnamed x16, local copies, waits for them, and re-layouts  1.44 us
  transfers between devices with their start and end apart: 16, of which 4 were waited for; matrix products, arithmetic and copies ran while one was open for 16% of the time, Pallas kernels for 0%

profile of v21, /device:TPU:0, one launch (start us, length us, event | category | flops | bytes accessed | tf_op | source)
XLA Modules:
  0.0 56.9 jit_solution(1397285457917302503)
XLA Ops:
  0.0 0.8 %copy.125 = s32[1,2,3]{2,1,0:T(2,128)S(1)} copy(s32[1,2,3]{2,1,0:T(2,128)} %param.21) | data formatting | bytes 48
  0.8 1.1 %fusion.6 = f32[32,8]{1,0:T(8,128)S(1)} fusion(bf16[1,32,8,512]{3,2,1,0:T(8,128)(2,1)} %param.14), kind=kLoop, calls=%fused_computation.25 | loop fusion | flops 392960 | bytes 263168 | tf_op jit(solution)/shard_map/reduce_sum | solution.py:27
  1.9 0.6 %copy-done.5 = f32[512]{0:T(512)S(1)} copy-done((f32[512]{0:T(512)S(1)}, f32[512]{0:T(512)}, u32[]{:S(2)}) %copy-start.5) | copy-done | bytes 2072
  2.5 0.1 fusion.8
  2.7 5.1 %collective-permute-start.2 = (bf16[1,2,8,512]{3,2,1,0:T(8,128)(2,1)S(1)}, bf16[1,2,8,512]{3,2,1,0:T(8,128)(2,1)S(1)}, u32[]{:S(2)}, u32[]{:S(2)}) collective-permute-start(bf16[1,2,8,512]{3,2,1,0:T(8,128)(2,1)S(1)} %get-tuple-element.72), channel_id=1, source_target_pairs={{0,12},{1,13},{2,14},{3,15},{4,8},{5,9},{6,10},{7,11},{8,4},{9,5},... | collective-permute-start | bytes 49160 | tf_op jit(solution)/shard_map/ppermute | solution.py:201
  7.8 0.6 %collective-permute-start = (bf16[1,2,8,512]{3,2,1,0:T(8,128)(2,1)S(1)}, bf16[1,2,8,512]{3,2,1,0:T(8,128)(2,1)S(1)}, u32[]{:S(2)}, u32[]{:S(2)}) collective-permute-start(bf16[1,2,8,512]{3,2,1,0:T(8,128)(2,1)S(1)} %get-tuple-element.72), channel_id=1, source_target_pairs={{0,4},{1,5},{2,6},{3,7},{4,0},{5,1},{6,2},{7,3},{8,12},{9,13},{10,... | collective-permute-start | bytes 49160 | tf_op jit(solution)/shard_map/ppermute | solution.py:201
  8.4 0.1 multiply_convert_fusion
  8.6 0.1 fusion.56
  8.7 4.4 %collective-permute-start.7 = (bf16[1,32,1,512]{3,2,1,0:T(2,128)(2,1)S(1)}, bf16[1,32,1,512]{3,2,1,0:T(2,128)(2,1)S(1)}, u32[]{:S(2)}, u32[]{:S(2)}) collective-permute-start(bf16[1,32,1,512]{3,2,1,0:T(2,128)(2,1)S(1)} %get-tuple-element.55), channel_id=1, source_target_pairs={{1,0},{2,1},{3,2},{4,3},{5,4},{6,5},{7,6},{8,7},{9,8},{10,9},{11,1... | collective-permute-start | bytes 98312 | tf_op jit(solution)/shard_map/ppermute | solution.py:20
  13.2 0.6 %compare_reduce_fusion = pred[]{:T(512)} fusion(), kind=kLoop, calls=%fused_computation.111 | loop fusion | flops 5 | bytes 1 | tf_op jit(solution)/shard_map/reduce.3
  13.8 0.2 compare_reduce_fusion.1
  14.0 0.2 slice_reduce_fusion.1
  14.4 0.7 %fusion.37 = (s32[2,1,1]{2,0,1:T(2,128)S(1)}, s32[2,1,1]{2,0,1:T(2,128)S(1)}, s32[2,1,1]{2,0,1:T(2,128)S(1)}) fusion(pred[]{:T(512)} %compare_reduce_fusion, s32[1,2,3]{2,1,0:T(2,128)S(1)} %copy.125, s32[2,3]{1,0:T(2,128)S(1)} %bitcast.160), kind=kLoop, calls=%fused_computation.123 | loop fusion | flops 78 | bytes 41 | tf_op jit(solution)/shard_map/stack | solution.py:227
  15.3 0.1 copy.98
  15.4 0.1 copy.99
  16.3 0.6 gather_fusion
  17.1 1.8 %collective-permute-start.3 = (bf16[4,1,2,8,512]{4,3,2,0,1:T(8,128)(2,1)S(1)}, bf16[4,1,2,8,512]{4,3,2,0,1:T(8,128)(2,1)S(1)}, u32[]{:S(2)}, u32[]{:S(2)}) collective-permute-start(bf16[4,1,2,8,512]{4,3,2,0,1:T(8,128)(2,1)S(1)} %bitcast_select_fusion.4), channel_id=1, source_target_pairs={{0,1},{1,0},{2,3},{3,2},{4,5},{5,4},{6,7},{7,6},{8,9},{9,8},{10,11... | collective-permute-start | bytes 196616 | tf_op jit(solution)/shard_map/ppermute | solution.py:201
  18.9 0.3 maximum_bitcast_fusion.1
  19.2 1.6 %collective-permute-done.5 = bf16[4,1,2,8,512]{4,3,2,0,1:T(8,128)(2,1)S(1)} collective-permute-done((bf16[4,1,2,8,512]{4,3,2,0,1:T(8,128)(2,1)S(1)}, bf16[4,1,2,8,512]{4,3,2,0,1:T(8,128)(2,1)S(1)}, u32[]{:S(2)}, u32[]{:S(2)}) %collective-permute-start.5) | collective-permute-done | bytes 65568 | tf_op jit(solution)/shard_map/ppermute | solution.py:201
  20.8 1.2 %collective-permute-done.4 = bf16[4,1,2,8,512]{4,3,2,0,1:T(8,128)(2,1)S(1)} collective-permute-done((bf16[4,1,2,8,512]{4,3,2,0,1:T(8,128)(2,1)S(1)}, bf16[4,1,2,8,512]{4,3,2,0,1:T(8,128)(2,1)S(1)}, u32[]{:S(2)}, u32[]{:S(2)}) %collective-permute-start.4) | collective-permute-done | bytes 65568 | tf_op jit(solution)/shard_map/ppermute | solution.py:201
  22.1 0.6 gather_fusion.1
  22.7 0.1 fusion.21
  22.8 0.2 copy.71
  23.1 0.3 fusion.2
  23.4 0.1 broadcast_select_fusion.1
  23.6 1.1 %fusion.67 = bf16[1,32,8,512]{3,2,1,0:T(8,128)(2,1)S(1)} fusion(bf16[1,10,512]{2,1,0:T(8,128)(2,1)S(1)} %copy.83, bf16[32,10,512]{2,1,0:T(8,128)(2,1)S(1)} %maximum_bitcast_fusion.1, f32[32,8]{1,0:T(8,128)S(1)} %copy.85, f32[32,8]{1,0:T(8,128)S(1)} %copy.84, f32[32,8]{1,0:T(8,128)S(1)} %copy.82, f32[32,8]{1,0:T(8,128)S(1)} %copy.81, f32[32,8]{1,0:T(8,128)S(1)} %copy.80, ...), kind=kLoop, calls=%fused_computation.151 | loop fusion | flops 5898240 | bytes 1753088 | tf_op jit(solution)/shard_map/broadcast_in_dim | solution.py:222
  24.6 1.1 %add_convert_fusion = bf16[32,8,512]{2,1,0:T(8,128)(2,1)S(1)} fusion(bf16[32,10,512]{2,1,0:T(8,128)(2,1)S(1)} %maximum_bitcast_fusion.1, bf16[1,10,512]{2,1,0:T(8,128)(2,1)S(1)} %copy.83, bf16[1,10,512]{2,1,0:T(8,128)(2,1)S(1)} %copy.76, f32[32,8]{1,0:T(8,128)S(1)} %copy.85, f32[32,8]{1,0:T(8,128)S(1)} %copy.84, f32[32,8]{1,0:T(8,128)S(1)} %copy.82, ...), kind=kLoop, calls=%fused_computation.30 | loop fusion | flops 5898240 | bytes 1753088 | tf_op jit(solution)/shard_map/convert_element_type | solution.py:69
  25.7 2.0 %collective-permute-start.12 = (bf16[1,6,8,512]{3,2,1,0:T(8,128)(2,1)S(1)}, bf16[1,6,8,512]{3,2,1,0:T(8,128)(2,1)S(1)}, u32[]{:S(2)}, u32[]{:S(2)}) collective-permute-start(bf16[1,6,8,512]{3,2,1,0:T(8,128)(2,1)S(1)} %get-tuple-element.59), channel_id=1, source_target_pairs={{0,12},{1,13},{2,14},{3,15},{4,8},{5,9},{6,10},{7,11},{8,4},{9,5},... | collective-permute-start | bytes 147464 | tf_op jit(solution)/shard_map/ppermute | solution.py:201
  27.7 2.4 %collective-permute-start.10 = (bf16[1,6,8,512]{3,2,1,0:T(8,128)(2,1)S(1)}, bf16[1,6,8,512]{3,2,1,0:T(8,128)(2,1)S(1)}, u32[]{:S(2)}, u32[]{:S(2)}) collective-permute-start(bf16[1,6,8,512]{3,2,1,0:T(8,128)(2,1)S(1)} %get-tuple-element.59), channel_id=1, source_target_pairs={{0,4},{1,5},{2,6},{3,7},{4,0},{5,1},{6,2},{7,3},{8,12},{9,13},{10,... | collective-permute-start | bytes 147464 | tf_op jit(solution)/shard_map/ppermute | solution.py:201
  30.2 1.0 %fusion.1.q_ref = bf16[256,512]{1,0:T(8,128)(2,1)} fusion(bf16[512,512]{1,0:T(8,128)(2,1)S(1)} %copy-done.3, bf16[32,8,512]{2,1,0:T(8,128)(2,1)S(1)} %add_convert_fusion), kind=kOutput, calls=%fused_computation.11 | convolution fusion | flops 134479872 | bytes 1048576 | tf_op jit(solution)/shard_map/dot_general | solution.py:76
  31.4 4.4 %collective-permute-start.9 = (bf16[1,32,3,512]{3,2,1,0:T(4,128)(2,1)S(1)}, bf16[1,32,3,512]{3,2,1,0:T(4,128)(2,1)S(1)}, u32[]{:S(2)}, u32[]{:S(2)}) collective-permute-start(bf16[1,32,3,512]{3,2,1,0:T(4,128)(2,1)S(1)} %get-tuple-element.47), channel_id=1, source_target_pairs={{1,0},{2,1},{3,2},{4,3},{5,4},{6,5},{7,6},{8,7},{9,8},{10,9},{11,1... | collective-permute-start | bytes 294920 | tf_op jit(solution)/shard_map/ppermute | solution.py:20
  35.8 0.6 gather_fusion.2
  36.8 1.8 %collective-permute-start.13 = (bf16[4,1,6,8,512]{4,3,2,0,1:T(8,128)(2,1)S(1)}, bf16[4,1,6,8,512]{4,3,2,0,1:T(8,128)(2,1)S(1)}, u32[]{:S(2)}, u32[]{:S(2)}) collective-permute-start(bf16[4,1,6,8,512]{4,3,2,0,1:T(8,128)(2,1)S(1)} %bitcast_select_fusion.2), channel_id=1, source_target_pairs={{0,1},{1,0},{2,3},{3,2},{4,5},{5,4},{6,7},{7,6},{8,9},{9,8},{10,11... | collective-permute-start | bytes 589832 | tf_op jit(solution)/shard_map/ppermute | solution.py:201
  38.5 0.3 pad_maximum_fusion
  38.9 0.1 reshape_squeeze.3
  39.0 1.2 %convolution_convert_fusion.vc_ref = bf16[448,512]{1,0:T(8,128)(2,1)} fusion(bf16[448,512]{1,0:T(8,128)(2,1)S(1)} %reshape_squeeze.3, bf16[512,512]{1,0:T(8,128)(2,1)S(1)} %copy-done), kind=kOutput, calls=%fused_computation.4 | convolution fusion | flops 235110400 | bytes 1441792 | tf_op jit(solution)/shard_map/dot_general | solution.py:76
  40.2 1.2 %convolution_convert_fusion.1.kc_ref = bf16[448,512]{1,0:T(8,128)(2,1)} fusion(bf16[448,512]{1,0:T(8,128)(2,1)S(1)} %reshape_squeeze.3, bf16[512,512]{1,0:T(8,128)(2,1)S(1)} %copy-done.2), kind=kOutput, calls=%fused_computation.5 | convolution fusion | flops 235110400 | bytes 1441792 | tf_op jit(solution)/shard_map/dot_general | solution.py:76
  41.4 2.5 %collective-permute-done.15 = bf16[4,1,6,8,512]{4,3,2,0,1:T(8,128)(2,1)S(1)} collective-permute-done((bf16[4,1,6,8,512]{4,3,2,0,1:T(8,128)(2,1)S(1)}, bf16[4,1,6,8,512]{4,3,2,0,1:T(8,128)(2,1)S(1)}, u32[]{:S(2)}, u32[]{:S(2)}) %collective-permute-start.15) | collective-permute-done | bytes 196640 | tf_op jit(solution)/shard_map/ppermute | solution.py:201
  43.9 1.7 %collective-permute-done.14 = bf16[4,1,6,8,512]{4,3,2,0,1:T(8,128)(2,1)S(1)} collective-permute-done((bf16[4,1,6,8,512]{4,3,2,0,1:T(8,128)(2,1)S(1)}, bf16[4,1,6,8,512]{4,3,2,0,1:T(8,128)(2,1)S(1)}, u32[]{:S(2)}, u32[]{:S(2)}) %collective-permute-start.14) | collective-permute-done | bytes 196640 | tf_op jit(solution)/shard_map/ppermute | solution.py:201
  45.6 0.1 maximum_bitcast_fusion
  45.7 0.6 %gather_fusion.3 = bf16[4,4,6,8,512]{4,3,2,1,0:T(8,128)(2,1)S(1)} fusion(bf16[4,4,6,8,512]{4,3,2,1,0:T(8,128)(2,1)S(1)} %maximum_bitcast_fusion, s32[1024]{0:T(1024)S(1)} %pad_clamp_fusion), kind=kCustom, calls=%fused_computation.3 | custom fusion | bytes 1572880 | tf_op jit(solution)/shard_map/jit(_take)/gather | solution.py:203
  46.3 0.1 fusion.4
  46.5 0.6 %fusion = bf16[2,3,3,8,512]{4,1,3,2,0:T(4,128)(2,1)S(1)} fusion(bf16[16,2,3,8,512]{4,3,2,1,0:T(8,128)(2,1)S(1)} %bitcast.149, pred[2,3,2]{1,2,0:T(4,128)(4,1)S(1)} %iota_compare_fusion.1, pred[2,3,16]{2,1,0:T(4,128)(4,1)S(1)} %iota_compare_fusion), kind=kOutput, calls=%fused_computation.8 | convolution fusion | flops 4792512 | bytes 933996 | tf_op jit(solution)/shard_map/...nf,nfrwc->...rwc/dot_general | solution.py:182
  47.2 0.1 slice.278
  47.5 0.2 rev.7
  48.0 1.0 %convolution_convert_fusion.3.vr_ref = bf16[192,512]{1,0:T(8,128)(2,1)} fusion(bf16[512,512]{1,0:T(8,128)(2,1)S(1)} %copy-done, bf16[84,512]{1,0:T(8,128)(2,1)S(1)} %reshape.407), kind=kOutput, calls=%fused_computation.9 | convolution fusion | flops 100761600 | bytes 806912 | tf_op jit(solution)/shard_map/dot_general | solution.py:76
  48.9 0.9 %convolution_convert_fusion.4.kr_ref = bf16[192,512]{1,0:T(8,128)(2,1)} fusion(bf16[512,512]{1,0:T(8,128)(2,1)S(1)} %copy-done.2, bf16[84,512]{1,0:T(8,128)(2,1)S(1)} %reshape.407), kind=kOutput, calls=%fused_computation.10 | convolution fusion | flops 100761600 | bytes 806912 | tf_op jit(solution)/shard_map/dot_general | solution.py:76
  49.9 7.1 %shard_map.82 = bf16[256,512]{1,0:T(8,128)(2,1)} custom-call(bf16[256,512]{1,0:T(8,128)(2,1)} %fusion.1.q_ref, bf16[448,512]{1,0:T(8,128)(2,1)} %convolution_convert_fusion.1.kc_ref, bf16[192,512]{1,0:T(8,128)(2,1)} %convolution_convert_fusion.4.kr_ref, bf16[448,512]{1,0:T(8,128)(2,1)} %convolution_convert_fusion.vc_ref, ...), custom_call_target="tpu_custom_call" | custom-call | tf_op jit(solution)/shard_map/pallas_call | solution.py:149
  (88 shorter events, 2.7 us)
Async XLA Ops:
  0.0 39.0 %copy-start = (bf16[512,512]{1,0:T(8,128)(2,1)S(1)}, bf16[512,512]{1,0:T(8,128)(2,1)}, u32[]{:S(2)}) copy-start(bf16[512,512]{1,0:T(8,128)(2,1)} %param.19) | copy-start | bytes 1572868
  0.0 1.9 %copy-start.1 = (bf16[1,32,8,512]{3,2,1,0:T(8,128)(2,1)S(1)}, bf16[1,32,8,512]{3,2,1,0:T(8,128)(2,1)}, u32[]{:S(2)}) copy-start(bf16[1,32,8,512]{3,2,1,0:T(8,128)(2,1)} %param.14) | copy-start | bytes 786436
  1.8 0.7 %copy-start.5 = (f32[512]{0:T(512)S(1)}, f32[512]{0:T(512)}, u32[]{:S(2)}) copy-start(f32[512]{0:T(512)} %param.15) | copy-start | bytes 6148
  2.7 13.6 %collective-permute-start.2 = (bf16[1,2,8,512]{3,2,1,0:T(8,128)(2,1)S(1)}, bf16[1,2,8,512]{3,2,1,0:T(8,128)(2,1)S(1)}, u32[]{:S(2)}, u32[]{:S(2)}) collective-permute-start(bf16[1,2,8,512]{3,2,1,0:T(8,128)(2,1)S(1)} %get-tuple-element.72), channel_id=1, source_target_pairs={{0,12},{1,13},{2,14},{3,15},{4,8},{5,9},{6,10},{7,11},{8,4},{9,5},... | collective-permute-start | bytes 49160 | tf_op jit(solution)/shard_map/ppermute | solution.py:201
  7.8 8.5 %collective-permute-start.1 = (bf16[1,2,8,512]{3,2,1,0:T(8,128)(2,1)S(1)}, bf16[1,2,8,512]{3,2,1,0:T(8,128)(2,1)S(1)}, u32[]{:S(2)}, u32[]{:S(2)}) collective-permute-start(bf16[1,2,8,512]{3,2,1,0:T(8,128)(2,1)S(1)} %get-tuple-element.72), channel_id=1, source_target_pairs={{0,8},{1,9},{2,10},{3,11},{4,12},{5,13},{6,14},{7,15},{8,0},{9,1},... | collective-permute-start | bytes 49160 | tf_op jit(solution)/shard_map/ppermute | solution.py:201
  7.8 8.5 %collective-permute-start = (bf16[1,2,8,512]{3,2,1,0:T(8,128)(2,1)S(1)}, bf16[1,2,8,512]{3,2,1,0:T(8,128)(2,1)S(1)}, u32[]{:S(2)}, u32[]{:S(2)}) collective-permute-start(bf16[1,2,8,512]{3,2,1,0:T(8,128)(2,1)S(1)} %get-tuple-element.72), channel_id=1, source_target_pairs={{0,4},{1,5},{2,6},{3,7},{4,0},{5,1},{6,2},{7,3},{8,12},{9,13},{10,... | collective-permute-start | bytes 49160 | tf_op jit(solution)/shard_map/ppermute | solution.py:201
  8.7 10.2 %collective-permute-start.6 = (bf16[1,32,1,512]{3,2,1,0:T(2,128)(2,1)S(1)}, bf16[1,32,1,512]{3,2,1,0:T(2,128)(2,1)S(1)}, u32[]{:S(2)}, u32[]{:S(2)}) collective-permute-start(bf16[1,32,1,512]{3,2,1,0:T(2,128)(2,1)S(1)} %get-tuple-element.54), channel_id=1, source_target_pairs={{0,1},{1,2},{2,3},{3,4},{4,5},{5,6},{6,7},{7,8},{8,9},{9,10},{10,1... | collective-permute-start | bytes 98312 | tf_op jit(solution)/shard_map/ppermute | solution.py:19
  8.7 10.2 %collective-permute-start.7 = (bf16[1,32,1,512]{3,2,1,0:T(2,128)(2,1)S(1)}, bf16[1,32,1,512]{3,2,1,0:T(2,128)(2,1)S(1)}, u32[]{:S(2)}, u32[]{:S(2)}) collective-permute-start(bf16[1,32,1,512]{3,2,1,0:T(2,128)(2,1)S(1)} %get-tuple-element.55), channel_id=1, source_target_pairs={{1,0},{2,1},{3,2},{4,3},{5,4},{6,5},{7,6},{8,7},{9,8},{10,9},{11,1... | collective-permute-start | bytes 98312 | tf_op jit(solution)/shard_map/ppermute | solution.py:20
  14.4 1.2 %copy-start.4 = (f32[1,9,32,8]{2,3,1,0:T(8,128)S(1)}, f32[1,9,32,8]{2,3,1,0:T(8,128)}, u32[]{:S(2)}) copy-start(f32[1,9,32,8]{2,3,1,0:T(8,128)} %param.16) | copy-start | bytes 27652
  17.0 3.8 %collective-permute-start.5 = (bf16[4,1,2,8,512]{4,3,2,0,1:T(8,128)(2,1)S(1)}, bf16[4,1,2,8,512]{4,3,2,0,1:T(8,128)(2,1)S(1)}, u32[]{:S(2)}, u32[]{:S(2)}) collective-permute-start(bf16[4,1,2,8,512]{4,3,2,0,1:T(8,128)(2,1)S(1)} %bitcast_select_fusion.4), channel_id=1, source_target_pairs={{0,3},{1,2},{2,1},{3,0},{4,7},{5,6},{6,5},{7,4},{8,11},{9,10},{10,... | collective-permute-start | bytes 196616 | tf_op jit(solution)/shard_map/ppermute | solution.py:201
  17.1 5.0 %collective-permute-start.4 = (bf16[4,1,2,8,512]{4,3,2,0,1:T(8,128)(2,1)S(1)}, bf16[4,1,2,8,512]{4,3,2,0,1:T(8,128)(2,1)S(1)}, u32[]{:S(2)}, u32[]{:S(2)}) collective-permute-start(bf16[4,1,2,8,512]{4,3,2,0,1:T(8,128)(2,1)S(1)} %bitcast_select_fusion.4), channel_id=1, source_target_pairs={{0,2},{1,3},{2,0},{3,1},{4,6},{5,7},{6,4},{7,5},{8,10},{9,11},{10,... | collective-permute-start | bytes 196616 | tf_op jit(solution)/shard_map/ppermute | solution.py:201
  17.1 4.9 %collective-permute-start.3 = (bf16[4,1,2,8,512]{4,3,2,0,1:T(8,128)(2,1)S(1)}, bf16[4,1,2,8,512]{4,3,2,0,1:T(8,128)(2,1)S(1)}, u32[]{:S(2)}, u32[]{:S(2)}) collective-permute-start(bf16[4,1,2,8,512]{4,3,2,0,1:T(8,128)(2,1)S(1)} %bitcast_select_fusion.4), channel_id=1, source_target_pairs={{0,1},{1,0},{2,3},{3,2},{4,5},{5,4},{6,7},{7,6},{8,9},{9,8},{10,11... | collective-permute-start | bytes 196616 | tf_op jit(solution)/shard_map/ppermute | solution.py:201
  24.6 5.6 %copy-start.3 = (bf16[512,512]{1,0:T(8,128)(2,1)S(1)}, bf16[512,512]{1,0:T(8,128)(2,1)}, u32[]{:S(2)}) copy-start(bf16[512,512]{1,0:T(8,128)(2,1)} %param.17) | copy-start | bytes 1572868
  25.7 10.1 %collective-permute-start.12 = (bf16[1,6,8,512]{3,2,1,0:T(8,128)(2,1)S(1)}, bf16[1,6,8,512]{3,2,1,0:T(8,128)(2,1)S(1)}, u32[]{:S(2)}, u32[]{:S(2)}) collective-permute-start(bf16[1,6,8,512]{3,2,1,0:T(8,128)(2,1)S(1)} %get-tuple-element.59), channel_id=1, source_target_pairs={{0,12},{1,13},{2,14},{3,15},{4,8},{5,9},{6,10},{7,11},{8,4},{9,5},... | collective-permute-start | bytes 147464 | tf_op jit(solution)/shard_map/ppermute | solution.py:201
  27.7 8.1 %collective-permute-start.11 = (bf16[1,6,8,512]{3,2,1,0:T(8,128)(2,1)S(1)}, bf16[1,6,8,512]{3,2,1,0:T(8,128)(2,1)S(1)}, u32[]{:S(2)}, u32[]{:S(2)}) collective-permute-start(bf16[1,6,8,512]{3,2,1,0:T(8,128)(2,1)S(1)} %get-tuple-element.59), channel_id=1, source_target_pairs={{0,8},{1,9},{2,10},{3,11},{4,12},{5,13},{6,14},{7,15},{8,0},{9,1},... | collective-permute-start | bytes 147464 | tf_op jit(solution)/shard_map/ppermute | solution.py:201
  27.7 8.1 %collective-permute-start.10 = (bf16[1,6,8,512]{3,2,1,0:T(8,128)(2,1)S(1)}, bf16[1,6,8,512]{3,2,1,0:T(8,128)(2,1)S(1)}, u32[]{:S(2)}, u32[]{:S(2)}) collective-permute-start(bf16[1,6,8,512]{3,2,1,0:T(8,128)(2,1)S(1)} %get-tuple-element.59), channel_id=1, source_target_pairs={{0,4},{1,5},{2,6},{3,7},{4,0},{5,1},{6,2},{7,3},{8,12},{9,13},{10,... | collective-permute-start | bytes 147464 | tf_op jit(solution)/shard_map/ppermute | solution.py:201
  31.3 7.2 %collective-permute-start.8 = (bf16[1,32,3,512]{3,2,1,0:T(4,128)(2,1)S(1)}, bf16[1,32,3,512]{3,2,1,0:T(4,128)(2,1)S(1)}, u32[]{:S(2)}, u32[]{:S(2)}) collective-permute-start(bf16[1,32,3,512]{3,2,1,0:T(4,128)(2,1)S(1)} %get-tuple-element.46), channel_id=1, source_target_pairs={{0,1},{1,2},{2,3},{3,4},{4,5},{5,6},{6,7},{7,8},{8,9},{9,10},{10,1... | collective-permute-start | bytes 294920 | tf_op jit(solution)/shard_map/ppermute | solution.py:19
  31.4 7.2 %collective-permute-start.9 = (bf16[1,32,3,512]{3,2,1,0:T(4,128)(2,1)S(1)}, bf16[1,32,3,512]{3,2,1,0:T(4,128)(2,1)S(1)}, u32[]{:S(2)}, u32[]{:S(2)}) collective-permute-start(bf16[1,32,3,512]{3,2,1,0:T(4,128)(2,1)S(1)} %get-tuple-element.47), channel_id=1, source_target_pairs={{1,0},{2,1},{3,2},{4,3},{5,4},{6,5},{7,6},{8,7},{9,8},{10,9},{11,1... | collective-permute-start | bytes 294920 | tf_op jit(solution)/shard_map/ppermute | solution.py:20
  36.6 7.3 %collective-permute-start.15 = (bf16[4,1,6,8,512]{4,3,2,0,1:T(8,128)(2,1)S(1)}, bf16[4,1,6,8,512]{4,3,2,0,1:T(8,128)(2,1)S(1)}, u32[]{:S(2)}, u32[]{:S(2)}) collective-permute-start(bf16[4,1,6,8,512]{4,3,2,0,1:T(8,128)(2,1)S(1)} %bitcast_select_fusion.2), channel_id=1, source_target_pairs={{0,3},{1,2},{2,1},{3,0},{4,7},{5,6},{6,5},{7,4},{8,11},{9,10},{10,... | collective-permute-start | bytes 589832 | tf_op jit(solution)/shard_map/ppermute | solution.py:201
  36.7 8.9 %collective-permute-start.14 = (bf16[4,1,6,8,512]{4,3,2,0,1:T(8,128)(2,1)S(1)}, bf16[4,1,6,8,512]{4,3,2,0,1:T(8,128)(2,1)S(1)}, u32[]{:S(2)}, u32[]{:S(2)}) collective-permute-start(bf16[4,1,6,8,512]{4,3,2,0,1:T(8,128)(2,1)S(1)} %bitcast_select_fusion.2), channel_id=1, source_target_pairs={{0,2},{1,3},{2,0},{3,1},{4,6},{5,7},{6,4},{7,5},{8,10},{9,11},{10,... | collective-permute-start | bytes 589832 | tf_op jit(solution)/shard_map/ppermute | solution.py:201
  36.8 8.8 %collective-permute-start.13 = (bf16[4,1,6,8,512]{4,3,2,0,1:T(8,128)(2,1)S(1)}, bf16[4,1,6,8,512]{4,3,2,0,1:T(8,128)(2,1)S(1)}, u32[]{:S(2)}, u32[]{:S(2)}) collective-permute-start(bf16[4,1,6,8,512]{4,3,2,0,1:T(8,128)(2,1)S(1)} %bitcast_select_fusion.2), channel_id=1, source_target_pairs={{0,1},{1,0},{2,3},{3,2},{4,5},{5,4},{6,7},{7,6},{8,9},{9,8},{10,11... | collective-permute-start | bytes 589832 | tf_op jit(solution)/shard_map/ppermute | solution.py:201
  39.0 1.2 %copy-start.2 = (bf16[512,512]{1,0:T(8,128)(2,1)S(1)}, bf16[512,512]{1,0:T(8,128)(2,1)}, u32[]{:S(2)}) copy-start(bf16[512,512]{1,0:T(8,128)(2,1)} %param.18) | copy-start | bytes 1572868

commit v22 on v21

--- a/solution.py
+++ b/solution.py
@@ -214,8 +214,15 @@
     seam_rows = seam_table[0]
     widened = padded_2(normed[None], (("blk", 2),), margin)
     rows1 = jnp.stack([normed[0], normed[-1]])
-    got1 = widen_tiles(doubling_gather(rows1[None], "blk"), 1)
-    received = pick_all(seam_rows, got1[:, :, None])
+    got1 = doubling_gather(rows1[None], "blk")
+    count = got1.shape[0]
+    near1 = jnp.stack(
+        [seam_rows.at[:, 0].set((seam_rows[:, 0] + count + k) % count) for k in (-1, 0, 1)], axis=1
+    )
+    picked1 = pick_all(near1, got1[:, :, None])
+    received = jnp.concatenate(
+        [picked1[:, 0, :, -1:], picked1[:, 1], picked1[:, 2, :, :1]], axis=2
+    )
     padded = place_rims(widened[0], received, seam_rows)
     smoothed = smooth(padded, metric[0])
     query = project(smoothed, w_query)

time: 57.8 us -> 57.6 us (level)
    unnamed x16 -> x17, local copies, waits for them, and re-layouts: 1.44 us -> 1.45 us
where the time goes in v22:
time: 57.6 us; the launch traced here: 56.7 us
  starting transfers between devices  22.9 us (40%)
  waiting for transfers between devices  7.08 us (12%)
  Pallas kernels  7.06 us (12%)
  other arithmetic  6.75 us (12%)
  matrix products  6.27 us (11%)
  local copies, waits for them, and re-layouts  6.12 us (11%)
    ppermute x12, starting transfers between devices, doubling_gather(): lax.ppermute(held, axis, [(i, i ^ d * stride) for i in range(count)])  14 us
    ppermute x2, starting transfers between devices, padded_2(): after = lax.ppermute(first, axis, down)  8.86 us
    pallas_call x1, Pallas kernels, attend_and_mix(): pl.pallas_call(attention_kernel, out_shape=jax.ShapeDtypeStruct((cells, c...  7.06 us
    ppermute x12, waiting for transfers between devices, doubling_gather(): lax.ppermute(held, axis, [(i, i ^ d * stride) for i in range(count)])  7.05 us
    dot_general x5, matrix products, project(): jnp.dot(flat, weight, preferred_element_type=jnp.float32)  5.3 us
    gather x4, local copies, waits for them, and re-layouts, doubling_gather(): jnp.take(jnp.stack(got), digit ^ jnp.arange(r, dtype=jnp.int32), axis=0)  2.27 us
    unnamed x17, local copies, waits for them, and re-layouts  1.45 us
  transfers between devices with their start and end apart: 16, of which 4 were waited for; matrix products, arithmetic and copies ran while one was open for 16% of the time, Pallas kernels for 0%

profile of v22, /device:TPU:0, one launch (start us, length us, event | category | flops | bytes accessed | tf_op | source)
XLA Modules:
  0.0 56.7 jit_solution(15115842969809431322)
XLA Ops:
  0.0 0.8 %copy.125 = s32[1,2,3]{2,1,0:T(2,128)S(1)} copy(s32[1,2,3]{2,1,0:T(2,128)} %param.27) | data formatting | bytes 48
  0.8 1.1 %fusion.7 = f32[32,8]{1,0:T(8,128)S(1)} fusion(bf16[1,32,8,512]{3,2,1,0:T(8,128)(2,1)} %param.20), kind=kLoop, calls=%fused_computation.26 | loop fusion | flops 392960 | bytes 263168 | tf_op jit(solution)/shard_map/reduce_sum | solution.py:27
  1.9 0.6 %copy-done.5 = f32[512]{0:T(512)S(1)} copy-done((f32[512]{0:T(512)S(1)}, f32[512]{0:T(512)}, u32[]{:S(2)}) %copy-start.5) | copy-done | bytes 2072
  2.5 0.1 fusion.9
  2.7 5.1 %collective-permute-start.2 = (bf16[1,2,8,512]{3,2,1,0:T(8,128)(2,1)S(1)}, bf16[1,2,8,512]{3,2,1,0:T(8,128)(2,1)S(1)}, u32[]{:S(2)}, u32[]{:S(2)}) collective-permute-start(bf16[1,2,8,512]{3,2,1,0:T(8,128)(2,1)S(1)} %get-tuple-element.91), channel_id=1, source_target_pairs={{0,12},{1,13},{2,14},{3,15},{4,8},{5,9},{6,10},{7,11},{8,4},{9,5},... | collective-permute-start | bytes 49160 | tf_op jit(solution)/shard_map/ppermute | solution.py:201
  7.8 0.6 %collective-permute-start = (bf16[1,2,8,512]{3,2,1,0:T(8,128)(2,1)S(1)}, bf16[1,2,8,512]{3,2,1,0:T(8,128)(2,1)S(1)}, u32[]{:S(2)}, u32[]{:S(2)}) collective-permute-start(bf16[1,2,8,512]{3,2,1,0:T(8,128)(2,1)S(1)} %get-tuple-element.91), channel_id=1, source_target_pairs={{0,4},{1,5},{2,6},{3,7},{4,0},{5,1},{6,2},{7,3},{8,12},{9,13},{10,... | collective-permute-start | bytes 49160 | tf_op jit(solution)/shard_map/ppermute | solution.py:201
  8.4 0.1 multiply_convert_fusion
  8.6 0.1 fusion.45
  8.7 4.4 %collective-permute-start.7 = (bf16[1,32,1,512]{3,2,1,0:T(2,128)(2,1)S(1)}, bf16[1,32,1,512]{3,2,1,0:T(2,128)(2,1)S(1)}, u32[]{:S(2)}, u32[]{:S(2)}) collective-permute-start(bf16[1,32,1,512]{3,2,1,0:T(2,128)(2,1)S(1)} %get-tuple-element.72), channel_id=1, source_target_pairs={{1,0},{2,1},{3,2},{4,3},{5,4},{6,5},{7,6},{8,7},{9,8},{10,9},{11,1... | collective-permute-start | bytes 98312 | tf_op jit(solution)/shard_map/ppermute | solution.py:20
  13.2 0.6 %compare_reduce_fusion = pred[]{:T(512)} fusion(), kind=kLoop, calls=%fused_computation.117 | loop fusion | flops 5 | bytes 1 | tf_op jit(solution)/shard_map/reduce.6
  13.8 0.2 slice_reduce_fusion
  14.0 0.2 compare_reduce_fusion.1
  14.3 0.7 %fusion.29 = (s32[2,1,1]{2,0,1:T(2,128)S(1)}, s32[2,1,1]{2,0,1:T(2,128)S(1)}, s32[2,1,1]{2,0,1:T(2,128)S(1)}) fusion(pred[]{:T(512)} %compare_reduce_fusion, s32[1,2,3]{2,1,0:T(2,128)S(1)} %copy.125, s32[2,3]{1,0:T(2,128)S(1)} %bitcast.188), kind=kLoop, calls=%fused_computation.123 | loop fusion | flops 78 | bytes 41 | tf_op jit(solution)/shard_map/stack | solution.py:219
  15.2 0.1 copy.78
  15.3 0.1 copy.79
  16.2 0.6 gather_fusion
  17.0 1.8 %collective-permute-start.3 = (bf16[4,1,2,8,512]{4,3,2,0,1:T(8,128)(2,1)S(1)}, bf16[4,1,2,8,512]{4,3,2,0,1:T(8,128)(2,1)S(1)}, u32[]{:S(2)}, u32[]{:S(2)}) collective-permute-start(bf16[4,1,2,8,512]{4,3,2,0,1:T(8,128)(2,1)S(1)} %bitcast_select_fusion.4), channel_id=1, source_target_pairs={{0,1},{1,0},{2,3},{3,2},{4,5},{5,4},{6,7},{7,6},{8,9},{9,8},{10,11... | collective-permute-start | bytes 196616 | tf_op jit(solution)/shard_map/ppermute | solution.py:201
  18.8 0.3 maximum_bitcast_fusion.1
  19.1 1.6 %collective-permute-done.5 = bf16[4,1,2,8,512]{4,3,2,0,1:T(8,128)(2,1)S(1)} collective-permute-done((bf16[4,1,2,8,512]{4,3,2,0,1:T(8,128)(2,1)S(1)}, bf16[4,1,2,8,512]{4,3,2,0,1:T(8,128)(2,1)S(1)}, u32[]{:S(2)}, u32[]{:S(2)}) %collective-permute-start.5) | collective-permute-done | bytes 65568 | tf_op jit(solution)/shard_map/ppermute | solution.py:201
  20.7 1.2 %collective-permute-done.4 = bf16[4,1,2,8,512]{4,3,2,0,1:T(8,128)(2,1)S(1)} collective-permute-done((bf16[4,1,2,8,512]{4,3,2,0,1:T(8,128)(2,1)S(1)}, bf16[4,1,2,8,512]{4,3,2,0,1:T(8,128)(2,1)S(1)}, u32[]{:S(2)}, u32[]{:S(2)}) %collective-permute-start.4) | collective-permute-done | bytes 65568 | tf_op jit(solution)/shard_map/ppermute | solution.py:201
  22.0 0.6 gather_fusion.1
  22.6 0.1 fusion.16
  22.7 0.3 fusion.3
  23.1 0.2 rev.9
  23.4 1.0 %fusion.55 = bf16[1,32,8,512]{3,2,1,0:T(8,128)(2,1)S(1)} fusion(bf16[1,10,512]{2,1,0:T(8,128)(2,1)S(1)} %get-tuple-element.89, bf16[32,10,512]{2,1,0:T(8,128)(2,1)S(1)} %maximum_bitcast_fusion.1, f32[32,8]{1,0:T(8,128)S(1)} %copy.91, f32[32,8]{1,0:T(8,128)S(1)} %copy.90, f32[32,8]{1,0:T(8,128)S(1)} %copy.89, f32[32,8]{1,0:T(8,128)S(1)} %copy.88, ...), kind=kLoop, calls=%fused_computation.143 | loop fusion | flops 5898240 | bytes 1753088 | tf_op jit(solution)/shard_map/broadcast_in_dim | solution.py:229
  24.5 1.1 %add_convert_fusion = bf16[32,8,512]{2,1,0:T(8,128)(2,1)S(1)} fusion(bf16[32,10,512]{2,1,0:T(8,128)(2,1)S(1)} %maximum_bitcast_fusion.1, bf16[1,10,512]{2,1,0:T(8,128)(2,1)S(1)} %get-tuple-element.89, bf16[1,10,512]{2,1,0:T(8,128)(2,1)S(1)} %get-tuple-element.88, f32[32,8]{1,0:T(8,128)S(1)} %copy.91, f32[32,8]{1,0:T(8,128)S(1)} %copy.90, ...), kind=kLoop, calls=%fused_computation.31 | loop fusion | flops 5898240 | bytes 1753088 | tf_op jit(solution)/shard_map/convert_element_type | solution.py:69
  25.6 2.0 %collective-permute-start.12 = (bf16[1,6,8,512]{3,2,1,0:T(8,128)(2,1)S(1)}, bf16[1,6,8,512]{3,2,1,0:T(8,128)(2,1)S(1)}, u32[]{:S(2)}, u32[]{:S(2)}) collective-permute-start(bf16[1,6,8,512]{3,2,1,0:T(8,128)(2,1)S(1)} %get-tuple-element.78), channel_id=1, source_target_pairs={{0,12},{1,13},{2,14},{3,15},{4,8},{5,9},{6,10},{7,11},{8,4},{9,5},... | collective-permute-start | bytes 147464 | tf_op jit(solution)/shard_map/ppermute | solution.py:201
  27.6 2.4 %collective-permute-start.10 = (bf16[1,6,8,512]{3,2,1,0:T(8,128)(2,1)S(1)}, bf16[1,6,8,512]{3,2,1,0:T(8,128)(2,1)S(1)}, u32[]{:S(2)}, u32[]{:S(2)}) collective-permute-start(bf16[1,6,8,512]{3,2,1,0:T(8,128)(2,1)S(1)} %get-tuple-element.78), channel_id=1, source_target_pairs={{0,4},{1,5},{2,6},{3,7},{4,0},{5,1},{6,2},{7,3},{8,12},{9,13},{10,... | collective-permute-start | bytes 147464 | tf_op jit(solution)/shard_map/ppermute | solution.py:201
  30.0 1.0 %fusion.1.q_ref = bf16[256,512]{1,0:T(8,128)(2,1)} fusion(bf16[512,512]{1,0:T(8,128)(2,1)S(1)} %copy-done.3, bf16[32,8,512]{2,1,0:T(8,128)(2,1)S(1)} %add_convert_fusion), kind=kOutput, calls=%fused_computation.11 | convolution fusion | flops 134479872 | bytes 1048576 | tf_op jit(solution)/shard_map/dot_general | solution.py:76
  31.2 4.4 %collective-permute-start.9 = (bf16[1,32,3,512]{3,2,1,0:T(4,128)(2,1)S(1)}, bf16[1,32,3,512]{3,2,1,0:T(4,128)(2,1)S(1)}, u32[]{:S(2)}, u32[]{:S(2)}) collective-permute-start(bf16[1,32,3,512]{3,2,1,0:T(4,128)(2,1)S(1)} %get-tuple-element.68), channel_id=1, source_target_pairs={{1,0},{2,1},{3,2},{4,3},{5,4},{6,5},{7,6},{8,7},{9,8},{10,9},{11,1... | collective-permute-start | bytes 294920 | tf_op jit(solution)/shard_map/ppermute | solution.py:20
  35.7 0.6 gather_fusion.2
  36.6 1.8 %collective-permute-start.13 = (bf16[4,1,6,8,512]{4,3,2,0,1:T(8,128)(2,1)S(1)}, bf16[4,1,6,8,512]{4,3,2,0,1:T(8,128)(2,1)S(1)}, u32[]{:S(2)}, u32[]{:S(2)}) collective-permute-start(bf16[4,1,6,8,512]{4,3,2,0,1:T(8,128)(2,1)S(1)} %bitcast_select_fusion.2), channel_id=1, source_target_pairs={{0,1},{1,0},{2,3},{3,2},{4,5},{5,4},{6,7},{7,6},{8,9},{9,8},{10,11... | collective-permute-start | bytes 589832 | tf_op jit(solution)/shard_map/ppermute | solution.py:201
  38.4 0.3 pad_maximum_fusion
  38.7 0.1 reshape_squeeze.3
  38.8 1.2 %convolution_convert_fusion.vc_ref = bf16[448,512]{1,0:T(8,128)(2,1)} fusion(bf16[448,512]{1,0:T(8,128)(2,1)S(1)} %reshape_squeeze.3, bf16[512,512]{1,0:T(8,128)(2,1)S(1)} %copy-done), kind=kOutput, calls=%fused_computation.4 | convolution fusion | flops 235110400 | bytes 1441792 | tf_op jit(solution)/shard_map/dot_general | solution.py:76
  40.0 1.2 %convolution_convert_fusion.1.kc_ref = bf16[448,512]{1,0:T(8,128)(2,1)} fusion(bf16[448,512]{1,0:T(8,128)(2,1)S(1)} %reshape_squeeze.3, bf16[512,512]{1,0:T(8,128)(2,1)S(1)} %copy-done.2), kind=kOutput, calls=%fused_computation.5 | convolution fusion | flops 235110400 | bytes 1441792 | tf_op jit(solution)/shard_map/dot_general | solution.py:76
  41.2 2.5 %collective-permute-done.15 = bf16[4,1,6,8,512]{4,3,2,0,1:T(8,128)(2,1)S(1)} collective-permute-done((bf16[4,1,6,8,512]{4,3,2,0,1:T(8,128)(2,1)S(1)}, bf16[4,1,6,8,512]{4,3,2,0,1:T(8,128)(2,1)S(1)}, u32[]{:S(2)}, u32[]{:S(2)}) %collective-permute-start.15) | collective-permute-done | bytes 196640 | tf_op jit(solution)/shard_map/ppermute | solution.py:201
  43.8 1.7 %collective-permute-done.14 = bf16[4,1,6,8,512]{4,3,2,0,1:T(8,128)(2,1)S(1)} collective-permute-done((bf16[4,1,6,8,512]{4,3,2,0,1:T(8,128)(2,1)S(1)}, bf16[4,1,6,8,512]{4,3,2,0,1:T(8,128)(2,1)S(1)}, u32[]{:S(2)}, u32[]{:S(2)}) %collective-permute-start.14) | collective-permute-done | bytes 196640 | tf_op jit(solution)/shard_map/ppermute | solution.py:201
  45.4 0.1 maximum_bitcast_fusion
  45.5 0.6 %gather_fusion.3 = bf16[4,4,6,8,512]{4,3,2,1,0:T(8,128)(2,1)S(1)} fusion(bf16[4,4,6,8,512]{4,3,2,1,0:T(8,128)(2,1)S(1)} %maximum_bitcast_fusion, s32[1024]{0:T(1024)S(1)} %pad_clamp_fusion), kind=kCustom, calls=%fused_computation.3 | custom fusion | bytes 1572880 | tf_op jit(solution)/shard_map/jit(_take)/gather | solution.py:203
  46.1 0.1 fusion.5
  46.3 0.6 %fusion = bf16[2,3,3,8,512]{4,1,3,2,0:T(4,128)(2,1)S(1)} fusion(bf16[16,2,3,8,512]{4,3,2,1,0:T(8,128)(2,1)S(1)} %bitcast.169, pred[2,3,2]{1,2,0:T(4,128)(4,1)S(1)} %iota_compare_fusion.1, pred[2,3,16]{2,1,0:T(4,128)(4,1)S(1)} %iota_compare_fusion), kind=kOutput, calls=%fused_computation.8 | convolution fusion | flops 4792512 | bytes 933996 | tf_op jit(solution)/shard_map/...nf,nfrwc->...rwc/dot_general | solution.py:182
  47.1 0.1 slice.280
  47.3 0.2 rev.10
  47.6 0.1 broadcast_select_fusion
  47.8 0.9 %convolution_convert_fusion.3.vr_ref = bf16[192,512]{1,0:T(8,128)(2,1)} fusion(bf16[512,512]{1,0:T(8,128)(2,1)S(1)} %copy-done, bf16[84,512]{1,0:T(8,128)(2,1)S(1)} %reshape.396), kind=kOutput, calls=%fused_computation.9 | convolution fusion | flops 100761600 | bytes 806912 | tf_op jit(solution)/shard_map/dot_general | solution.py:76
  48.7 1.0 %convolution_convert_fusion.4.kr_ref = bf16[192,512]{1,0:T(8,128)(2,1)} fusion(bf16[512,512]{1,0:T(8,128)(2,1)S(1)} %copy-done.2, bf16[84,512]{1,0:T(8,128)(2,1)S(1)} %reshape.396), kind=kOutput, calls=%fused_computation.10 | convolution fusion | flops 100761600 | bytes 806912 | tf_op jit(solution)/shard_map/dot_general | solution.py:76
  49.7 7.1 %shard_map.82 = bf16[256,512]{1,0:T(8,128)(2,1)} custom-call(bf16[256,512]{1,0:T(8,128)(2,1)} %fusion.1.q_ref, bf16[448,512]{1,0:T(8,128)(2,1)} %convolution_convert_fusion.1.kc_ref, bf16[192,512]{1,0:T(8,128)(2,1)} %convolution_convert_fusion.4.kr_ref, bf16[448,512]{1,0:T(8,128)(2,1)} %convolution_convert_fusion.vc_ref, ...), custom_call_target="tpu_custom_call" | custom-call | tf_op jit(solution)/shard_map/pallas_call | solution.py:149
  (86 shorter events, 2.5 us)
Async XLA Ops:
  0.0 38.8 %copy-start = (bf16[512,512]{1,0:T(8,128)(2,1)S(1)}, bf16[512,512]{1,0:T(8,128)(2,1)}, u32[]{:S(2)}) copy-start(bf16[512,512]{1,0:T(8,128)(2,1)} %param.25) | copy-start | bytes 1572868
  0.0 1.9 %copy-start.1 = (bf16[1,32,8,512]{3,2,1,0:T(8,128)(2,1)S(1)}, bf16[1,32,8,512]{3,2,1,0:T(8,128)(2,1)}, u32[]{:S(2)}) copy-start(bf16[1,32,8,512]{3,2,1,0:T(8,128)(2,1)} %param.20) | copy-start | bytes 786436
  1.8 0.7 %copy-start.5 = (f32[512]{0:T(512)S(1)}, f32[512]{0:T(512)}, u32[]{:S(2)}) copy-start(f32[512]{0:T(512)} %param.21) | copy-start | bytes 6148
  2.7 13.5 %collective-permute-start.2 = (bf16[1,2,8,512]{3,2,1,0:T(8,128)(2,1)S(1)}, bf16[1,2,8,512]{3,2,1,0:T(8,128)(2,1)S(1)}, u32[]{:S(2)}, u32[]{:S(2)}) collective-permute-start(bf16[1,2,8,512]{3,2,1,0:T(8,128)(2,1)S(1)} %get-tuple-element.91), channel_id=1, source_target_pairs={{0,12},{1,13},{2,14},{3,15},{4,8},{5,9},{6,10},{7,11},{8,4},{9,5},... | collective-permute-start | bytes 49160 | tf_op jit(solution)/shard_map/ppermute | solution.py:201
  7.8 8.4 %collective-permute-start.1 = (bf16[1,2,8,512]{3,2,1,0:T(8,128)(2,1)S(1)}, bf16[1,2,8,512]{3,2,1,0:T(8,128)(2,1)S(1)}, u32[]{:S(2)}, u32[]{:S(2)}) collective-permute-start(bf16[1,2,8,512]{3,2,1,0:T(8,128)(2,1)S(1)} %get-tuple-element.91), channel_id=1, source_target_pairs={{0,8},{1,9},{2,10},{3,11},{4,12},{5,13},{6,14},{7,15},{8,0},{9,1},... | collective-permute-start | bytes 49160 | tf_op jit(solution)/shard_map/ppermute | solution.py:201
  7.8 8.4 %collective-permute-start = (bf16[1,2,8,512]{3,2,1,0:T(8,128)(2,1)S(1)}, bf16[1,2,8,512]{3,2,1,0:T(8,128)(2,1)S(1)}, u32[]{:S(2)}, u32[]{:S(2)}) collective-permute-start(bf16[1,2,8,512]{3,2,1,0:T(8,128)(2,1)S(1)} %get-tuple-element.91), channel_id=1, source_target_pairs={{0,4},{1,5},{2,6},{3,7},{4,0},{5,1},{6,2},{7,3},{8,12},{9,13},{10,... | collective-permute-start | bytes 49160 | tf_op jit(solution)/shard_map/ppermute | solution.py:201
  8.7 10.1 %collective-permute-start.6 = (bf16[1,32,1,512]{3,2,1,0:T(2,128)(2,1)S(1)}, bf16[1,32,1,512]{3,2,1,0:T(2,128)(2,1)S(1)}, u32[]{:S(2)}, u32[]{:S(2)}) collective-permute-start(bf16[1,32,1,512]{3,2,1,0:T(2,128)(2,1)S(1)} %get-tuple-element.71), channel_id=1, source_target_pairs={{0,1},{1,2},{2,3},{3,4},{4,5},{5,6},{6,7},{7,8},{8,9},{9,10},{10,1... | collective-permute-start | bytes 98312 | tf_op jit(solution)/shard_map/ppermute | solution.py:19
  8.7 10.1 %collective-permute-start.7 = (bf16[1,32,1,512]{3,2,1,0:T(2,128)(2,1)S(1)}, bf16[1,32,1,512]{3,2,1,0:T(2,128)(2,1)S(1)}, u32[]{:S(2)}, u32[]{:S(2)}) collective-permute-start(bf16[1,32,1,512]{3,2,1,0:T(2,128)(2,1)S(1)} %get-tuple-element.72), channel_id=1, source_target_pairs={{1,0},{2,1},{3,2},{4,3},{5,4},{6,5},{7,6},{8,7},{9,8},{10,9},{11,1... | collective-permute-start | bytes 98312 | tf_op jit(solution)/shard_map/ppermute | solution.py:20
  14.2 1.2 %copy-start.4 = (f32[1,9,32,8]{2,3,1,0:T(8,128)S(1)}, f32[1,9,32,8]{2,3,1,0:T(8,128)}, u32[]{:S(2)}) copy-start(f32[1,9,32,8]{2,3,1,0:T(8,128)} %param.22) | copy-start | bytes 27652
  16.9 3.8 %collective-permute-start.5 = (bf16[4,1,2,8,512]{4,3,2,0,1:T(8,128)(2,1)S(1)}, bf16[4,1,2,8,512]{4,3,2,0,1:T(8,128)(2,1)S(1)}, u32[]{:S(2)}, u32[]{:S(2)}) collective-permute-start(bf16[4,1,2,8,512]{4,3,2,0,1:T(8,128)(2,1)S(1)} %bitcast_select_fusion.4), channel_id=1, source_target_pairs={{0,3},{1,2},{2,1},{3,0},{4,7},{5,6},{6,5},{7,4},{8,11},{9,10},{10,... | collective-permute-start | bytes 196616 | tf_op jit(solution)/shard_map/ppermute | solution.py:201
  17.0 5.0 %collective-permute-start.4 = (bf16[4,1,2,8,512]{4,3,2,0,1:T(8,128)(2,1)S(1)}, bf16[4,1,2,8,512]{4,3,2,0,1:T(8,128)(2,1)S(1)}, u32[]{:S(2)}, u32[]{:S(2)}) collective-permute-start(bf16[4,1,2,8,512]{4,3,2,0,1:T(8,128)(2,1)S(1)} %bitcast_select_fusion.4), channel_id=1, source_target_pairs={{0,2},{1,3},{2,0},{3,1},{4,6},{5,7},{6,4},{7,5},{8,10},{9,11},{10,... | collective-permute-start | bytes 196616 | tf_op jit(solution)/shard_map/ppermute | solution.py:201
  17.0 4.9 %collective-permute-start.3 = (bf16[4,1,2,8,512]{4,3,2,0,1:T(8,128)(2,1)S(1)}, bf16[4,1,2,8,512]{4,3,2,0,1:T(8,128)(2,1)S(1)}, u32[]{:S(2)}, u32[]{:S(2)}) collective-permute-start(bf16[4,1,2,8,512]{4,3,2,0,1:T(8,128)(2,1)S(1)} %bitcast_select_fusion.4), channel_id=1, source_target_pairs={{0,1},{1,0},{2,3},{3,2},{4,5},{5,4},{6,7},{7,6},{8,9},{9,8},{10,11... | collective-permute-start | bytes 196616 | tf_op jit(solution)/shard_map/ppermute | solution.py:201
  24.4 5.6 %copy-start.3 = (bf16[512,512]{1,0:T(8,128)(2,1)S(1)}, bf16[512,512]{1,0:T(8,128)(2,1)}, u32[]{:S(2)}) copy-start(bf16[512,512]{1,0:T(8,128)(2,1)} %param.23) | copy-start | bytes 1572868
  25.6 10.1 %collective-permute-start.12 = (bf16[1,6,8,512]{3,2,1,0:T(8,128)(2,1)S(1)}, bf16[1,6,8,512]{3,2,1,0:T(8,128)(2,1)S(1)}, u32[]{:S(2)}, u32[]{:S(2)}) collective-permute-start(bf16[1,6,8,512]{3,2,1,0:T(8,128)(2,1)S(1)} %get-tuple-element.78), channel_id=1, source_target_pairs={{0,12},{1,13},{2,14},{3,15},{4,8},{5,9},{6,10},{7,11},{8,4},{9,5},... | collective-permute-start | bytes 147464 | tf_op jit(solution)/shard_map/ppermute | solution.py:201
  27.6 8.1 %collective-permute-start.11 = (bf16[1,6,8,512]{3,2,1,0:T(8,128)(2,1)S(1)}, bf16[1,6,8,512]{3,2,1,0:T(8,128)(2,1)S(1)}, u32[]{:S(2)}, u32[]{:S(2)}) collective-permute-start(bf16[1,6,8,512]{3,2,1,0:T(8,128)(2,1)S(1)} %get-tuple-element.78), channel_id=1, source_target_pairs={{0,8},{1,9},{2,10},{3,11},{4,12},{5,13},{6,14},{7,15},{8,0},{9,1},... | collective-permute-start | bytes 147464 | tf_op jit(solution)/shard_map/ppermute | solution.py:201
  27.6 8.1 %collective-permute-start.10 = (bf16[1,6,8,512]{3,2,1,0:T(8,128)(2,1)S(1)}, bf16[1,6,8,512]{3,2,1,0:T(8,128)(2,1)S(1)}, u32[]{:S(2)}, u32[]{:S(2)}) collective-permute-start(bf16[1,6,8,512]{3,2,1,0:T(8,128)(2,1)S(1)} %get-tuple-element.78), channel_id=1, source_target_pairs={{0,4},{1,5},{2,6},{3,7},{4,0},{5,1},{6,2},{7,3},{8,12},{9,13},{10,... | collective-permute-start | bytes 147464 | tf_op jit(solution)/shard_map/ppermute | solution.py:201
  31.1 7.2 %collective-permute-start.8 = (bf16[1,32,3,512]{3,2,1,0:T(4,128)(2,1)S(1)}, bf16[1,32,3,512]{3,2,1,0:T(4,128)(2,1)S(1)}, u32[]{:S(2)}, u32[]{:S(2)}) collective-permute-start(bf16[1,32,3,512]{3,2,1,0:T(4,128)(2,1)S(1)} %get-tuple-element.67), channel_id=1, source_target_pairs={{0,1},{1,2},{2,3},{3,4},{4,5},{5,6},{6,7},{7,8},{8,9},{9,10},{10,1... | collective-permute-start | bytes 294920 | tf_op jit(solution)/shard_map/ppermute | solution.py:19
  31.2 7.2 %collective-permute-start.9 = (bf16[1,32,3,512]{3,2,1,0:T(4,128)(2,1)S(1)}, bf16[1,32,3,512]{3,2,1,0:T(4,128)(2,1)S(1)}, u32[]{:S(2)}, u32[]{:S(2)}) collective-permute-start(bf16[1,32,3,512]{3,2,1,0:T(4,128)(2,1)S(1)} %get-tuple-element.68), channel_id=1, source_target_pairs={{1,0},{2,1},{3,2},{4,3},{5,4},{6,5},{7,6},{8,7},{9,8},{10,9},{11,1... | collective-permute-start | bytes 294920 | tf_op jit(solution)/shard_map/ppermute | solution.py:20
  36.4 7.3 %collective-permute-start.15 = (bf16[4,1,6,8,512]{4,3,2,0,1:T(8,128)(2,1)S(1)}, bf16[4,1,6,8,512]{4,3,2,0,1:T(8,128)(2,1)S(1)}, u32[]{:S(2)}, u32[]{:S(2)}) collective-permute-start(bf16[4,1,6,8,512]{4,3,2,0,1:T(8,128)(2,1)S(1)} %bitcast_select_fusion.2), channel_id=1, source_target_pairs={{0,3},{1,2},{2,1},{3,0},{4,7},{5,6},{6,5},{7,4},{8,11},{9,10},{10,... | collective-permute-start | bytes 589832 | tf_op jit(solution)/shard_map/ppermute | solution.py:201
  36.5 8.9 %collective-permute-start.14 = (bf16[4,1,6,8,512]{4,3,2,0,1:T(8,128)(2,1)S(1)}, bf16[4,1,6,8,512]{4,3,2,0,1:T(8,128)(2,1)S(1)}, u32[]{:S(2)}, u32[]{:S(2)}) collective-permute-start(bf16[4,1,6,8,512]{4,3,2,0,1:T(8,128)(2,1)S(1)} %bitcast_select_fusion.2), channel_id=1, source_target_pairs={{0,2},{1,3},{2,0},{3,1},{4,6},{5,7},{6,4},{7,5},{8,10},{9,11},{10,... | collective-permute-start | bytes 589832 | tf_op jit(solution)/shard_map/ppermute | solution.py:201
  36.6 8.8 %collective-permute-start.13 = (bf16[4,1,6,8,512]{4,3,2,0,1:T(8,128)(2,1)S(1)}, bf16[4,1,6,8,512]{4,3,2,0,1:T(8,128)(2,1)S(1)}, u32[]{:S(2)}, u32[]{:S(2)}) collective-permute-start(bf16[4,1,6,8,512]{4,3,2,0,1:T(8,128)(2,1)S(1)} %bitcast_select_fusion.2), channel_id=1, source_target_pairs={{0,1},{1,0},{2,3},{3,2},{4,5},{5,4},{6,7},{7,6},{8,9},{9,8},{10,11... | collective-permute-start | bytes 589832 | tf_op jit(solution)/shard_map/ppermute | solution.py:201
  38.8 1.2 %copy-start.2 = (bf16[512,512]{1,0:T(8,128)(2,1)S(1)}, bf16[512,512]{1,0:T(8,128)(2,1)}, u32[]{:S(2)}) copy-start(bf16[512,512]{1,0:T(8,128)(2,1)} %param.24) | copy-start | bytes 1572868

commit v23 on v22

--- a/solution.py
+++ b/solution.py
@@ -214,7 +214,7 @@
     seam_rows = seam_table[0]
     widened = padded_2(normed[None], (("blk", 2),), margin)
     rows1 = jnp.stack([normed[0], normed[-1]])
-    got1 = doubling_gather(rows1[None], "blk")
+    got1 = doubling_gather(rows1[None], "blk", radix=2)
     count = got1.shape[0]
     near1 = jnp.stack(
         [seam_rows.at[:, 0].set((seam_rows[:, 0] + count + k) % count) for k in (-1, 0, 1)], axis=1

time: 57.6 us -> 60.9 us (1.057)
  waiting for transfers between devices: 7.08 us -> 11.1 us
  starting transfers between devices: 22.9 us -> 19.9 us
  local copies, waits for them, and re-layouts: 6.12 us -> 7.43 us
  other arithmetic: 6.75 us -> 7.6 us
    ppermute x12 -> x10, starting transfers between devices: 14 us -> 9.88 us  [doubling_gather(): lax.ppermute(held, axis, [(i, i ^ d * stride) for i in range(count)])]
    ppermute x12 -> x10, waiting for transfers between devices: 7.05 us -> 11.1 us  [doubling_gather(): lax.ppermute(held, axis, [(i, i ^ d * stride) for i in range(count)])]
    gather x4 -> x6, local copies, waits for them, and re-layouts: 2.27 us -> 3.38 us  [doubling_gather(): jnp.take(jnp.stack(got), digit ^ jnp.arange(r, dtype=jnp.int32), axis=0)]
    select_n x6 -> x14, other arithmetic: 0.34 us -> 1.13 us  [doubling_gather(): jnp.take(jnp.stack(got), digit ^ jnp.arange(r, dtype=jnp.int32), axis=0)]
    ppermute x2, starting transfers between devices: 8.86 us -> 9.49 us  [padded_2(): after = lax.ppermute(first, axis, down)]
  transfers between devices with their start and end apart: 16 -> 14, of which waited for: 4 -> 5; matrix products, arithmetic and copies ran while one was open for 16% -> 16% of each run, Pallas kernels for 0% -> 0%
where the time goes in v23:
time: 60.9 us; the launch traced here: 59.9 us
  starting transfers between devices  19.9 us (33%)
  waiting for transfers between devices  11.1 us (18%)
  other arithmetic  7.6 us (12%)
  local copies, waits for them, and re-layouts  7.43 us (12%)
  Pallas kernels  7.06 us (12%)
  matrix products  6.23 us (10%)
    ppermute x10, waiting for transfers between devices, doubling_gather(): lax.ppermute(held, axis, [(i, i ^ d * stride) for i in range(count)])  11.1 us
    ppermute x10, starting transfers between devices, doubling_gather(): lax.ppermute(held, axis, [(i, i ^ d * stride) for i in range(count)])  9.88 us
    ppermute x2, starting transfers between devices, padded_2(): after = lax.ppermute(first, axis, down)  9.49 us
    pallas_call x1, Pallas kernels, attend_and_mix(): pl.pallas_call(attention_kernel, out_shape=jax.ShapeDtypeStruct((cells, c...  7.06 us
    dot_general x5, matrix products, project(): jnp.dot(flat, weight, preferred_element_type=jnp.float32)  5.25 us
    gather x6, local copies, waits for them, and re-layouts, doubling_gather(): jnp.take(jnp.stack(got), digit ^ jnp.arange(r, dtype=jnp.int32), axis=0)  3.38 us
    unnamed x17, local copies, waits for them, and re-layouts  1.66 us
  transfers between devices with their start and end apart: 14, of which 5 were waited for; matrix products, arithmetic and copies ran while one was open for 16% of the time, Pallas kernels for 0%

profile of v23, /device:TPU:0, one launch (start us, length us, event | category | flops | bytes accessed | tf_op | source)
XLA Modules:
  0.0 59.9 jit_solution(16731240085200461757)
XLA Ops:
  0.0 0.8 %copy.125 = s32[1,2,3]{2,1,0:T(2,128)S(1)} copy(s32[1,2,3]{2,1,0:T(2,128)} %param.27) | data formatting | bytes 48
  0.8 1.1 %fusion.7 = f32[32,8]{1,0:T(8,128)S(1)} fusion(bf16[1,32,8,512]{3,2,1,0:T(8,128)(2,1)} %param.20), kind=kLoop, calls=%fused_computation.28 | loop fusion | flops 392960 | bytes 263168 | tf_op jit(solution)/shard_map/reduce_sum | solution.py:27
  1.9 0.6 %copy-done.5 = f32[512]{0:T(512)S(1)} copy-done((f32[512]{0:T(512)S(1)}, f32[512]{0:T(512)}, u32[]{:S(2)}) %copy-start.5) | copy-done | bytes 2072
  2.5 0.1 multiply_convert_fusion
  2.7 0.5 collective-permute-start.4
  3.3 5.1 %collective-permute-start.5 = (bf16[1,32,1,512]{3,2,1,0:T(2,128)(2,1)S(1)}, bf16[1,32,1,512]{3,2,1,0:T(2,128)(2,1)S(1)}, u32[]{:S(2)}, u32[]{:S(2)}) collective-permute-start(bf16[1,32,1,512]{3,2,1,0:T(2,128)(2,1)S(1)} %get-tuple-element.72), channel_id=1, source_target_pairs={{1,0},{2,1},{3,2},{4,3},{5,4},{6,5},{7,6},{8,7},{9,8},{10,9},{11,1... | collective-permute-start | bytes 98312 | tf_op jit(solution)/shard_map/ppermute | solution.py:20
  8.3 0.1 fusion.9
  8.5 1.2 %collective-permute-start = (bf16[1,2,8,512]{3,2,1,0:T(8,128)(2,1)S(1)}, bf16[1,2,8,512]{3,2,1,0:T(8,128)(2,1)S(1)}, u32[]{:S(2)}, u32[]{:S(2)}) collective-permute-start(bf16[1,2,8,512]{3,2,1,0:T(8,128)(2,1)S(1)} %get-tuple-element.91), channel_id=1, source_target_pairs={{0,8},{1,9},{2,10},{3,11},{4,12},{5,13},{6,14},{7,15},{8,0},{9,1},... | collective-permute-start | bytes 49160 | tf_op jit(solution)/shard_map/ppermute | solution.py:201
  9.7 0.6 %compare_reduce_fusion = pred[]{:T(512)} fusion(), kind=kLoop, calls=%fused_computation.141 | loop fusion | flops 5 | bytes 1 | tf_op jit(solution)/shard_map/reduce.6
  10.5 0.1 fusion.37
  10.9 0.2 slice_reduce_fusion
  11.1 0.2 compare_reduce_fusion.1
  11.3 0.7 %fusion.29 = (s32[2,1,1]{2,0,1:T(2,128)S(1)}, s32[2,1,1]{2,0,1:T(2,128)S(1)}, s32[2,1,1]{2,0,1:T(2,128)S(1)}) fusion(pred[]{:T(512)} %compare_reduce_fusion, s32[1,2,3]{2,1,0:T(2,128)S(1)} %copy.125, s32[2,3]{1,0:T(2,128)S(1)} %bitcast.197), kind=kLoop, calls=%fused_computation.147 | loop fusion | flops 78 | bytes 41 | tf_op jit(solution)/shard_map/stack | solution.py:219
  12.6 0.2 copy-done.4
  13.5 0.5 gather_fusion
  14.2 1.6 %collective-permute-start.1 = (bf16[2,1,2,8,512]{4,3,2,0,1:T(8,128)(2,1)S(1)}, bf16[2,1,2,8,512]{4,3,2,0,1:T(8,128)(2,1)S(1)}, u32[]{:S(2)}, u32[]{:S(2)}) collective-permute-start(bf16[2,1,2,8,512]{4,3,2,0,1:T(8,128)(2,1)S(1)} %bitcast_select_fusion.8), channel_id=1, source_target_pairs={{0,4},{1,5},{2,6},{3,7},{4,0},{5,1},{6,2},{7,3},{8,12},{9,13},{10,... | collective-permute-start | bytes 98312 | tf_op jit(solution)/shard_map/ppermute | solution.py:201
  15.8 0.3 maximum_bitcast_fusion.1
  16.1 2.0 %collective-permute-done.1 = bf16[2,1,2,8,512]{4,3,2,0,1:T(8,128)(2,1)S(1)} collective-permute-done((bf16[2,1,2,8,512]{4,3,2,0,1:T(8,128)(2,1)S(1)}, bf16[2,1,2,8,512]{4,3,2,0,1:T(8,128)(2,1)S(1)}, u32[]{:S(2)}, u32[]{:S(2)}) %collective-permute-start.1) | collective-permute-done | bytes 32800 | tf_op jit(solution)/shard_map/ppermute | solution.py:201
  18.2 0.6 gather_fusion.1
  18.8 0.6 %collective-permute-start.2 = (bf16[2,2,1,2,8,512]{5,4,3,1,0,2:T(8,128)(2,1)S(1)}, bf16[2,2,1,2,8,512]{5,4,3,1,0,2:T(8,128)(2,1)S(1)}, u32[]{:S(2)}, u32[]{:S(2)}) collective-permute-start(bf16[2,2,1,2,8,512]{5,4,3,1,0,2:T(8,128)(2,1)S(1)} %bitcast_select_fusion.6), channel_id=1, source_target_pairs={{0,2},{1,3},{2,0},{3,1},{4,6},{5,7},{6,4},{7,5},{8,10},{9,11},{10,... | collective-permute-start | bytes 196616 | tf_op jit(solution)/shard_map/ppermute | solution.py:201
  19.5 3.6 %collective-permute-done.2 = bf16[2,2,1,2,8,512]{5,4,3,1,0,2:T(8,128)(2,1)S(1)} collective-permute-done((bf16[2,2,1,2,8,512]{5,4,3,1,0,2:T(8,128)(2,1)S(1)}, bf16[2,2,1,2,8,512]{5,4,3,1,0,2:T(8,128)(2,1)S(1)}, u32[]{:S(2)}, u32[]{:S(2)}) %collective-permute-start.2) | collective-permute-done | bytes 65568 | tf_op jit(solution)/shard_map/ppermute | solution.py:201
  23.1 0.6 gather_fusion.2
  23.9 1.2 %collective-permute-done.3 = bf16[2,2,2,1,2,8,512]{6,5,4,2,1,0,3:T(8,128)(2,1)S(1)} collective-permute-done((bf16[2,2,2,1,2,8,512]{6,5,4,2,1,0,3:T(8,128)(2,1)S(1)}, bf16[2,2,2,1,2,8,512]{6,5,4,2,1,0,3:T(8,128)(2,1)S(1)}, u32[]{:S(2)}, u32[]{:S(2)}) %collective-permute-start.3) | collective-permute-done | bytes 131104 | tf_op jit(solution)/shard_map/ppermute | solution.py:201
  25.2 0.6 gather_fusion.3
  25.9 0.3 fusion.3
  26.3 0.2 rev.9
  26.6 1.1 %fusion.59 = bf16[1,32,8,512]{3,2,1,0:T(8,128)(2,1)S(1)} fusion(bf16[1,10,512]{2,1,0:T(8,128)(2,1)S(1)} %get-tuple-element.89, bf16[32,10,512]{2,1,0:T(8,128)(2,1)S(1)} %maximum_bitcast_fusion.1, f32[32,8]{1,0:T(8,128)S(1)} %copy.91, f32[32,8]{1,0:T(8,128)S(1)} %copy.90, f32[32,8]{1,0:T(8,128)S(1)} %copy.89, f32[32,8]{1,0:T(8,128)S(1)} %copy.88, ...), kind=kLoop, calls=%fused_computation.171 | loop fusion | flops 5898240 | bytes 1753088 | tf_op jit(solution)/shard_map/broadcast_in_dim | solution.py:229
  27.7 1.1 %add_convert_fusion = bf16[32,8,512]{2,1,0:T(8,128)(2,1)S(1)} fusion(bf16[32,10,512]{2,1,0:T(8,128)(2,1)S(1)} %maximum_bitcast_fusion.1, bf16[1,10,512]{2,1,0:T(8,128)(2,1)S(1)} %get-tuple-element.89, bf16[1,10,512]{2,1,0:T(8,128)(2,1)S(1)} %get-tuple-element.88, f32[32,8]{1,0:T(8,128)S(1)} %copy.91, f32[32,8]{1,0:T(8,128)S(1)} %copy.90, ...), kind=kLoop, calls=%fused_computation.33 | loop fusion | flops 5898240 | bytes 1753088 | tf_op jit(solution)/shard_map/convert_element_type | solution.py:69
  28.8 2.0 %collective-permute-start.10 = (bf16[1,6,8,512]{3,2,1,0:T(8,128)(2,1)S(1)}, bf16[1,6,8,512]{3,2,1,0:T(8,128)(2,1)S(1)}, u32[]{:S(2)}, u32[]{:S(2)}) collective-permute-start(bf16[1,6,8,512]{3,2,1,0:T(8,128)(2,1)S(1)} %get-tuple-element.78), channel_id=1, source_target_pairs={{0,12},{1,13},{2,14},{3,15},{4,8},{5,9},{6,10},{7,11},{8,4},{9,5},... | collective-permute-start | bytes 147464 | tf_op jit(solution)/shard_map/ppermute | solution.py:201
  30.7 1.1 %collective-permute-start.9 = (bf16[1,6,8,512]{3,2,1,0:T(8,128)(2,1)S(1)}, bf16[1,6,8,512]{3,2,1,0:T(8,128)(2,1)S(1)}, u32[]{:S(2)}, u32[]{:S(2)}) collective-permute-start(bf16[1,6,8,512]{3,2,1,0:T(8,128)(2,1)S(1)} %get-tuple-element.78), channel_id=1, source_target_pairs={{0,8},{1,9},{2,10},{3,11},{4,12},{5,13},{6,14},{7,15},{8,0},{9,1},... | collective-permute-start | bytes 147464 | tf_op jit(solution)/shard_map/ppermute | solution.py:201
  31.9 1.3 %collective-permute-start.8 = (bf16[1,6,8,512]{3,2,1,0:T(8,128)(2,1)S(1)}, bf16[1,6,8,512]{3,2,1,0:T(8,128)(2,1)S(1)}, u32[]{:S(2)}, u32[]{:S(2)}) collective-permute-start(bf16[1,6,8,512]{3,2,1,0:T(8,128)(2,1)S(1)} %get-tuple-element.78), channel_id=1, source_target_pairs={{0,4},{1,5},{2,6},{3,7},{4,0},{5,1},{6,2},{7,3},{8,12},{9,13},{10,... | collective-permute-start | bytes 147464 | tf_op jit(solution)/shard_map/ppermute | solution.py:201
  33.2 1.0 %fusion.1.q_ref = bf16[256,512]{1,0:T(8,128)(2,1)} fusion(bf16[512,512]{1,0:T(8,128)(2,1)S(1)} %copy-done.3, bf16[32,8,512]{2,1,0:T(8,128)(2,1)S(1)} %add_convert_fusion), kind=kOutput, calls=%fused_computation.13 | convolution fusion | flops 134479872 | bytes 1048576 | tf_op jit(solution)/shard_map/dot_general | solution.py:76
  34.4 4.4 %collective-permute-start.7 = (bf16[1,32,3,512]{3,2,1,0:T(4,128)(2,1)S(1)}, bf16[1,32,3,512]{3,2,1,0:T(4,128)(2,1)S(1)}, u32[]{:S(2)}, u32[]{:S(2)}) collective-permute-start(bf16[1,32,3,512]{3,2,1,0:T(4,128)(2,1)S(1)} %get-tuple-element.68), channel_id=1, source_target_pairs={{1,0},{2,1},{3,2},{4,3},{5,4},{6,5},{7,6},{8,7},{9,8},{10,9},{11,1... | collective-permute-start | bytes 294920 | tf_op jit(solution)/shard_map/ppermute | solution.py:20
  38.9 0.6 gather_fusion.4
  39.8 1.8 %collective-permute-start.11 = (bf16[4,1,6,8,512]{4,3,2,0,1:T(8,128)(2,1)S(1)}, bf16[4,1,6,8,512]{4,3,2,0,1:T(8,128)(2,1)S(1)}, u32[]{:S(2)}, u32[]{:S(2)}) collective-permute-start(bf16[4,1,6,8,512]{4,3,2,0,1:T(8,128)(2,1)S(1)} %bitcast_select_fusion.2), channel_id=1, source_target_pairs={{0,1},{1,0},{2,3},{3,2},{4,5},{5,4},{6,7},{7,6},{8,9},{9,8},{10,11... | collective-permute-start | bytes 589832 | tf_op jit(solution)/shard_map/ppermute | solution.py:201
  41.6 0.3 pad_maximum_fusion
  41.9 0.1 reshape_squeeze.3
  42.0 1.2 %convolution_convert_fusion.vc_ref = bf16[448,512]{1,0:T(8,128)(2,1)} fusion(bf16[448,512]{1,0:T(8,128)(2,1)S(1)} %reshape_squeeze.3, bf16[512,512]{1,0:T(8,128)(2,1)S(1)} %copy-done), kind=kOutput, calls=%fused_computation.6 | convolution fusion | flops 235110400 | bytes 1441792 | tf_op jit(solution)/shard_map/dot_general | solution.py:76
  43.2 1.2 %convolution_convert_fusion.1.kc_ref = bf16[448,512]{1,0:T(8,128)(2,1)} fusion(bf16[448,512]{1,0:T(8,128)(2,1)S(1)} %reshape_squeeze.3, bf16[512,512]{1,0:T(8,128)(2,1)S(1)} %copy-done.2), kind=kOutput, calls=%fused_computation.7 | convolution fusion | flops 235110400 | bytes 1441792 | tf_op jit(solution)/shard_map/dot_general | solution.py:76
  44.4 2.6 %collective-permute-done.13 = bf16[4,1,6,8,512]{4,3,2,0,1:T(8,128)(2,1)S(1)} collective-permute-done((bf16[4,1,6,8,512]{4,3,2,0,1:T(8,128)(2,1)S(1)}, bf16[4,1,6,8,512]{4,3,2,0,1:T(8,128)(2,1)S(1)}, u32[]{:S(2)}, u32[]{:S(2)}) %collective-permute-start.13) | collective-permute-done | bytes 196640 | tf_op jit(solution)/shard_map/ppermute | solution.py:201
  47.0 1.7 %collective-permute-done.12 = bf16[4,1,6,8,512]{4,3,2,0,1:T(8,128)(2,1)S(1)} collective-permute-done((bf16[4,1,6,8,512]{4,3,2,0,1:T(8,128)(2,1)S(1)}, bf16[4,1,6,8,512]{4,3,2,0,1:T(8,128)(2,1)S(1)}, u32[]{:S(2)}, u32[]{:S(2)}) %collective-permute-start.12) | collective-permute-done | bytes 196640 | tf_op jit(solution)/shard_map/ppermute | solution.py:201
  48.7 0.6 gather_fusion.5
  49.3 0.1 fusion.5
  49.5 0.6 %fusion = bf16[2,3,3,8,512]{4,1,3,2,0:T(4,128)(2,1)S(1)} fusion(bf16[16,2,3,8,512]{4,3,2,1,0:T(8,128)(2,1)S(1)} %bitcast.179, pred[2,3,2]{1,2,0:T(4,128)(4,1)S(1)} %iota_compare_fusion.1, pred[2,3,16]{2,1,0:T(4,128)(4,1)S(1)} %iota_compare_fusion), kind=kOutput, calls=%fused_computation.10 | convolution fusion | flops 4792512 | bytes 933996 | tf_op jit(solution)/shard_map/...nf,nfrwc->...rwc/dot_general | solution.py:182
  50.5 0.2 rev.10
  51.0 0.9 %convolution_convert_fusion.3.vr_ref = bf16[192,512]{1,0:T(8,128)(2,1)} fusion(bf16[512,512]{1,0:T(8,128)(2,1)S(1)} %copy-done, bf16[84,512]{1,0:T(8,128)(2,1)S(1)} %reshape.516), kind=kOutput, calls=%fused_computation.11 | convolution fusion | flops 100761600 | bytes 806912 | tf_op jit(solution)/shard_map/dot_general | solution.py:76
  51.9 1.0 %convolution_convert_fusion.4.kr_ref = bf16[192,512]{1,0:T(8,128)(2,1)} fusion(bf16[512,512]{1,0:T(8,128)(2,1)S(1)} %copy-done.2, bf16[84,512]{1,0:T(8,128)(2,1)S(1)} %reshape.516), kind=kOutput, calls=%fused_computation.12 | convolution fusion | flops 100761600 | bytes 806912 | tf_op jit(solution)/shard_map/dot_general | solution.py:76
  52.9 7.1 %shard_map.82 = bf16[256,512]{1,0:T(8,128)(2,1)} custom-call(bf16[256,512]{1,0:T(8,128)(2,1)} %fusion.1.q_ref, bf16[448,512]{1,0:T(8,128)(2,1)} %convolution_convert_fusion.1.kc_ref, bf16[192,512]{1,0:T(8,128)(2,1)} %convolution_convert_fusion.4.kr_ref, bf16[448,512]{1,0:T(8,128)(2,1)} %convolution_convert_fusion.vc_ref, ...), custom_call_target="tpu_custom_call" | custom-call | tf_op jit(solution)/shard_map/pallas_call | solution.py:149
  (102 shorter events, 3.8 us)
Async XLA Ops:
  0.0 42.0 %copy-start = (bf16[512,512]{1,0:T(8,128)(2,1)S(1)}, bf16[512,512]{1,0:T(8,128)(2,1)}, u32[]{:S(2)}) copy-start(bf16[512,512]{1,0:T(8,128)(2,1)} %param.25) | copy-start | bytes 1572868
  0.0 1.9 %copy-start.1 = (bf16[1,32,8,512]{3,2,1,0:T(8,128)(2,1)S(1)}, bf16[1,32,8,512]{3,2,1,0:T(8,128)(2,1)}, u32[]{:S(2)}) copy-start(bf16[1,32,8,512]{3,2,1,0:T(8,128)(2,1)} %param.20) | copy-start | bytes 786436
  1.8 0.7 %copy-start.5 = (f32[512]{0:T(512)S(1)}, f32[512]{0:T(512)}, u32[]{:S(2)}) copy-start(f32[512]{0:T(512)} %param.21) | copy-start | bytes 6148
  2.7 13.1 %collective-permute-start.4 = (bf16[1,32,1,512]{3,2,1,0:T(2,128)(2,1)S(1)}, bf16[1,32,1,512]{3,2,1,0:T(2,128)(2,1)S(1)}, u32[]{:S(2)}, u32[]{:S(2)}) collective-permute-start(bf16[1,32,1,512]{3,2,1,0:T(2,128)(2,1)S(1)} %get-tuple-element.71), channel_id=1, source_target_pairs={{0,1},{1,2},{2,3},{3,4},{4,5},{5,6},{6,7},{7,8},{8,9},{9,10},{10,1... | collective-permute-start | bytes 98312 | tf_op jit(solution)/shard_map/ppermute | solution.py:19
  3.3 12.6 %collective-permute-start.5 = (bf16[1,32,1,512]{3,2,1,0:T(2,128)(2,1)S(1)}, bf16[1,32,1,512]{3,2,1,0:T(2,128)(2,1)S(1)}, u32[]{:S(2)}, u32[]{:S(2)}) collective-permute-start(bf16[1,32,1,512]{3,2,1,0:T(2,128)(2,1)S(1)} %get-tuple-element.72), channel_id=1, source_target_pairs={{1,0},{2,1},{3,2},{4,3},{5,4},{6,5},{7,6},{8,7},{9,8},{10,9},{11,1... | collective-permute-start | bytes 98312 | tf_op jit(solution)/shard_map/ppermute | solution.py:20
  8.5 5.1 %collective-permute-start = (bf16[1,2,8,512]{3,2,1,0:T(8,128)(2,1)S(1)}, bf16[1,2,8,512]{3,2,1,0:T(8,128)(2,1)S(1)}, u32[]{:S(2)}, u32[]{:S(2)}) collective-permute-start(bf16[1,2,8,512]{3,2,1,0:T(8,128)(2,1)S(1)} %get-tuple-element.91), channel_id=1, source_target_pairs={{0,8},{1,9},{2,10},{3,11},{4,12},{5,13},{6,14},{7,15},{8,0},{9,1},... | collective-permute-start | bytes 49160 | tf_op jit(solution)/shard_map/ppermute | solution.py:201
  12.1 0.8 %copy-start.4 = (f32[1,9,32,8]{2,3,1,0:T(8,128)S(1)}, f32[1,9,32,8]{2,3,1,0:T(8,128)}, u32[]{:S(2)}) copy-start(f32[1,9,32,8]{2,3,1,0:T(8,128)} %param.22) | copy-start | bytes 27652
  14.2 3.9 %collective-permute-start.1 = (bf16[2,1,2,8,512]{4,3,2,0,1:T(8,128)(2,1)S(1)}, bf16[2,1,2,8,512]{4,3,2,0,1:T(8,128)(2,1)S(1)}, u32[]{:S(2)}, u32[]{:S(2)}) collective-permute-start(bf16[2,1,2,8,512]{4,3,2,0,1:T(8,128)(2,1)S(1)} %bitcast_select_fusion.8), channel_id=1, source_target_pairs={{0,4},{1,5},{2,6},{3,7},{4,0},{5,1},{6,2},{7,3},{8,12},{9,13},{10,... | collective-permute-start | bytes 98312 | tf_op jit(solution)/shard_map/ppermute | solution.py:201
  18.8 4.3 %collective-permute-start.2 = (bf16[2,2,1,2,8,512]{5,4,3,1,0,2:T(8,128)(2,1)S(1)}, bf16[2,2,1,2,8,512]{5,4,3,1,0,2:T(8,128)(2,1)S(1)}, u32[]{:S(2)}, u32[]{:S(2)}) collective-permute-start(bf16[2,2,1,2,8,512]{5,4,3,1,0,2:T(8,128)(2,1)S(1)} %bitcast_select_fusion.6), channel_id=1, source_target_pairs={{0,2},{1,3},{2,0},{3,1},{4,6},{5,7},{6,4},{7,5},{8,10},{9,11},{10,... | collective-permute-start | bytes 196616 | tf_op jit(solution)/shard_map/ppermute | solution.py:201
  23.8 1.4 %collective-permute-start.3 = (bf16[2,2,2,1,2,8,512]{6,5,4,2,1,0,3:T(8,128)(2,1)S(1)}, bf16[2,2,2,1,2,8,512]{6,5,4,2,1,0,3:T(8,128)(2,1)S(1)}, u32[]{:S(2)}, u32[]{:S(2)}) collective-permute-start(bf16[2,2,2,1,2,8,512]{6,5,4,2,1,0,3:T(8,128)(2,1)S(1)} %bitcast_select_fusion.4), channel_id=1, source_target_pairs={{0,1},{1,0},{2,3},{3,2},{4,5},{5,4},{6,7},{7,6},{8,9},{9,8},{10,11... | collective-permute-start | bytes 393224 | tf_op jit(solution)/shard_map/ppermute | solution.py:201
  27.7 5.6 %copy-start.3 = (bf16[512,512]{1,0:T(8,128)(2,1)S(1)}, bf16[512,512]{1,0:T(8,128)(2,1)}, u32[]{:S(2)}) copy-start(bf16[512,512]{1,0:T(8,128)(2,1)} %param.23) | copy-start | bytes 1572868
  28.8 10.1 %collective-permute-start.10 = (bf16[1,6,8,512]{3,2,1,0:T(8,128)(2,1)S(1)}, bf16[1,6,8,512]{3,2,1,0:T(8,128)(2,1)S(1)}, u32[]{:S(2)}, u32[]{:S(2)}) collective-permute-start(bf16[1,6,8,512]{3,2,1,0:T(8,128)(2,1)S(1)} %get-tuple-element.78), channel_id=1, source_target_pairs={{0,12},{1,13},{2,14},{3,15},{4,8},{5,9},{6,10},{7,11},{8,4},{9,5},... | collective-permute-start | bytes 147464 | tf_op jit(solution)/shard_map/ppermute | solution.py:201
  30.7 8.1 %collective-permute-start.9 = (bf16[1,6,8,512]{3,2,1,0:T(8,128)(2,1)S(1)}, bf16[1,6,8,512]{3,2,1,0:T(8,128)(2,1)S(1)}, u32[]{:S(2)}, u32[]{:S(2)}) collective-permute-start(bf16[1,6,8,512]{3,2,1,0:T(8,128)(2,1)S(1)} %get-tuple-element.78), channel_id=1, source_target_pairs={{0,8},{1,9},{2,10},{3,11},{4,12},{5,13},{6,14},{7,15},{8,0},{9,1},... | collective-permute-start | bytes 147464 | tf_op jit(solution)/shard_map/ppermute | solution.py:201
  31.9 7.0 %collective-permute-start.8 = (bf16[1,6,8,512]{3,2,1,0:T(8,128)(2,1)S(1)}, bf16[1,6,8,512]{3,2,1,0:T(8,128)(2,1)S(1)}, u32[]{:S(2)}, u32[]{:S(2)}) collective-permute-start(bf16[1,6,8,512]{3,2,1,0:T(8,128)(2,1)S(1)} %get-tuple-element.78), channel_id=1, source_target_pairs={{0,4},{1,5},{2,6},{3,7},{4,0},{5,1},{6,2},{7,3},{8,12},{9,13},{10,... | collective-permute-start | bytes 147464 | tf_op jit(solution)/shard_map/ppermute | solution.py:201
  34.3 7.2 %collective-permute-start.6 = (bf16[1,32,3,512]{3,2,1,0:T(4,128)(2,1)S(1)}, bf16[1,32,3,512]{3,2,1,0:T(4,128)(2,1)S(1)}, u32[]{:S(2)}, u32[]{:S(2)}) collective-permute-start(bf16[1,32,3,512]{3,2,1,0:T(4,128)(2,1)S(1)} %get-tuple-element.67), channel_id=1, source_target_pairs={{0,1},{1,2},{2,3},{3,4},{4,5},{5,6},{6,7},{7,8},{8,9},{9,10},{10,1... | collective-permute-start | bytes 294920 | tf_op jit(solution)/shard_map/ppermute | solution.py:19
  34.4 7.2 %collective-permute-start.7 = (bf16[1,32,3,512]{3,2,1,0:T(4,128)(2,1)S(1)}, bf16[1,32,3,512]{3,2,1,0:T(4,128)(2,1)S(1)}, u32[]{:S(2)}, u32[]{:S(2)}) collective-permute-start(bf16[1,32,3,512]{3,2,1,0:T(4,128)(2,1)S(1)} %get-tuple-element.68), channel_id=1, source_target_pairs={{1,0},{2,1},{3,2},{4,3},{5,4},{6,5},{7,6},{8,7},{9,8},{10,9},{11,1... | collective-permute-start | bytes 294920 | tf_op jit(solution)/shard_map/ppermute | solution.py:20
  39.6 7.3 %collective-permute-start.13 = (bf16[4,1,6,8,512]{4,3,2,0,1:T(8,128)(2,1)S(1)}, bf16[4,1,6,8,512]{4,3,2,0,1:T(8,128)(2,1)S(1)}, u32[]{:S(2)}, u32[]{:S(2)}) collective-permute-start(bf16[4,1,6,8,512]{4,3,2,0,1:T(8,128)(2,1)S(1)} %bitcast_select_fusion.2), channel_id=1, source_target_pairs={{0,3},{1,2},{2,1},{3,0},{4,7},{5,6},{6,5},{7,4},{8,11},{9,10},{10,... | collective-permute-start | bytes 589832 | tf_op jit(solution)/shard_map/ppermute | solution.py:201
  39.7 8.9 %collective-permute-start.12 = (bf16[4,1,6,8,512]{4,3,2,0,1:T(8,128)(2,1)S(1)}, bf16[4,1,6,8,512]{4,3,2,0,1:T(8,128)(2,1)S(1)}, u32[]{:S(2)}, u32[]{:S(2)}) collective-permute-start(bf16[4,1,6,8,512]{4,3,2,0,1:T(8,128)(2,1)S(1)} %bitcast_select_fusion.2), channel_id=1, source_target_pairs={{0,2},{1,3},{2,0},{3,1},{4,6},{5,7},{6,4},{7,5},{8,10},{9,11},{10,... | collective-permute-start | bytes 589832 | tf_op jit(solution)/shard_map/ppermute | solution.py:201
  39.8 8.8 %collective-permute-start.11 = (bf16[4,1,6,8,512]{4,3,2,0,1:T(8,128)(2,1)S(1)}, bf16[4,1,6,8,512]{4,3,2,0,1:T(8,128)(2,1)S(1)}, u32[]{:S(2)}, u32[]{:S(2)}) collective-permute-start(bf16[4,1,6,8,512]{4,3,2,0,1:T(8,128)(2,1)S(1)} %bitcast_select_fusion.2), channel_id=1, source_target_pairs={{0,1},{1,0},{2,3},{3,2},{4,5},{5,4},{6,7},{7,6},{8,9},{9,8},{10,11... | collective-permute-start | bytes 589832 | tf_op jit(solution)/shard_map/ppermute | solution.py:201
  42.0 1.2 %copy-start.2 = (bf16[512,512]{1,0:T(8,128)(2,1)S(1)}, bf16[512,512]{1,0:T(8,128)(2,1)}, u32[]{:S(2)}) copy-start(bf16[512,512]{1,0:T(8,128)(2,1)} %param.24) | copy-start | bytes 1572868

commit v24 on v22

--- a/solution.py
+++ b/solution.py
@@ -80,8 +80,13 @@
 
 
 def attention_kernel(
-    q_ref, kc_ref, kr_ref, vc_ref, vr_ref, lat_ref, wo_ref, out_ref, att_ref, k_ref, v_ref
+    q_ref, kc_ref, kr_ref, vc_ref, vr_ref, lat_hbm, wo_hbm, out_ref, att_ref, k_ref, v_ref,
+    lat_ref, wo_ref, sems,
 ):
+    lat_copy = pltpu.make_async_copy(lat_hbm, lat_ref, sems.at[0])
+    wo_copy = pltpu.make_async_copy(wo_hbm, wo_ref, sems.at[1])
+    lat_copy.start()
+    wo_copy.start()
     middle = kc_ref.shape[0]
     k_ref[pl.ds(0, middle)] = kc_ref[...]
     k_ref[pl.ds(middle, kr_ref.shape[0])] = kr_ref[...]
@@ -132,6 +137,8 @@
             o = jnp.dot(w, v_g, preferred_element_type=jnp.float32)
             acc = jnp.where(lane == part, o, acc)
         att_ref[:, lanes] = acc.astype(jnp.bfloat16)
+    wo_copy.wait()
+    lat_copy.wait()
     mixed = jnp.dot(att_ref[...], wo_ref[...], preferred_element_type=jnp.float32)
     lat = lat_ref[...].reshape(cells, channels)
     out_ref[...] = (lat.astype(jnp.float32) + mixed).astype(out_ref.dtype)
@@ -149,12 +156,15 @@
     out = pl.pallas_call(
         attention_kernel,
         out_shape=jax.ShapeDtypeStruct((cells, channels), own_tile.dtype),
-        in_specs=[vmem] * 7,
+        in_specs=[vmem] * 5 + [pl.BlockSpec(memory_space=pl.ANY)] * 2,
         out_specs=vmem,
         scratch_shapes=[
             pltpu.VMEM((cells, channels), jnp.bfloat16),
             pltpu.VMEM((positions, channels), jnp.bfloat16),
             pltpu.VMEM((positions, channels), jnp.bfloat16),
+            pltpu.VMEM(own_tile.shape, own_tile.dtype),
+            pltpu.VMEM(w_output.shape, w_output.dtype),
+            pltpu.SemaphoreType.DMA((2,)),
         ],
     )(
         query.reshape(cells, channels) * jnp.asarray((channels // HEADS) ** (-0.5), query.dtype),

time: 57.6 us -> 57.5 us (level)
  no operation moved by 1% of the time
where the time goes in v24:
time: 57.5 us; the launch traced here: 56.6 us
  starting transfers between devices  22.9 us (40%)
  waiting for transfers between devices  7.08 us (12%)
  Pallas kernels  6.93 us (12%)
  other arithmetic  6.75 us (12%)
  matrix products  6.27 us (11%)
  local copies, waits for them, and re-layouts  6.12 us (11%)
    ppermute x12, starting transfers between devices, doubling_gather(): lax.ppermute(held, axis, [(i, i ^ d * stride) for i in range(count)])  14 us
    ppermute x2, starting transfers between devices, padded_2(): after = lax.ppermute(first, axis, down)  8.86 us
    ppermute x12, waiting for transfers between devices, doubling_gather(): lax.ppermute(held, axis, [(i, i ^ d * stride) for i in range(count)])  7.05 us
    pallas_call x1, Pallas kernels, attend_and_mix(): pl.pallas_call(attention_kernel, out_shape=jax.ShapeDtypeStruct((cells, c...  6.93 us
    dot_general x5, matrix products, project(): jnp.dot(flat, weight, preferred_element_type=jnp.float32)  5.3 us
    gather x4, local copies, waits for them, and re-layouts, doubling_gather(): jnp.take(jnp.stack(got), digit ^ jnp.arange(r, dtype=jnp.int32), axis=0)  2.27 us
    unnamed x17, local copies, waits for them, and re-layouts  1.45 us
  transfers between devices with their start and end apart: 16, of which 4 were waited for; matrix products, arithmetic and copies ran while one was open for 16% of the time, Pallas kernels for 0%

profile of v24, /device:TPU:0, one launch (start us, length us, event | category | flops | bytes accessed | tf_op | source)
XLA Modules:
  0.0 56.6 jit_solution(3397493725751176862)
XLA Ops:
  0.0 0.8 %copy.125 = s32[1,2,3]{2,1,0:T(2,128)S(1)} copy(s32[1,2,3]{2,1,0:T(2,128)} %param.27) | data formatting | bytes 48
  0.8 1.1 %fusion.7 = f32[32,8]{1,0:T(8,128)S(1)} fusion(bf16[1,32,8,512]{3,2,1,0:T(8,128)(2,1)} %param.20), kind=kLoop, calls=%fused_computation.26 | loop fusion | flops 392960 | bytes 263168 | tf_op jit(solution)/shard_map/reduce_sum | solution.py:27
  1.9 0.6 %copy-done.5 = f32[512]{0:T(512)S(1)} copy-done((f32[512]{0:T(512)S(1)}, f32[512]{0:T(512)}, u32[]{:S(2)}) %copy-start.5) | copy-done | bytes 2072
  2.5 0.1 fusion.9
  2.7 5.1 %collective-permute-start.2 = (bf16[1,2,8,512]{3,2,1,0:T(8,128)(2,1)S(1)}, bf16[1,2,8,512]{3,2,1,0:T(8,128)(2,1)S(1)}, u32[]{:S(2)}, u32[]{:S(2)}) collective-permute-start(bf16[1,2,8,512]{3,2,1,0:T(8,128)(2,1)S(1)} %get-tuple-element.91), channel_id=1, source_target_pairs={{0,12},{1,13},{2,14},{3,15},{4,8},{5,9},{6,10},{7,11},{8,4},{9,5},... | collective-permute-start | bytes 49160 | tf_op jit(solution)/shard_map/ppermute | solution.py:211
  7.8 0.6 %collective-permute-start = (bf16[1,2,8,512]{3,2,1,0:T(8,128)(2,1)S(1)}, bf16[1,2,8,512]{3,2,1,0:T(8,128)(2,1)S(1)}, u32[]{:S(2)}, u32[]{:S(2)}) collective-permute-start(bf16[1,2,8,512]{3,2,1,0:T(8,128)(2,1)S(1)} %get-tuple-element.91), channel_id=1, source_target_pairs={{0,4},{1,5},{2,6},{3,7},{4,0},{5,1},{6,2},{7,3},{8,12},{9,13},{10,... | collective-permute-start | bytes 49160 | tf_op jit(solution)/shard_map/ppermute | solution.py:211
  8.4 0.1 multiply_convert_fusion
  8.6 0.1 fusion.45
  8.7 4.4 %collective-permute-start.7 = (bf16[1,32,1,512]{3,2,1,0:T(2,128)(2,1)S(1)}, bf16[1,32,1,512]{3,2,1,0:T(2,128)(2,1)S(1)}, u32[]{:S(2)}, u32[]{:S(2)}) collective-permute-start(bf16[1,32,1,512]{3,2,1,0:T(2,128)(2,1)S(1)} %get-tuple-element.72), channel_id=1, source_target_pairs={{1,0},{2,1},{3,2},{4,3},{5,4},{6,5},{7,6},{8,7},{9,8},{10,9},{11,1... | collective-permute-start | bytes 98312 | tf_op jit(solution)/shard_map/ppermute | solution.py:20
  13.2 0.6 %compare_reduce_fusion = pred[]{:T(512)} fusion(), kind=kLoop, calls=%fused_computation.117 | loop fusion | flops 5 | bytes 1 | tf_op jit(solution)/shard_map/reduce.6
  13.8 0.2 slice_reduce_fusion
  14.0 0.2 compare_reduce_fusion.1
  14.3 0.7 %fusion.29 = (s32[2,1,1]{2,0,1:T(2,128)S(1)}, s32[2,1,1]{2,0,1:T(2,128)S(1)}, s32[2,1,1]{2,0,1:T(2,128)S(1)}) fusion(pred[]{:T(512)} %compare_reduce_fusion, s32[1,2,3]{2,1,0:T(2,128)S(1)} %copy.125, s32[2,3]{1,0:T(2,128)S(1)} %bitcast.188), kind=kLoop, calls=%fused_computation.123 | loop fusion | flops 78 | bytes 41 | tf_op jit(solution)/shard_map/stack | solution.py:229
  15.2 0.1 copy.78
  15.3 0.1 copy.79
  16.2 0.6 gather_fusion
  17.0 1.8 %collective-permute-start.3 = (bf16[4,1,2,8,512]{4,3,2,0,1:T(8,128)(2,1)S(1)}, bf16[4,1,2,8,512]{4,3,2,0,1:T(8,128)(2,1)S(1)}, u32[]{:S(2)}, u32[]{:S(2)}) collective-permute-start(bf16[4,1,2,8,512]{4,3,2,0,1:T(8,128)(2,1)S(1)} %bitcast_select_fusion.4), channel_id=1, source_target_pairs={{0,1},{1,0},{2,3},{3,2},{4,5},{5,4},{6,7},{7,6},{8,9},{9,8},{10,11... | collective-permute-start | bytes 196616 | tf_op jit(solution)/shard_map/ppermute | solution.py:211
  18.8 0.3 maximum_bitcast_fusion.1
  19.1 1.6 %collective-permute-done.5 = bf16[4,1,2,8,512]{4,3,2,0,1:T(8,128)(2,1)S(1)} collective-permute-done((bf16[4,1,2,8,512]{4,3,2,0,1:T(8,128)(2,1)S(1)}, bf16[4,1,2,8,512]{4,3,2,0,1:T(8,128)(2,1)S(1)}, u32[]{:S(2)}, u32[]{:S(2)}) %collective-permute-start.5) | collective-permute-done | bytes 65568 | tf_op jit(solution)/shard_map/ppermute | solution.py:211
  20.7 1.2 %collective-permute-done.4 = bf16[4,1,2,8,512]{4,3,2,0,1:T(8,128)(2,1)S(1)} collective-permute-done((bf16[4,1,2,8,512]{4,3,2,0,1:T(8,128)(2,1)S(1)}, bf16[4,1,2,8,512]{4,3,2,0,1:T(8,128)(2,1)S(1)}, u32[]{:S(2)}, u32[]{:S(2)}) %collective-permute-start.4) | collective-permute-done | bytes 65568 | tf_op jit(solution)/shard_map/ppermute | solution.py:211
  22.0 0.6 gather_fusion.1
  22.6 0.1 fusion.16
  22.7 0.3 fusion.3
  23.1 0.2 rev.9
  23.4 1.0 %fusion.55 = bf16[1,32,8,512]{3,2,1,0:T(8,128)(2,1)S(1)} fusion(bf16[1,10,512]{2,1,0:T(8,128)(2,1)S(1)} %get-tuple-element.89, bf16[32,10,512]{2,1,0:T(8,128)(2,1)S(1)} %maximum_bitcast_fusion.1, f32[32,8]{1,0:T(8,128)S(1)} %copy.91, f32[32,8]{1,0:T(8,128)S(1)} %copy.90, f32[32,8]{1,0:T(8,128)S(1)} %copy.89, f32[32,8]{1,0:T(8,128)S(1)} %copy.88, ...), kind=kLoop, calls=%fused_computation.143 | loop fusion | flops 5898240 | bytes 1753088 | tf_op jit(solution)/shard_map/broadcast_in_dim | solution.py:239
  24.5 1.1 %add_convert_fusion = bf16[32,8,512]{2,1,0:T(8,128)(2,1)S(1)} fusion(bf16[32,10,512]{2,1,0:T(8,128)(2,1)S(1)} %maximum_bitcast_fusion.1, bf16[1,10,512]{2,1,0:T(8,128)(2,1)S(1)} %get-tuple-element.89, bf16[1,10,512]{2,1,0:T(8,128)(2,1)S(1)} %get-tuple-element.88, f32[32,8]{1,0:T(8,128)S(1)} %copy.91, f32[32,8]{1,0:T(8,128)S(1)} %copy.90, ...), kind=kLoop, calls=%fused_computation.31 | loop fusion | flops 5898240 | bytes 1753088 | tf_op jit(solution)/shard_map/convert_element_type | solution.py:69
  25.6 2.0 %collective-permute-start.12 = (bf16[1,6,8,512]{3,2,1,0:T(8,128)(2,1)S(1)}, bf16[1,6,8,512]{3,2,1,0:T(8,128)(2,1)S(1)}, u32[]{:S(2)}, u32[]{:S(2)}) collective-permute-start(bf16[1,6,8,512]{3,2,1,0:T(8,128)(2,1)S(1)} %get-tuple-element.78), channel_id=1, source_target_pairs={{0,12},{1,13},{2,14},{3,15},{4,8},{5,9},{6,10},{7,11},{8,4},{9,5},... | collective-permute-start | bytes 147464 | tf_op jit(solution)/shard_map/ppermute | solution.py:211
  27.6 2.4 %collective-permute-start.10 = (bf16[1,6,8,512]{3,2,1,0:T(8,128)(2,1)S(1)}, bf16[1,6,8,512]{3,2,1,0:T(8,128)(2,1)S(1)}, u32[]{:S(2)}, u32[]{:S(2)}) collective-permute-start(bf16[1,6,8,512]{3,2,1,0:T(8,128)(2,1)S(1)} %get-tuple-element.78), channel_id=1, source_target_pairs={{0,4},{1,5},{2,6},{3,7},{4,0},{5,1},{6,2},{7,3},{8,12},{9,13},{10,... | collective-permute-start | bytes 147464 | tf_op jit(solution)/shard_map/ppermute | solution.py:211
  30.0 1.0 %fusion.1.q_ref = bf16[256,512]{1,0:T(8,128)(2,1)} fusion(bf16[512,512]{1,0:T(8,128)(2,1)S(1)} %copy-done.3, bf16[32,8,512]{2,1,0:T(8,128)(2,1)S(1)} %add_convert_fusion), kind=kOutput, calls=%fused_computation.11 | convolution fusion | flops 134479872 | bytes 1048576 | tf_op jit(solution)/shard_map/dot_general | solution.py:76
  31.2 4.4 %collective-permute-start.9 = (bf16[1,32,3,512]{3,2,1,0:T(4,128)(2,1)S(1)}, bf16[1,32,3,512]{3,2,1,0:T(4,128)(2,1)S(1)}, u32[]{:S(2)}, u32[]{:S(2)}) collective-permute-start(bf16[1,32,3,512]{3,2,1,0:T(4,128)(2,1)S(1)} %get-tuple-element.68), channel_id=1, source_target_pairs={{1,0},{2,1},{3,2},{4,3},{5,4},{6,5},{7,6},{8,7},{9,8},{10,9},{11,1... | collective-permute-start | bytes 294920 | tf_op jit(solution)/shard_map/ppermute | solution.py:20
  35.7 0.6 gather_fusion.2
  36.6 1.8 %collective-permute-start.13 = (bf16[4,1,6,8,512]{4,3,2,0,1:T(8,128)(2,1)S(1)}, bf16[4,1,6,8,512]{4,3,2,0,1:T(8,128)(2,1)S(1)}, u32[]{:S(2)}, u32[]{:S(2)}) collective-permute-start(bf16[4,1,6,8,512]{4,3,2,0,1:T(8,128)(2,1)S(1)} %bitcast_select_fusion.2), channel_id=1, source_target_pairs={{0,1},{1,0},{2,3},{3,2},{4,5},{5,4},{6,7},{7,6},{8,9},{9,8},{10,11... | collective-permute-start | bytes 589832 | tf_op jit(solution)/shard_map/ppermute | solution.py:211
  38.4 0.3 pad_maximum_fusion
  38.7 0.1 reshape_squeeze.3
  38.8 1.2 %convolution_convert_fusion.vc_ref = bf16[448,512]{1,0:T(8,128)(2,1)} fusion(bf16[448,512]{1,0:T(8,128)(2,1)S(1)} %reshape_squeeze.3, bf16[512,512]{1,0:T(8,128)(2,1)S(1)} %copy-done), kind=kOutput, calls=%fused_computation.4 | convolution fusion | flops 235110400 | bytes 1441792 | tf_op jit(solution)/shard_map/dot_general | solution.py:76
  40.0 1.2 %convolution_convert_fusion.1.kc_ref = bf16[448,512]{1,0:T(8,128)(2,1)} fusion(bf16[448,512]{1,0:T(8,128)(2,1)S(1)} %reshape_squeeze.3, bf16[512,512]{1,0:T(8,128)(2,1)S(1)} %copy-done.2), kind=kOutput, calls=%fused_computation.5 | convolution fusion | flops 235110400 | bytes 1441792 | tf_op jit(solution)/shard_map/dot_general | solution.py:76
  41.2 2.5 %collective-permute-done.15 = bf16[4,1,6,8,512]{4,3,2,0,1:T(8,128)(2,1)S(1)} collective-permute-done((bf16[4,1,6,8,512]{4,3,2,0,1:T(8,128)(2,1)S(1)}, bf16[4,1,6,8,512]{4,3,2,0,1:T(8,128)(2,1)S(1)}, u32[]{:S(2)}, u32[]{:S(2)}) %collective-permute-start.15) | collective-permute-done | bytes 196640 | tf_op jit(solution)/shard_map/ppermute | solution.py:211
  43.8 1.7 %collective-permute-done.14 = bf16[4,1,6,8,512]{4,3,2,0,1:T(8,128)(2,1)S(1)} collective-permute-done((bf16[4,1,6,8,512]{4,3,2,0,1:T(8,128)(2,1)S(1)}, bf16[4,1,6,8,512]{4,3,2,0,1:T(8,128)(2,1)S(1)}, u32[]{:S(2)}, u32[]{:S(2)}) %collective-permute-start.14) | collective-permute-done | bytes 196640 | tf_op jit(solution)/shard_map/ppermute | solution.py:211
  45.4 0.1 maximum_bitcast_fusion
  45.5 0.6 %gather_fusion.3 = bf16[4,4,6,8,512]{4,3,2,1,0:T(8,128)(2,1)S(1)} fusion(bf16[4,4,6,8,512]{4,3,2,1,0:T(8,128)(2,1)S(1)} %maximum_bitcast_fusion, s32[1024]{0:T(1024)S(1)} %pad_clamp_fusion), kind=kCustom, calls=%fused_computation.3 | custom fusion | bytes 1572880 | tf_op jit(solution)/shard_map/jit(_take)/gather | solution.py:213
  46.1 0.1 fusion.5
  46.3 0.6 %fusion = bf16[2,3,3,8,512]{4,1,3,2,0:T(4,128)(2,1)S(1)} fusion(bf16[16,2,3,8,512]{4,3,2,1,0:T(8,128)(2,1)S(1)} %bitcast.169, pred[2,3,2]{1,2,0:T(4,128)(4,1)S(1)} %iota_compare_fusion.1, pred[2,3,16]{2,1,0:T(4,128)(4,1)S(1)} %iota_compare_fusion), kind=kOutput, calls=%fused_computation.8 | convolution fusion | flops 4792512 | bytes 933996 | tf_op jit(solution)/shard_map/...nf,nfrwc->...rwc/dot_general | solution.py:192
  47.1 0.1 slice.280
  47.3 0.2 rev.10
  47.6 0.1 broadcast_select_fusion
  47.8 0.9 %convolution_convert_fusion.3.vr_ref = bf16[192,512]{1,0:T(8,128)(2,1)} fusion(bf16[512,512]{1,0:T(8,128)(2,1)S(1)} %copy-done, bf16[84,512]{1,0:T(8,128)(2,1)S(1)} %reshape.396), kind=kOutput, calls=%fused_computation.9 | convolution fusion | flops 100761600 | bytes 806912 | tf_op jit(solution)/shard_map/dot_general | solution.py:76
  48.7 1.0 %convolution_convert_fusion.4.kr_ref = bf16[192,512]{1,0:T(8,128)(2,1)} fusion(bf16[512,512]{1,0:T(8,128)(2,1)S(1)} %copy-done.2, bf16[84,512]{1,0:T(8,128)(2,1)S(1)} %reshape.396), kind=kOutput, calls=%fused_computation.10 | convolution fusion | flops 100761600 | bytes 806912 | tf_op jit(solution)/shard_map/dot_general | solution.py:76
  49.7 6.9 %shard_map.82 = bf16[256,512]{1,0:T(8,128)(2,1)} custom-call(bf16[256,512]{1,0:T(8,128)(2,1)} %fusion.1.q_ref, bf16[448,512]{1,0:T(8,128)(2,1)} %convolution_convert_fusion.1.kc_ref, bf16[192,512]{1,0:T(8,128)(2,1)} %convolution_convert_fusion.4.kr_ref, bf16[448,512]{1,0:T(8,128)(2,1)} %convolution_convert_fusion.vc_ref, ...), custom_call_target="tpu_custom_call" | custom-call | tf_op jit(solution)/shard_map/pallas_call | solution.py:156
  (86 shorter events, 2.5 us)
Async XLA Ops:
  0.0 38.8 %copy-start = (bf16[512,512]{1,0:T(8,128)(2,1)S(1)}, bf16[512,512]{1,0:T(8,128)(2,1)}, u32[]{:S(2)}) copy-start(bf16[512,512]{1,0:T(8,128)(2,1)} %param.25) | copy-start | bytes 1572868
  0.0 1.9 %copy-start.1 = (bf16[1,32,8,512]{3,2,1,0:T(8,128)(2,1)S(1)}, bf16[1,32,8,512]{3,2,1,0:T(8,128)(2,1)}, u32[]{:S(2)}) copy-start(bf16[1,32,8,512]{3,2,1,0:T(8,128)(2,1)} %param.20) | copy-start | bytes 786436
  1.8 0.7 %copy-start.5 = (f32[512]{0:T(512)S(1)}, f32[512]{0:T(512)}, u32[]{:S(2)}) copy-start(f32[512]{0:T(512)} %param.21) | copy-start | bytes 6148
  2.7 13.5 %collective-permute-start.2 = (bf16[1,2,8,512]{3,2,1,0:T(8,128)(2,1)S(1)}, bf16[1,2,8,512]{3,2,1,0:T(8,128)(2,1)S(1)}, u32[]{:S(2)}, u32[]{:S(2)}) collective-permute-start(bf16[1,2,8,512]{3,2,1,0:T(8,128)(2,1)S(1)} %get-tuple-element.91), channel_id=1, source_target_pairs={{0,12},{1,13},{2,14},{3,15},{4,8},{5,9},{6,10},{7,11},{8,4},{9,5},... | collective-permute-start | bytes 49160 | tf_op jit(solution)/shard_map/ppermute | solution.py:211
  7.8 8.4 %collective-permute-start.1 = (bf16[1,2,8,512]{3,2,1,0:T(8,128)(2,1)S(1)}, bf16[1,2,8,512]{3,2,1,0:T(8,128)(2,1)S(1)}, u32[]{:S(2)}, u32[]{:S(2)}) collective-permute-start(bf16[1,2,8,512]{3,2,1,0:T(8,128)(2,1)S(1)} %get-tuple-element.91), channel_id=1, source_target_pairs={{0,8},{1,9},{2,10},{3,11},{4,12},{5,13},{6,14},{7,15},{8,0},{9,1},... | collective-permute-start | bytes 49160 | tf_op jit(solution)/shard_map/ppermute | solution.py:211
  7.8 8.4 %collective-permute-start = (bf16[1,2,8,512]{3,2,1,0:T(8,128)(2,1)S(1)}, bf16[1,2,8,512]{3,2,1,0:T(8,128)(2,1)S(1)}, u32[]{:S(2)}, u32[]{:S(2)}) collective-permute-start(bf16[1,2,8,512]{3,2,1,0:T(8,128)(2,1)S(1)} %get-tuple-element.91), channel_id=1, source_target_pairs={{0,4},{1,5},{2,6},{3,7},{4,0},{5,1},{6,2},{7,3},{8,12},{9,13},{10,... | collective-permute-start | bytes 49160 | tf_op jit(solution)/shard_map/ppermute | solution.py:211
  8.7 10.1 %collective-permute-start.6 = (bf16[1,32,1,512]{3,2,1,0:T(2,128)(2,1)S(1)}, bf16[1,32,1,512]{3,2,1,0:T(2,128)(2,1)S(1)}, u32[]{:S(2)}, u32[]{:S(2)}) collective-permute-start(bf16[1,32,1,512]{3,2,1,0:T(2,128)(2,1)S(1)} %get-tuple-element.71), channel_id=1, source_target_pairs={{0,1},{1,2},{2,3},{3,4},{4,5},{5,6},{6,7},{7,8},{8,9},{9,10},{10,1... | collective-permute-start | bytes 98312 | tf_op jit(solution)/shard_map/ppermute | solution.py:19
  8.7 10.1 %collective-permute-start.7 = (bf16[1,32,1,512]{3,2,1,0:T(2,128)(2,1)S(1)}, bf16[1,32,1,512]{3,2,1,0:T(2,128)(2,1)S(1)}, u32[]{:S(2)}, u32[]{:S(2)}) collective-permute-start(bf16[1,32,1,512]{3,2,1,0:T(2,128)(2,1)S(1)} %get-tuple-element.72), channel_id=1, source_target_pairs={{1,0},{2,1},{3,2},{4,3},{5,4},{6,5},{7,6},{8,7},{9,8},{10,9},{11,1... | collective-permute-start | bytes 98312 | tf_op jit(solution)/shard_map/ppermute | solution.py:20
  14.2 1.2 %copy-start.4 = (f32[1,9,32,8]{2,3,1,0:T(8,128)S(1)}, f32[1,9,32,8]{2,3,1,0:T(8,128)}, u32[]{:S(2)}) copy-start(f32[1,9,32,8]{2,3,1,0:T(8,128)} %param.22) | copy-start | bytes 27652
  16.9 3.8 %collective-permute-start.5 = (bf16[4,1,2,8,512]{4,3,2,0,1:T(8,128)(2,1)S(1)}, bf16[4,1,2,8,512]{4,3,2,0,1:T(8,128)(2,1)S(1)}, u32[]{:S(2)}, u32[]{:S(2)}) collective-permute-start(bf16[4,1,2,8,512]{4,3,2,0,1:T(8,128)(2,1)S(1)} %bitcast_select_fusion.4), channel_id=1, source_target_pairs={{0,3},{1,2},{2,1},{3,0},{4,7},{5,6},{6,5},{7,4},{8,11},{9,10},{10,... | collective-permute-start | bytes 196616 | tf_op jit(solution)/shard_map/ppermute | solution.py:211
  17.0 5.0 %collective-permute-start.4 = (bf16[4,1,2,8,512]{4,3,2,0,1:T(8,128)(2,1)S(1)}, bf16[4,1,2,8,512]{4,3,2,0,1:T(8,128)(2,1)S(1)}, u32[]{:S(2)}, u32[]{:S(2)}) collective-permute-start(bf16[4,1,2,8,512]{4,3,2,0,1:T(8,128)(2,1)S(1)} %bitcast_select_fusion.4), channel_id=1, source_target_pairs={{0,2},{1,3},{2,0},{3,1},{4,6},{5,7},{6,4},{7,5},{8,10},{9,11},{10,... | collective-permute-start | bytes 196616 | tf_op jit(solution)/shard_map/ppermute | solution.py:211
  17.0 4.9 %collective-permute-start.3 = (bf16[4,1,2,8,512]{4,3,2,0,1:T(8,128)(2,1)S(1)}, bf16[4,1,2,8,512]{4,3,2,0,1:T(8,128)(2,1)S(1)}, u32[]{:S(2)}, u32[]{:S(2)}) collective-permute-start(bf16[4,1,2,8,512]{4,3,2,0,1:T(8,128)(2,1)S(1)} %bitcast_select_fusion.4), channel_id=1, source_target_pairs={{0,1},{1,0},{2,3},{3,2},{4,5},{5,4},{6,7},{7,6},{8,9},{9,8},{10,11... | collective-permute-start | bytes 196616 | tf_op jit(solution)/shard_map/ppermute | solution.py:211
  24.4 5.6 %copy-start.3 = (bf16[512,512]{1,0:T(8,128)(2,1)S(1)}, bf16[512,512]{1,0:T(8,128)(2,1)}, u32[]{:S(2)}) copy-start(bf16[512,512]{1,0:T(8,128)(2,1)} %param.23) | copy-start | bytes 1572868
  25.6 10.1 %collective-permute-start.12 = (bf16[1,6,8,512]{3,2,1,0:T(8,128)(2,1)S(1)}, bf16[1,6,8,512]{3,2,1,0:T(8,128)(2,1)S(1)}, u32[]{:S(2)}, u32[]{:S(2)}) collective-permute-start(bf16[1,6,8,512]{3,2,1,0:T(8,128)(2,1)S(1)} %get-tuple-element.78), channel_id=1, source_target_pairs={{0,12},{1,13},{2,14},{3,15},{4,8},{5,9},{6,10},{7,11},{8,4},{9,5},... | collective-permute-start | bytes 147464 | tf_op jit(solution)/shard_map/ppermute | solution.py:211
  27.6 8.1 %collective-permute-start.11 = (bf16[1,6,8,512]{3,2,1,0:T(8,128)(2,1)S(1)}, bf16[1,6,8,512]{3,2,1,0:T(8,128)(2,1)S(1)}, u32[]{:S(2)}, u32[]{:S(2)}) collective-permute-start(bf16[1,6,8,512]{3,2,1,0:T(8,128)(2,1)S(1)} %get-tuple-element.78), channel_id=1, source_target_pairs={{0,8},{1,9},{2,10},{3,11},{4,12},{5,13},{6,14},{7,15},{8,0},{9,1},... | collective-permute-start | bytes 147464 | tf_op jit(solution)/shard_map/ppermute | solution.py:211
  27.6 8.1 %collective-permute-start.10 = (bf16[1,6,8,512]{3,2,1,0:T(8,128)(2,1)S(1)}, bf16[1,6,8,512]{3,2,1,0:T(8,128)(2,1)S(1)}, u32[]{:S(2)}, u32[]{:S(2)}) collective-permute-start(bf16[1,6,8,512]{3,2,1,0:T(8,128)(2,1)S(1)} %get-tuple-element.78), channel_id=1, source_target_pairs={{0,4},{1,5},{2,6},{3,7},{4,0},{5,1},{6,2},{7,3},{8,12},{9,13},{10,... | collective-permute-start | bytes 147464 | tf_op jit(solution)/shard_map/ppermute | solution.py:211
  31.1 7.2 %collective-permute-start.8 = (bf16[1,32,3,512]{3,2,1,0:T(4,128)(2,1)S(1)}, bf16[1,32,3,512]{3,2,1,0:T(4,128)(2,1)S(1)}, u32[]{:S(2)}, u32[]{:S(2)}) collective-permute-start(bf16[1,32,3,512]{3,2,1,0:T(4,128)(2,1)S(1)} %get-tuple-element.67), channel_id=1, source_target_pairs={{0,1},{1,2},{2,3},{3,4},{4,5},{5,6},{6,7},{7,8},{8,9},{9,10},{10,1... | collective-permute-start | bytes 294920 | tf_op jit(solution)/shard_map/ppermute | solution.py:19
  31.2 7.2 %collective-permute-start.9 = (bf16[1,32,3,512]{3,2,1,0:T(4,128)(2,1)S(1)}, bf16[1,32,3,512]{3,2,1,0:T(4,128)(2,1)S(1)}, u32[]{:S(2)}, u32[]{:S(2)}) collective-permute-start(bf16[1,32,3,512]{3,2,1,0:T(4,128)(2,1)S(1)} %get-tuple-element.68), channel_id=1, source_target_pairs={{1,0},{2,1},{3,2},{4,3},{5,4},{6,5},{7,6},{8,7},{9,8},{10,9},{11,1... | collective-permute-start | bytes 294920 | tf_op jit(solution)/shard_map/ppermute | solution.py:20
  36.4 7.3 %collective-permute-start.15 = (bf16[4,1,6,8,512]{4,3,2,0,1:T(8,128)(2,1)S(1)}, bf16[4,1,6,8,512]{4,3,2,0,1:T(8,128)(2,1)S(1)}, u32[]{:S(2)}, u32[]{:S(2)}) collective-permute-start(bf16[4,1,6,8,512]{4,3,2,0,1:T(8,128)(2,1)S(1)} %bitcast_select_fusion.2), channel_id=1, source_target_pairs={{0,3},{1,2},{2,1},{3,0},{4,7},{5,6},{6,5},{7,4},{8,11},{9,10},{10,... | collective-permute-start | bytes 589832 | tf_op jit(solution)/shard_map/ppermute | solution.py:211
  36.5 8.9 %collective-permute-start.14 = (bf16[4,1,6,8,512]{4,3,2,0,1:T(8,128)(2,1)S(1)}, bf16[4,1,6,8,512]{4,3,2,0,1:T(8,128)(2,1)S(1)}, u32[]{:S(2)}, u32[]{:S(2)}) collective-permute-start(bf16[4,1,6,8,512]{4,3,2,0,1:T(8,128)(2,1)S(1)} %bitcast_select_fusion.2), channel_id=1, source_target_pairs={{0,2},{1,3},{2,0},{3,1},{4,6},{5,7},{6,4},{7,5},{8,10},{9,11},{10,... | collective-permute-start | bytes 589832 | tf_op jit(solution)/shard_map/ppermute | solution.py:211
  36.6 8.8 %collective-permute-start.13 = (bf16[4,1,6,8,512]{4,3,2,0,1:T(8,128)(2,1)S(1)}, bf16[4,1,6,8,512]{4,3,2,0,1:T(8,128)(2,1)S(1)}, u32[]{:S(2)}, u32[]{:S(2)}) collective-permute-start(bf16[4,1,6,8,512]{4,3,2,0,1:T(8,128)(2,1)S(1)} %bitcast_select_fusion.2), channel_id=1, source_target_pairs={{0,1},{1,0},{2,3},{3,2},{4,5},{5,4},{6,7},{7,6},{8,9},{9,8},{10,11... | collective-permute-start | bytes 589832 | tf_op jit(solution)/shard_map/ppermute | solution.py:211
  38.8 1.2 %copy-start.2 = (bf16[512,512]{1,0:T(8,128)(2,1)S(1)}, bf16[512,512]{1,0:T(8,128)(2,1)}, u32[]{:S(2)}) copy-start(bf16[512,512]{1,0:T(8,128)(2,1)} %param.24) | copy-start | bytes 1572868

commit v25 on v22

--- a/solution.py
+++ b/solution.py
@@ -206,6 +206,34 @@
     return held.reshape((count * block.shape[0],) + block.shape[1:])
 
 
+def raw_gather(block, axis, radix=4):
+    count = lax.axis_size(axis)
+    me = lax.axis_index(axis)
+    if count & (count - 1):
+        return lax.all_gather(block[None], axis, axis=0, tiled=True), (lambda j: j)
+    levels = []
+    stride = 1
+    while stride < count:
+        r = min(radix, count // stride)
+        levels.append((stride, r))
+        stride *= r
+    held = block
+    for stride, r in reversed(levels):
+        got = [held]
+        for d in range(1, r):
+            got.append(lax.ppermute(held, axis, [(i, i ^ (d * stride)) for i in range(count)]))
+        held = jnp.stack(got)
+
+    def locate(j):
+        gap = j ^ me
+        flat = 0
+        for stride, r in levels:
+            flat = flat * r + (gap // stride) % r
+        return flat
+
+    return held.reshape((count,) + block.shape), locate
+
+
 def local(latents, norm_gain, metric, w_query, w_key, w_value, w_output, seam_table):
     own_tile = latents[0]
     channels = own_tile.shape[-1]
@@ -228,11 +256,12 @@
     query = project(smoothed, w_query)
     field_wide = padded_2(smoothed[None], (("blk", 2),), RADIUS)
     rows3 = jnp.concatenate([smoothed[:RADIUS], smoothed[-RADIUS:]], axis=0)
-    got3 = doubling_gather(rows3[None], "blk")
+    got3, locate3 = raw_gather(rows3, "blk")
     count = got3.shape[0]
     edges3 = got3.reshape((count, 2, RADIUS) + got3.shape[2:])
     near = jnp.stack(
-        [seam_rows.at[:, 0].set((seam_rows[:, 0] + count + k) % count) for k in (-1, 0, 1)], axis=1
+        [seam_rows.at[:, 0].set(locate3((seam_rows[:, 0] + count + k) % count)) for k in (-1, 0, 1)],
+        axis=1,
     )
     picked = pick_all(near, edges3)
     field_got = jnp.concatenate(

time: 57.6 us -> 56.5 us (0.981)
  the two profiles are of different devices: /device:TPU:0 before, /device:TPU:1 now
where the time goes in v25:
time: 56.5 us; the launch traced here: 56.3 us
  starting transfers between devices  22 us (39%)
  waiting for transfers between devices  8.58 us (15%)
  Pallas kernels  7.05 us (12%)
  other arithmetic  6.57 us (12%)
  matrix products  6.27 us (11%)
  local copies, waits for them, and re-layouts  5.29 us (9%)
    ppermute x6, starting transfers between devices, doubling_gather(): lax.ppermute(held, axis, [(i, i ^ d * stride) for i in range(count)])  9.11 us
    ppermute x6, starting transfers between devices, raw_gather(): lax.ppermute(held, axis, [(i, i ^ d * stride) for i in range(count)])  9.01 us
    pallas_call x1, Pallas kernels, attend_and_mix(): pl.pallas_call(attention_kernel, out_shape=jax.ShapeDtypeStruct((cells, c...  7.05 us
    dot_general x5, matrix products, project(): jnp.dot(flat, weight, preferred_element_type=jnp.float32)  5.3 us
    ppermute x6, waiting for transfers between devices, raw_gather(): lax.ppermute(held, axis, [(i, i ^ d * stride) for i in range(count)])  5.15 us
    ppermute x2, starting transfers between devices, padded_2(): before = lax.ppermute(last, axis, up)  3.64 us
    ppermute x6, waiting for transfers between devices, doubling_gather(): lax.ppermute(held, axis, [(i, i ^ d * stride) for i in range(count)])  2.94 us
    unnamed x20, local copies, waits for them, and re-layouts  1.45 us
  transfers between devices with their start and end apart: 16, of which 4 were waited for; matrix products, arithmetic and copies ran while one was open for 15% of the time, Pallas kernels for 0%

profile of v25, /device:TPU:1, one launch (start us, length us, event | category | flops | bytes accessed | tf_op | source)
XLA Modules:
  0.0 56.3 jit_solution(11319688513738412271)
XLA Ops:
  0.0 0.8 %copy.139 = s32[1,2,3]{2,1,0:T(2,128)S(1)} copy(s32[1,2,3]{2,1,0:T(2,128)} %param.27) | data formatting | bytes 48
  0.8 1.1 %fusion.6 = f32[32,8]{1,0:T(8,128)S(1)} fusion(bf16[1,32,8,512]{3,2,1,0:T(8,128)(2,1)} %param.20), kind=kLoop, calls=%fused_computation.22 | loop fusion | flops 392960 | bytes 263168 | tf_op jit(solution)/shard_map/reduce_sum | solution.py:27
  1.9 0.6 %copy-done.5 = f32[512]{0:T(512)S(1)} copy-done((f32[512]{0:T(512)S(1)}, f32[512]{0:T(512)}, u32[]{:S(2)}) %copy-start.5) | copy-done | bytes 2072
  2.5 0.1 fusion.8
  2.7 4.2 %collective-permute-start.2 = (bf16[1,2,8,512]{3,2,1,0:T(8,128)(2,1)S(1)}, bf16[1,2,8,512]{3,2,1,0:T(8,128)(2,1)S(1)}, u32[]{:S(2)}, u32[]{:S(2)}) collective-permute-start(bf16[1,2,8,512]{3,2,1,0:T(8,128)(2,1)S(1)} %get-tuple-element.105), channel_id=1, source_target_pairs={{0,12},{1,13},{2,14},{3,15},{4,8},{5,9},{6,10},{7,11},{8,4},{9,5},... | collective-permute-start | bytes 49160 | tf_op jit(solution)/shard_map/ppermute | solution.py:201
  6.9 0.4 collective-permute-start
  7.3 0.1 multiply_convert_fusion
  7.5 2.6 %collective-permute-start.6 = (bf16[1,32,1,512]{3,2,1,0:T(2,128)(2,1)S(1)}, bf16[1,32,1,512]{3,2,1,0:T(2,128)(2,1)S(1)}, u32[]{:S(2)}, u32[]{:S(2)}) collective-permute-start(bf16[1,32,1,512]{3,2,1,0:T(2,128)(2,1)S(1)} %get-tuple-element.83), channel_id=1, source_target_pairs={{0,1},{1,2},{2,3},{3,4},{4,5},{5,6},{6,7},{7,8},{8,9},{9,10},{10,1... | collective-permute-start | bytes 98312 | tf_op jit(solution)/shard_map/ppermute | solution.py:19
  10.0 0.6 %compare_reduce_fusion = pred[]{:T(512)} fusion(), kind=kLoop, calls=%fused_computation.128 | loop fusion | flops 5 | bytes 1 | tf_op jit(solution)/shard_map/reduce.6
  10.7 0.2 slice_reduce_fusion
  10.9 0.2 compare_reduce_fusion.1
  11.2 0.7 %fusion.34 = (s32[2,1,1]{2,0,1:T(2,128)S(1)}, s32[2,1,1]{2,0,1:T(2,128)S(1)}, s32[2,1,1]{2,0,1:T(2,128)S(1)}, s32[2,1,1]{2,0,1:T(2,128)S(1)}, s32[2,1,1]{2,0,1:T(2,128)S(1)}, /*index=5*/s32[2,1,1]{2,0,1:T(2,128)S(1)}) fusion(pred[]{:T(512)} %compare_reduce_fusion, s32[]{:T(128)S(6)} %axis_index.16, s32[2,3]{1,0:T(2,128)S(1)} %bitcast.183, ...), kind=kLoop, calls=%fused_computation.148 | loop fusion | flops 282 | bytes 69 | tf_op jit(solution)/shard_map/stack | solution.py:262
  12.1 0.1 copy.105
  12.3 0.1 copy.106
  12.6 0.1 copy.88
  12.8 0.1 copy.89
  13.6 0.6 gather_fusion
  14.4 1.7 %collective-permute-start.5 = (bf16[4,1,2,8,512]{4,3,2,0,1:T(8,128)(2,1)S(1)}, bf16[4,1,2,8,512]{4,3,2,0,1:T(8,128)(2,1)S(1)}, u32[]{:S(2)}, u32[]{:S(2)}) collective-permute-start(bf16[4,1,2,8,512]{4,3,2,0,1:T(8,128)(2,1)S(1)} %bitcast_select_fusion.1), channel_id=1, source_target_pairs={{0,3},{1,2},{2,1},{3,0},{4,7},{5,6},{6,5},{7,4},{8,11},{9,10},{10,... | collective-permute-start | bytes 196616 | tf_op jit(solution)/shard_map/ppermute | solution.py:201
  16.1 2.8 %collective-permute-start.4 = (bf16[4,1,2,8,512]{4,3,2,0,1:T(8,128)(2,1)S(1)}, bf16[4,1,2,8,512]{4,3,2,0,1:T(8,128)(2,1)S(1)}, u32[]{:S(2)}, u32[]{:S(2)}) collective-permute-start(bf16[4,1,2,8,512]{4,3,2,0,1:T(8,128)(2,1)S(1)} %bitcast_select_fusion.1), channel_id=1, source_target_pairs={{0,2},{1,3},{2,0},{3,1},{4,6},{5,7},{6,4},{7,5},{8,10},{9,11},{10,... | collective-permute-start | bytes 196616 | tf_op jit(solution)/shard_map/ppermute | solution.py:201
  18.9 0.3 maximum_bitcast_fusion
  19.2 2.9 %collective-permute-done.4 = bf16[4,1,2,8,512]{4,3,2,0,1:T(8,128)(2,1)S(1)} collective-permute-done((bf16[4,1,2,8,512]{4,3,2,0,1:T(8,128)(2,1)S(1)}, bf16[4,1,2,8,512]{4,3,2,0,1:T(8,128)(2,1)S(1)}, u32[]{:S(2)}, u32[]{:S(2)}) %collective-permute-start.4) | collective-permute-done | bytes 65568 | tf_op jit(solution)/shard_map/ppermute | solution.py:201
  22.2 0.6 %gather_fusion.1 = bf16[4,4,2,8,512]{4,3,2,1,0:T(8,128)(2,1)S(1)} fusion(bf16[4,4,2,8,512]{4,3,2,1,0:T(8,128)(2,1)S(1)} %maximum_bitcast_fusion.1, s32[1024]{0:T(1024)S(1)} %pad_clamp_fusion), kind=kCustom, calls=%fused_computation.1 | custom fusion | bytes 524304 | tf_op jit(solution)/shard_map/jit(_take)/gather | solution.py:203
  22.9 0.3 fusion.3
  23.3 0.2 rev.9
  23.6 1.0 %fusion.67 = bf16[1,32,8,512]{3,2,1,0:T(8,128)(2,1)S(1)} fusion(bf16[1,10,512]{2,1,0:T(8,128)(2,1)S(1)} %get-tuple-element.103, bf16[32,10,512]{2,1,0:T(8,128)(2,1)S(1)} %maximum_bitcast_fusion, f32[32,8]{1,0:T(8,128)S(1)} %copy.101, f32[32,8]{1,0:T(8,128)S(1)} %copy.100, f32[32,8]{1,0:T(8,128)S(1)} %copy.99, f32[32,8]{1,0:T(8,128)S(1)} %copy.98, ...), kind=kLoop, calls=%fused_computation.178 | loop fusion | flops 5898240 | bytes 1753088 | tf_op jit(solution)/shard_map/broadcast_in_dim | solution.py:257
  24.7 1.1 %add_convert_fusion = bf16[32,8,512]{2,1,0:T(8,128)(2,1)S(1)} fusion(bf16[32,10,512]{2,1,0:T(8,128)(2,1)S(1)} %maximum_bitcast_fusion, bf16[1,10,512]{2,1,0:T(8,128)(2,1)S(1)} %get-tuple-element.103, bf16[1,10,512]{2,1,0:T(8,128)(2,1)S(1)} %get-tuple-element.102, f32[32,8]{1,0:T(8,128)S(1)} %copy.101, f32[32,8]{1,0:T(8,128)S(1)} %copy.100, ...), kind=kLoop, calls=%fused_computation.27 | loop fusion | flops 5898240 | bytes 1753088 | tf_op jit(solution)/shard_map/convert_element_type | solution.py:69
  25.8 1.9 %collective-permute-start.10 = (bf16[6,8,512]{2,1,0:T(8,128)(2,1)S(1)}, bf16[6,8,512]{2,1,0:T(8,128)(2,1)S(1)}, u32[]{:S(2)}, u32[]{:S(2)}) collective-permute-start(bf16[6,8,512]{2,1,0:T(8,128)(2,1)S(1)} %get-tuple-element.92), channel_id=1, source_target_pairs={{0,4},{1,5},{2,6},{3,7},{4,0},{5,1},{6,2},{7,3},{8,12},{9,13},{10,... | collective-permute-start | bytes 147464 | tf_op jit(solution)/shard_map/ppermute | solution.py:224
  27.8 1.6 %collective-permute-start.12 = (bf16[6,8,512]{2,1,0:T(8,128)(2,1)S(1)}, bf16[6,8,512]{2,1,0:T(8,128)(2,1)S(1)}, u32[]{:S(2)}, u32[]{:S(2)}) collective-permute-start(bf16[6,8,512]{2,1,0:T(8,128)(2,1)S(1)} %get-tuple-element.92), channel_id=1, source_target_pairs={{0,12},{1,13},{2,14},{3,15},{4,8},{5,9},{6,10},{7,11},{8,4},{9,5},... | collective-permute-start | bytes 147464 | tf_op jit(solution)/shard_map/ppermute | solution.py:224
  29.4 1.0 %fusion.1.q_ref = bf16[256,512]{1,0:T(8,128)(2,1)} fusion(bf16[512,512]{1,0:T(8,128)(2,1)S(1)} %copy-done.3, bf16[32,8,512]{2,1,0:T(8,128)(2,1)S(1)} %add_convert_fusion), kind=kOutput, calls=%fused_computation.9 | convolution fusion | flops 134479872 | bytes 1048576 | tf_op jit(solution)/shard_map/dot_general | solution.py:76
  30.5 1.1 %collective-permute-start.8 = (bf16[1,32,3,512]{3,2,1,0:T(4,128)(2,1)S(1)}, bf16[1,32,3,512]{3,2,1,0:T(4,128)(2,1)S(1)}, u32[]{:S(2)}, u32[]{:S(2)}) collective-permute-start(bf16[1,32,3,512]{3,2,1,0:T(4,128)(2,1)S(1)} %get-tuple-element.79), channel_id=1, source_target_pairs={{0,1},{1,2},{2,3},{3,4},{4,5},{5,6},{6,7},{7,8},{8,9},{9,10},{10,1... | collective-permute-start | bytes 294920 | tf_op jit(solution)/shard_map/ppermute | solution.py:19
  31.6 0.3 collective-permute-start.9
  31.8 0.7 %collective-permute-done.12 = bf16[6,8,512]{2,1,0:T(8,128)(2,1)S(1)} collective-permute-done((bf16[6,8,512]{2,1,0:T(8,128)(2,1)S(1)}, bf16[6,8,512]{2,1,0:T(8,128)(2,1)S(1)}, u32[]{:S(2)}, u32[]{:S(2)}) %collective-permute-start.12) | collective-permute-done | bytes 49184 | tf_op jit(solution)/shard_map/ppermute | solution.py:224
  32.5 1.1 %collective-permute-start.14 = (bf16[4,6,8,512]{3,2,1,0:T(8,128)(2,1)S(1)}, bf16[4,6,8,512]{3,2,1,0:T(8,128)(2,1)S(1)}, u32[]{:S(2)}, u32[]{:S(2)}) collective-permute-start(bf16[4,6,8,512]{3,2,1,0:T(8,128)(2,1)S(1)} %get-tuple-element.88), channel_id=1, source_target_pairs={{0,2},{1,3},{2,0},{3,1},{4,6},{5,7},{6,4},{7,5},{8,10},{9,11},{10,... | collective-permute-start | bytes 589832 | tf_op jit(solution)/shard_map/ppermute | solution.py:224
  33.7 2.7 %collective-permute-start.13 = (bf16[4,6,8,512]{3,2,1,0:T(8,128)(2,1)S(1)}, bf16[4,6,8,512]{3,2,1,0:T(8,128)(2,1)S(1)}, u32[]{:S(2)}, u32[]{:S(2)}) collective-permute-start(bf16[4,6,8,512]{3,2,1,0:T(8,128)(2,1)S(1)} %get-tuple-element.88), channel_id=1, source_target_pairs={{0,1},{1,0},{2,3},{3,2},{4,5},{5,4},{6,7},{7,6},{8,9},{9,8},{10,11... | collective-permute-start | bytes 589832 | tf_op jit(solution)/shard_map/ppermute | solution.py:224
  36.4 1.6 %collective-permute-start.15 = (bf16[4,6,8,512]{3,2,1,0:T(8,128)(2,1)S(1)}, bf16[4,6,8,512]{3,2,1,0:T(8,128)(2,1)S(1)}, u32[]{:S(2)}, u32[]{:S(2)}) collective-permute-start(bf16[4,6,8,512]{3,2,1,0:T(8,128)(2,1)S(1)} %get-tuple-element.88), channel_id=1, source_target_pairs={{0,3},{1,2},{2,1},{3,0},{4,7},{5,6},{6,5},{7,4},{8,11},{9,10},{10,... | collective-permute-start | bytes 589832 | tf_op jit(solution)/shard_map/ppermute | solution.py:224
  38.0 0.5 collective-permute-done.9
  38.5 0.3 pad_maximum_fusion.1
  38.8 0.1 reshape_squeeze.3
  38.9 1.2 %convolution_convert_fusion.vc_ref = bf16[448,512]{1,0:T(8,128)(2,1)} fusion(bf16[448,512]{1,0:T(8,128)(2,1)S(1)} %reshape_squeeze.3, bf16[512,512]{1,0:T(8,128)(2,1)S(1)} %copy-done), kind=kOutput, calls=%fused_computation.2 | convolution fusion | flops 235110400 | bytes 1441792 | tf_op jit(solution)/shard_map/dot_general | solution.py:76
  40.1 1.2 %convolution_convert_fusion.1.kc_ref = bf16[448,512]{1,0:T(8,128)(2,1)} fusion(bf16[448,512]{1,0:T(8,128)(2,1)S(1)} %reshape_squeeze.3, bf16[512,512]{1,0:T(8,128)(2,1)S(1)} %copy-done.2), kind=kOutput, calls=%fused_computation.3 | convolution fusion | flops 235110400 | bytes 1441792 | tf_op jit(solution)/shard_map/dot_general | solution.py:76
  41.3 4.5 %collective-permute-done.15 = bf16[4,6,8,512]{3,2,1,0:T(8,128)(2,1)S(1)} collective-permute-done((bf16[4,6,8,512]{3,2,1,0:T(8,128)(2,1)S(1)}, bf16[4,6,8,512]{3,2,1,0:T(8,128)(2,1)S(1)}, u32[]{:S(2)}, u32[]{:S(2)}) %collective-permute-start.15) | collective-permute-done | bytes 196640 | tf_op jit(solution)/shard_map/ppermute | solution.py:224
  45.8 0.1 pad_maximum_fusion
  45.9 0.6 %fusion = bf16[2,3,3,8,512]{4,1,3,2,0:T(4,128)(2,1)S(1)} fusion(bf16[16,2,3,8,512]{4,3,2,1,0:T(8,128)(2,1)S(1)} %bitcast.167, pred[2,3,2]{1,2,0:T(4,128)(4,1)S(1)} %iota_compare_fusion.2, pred[2,3,16]{2,1,0:T(4,128)(4,1)S(1)} %iota_compare_fusion), kind=kOutput, calls=%fused_computation.6 | convolution fusion | flops 4792512 | bytes 933996 | tf_op jit(solution)/shard_map/...nf,nfrwc->...rwc/dot_general | solution.py:182
  46.6 0.1 slice.302
  46.9 0.2 rev.10
  47.3 0.9 %convolution_convert_fusion.3.vr_ref = bf16[192,512]{1,0:T(8,128)(2,1)} fusion(bf16[512,512]{1,0:T(8,128)(2,1)S(1)} %copy-done, bf16[84,512]{1,0:T(8,128)(2,1)S(1)} %reshape.652), kind=kOutput, calls=%fused_computation.7 | convolution fusion | flops 100761600 | bytes 806912 | tf_op jit(solution)/shard_map/dot_general | solution.py:76
  48.3 1.0 %convolution_convert_fusion.4.kr_ref = bf16[192,512]{1,0:T(8,128)(2,1)} fusion(bf16[512,512]{1,0:T(8,128)(2,1)S(1)} %copy-done.2, bf16[84,512]{1,0:T(8,128)(2,1)S(1)} %reshape.652), kind=kOutput, calls=%fused_computation.8 | convolution fusion | flops 100761600 | bytes 806912 | tf_op jit(solution)/shard_map/dot_general | solution.py:76
  49.2 7.0 %shard_map.82 = bf16[256,512]{1,0:T(8,128)(2,1)} custom-call(bf16[256,512]{1,0:T(8,128)(2,1)} %fusion.1.q_ref, bf16[448,512]{1,0:T(8,128)(2,1)} %convolution_convert_fusion.1.kc_ref, bf16[192,512]{1,0:T(8,128)(2,1)} %convolution_convert_fusion.4.kr_ref, bf16[448,512]{1,0:T(8,128)(2,1)} %convolution_convert_fusion.vc_ref, ...), custom_call_target="tpu_custom_call" | custom-call | tf_op jit(solution)/shard_map/pallas_call | solution.py:149
  (92 shorter events, 2.6 us)
Async XLA Ops:
  0.0 38.9 %copy-start = (bf16[512,512]{1,0:T(8,128)(2,1)S(1)}, bf16[512,512]{1,0:T(8,128)(2,1)}, u32[]{:S(2)}) copy-start(bf16[512,512]{1,0:T(8,128)(2,1)} %param.25) | copy-start | bytes 1572868
  0.0 1.9 %copy-start.1 = (bf16[1,32,8,512]{3,2,1,0:T(8,128)(2,1)S(1)}, bf16[1,32,8,512]{3,2,1,0:T(8,128)(2,1)}, u32[]{:S(2)}) copy-start(bf16[1,32,8,512]{3,2,1,0:T(8,128)(2,1)} %param.20) | copy-start | bytes 786436
  1.8 0.7 %copy-start.5 = (f32[512]{0:T(512)S(1)}, f32[512]{0:T(512)}, u32[]{:S(2)}) copy-start(f32[512]{0:T(512)} %param.21) | copy-start | bytes 6148
  2.7 10.9 %collective-permute-start.2 = (bf16[1,2,8,512]{3,2,1,0:T(8,128)(2,1)S(1)}, bf16[1,2,8,512]{3,2,1,0:T(8,128)(2,1)S(1)}, u32[]{:S(2)}, u32[]{:S(2)}) collective-permute-start(bf16[1,2,8,512]{3,2,1,0:T(8,128)(2,1)S(1)} %get-tuple-element.105), channel_id=1, source_target_pairs={{0,12},{1,13},{2,14},{3,15},{4,8},{5,9},{6,10},{7,11},{8,4},{9,5},... | collective-permute-start | bytes 49160 | tf_op jit(solution)/shard_map/ppermute | solution.py:201
  6.9 6.7 %collective-permute-start.1 = (bf16[1,2,8,512]{3,2,1,0:T(8,128)(2,1)S(1)}, bf16[1,2,8,512]{3,2,1,0:T(8,128)(2,1)S(1)}, u32[]{:S(2)}, u32[]{:S(2)}) collective-permute-start(bf16[1,2,8,512]{3,2,1,0:T(8,128)(2,1)S(1)} %get-tuple-element.105), channel_id=1, source_target_pairs={{0,8},{1,9},{2,10},{3,11},{4,12},{5,13},{6,14},{7,15},{8,0},{9,1},... | collective-permute-start | bytes 49160 | tf_op jit(solution)/shard_map/ppermute | solution.py:201
  6.9 6.7 %collective-permute-start = (bf16[1,2,8,512]{3,2,1,0:T(8,128)(2,1)S(1)}, bf16[1,2,8,512]{3,2,1,0:T(8,128)(2,1)S(1)}, u32[]{:S(2)}, u32[]{:S(2)}) collective-permute-start(bf16[1,2,8,512]{3,2,1,0:T(8,128)(2,1)S(1)} %get-tuple-element.105), channel_id=1, source_target_pairs={{0,4},{1,5},{2,6},{3,7},{4,0},{5,1},{6,2},{7,3},{8,12},{9,13},{10,... | collective-permute-start | bytes 49160 | tf_op jit(solution)/shard_map/ppermute | solution.py:201
  7.5 11.4 %collective-permute-start.6 = (bf16[1,32,1,512]{3,2,1,0:T(2,128)(2,1)S(1)}, bf16[1,32,1,512]{3,2,1,0:T(2,128)(2,1)S(1)}, u32[]{:S(2)}, u32[]{:S(2)}) collective-permute-start(bf16[1,32,1,512]{3,2,1,0:T(2,128)(2,1)S(1)} %get-tuple-element.83), channel_id=1, source_target_pairs={{0,1},{1,2},{2,3},{3,4},{4,5},{5,6},{6,7},{7,8},{8,9},{9,10},{10,1... | collective-permute-start | bytes 98312 | tf_op jit(solution)/shard_map/ppermute | solution.py:19
  10.0 8.9 %collective-permute-start.7 = (bf16[1,32,1,512]{3,2,1,0:T(2,128)(2,1)S(1)}, bf16[1,32,1,512]{3,2,1,0:T(2,128)(2,1)S(1)}, u32[]{:S(2)}, u32[]{:S(2)}) collective-permute-start(bf16[1,32,1,512]{3,2,1,0:T(2,128)(2,1)S(1)} %get-tuple-element.84), channel_id=1, source_target_pairs={{1,0},{2,1},{3,2},{4,3},{5,4},{6,5},{7,6},{8,7},{9,8},{10,9},{11,1... | collective-permute-start | bytes 98312 | tf_op jit(solution)/shard_map/ppermute | solution.py:20
  12.1 0.8 %copy-start.4 = (f32[1,9,32,8]{2,3,1,0:T(8,128)S(1)}, f32[1,9,32,8]{2,3,1,0:T(8,128)}, u32[]{:S(2)}) copy-start(f32[1,9,32,8]{2,3,1,0:T(8,128)} %param.22) | copy-start | bytes 27652
  14.4 4.8 %collective-permute-start.5 = (bf16[4,1,2,8,512]{4,3,2,0,1:T(8,128)(2,1)S(1)}, bf16[4,1,2,8,512]{4,3,2,0,1:T(8,128)(2,1)S(1)}, u32[]{:S(2)}, u32[]{:S(2)}) collective-permute-start(bf16[4,1,2,8,512]{4,3,2,0,1:T(8,128)(2,1)S(1)} %bitcast_select_fusion.1), channel_id=1, source_target_pairs={{0,3},{1,2},{2,1},{3,0},{4,7},{5,6},{6,5},{7,4},{8,11},{9,10},{10,... | collective-permute-start | bytes 196616 | tf_op jit(solution)/shard_map/ppermute | solution.py:201
  16.1 6.0 %collective-permute-start.4 = (bf16[4,1,2,8,512]{4,3,2,0,1:T(8,128)(2,1)S(1)}, bf16[4,1,2,8,512]{4,3,2,0,1:T(8,128)(2,1)S(1)}, u32[]{:S(2)}, u32[]{:S(2)}) collective-permute-start(bf16[4,1,2,8,512]{4,3,2,0,1:T(8,128)(2,1)S(1)} %bitcast_select_fusion.1), channel_id=1, source_target_pairs={{0,2},{1,3},{2,0},{3,1},{4,6},{5,7},{6,4},{7,5},{8,10},{9,11},{10,... | collective-permute-start | bytes 196616 | tf_op jit(solution)/shard_map/ppermute | solution.py:201
  18.9 3.3 %collective-permute-start.3 = (bf16[4,1,2,8,512]{4,3,2,0,1:T(8,128)(2,1)S(1)}, bf16[4,1,2,8,512]{4,3,2,0,1:T(8,128)(2,1)S(1)}, u32[]{:S(2)}, u32[]{:S(2)}) collective-permute-start(bf16[4,1,2,8,512]{4,3,2,0,1:T(8,128)(2,1)S(1)} %bitcast_select_fusion.1), channel_id=1, source_target_pairs={{0,1},{1,0},{2,3},{3,2},{4,5},{5,4},{6,7},{7,6},{8,9},{9,8},{10,11... | collective-permute-start | bytes 196616 | tf_op jit(solution)/shard_map/ppermute | solution.py:201
  24.6 4.7 %copy-start.3 = (bf16[512,512]{1,0:T(8,128)(2,1)S(1)}, bf16[512,512]{1,0:T(8,128)(2,1)}, u32[]{:S(2)}) copy-start(bf16[512,512]{1,0:T(8,128)(2,1)} %param.23) | copy-start | bytes 1572868
  25.8 6.1 %collective-permute-start.11 = (bf16[6,8,512]{2,1,0:T(8,128)(2,1)S(1)}, bf16[6,8,512]{2,1,0:T(8,128)(2,1)S(1)}, u32[]{:S(2)}, u32[]{:S(2)}) collective-permute-start(bf16[6,8,512]{2,1,0:T(8,128)(2,1)S(1)} %get-tuple-element.92), channel_id=1, source_target_pairs={{0,8},{1,9},{2,10},{3,11},{4,12},{5,13},{6,14},{7,15},{8,0},{9,1},... | collective-permute-start | bytes 147464 | tf_op jit(solution)/shard_map/ppermute | solution.py:224
  25.8 6.0 %collective-permute-start.10 = (bf16[6,8,512]{2,1,0:T(8,128)(2,1)S(1)}, bf16[6,8,512]{2,1,0:T(8,128)(2,1)S(1)}, u32[]{:S(2)}, u32[]{:S(2)}) collective-permute-start(bf16[6,8,512]{2,1,0:T(8,128)(2,1)S(1)} %get-tuple-element.92), channel_id=1, source_target_pairs={{0,4},{1,5},{2,6},{3,7},{4,0},{5,1},{6,2},{7,3},{8,12},{9,13},{10,... | collective-permute-start | bytes 147464 | tf_op jit(solution)/shard_map/ppermute | solution.py:224
  27.8 4.7 %collective-permute-start.12 = (bf16[6,8,512]{2,1,0:T(8,128)(2,1)S(1)}, bf16[6,8,512]{2,1,0:T(8,128)(2,1)S(1)}, u32[]{:S(2)}, u32[]{:S(2)}) collective-permute-start(bf16[6,8,512]{2,1,0:T(8,128)(2,1)S(1)} %get-tuple-element.92), channel_id=1, source_target_pairs={{0,12},{1,13},{2,14},{3,15},{4,8},{5,9},{6,10},{7,11},{8,4},{9,5},... | collective-permute-start | bytes 147464 | tf_op jit(solution)/shard_map/ppermute | solution.py:224
  30.5 7.5 %collective-permute-start.8 = (bf16[1,32,3,512]{3,2,1,0:T(4,128)(2,1)S(1)}, bf16[1,32,3,512]{3,2,1,0:T(4,128)(2,1)S(1)}, u32[]{:S(2)}, u32[]{:S(2)}) collective-permute-start(bf16[1,32,3,512]{3,2,1,0:T(4,128)(2,1)S(1)} %get-tuple-element.79), channel_id=1, source_target_pairs={{0,1},{1,2},{2,3},{3,4},{4,5},{5,6},{6,7},{7,8},{8,9},{9,10},{10,1... | collective-permute-start | bytes 294920 | tf_op jit(solution)/shard_map/ppermute | solution.py:19
  31.6 6.9 %collective-permute-start.9 = (bf16[1,32,3,512]{3,2,1,0:T(4,128)(2,1)S(1)}, bf16[1,32,3,512]{3,2,1,0:T(4,128)(2,1)S(1)}, u32[]{:S(2)}, u32[]{:S(2)}) collective-permute-start(bf16[1,32,3,512]{3,2,1,0:T(4,128)(2,1)S(1)} %get-tuple-element.80), channel_id=1, source_target_pairs={{1,0},{2,1},{3,2},{4,3},{5,4},{6,5},{7,6},{8,7},{9,8},{10,9},{11,1... | collective-permute-start | bytes 294920 | tf_op jit(solution)/shard_map/ppermute | solution.py:20
  32.5 8.8 %collective-permute-start.14 = (bf16[4,6,8,512]{3,2,1,0:T(8,128)(2,1)S(1)}, bf16[4,6,8,512]{3,2,1,0:T(8,128)(2,1)S(1)}, u32[]{:S(2)}, u32[]{:S(2)}) collective-permute-start(bf16[4,6,8,512]{3,2,1,0:T(8,128)(2,1)S(1)} %get-tuple-element.88), channel_id=1, source_target_pairs={{0,2},{1,3},{2,0},{3,1},{4,6},{5,7},{6,4},{7,5},{8,10},{9,11},{10,... | collective-permute-start | bytes 589832 | tf_op jit(solution)/shard_map/ppermute | solution.py:224
  33.7 7.6 %collective-permute-start.13 = (bf16[4,6,8,512]{3,2,1,0:T(8,128)(2,1)S(1)}, bf16[4,6,8,512]{3,2,1,0:T(8,128)(2,1)S(1)}, u32[]{:S(2)}, u32[]{:S(2)}) collective-permute-start(bf16[4,6,8,512]{3,2,1,0:T(8,128)(2,1)S(1)} %get-tuple-element.88), channel_id=1, source_target_pairs={{0,1},{1,0},{2,3},{3,2},{4,5},{5,4},{6,7},{7,6},{8,9},{9,8},{10,11... | collective-permute-start | bytes 589832 | tf_op jit(solution)/shard_map/ppermute | solution.py:224
  36.4 9.4 %collective-permute-start.15 = (bf16[4,6,8,512]{3,2,1,0:T(8,128)(2,1)S(1)}, bf16[4,6,8,512]{3,2,1,0:T(8,128)(2,1)S(1)}, u32[]{:S(2)}, u32[]{:S(2)}) collective-permute-start(bf16[4,6,8,512]{3,2,1,0:T(8,128)(2,1)S(1)} %get-tuple-element.88), channel_id=1, source_target_pairs={{0,3},{1,2},{2,1},{3,0},{4,7},{5,6},{6,5},{7,4},{8,11},{9,10},{10,... | collective-permute-start | bytes 589832 | tf_op jit(solution)/shard_map/ppermute | solution.py:224
  38.9 1.2 %copy-start.2 = (bf16[512,512]{1,0:T(8,128)(2,1)S(1)}, bf16[512,512]{1,0:T(8,128)(2,1)}, u32[]{:S(2)}) copy-start(bf16[512,512]{1,0:T(8,128)(2,1)} %param.24) | copy-start | bytes 1572868

commit v26 on v25

--- a/solution.py
+++ b/solution.py
@@ -242,10 +242,11 @@
     seam_rows = seam_table[0]
     widened = padded_2(normed[None], (("blk", 2),), margin)
     rows1 = jnp.stack([normed[0], normed[-1]])
-    got1 = doubling_gather(rows1[None], "blk")
+    got1, locate1 = raw_gather(rows1, "blk")
     count = got1.shape[0]
     near1 = jnp.stack(
-        [seam_rows.at[:, 0].set((seam_rows[:, 0] + count + k) % count) for k in (-1, 0, 1)], axis=1
+        [seam_rows.at[:, 0].set(locate1((seam_rows[:, 0] + count + k) % count)) for k in (-1, 0, 1)],
+        axis=1,
     )
     picked1 = pick_all(near1, got1[:, :, None])
     received = jnp.concatenate(

time: 56.5 us -> 55.1 us (0.975)
  the two profiles are of different devices: /device:TPU:1 before, /device:TPU:0 now
where the time goes in v26:
time: 55.1 us; the launch traced here: 54.3 us
  starting transfers between devices  23.5 us (43%)
  waiting for transfers between devices  7.14 us (13%)
  Pallas kernels  7.06 us (13%)
  matrix products  6.28 us (11%)
  other arithmetic  6.19 us (11%)
  local copies, waits for them, and re-layouts  3.76 us (7%)
    ppermute x12, starting transfers between devices, raw_gather(): lax.ppermute(held, axis, [(i, i ^ d * stride) for i in range(count)])  14.5 us
    ppermute x2, starting transfers between devices, padded_2(): after = lax.ppermute(first, axis, down)  8.86 us
    pallas_call x1, Pallas kernels, attend_and_mix(): pl.pallas_call(attention_kernel, out_shape=jax.ShapeDtypeStruct((cells, c...  7.06 us
    ppermute x12, waiting for transfers between devices, raw_gather(): lax.ppermute(held, axis, [(i, i ^ d * stride) for i in range(count)])  6.65 us
    dot_general x5, matrix products, project(): jnp.dot(flat, weight, preferred_element_type=jnp.float32)  5.3 us
    unnamed x17, local copies, waits for them, and re-layouts  1.45 us
  transfers between devices with their start and end apart: 16, of which 4 were waited for; matrix products, arithmetic and copies ran while one was open for 14% of the time, Pallas kernels for 0%

profile of v26, /device:TPU:0, one launch (start us, length us, event | category | flops | bytes accessed | tf_op | source)
XLA Modules:
  0.0 54.3 jit_solution(5864029897605997296)
XLA Ops:
  0.0 0.8 %copy.120 = s32[1,2,3]{2,1,0:T(2,128)S(1)} copy(s32[1,2,3]{2,1,0:T(2,128)} %param.27) | data formatting | bytes 48
  0.8 1.1 %fusion.6 = f32[32,8]{1,0:T(8,128)S(1)} fusion(bf16[1,32,8,512]{3,2,1,0:T(8,128)(2,1)} %param.20), kind=kLoop, calls=%fused_computation.20 | loop fusion | flops 392960 | bytes 263168 | tf_op jit(solution)/shard_map/reduce_sum | solution.py:27
  1.9 0.6 %copy-done.5 = f32[512]{0:T(512)S(1)} copy-done((f32[512]{0:T(512)S(1)}, f32[512]{0:T(512)}, u32[]{:S(2)}) %copy-start.5) | copy-done | bytes 2072
  2.5 0.1 fusion.8
  2.7 4.1 %collective-permute-start.1 = (bf16[2,8,512]{2,1,0:T(8,128)(2,1)S(1)}, bf16[2,8,512]{2,1,0:T(8,128)(2,1)S(1)}, u32[]{:S(2)}, u32[]{:S(2)}) collective-permute-start(bf16[2,8,512]{2,1,0:T(8,128)(2,1)S(1)} %get-tuple-element.95), channel_id=1, source_target_pairs={{0,8},{1,9},{2,10},{3,11},{4,12},{5,13},{6,14},{7,15},{8,0},{9,1},... | collective-permute-start | bytes 49160 | tf_op jit(solution)/shard_map/ppermute | solution.py:224
  6.8 1.6 %collective-permute-start = (bf16[2,8,512]{2,1,0:T(8,128)(2,1)S(1)}, bf16[2,8,512]{2,1,0:T(8,128)(2,1)S(1)}, u32[]{:S(2)}, u32[]{:S(2)}) collective-permute-start(bf16[2,8,512]{2,1,0:T(8,128)(2,1)S(1)} %get-tuple-element.95), channel_id=1, source_target_pairs={{0,4},{1,5},{2,6},{3,7},{4,0},{5,1},{6,2},{7,3},{8,12},{9,13},{10,... | collective-permute-start | bytes 49160 | tf_op jit(solution)/shard_map/ppermute | solution.py:224
  8.4 0.1 multiply_convert_fusion
  8.5 0.1 fusion.52
  8.7 4.4 %collective-permute-start.7 = (bf16[1,32,1,512]{3,2,1,0:T(2,128)(2,1)S(1)}, bf16[1,32,1,512]{3,2,1,0:T(2,128)(2,1)S(1)}, u32[]{:S(2)}, u32[]{:S(2)}) collective-permute-start(bf16[1,32,1,512]{3,2,1,0:T(2,128)(2,1)S(1)} %get-tuple-element.72), channel_id=1, source_target_pairs={{1,0},{2,1},{3,2},{4,3},{5,4},{6,5},{7,6},{8,7},{9,8},{10,9},{11,1... | collective-permute-start | bytes 98312 | tf_op jit(solution)/shard_map/ppermute | solution.py:20
  13.1 0.6 %compare_reduce_fusion = pred[]{:T(512)} fusion(), kind=kLoop, calls=%fused_computation.107 | loop fusion | flops 5 | bytes 1 | tf_op jit(solution)/shard_map/reduce.6
  13.7 0.2 slice_reduce_fusion
  13.9 0.2 compare_reduce_fusion.1
  14.1 0.7 %fusion.27 = (s32[2,1,1]{2,0,1:T(2,128)S(1)}, s32[2,1,1]{2,0,1:T(2,128)S(1)}, s32[2,1,1]{2,0,1:T(2,128)S(1)}) fusion(pred[]{:T(512)} %compare_reduce_fusion, s32[1,2,3]{2,1,0:T(2,128)S(1)} %copy.120, s32[2,3]{1,0:T(2,128)S(1)} %bitcast.154, s32[]{:T(128)S(6)} %axis_index.16), kind=kLoop, calls=%fused_computation.127 | loop fusion | flops 276 | bytes 45 | tf_op jit(solution)/shard_map/stack | solution.py:247
  15.0 0.1 copy.78
  15.1 0.1 iota_compare_fusion
  15.2 0.1 copy.79
  15.4 0.1 copy.65
  16.2 2.0 %collective-permute-start.5 = (bf16[4,2,8,512]{3,2,1,0:T(8,128)(2,1)S(1)}, bf16[4,2,8,512]{3,2,1,0:T(8,128)(2,1)S(1)}, u32[]{:S(2)}, u32[]{:S(2)}) collective-permute-start(bf16[4,2,8,512]{3,2,1,0:T(8,128)(2,1)S(1)} %get-tuple-element.80), channel_id=1, source_target_pairs={{0,3},{1,2},{2,1},{3,0},{4,7},{5,6},{6,5},{7,4},{8,11},{9,10},{10,... | collective-permute-start | bytes 196616 | tf_op jit(solution)/shard_map/ppermute | solution.py:224
  18.3 0.3 maximum_bitcast_fusion
  18.6 2.3 %collective-permute-done.4 = bf16[4,2,8,512]{3,2,1,0:T(8,128)(2,1)S(1)} collective-permute-done((bf16[4,2,8,512]{3,2,1,0:T(8,128)(2,1)S(1)}, bf16[4,2,8,512]{3,2,1,0:T(8,128)(2,1)S(1)}, u32[]{:S(2)}, u32[]{:S(2)}) %collective-permute-start.4) | collective-permute-done | bytes 65568 | tf_op jit(solution)/shard_map/ppermute | solution.py:224
  21.0 0.3 fusion.3
  21.4 0.2 rev.9
  21.6 0.1 broadcast_select_fusion.1
  21.7 1.1 %fusion.62 = bf16[1,32,8,512]{3,2,1,0:T(8,128)(2,1)S(1)} fusion(bf16[1,10,512]{2,1,0:T(8,128)(2,1)S(1)} %get-tuple-element.93, bf16[32,10,512]{2,1,0:T(8,128)(2,1)S(1)} %maximum_bitcast_fusion, f32[32,8]{1,0:T(8,128)S(1)} %copy.90, f32[32,8]{1,0:T(8,128)S(1)} %copy.89, f32[32,8]{1,0:T(8,128)S(1)} %copy.88, f32[32,8]{1,0:T(8,128)S(1)} %copy.87, ...), kind=kLoop, calls=%fused_computation.156 | loop fusion | flops 5898240 | bytes 1753088 | tf_op jit(solution)/shard_map/broadcast_in_dim | solution.py:258
  22.8 1.1 %add_convert_fusion = bf16[32,8,512]{2,1,0:T(8,128)(2,1)S(1)} fusion(bf16[32,10,512]{2,1,0:T(8,128)(2,1)S(1)} %maximum_bitcast_fusion, bf16[1,10,512]{2,1,0:T(8,128)(2,1)S(1)} %get-tuple-element.93, bf16[1,10,512]{2,1,0:T(8,128)(2,1)S(1)} %get-tuple-element.92, f32[32,8]{1,0:T(8,128)S(1)} %copy.90, f32[32,8]{1,0:T(8,128)S(1)} %copy.89, ...), kind=kLoop, calls=%fused_computation.25 | loop fusion | flops 5898240 | bytes 1753088 | tf_op jit(solution)/shard_map/convert_element_type | solution.py:69
  23.9 0.8 %collective-permute-start.11 = (bf16[6,8,512]{2,1,0:T(8,128)(2,1)S(1)}, bf16[6,8,512]{2,1,0:T(8,128)(2,1)S(1)}, u32[]{:S(2)}, u32[]{:S(2)}) collective-permute-start(bf16[6,8,512]{2,1,0:T(8,128)(2,1)S(1)} %get-tuple-element.82), channel_id=1, source_target_pairs={{0,8},{1,9},{2,10},{3,11},{4,12},{5,13},{6,14},{7,15},{8,0},{9,1},... | collective-permute-start | bytes 147464 | tf_op jit(solution)/shard_map/ppermute | solution.py:224
  24.7 2.0 %collective-permute-start.10 = (bf16[6,8,512]{2,1,0:T(8,128)(2,1)S(1)}, bf16[6,8,512]{2,1,0:T(8,128)(2,1)S(1)}, u32[]{:S(2)}, u32[]{:S(2)}) collective-permute-start(bf16[6,8,512]{2,1,0:T(8,128)(2,1)S(1)} %get-tuple-element.82), channel_id=1, source_target_pairs={{0,4},{1,5},{2,6},{3,7},{4,0},{5,1},{6,2},{7,3},{8,12},{9,13},{10,... | collective-permute-start | bytes 147464 | tf_op jit(solution)/shard_map/ppermute | solution.py:224
  26.7 1.6 %collective-permute-start.12 = (bf16[6,8,512]{2,1,0:T(8,128)(2,1)S(1)}, bf16[6,8,512]{2,1,0:T(8,128)(2,1)S(1)}, u32[]{:S(2)}, u32[]{:S(2)}) collective-permute-start(bf16[6,8,512]{2,1,0:T(8,128)(2,1)S(1)} %get-tuple-element.82), channel_id=1, source_target_pairs={{0,12},{1,13},{2,14},{3,15},{4,8},{5,9},{6,10},{7,11},{8,4},{9,5},... | collective-permute-start | bytes 147464 | tf_op jit(solution)/shard_map/ppermute | solution.py:224
  28.3 1.0 %fusion.1.q_ref = bf16[256,512]{1,0:T(8,128)(2,1)} fusion(bf16[512,512]{1,0:T(8,128)(2,1)S(1)} %copy-done.3, bf16[32,8,512]{2,1,0:T(8,128)(2,1)S(1)} %add_convert_fusion), kind=kOutput, calls=%fused_computation.7 | convolution fusion | flops 134479872 | bytes 1048576 | tf_op jit(solution)/shard_map/dot_general | solution.py:76
  29.3 0.1 fusion.50
  29.5 4.4 %collective-permute-start.9 = (bf16[1,32,3,512]{3,2,1,0:T(4,128)(2,1)S(1)}, bf16[1,32,3,512]{3,2,1,0:T(4,128)(2,1)S(1)}, u32[]{:S(2)}, u32[]{:S(2)}) collective-permute-start(bf16[1,32,3,512]{3,2,1,0:T(4,128)(2,1)S(1)} %get-tuple-element.68), channel_id=1, source_target_pairs={{1,0},{2,1},{3,2},{4,3},{5,4},{6,5},{7,6},{8,7},{9,8},{10,9},{11,1... | collective-permute-start | bytes 294920 | tf_op jit(solution)/shard_map/ppermute | solution.py:20
  34.1 2.0 %collective-permute-start.15 = (bf16[4,6,8,512]{3,2,1,0:T(8,128)(2,1)S(1)}, bf16[4,6,8,512]{3,2,1,0:T(8,128)(2,1)S(1)}, u32[]{:S(2)}, u32[]{:S(2)}) collective-permute-start(bf16[4,6,8,512]{3,2,1,0:T(8,128)(2,1)S(1)} %get-tuple-element.76), channel_id=1, source_target_pairs={{0,3},{1,2},{2,1},{3,0},{4,7},{5,6},{6,5},{7,4},{8,11},{9,10},{10,... | collective-permute-start | bytes 589832 | tf_op jit(solution)/shard_map/ppermute | solution.py:224
  36.2 0.5 collective-permute-done.8
  36.7 0.3 pad_maximum_fusion.1
  37.0 0.1 reshape_squeeze.3
  37.1 1.2 %convolution_convert_fusion.vc_ref = bf16[448,512]{1,0:T(8,128)(2,1)} fusion(bf16[448,512]{1,0:T(8,128)(2,1)S(1)} %reshape_squeeze.3, bf16[512,512]{1,0:T(8,128)(2,1)S(1)} %copy-done), kind=kOutput, calls=%fused_computation | convolution fusion | flops 235110400 | bytes 1441792 | tf_op jit(solution)/shard_map/dot_general | solution.py:76
  38.3 1.2 %convolution_convert_fusion.1.kc_ref = bf16[448,512]{1,0:T(8,128)(2,1)} fusion(bf16[448,512]{1,0:T(8,128)(2,1)S(1)} %reshape_squeeze.3, bf16[512,512]{1,0:T(8,128)(2,1)S(1)} %copy-done.2), kind=kOutput, calls=%fused_computation.1 | convolution fusion | flops 235110400 | bytes 1441792 | tf_op jit(solution)/shard_map/dot_general | solution.py:76
  39.5 2.4 %collective-permute-done.14 = bf16[4,6,8,512]{3,2,1,0:T(8,128)(2,1)S(1)} collective-permute-done((bf16[4,6,8,512]{3,2,1,0:T(8,128)(2,1)S(1)}, bf16[4,6,8,512]{3,2,1,0:T(8,128)(2,1)S(1)}, u32[]{:S(2)}, u32[]{:S(2)}) %collective-permute-start.14) | collective-permute-done | bytes 196640 | tf_op jit(solution)/shard_map/ppermute | solution.py:224
  41.9 1.9 %collective-permute-done.15 = bf16[4,6,8,512]{3,2,1,0:T(8,128)(2,1)S(1)} collective-permute-done((bf16[4,6,8,512]{3,2,1,0:T(8,128)(2,1)S(1)}, bf16[4,6,8,512]{3,2,1,0:T(8,128)(2,1)S(1)}, u32[]{:S(2)}, u32[]{:S(2)}) %collective-permute-start.15) | collective-permute-done | bytes 196640 | tf_op jit(solution)/shard_map/ppermute | solution.py:224
  43.8 0.1 pad_maximum_fusion
  43.9 0.6 %fusion = bf16[2,3,3,8,512]{4,1,3,2,0:T(4,128)(2,1)S(1)} fusion(bf16[16,2,3,8,512]{4,3,2,1,0:T(8,128)(2,1)S(1)} %bitcast.135, pred[2,3,2]{1,2,0:T(4,128)(4,1)S(1)} %iota_compare_fusion.1, pred[2,3,16]{2,1,0:T(4,128)(4,1)S(1)} %iota_compare_fusion), kind=kOutput, calls=%fused_computation.4 | convolution fusion | flops 4792512 | bytes 933996 | tf_op jit(solution)/shard_map/...nf,nfrwc->...rwc/dot_general | solution.py:182
  44.6 0.1 slice.272
  44.9 0.2 rev.10
  45.2 0.1 broadcast_select_fusion
  45.3 0.1 reverse_select_fusion
  45.4 0.9 %convolution_convert_fusion.3.vr_ref = bf16[192,512]{1,0:T(8,128)(2,1)} fusion(bf16[512,512]{1,0:T(8,128)(2,1)S(1)} %copy-done, bf16[84,512]{1,0:T(8,128)(2,1)S(1)} %reshape.500), kind=kOutput, calls=%fused_computation.5 | convolution fusion | flops 100761600 | bytes 806912 | tf_op jit(solution)/shard_map/dot_general | solution.py:76
  46.3 1.0 %convolution_convert_fusion.4.kr_ref = bf16[192,512]{1,0:T(8,128)(2,1)} fusion(bf16[512,512]{1,0:T(8,128)(2,1)S(1)} %copy-done.2, bf16[84,512]{1,0:T(8,128)(2,1)S(1)} %reshape.500), kind=kOutput, calls=%fused_computation.6 | convolution fusion | flops 100761600 | bytes 806912 | tf_op jit(solution)/shard_map/dot_general | solution.py:76
  47.3 7.1 %shard_map.82 = bf16[256,512]{1,0:T(8,128)(2,1)} custom-call(bf16[256,512]{1,0:T(8,128)(2,1)} %fusion.1.q_ref, bf16[448,512]{1,0:T(8,128)(2,1)} %convolution_convert_fusion.1.kc_ref, bf16[192,512]{1,0:T(8,128)(2,1)} %convolution_convert_fusion.4.kr_ref, bf16[448,512]{1,0:T(8,128)(2,1)} %convolution_convert_fusion.vc_ref, ...), custom_call_target="tpu_custom_call" | custom-call | tf_op jit(solution)/shard_map/pallas_call | solution.py:149
  (68 shorter events, 1.7 us)
Async XLA Ops:
  0.0 37.1 %copy-start = (bf16[512,512]{1,0:T(8,128)(2,1)S(1)}, bf16[512,512]{1,0:T(8,128)(2,1)}, u32[]{:S(2)}) copy-start(bf16[512,512]{1,0:T(8,128)(2,1)} %param.25) | copy-start | bytes 1572868
  0.0 1.9 %copy-start.1 = (bf16[1,32,8,512]{3,2,1,0:T(8,128)(2,1)S(1)}, bf16[1,32,8,512]{3,2,1,0:T(8,128)(2,1)}, u32[]{:S(2)}) copy-start(bf16[1,32,8,512]{3,2,1,0:T(8,128)(2,1)} %param.20) | copy-start | bytes 786436
  1.8 0.7 %copy-start.5 = (f32[512]{0:T(512)S(1)}, f32[512]{0:T(512)}, u32[]{:S(2)}) copy-start(f32[512]{0:T(512)} %param.21) | copy-start | bytes 6148
  2.7 13.4 %collective-permute-start.1 = (bf16[2,8,512]{2,1,0:T(8,128)(2,1)S(1)}, bf16[2,8,512]{2,1,0:T(8,128)(2,1)S(1)}, u32[]{:S(2)}, u32[]{:S(2)}) collective-permute-start(bf16[2,8,512]{2,1,0:T(8,128)(2,1)S(1)} %get-tuple-element.95), channel_id=1, source_target_pairs={{0,8},{1,9},{2,10},{3,11},{4,12},{5,13},{6,14},{7,15},{8,0},{9,1},... | collective-permute-start | bytes 49160 | tf_op jit(solution)/shard_map/ppermute | solution.py:224
  6.8 9.3 %collective-permute-start = (bf16[2,8,512]{2,1,0:T(8,128)(2,1)S(1)}, bf16[2,8,512]{2,1,0:T(8,128)(2,1)S(1)}, u32[]{:S(2)}, u32[]{:S(2)}) collective-permute-start(bf16[2,8,512]{2,1,0:T(8,128)(2,1)S(1)} %get-tuple-element.95), channel_id=1, source_target_pairs={{0,4},{1,5},{2,6},{3,7},{4,0},{5,1},{6,2},{7,3},{8,12},{9,13},{10,... | collective-permute-start | bytes 49160 | tf_op jit(solution)/shard_map/ppermute | solution.py:224
  8.4 7.7 %collective-permute-start.2 = (bf16[2,8,512]{2,1,0:T(8,128)(2,1)S(1)}, bf16[2,8,512]{2,1,0:T(8,128)(2,1)S(1)}, u32[]{:S(2)}, u32[]{:S(2)}) collective-permute-start(bf16[2,8,512]{2,1,0:T(8,128)(2,1)S(1)} %get-tuple-element.95), channel_id=1, source_target_pairs={{0,12},{1,13},{2,14},{3,15},{4,8},{5,9},{6,10},{7,11},{8,4},{9,5},... | collective-permute-start | bytes 49160 | tf_op jit(solution)/shard_map/ppermute | solution.py:224
  8.6 9.7 %collective-permute-start.6 = (bf16[1,32,1,512]{3,2,1,0:T(2,128)(2,1)S(1)}, bf16[1,32,1,512]{3,2,1,0:T(2,128)(2,1)S(1)}, u32[]{:S(2)}, u32[]{:S(2)}) collective-permute-start(bf16[1,32,1,512]{3,2,1,0:T(2,128)(2,1)S(1)} %get-tuple-element.71), channel_id=1, source_target_pairs={{0,1},{1,2},{2,3},{3,4},{4,5},{5,6},{6,7},{7,8},{8,9},{9,10},{10,1... | collective-permute-start | bytes 98312 | tf_op jit(solution)/shard_map/ppermute | solution.py:19
  8.7 9.6 %collective-permute-start.7 = (bf16[1,32,1,512]{3,2,1,0:T(2,128)(2,1)S(1)}, bf16[1,32,1,512]{3,2,1,0:T(2,128)(2,1)S(1)}, u32[]{:S(2)}, u32[]{:S(2)}) collective-permute-start(bf16[1,32,1,512]{3,2,1,0:T(2,128)(2,1)S(1)} %get-tuple-element.72), channel_id=1, source_target_pairs={{1,0},{2,1},{3,2},{4,3},{5,4},{6,5},{7,6},{8,7},{9,8},{10,9},{11,1... | collective-permute-start | bytes 98312 | tf_op jit(solution)/shard_map/ppermute | solution.py:20
  13.9 1.4 %copy-start.4 = (f32[1,9,32,8]{2,3,1,0:T(8,128)S(1)}, f32[1,9,32,8]{2,3,1,0:T(8,128)}, u32[]{:S(2)}) copy-start(f32[1,9,32,8]{2,3,1,0:T(8,128)} %param.22) | copy-start | bytes 27652
  16.1 4.9 %collective-permute-start.4 = (bf16[4,2,8,512]{3,2,1,0:T(8,128)(2,1)S(1)}, bf16[4,2,8,512]{3,2,1,0:T(8,128)(2,1)S(1)}, u32[]{:S(2)}, u32[]{:S(2)}) collective-permute-start(bf16[4,2,8,512]{3,2,1,0:T(8,128)(2,1)S(1)} %get-tuple-element.80), channel_id=1, source_target_pairs={{0,2},{1,3},{2,0},{3,1},{4,6},{5,7},{6,4},{7,5},{8,10},{9,11},{10,... | collective-permute-start | bytes 196616 | tf_op jit(solution)/shard_map/ppermute | solution.py:224
  16.2 4.8 %collective-permute-start.3 = (bf16[4,2,8,512]{3,2,1,0:T(8,128)(2,1)S(1)}, bf16[4,2,8,512]{3,2,1,0:T(8,128)(2,1)S(1)}, u32[]{:S(2)}, u32[]{:S(2)}) collective-permute-start(bf16[4,2,8,512]{3,2,1,0:T(8,128)(2,1)S(1)} %get-tuple-element.80), channel_id=1, source_target_pairs={{0,1},{1,0},{2,3},{3,2},{4,5},{5,4},{6,7},{7,6},{8,9},{9,8},{10,11... | collective-permute-start | bytes 196616 | tf_op jit(solution)/shard_map/ppermute | solution.py:224
  16.2 4.7 %collective-permute-start.5 = (bf16[4,2,8,512]{3,2,1,0:T(8,128)(2,1)S(1)}, bf16[4,2,8,512]{3,2,1,0:T(8,128)(2,1)S(1)}, u32[]{:S(2)}, u32[]{:S(2)}) collective-permute-start(bf16[4,2,8,512]{3,2,1,0:T(8,128)(2,1)S(1)} %get-tuple-element.80), channel_id=1, source_target_pairs={{0,3},{1,2},{2,1},{3,0},{4,7},{5,6},{6,5},{7,4},{8,11},{9,10},{10,... | collective-permute-start | bytes 196616 | tf_op jit(solution)/shard_map/ppermute | solution.py:224
  22.8 5.6 %copy-start.3 = (bf16[512,512]{1,0:T(8,128)(2,1)S(1)}, bf16[512,512]{1,0:T(8,128)(2,1)}, u32[]{:S(2)}) copy-start(bf16[512,512]{1,0:T(8,128)(2,1)} %param.23) | copy-start | bytes 1572868
  23.9 10.1 %collective-permute-start.11 = (bf16[6,8,512]{2,1,0:T(8,128)(2,1)S(1)}, bf16[6,8,512]{2,1,0:T(8,128)(2,1)S(1)}, u32[]{:S(2)}, u32[]{:S(2)}) collective-permute-start(bf16[6,8,512]{2,1,0:T(8,128)(2,1)S(1)} %get-tuple-element.82), channel_id=1, source_target_pairs={{0,8},{1,9},{2,10},{3,11},{4,12},{5,13},{6,14},{7,15},{8,0},{9,1},... | collective-permute-start | bytes 147464 | tf_op jit(solution)/shard_map/ppermute | solution.py:224
  24.7 9.2 %collective-permute-start.10 = (bf16[6,8,512]{2,1,0:T(8,128)(2,1)S(1)}, bf16[6,8,512]{2,1,0:T(8,128)(2,1)S(1)}, u32[]{:S(2)}, u32[]{:S(2)}) collective-permute-start(bf16[6,8,512]{2,1,0:T(8,128)(2,1)S(1)} %get-tuple-element.82), channel_id=1, source_target_pairs={{0,4},{1,5},{2,6},{3,7},{4,0},{5,1},{6,2},{7,3},{8,12},{9,13},{10,... | collective-permute-start | bytes 147464 | tf_op jit(solution)/shard_map/ppermute | solution.py:224
  26.7 7.2 %collective-permute-start.12 = (bf16[6,8,512]{2,1,0:T(8,128)(2,1)S(1)}, bf16[6,8,512]{2,1,0:T(8,128)(2,1)S(1)}, u32[]{:S(2)}, u32[]{:S(2)}) collective-permute-start(bf16[6,8,512]{2,1,0:T(8,128)(2,1)S(1)} %get-tuple-element.82), channel_id=1, source_target_pairs={{0,12},{1,13},{2,14},{3,15},{4,8},{5,9},{6,10},{7,11},{8,4},{9,5},... | collective-permute-start | bytes 147464 | tf_op jit(solution)/shard_map/ppermute | solution.py:224
  29.4 7.3 %collective-permute-start.8 = (bf16[1,32,3,512]{3,2,1,0:T(4,128)(2,1)S(1)}, bf16[1,32,3,512]{3,2,1,0:T(4,128)(2,1)S(1)}, u32[]{:S(2)}, u32[]{:S(2)}) collective-permute-start(bf16[1,32,3,512]{3,2,1,0:T(4,128)(2,1)S(1)} %get-tuple-element.67), channel_id=1, source_target_pairs={{0,1},{1,2},{2,3},{3,4},{4,5},{5,6},{6,7},{7,8},{8,9},{9,10},{10,1... | collective-permute-start | bytes 294920 | tf_op jit(solution)/shard_map/ppermute | solution.py:19
  29.5 7.2 %collective-permute-start.9 = (bf16[1,32,3,512]{3,2,1,0:T(4,128)(2,1)S(1)}, bf16[1,32,3,512]{3,2,1,0:T(4,128)(2,1)S(1)}, u32[]{:S(2)}, u32[]{:S(2)}) collective-permute-start(bf16[1,32,3,512]{3,2,1,0:T(4,128)(2,1)S(1)} %get-tuple-element.68), channel_id=1, source_target_pairs={{1,0},{2,1},{3,2},{4,3},{5,4},{6,5},{7,6},{8,7},{9,8},{10,9},{11,1... | collective-permute-start | bytes 294920 | tf_op jit(solution)/shard_map/ppermute | solution.py:20
  34.0 7.9 %collective-permute-start.14 = (bf16[4,6,8,512]{3,2,1,0:T(8,128)(2,1)S(1)}, bf16[4,6,8,512]{3,2,1,0:T(8,128)(2,1)S(1)}, u32[]{:S(2)}, u32[]{:S(2)}) collective-permute-start(bf16[4,6,8,512]{3,2,1,0:T(8,128)(2,1)S(1)} %get-tuple-element.76), channel_id=1, source_target_pairs={{0,2},{1,3},{2,0},{3,1},{4,6},{5,7},{6,4},{7,5},{8,10},{9,11},{10,... | collective-permute-start | bytes 589832 | tf_op jit(solution)/shard_map/ppermute | solution.py:224
  34.1 7.9 %collective-permute-start.13 = (bf16[4,6,8,512]{3,2,1,0:T(8,128)(2,1)S(1)}, bf16[4,6,8,512]{3,2,1,0:T(8,128)(2,1)S(1)}, u32[]{:S(2)}, u32[]{:S(2)}) collective-permute-start(bf16[4,6,8,512]{3,2,1,0:T(8,128)(2,1)S(1)} %get-tuple-element.76), channel_id=1, source_target_pairs={{0,1},{1,0},{2,3},{3,2},{4,5},{5,4},{6,7},{7,6},{8,9},{9,8},{10,11... | collective-permute-start | bytes 589832 | tf_op jit(solution)/shard_map/ppermute | solution.py:224
  34.1 9.7 %collective-permute-start.15 = (bf16[4,6,8,512]{3,2,1,0:T(8,128)(2,1)S(1)}, bf16[4,6,8,512]{3,2,1,0:T(8,128)(2,1)S(1)}, u32[]{:S(2)}, u32[]{:S(2)}) collective-permute-start(bf16[4,6,8,512]{3,2,1,0:T(8,128)(2,1)S(1)} %get-tuple-element.76), channel_id=1, source_target_pairs={{0,3},{1,2},{2,1},{3,0},{4,7},{5,6},{6,5},{7,4},{8,11},{9,10},{10,... | collective-permute-start | bytes 589832 | tf_op jit(solution)/shard_map/ppermute | solution.py:224
  37.1 1.2 %copy-start.2 = (bf16[512,512]{1,0:T(8,128)(2,1)S(1)}, bf16[512,512]{1,0:T(8,128)(2,1)}, u32[]{:S(2)}) copy-start(bf16[512,512]{1,0:T(8,128)(2,1)} %param.24) | copy-start | bytes 1572868
